TPU v7x, 32 devices: a whole 2x2x4 slice. The times are simulated.
32 devices in a mesh: groups: 2 (over x), ctx: 16 (over z, y, core).
Axes of the slice: x: 2, y: 2, z: 4, core: 2. Of those that a mesh axis runs over, the one named last changes fastest.
Arguments:
- queries: bfloat16 [4096, 2048], P(('groups', 'ctx')), parts along dimension 0, may hold values from -60 to 60, as said below
- key_vectors: bfloat16 [4096, 2048], P(('groups', 'ctx')), parts along dimension 0, may hold values from -60 to 60, as said below
- values: bfloat16 [4096, 2048], P(('groups', 'ctx')), parts along dimension 0, may hold values from -6 to 6
- grad_out: bfloat16 [4096, 2048], P(('groups', 'ctx')), parts along dimension 0, may hold values from -6 to 6
- file_lengths: int32 [128], P('groups'), parts along dimension 0, may hold values from 1 to 512, 2048 in all
- reach_table: int32 [32], P(('groups', 'ctx')), parts along dimension 0, may hold values from 1 to 11
Outputs:
- attended: bfloat16 [4096, 2048], P(('groups', 'ctx')), parts along dimension 0
- grad_queries: bfloat16 [4096, 2048], P(('groups', 'ctx')), parts along dimension 0
- grad_keys: bfloat16 [4096, 2048], P(('groups', 'ctx')), parts along dimension 0
- grad_values: bfloat16 [4096, 2048], P(('groups', 'ctx')), parts along dimension 0
There are 2 independent parts, one for each index of `groups`. A program takes and returns all parts, laid end to end along the dimension named above; each array names one. Nothing has to cross between parts.
Inputs may be any that keep to these rules, and one draw needn't show every extreme that they name: `queries`: entries are finite. `key_vectors`: entries are finite.
All inputs are finite; a program needn't handle non-finite values.
Results may differ from a plain program's by a relative error of at most 0.0045.
The roundings to bfloat16 on the way count: a program that leaves them out, or rounds other values in their place, can miss the bound.
Values may be sent and summed in bfloat16 or wider, within the bound.
No kernel may reach another device: no remote copies, remote signals or barrier semaphores. Data moves between devices by JAX's collectives and lax.ppermute only.
A program may use at most 128 MiB of HBM per device.

v0:
```python
import math

import jax
import jax.numpy as jnp
from jax import lax
from jax.sharding import PartitionSpec as P

HEADS = 16
HEAD_DIM = 128
BLOCK = 128


def from_behind(value, axis, steps):
    count = lax.axis_size(axis)
    leading, last = (max(0, -steps), min(count, count - steps))
    return lax.ppermute(value, axis, [(source, source + steps) for source in range(leading, last)])


def rounded(matrix):
    return lax.optimization_barrier(matrix.astype(jnp.bfloat16))


def file_positions(file_lengths, global_rows):
    file_ends = jnp.cumsum(file_lengths)
    starts = file_ends - file_lengths
    owned_mask = starts[None, :] <= global_rows[:, None]
    latest = jnp.max(jnp.where(owned_mask, starts[None, :], 0), axis=1)
    return global_rows - latest


def rotary(matrix, positions, head_count, head_width, inverse):
    half_width = head_width // 2
    exponent = jnp.arange(half_width, dtype=jnp.float32) * (2.0 / head_width)
    frequency = jnp.exp(exponent * -math.log(10000.0))
    angles = positions.astype(jnp.float32)[:, None] * frequency[None, :]
    cosine = jnp.cos(angles)[:, None, :]
    sine_table = jnp.sin(angles)[:, None, :]
    shaped = matrix.astype(jnp.float32).reshape(matrix.shape[0], head_count, head_width)
    former = shaped[..., :half_width]
    latter = shaped[..., half_width:]
    if inverse:
        turned = jnp.concatenate(
            [former * cosine + latter * sine_table, latter * cosine - former * sine_table], axis=-1
        )
    else:
        turned = jnp.concatenate(
            [former * cosine - latter * sine_table, latter * cosine + former * sine_table], axis=-1
        )
    return turned.reshape(matrix.shape[0], head_count * head_width)


def block_sources(per_shard, levels):
    entries = [(0, 0)]
    for level_index in range(levels):
        target = 0 - 2**level_index
        entries.append((-(target // per_shard), target % per_shard))
    layout = [entries]
    return layout


def reach_mask(reach_rows, first_block, per_shard, levels):
    block_ids = first_block + jnp.arange(per_shard, dtype=jnp.int32)
    level_ids = jnp.arange(levels, dtype=jnp.int32)
    distances = jnp.array([2**level_index for level_index in range(levels)], dtype=jnp.int32)
    reached = (level_ids[None, :] < reach_rows[:, None]) & (
        block_ids[:, None] - distances[None, :] >= 0
    )
    return jnp.concatenate([jnp.ones((per_shard, 1), dtype=bool), reached], axis=1)


def score_mask(valid_slots, block_rows):
    row_ids = jnp.arange(block_rows)
    causal = row_ids[None, :] <= row_ids[:, None]
    first_slot = jnp.arange(valid_slots.shape[1]) == 0
    inside = jnp.where(first_slot[:, None, None], causal[None], True)
    allowed = inside[None] & valid_slots[:, :, None, None]
    return jnp.transpose(allowed, (0, 2, 1, 3))[:, None]


def on_device(queries, key_vectors, values, grad_out, file_lengths, reach_table):
    local_rows = queries.shape[0]
    width_all = queries.shape[1]
    per_shard = local_rows // BLOCK
    ctx_size = lax.axis_size("ctx")
    levels = (per_shard * ctx_size - 1).bit_length()
    layout = block_sources(per_shard, levels)
    slot_count = ctx_size.bit_length()
    scale_factor = 1.0 / math.sqrt(HEAD_DIM)
    shard_index = lax.axis_index("ctx")
    global_rows = shard_index * local_rows + jnp.arange(local_rows, dtype=jnp.int32)
    positions = file_positions(file_lengths, global_rows)
    query_rot = rounded(rotary(queries, positions, HEADS, HEAD_DIM, False))
    key_rot = rounded(rotary(key_vectors, positions, HEADS, HEAD_DIM, False))
    block_shape = (per_shard, BLOCK, HEADS, HEAD_DIM)
    query_stack = query_rot.reshape(block_shape)
    grad_stack = grad_out.reshape(block_shape)
    valid_slots = reach_mask(reach_table, shard_index * per_shard, per_shard, levels)
    allowed = score_mask(valid_slots, BLOCK)

    def fetch_first(offset):
        return from_behind((key_rot, values), "ctx", offset)

    def assemble(fetcher):
        sources = {0: (key_rot.reshape(block_shape), values.reshape(block_shape))}
        for slot_index in range(1, slot_count):
            offset = 2 ** (slot_index - 1)
            moved_keys, moved_values = fetcher(offset)
            sources[offset] = (moved_keys.reshape(block_shape), moved_values.reshape(block_shape))
        key_stack = jnp.stack(
            [
                jnp.stack([sources[offset][0][block_index] for offset, block_index in entries])
                for entries in layout
            ]
        )
        value_stack = jnp.stack(
            [
                jnp.stack([sources[offset][1][block_index] for offset, block_index in entries])
                for entries in layout
            ]
        )
        return (key_stack, value_stack)

    key_stack, value_stack = assemble(fetch_first)
    raw_scores = (
        jnp.einsum("bthd,bnuhd->bhtnu", query_stack, key_stack, preferred_element_type=jnp.float32)
        * scale_factor
    )
    scores = jnp.where(allowed, raw_scores, -1e30)
    row_peak = jnp.max(scores, axis=(3, 4), keepdims=True)
    summed = jnp.sum(jnp.exp(scores - row_peak), axis=(3, 4), keepdims=True)
    log_total = row_peak + jnp.log(summed)
    weights32 = jnp.exp(scores - log_total)
    weights = rounded(weights32)
    output = rounded(
        jnp.einsum("bhtnu,bnuhd->bthd", weights, value_stack, preferred_element_type=jnp.float32)
    )
    grad_probs = jnp.einsum(
        "bthd,bnuhd->bhtnu", grad_stack, value_stack, preferred_element_type=jnp.float32
    )
    delta_rows = jnp.sum(grad_stack.astype(jnp.float32) * output.astype(jnp.float32), axis=-1)
    delta_rows = jnp.transpose(delta_rows, (0, 2, 1))[:, :, :, None, None]
    grad_scores = rounded(weights32 * (grad_probs - delta_rows) * scale_factor)
    query_grad = jnp.einsum(
        "bhtnu,bnuhd->bthd", grad_scores, key_stack, preferred_element_type=jnp.float32
    )
    key_terms = jnp.einsum(
        "bhtnu,bthd->bnuhd", grad_scores, query_stack, preferred_element_type=jnp.float32
    )
    value_terms = jnp.einsum(
        "bhtnu,bthd->bnuhd", weights, grad_stack, preferred_element_type=jnp.float32
    )
    key_parts = [jnp.zeros(block_shape, jnp.float32) for slot_index in range(slot_count)]
    value_parts = [jnp.zeros(block_shape, jnp.float32) for slot_index in range(slot_count)]
    for query_block, entries in enumerate(layout):
        for slot_position, (offset, block_index) in enumerate(entries):
            slot_number = offset.bit_length()
            key_parts[slot_number] = (
                key_parts[slot_number].at[block_index].add(key_terms[query_block, slot_position])
            )
            value_parts[slot_number] = (
                value_parts[slot_number]
                .at[block_index]
                .add(value_terms[query_block, slot_position])
            )
    key_accum = rounded(key_parts[0]).astype(jnp.float32)
    value_accum = rounded(value_parts[0]).astype(jnp.float32)
    for slot_index in range(1, slot_count):
        offset = 2 ** (slot_index - 1)
        outgoing_keys = key_parts[slot_index].astype(jnp.bfloat16)
        outgoing_values = value_parts[slot_index].astype(jnp.bfloat16)
        returned_keys, returned_values = from_behind(
            (outgoing_keys, outgoing_values), "ctx", -offset
        )
        key_accum = key_accum + returned_keys.astype(jnp.float32)
        value_accum = value_accum + returned_values.astype(jnp.float32)
    attended = output.reshape(local_rows, width_all)
    grad_queries = rotary(
        query_grad.reshape(local_rows, width_all), positions, HEADS, HEAD_DIM, True
    ).astype(jnp.bfloat16)
    grad_keys = rotary(
        key_accum.reshape(local_rows, width_all), positions, HEADS, HEAD_DIM, True
    ).astype(jnp.bfloat16)
    grad_values = value_accum.reshape(local_rows, width_all).astype(jnp.bfloat16)
    return (attended, grad_queries, grad_keys, grad_values)


def solution(mesh):
    placed = (
        P(("groups", "ctx"), None),
        P(("groups", "ctx"), None),
        P(("groups", "ctx"), None),
        P(("groups", "ctx"), None),
        P("groups"),
        P(("groups", "ctx")),
    )
    return jax.shard_map(
        on_device,
        mesh=mesh,
        in_specs=placed,
        out_specs=(
            P(("groups", "ctx"), None),
            P(("groups", "ctx"), None),
            P(("groups", "ctx"), None),
            P(("groups", "ctx"), None),
        ),
        check_vma=False,
    )
```

profile of v0, /device:TPU:15, one launch (start us, length us, event | category | flops | bytes accessed | tf_op | source)
XLA Modules:
  0.0 238.3 jit_solution(87278662829536751)
XLA Ops:
  6.3 5.0 %collective-permute-start.7 = (bf16[128,2048]{0,1:T(8,128)(2,1)}, bf16[128,2048]{0,1:T(8,128)(2,1)}, u32[]{:S(2)}, u32[]{:S(2)}) collective-permute-start(bf16[128,2048]{0,1:T(8,128)(2,1)} %bitcast.15), channel_id=1, source_target_pairs={{0,8},{1,9},{2,10},{3,11},{4,12},{5,13},{6,14},{7,15},{16,24},{17,... | collective-permute-start | bytes 1572872 | tf_op jit(solution)/shard_map/ppermute | solution.py:16
  15.2 3.1 %collective-permute-start.4 = (bf16[128,2048]{0,1:T(8,128)(2,1)}, bf16[128,2048]{0,1:T(8,128)(2,1)}, u32[]{:S(2)}, u32[]{:S(2)}) collective-permute-start(bf16[128,2048]{0,1:T(8,128)(2,1)} %bitcast.15), channel_id=1, source_target_pairs={{0,1},{1,2},{2,3},{3,4},{4,5},{5,6},{6,7},{7,8},{8,9},{9,10},{10,1... | collective-permute-start | bytes 1572872 | tf_op jit(solution)/shard_map/ppermute | solution.py:16
  21.0 2.0 copy.68
  25.1 2.0 copy.76
  28.2 2.0 constant_dynamic-update-slice_fusion.4
  30.3 3.3 %collective-permute-done.7 = bf16[128,2048]{0,1:T(8,128)(2,1)} collective-permute-done((bf16[128,2048]{0,1:T(8,128)(2,1)}, bf16[128,2048]{0,1:T(8,128)(2,1)}, u32[]{:S(2)}, u32[]{:S(2)}) %collective-permute-start.7) | collective-permute-done | bytes 524320 | tf_op jit(solution)/shard_map/ppermute | solution.py:16
  35.5 2.1 copy.80
  37.6 7.2 %collective-permute-done.6 = bf16[128,2048]{0,1:T(8,128)(2,1)} collective-permute-done((bf16[128,2048]{0,1:T(8,128)(2,1)}, bf16[128,2048]{0,1:T(8,128)(2,1)}, u32[]{:S(2)}, u32[]{:S(2)}) %collective-permute-start.6) | collective-permute-done | bytes 524320 | tf_op jit(solution)/shard_map/ppermute | solution.py:16
  44.9 2.1 collective-permute-start.3
  46.9 2.0 copy.79
  49.0 7.1 %collective-permute-done.5 = bf16[128,2048]{0,1:T(8,128)(2,1)} collective-permute-done((bf16[128,2048]{0,1:T(8,128)(2,1)}, bf16[128,2048]{0,1:T(8,128)(2,1)}, u32[]{:S(2)}, u32[]{:S(2)}) %collective-permute-start.5) | collective-permute-done | bytes 524320 | tf_op jit(solution)/shard_map/ppermute | solution.py:16
  56.1 2.1 collective-permute-start.2
  58.2 2.0 copy.78
  60.2 12.7 %collective-permute-done.4 = bf16[128,2048]{0,1:T(8,128)(2,1)} collective-permute-done((bf16[128,2048]{0,1:T(8,128)(2,1)}, bf16[128,2048]{0,1:T(8,128)(2,1)}, u32[]{:S(2)}, u32[]{:S(2)}) %collective-permute-start.4) | collective-permute-done | bytes 524320 | tf_op jit(solution)/shard_map/ppermute | solution.py:16
  72.9 2.0 copy.77
  83.5 6.3 %collective-permute-done.1 = bf16[128,2048]{1,0:T(8,128)(2,1)} collective-permute-done((bf16[128,2048]{1,0:T(8,128)(2,1)}, bf16[128,2048]{1,0:T(8,128)(2,1)}, u32[]{:S(2)}, u32[]{:S(2)}) %collective-permute-start.1) | collective-permute-done | bytes 524320 | tf_op jit(solution)/shard_map/ppermute | solution.py:16
  91.1 9.9 %collective-permute-done = bf16[128,2048]{1,0:T(8,128)(2,1)} collective-permute-done((bf16[128,2048]{1,0:T(8,128)(2,1)}, bf16[128,2048]{1,0:T(8,128)(2,1)}, u32[]{:S(2)}, u32[]{:S(2)}) %collective-permute-start) | collective-permute-done | bytes 524320 | tf_op jit(solution)/shard_map/ppermute | solution.py:16
  101.0 2.0 copy.69
  103.1 9.3 %collective-permute-done.2 = bf16[128,2048]{1,0:T(8,128)(2,1)} collective-permute-done((bf16[128,2048]{1,0:T(8,128)(2,1)}, bf16[128,2048]{1,0:T(8,128)(2,1)}, u32[]{:S(2)}, u32[]{:S(2)}) %collective-permute-start.2) | collective-permute-done | bytes 524320 | tf_op jit(solution)/shard_map/ppermute | solution.py:16
  112.4 2.0 copy.71
  114.4 2.0 constant_dynamic-update-slice_fusion.3
  117.2 2.0 constant_dynamic-update-slice_fusion.1
  121.5 2.7 %fusion.22 = bf16[1,128,16,128]{1,3,2,0:T(8,128)(2,1)S(1)} fusion(bf16[5,128,16,128]{1,3,0,2:T(8,128)(2,1)} %constant_dynamic-update-slice_fusion, bf16[1,16,128,5,128]{2,4,3,1,0:T(8,128)(2,1)S(1)} %fusion.4), kind=kOutput, calls=%fused_computation.21 | convolution fusion | flops 335806464 | bytes 5767168 | tf_op jit(solution)/shard_map/bhtnu,bnuhd->bthd/dot_general | solution.py:135
  124.2 2.4 %convert_bitcast_fusion = bf16[1,5,128,16,128]{4,2,1,3,0:T(8,128)(2,1)} fusion(bf16[1,16,128,5,128]{2,4,3,1,0:T(8,128)(2,1)S(1)} %fusion.4, bf16[128,16,128,1]{2,1,0,3:T(8,128)(2,1)S(1)} %bitcast.162), kind=kOutput, calls=%fused_computation.16 | convolution fusion | flops 336855040 | bytes 5767168 | tf_op jit(solution)/shard_map/bhtnu,bthd->bnuhd/dot_general | solution.py:149
  127.7 2.5 %fusion.5 = bf16[1,16,128,5,128]{2,4,3,1,0:T(8,128)(2,1)S(1)} fusion(f32[16,128,5,128]{1,3,2,0:T(8,128)S(1)} %bitcast.146, f32[16,128]{1,0:T(8,128)S(1)} %bitcast.164, f32[16,128]{1,0:T(8,128)S(1)} %log_add_fusion, pred[128,5,128]{0,2,1:T(8,128)(4,1)S(1)} %and_bitcast_fusion, bf16[5,128,16,128]{1,3,0,2:T(8,128)(2,1)S(1)} %copy-done.8, ...), kind=kOutput, calls=%fused_computation.9 | convolution fusion | flops 344719360 | bytes 11108352 | tf_op jit(solution)/shard_map/bthd,bnuhd->bhtnu/dot_general | solution.py:137
  138.3 2.1 collective-permute-start.14
  144.3 3.0 %collective-permute-done.13 = bf16[1,128,16,128]{3,1,2,0:T(8,128)(2,1)S(1)} collective-permute-done((bf16[1,128,16,128]{3,1,2,0:T(8,128)(2,1)S(1)}, bf16[1,128,16,128]{3,1,2,0:T(8,128)(2,1)S(1)}, u32[]{:S(2)}, u32[]{:S(2)}) %collective-permute-start.13) | collective-permute-done | bytes 524320 | tf_op jit(solution)/shard_map/ppermute | solution.py:16
  149.2 12.5 %collective-permute-done.12 = bf16[1,128,16,128]{3,1,2,0:T(8,128)(2,1)S(1)} collective-permute-done((bf16[1,128,16,128]{3,1,2,0:T(8,128)(2,1)S(1)}, bf16[1,128,16,128]{3,1,2,0:T(8,128)(2,1)S(1)}, u32[]{:S(2)}, u32[]{:S(2)}) %collective-permute-start.12) | collective-permute-done | bytes 524320 | tf_op jit(solution)/shard_map/ppermute | solution.py:16
  167.5 17.8 %collective-permute-done.14 = bf16[1,128,16,128]{3,1,2,0:T(8,128)(2,1)S(1)} collective-permute-done((bf16[1,128,16,128]{3,1,2,0:T(8,128)(2,1)S(1)}, bf16[1,128,16,128]{3,1,2,0:T(8,128)(2,1)S(1)}, u32[]{:S(2)}, u32[]{:S(2)}) %collective-permute-start.14) | collective-permute-done | bytes 524320 | tf_op jit(solution)/shard_map/ppermute | solution.py:16
  187.0 20.8 %collective-permute-done.10 = bf16[1,128,16,128]{1,3,2,0:T(8,128)(2,1)} collective-permute-done((bf16[1,128,16,128]{1,3,2,0:T(8,128)(2,1)}, bf16[1,128,16,128]{1,3,2,0:T(8,128)(2,1)}, u32[]{:S(2)}, u32[]{:S(2)}) %collective-permute-start.10) | collective-permute-done | bytes 524320 | tf_op jit(solution)/shard_map/ppermute | solution.py:16
  207.8 18.2 %collective-permute-done.9 = bf16[1,128,16,128]{1,3,2,0:T(8,128)(2,1)} collective-permute-done((bf16[1,128,16,128]{1,3,2,0:T(8,128)(2,1)}, bf16[1,128,16,128]{1,3,2,0:T(8,128)(2,1)}, u32[]{:S(2)}, u32[]{:S(2)}) %collective-permute-start.9) | collective-permute-done | bytes 524320 | tf_op jit(solution)/shard_map/ppermute | solution.py:16
  226.0 7.9 %collective-permute-done.8 = bf16[1,128,16,128]{1,3,2,0:T(8,128)(2,1)} collective-permute-done((bf16[1,128,16,128]{1,3,2,0:T(8,128)(2,1)}, bf16[1,128,16,128]{1,3,2,0:T(8,128)(2,1)}, u32[]{:S(2)}, u32[]{:S(2)}) %collective-permute-start.8) | collective-permute-done | bytes 524320 | tf_op jit(solution)/shard_map/ppermute | solution.py:16
  (89 shorter events, 56.2 us)
Async XLA Ops:
  5.1 15.8 %copy-start.12 = (s32[4]{0:T(128)S(1)}, s32[4]{0:T(128)}, u32[]{:S(2)}) copy-start(s32[4]{0:T(128)} %constant.222) | copy-start | bytes 52
  5.1 17.9 %copy-start.9 = (bf16[128,2048]{1,0:T(8,128)(2,1)S(1)}, bf16[128,2048]{1,0:T(8,128)(2,1)}, u32[]{:S(2)}) copy-start(bf16[128,2048]{1,0:T(8,128)(2,1)} %param.30) | copy-start | bytes 1572868
  6.3 72.2 %copy-start.4 = (bf16[128,16,128]{0,2,1:T(8,128)(2,1)}, bf16[128,16,128]{0,2,1:T(8,128)(2,1)S(1)}, u32[]{:S(2)}) copy-start(bf16[128,16,128]{0,2,1:T(8,128)(2,1)S(1)} %get-tuple-element.161) | copy-start | bytes 1572868
  6.3 27.3 %collective-permute-start.7 = (bf16[128,2048]{0,1:T(8,128)(2,1)}, bf16[128,2048]{0,1:T(8,128)(2,1)}, u32[]{:S(2)}, u32[]{:S(2)}) collective-permute-start(bf16[128,2048]{0,1:T(8,128)(2,1)} %bitcast.15), channel_id=1, source_target_pairs={{0,8},{1,9},{2,10},{3,11},{4,12},{5,13},{6,14},{7,15},{16,24},{17,... | collective-permute-start | bytes 1572872 | tf_op jit(solution)/shard_map/ppermute | solution.py:16
  11.3 33.5 %collective-permute-start.6 = (bf16[128,2048]{0,1:T(8,128)(2,1)}, bf16[128,2048]{0,1:T(8,128)(2,1)}, u32[]{:S(2)}, u32[]{:S(2)}) collective-permute-start(bf16[128,2048]{0,1:T(8,128)(2,1)} %bitcast.15), channel_id=1, source_target_pairs={{0,4},{1,5},{2,6},{3,7},{4,8},{5,9},{6,10},{7,11},{8,12},{9,13},{1... | collective-permute-start | bytes 1572872 | tf_op jit(solution)/shard_map/ppermute | solution.py:16
  13.2 42.9 %collective-permute-start.5 = (bf16[128,2048]{0,1:T(8,128)(2,1)}, bf16[128,2048]{0,1:T(8,128)(2,1)}, u32[]{:S(2)}, u32[]{:S(2)}) collective-permute-start(bf16[128,2048]{0,1:T(8,128)(2,1)} %bitcast.15), channel_id=1, source_target_pairs={{0,2},{1,3},{2,4},{3,5},{4,6},{5,7},{6,8},{7,9},{8,10},{9,11},{10,... | collective-permute-start | bytes 1572872 | tf_op jit(solution)/shard_map/ppermute | solution.py:16
  15.2 57.8 %collective-permute-start.4 = (bf16[128,2048]{0,1:T(8,128)(2,1)}, bf16[128,2048]{0,1:T(8,128)(2,1)}, u32[]{:S(2)}, u32[]{:S(2)}) collective-permute-start(bf16[128,2048]{0,1:T(8,128)(2,1)} %bitcast.15), channel_id=1, source_target_pairs={{0,1},{1,2},{2,3},{3,4},{4,5},{5,6},{6,7},{7,8},{8,9},{9,10},{10,1... | collective-permute-start | bytes 1572872 | tf_op jit(solution)/shard_map/ppermute | solution.py:16
  18.2 71.6 %collective-permute-start.1 = (bf16[128,2048]{1,0:T(8,128)(2,1)}, bf16[128,2048]{1,0:T(8,128)(2,1)}, u32[]{:S(2)}, u32[]{:S(2)}) collective-permute-start(bf16[128,2048]{1,0:T(8,128)(2,1)} %param.29), channel_id=1, source_target_pairs={{0,2},{1,3},{2,4},{3,5},{4,6},{5,7},{6,8},{7,9},{8,10},{9,11},{10,... | collective-permute-start | bytes 1572872 | tf_op jit(solution)/shard_map/ppermute | solution.py:16
  33.6 67.4 %collective-permute-start = (bf16[128,2048]{1,0:T(8,128)(2,1)}, bf16[128,2048]{1,0:T(8,128)(2,1)}, u32[]{:S(2)}, u32[]{:S(2)}) collective-permute-start(bf16[128,2048]{1,0:T(8,128)(2,1)} %param.29), channel_id=1, source_target_pairs={{0,1},{1,2},{2,3},{3,4},{4,5},{5,6},{6,7},{7,8},{8,9},{9,10},{10,1... | collective-permute-start | bytes 1572872 | tf_op jit(solution)/shard_map/ppermute | solution.py:16
  44.9 74.4 %collective-permute-start.3 = (bf16[128,2048]{1,0:T(8,128)(2,1)}, bf16[128,2048]{1,0:T(8,128)(2,1)}, u32[]{:S(2)}, u32[]{:S(2)}) collective-permute-start(bf16[128,2048]{1,0:T(8,128)(2,1)} %param.29), channel_id=1, source_target_pairs={{0,8},{1,9},{2,10},{3,11},{4,12},{5,13},{6,14},{7,15},{16,24},{17,... | collective-permute-start | bytes 1572872 | tf_op jit(solution)/shard_map/ppermute | solution.py:16
  56.1 56.3 %collective-permute-start.2 = (bf16[128,2048]{1,0:T(8,128)(2,1)}, bf16[128,2048]{1,0:T(8,128)(2,1)}, u32[]{:S(2)}, u32[]{:S(2)}) collective-permute-start(bf16[128,2048]{1,0:T(8,128)(2,1)} %param.29), channel_id=1, source_target_pairs={{0,4},{1,5},{2,6},{3,7},{4,8},{5,9},{6,10},{7,11},{8,12},{9,13},{1... | collective-permute-start | bytes 1572872 | tf_op jit(solution)/shard_map/ppermute | solution.py:16
  75.0 3.5 %copy-start.10 = (bf16[1,128,16,128]{3,1,0,2:T(8,128)(2,1)S(1)}, bf16[1,128,16,128]{3,1,0,2:T(8,128)(2,1)}, u32[]{:S(2)}) copy-start(bf16[1,128,16,128]{3,1,0,2:T(8,128)(2,1)} %copy.80) | copy-start | bytes 1572868
  78.5 1.5 copy-start.2
  80.0 2.3 copy-start
  121.5 2.7 %copy-start.11 = (bf16[16,8,16,128]{3,2,1,0:T(8,128)(2,1)S(1)}, bf16[16,8,16,128]{3,2,1,0:T(8,128)(2,1)}, u32[]{:S(2)}) copy-start(bf16[16,8,16,128]{3,2,1,0:T(8,128)(2,1)} %copy.120) | copy-start | bytes 1572868
  121.5 5.2 %copy-start.6 = (f32[128,2048]{0,1:T(8,128)S(1)}, f32[128,2048]{0,1:T(8,128)}, u32[]{:S(2)}) copy-start(f32[128,2048]{0,1:T(8,128)} %copy.85) | copy-start | bytes 3145732
  121.5 5.3 %copy-start.8 = (bf16[5,128,16,128]{1,3,0,2:T(8,128)(2,1)S(1)}, bf16[5,128,16,128]{1,3,0,2:T(8,128)(2,1)}, u32[]{:S(2)}) copy-start(bf16[5,128,16,128]{1,3,0,2:T(8,128)(2,1)} %constant_dynamic-update-slice_fusion) | copy-start | bytes 7864324
  124.2 3.5 %copy-start.1 = (f32[16,128,640]{1,2,0:S(1)}, f32[16,128,640]{1,2,0}, u32[]{:S(2)}) copy-start(f32[16,128,640]{1,2,0} %copy-done) | copy-start | bytes 15728644
  131.2 9.2 %copy-start.5 = (bf16[128,16,128]{0,2,1:T(8,128)(2,1)S(1)}, bf16[128,16,128]{0,2,1:T(8,128)(2,1)}, u32[]{:S(2)}) copy-start(bf16[128,16,128]{0,2,1:T(8,128)(2,1)} %copy-done.4) | copy-start | bytes 1572868
  133.1 14.2 %collective-permute-start.13 = (bf16[1,128,16,128]{3,1,2,0:T(8,128)(2,1)S(1)}, bf16[1,128,16,128]{3,1,2,0:T(8,128)(2,1)S(1)}, u32[]{:S(2)}, u32[]{:S(2)}) collective-permute-start(bf16[1,128,16,128]{3,1,2,0:T(8,128)(2,1)S(1)} %get-tuple-element.137), channel_id=1, source_target_pairs={{2,0},{3,1},{4,2},{5,3},{6,4},{7,5},{8,6},{9,7},{10,8},{11,9},{12,... | collective-permute-start | bytes 1572872 | tf_op jit(solution)/shard_map/ppermute | solution.py:16
  135.0 26.6 %collective-permute-start.12 = (bf16[1,128,16,128]{3,1,2,0:T(8,128)(2,1)S(1)}, bf16[1,128,16,128]{3,1,2,0:T(8,128)(2,1)S(1)}, u32[]{:S(2)}, u32[]{:S(2)}) collective-permute-start(bf16[1,128,16,128]{3,1,2,0:T(8,128)(2,1)S(1)} %get-tuple-element.138), channel_id=1, source_target_pairs={{1,0},{2,1},{3,2},{4,3},{5,4},{6,5},{7,6},{8,7},{9,8},{10,9},{11,1... | collective-permute-start | bytes 1572872 | tf_op jit(solution)/shard_map/ppermute | solution.py:16
  137.0 26.6 %collective-permute-start.15 = (bf16[1,128,16,128]{3,1,2,0:T(8,128)(2,1)S(1)}, bf16[1,128,16,128]{3,1,2,0:T(8,128)(2,1)S(1)}, u32[]{:S(2)}, u32[]{:S(2)}) collective-permute-start(bf16[1,128,16,128]{3,1,2,0:T(8,128)(2,1)S(1)} %get-tuple-element.139), channel_id=1, source_target_pairs={{8,0},{9,1},{10,2},{11,3},{12,4},{13,5},{14,6},{15,7},{24,16},{25,... | collective-permute-start | bytes 1572872 | tf_op jit(solution)/shard_map/ppermute | solution.py:16
  138.3 47.0 %collective-permute-start.14 = (bf16[1,128,16,128]{3,1,2,0:T(8,128)(2,1)S(1)}, bf16[1,128,16,128]{3,1,2,0:T(8,128)(2,1)S(1)}, u32[]{:S(2)}, u32[]{:S(2)}) collective-permute-start(bf16[1,128,16,128]{3,1,2,0:T(8,128)(2,1)S(1)} %get-tuple-element.140), channel_id=1, source_target_pairs={{4,0},{5,1},{6,2},{7,3},{8,4},{9,5},{10,6},{11,7},{12,8},{13,9},{1... | collective-permute-start | bytes 1572872 | tf_op jit(solution)/shard_map/ppermute | solution.py:16
  141.5 24.0 %copy-start.3 = (bf16[5,128,16,128]{3,1,0,2:T(8,128)(2,1)S(1)}, bf16[5,128,16,128]{3,1,0,2:T(8,128)(2,1)}, u32[]{:S(2)}) copy-start(bf16[5,128,16,128]{3,1,0,2:T(8,128)(2,1)} %copy-done.2) | copy-start | bytes 7864324
  142.9 44.1 %collective-permute-start.11 = (bf16[1,128,16,128]{1,3,2,0:T(8,128)(2,1)}, bf16[1,128,16,128]{1,3,2,0:T(8,128)(2,1)}, u32[]{:S(2)}, u32[]{:S(2)}) collective-permute-start(bf16[1,128,16,128]{1,3,2,0:T(8,128)(2,1)} %get-tuple-element.142), channel_id=1, source_target_pairs={{8,0},{9,1},{10,2},{11,3},{12,4},{13,5},{14,6},{15,7},{24,16},{25,... | collective-permute-start | bytes 1572872 | tf_op jit(solution)/shard_map/ppermute | solution.py:16
  147.3 60.6 %collective-permute-start.10 = (bf16[1,128,16,128]{1,3,2,0:T(8,128)(2,1)}, bf16[1,128,16,128]{1,3,2,0:T(8,128)(2,1)}, u32[]{:S(2)}, u32[]{:S(2)}) collective-permute-start(bf16[1,128,16,128]{1,3,2,0:T(8,128)(2,1)} %get-tuple-element.143), channel_id=1, source_target_pairs={{4,0},{5,1},{6,2},{7,3},{8,4},{9,5},{10,6},{11,7},{12,8},{13,9},{1... | collective-permute-start | bytes 1572872 | tf_op jit(solution)/shard_map/ppermute | solution.py:16
  161.7 64.3 %collective-permute-start.9 = (bf16[1,128,16,128]{1,3,2,0:T(8,128)(2,1)}, bf16[1,128,16,128]{1,3,2,0:T(8,128)(2,1)}, u32[]{:S(2)}, u32[]{:S(2)}) collective-permute-start(bf16[1,128,16,128]{1,3,2,0:T(8,128)(2,1)} %get-tuple-element.144), channel_id=1, source_target_pairs={{2,0},{3,1},{4,2},{5,3},{6,4},{7,5},{8,6},{9,7},{10,8},{11,9},{12,... | collective-permute-start | bytes 1572872 | tf_op jit(solution)/shard_map/ppermute | solution.py:16
  163.6 70.3 %collective-permute-start.8 = (bf16[1,128,16,128]{1,3,2,0:T(8,128)(2,1)}, bf16[1,128,16,128]{1,3,2,0:T(8,128)(2,1)}, u32[]{:S(2)}, u32[]{:S(2)}) collective-permute-start(bf16[1,128,16,128]{1,3,2,0:T(8,128)(2,1)} %get-tuple-element.145), channel_id=1, source_target_pairs={{1,0},{2,1},{3,2},{4,3},{5,4},{6,5},{7,6},{8,7},{9,8},{10,9},{11,1... | collective-permute-start | bytes 1572872 | tf_op jit(solution)/shard_map/ppermute | solution.py:16
  186.0 49.8 %copy-start.7 = (f32[128,16,128]{0,2,1:T(8,128)S(1)}, f32[128,16,128]{0,2,1:T(8,128)}, u32[]{:S(2)}) copy-start(f32[128,16,128]{0,2,1:T(8,128)} %convolution_bitcast_fusion) | copy-start | bytes 3145732
where the time goes:
time: 240 us; the launch traced here: 238 us
  waiting for transfers between devices  136 us (57%)
  local copies, waits for them, and re-layouts  46.2 us (19%)
  starting transfers between devices  34.4 us (14%)
  matrix products  11.4 us (5%)
  other arithmetic  8.52 us (4%)
    ppermute x16, waiting for transfers between devices, from_behind(): lax.ppermute(value, axis, [(source, source + steps) for source in range(l...  136 us
    ppermute x16, starting transfers between devices, from_behind(): lax.ppermute(value, axis, [(source, source + steps) for source in range(l...  34.4 us
    unnamed x40, local copies, waits for them, and re-layouts  20.3 us
    another operation x6, local copies, waits for them, and re-layouts, assemble(): jnp.stack([sources[offset][0][block_index] for offset, block_index in ent...  10.3 us
    ppermute x4, local copies, waits for them, and re-layouts, from_behind(): lax.ppermute(value, axis, [(source, source + steps) for source in range(l...  6.7 us
  transfers between devices with their start and end apart: 16, of which 13 were waited for; matrix products, arithmetic and copies ran while one was open for 17% of the time, Pallas kernels for 0%

commit v1 on v0

v1 whole, which is shorter than its diff:
```python
import math

import jax
import jax.numpy as jnp
from jax import lax
from jax.sharding import PartitionSpec as P

HEADS = 16
HEAD_DIM = 128
BLOCK = 128
CHUNKS = 4


def from_behind(value, axis, steps):
    count = lax.axis_size(axis)
    leading, last = (max(0, -steps), min(count, count - steps))
    return lax.ppermute(value, axis, [(source, source + steps) for source in range(leading, last)])


def rounded(matrix):
    return lax.optimization_barrier(matrix.astype(jnp.bfloat16))


def file_positions(file_lengths, global_rows):
    file_ends = jnp.cumsum(file_lengths)
    starts = file_ends - file_lengths
    owned_mask = starts[None, :] <= global_rows[:, None]
    latest = jnp.max(jnp.where(owned_mask, starts[None, :], 0), axis=1)
    return global_rows - latest


def rotary(matrix, positions, head_count, head_width, inverse):
    half_width = head_width // 2
    exponent = jnp.arange(half_width, dtype=jnp.float32) * (2.0 / head_width)
    frequency = jnp.exp(exponent * -math.log(10000.0))
    angles = positions.astype(jnp.float32)[:, None] * frequency[None, :]
    cosine = jnp.cos(angles)[:, None, :]
    sine_table = jnp.sin(angles)[:, None, :]
    shaped = matrix.astype(jnp.float32).reshape(matrix.shape[0], head_count, head_width)
    former = shaped[..., :half_width]
    latter = shaped[..., half_width:]
    if inverse:
        turned = jnp.concatenate(
            [former * cosine + latter * sine_table, latter * cosine - former * sine_table], axis=-1
        )
    else:
        turned = jnp.concatenate(
            [former * cosine - latter * sine_table, latter * cosine + former * sine_table], axis=-1
        )
    return turned.reshape(matrix.shape[0], head_count * head_width)


def reach_mask(reach_rows, first_block, per_shard, levels):
    block_ids = first_block + jnp.arange(per_shard, dtype=jnp.int32)
    level_ids = jnp.arange(levels, dtype=jnp.int32)
    distances = jnp.array([2**level_index for level_index in range(levels)], dtype=jnp.int32)
    reached = (level_ids[None, :] < reach_rows[:, None]) & (
        block_ids[:, None] - distances[None, :] >= 0
    )
    return jnp.concatenate([jnp.ones((per_shard, 1), dtype=bool), reached], axis=1)


def score_mask(valid_slots, block_rows):
    row_ids = jnp.arange(block_rows)
    causal = row_ids[None, :] <= row_ids[:, None]
    first_slot = jnp.arange(valid_slots.shape[1]) == 0
    inside = jnp.where(first_slot[:, None, None], causal[None], True)
    allowed = inside[None] & valid_slots[:, :, None, None]
    return jnp.transpose(allowed, (0, 2, 1, 3))[:, None]


def attend_chunk(query_c, key_c, value_c, grad_c, allowed, offsets, heads):
    scale_factor = 1.0 / math.sqrt(HEAD_DIM)
    rows = query_c.shape[0]
    head_shape = (rows, heads, HEAD_DIM)
    pair = jnp.stack([key_c, value_c])
    received = [pair] + [from_behind(pair, "ctx", offset) for offset in offsets]
    key_stack = jnp.stack([moved[0].reshape(head_shape) for moved in received])[None]
    value_stack = jnp.stack([moved[1].reshape(head_shape) for moved in received])[None]
    query_stack = query_c.reshape((1,) + head_shape)
    grad_stack = grad_c.reshape((1,) + head_shape)
    raw_scores = (
        jnp.einsum("bthd,bnuhd->bhtnu", query_stack, key_stack, preferred_element_type=jnp.float32)
        * scale_factor
    )
    scores = jnp.where(allowed, raw_scores, -1e30)
    row_peak = jnp.max(scores, axis=(3, 4), keepdims=True)
    summed = jnp.sum(jnp.exp(scores - row_peak), axis=(3, 4), keepdims=True)
    log_total = row_peak + jnp.log(summed)
    weights32 = jnp.exp(scores - log_total)
    weights = rounded(weights32)
    output = rounded(
        jnp.einsum("bhtnu,bnuhd->bthd", weights, value_stack, preferred_element_type=jnp.float32)
    )
    grad_probs = jnp.einsum(
        "bthd,bnuhd->bhtnu", grad_stack, value_stack, preferred_element_type=jnp.float32
    )
    delta_rows = jnp.sum(grad_stack.astype(jnp.float32) * output.astype(jnp.float32), axis=-1)
    delta_rows = jnp.transpose(delta_rows, (0, 2, 1))[:, :, :, None, None]
    grad_scores = rounded(weights32 * (grad_probs - delta_rows) * scale_factor)
    query_grad = jnp.einsum(
        "bhtnu,bnuhd->bthd", grad_scores, key_stack, preferred_element_type=jnp.float32
    )
    key_terms = jnp.einsum(
        "bhtnu,bthd->bnuhd", grad_scores, query_stack, preferred_element_type=jnp.float32
    )
    value_terms = jnp.einsum(
        "bhtnu,bthd->bnuhd", weights, grad_stack, preferred_element_type=jnp.float32
    )
    key_accum = rounded(key_terms[0, 0]).astype(jnp.float32)
    value_accum = rounded(value_terms[0, 0]).astype(jnp.float32)
    for slot_index, offset in enumerate(offsets, start=1):
        outgoing = jnp.stack([key_terms[0, slot_index], value_terms[0, slot_index]]).astype(
            jnp.bfloat16
        )
        returned = from_behind(outgoing, "ctx", -offset)
        key_accum = key_accum + returned[0].astype(jnp.float32)
        value_accum = value_accum + returned[1].astype(jnp.float32)
    width = heads * HEAD_DIM
    return (
        output.reshape(rows, width),
        query_grad.reshape(rows, width),
        key_accum.reshape(rows, width),
        value_accum.reshape(rows, width),
    )


def on_device(queries, key_vectors, values, grad_out, file_lengths, reach_table):
    local_rows = queries.shape[0]
    width_all = queries.shape[1]
    per_shard = local_rows // BLOCK
    ctx_size = lax.axis_size("ctx")
    levels = (per_shard * ctx_size - 1).bit_length()
    offsets = [2**level_index for level_index in range(levels)]
    shard_index = lax.axis_index("ctx")
    global_rows = shard_index * local_rows + jnp.arange(local_rows, dtype=jnp.int32)
    positions = file_positions(file_lengths, global_rows)
    query_rot = rounded(rotary(queries, positions, HEADS, HEAD_DIM, False))
    key_rot = rounded(rotary(key_vectors, positions, HEADS, HEAD_DIM, False))
    valid_slots = reach_mask(reach_table, shard_index * per_shard, per_shard, levels)
    allowed = score_mask(valid_slots, BLOCK)
    chunk_heads = HEADS // CHUNKS
    chunk_width = chunk_heads * HEAD_DIM
    pieces = []
    for chunk in range(CHUNKS):
        cols = slice(chunk * chunk_width, (chunk + 1) * chunk_width)
        pieces.append(
            attend_chunk(
                query_rot[:, cols],
                key_rot[:, cols],
                values[:, cols],
                grad_out[:, cols],
                allowed,
                offsets,
                chunk_heads,
            )
        )
    attended, query_grad, key_accum, value_accum = [
        jnp.concatenate(parts, axis=1) for parts in zip(*pieces)
    ]
    grad_queries = rotary(query_grad, positions, HEADS, HEAD_DIM, True).astype(jnp.bfloat16)
    grad_keys = rotary(key_accum, positions, HEADS, HEAD_DIM, True).astype(jnp.bfloat16)
    grad_values = value_accum.astype(jnp.bfloat16)
    return (attended, grad_queries, grad_keys, grad_values)


def solution(mesh):
    placed = (
        P(("groups", "ctx"), None),
        P(("groups", "ctx"), None),
        P(("groups", "ctx"), None),
        P(("groups", "ctx"), None),
        P("groups"),
        P(("groups", "ctx")),
    )
    return jax.shard_map(
        on_device,
        mesh=mesh,
        in_specs=placed,
        out_specs=(
            P(("groups", "ctx"), None),
            P(("groups", "ctx"), None),
            P(("groups", "ctx"), None),
            P(("groups", "ctx"), None),
        ),
        check_vma=False,
    )
```

time: 240 us -> 297 us (1.24)
  local copies, waits for them, and re-layouts: 46.2 us -> 89.2 us
  waiting for transfers between devices: 136 us -> 99.8 us
  starting transfers between devices: 34.4 us -> 70.3 us
  other arithmetic: 8.52 us -> 17.7 us
  matrix products: 11.4 us -> 15 us
    ppermute x16 -> x32, waiting for transfers between devices: 136 us -> 99.8 us  [from_behind(): lax.ppermute(value, axis, [(source, source + steps) for source in range(l...]
    ppermute x16 -> x32, starting transfers between devices: 34.4 us -> 70.3 us  [from_behind(): lax.ppermute(value, axis, [(source, source + steps) for source in range(l...]
    slice x0 -> x19, local copies, waits for them, and re-layouts: none -> 20.9 us  [the longest x12 11.5 us: attend_chunk(): moved[1].reshape(head_shape)]
    another operation x8 -> x34, local copies, waits for them, and re-layouts: 11.9 us -> 28.9 us  [the longest x24 21.3 us: attend_chunk(): jnp.stack([moved[0].reshape(head_shape) for moved in received])[None]]
    unnamed x40 -> x224, local copies, waits for them, and re-layouts: 20.3 us -> 31.1 us
    another operation x5 -> x28, other arithmetic: 2.72 us -> 10.2 us  [the longest x1 1.92 us: rotary(): matrix.astype(jnp.float32).reshape(matrix.shape[0], head_count, head_width)]
    ppermute x4 -> x0, local copies, waits for them, and re-layouts: 6.7 us -> none  [from_behind(): lax.ppermute(value, axis, [(source, source + steps) for source in range(l...]
    reshape x0 -> x8, local copies, waits for them, and re-layouts: none -> 4.66 us  [the longest x4 4.21 us: attend_chunk(): output.reshape(rows, width)]
  transfers between devices with their start and end apart: 16 -> 32, of which waited for: 13 -> 16; matrix products, arithmetic and copies ran while one was open for 17% -> 18% of each run, Pallas kernels for 0% -> 0%
where the time goes in v1:
time: 297 us; the launch traced here: 295 us
  waiting for transfers between devices  99.8 us (34%)
  local copies, waits for them, and re-layouts  89.2 us (30%)
  starting transfers between devices  70.3 us (24%)
  other arithmetic  17.7 us (6%)
  matrix products  15 us (5%)
  between operations  3.29 us (1%)
    ppermute x32, waiting for transfers between devices, from_behind(): lax.ppermute(value, axis, [(source, source + steps) for source in range(l...  99.8 us
    ppermute x32, starting transfers between devices, from_behind(): lax.ppermute(value, axis, [(source, source + steps) for source in range(l...  70.3 us
    unnamed x224, local copies, waits for them, and re-layouts  31.1 us
    another operation x24, local copies, waits for them, and re-layouts, attend_chunk(): jnp.stack([moved[0].reshape(head_shape) for moved in received])[None]  21.3 us
    slice x12, local copies, waits for them, and re-layouts, attend_chunk(): moved[1].reshape(head_shape)  11.5 us
    slice x4, local copies, waits for them, and re-layouts, attend_chunk(): moved[0].reshape(head_shape)  6.55 us
  transfers between devices with their start and end apart: 32, of which 16 were waited for; matrix products, arithmetic and copies ran while one was open for 18% of the time, Pallas kernels for 0%

profile of v1, /device:TPU:15, one launch (start us, length us, event | category | flops | bytes accessed | tf_op | source)
XLA Modules:
  0.0 295.2 jit_solution(17428560662675793151)
XLA Ops:
  5.7 4.9 %collective-permute-start.15 = (bf16[2,128,512]{1,2,0:T(8,128)(2,1)}, bf16[2,128,512]{1,2,0:T(8,128)(2,1)}, u32[]{:S(2)}, u32[]{:S(2)}) collective-permute-start(bf16[2,128,512]{1,2,0:T(8,128)(2,1)} %pad_maximum_fusion.11), channel_id=1, source_target_pairs={{0,8},{1,9},{2,10},{3,11},{4,12},{5,13},{6,14},{7,15},{16,24},{17,... | collective-permute-start | bytes 786440 | tf_op jit(solution)/shard_map/ppermute | solution.py:17
  12.5 1.9 collective-permute-start.13
  14.5 3.2 %collective-permute-start.12 = (bf16[2,128,512]{1,2,0:T(8,128)(2,1)}, bf16[2,128,512]{1,2,0:T(8,128)(2,1)}, u32[]{:S(2)}, u32[]{:S(2)}) collective-permute-start(bf16[2,128,512]{1,2,0:T(8,128)(2,1)} %pad_maximum_fusion.11), channel_id=1, source_target_pairs={{0,1},{1,2},{2,3},{3,4},{4,5},{5,6},{6,7},{7,8},{8,9},{9,10},{10,1... | collective-permute-start | bytes 786440 | tf_op jit(solution)/shard_map/ppermute | solution.py:17
  18.5 2.0 collective-permute-start.7
  32.3 2.1 collective-permute-start.6
  39.5 4.6 %collective-permute-start.4 = (bf16[2,128,512]{1,2,0:T(8,128)(2,1)}, bf16[2,128,512]{1,2,0:T(8,128)(2,1)S(1)}, u32[]{:S(2)}, u32[]{:S(2)}) collective-permute-start(bf16[2,128,512]{1,2,0:T(8,128)(2,1)} %pad_maximum_fusion.9), channel_id=1, source_target_pairs={{0,1},{1,2},{2,3},{3,4},{4,5},{5,6},{6,7},{7,8},{8,9},{9,10},{10,1... | collective-permute-start | bytes 786440 | tf_op jit(solution)/shard_map/ppermute | solution.py:17
  48.7 2.5 collective-permute-done.7
  54.8 6.3 %collective-permute-done.6 = bf16[2,128,512]{1,2,0:T(8,128)(2,1)S(1)} collective-permute-done((bf16[2,128,512]{1,2,0:T(8,128)(2,1)}, bf16[2,128,512]{1,2,0:T(8,128)(2,1)S(1)}, u32[]{:S(2)}, u32[]{:S(2)}) %collective-permute-start.6) | collective-permute-done | bytes 262176 | tf_op jit(solution)/shard_map/ppermute | solution.py:17
  63.8 3.0 %collective-permute-done.5 = bf16[2,128,512]{1,2,0:T(8,128)(2,1)S(1)} collective-permute-done((bf16[2,128,512]{1,2,0:T(8,128)(2,1)}, bf16[2,128,512]{1,2,0:T(8,128)(2,1)S(1)}, u32[]{:S(2)}, u32[]{:S(2)}) %collective-permute-start.5) | collective-permute-done | bytes 262176 | tf_op jit(solution)/shard_map/ppermute | solution.py:17
  69.4 8.5 %collective-permute-done.4 = bf16[2,128,512]{1,2,0:T(8,128)(2,1)S(1)} collective-permute-done((bf16[2,128,512]{1,2,0:T(8,128)(2,1)}, bf16[2,128,512]{1,2,0:T(8,128)(2,1)S(1)}, u32[]{:S(2)}, u32[]{:S(2)}) %collective-permute-start.4) | collective-permute-done | bytes 262176 | tf_op jit(solution)/shard_map/ppermute | solution.py:17
  79.8 3.7 %collective-permute-done.3 = bf16[2,128,512]{1,2,0:T(8,128)(2,1)S(1)} collective-permute-done((bf16[2,128,512]{1,2,0:T(8,128)(2,1)}, bf16[2,128,512]{1,2,0:T(8,128)(2,1)S(1)}, u32[]{:S(2)}, u32[]{:S(2)}) %collective-permute-start.3) | collective-permute-done | bytes 262176 | tf_op jit(solution)/shard_map/ppermute | solution.py:17
  86.2 3.0 %collective-permute-done.2 = bf16[2,128,512]{1,2,0:T(8,128)(2,1)S(1)} collective-permute-done((bf16[2,128,512]{1,2,0:T(8,128)(2,1)}, bf16[2,128,512]{1,2,0:T(8,128)(2,1)S(1)}, u32[]{:S(2)}, u32[]{:S(2)}) %collective-permute-start.2) | collective-permute-done | bytes 262176 | tf_op jit(solution)/shard_map/ppermute | solution.py:17
  91.8 2.9 collective-permute-done.1
  94.7 2.1 collective-permute-start.8
  97.5 2.8 collective-permute-done
  101.1 2.3 collective-permute-done.11
  104.1 2.1 collective-permute-done.10
  141.2 2.3 fusion.47
  186.8 2.1 collective-permute-start.29
  188.9 2.1 collective-permute-start.30
  192.5 2.1 collective-permute-start.28
  194.6 2.1 collective-permute-start.25
  200.8 2.1 collective-permute-start.26
  202.9 2.1 collective-permute-done.30
  206.5 2.1 collective-permute-start.24
  208.6 5.4 %collective-permute-done.28 = bf16[2,128,4,128]{1,3,2,0:T(8,128)(2,1)S(1)} collective-permute-done((bf16[2,128,4,128]{1,3,2,0:T(8,128)(2,1)S(1)}, bf16[2,128,4,128]{1,3,2,0:T(8,128)(2,1)S(1)}, u32[]{:S(2)}, u32[]{:S(2)}) %collective-permute-start.28) | collective-permute-done | bytes 262176 | tf_op jit(solution)/shard_map/ppermute | solution.py:17
  215.9 4.9 %collective-permute-done.25 = bf16[2,128,4,128]{1,3,2,0:T(8,128)(2,1)S(1)} collective-permute-done((bf16[2,128,4,128]{1,3,2,0:T(8,128)(2,1)S(1)}, bf16[2,128,4,128]{1,3,2,0:T(8,128)(2,1)S(1)}, u32[]{:S(2)}, u32[]{:S(2)}) %collective-permute-start.25) | collective-permute-done | bytes 262176 | tf_op jit(solution)/shard_map/ppermute | solution.py:17
  226.3 21.3 %collective-permute-done.24 = bf16[2,128,4,128]{1,3,2,0:T(8,128)(2,1)S(1)} collective-permute-done((bf16[2,128,4,128]{1,3,2,0:T(8,128)(2,1)S(1)}, bf16[2,128,4,128]{1,3,2,0:T(8,128)(2,1)S(1)}, u32[]{:S(2)}, u32[]{:S(2)}) %collective-permute-start.24) | collective-permute-done | bytes 262176 | tf_op jit(solution)/shard_map/ppermute | solution.py:17
  249.5 1.9 collective-permute-start.22
  252.8 6.4 %collective-permute-start.20 = (bf16[2,128,4,128]{1,3,2,0:T(8,128)(2,1)}, bf16[2,128,4,128]{1,3,2,0:T(8,128)(2,1)}, u32[]{:S(2)}, u32[]{:S(2)}) collective-permute-start(bf16[2,128,4,128]{1,3,2,0:T(8,128)(2,1)} %pad_maximum_fusion.16), channel_id=1, source_target_pairs={{1,0},{2,1},{3,2},{4,3},{5,4},{6,5},{7,6},{8,7},{9,8},{10,9},{11,1... | collective-permute-start | bytes 786440 | tf_op jit(solution)/shard_map/ppermute | solution.py:17
  259.7 16.2 %collective-permute-done.16 = bf16[2,128,4,128]{1,3,2,0:T(8,128)(2,1)} collective-permute-done((bf16[2,128,4,128]{1,3,2,0:T(8,128)(2,1)S(1)}, bf16[2,128,4,128]{1,3,2,0:T(8,128)(2,1)}, u32[]{:S(2)}, u32[]{:S(2)}) %collective-permute-start.16) | collective-permute-done | bytes 262176 | tf_op jit(solution)/shard_map/ppermute | solution.py:17
  277.5 12.8 %collective-permute-done.20 = bf16[2,128,4,128]{1,3,2,0:T(8,128)(2,1)} collective-permute-done((bf16[2,128,4,128]{1,3,2,0:T(8,128)(2,1)}, bf16[2,128,4,128]{1,3,2,0:T(8,128)(2,1)}, u32[]{:S(2)}, u32[]{:S(2)}) %collective-permute-start.20) | collective-permute-done | bytes 262176 | tf_op jit(solution)/shard_map/ppermute | solution.py:17
  (405 shorter events, 148.5 us)
Async XLA Ops:
  5.7 26.5 %collective-permute-start.15 = (bf16[2,128,512]{1,2,0:T(8,128)(2,1)}, bf16[2,128,512]{1,2,0:T(8,128)(2,1)}, u32[]{:S(2)}, u32[]{:S(2)}) collective-permute-start(bf16[2,128,512]{1,2,0:T(8,128)(2,1)} %pad_maximum_fusion.11), channel_id=1, source_target_pairs={{0,8},{1,9},{2,10},{3,11},{4,12},{5,13},{6,14},{7,15},{16,24},{17,... | collective-permute-start | bytes 786440 | tf_op jit(solution)/shard_map/ppermute | solution.py:17
  10.6 25.3 %collective-permute-start.14 = (bf16[2,128,512]{1,2,0:T(8,128)(2,1)}, bf16[2,128,512]{1,2,0:T(8,128)(2,1)}, u32[]{:S(2)}, u32[]{:S(2)}) collective-permute-start(bf16[2,128,512]{1,2,0:T(8,128)(2,1)} %pad_maximum_fusion.11), channel_id=1, source_target_pairs={{0,4},{1,5},{2,6},{3,7},{4,8},{5,9},{6,10},{7,11},{8,12},{9,13},{1... | collective-permute-start | bytes 786440 | tf_op jit(solution)/shard_map/ppermute | solution.py:17
  12.5 27.0 %collective-permute-start.13 = (bf16[2,128,512]{1,2,0:T(8,128)(2,1)}, bf16[2,128,512]{1,2,0:T(8,128)(2,1)}, u32[]{:S(2)}, u32[]{:S(2)}) collective-permute-start(bf16[2,128,512]{1,2,0:T(8,128)(2,1)} %pad_maximum_fusion.11), channel_id=1, source_target_pairs={{0,2},{1,3},{2,4},{3,5},{4,6},{5,7},{6,8},{7,9},{8,10},{9,11},{10,... | collective-permute-start | bytes 786440 | tf_op jit(solution)/shard_map/ppermute | solution.py:17
  14.5 31.3 %collective-permute-start.12 = (bf16[2,128,512]{1,2,0:T(8,128)(2,1)}, bf16[2,128,512]{1,2,0:T(8,128)(2,1)}, u32[]{:S(2)}, u32[]{:S(2)}) collective-permute-start(bf16[2,128,512]{1,2,0:T(8,128)(2,1)} %pad_maximum_fusion.11), channel_id=1, source_target_pairs={{0,1},{1,2},{2,3},{3,4},{4,5},{5,6},{6,7},{7,8},{8,9},{9,10},{10,1... | collective-permute-start | bytes 786440 | tf_op jit(solution)/shard_map/ppermute | solution.py:17
  18.5 32.7 %collective-permute-start.7 = (bf16[2,128,512]{1,2,0:T(8,128)(2,1)}, bf16[2,128,512]{1,2,0:T(8,128)(2,1)}, u32[]{:S(2)}, u32[]{:S(2)}) collective-permute-start(bf16[2,128,512]{1,2,0:T(8,128)(2,1)} %pad_maximum_fusion.9), channel_id=1, source_target_pairs={{0,8},{1,9},{2,10},{3,11},{4,12},{5,13},{6,14},{7,15},{16,24},{17,... | collective-permute-start | bytes 786440 | tf_op jit(solution)/shard_map/ppermute | solution.py:17
  32.3 28.9 %collective-permute-start.6 = (bf16[2,128,512]{1,2,0:T(8,128)(2,1)}, bf16[2,128,512]{1,2,0:T(8,128)(2,1)S(1)}, u32[]{:S(2)}, u32[]{:S(2)}) collective-permute-start(bf16[2,128,512]{1,2,0:T(8,128)(2,1)} %pad_maximum_fusion.9), channel_id=1, source_target_pairs={{0,4},{1,5},{2,6},{3,7},{4,8},{5,9},{6,10},{7,11},{8,12},{9,13},{1... | collective-permute-start | bytes 786440 | tf_op jit(solution)/shard_map/ppermute | solution.py:17
  36.0 30.8 %collective-permute-start.5 = (bf16[2,128,512]{1,2,0:T(8,128)(2,1)}, bf16[2,128,512]{1,2,0:T(8,128)(2,1)S(1)}, u32[]{:S(2)}, u32[]{:S(2)}) collective-permute-start(bf16[2,128,512]{1,2,0:T(8,128)(2,1)} %pad_maximum_fusion.9), channel_id=1, source_target_pairs={{0,2},{1,3},{2,4},{3,5},{4,6},{5,7},{6,8},{7,9},{8,10},{9,11},{10,... | collective-permute-start | bytes 786440 | tf_op jit(solution)/shard_map/ppermute | solution.py:17
  39.5 38.3 %collective-permute-start.4 = (bf16[2,128,512]{1,2,0:T(8,128)(2,1)}, bf16[2,128,512]{1,2,0:T(8,128)(2,1)S(1)}, u32[]{:S(2)}, u32[]{:S(2)}) collective-permute-start(bf16[2,128,512]{1,2,0:T(8,128)(2,1)} %pad_maximum_fusion.9), channel_id=1, source_target_pairs={{0,1},{1,2},{2,3},{3,4},{4,5},{5,6},{6,7},{7,8},{8,9},{9,10},{10,1... | collective-permute-start | bytes 786440 | tf_op jit(solution)/shard_map/ppermute | solution.py:17
  45.8 37.8 %collective-permute-start.3 = (bf16[2,128,512]{1,2,0:T(8,128)(2,1)}, bf16[2,128,512]{1,2,0:T(8,128)(2,1)S(1)}, u32[]{:S(2)}, u32[]{:S(2)}) collective-permute-start(bf16[2,128,512]{1,2,0:T(8,128)(2,1)} %pad_maximum_fusion.8), channel_id=1, source_target_pairs={{0,8},{1,9},{2,10},{3,11},{4,12},{5,13},{6,14},{7,15},{16,24},{17,... | collective-permute-start | bytes 786440 | tf_op jit(solution)/shard_map/ppermute | solution.py:17
  51.2 38.0 %collective-permute-start.2 = (bf16[2,128,512]{1,2,0:T(8,128)(2,1)}, bf16[2,128,512]{1,2,0:T(8,128)(2,1)S(1)}, u32[]{:S(2)}, u32[]{:S(2)}) collective-permute-start(bf16[2,128,512]{1,2,0:T(8,128)(2,1)} %pad_maximum_fusion.8), channel_id=1, source_target_pairs={{0,4},{1,5},{2,6},{3,7},{4,8},{5,9},{6,10},{7,11},{8,12},{9,13},{1... | collective-permute-start | bytes 786440 | tf_op jit(solution)/shard_map/ppermute | solution.py:17
  61.1 33.6 %collective-permute-start.1 = (bf16[2,128,512]{1,2,0:T(8,128)(2,1)S(1)}, bf16[2,128,512]{1,2,0:T(8,128)(2,1)S(1)}, u32[]{:S(2)}, u32[]{:S(2)}) collective-permute-start(bf16[2,128,512]{1,2,0:T(8,128)(2,1)S(1)} %copy-done.80), channel_id=1, source_target_pairs={{0,2},{1,3},{2,4},{3,5},{4,6},{5,7},{6,8},{7,9},{8,10},{9,11},{10,... | collective-permute-start | bytes 786440 | tf_op jit(solution)/shard_map/ppermute | solution.py:17
  66.7 33.6 %collective-permute-start = (bf16[2,128,512]{1,2,0:T(8,128)(2,1)S(1)}, bf16[2,128,512]{1,2,0:T(8,128)(2,1)S(1)}, u32[]{:S(2)}, u32[]{:S(2)}) collective-permute-start(bf16[2,128,512]{1,2,0:T(8,128)(2,1)S(1)} %copy-done.80), channel_id=1, source_target_pairs={{0,1},{1,2},{2,3},{3,4},{4,5},{5,6},{6,7},{7,8},{8,9},{9,10},{10,1... | collective-permute-start | bytes 786440 | tf_op jit(solution)/shard_map/ppermute | solution.py:17
  77.8 25.5 %collective-permute-start.11 = (bf16[2,128,512]{1,2,0:T(8,128)(2,1)}, bf16[2,128,512]{1,2,0:T(8,128)(2,1)S(1)}, u32[]{:S(2)}, u32[]{:S(2)}) collective-permute-start(bf16[2,128,512]{1,2,0:T(8,128)(2,1)} %pad_maximum_fusion.10), channel_id=1, source_target_pairs={{0,8},{1,9},{2,10},{3,11},{4,12},{5,13},{6,14},{7,15},{16,24},{17,... | collective-permute-start | bytes 786440 | tf_op jit(solution)/shard_map/ppermute | solution.py:17
  83.6 22.6 %collective-permute-start.10 = (bf16[2,128,512]{1,2,0:T(8,128)(2,1)}, bf16[2,128,512]{1,2,0:T(8,128)(2,1)S(1)}, u32[]{:S(2)}, u32[]{:S(2)}) collective-permute-start(bf16[2,128,512]{1,2,0:T(8,128)(2,1)} %pad_maximum_fusion.10), channel_id=1, source_target_pairs={{0,4},{1,5},{2,6},{3,7},{4,8},{5,9},{6,10},{7,11},{8,12},{9,13},{1... | collective-permute-start | bytes 786440 | tf_op jit(solution)/shard_map/ppermute | solution.py:17
  89.2 34.2 %collective-permute-start.9 = (bf16[2,128,512]{1,2,0:T(8,128)(2,1)}, bf16[2,128,512]{1,2,0:T(8,128)(2,1)}, u32[]{:S(2)}, u32[]{:S(2)}) collective-permute-start(bf16[2,128,512]{1,2,0:T(8,128)(2,1)} %pad_maximum_fusion.10), channel_id=1, source_target_pairs={{0,2},{1,3},{2,4},{3,5},{4,6},{5,7},{6,8},{7,9},{8,10},{9,11},{10,... | collective-permute-start | bytes 786440 | tf_op jit(solution)/shard_map/ppermute | solution.py:17
  94.7 32.0 %collective-permute-start.8 = (bf16[2,128,512]{1,2,0:T(8,128)(2,1)}, bf16[2,128,512]{1,2,0:T(8,128)(2,1)}, u32[]{:S(2)}, u32[]{:S(2)}) collective-permute-start(bf16[2,128,512]{1,2,0:T(8,128)(2,1)} %pad_maximum_fusion.10), channel_id=1, source_target_pairs={{0,1},{1,2},{2,3},{3,4},{4,5},{5,6},{6,7},{7,8},{8,9},{9,10},{10,1... | collective-permute-start | bytes 786440 | tf_op jit(solution)/shard_map/ppermute | solution.py:17
  186.8 14.0 %collective-permute-start.29 = (bf16[2,128,4,128]{1,3,2,0:T(8,128)(2,1)S(1)}, bf16[2,128,4,128]{1,3,2,0:T(8,128)(2,1)S(1)}, u32[]{:S(2)}, u32[]{:S(2)}) collective-permute-start(bf16[2,128,4,128]{1,3,2,0:T(8,128)(2,1)S(1)} %pad_maximum_fusion.25), channel_id=1, source_target_pairs={{2,0},{3,1},{4,2},{5,3},{6,4},{7,5},{8,6},{9,7},{10,8},{11,9},{12,... | collective-permute-start | bytes 786440 | tf_op jit(solution)/shard_map/ppermute | solution.py:17
  188.9 16.1 %collective-permute-start.30 = (bf16[2,128,4,128]{1,3,2,0:T(8,128)(2,1)S(1)}, bf16[2,128,4,128]{1,3,2,0:T(8,128)(2,1)S(1)}, u32[]{:S(2)}, u32[]{:S(2)}) collective-permute-start(bf16[2,128,4,128]{1,3,2,0:T(8,128)(2,1)S(1)} %pad_maximum_fusion.26), channel_id=1, source_target_pairs={{4,0},{5,1},{6,2},{7,3},{8,4},{9,5},{10,6},{11,7},{12,8},{13,9},{1... | collective-permute-start | bytes 786440 | tf_op jit(solution)/shard_map/ppermute | solution.py:17
  191.0 15.5 %collective-permute-start.31 = (bf16[2,128,4,128]{1,3,2,0:T(8,128)(2,1)S(1)}, bf16[2,128,4,128]{1,3,2,0:T(8,128)(2,1)S(1)}, u32[]{:S(2)}, u32[]{:S(2)}) collective-permute-start(bf16[2,128,4,128]{1,3,2,0:T(8,128)(2,1)S(1)} %pad_maximum_fusion.27), channel_id=1, source_target_pairs={{8,0},{9,1},{10,2},{11,3},{12,4},{13,5},{14,6},{15,7},{24,16},{25,... | collective-permute-start | bytes 786440 | tf_op jit(solution)/shard_map/ppermute | solution.py:17
  192.5 21.5 %collective-permute-start.28 = (bf16[2,128,4,128]{1,3,2,0:T(8,128)(2,1)S(1)}, bf16[2,128,4,128]{1,3,2,0:T(8,128)(2,1)S(1)}, u32[]{:S(2)}, u32[]{:S(2)}) collective-permute-start(bf16[2,128,4,128]{1,3,2,0:T(8,128)(2,1)S(1)} %pad_maximum_fusion.24), channel_id=1, source_target_pairs={{1,0},{2,1},{3,2},{4,3},{5,4},{6,5},{7,6},{8,7},{9,8},{10,9},{11,1... | collective-permute-start | bytes 786440 | tf_op jit(solution)/shard_map/ppermute | solution.py:17
  194.6 26.2 %collective-permute-start.25 = (bf16[2,128,4,128]{1,3,2,0:T(8,128)(2,1)S(1)}, bf16[2,128,4,128]{1,3,2,0:T(8,128)(2,1)S(1)}, u32[]{:S(2)}, u32[]{:S(2)}) collective-permute-start(bf16[2,128,4,128]{1,3,2,0:T(8,128)(2,1)S(1)} %pad_maximum_fusion.21), channel_id=1, source_target_pairs={{2,0},{3,1},{4,2},{5,3},{6,4},{7,5},{8,6},{9,7},{10,8},{11,9},{12,... | collective-permute-start | bytes 786440 | tf_op jit(solution)/shard_map/ppermute | solution.py:17
  200.8 22.0 %collective-permute-start.26 = (bf16[2,128,4,128]{1,3,2,0:T(8,128)(2,1)S(1)}, bf16[2,128,4,128]{1,3,2,0:T(8,128)(2,1)S(1)}, u32[]{:S(2)}, u32[]{:S(2)}) collective-permute-start(bf16[2,128,4,128]{1,3,2,0:T(8,128)(2,1)S(1)} %pad_maximum_fusion.22), channel_id=1, source_target_pairs={{4,0},{5,1},{6,2},{7,3},{8,4},{9,5},{10,6},{11,7},{12,8},{13,9},{1... | collective-permute-start | bytes 786440 | tf_op jit(solution)/shard_map/ppermute | solution.py:17
  205.0 19.2 %collective-permute-start.27 = (bf16[2,128,4,128]{1,3,2,0:T(8,128)(2,1)S(1)}, bf16[2,128,4,128]{1,3,2,0:T(8,128)(2,1)S(1)}, u32[]{:S(2)}, u32[]{:S(2)}) collective-permute-start(bf16[2,128,4,128]{1,3,2,0:T(8,128)(2,1)S(1)} %pad_maximum_fusion.23), channel_id=1, source_target_pairs={{8,0},{9,1},{10,2},{11,3},{12,4},{13,5},{14,6},{15,7},{24,16},{25,... | collective-permute-start | bytes 786440 | tf_op jit(solution)/shard_map/ppermute | solution.py:17
  206.5 41.1 %collective-permute-start.24 = (bf16[2,128,4,128]{1,3,2,0:T(8,128)(2,1)S(1)}, bf16[2,128,4,128]{1,3,2,0:T(8,128)(2,1)S(1)}, u32[]{:S(2)}, u32[]{:S(2)}) collective-permute-start(bf16[2,128,4,128]{1,3,2,0:T(8,128)(2,1)S(1)} %pad_maximum_fusion.20), channel_id=1, source_target_pairs={{1,0},{2,1},{3,2},{4,3},{5,4},{6,5},{7,6},{8,7},{9,8},{10,9},{11,1... | collective-permute-start | bytes 786440 | tf_op jit(solution)/shard_map/ppermute | solution.py:17
  214.0 35.5 %collective-permute-start.17 = (bf16[2,128,4,128]{1,3,2,0:T(8,128)(2,1)S(1)}, bf16[2,128,4,128]{1,3,2,0:T(8,128)(2,1)S(1)}, u32[]{:S(2)}, u32[]{:S(2)}) collective-permute-start(bf16[2,128,4,128]{1,3,2,0:T(8,128)(2,1)S(1)} %pad_maximum_fusion.13), channel_id=1, source_target_pairs={{2,0},{3,1},{4,2},{5,3},{6,4},{7,5},{8,6},{9,7},{10,8},{11,9},{12,... | collective-permute-start | bytes 786440 | tf_op jit(solution)/shard_map/ppermute | solution.py:17
  220.9 30.6 %collective-permute-start.18 = (bf16[2,128,4,128]{1,3,2,0:T(8,128)(2,1)S(1)}, bf16[2,128,4,128]{1,3,2,0:T(8,128)(2,1)S(1)}, u32[]{:S(2)}, u32[]{:S(2)}) collective-permute-start(bf16[2,128,4,128]{1,3,2,0:T(8,128)(2,1)S(1)} %pad_maximum_fusion.14), channel_id=1, source_target_pairs={{4,0},{5,1},{6,2},{7,3},{8,4},{9,5},{10,6},{11,7},{12,8},{13,9},{1... | collective-permute-start | bytes 786440 | tf_op jit(solution)/shard_map/ppermute | solution.py:17
  222.8 30.0 %collective-permute-start.19 = (bf16[2,128,4,128]{1,3,2,0:T(8,128)(2,1)S(1)}, bf16[2,128,4,128]{1,3,2,0:T(8,128)(2,1)S(1)}, u32[]{:S(2)}, u32[]{:S(2)}) collective-permute-start(bf16[2,128,4,128]{1,3,2,0:T(8,128)(2,1)S(1)} %pad_maximum_fusion.15), channel_id=1, source_target_pairs={{8,0},{9,1},{10,2},{11,3},{12,4},{13,5},{14,6},{15,7},{24,16},{25,... | collective-permute-start | bytes 786440 | tf_op jit(solution)/shard_map/ppermute | solution.py:17
  224.1 51.8 %collective-permute-start.16 = (bf16[2,128,4,128]{1,3,2,0:T(8,128)(2,1)S(1)}, bf16[2,128,4,128]{1,3,2,0:T(8,128)(2,1)}, u32[]{:S(2)}, u32[]{:S(2)}) collective-permute-start(bf16[2,128,4,128]{1,3,2,0:T(8,128)(2,1)S(1)} %pad_maximum_fusion.12), channel_id=1, source_target_pairs={{1,0},{2,1},{3,2},{4,3},{5,4},{6,5},{7,6},{8,7},{9,8},{10,9},{11,1... | collective-permute-start | bytes 786440 | tf_op jit(solution)/shard_map/ppermute | solution.py:17
  247.5 29.9 %collective-permute-start.21 = (bf16[2,128,4,128]{1,3,2,0:T(8,128)(2,1)}, bf16[2,128,4,128]{1,3,2,0:T(8,128)(2,1)}, u32[]{:S(2)}, u32[]{:S(2)}) collective-permute-start(bf16[2,128,4,128]{1,3,2,0:T(8,128)(2,1)} %pad_maximum_fusion.17), channel_id=1, source_target_pairs={{2,0},{3,1},{4,2},{5,3},{6,4},{7,5},{8,6},{9,7},{10,8},{11,9},{12,... | collective-permute-start | bytes 786440 | tf_op jit(solution)/shard_map/ppermute | solution.py:17
  249.5 28.0 %collective-permute-start.22 = (bf16[2,128,4,128]{1,3,2,0:T(8,128)(2,1)}, bf16[2,128,4,128]{1,3,2,0:T(8,128)(2,1)}, u32[]{:S(2)}, u32[]{:S(2)}) collective-permute-start(bf16[2,128,4,128]{1,3,2,0:T(8,128)(2,1)} %pad_maximum_fusion.18), channel_id=1, source_target_pairs={{4,0},{5,1},{6,2},{7,3},{8,4},{9,5},{10,6},{11,7},{12,8},{13,9},{1... | collective-permute-start | bytes 786440 | tf_op jit(solution)/shard_map/ppermute | solution.py:17
  251.4 26.1 %collective-permute-start.23 = (bf16[2,128,4,128]{1,3,2,0:T(8,128)(2,1)}, bf16[2,128,4,128]{1,3,2,0:T(8,128)(2,1)}, u32[]{:S(2)}, u32[]{:S(2)}) collective-permute-start(bf16[2,128,4,128]{1,3,2,0:T(8,128)(2,1)} %pad_maximum_fusion.19), channel_id=1, source_target_pairs={{8,0},{9,1},{10,2},{11,3},{12,4},{13,5},{14,6},{15,7},{24,16},{25,... | collective-permute-start | bytes 786440 | tf_op jit(solution)/shard_map/ppermute | solution.py:17
  252.8 37.5 %collective-permute-start.20 = (bf16[2,128,4,128]{1,3,2,0:T(8,128)(2,1)}, bf16[2,128,4,128]{1,3,2,0:T(8,128)(2,1)}, u32[]{:S(2)}, u32[]{:S(2)}) collective-permute-start(bf16[2,128,4,128]{1,3,2,0:T(8,128)(2,1)} %pad_maximum_fusion.16), channel_id=1, source_target_pairs={{1,0},{2,1},{3,2},{4,3},{5,4},{6,5},{7,6},{8,7},{9,8},{10,9},{11,1... | collective-permute-start | bytes 786440 | tf_op jit(solution)/shard_map/ppermute | solution.py:17
  (91 other events, 656.2 us)

commit v2 on v1

--- a/solution.py
+++ b/solution.py
@@ -69,12 +69,15 @@
     return jnp.transpose(allowed, (0, 2, 1, 3))[:, None]
 
 
-def attend_chunk(query_c, key_c, value_c, grad_c, allowed, offsets, heads):
+def send_chunk(key_c, value_c, offsets):
+    pair = jnp.stack([key_c, value_c])
+    return [pair] + [from_behind(pair, "ctx", offset) for offset in offsets]
+
+
+def attend_chunk(query_c, received, grad_c, allowed, offsets, heads):
     scale_factor = 1.0 / math.sqrt(HEAD_DIM)
     rows = query_c.shape[0]
     head_shape = (rows, heads, HEAD_DIM)
-    pair = jnp.stack([key_c, value_c])
-    received = [pair] + [from_behind(pair, "ctx", offset) for offset in offsets]
     key_stack = jnp.stack([moved[0].reshape(head_shape) for moved in received])[None]
     value_stack = jnp.stack([moved[1].reshape(head_shape) for moved in received])[None]
     query_stack = query_c.reshape((1,) + head_shape)
@@ -107,22 +110,22 @@
     value_terms = jnp.einsum(
         "bhtnu,bthd->bnuhd", weights, grad_stack, preferred_element_type=jnp.float32
     )
-    key_accum = rounded(key_terms[0, 0]).astype(jnp.float32)
-    value_accum = rounded(value_terms[0, 0]).astype(jnp.float32)
-    for slot_index, offset in enumerate(offsets, start=1):
-        outgoing = jnp.stack([key_terms[0, slot_index], value_terms[0, slot_index]]).astype(
-            jnp.bfloat16
-        )
-        returned = from_behind(outgoing, "ctx", -offset)
+    own = (rounded(key_terms[0, 0]), rounded(value_terms[0, 0]))
+    outgoing = [
+        jnp.stack([key_terms[0, slot_index], value_terms[0, slot_index]]).astype(jnp.bfloat16)
+        for slot_index in range(1, len(offsets) + 1)
+    ]
+    return output, query_grad, own, outgoing
+
+
+def gather_back(own, outgoing, offsets):
+    key_accum = own[0].astype(jnp.float32)
+    value_accum = own[1].astype(jnp.float32)
+    for parts, offset in zip(outgoing, offsets):
+        returned = from_behind(parts, "ctx", -offset)
         key_accum = key_accum + returned[0].astype(jnp.float32)
         value_accum = value_accum + returned[1].astype(jnp.float32)
-    width = heads * HEAD_DIM
-    return (
-        output.reshape(rows, width),
-        query_grad.reshape(rows, width),
-        key_accum.reshape(rows, width),
-        value_accum.reshape(rows, width),
-    )
+    return key_accum, value_accum
 
 
 def on_device(queries, key_vectors, values, grad_out, file_lengths, reach_table):
@@ -141,18 +144,30 @@
     allowed = score_mask(valid_slots, BLOCK)
     chunk_heads = HEADS // CHUNKS
     chunk_width = chunk_heads * HEAD_DIM
+    columns = [slice(chunk * chunk_width, (chunk + 1) * chunk_width) for chunk in range(CHUNKS)]
     pieces = []
-    for chunk in range(CHUNKS):
-        cols = slice(chunk * chunk_width, (chunk + 1) * chunk_width)
+    pending = []
+    previous = None
+    for chunk, cols in enumerate(columns):
+        key_c, value_c = key_rot[:, cols], values[:, cols]
+        if previous is not None:
+            key_c, value_c, _ = lax.optimization_barrier((key_c, value_c, previous))
+        if len(pending) >= 2:
+            key_c, value_c, _ = lax.optimization_barrier((key_c, value_c, pending[-2]))
+        received = send_chunk(key_c, value_c, offsets)
+        previous = received[1:]
+        output, query_grad, own, outgoing = attend_chunk(
+            query_rot[:, cols], received, grad_out[:, cols], allowed, offsets, chunk_heads
+        )
+        pending.append(outgoing)
+        key_accum_c, value_accum_c = gather_back(own, outgoing, offsets)
+        rows = query_rot.shape[0]
         pieces.append(
-            attend_chunk(
-                query_rot[:, cols],
-                key_rot[:, cols],
-                values[:, cols],
-                grad_out[:, cols],
-                allowed,
-                offsets,
-                chunk_heads,
+            (
+                output.reshape(rows, chunk_width),
+                query_grad.reshape(rows, chunk_width),
+                key_accum_c.reshape(rows, chunk_width),
+                value_accum_c.reshape(rows, chunk_width),
             )
         )
     attended, query_grad, key_accum, value_accum = [

time: 297 us -> 249 us (0.84)
  waiting for transfers between devices: 99.8 us -> 47.2 us
  local copies, waits for them, and re-layouts: 89.2 us -> 62.6 us
  starting transfers between devices: 70.3 us -> 90.5 us
  other arithmetic: 17.7 us -> 27.6 us
    ppermute x32, waiting for transfers between devices: 99.8 us -> 47.2 us  [from_behind(): lax.ppermute(value, axis, [(source, source + steps) for source in range(l...]
    ppermute x32, starting transfers between devices: 70.3 us -> 90.5 us  [from_behind(): lax.ppermute(value, axis, [(source, source + steps) for source in range(l...]
    another operation x24, local copies, waits for them, and re-layouts: 21.3 us -> 3.98 us  [attend_chunk(): jnp.stack([moved[0].reshape(head_shape) for moved in received])[None]]
    unnamed x224 -> x121, local copies, waits for them, and re-layouts: 31.1 us -> 21 us
    slice x12, local copies, waits for them, and re-layouts: 11.5 us -> 19 us  [attend_chunk(): moved[1].reshape(head_shape)]
    another operation x16, other arithmetic: 3.23 us -> 10.2 us  [attend_chunk(): jnp.stack([key_terms[0, slot_index], value_terms[0, slot_index]])]
    another operation x12, other arithmetic: 6.95 us -> 10.2 us
  transfers between devices with their start and end apart: 32 -> 32, of which waited for: 16 -> 8; matrix products, arithmetic and copies ran while one was open for 18% -> 31% of each run, Pallas kernels for 0% -> 0%
where the time goes in v2:
time: 249 us; the launch traced here: 247 us
  starting transfers between devices  90.5 us (36%)
  local copies, waits for them, and re-layouts  62.6 us (25%)
  waiting for transfers between devices  47.2 us (19%)
  other arithmetic  27.6 us (11%)
  matrix products  16.7 us (7%)
  between operations  2.77 us (1%)
    ppermute x32, starting transfers between devices, from_behind(): lax.ppermute(value, axis, [(source, source + steps) for source in range(l...  90.5 us
    ppermute x32, waiting for transfers between devices, from_behind(): lax.ppermute(value, axis, [(source, source + steps) for source in range(l...  47.2 us
    unnamed x121, local copies, waits for them, and re-layouts  21 us
    slice x12, local copies, waits for them, and re-layouts, attend_chunk(): moved[1].reshape(head_shape)  19 us
    another operation x16, other arithmetic, attend_chunk(): jnp.stack([key_terms[0, slot_index], value_terms[0, slot_index]])  10.2 us
    another operation x8, other arithmetic  7.31 us
  transfers between devices with their start and end apart: 32, of which 8 were waited for; matrix products, arithmetic and copies ran while one was open for 31% of the time, Pallas kernels for 0%

profile of v2, /device:TPU:15, one launch (start us, length us, event | category | flops | bytes accessed | tf_op | source)
XLA Modules:
  0.0 247.3 jit_solution(14584190593318265899)
XLA Ops:
  7.3 4.9 %collective-permute-start.3 = (bf16[2,128,512]{1,2,0:T(8,128)(2,1)}, bf16[2,128,512]{1,2,0:T(8,128)(2,1)}, u32[]{:S(2)}, u32[]{:S(2)}) collective-permute-start(bf16[2,128,512]{1,2,0:T(8,128)(2,1)} %pad_maximum_fusion.8), channel_id=1, source_target_pairs={{0,8},{1,9},{2,10},{3,11},{4,12},{5,13},{6,14},{7,15},{16,24},{17,... | collective-permute-start | bytes 786440 | tf_op jit(solution)/shard_map/ppermute | solution.py:17
  14.1 1.9 collective-permute-start.1
  16.0 3.2 %collective-permute-start = (bf16[2,128,512]{1,2,0:T(8,128)(2,1)}, bf16[2,128,512]{1,2,0:T(8,128)(2,1)}, u32[]{:S(2)}, u32[]{:S(2)}) collective-permute-start(bf16[2,128,512]{1,2,0:T(8,128)(2,1)} %pad_maximum_fusion.8), channel_id=1, source_target_pairs={{0,1},{1,2},{2,3},{3,4},{4,5},{5,6},{6,7},{7,8},{8,9},{9,10},{10,1... | collective-permute-start | bytes 786440 | tf_op jit(solution)/shard_map/ppermute | solution.py:17
  26.1 2.9 %collective-permute-done.2 = bf16[2,128,512]{1,2,0:T(8,128)(2,1)} collective-permute-done((bf16[2,128,512]{1,2,0:T(8,128)(2,1)}, bf16[2,128,512]{1,2,0:T(8,128)(2,1)}, u32[]{:S(2)}, u32[]{:S(2)}) %collective-permute-start.2) | collective-permute-done | bytes 262176 | tf_op jit(solution)/shard_map/ppermute | solution.py:17
  29.0 5.6 %collective-permute-done.1 = bf16[2,128,512]{1,2,0:T(8,128)(2,1)} collective-permute-done((bf16[2,128,512]{1,2,0:T(8,128)(2,1)}, bf16[2,128,512]{1,2,0:T(8,128)(2,1)}, u32[]{:S(2)}, u32[]{:S(2)}) %collective-permute-start.1) | collective-permute-done | bytes 262176 | tf_op jit(solution)/shard_map/ppermute | solution.py:17
  34.6 8.7 %collective-permute-done = bf16[2,128,512]{1,2,0:T(8,128)(2,1)} collective-permute-done((bf16[2,128,512]{1,2,0:T(8,128)(2,1)}, bf16[2,128,512]{1,2,0:T(8,128)(2,1)}, u32[]{:S(2)}, u32[]{:S(2)}) %collective-permute-start) | collective-permute-done | bytes 262176 | tf_op jit(solution)/shard_map/ppermute | solution.py:17
  44.1 2.0 collective-permute-start.7
  48.0 1.9 collective-permute-start.5
  49.9 4.7 %collective-permute-start.4 = (bf16[2,128,512]{1,2,0:T(8,128)(2,1)}, bf16[2,128,512]{1,2,0:T(8,128)(2,1)}, u32[]{:S(2)}, u32[]{:S(2)}) collective-permute-start(bf16[2,128,512]{1,2,0:T(8,128)(2,1)} %pad_maximum_fusion.9), channel_id=1, source_target_pairs={{0,1},{1,2},{2,3},{3,4},{4,5},{5,6},{6,7},{7,8},{8,9},{9,10},{10,1... | collective-permute-start | bytes 786440 | tf_op jit(solution)/shard_map/ppermute | solution.py:17
  75.5 2.3 collective-permute-start.16
  79.4 3.2 %collective-permute-start.17 = (bf16[2,128,4,128]{1,3,2,0:T(8,128)(2,1)}, bf16[2,128,4,128]{1,3,2,0:T(8,128)(2,1)}, u32[]{:S(2)}, u32[]{:S(2)}) collective-permute-start(bf16[2,128,4,128]{1,3,2,0:T(8,128)(2,1)} %pad_maximum_fusion.11), channel_id=1, source_target_pairs={{2,0},{3,1},{4,2},{5,3},{6,4},{7,5},{8,6},{9,7},{10,8},{11,9},{12,... | collective-permute-start | bytes 786440 | tf_op jit(solution)/shard_map/ppermute | solution.py:17
  84.6 3.6 %collective-permute-start.18 = (bf16[2,128,4,128]{1,3,2,0:T(8,128)(2,1)}, bf16[2,128,4,128]{1,3,2,0:T(8,128)(2,1)}, u32[]{:S(2)}, u32[]{:S(2)}) collective-permute-start(bf16[2,128,4,128]{1,3,2,0:T(8,128)(2,1)} %pad_maximum_fusion.12), channel_id=1, source_target_pairs={{4,0},{5,1},{6,2},{7,3},{8,4},{9,5},{10,6},{11,7},{12,8},{13,9},{1... | collective-permute-start | bytes 786440 | tf_op jit(solution)/shard_map/ppermute | solution.py:17
  92.1 7.2 %collective-permute-start.11 = (bf16[2,128,512]{1,2,0:T(8,128)(2,1)}, bf16[2,128,512]{1,2,0:T(8,128)(2,1)}, u32[]{:S(2)}, u32[]{:S(2)}) collective-permute-start(bf16[2,128,512]{1,2,0:T(8,128)(2,1)} %pad_maximum_fusion.14), channel_id=1, source_target_pairs={{0,8},{1,9},{2,10},{3,11},{4,12},{5,13},{6,14},{7,15},{16,24},{17,... | collective-permute-start | bytes 786440 | tf_op jit(solution)/shard_map/ppermute | solution.py:17
  101.1 2.1 collective-permute-start.10
  103.2 1.9 collective-permute-start.9
  105.1 3.2 %collective-permute-start.8 = (bf16[2,128,512]{1,2,0:T(8,128)(2,1)}, bf16[2,128,512]{1,2,0:T(8,128)(2,1)}, u32[]{:S(2)}, u32[]{:S(2)}) collective-permute-start(bf16[2,128,512]{1,2,0:T(8,128)(2,1)} %pad_maximum_fusion.14), channel_id=1, source_target_pairs={{0,1},{1,2},{2,3},{3,4},{4,5},{5,6},{6,7},{7,8},{8,9},{9,10},{10,1... | collective-permute-start | bytes 786440 | tf_op jit(solution)/shard_map/ppermute | solution.py:17
  108.4 2.2 fusion.60
  117.1 3.7 %collective-permute-done.9 = bf16[2,128,512]{1,2,0:T(8,128)(2,1)} collective-permute-done((bf16[2,128,512]{1,2,0:T(8,128)(2,1)}, bf16[2,128,512]{1,2,0:T(8,128)(2,1)}, u32[]{:S(2)}, u32[]{:S(2)}) %collective-permute-start.9) | collective-permute-done | bytes 262176 | tf_op jit(solution)/shard_map/ppermute | solution.py:17
  138.2 2.0 collective-permute-start.15
  142.1 3.2 %collective-permute-start.13 = (bf16[2,128,512]{1,2,0:T(8,128)(2,1)}, bf16[2,128,512]{1,2,0:T(8,128)(2,1)}, u32[]{:S(2)}, u32[]{:S(2)}) collective-permute-start(bf16[2,128,512]{1,2,0:T(8,128)(2,1)} %pad_maximum_fusion.19), channel_id=1, source_target_pairs={{0,2},{1,3},{2,4},{3,5},{4,6},{5,7},{6,8},{7,9},{8,10},{9,11},{10,... | collective-permute-start | bytes 786440 | tf_op jit(solution)/shard_map/ppermute | solution.py:17
  145.3 3.3 %collective-permute-start.12 = (bf16[2,128,512]{1,2,0:T(8,128)(2,1)}, bf16[2,128,512]{1,2,0:T(8,128)(2,1)}, u32[]{:S(2)}, u32[]{:S(2)}) collective-permute-start(bf16[2,128,512]{1,2,0:T(8,128)(2,1)} %pad_maximum_fusion.19), channel_id=1, source_target_pairs={{0,1},{1,2},{2,3},{3,4},{4,5},{5,6},{6,7},{7,8},{8,9},{9,10},{10,1... | collective-permute-start | bytes 786440 | tf_op jit(solution)/shard_map/ppermute | solution.py:17
  148.6 2.3 collective-permute-start.20
  162.3 3.3 %collective-permute-start.21 = (bf16[2,128,4,128]{1,3,2,0:T(8,128)(2,1)}, bf16[2,128,4,128]{1,3,2,0:T(8,128)(2,1)}, u32[]{:S(2)}, u32[]{:S(2)}) collective-permute-start(bf16[2,128,4,128]{1,3,2,0:T(8,128)(2,1)} %pad_maximum_fusion.16), channel_id=1, source_target_pairs={{2,0},{3,1},{4,2},{5,3},{6,4},{7,5},{8,6},{9,7},{10,8},{11,9},{12,... | collective-permute-start | bytes 786440 | tf_op jit(solution)/shard_map/ppermute | solution.py:17
  166.5 3.6 %collective-permute-start.22 = (bf16[2,128,4,128]{1,3,2,0:T(8,128)(2,1)}, bf16[2,128,4,128]{1,3,2,0:T(8,128)(2,1)}, u32[]{:S(2)}, u32[]{:S(2)}) collective-permute-start(bf16[2,128,4,128]{1,3,2,0:T(8,128)(2,1)} %pad_maximum_fusion.17), channel_id=1, source_target_pairs={{4,0},{5,1},{6,2},{7,3},{8,4},{9,5},{10,6},{11,7},{12,8},{13,9},{1... | collective-permute-start | bytes 786440 | tf_op jit(solution)/shard_map/ppermute | solution.py:17
  183.1 2.1 collective-permute-start.25
  191.8 2.0 collective-permute-start.26
  195.2 4.0 %collective-permute-start.24 = (bf16[2,128,4,128]{1,3,2,0:T(8,128)(2,1)}, bf16[2,128,4,128]{1,3,2,0:T(8,128)(2,1)}, u32[]{:S(2)}, u32[]{:S(2)}) collective-permute-start(bf16[2,128,4,128]{1,3,2,0:T(8,128)(2,1)} %pad_maximum_fusion.20), channel_id=1, source_target_pairs={{1,0},{2,1},{3,2},{4,3},{5,4},{6,5},{7,6},{8,7},{9,8},{10,9},{11,1... | collective-permute-start | bytes 786440 | tf_op jit(solution)/shard_map/ppermute | solution.py:17
  199.2 1.9 collective-permute-start.29
  204.1 2.0 collective-permute-start.30
  208.2 7.4 %collective-permute-start.28 = (bf16[2,128,4,128]{1,3,2,0:T(8,128)(2,1)S(1)}, bf16[2,128,4,128]{1,3,2,0:T(8,128)(2,1)}, u32[]{:S(2)}, u32[]{:S(2)}) collective-permute-start(bf16[2,128,4,128]{1,3,2,0:T(8,128)(2,1)S(1)} %pad_maximum_fusion.24), channel_id=1, source_target_pairs={{1,0},{2,1},{3,2},{4,3},{5,4},{6,5},{7,6},{8,7},{9,8},{10,9},{11,1... | collective-permute-start | bytes 786440 | tf_op jit(solution)/shard_map/ppermute | solution.py:17
  215.9 8.7 %collective-permute-done.24 = bf16[2,128,4,128]{1,3,2,0:T(8,128)(2,1)} collective-permute-done((bf16[2,128,4,128]{1,3,2,0:T(8,128)(2,1)}, bf16[2,128,4,128]{1,3,2,0:T(8,128)(2,1)}, u32[]{:S(2)}, u32[]{:S(2)}) %collective-permute-start.24) | collective-permute-done | bytes 262176 | tf_op jit(solution)/shard_map/ppermute | solution.py:17
  226.3 16.1 %collective-permute-done.28 = bf16[2,128,4,128]{1,3,2,0:T(8,128)(2,1)} collective-permute-done((bf16[2,128,4,128]{1,3,2,0:T(8,128)(2,1)S(1)}, bf16[2,128,4,128]{1,3,2,0:T(8,128)(2,1)}, u32[]{:S(2)}, u32[]{:S(2)}) %collective-permute-start.28) | collective-permute-done | bytes 262176 | tf_op jit(solution)/shard_map/ppermute | solution.py:17
  (311 shorter events, 117.0 us)
Async XLA Ops:
  7.3 18.8 %collective-permute-start.3 = (bf16[2,128,512]{1,2,0:T(8,128)(2,1)}, bf16[2,128,512]{1,2,0:T(8,128)(2,1)}, u32[]{:S(2)}, u32[]{:S(2)}) collective-permute-start(bf16[2,128,512]{1,2,0:T(8,128)(2,1)} %pad_maximum_fusion.8), channel_id=1, source_target_pairs={{0,8},{1,9},{2,10},{3,11},{4,12},{5,13},{6,14},{7,15},{16,24},{17,... | collective-permute-start | bytes 786440 | tf_op jit(solution)/shard_map/ppermute | solution.py:17
  12.2 16.8 %collective-permute-start.2 = (bf16[2,128,512]{1,2,0:T(8,128)(2,1)}, bf16[2,128,512]{1,2,0:T(8,128)(2,1)}, u32[]{:S(2)}, u32[]{:S(2)}) collective-permute-start(bf16[2,128,512]{1,2,0:T(8,128)(2,1)} %pad_maximum_fusion.8), channel_id=1, source_target_pairs={{0,4},{1,5},{2,6},{3,7},{4,8},{5,9},{6,10},{7,11},{8,12},{9,13},{1... | collective-permute-start | bytes 786440 | tf_op jit(solution)/shard_map/ppermute | solution.py:17
  14.1 20.5 %collective-permute-start.1 = (bf16[2,128,512]{1,2,0:T(8,128)(2,1)}, bf16[2,128,512]{1,2,0:T(8,128)(2,1)}, u32[]{:S(2)}, u32[]{:S(2)}) collective-permute-start(bf16[2,128,512]{1,2,0:T(8,128)(2,1)} %pad_maximum_fusion.8), channel_id=1, source_target_pairs={{0,2},{1,3},{2,4},{3,5},{4,6},{5,7},{6,8},{7,9},{8,10},{9,11},{10,... | collective-permute-start | bytes 786440 | tf_op jit(solution)/shard_map/ppermute | solution.py:17
  16.0 27.3 %collective-permute-start = (bf16[2,128,512]{1,2,0:T(8,128)(2,1)}, bf16[2,128,512]{1,2,0:T(8,128)(2,1)}, u32[]{:S(2)}, u32[]{:S(2)}) collective-permute-start(bf16[2,128,512]{1,2,0:T(8,128)(2,1)} %pad_maximum_fusion.8), channel_id=1, source_target_pairs={{0,1},{1,2},{2,3},{3,4},{4,5},{5,6},{6,7},{7,8},{8,9},{9,10},{10,1... | collective-permute-start | bytes 786440 | tf_op jit(solution)/shard_map/ppermute | solution.py:17
  44.1 31.4 %collective-permute-start.7 = (bf16[2,128,512]{1,2,0:T(8,128)(2,1)}, bf16[2,128,512]{1,2,0:T(8,128)(2,1)}, u32[]{:S(2)}, u32[]{:S(2)}) collective-permute-start(bf16[2,128,512]{1,2,0:T(8,128)(2,1)} %pad_maximum_fusion.9), channel_id=1, source_target_pairs={{0,8},{1,9},{2,10},{3,11},{4,12},{5,13},{6,14},{7,15},{16,24},{17,... | collective-permute-start | bytes 786440 | tf_op jit(solution)/shard_map/ppermute | solution.py:17
  46.1 33.4 %collective-permute-start.6 = (bf16[2,128,512]{1,2,0:T(8,128)(2,1)}, bf16[2,128,512]{1,2,0:T(8,128)(2,1)}, u32[]{:S(2)}, u32[]{:S(2)}) collective-permute-start(bf16[2,128,512]{1,2,0:T(8,128)(2,1)} %pad_maximum_fusion.9), channel_id=1, source_target_pairs={{0,4},{1,5},{2,6},{3,7},{4,8},{5,9},{6,10},{7,11},{8,12},{9,13},{1... | collective-permute-start | bytes 786440 | tf_op jit(solution)/shard_map/ppermute | solution.py:17
  48.0 36.6 %collective-permute-start.5 = (bf16[2,128,512]{1,2,0:T(8,128)(2,1)}, bf16[2,128,512]{1,2,0:T(8,128)(2,1)}, u32[]{:S(2)}, u32[]{:S(2)}) collective-permute-start(bf16[2,128,512]{1,2,0:T(8,128)(2,1)} %pad_maximum_fusion.9), channel_id=1, source_target_pairs={{0,2},{1,3},{2,4},{3,5},{4,6},{5,7},{6,8},{7,9},{8,10},{9,11},{10,... | collective-permute-start | bytes 786440 | tf_op jit(solution)/shard_map/ppermute | solution.py:17
  49.9 40.1 %collective-permute-start.4 = (bf16[2,128,512]{1,2,0:T(8,128)(2,1)}, bf16[2,128,512]{1,2,0:T(8,128)(2,1)}, u32[]{:S(2)}, u32[]{:S(2)}) collective-permute-start(bf16[2,128,512]{1,2,0:T(8,128)(2,1)} %pad_maximum_fusion.9), channel_id=1, source_target_pairs={{0,1},{1,2},{2,3},{3,4},{4,5},{5,6},{6,7},{7,8},{8,9},{9,10},{10,1... | collective-permute-start | bytes 786440 | tf_op jit(solution)/shard_map/ppermute | solution.py:17
  72.0 29.1 %collective-permute-start.19 = (bf16[2,128,4,128]{1,3,2,0:T(8,128)(2,1)}, bf16[2,128,4,128]{1,3,2,0:T(8,128)(2,1)}, u32[]{:S(2)}, u32[]{:S(2)}) collective-permute-start(bf16[2,128,4,128]{1,3,2,0:T(8,128)(2,1)} %pad_maximum_fusion.13), channel_id=1, source_target_pairs={{8,0},{9,1},{10,2},{11,3},{12,4},{13,5},{14,6},{15,7},{24,16},{25,... | collective-permute-start | bytes 786440 | tf_op jit(solution)/shard_map/ppermute | solution.py:17
  75.5 27.6 %collective-permute-start.16 = (bf16[2,128,4,128]{1,3,2,0:T(8,128)(2,1)}, bf16[2,128,4,128]{1,3,2,0:T(8,128)(2,1)}, u32[]{:S(2)}, u32[]{:S(2)}) collective-permute-start(bf16[2,128,4,128]{1,3,2,0:T(8,128)(2,1)} %pad_maximum_fusion.10), channel_id=1, source_target_pairs={{1,0},{2,1},{3,2},{4,3},{5,4},{6,5},{7,6},{8,7},{9,8},{10,9},{11,1... | collective-permute-start | bytes 786440 | tf_op jit(solution)/shard_map/ppermute | solution.py:17
  79.4 25.6 %collective-permute-start.17 = (bf16[2,128,4,128]{1,3,2,0:T(8,128)(2,1)}, bf16[2,128,4,128]{1,3,2,0:T(8,128)(2,1)}, u32[]{:S(2)}, u32[]{:S(2)}) collective-permute-start(bf16[2,128,4,128]{1,3,2,0:T(8,128)(2,1)} %pad_maximum_fusion.11), channel_id=1, source_target_pairs={{2,0},{3,1},{4,2},{5,3},{6,4},{7,5},{8,6},{9,7},{10,8},{11,9},{12,... | collective-permute-start | bytes 786440 | tf_op jit(solution)/shard_map/ppermute | solution.py:17
  84.6 23.7 %collective-permute-start.18 = (bf16[2,128,4,128]{1,3,2,0:T(8,128)(2,1)}, bf16[2,128,4,128]{1,3,2,0:T(8,128)(2,1)}, u32[]{:S(2)}, u32[]{:S(2)}) collective-permute-start(bf16[2,128,4,128]{1,3,2,0:T(8,128)(2,1)} %pad_maximum_fusion.12), channel_id=1, source_target_pairs={{4,0},{5,1},{6,2},{7,3},{8,4},{9,5},{10,6},{11,7},{12,8},{13,9},{1... | collective-permute-start | bytes 786440 | tf_op jit(solution)/shard_map/ppermute | solution.py:17
  92.1 21.3 %collective-permute-start.11 = (bf16[2,128,512]{1,2,0:T(8,128)(2,1)}, bf16[2,128,512]{1,2,0:T(8,128)(2,1)}, u32[]{:S(2)}, u32[]{:S(2)}) collective-permute-start(bf16[2,128,512]{1,2,0:T(8,128)(2,1)} %pad_maximum_fusion.14), channel_id=1, source_target_pairs={{0,8},{1,9},{2,10},{3,11},{4,12},{5,13},{6,14},{7,15},{16,24},{17,... | collective-permute-start | bytes 786440 | tf_op jit(solution)/shard_map/ppermute | solution.py:17
  101.1 14.1 %collective-permute-start.10 = (bf16[2,128,512]{1,2,0:T(8,128)(2,1)}, bf16[2,128,512]{1,2,0:T(8,128)(2,1)}, u32[]{:S(2)}, u32[]{:S(2)}) collective-permute-start(bf16[2,128,512]{1,2,0:T(8,128)(2,1)} %pad_maximum_fusion.14), channel_id=1, source_target_pairs={{0,4},{1,5},{2,6},{3,7},{4,8},{5,9},{6,10},{7,11},{8,12},{9,13},{1... | collective-permute-start | bytes 786440 | tf_op jit(solution)/shard_map/ppermute | solution.py:17
  103.2 17.6 %collective-permute-start.9 = (bf16[2,128,512]{1,2,0:T(8,128)(2,1)}, bf16[2,128,512]{1,2,0:T(8,128)(2,1)}, u32[]{:S(2)}, u32[]{:S(2)}) collective-permute-start(bf16[2,128,512]{1,2,0:T(8,128)(2,1)} %pad_maximum_fusion.14), channel_id=1, source_target_pairs={{0,2},{1,3},{2,4},{3,5},{4,6},{5,7},{6,8},{7,9},{8,10},{9,11},{10,... | collective-permute-start | bytes 786440 | tf_op jit(solution)/shard_map/ppermute | solution.py:17
  105.1 18.6 %collective-permute-start.8 = (bf16[2,128,512]{1,2,0:T(8,128)(2,1)}, bf16[2,128,512]{1,2,0:T(8,128)(2,1)}, u32[]{:S(2)}, u32[]{:S(2)}) collective-permute-start(bf16[2,128,512]{1,2,0:T(8,128)(2,1)} %pad_maximum_fusion.14), channel_id=1, source_target_pairs={{0,1},{1,2},{2,3},{3,4},{4,5},{5,6},{6,7},{7,8},{8,9},{9,10},{10,1... | collective-permute-start | bytes 786440 | tf_op jit(solution)/shard_map/ppermute | solution.py:17
  138.2 24.1 %collective-permute-start.15 = (bf16[2,128,512]{1,2,0:T(8,128)(2,1)}, bf16[2,128,512]{1,2,0:T(8,128)(2,1)}, u32[]{:S(2)}, u32[]{:S(2)}) collective-permute-start(bf16[2,128,512]{1,2,0:T(8,128)(2,1)} %pad_maximum_fusion.19), channel_id=1, source_target_pairs={{0,8},{1,9},{2,10},{3,11},{4,12},{5,13},{6,14},{7,15},{16,24},{17,... | collective-permute-start | bytes 786440 | tf_op jit(solution)/shard_map/ppermute | solution.py:17
  140.2 26.3 %collective-permute-start.14 = (bf16[2,128,512]{1,2,0:T(8,128)(2,1)}, bf16[2,128,512]{1,2,0:T(8,128)(2,1)}, u32[]{:S(2)}, u32[]{:S(2)}) collective-permute-start(bf16[2,128,512]{1,2,0:T(8,128)(2,1)} %pad_maximum_fusion.19), channel_id=1, source_target_pairs={{0,4},{1,5},{2,6},{3,7},{4,8},{5,9},{6,10},{7,11},{8,12},{9,13},{1... | collective-permute-start | bytes 786440 | tf_op jit(solution)/shard_map/ppermute | solution.py:17
  142.1 29.3 %collective-permute-start.13 = (bf16[2,128,512]{1,2,0:T(8,128)(2,1)}, bf16[2,128,512]{1,2,0:T(8,128)(2,1)}, u32[]{:S(2)}, u32[]{:S(2)}) collective-permute-start(bf16[2,128,512]{1,2,0:T(8,128)(2,1)} %pad_maximum_fusion.19), channel_id=1, source_target_pairs={{0,2},{1,3},{2,4},{3,5},{4,6},{5,7},{6,8},{7,9},{8,10},{9,11},{10,... | collective-permute-start | bytes 786440 | tf_op jit(solution)/shard_map/ppermute | solution.py:17
  145.3 28.7 %collective-permute-start.12 = (bf16[2,128,512]{1,2,0:T(8,128)(2,1)}, bf16[2,128,512]{1,2,0:T(8,128)(2,1)}, u32[]{:S(2)}, u32[]{:S(2)}) collective-permute-start(bf16[2,128,512]{1,2,0:T(8,128)(2,1)} %pad_maximum_fusion.19), channel_id=1, source_target_pairs={{0,1},{1,2},{2,3},{3,4},{4,5},{5,6},{6,7},{7,8},{8,9},{9,10},{10,1... | collective-permute-start | bytes 786440 | tf_op jit(solution)/shard_map/ppermute | solution.py:17
  148.6 43.2 %collective-permute-start.20 = (bf16[2,128,4,128]{1,3,2,0:T(8,128)(2,1)}, bf16[2,128,4,128]{1,3,2,0:T(8,128)(2,1)}, u32[]{:S(2)}, u32[]{:S(2)}) collective-permute-start(bf16[2,128,4,128]{1,3,2,0:T(8,128)(2,1)} %pad_maximum_fusion.15), channel_id=1, source_target_pairs={{1,0},{2,1},{3,2},{4,3},{5,4},{6,5},{7,6},{8,7},{9,8},{10,9},{11,1... | collective-permute-start | bytes 786440 | tf_op jit(solution)/shard_map/ppermute | solution.py:17
  162.3 31.6 %collective-permute-start.21 = (bf16[2,128,4,128]{1,3,2,0:T(8,128)(2,1)}, bf16[2,128,4,128]{1,3,2,0:T(8,128)(2,1)}, u32[]{:S(2)}, u32[]{:S(2)}) collective-permute-start(bf16[2,128,4,128]{1,3,2,0:T(8,128)(2,1)} %pad_maximum_fusion.16), channel_id=1, source_target_pairs={{2,0},{3,1},{4,2},{5,3},{6,4},{7,5},{8,6},{9,7},{10,8},{11,9},{12,... | collective-permute-start | bytes 786440 | tf_op jit(solution)/shard_map/ppermute | solution.py:17
  166.5 28.7 %collective-permute-start.22 = (bf16[2,128,4,128]{1,3,2,0:T(8,128)(2,1)}, bf16[2,128,4,128]{1,3,2,0:T(8,128)(2,1)}, u32[]{:S(2)}, u32[]{:S(2)}) collective-permute-start(bf16[2,128,4,128]{1,3,2,0:T(8,128)(2,1)} %pad_maximum_fusion.17), channel_id=1, source_target_pairs={{4,0},{5,1},{6,2},{7,3},{8,4},{9,5},{10,6},{11,7},{12,8},{13,9},{1... | collective-permute-start | bytes 786440 | tf_op jit(solution)/shard_map/ppermute | solution.py:17
  171.5 27.8 %collective-permute-start.23 = (bf16[2,128,4,128]{1,3,2,0:T(8,128)(2,1)}, bf16[2,128,4,128]{1,3,2,0:T(8,128)(2,1)}, u32[]{:S(2)}, u32[]{:S(2)}) collective-permute-start(bf16[2,128,4,128]{1,3,2,0:T(8,128)(2,1)} %pad_maximum_fusion.18), channel_id=1, source_target_pairs={{8,0},{9,1},{10,2},{11,3},{12,4},{13,5},{14,6},{15,7},{24,16},{25,... | collective-permute-start | bytes 786440 | tf_op jit(solution)/shard_map/ppermute | solution.py:17
  183.1 21.0 %collective-permute-start.25 = (bf16[2,128,4,128]{1,3,2,0:T(8,128)(2,1)}, bf16[2,128,4,128]{1,3,2,0:T(8,128)(2,1)}, u32[]{:S(2)}, u32[]{:S(2)}) collective-permute-start(bf16[2,128,4,128]{1,3,2,0:T(8,128)(2,1)} %pad_maximum_fusion.21), channel_id=1, source_target_pairs={{2,0},{3,1},{4,2},{5,3},{6,4},{7,5},{8,6},{9,7},{10,8},{11,9},{12,... | collective-permute-start | bytes 786440 | tf_op jit(solution)/shard_map/ppermute | solution.py:17
  191.8 14.4 %collective-permute-start.26 = (bf16[2,128,4,128]{1,3,2,0:T(8,128)(2,1)}, bf16[2,128,4,128]{1,3,2,0:T(8,128)(2,1)S(1)}, u32[]{:S(2)}, u32[]{:S(2)}) collective-permute-start(bf16[2,128,4,128]{1,3,2,0:T(8,128)(2,1)} %pad_maximum_fusion.22), channel_id=1, source_target_pairs={{4,0},{5,1},{6,2},{7,3},{8,4},{9,5},{10,6},{11,7},{12,8},{13,9},{1... | collective-permute-start | bytes 786440 | tf_op jit(solution)/shard_map/ppermute | solution.py:17
  193.9 13.6 %collective-permute-start.27 = (bf16[2,128,4,128]{1,3,2,0:T(8,128)(2,1)}, bf16[2,128,4,128]{1,3,2,0:T(8,128)(2,1)S(1)}, u32[]{:S(2)}, u32[]{:S(2)}) collective-permute-start(bf16[2,128,4,128]{1,3,2,0:T(8,128)(2,1)} %pad_maximum_fusion.23), channel_id=1, source_target_pairs={{8,0},{9,1},{10,2},{11,3},{12,4},{13,5},{14,6},{15,7},{24,16},{25,... | collective-permute-start | bytes 786440 | tf_op jit(solution)/shard_map/ppermute | solution.py:17
  195.2 29.5 %collective-permute-start.24 = (bf16[2,128,4,128]{1,3,2,0:T(8,128)(2,1)}, bf16[2,128,4,128]{1,3,2,0:T(8,128)(2,1)}, u32[]{:S(2)}, u32[]{:S(2)}) collective-permute-start(bf16[2,128,4,128]{1,3,2,0:T(8,128)(2,1)} %pad_maximum_fusion.20), channel_id=1, source_target_pairs={{1,0},{2,1},{3,2},{4,3},{5,4},{6,5},{7,6},{8,7},{9,8},{10,9},{11,1... | collective-permute-start | bytes 786440 | tf_op jit(solution)/shard_map/ppermute | solution.py:17
  199.2 27.0 %collective-permute-start.29 = (bf16[2,128,4,128]{1,3,2,0:T(8,128)(2,1)S(1)}, bf16[2,128,4,128]{1,3,2,0:T(8,128)(2,1)}, u32[]{:S(2)}, u32[]{:S(2)}) collective-permute-start(bf16[2,128,4,128]{1,3,2,0:T(8,128)(2,1)S(1)} %pad_maximum_fusion.25), channel_id=1, source_target_pairs={{2,0},{3,1},{4,2},{5,3},{6,4},{7,5},{8,6},{9,7},{10,8},{11,9},{12,... | collective-permute-start | bytes 786440 | tf_op jit(solution)/shard_map/ppermute | solution.py:17
  204.1 22.1 %collective-permute-start.30 = (bf16[2,128,4,128]{1,3,2,0:T(8,128)(2,1)}, bf16[2,128,4,128]{1,3,2,0:T(8,128)(2,1)}, u32[]{:S(2)}, u32[]{:S(2)}) collective-permute-start(bf16[2,128,4,128]{1,3,2,0:T(8,128)(2,1)} %pad_maximum_fusion.26), channel_id=1, source_target_pairs={{4,0},{5,1},{6,2},{7,3},{8,4},{9,5},{10,6},{11,7},{12,8},{13,9},{1... | collective-permute-start | bytes 786440 | tf_op jit(solution)/shard_map/ppermute | solution.py:17
  206.2 20.1 %collective-permute-start.31 = (bf16[2,128,4,128]{1,3,2,0:T(8,128)(2,1)}, bf16[2,128,4,128]{1,3,2,0:T(8,128)(2,1)}, u32[]{:S(2)}, u32[]{:S(2)}) collective-permute-start(bf16[2,128,4,128]{1,3,2,0:T(8,128)(2,1)} %pad_maximum_fusion.27), channel_id=1, source_target_pairs={{8,0},{9,1},{10,2},{11,3},{12,4},{13,5},{14,6},{15,7},{24,16},{25,... | collective-permute-start | bytes 786440 | tf_op jit(solution)/shard_map/ppermute | solution.py:17
  208.2 34.2 %collective-permute-start.28 = (bf16[2,128,4,128]{1,3,2,0:T(8,128)(2,1)S(1)}, bf16[2,128,4,128]{1,3,2,0:T(8,128)(2,1)}, u32[]{:S(2)}, u32[]{:S(2)}) collective-permute-start(bf16[2,128,4,128]{1,3,2,0:T(8,128)(2,1)S(1)} %pad_maximum_fusion.24), channel_id=1, source_target_pairs={{1,0},{2,1},{3,2},{4,3},{5,4},{6,5},{7,6},{8,7},{9,8},{10,9},{11,1... | collective-permute-start | bytes 786440 | tf_op jit(solution)/shard_map/ppermute | solution.py:17
  (41 other events, 348.0 us)

commit v3 on v2

--- a/solution.py
+++ b/solution.py
@@ -8,7 +8,7 @@
 HEADS = 16
 HEAD_DIM = 128
 BLOCK = 128
-CHUNKS = 4
+CHUNKS = 1
 
 
 def from_behind(value, axis, steps):

time: 249 us -> 251 us (level)
  waiting for transfers between devices: 47.2 us -> 170 us
  starting transfers between devices: 90.5 us -> 18.9 us
  local copies, waits for them, and re-layouts: 62.6 us -> 34.4 us
  other arithmetic: 27.6 us -> 14.4 us
  matrix products: 16.7 us -> 10.3 us
    ppermute x32 -> x8, waiting for transfers between devices: 47.2 us -> 170 us  [from_behind(): lax.ppermute(value, axis, [(source, source + steps) for source in range(l...]
    ppermute x32 -> x8, starting transfers between devices: 90.5 us -> 18.9 us  [from_behind(): lax.ppermute(value, axis, [(source, source + steps) for source in range(l...]
    slice x16 -> x0, local copies, waits for them, and re-layouts: 22.4 us -> none  [the longest x12 19 us: attend_chunk(): moved[1].reshape(head_shape)]
    unnamed x121 -> x50, local copies, waits for them, and re-layouts: 21 us -> 14.1 us
    another operation x8 -> x4, other arithmetic: 7.31 us -> 0.79 us
    another operation x16 -> x4, other arithmetic: 10.2 us -> 4.24 us  [attend_chunk(): jnp.stack([key_terms[0, slot_index], value_terms[0, slot_index]])]
    slice x4, local copies, waits for them, and re-layouts: 3.95 us -> 8.47 us  [attend_chunk(): moved[0].reshape(head_shape)]
    convert_element_type x0 -> x1, other arithmetic: none -> 2.99 us  [on_device(): grad_values = value_accum.astype(jnp.bfloat16)]
  transfers between devices with their start and end apart: 32 -> 8, of which waited for: 8 -> 7; matrix products, arithmetic and copies ran while one was open for 31% -> 9% of each run, Pallas kernels for 0% -> 0%
where the time goes in v3:
time: 251 us; the launch traced here: 250 us
  waiting for transfers between devices  170 us (68%)
  local copies, waits for them, and re-layouts  34.4 us (14%)
  starting transfers between devices  18.9 us (8%)
  other arithmetic  14.4 us (6%)
  matrix products  10.3 us (4%)
    ppermute x8, waiting for transfers between devices, from_behind(): lax.ppermute(value, axis, [(source, source + steps) for source in range(l...  170 us
    ppermute x8, starting transfers between devices, from_behind(): lax.ppermute(value, axis, [(source, source + steps) for source in range(l...  18.9 us
    unnamed x50, local copies, waits for them, and re-layouts  14.1 us
    slice x4, local copies, waits for them, and re-layouts, attend_chunk(): moved[0].reshape(head_shape)  8.47 us
    another operation x6, local copies, waits for them, and re-layouts, attend_chunk(): jnp.stack([moved[0].reshape(head_shape) for moved in received])[None]  6.25 us
  transfers between devices with their start and end apart: 8, of which 7 were waited for; matrix products, arithmetic and copies ran while one was open for 9% of the time, Pallas kernels for 0%

profile of v3, /device:TPU:15, one launch (start us, length us, event | category | flops | bytes accessed | tf_op | source)
XLA Modules:
  0.0 250.2 jit_solution(287888169968929218)
XLA Ops:
  2.5 1.3 copy.60
  3.8 1.2 copy.64
  7.7 5.2 %collective-permute-start.3 = (bf16[2,128,2048]{1,2,0:T(8,128)(2,1)}, bf16[2,128,2048]{1,2,0:T(8,128)(2,1)}, u32[]{:S(2)}, u32[]{:S(2)}) collective-permute-start(bf16[2,128,2048]{1,2,0:T(8,128)(2,1)} %pad_maximum_fusion), channel_id=1, source_target_pairs={{0,8},{1,9},{2,10},{3,11},{4,12},{5,13},{6,14},{7,15},{16,24},{17,... | collective-permute-start | bytes 3145736 | tf_op jit(solution)/shard_map/ppermute | solution.py:17
  13.0 1.9 collective-permute-start.2
  14.9 1.9 collective-permute-start.1
  16.8 2.8 %collective-permute-start = (bf16[2,128,2048]{1,2,0:T(8,128)(2,1)}, bf16[2,128,2048]{1,2,0:T(8,128)(2,1)}, u32[]{:S(2)}, u32[]{:S(2)}) collective-permute-start(bf16[2,128,2048]{1,2,0:T(8,128)(2,1)} %pad_maximum_fusion), channel_id=1, source_target_pairs={{0,1},{1,2},{2,3},{3,4},{4,5},{5,6},{6,7},{7,8},{8,9},{9,10},{10,1... | collective-permute-start | bytes 3145736 | tf_op jit(solution)/shard_map/ppermute | solution.py:17
  20.3 1.2 copy.74
  25.6 31.9 %collective-permute-done.3 = bf16[2,128,2048]{1,2,0:T(8,128)(2,1)} collective-permute-done((bf16[2,128,2048]{1,2,0:T(8,128)(2,1)}, bf16[2,128,2048]{1,2,0:T(8,128)(2,1)}, u32[]{:S(2)}, u32[]{:S(2)}) %collective-permute-start.3) | collective-permute-done | bytes 1048608 | tf_op jit(solution)/shard_map/ppermute | solution.py:17
  57.5 2.1 fusion.21
  60.6 19.3 %collective-permute-done.2 = bf16[2,128,2048]{1,2,0:T(8,128)(2,1)} collective-permute-done((bf16[2,128,2048]{1,2,0:T(8,128)(2,1)}, bf16[2,128,2048]{1,2,0:T(8,128)(2,1)}, u32[]{:S(2)}, u32[]{:S(2)}) %collective-permute-start.2) | collective-permute-done | bytes 1048608 | tf_op jit(solution)/shard_map/ppermute | solution.py:17
  80.0 2.1 fusion.22
  83.1 19.4 %collective-permute-done.1 = bf16[2,128,2048]{1,2,0:T(8,128)(2,1)} collective-permute-done((bf16[2,128,2048]{1,2,0:T(8,128)(2,1)}, bf16[2,128,2048]{1,2,0:T(8,128)(2,1)}, u32[]{:S(2)}, u32[]{:S(2)}) %collective-permute-start.1) | collective-permute-done | bytes 1048608 | tf_op jit(solution)/shard_map/ppermute | solution.py:17
  102.5 2.1 fusion.23
  105.5 8.3 %collective-permute-done = bf16[2,128,2048]{1,2,0:T(8,128)(2,1)} collective-permute-done((bf16[2,128,2048]{1,2,0:T(8,128)(2,1)}, bf16[2,128,2048]{1,2,0:T(8,128)(2,1)}, u32[]{:S(2)}, u32[]{:S(2)}) %collective-permute-start) | collective-permute-done | bytes 1048608 | tf_op jit(solution)/shard_map/ppermute | solution.py:17
  113.8 2.2 fusion.24
  116.0 2.1 copy.66
  118.1 1.2 constant_dynamic-update-slice_fusion.8
  119.3 1.1 constant_dynamic-update-slice_fusion.7
  120.4 1.1 constant_dynamic-update-slice_fusion.6
  123.2 1.1 exponential_reduce_fusion
  124.4 1.2 fusion.4
  129.6 2.5 fusion.5
  133.7 1.3 convert_bitcast_fusion.1
  137.2 1.9 collective-permute-start.5
  140.1 1.9 collective-permute-start.6
  143.1 1.3 collective-permute-start.7
  145.4 1.9 collective-permute-start.4
  148.4 3.8 %convolution_bitcast_fusion = f32[128,16,128]{0,2,1:T(8,128)} fusion(bf16[5,128,16,128]{3,1,0,2:T(8,128)(2,1)S(1)} %constant_dynamic-update-slice_fusion.5, bf16[1,16,128,5,128]{2,4,3,1,0:T(8,128)(2,1)} %copy-done), kind=kOutput, calls=%fused_computation.16 | convolution fusion | flops 335544320 | bytes 6291456 | tf_op jit(solution)/shard_map/bhtnu,bnuhd->bthd/dot_general | solution.py:104
  152.2 11.9 %collective-permute-done.5 = bf16[2,128,16,128]{1,3,2,0:T(8,128)(2,1)} collective-permute-done((bf16[2,128,16,128]{1,3,2,0:T(8,128)(2,1)}, bf16[2,128,16,128]{1,3,2,0:T(8,128)(2,1)}, u32[]{:S(2)}, u32[]{:S(2)}) %collective-permute-start.5) | collective-permute-done | bytes 1048608 | tf_op jit(solution)/shard_map/ppermute | solution.py:17
  164.1 23.1 %collective-permute-done.6 = bf16[2,128,16,128]{1,3,2,0:T(8,128)(2,1)} collective-permute-done((bf16[2,128,16,128]{1,3,2,0:T(8,128)(2,1)}, bf16[2,128,16,128]{1,3,2,0:T(8,128)(2,1)}, u32[]{:S(2)}, u32[]{:S(2)}) %collective-permute-start.6) | collective-permute-done | bytes 1048608 | tf_op jit(solution)/shard_map/ppermute | solution.py:17
  187.2 56.6 %collective-permute-done.4 = bf16[2,128,16,128]{1,3,2,0:T(8,128)(2,1)} collective-permute-done((bf16[2,128,16,128]{1,3,2,0:T(8,128)(2,1)}, bf16[2,128,16,128]{1,3,2,0:T(8,128)(2,1)}, u32[]{:S(2)}, u32[]{:S(2)}) %collective-permute-start.4) | collective-permute-done | bytes 1048608 | tf_op jit(solution)/shard_map/ppermute | solution.py:17
  243.8 3.0 %fusion.16 = (bf16[128,16,128]{0,2,1:T(8,128)(2,1)S(1)}, f32[128,16,128]{0,2,1:T(8,128)S(1)}) fusion(bf16[128,16,128]{0,2,1:T(8,128)(2,1)S(1)} %copy-done.13, bf16[2,128,16,128]{1,3,2,0:T(8,128)(2,1)} %collective-permute-done.7, bf16[2,128,16,128]{1,3,2,0:T(8,128)(2,1)} %collective-permute-done.6, bf16[2,128,16,128]{1,3,2,0:T(8,128)(2,1)} %collective-permute-done.5, ...), kind=kLoop, calls=%fused_computation.26 | loop fusion | flops 4980736 | bytes 6815744 | tf_op jit(solution)/shard_map/convert_element_type | solution.py:178
  (86 shorter events, 28.6 us)
Async XLA Ops:
  0.6 4.4 %copy-start.15 = (bf16[128,2048]{1,0:T(8,128)(2,1)S(1)}, bf16[128,2048]{1,0:T(8,128)(2,1)}, u32[]{:S(2)}) copy-start(bf16[128,2048]{1,0:T(8,128)(2,1)} %param.8) | copy-start | bytes 1572868
  5.7 14.6 %copy-start.1 = (bf16[128,2048]{1,0:T(8,128)(2,1)S(1)}, bf16[128,2048]{1,0:T(8,128)(2,1)}, u32[]{:S(2)}) copy-start(bf16[128,2048]{1,0:T(8,128)(2,1)} %param.10) | copy-start | bytes 1572868
  6.6 16.8 %copy-start.17 = (s32[4]{0:T(128)S(1)}, s32[4]{0:T(128)}, u32[]{:S(2)}) copy-start(s32[4]{0:T(128)} %constant.35) | copy-start | bytes 52
  7.7 49.8 %collective-permute-start.3 = (bf16[2,128,2048]{1,2,0:T(8,128)(2,1)}, bf16[2,128,2048]{1,2,0:T(8,128)(2,1)}, u32[]{:S(2)}, u32[]{:S(2)}) collective-permute-start(bf16[2,128,2048]{1,2,0:T(8,128)(2,1)} %pad_maximum_fusion), channel_id=1, source_target_pairs={{0,8},{1,9},{2,10},{3,11},{4,12},{5,13},{6,14},{7,15},{16,24},{17,... | collective-permute-start | bytes 3145736 | tf_op jit(solution)/shard_map/ppermute | solution.py:17
  13.0 67.0 %collective-permute-start.2 = (bf16[2,128,2048]{1,2,0:T(8,128)(2,1)}, bf16[2,128,2048]{1,2,0:T(8,128)(2,1)}, u32[]{:S(2)}, u32[]{:S(2)}) collective-permute-start(bf16[2,128,2048]{1,2,0:T(8,128)(2,1)} %pad_maximum_fusion), channel_id=1, source_target_pairs={{0,4},{1,5},{2,6},{3,7},{4,8},{5,9},{6,10},{7,11},{8,12},{9,13},{1... | collective-permute-start | bytes 3145736 | tf_op jit(solution)/shard_map/ppermute | solution.py:17
  14.9 87.6 %collective-permute-start.1 = (bf16[2,128,2048]{1,2,0:T(8,128)(2,1)}, bf16[2,128,2048]{1,2,0:T(8,128)(2,1)}, u32[]{:S(2)}, u32[]{:S(2)}) collective-permute-start(bf16[2,128,2048]{1,2,0:T(8,128)(2,1)} %pad_maximum_fusion), channel_id=1, source_target_pairs={{0,2},{1,3},{2,4},{3,5},{4,6},{5,7},{6,8},{7,9},{8,10},{9,11},{10,... | collective-permute-start | bytes 3145736 | tf_op jit(solution)/shard_map/ppermute | solution.py:17
  16.8 97.0 %collective-permute-start = (bf16[2,128,2048]{1,2,0:T(8,128)(2,1)}, bf16[2,128,2048]{1,2,0:T(8,128)(2,1)}, u32[]{:S(2)}, u32[]{:S(2)}) collective-permute-start(bf16[2,128,2048]{1,2,0:T(8,128)(2,1)} %pad_maximum_fusion), channel_id=1, source_target_pairs={{0,1},{1,2},{2,3},{3,4},{4,5},{5,6},{6,7},{7,8},{8,9},{9,10},{10,1... | collective-permute-start | bytes 3145736 | tf_op jit(solution)/shard_map/ppermute | solution.py:17
  116.0 5.6 %copy-start.3 = (bf16[128,16,128]{0,2,1:T(8,128)(2,1)S(1)}, bf16[128,16,128]{0,2,1:T(8,128)(2,1)}, u32[]{:S(2)}) copy-start(bf16[128,16,128]{0,2,1:T(8,128)(2,1)} %get-tuple-element.51) | copy-start | bytes 1572868
  118.1 3.5 %copy-start.8 = (bf16[1,128,16,128]{3,1,0,2:T(8,128)(2,1)S(1)}, bf16[1,128,16,128]{3,1,0,2:T(8,128)(2,1)}, u32[]{:S(2)}) copy-start(bf16[1,128,16,128]{3,1,0,2:T(8,128)(2,1)} %copy.69) | copy-start | bytes 1572868
  124.3 1.2 copy-start.2
  125.6 1.7 copy-start.7
  125.6 1.8 copy-start.12
  125.6 2.0 copy-start.11
  125.6 2.1 copy-start.10
  126.7 1.4 copy-start.9
  128.2 1.2 copy-start.5
  128.2 1.4 copy-start.16
  132.1 1.7 copy-start
  132.1 1.7 copy-start.4
  137.2 26.9 %collective-permute-start.5 = (bf16[2,128,16,128]{1,3,2,0:T(8,128)(2,1)}, bf16[2,128,16,128]{1,3,2,0:T(8,128)(2,1)}, u32[]{:S(2)}, u32[]{:S(2)}) collective-permute-start(bf16[2,128,16,128]{1,3,2,0:T(8,128)(2,1)} %pad_maximum_fusion.2), channel_id=1, source_target_pairs={{2,0},{3,1},{4,2},{5,3},{6,4},{7,5},{8,6},{9,7},{10,8},{11,9},{12,... | collective-permute-start | bytes 3145736 | tf_op jit(solution)/shard_map/ppermute | solution.py:17
  140.1 47.0 %collective-permute-start.6 = (bf16[2,128,16,128]{1,3,2,0:T(8,128)(2,1)}, bf16[2,128,16,128]{1,3,2,0:T(8,128)(2,1)}, u32[]{:S(2)}, u32[]{:S(2)}) collective-permute-start(bf16[2,128,16,128]{1,3,2,0:T(8,128)(2,1)} %pad_maximum_fusion.3), channel_id=1, source_target_pairs={{4,0},{5,1},{6,2},{7,3},{8,4},{9,5},{10,6},{11,7},{12,8},{13,9},{1... | collective-permute-start | bytes 3145736 | tf_op jit(solution)/shard_map/ppermute | solution.py:17
  143.1 44.0 %collective-permute-start.7 = (bf16[2,128,16,128]{1,3,2,0:T(8,128)(2,1)}, bf16[2,128,16,128]{1,3,2,0:T(8,128)(2,1)}, u32[]{:S(2)}, u32[]{:S(2)}) collective-permute-start(bf16[2,128,16,128]{1,3,2,0:T(8,128)(2,1)} %pad_maximum_fusion.4), channel_id=1, source_target_pairs={{8,0},{9,1},{10,2},{11,3},{12,4},{13,5},{14,6},{15,7},{24,16},{25,... | collective-permute-start | bytes 3145736 | tf_op jit(solution)/shard_map/ppermute | solution.py:17
  145.4 98.3 %collective-permute-start.4 = (bf16[2,128,16,128]{1,3,2,0:T(8,128)(2,1)}, bf16[2,128,16,128]{1,3,2,0:T(8,128)(2,1)}, u32[]{:S(2)}, u32[]{:S(2)}) collective-permute-start(bf16[2,128,16,128]{1,3,2,0:T(8,128)(2,1)} %pad_maximum_fusion.1), channel_id=1, source_target_pairs={{1,0},{2,1},{3,2},{4,3},{5,4},{6,5},{7,6},{8,7},{9,8},{10,9},{11,1... | collective-permute-start | bytes 3145736 | tf_op jit(solution)/shard_map/ppermute | solution.py:17
  148.4 95.4 %copy-start.13 = (bf16[128,16,128]{0,2,1:T(8,128)(2,1)S(1)}, bf16[128,16,128]{0,2,1:T(8,128)(2,1)}, u32[]{:S(2)}) copy-start(bf16[128,16,128]{0,2,1:T(8,128)(2,1)} %get-tuple-element.18) | copy-start | bytes 1572868
  148.4 95.4 %copy-start.14 = (bf16[128,16,128]{0,2,1:T(8,128)(2,1)S(1)}, bf16[128,16,128]{0,2,1:T(8,128)(2,1)}, u32[]{:S(2)}) copy-start(bf16[128,16,128]{0,2,1:T(8,128)(2,1)} %get-tuple-element.27) | copy-start | bytes 1572868
  152.2 95.6 %copy-start.6 = (f32[128,16,128]{0,2,1:T(8,128)S(1)}, f32[128,16,128]{0,2,1:T(8,128)}, u32[]{:S(2)}) copy-start(f32[128,16,128]{0,2,1:T(8,128)} %convolution_bitcast_fusion) | copy-start | bytes 3145732

commit v4 on v3

--- a/solution.py
+++ b/solution.py
@@ -71,7 +71,14 @@
 
 def send_chunk(key_c, value_c, offsets):
     pair = jnp.stack([key_c, value_c])
-    return [pair] + [from_behind(pair, "ctx", offset) for offset in offsets]
+    received = {0: pair}
+    for offset in offsets:
+        if (offset.bit_length() - 1) % 2 == 1:
+            half = offset // 2
+            received[offset] = from_behind(received[half], "ctx", half)
+        else:
+            received[offset] = from_behind(pair, "ctx", offset)
+    return [received[0]] + [received[offset] for offset in offsets]
 
 
 def attend_chunk(query_c, received, grad_c, allowed, offsets, heads):

time: 251 us -> 216 us (0.86)
  waiting for transfers between devices: 170 us -> 126 us
  starting transfers between devices: 18.9 us -> 25.8 us
    ppermute x8, waiting for transfers between devices: 170 us -> 126 us  [from_behind(): lax.ppermute(value, axis, [(source, source + steps) for source in range(l...]
    ppermute x8, starting transfers between devices: 18.9 us -> 25.8 us  [from_behind(): lax.ppermute(value, axis, [(source, source + steps) for source in range(l...]
    unnamed x50 -> x46, local copies, waits for them, and re-layouts: 14.1 us -> 14.6 us
  transfers between devices with their start and end apart: 8 -> 8, of which waited for: 7 -> 8; matrix products, arithmetic and copies ran while one was open for 9% -> 12% of each run, Pallas kernels for 0% -> 0%
where the time goes in v4:
time: 216 us; the launch traced here: 215 us
  waiting for transfers between devices  126 us (58%)
  local copies, waits for them, and re-layouts  36.4 us (17%)
  starting transfers between devices  25.8 us (12%)
  other arithmetic  14.5 us (7%)
  matrix products  10.1 us (5%)
    ppermute x8, waiting for transfers between devices, from_behind(): lax.ppermute(value, axis, [(source, source + steps) for source in range(l...  126 us
    ppermute x8, starting transfers between devices, from_behind(): lax.ppermute(value, axis, [(source, source + steps) for source in range(l...  25.8 us
    unnamed x46, local copies, waits for them, and re-layouts  14.6 us
    slice x4, local copies, waits for them, and re-layouts, attend_chunk(): moved[0].reshape(head_shape)  8.61 us
    another operation x6, local copies, waits for them, and re-layouts, attend_chunk(): jnp.stack([moved[0].reshape(head_shape) for moved in received])[None]  7.65 us
  transfers between devices with their start and end apart: 8, of which 8 were waited for; matrix products, arithmetic and copies ran while one was open for 12% of the time, Pallas kernels for 0%

profile of v4, /device:TPU:15, one launch (start us, length us, event | category | flops | bytes accessed | tf_op | source)
XLA Modules:
  0.0 214.8 jit_solution(16716763801962700838)
XLA Ops:
  2.5 1.3 copy.60
  3.8 1.2 copy.64
  7.7 3.2 %collective-permute-start.2 = (bf16[2,128,2048]{1,2,0:T(8,128)(2,1)}, bf16[2,128,2048]{1,2,0:T(8,128)(2,1)}, u32[]{:S(2)}, u32[]{:S(2)}) collective-permute-start(bf16[2,128,2048]{1,2,0:T(8,128)(2,1)} %pad_maximum_fusion), channel_id=1, source_target_pairs={{0,4},{1,5},{2,6},{3,7},{4,8},{5,9},{6,10},{7,11},{8,12},{9,13},{1... | collective-permute-start | bytes 3145736 | tf_op jit(solution)/shard_map/ppermute | solution.py:17
  10.9 4.0 %collective-permute-start = (bf16[2,128,2048]{1,2,0:T(8,128)(2,1)}, bf16[2,128,2048]{1,2,0:T(8,128)(2,1)}, u32[]{:S(2)}, u32[]{:S(2)}) collective-permute-start(bf16[2,128,2048]{1,2,0:T(8,128)(2,1)} %pad_maximum_fusion), channel_id=1, source_target_pairs={{0,1},{1,2},{2,3},{3,4},{4,5},{5,6},{6,7},{7,8},{8,9},{9,10},{10,1... | collective-permute-start | bytes 3145736 | tf_op jit(solution)/shard_map/ppermute | solution.py:17
  15.6 1.2 copy.74
  20.9 13.0 %collective-permute-done.2 = bf16[2,128,2048]{1,2,0:T(8,128)(2,1)} collective-permute-done((bf16[2,128,2048]{1,2,0:T(8,128)(2,1)}, bf16[2,128,2048]{1,2,0:T(8,128)(2,1)}, u32[]{:S(2)}, u32[]{:S(2)}) %collective-permute-start.2) | collective-permute-done | bytes 1048608 | tf_op jit(solution)/shard_map/ppermute | solution.py:17
  33.9 3.2 %collective-permute-start.3 = (bf16[2,128,2048]{1,2,0:T(8,128)(2,1)}, bf16[2,128,2048]{1,2,0:T(8,128)(2,1)}, u32[]{:S(2)}, u32[]{:S(2)}) collective-permute-start(bf16[2,128,2048]{1,2,0:T(8,128)(2,1)} %collective-permute-done.2), channel_id=1, source_target_pairs={{0,4},{1,5},{2,6},{3,7},{4,8},{5,9},{6,10},{7,11},{8,12},{9,13},{1... | collective-permute-start | bytes 3145736 | tf_op jit(solution)/shard_map/ppermute | solution.py:17
  37.1 2.1 fusion.22
  40.3 9.4 %collective-permute-done = bf16[2,128,2048]{1,2,0:T(8,128)(2,1)} collective-permute-done((bf16[2,128,2048]{1,2,0:T(8,128)(2,1)}, bf16[2,128,2048]{1,2,0:T(8,128)(2,1)}, u32[]{:S(2)}, u32[]{:S(2)}) %collective-permute-start) | collective-permute-done | bytes 1048608 | tf_op jit(solution)/shard_map/ppermute | solution.py:17
  49.7 5.5 %collective-permute-start.1 = (bf16[2,128,2048]{1,2,0:T(8,128)(2,1)}, bf16[2,128,2048]{1,2,0:T(8,128)(2,1)}, u32[]{:S(2)}, u32[]{:S(2)}) collective-permute-start(bf16[2,128,2048]{1,2,0:T(8,128)(2,1)} %collective-permute-done), channel_id=1, source_target_pairs={{0,1},{1,2},{2,3},{3,4},{4,5},{5,6},{6,7},{7,8},{8,9},{9,10},{10,1... | collective-permute-start | bytes 3145736 | tf_op jit(solution)/shard_map/ppermute | solution.py:17
  55.2 2.2 %fusion.24 = (bf16[1,128,2048]{1,2,0:T(8,128)(2,1)}, bf16[1,128,2048]{1,2,0:T(8,128)(2,1)}) fusion(bf16[2,128,2048]{1,2,0:T(8,128)(2,1)} %collective-permute-done), kind=kLoop, calls=%fused_computation.95 | loop fusion | bytes 2097152 | tf_op jit(solution)/shard_map/slice | solution.py:88
  57.4 1.3 copy.66
  58.8 2.0 constant_dynamic-update-slice_fusion.3
  60.7 7.8 %collective-permute-done.3 = bf16[2,128,2048]{1,2,0:T(8,128)(2,1)} collective-permute-done((bf16[2,128,2048]{1,2,0:T(8,128)(2,1)}, bf16[2,128,2048]{1,2,0:T(8,128)(2,1)}, u32[]{:S(2)}, u32[]{:S(2)}) %collective-permute-start.3) | collective-permute-done | bytes 1048608 | tf_op jit(solution)/shard_map/ppermute | solution.py:17
  68.5 2.1 fusion.21
  71.6 7.5 %collective-permute-done.1 = bf16[2,128,2048]{1,2,0:T(8,128)(2,1)} collective-permute-done((bf16[2,128,2048]{1,2,0:T(8,128)(2,1)}, bf16[2,128,2048]{1,2,0:T(8,128)(2,1)}, u32[]{:S(2)}, u32[]{:S(2)}) %collective-permute-start.1) | collective-permute-done | bytes 1048608 | tf_op jit(solution)/shard_map/ppermute | solution.py:17
  79.1 2.2 %fusion.23 = (bf16[1,128,2048]{1,2,0:T(8,128)(2,1)}, bf16[1,128,2048]{1,2,0:T(8,128)(2,1)}) fusion(bf16[2,128,2048]{1,2,0:T(8,128)(2,1)} %collective-permute-done.1), kind=kLoop, calls=%fused_computation.94 | loop fusion | bytes 2097152 | tf_op jit(solution)/shard_map/slice | solution.py:88
  81.4 2.1 copy.67
  83.5 1.1 constant_dynamic-update-slice_fusion.7
  84.6 1.1 constant_dynamic-update-slice_fusion.6
  85.7 1.1 constant_dynamic-update-slice_fusion.5
  89.6 1.2 fusion.4
  94.4 2.5 %fusion.5 = bf16[1,16,128,5,128]{2,4,3,1,0:T(8,128)(2,1)S(1)} fusion(f32[16,128,5,128]{1,3,2,0:T(8,128)S(1)} %bitcast.180, f32[16,128]{1,0:T(8,128)S(1)} %bitcast.204, f32[16,128]{1,0:T(8,128)S(1)} %log_add_fusion, pred[128,5,128]{0,2,1:T(8,128)(4,1)S(1)} %and_bitcast_fusion, bf16[5,128,16,128]{1,3,0,2:T(8,128)(2,1)S(1)} %constant_dynamic-update-slice_fusion, ...), kind=kOutput, calls=%fused_computation.9 | convolution fusion | flops 344719360 | bytes 11108352 | tf_op jit(solution)/shard_map/bthd,bnuhd->bhtnu/dot_general | solution.py:105
  101.8 1.9 collective-permute-start.5
  104.7 2.1 collective-permute-start.6
  107.9 1.5 collective-permute-start.7
  110.5 4.5 %collective-permute-start.4 = (bf16[2,128,16,128]{1,3,2,0:T(8,128)(2,1)}, bf16[2,128,16,128]{1,3,2,0:T(8,128)(2,1)}, u32[]{:S(2)}, u32[]{:S(2)}) collective-permute-start(bf16[2,128,16,128]{1,3,2,0:T(8,128)(2,1)} %pad_maximum_fusion.1), channel_id=1, source_target_pairs={{1,0},{2,1},{3,2},{4,3},{5,4},{6,5},{7,6},{8,7},{9,8},{10,9},{11,1... | collective-permute-start | bytes 3145736 | tf_op jit(solution)/shard_map/ppermute | solution.py:17
  116.0 3.8 %convolution_bitcast_fusion = f32[128,16,128]{0,2,1:T(8,128)} fusion(bf16[5,128,16,128]{3,1,0,2:T(8,128)(2,1)S(1)} %constant_dynamic-update-slice_fusion.5, bf16[1,16,128,5,128]{2,4,3,1,0:T(8,128)(2,1)} %copy-done), kind=kOutput, calls=%fused_computation.16 | convolution fusion | flops 335544320 | bytes 6291456 | tf_op jit(solution)/shard_map/bhtnu,bnuhd->bthd/dot_general | solution.py:111
  119.8 8.9 %collective-permute-done.5 = bf16[2,128,16,128]{1,3,2,0:T(8,128)(2,1)} collective-permute-done((bf16[2,128,16,128]{1,3,2,0:T(8,128)(2,1)}, bf16[2,128,16,128]{1,3,2,0:T(8,128)(2,1)}, u32[]{:S(2)}, u32[]{:S(2)}) %collective-permute-start.5) | collective-permute-done | bytes 1048608 | tf_op jit(solution)/shard_map/ppermute | solution.py:17
  128.8 23.5 %collective-permute-done.7 = bf16[2,128,16,128]{1,3,2,0:T(8,128)(2,1)} collective-permute-done((bf16[2,128,16,128]{1,3,2,0:T(8,128)(2,1)}, bf16[2,128,16,128]{1,3,2,0:T(8,128)(2,1)}, u32[]{:S(2)}, u32[]{:S(2)}) %collective-permute-start.7) | collective-permute-done | bytes 1048608 | tf_op jit(solution)/shard_map/ppermute | solution.py:17
  152.4 56.0 %collective-permute-done.4 = bf16[2,128,16,128]{1,3,2,0:T(8,128)(2,1)} collective-permute-done((bf16[2,128,16,128]{1,3,2,0:T(8,128)(2,1)}, bf16[2,128,16,128]{1,3,2,0:T(8,128)(2,1)}, u32[]{:S(2)}, u32[]{:S(2)}) %collective-permute-start.4) | collective-permute-done | bytes 1048608 | tf_op jit(solution)/shard_map/ppermute | solution.py:17
  208.4 3.0 %fusion.16 = (bf16[128,16,128]{0,2,1:T(8,128)(2,1)S(1)}, f32[128,16,128]{0,2,1:T(8,128)S(1)}) fusion(bf16[128,16,128]{0,2,1:T(8,128)(2,1)S(1)} %copy-done.11, bf16[2,128,16,128]{1,3,2,0:T(8,128)(2,1)} %collective-permute-done.7, bf16[2,128,16,128]{1,3,2,0:T(8,128)(2,1)} %collective-permute-done.6, bf16[2,128,16,128]{1,3,2,0:T(8,128)(2,1)} %collective-permute-done.5, ...), kind=kLoop, calls=%fused_computation.26 | loop fusion | flops 4980736 | bytes 6815744 | tf_op jit(solution)/shard_map/convert_element_type | solution.py:185
  (82 shorter events, 29.6 us)
Async XLA Ops:
  0.6 4.4 %copy-start.13 = (bf16[128,2048]{1,0:T(8,128)(2,1)S(1)}, bf16[128,2048]{1,0:T(8,128)(2,1)}, u32[]{:S(2)}) copy-start(bf16[128,2048]{1,0:T(8,128)(2,1)} %param.8) | copy-start | bytes 1572868
  5.7 9.8 %copy-start.1 = (bf16[128,2048]{1,0:T(8,128)(2,1)S(1)}, bf16[128,2048]{1,0:T(8,128)(2,1)}, u32[]{:S(2)}) copy-start(bf16[128,2048]{1,0:T(8,128)(2,1)} %param.10) | copy-start | bytes 1572868
  6.6 12.1 %copy-start.15 = (s32[4]{0:T(128)S(1)}, s32[4]{0:T(128)}, u32[]{:S(2)}) copy-start(s32[4]{0:T(128)} %constant.35) | copy-start | bytes 52
  7.7 26.2 %collective-permute-start.2 = (bf16[2,128,2048]{1,2,0:T(8,128)(2,1)}, bf16[2,128,2048]{1,2,0:T(8,128)(2,1)}, u32[]{:S(2)}, u32[]{:S(2)}) collective-permute-start(bf16[2,128,2048]{1,2,0:T(8,128)(2,1)} %pad_maximum_fusion), channel_id=1, source_target_pairs={{0,4},{1,5},{2,6},{3,7},{4,8},{5,9},{6,10},{7,11},{8,12},{9,13},{1... | collective-permute-start | bytes 3145736 | tf_op jit(solution)/shard_map/ppermute | solution.py:17
  10.9 38.8 %collective-permute-start = (bf16[2,128,2048]{1,2,0:T(8,128)(2,1)}, bf16[2,128,2048]{1,2,0:T(8,128)(2,1)}, u32[]{:S(2)}, u32[]{:S(2)}) collective-permute-start(bf16[2,128,2048]{1,2,0:T(8,128)(2,1)} %pad_maximum_fusion), channel_id=1, source_target_pairs={{0,1},{1,2},{2,3},{3,4},{4,5},{5,6},{6,7},{7,8},{8,9},{9,10},{10,1... | collective-permute-start | bytes 3145736 | tf_op jit(solution)/shard_map/ppermute | solution.py:17
  33.9 34.6 %collective-permute-start.3 = (bf16[2,128,2048]{1,2,0:T(8,128)(2,1)}, bf16[2,128,2048]{1,2,0:T(8,128)(2,1)}, u32[]{:S(2)}, u32[]{:S(2)}) collective-permute-start(bf16[2,128,2048]{1,2,0:T(8,128)(2,1)} %collective-permute-done.2), channel_id=1, source_target_pairs={{0,4},{1,5},{2,6},{3,7},{4,8},{5,9},{6,10},{7,11},{8,12},{9,13},{1... | collective-permute-start | bytes 3145736 | tf_op jit(solution)/shard_map/ppermute | solution.py:17
  49.7 29.4 %collective-permute-start.1 = (bf16[2,128,2048]{1,2,0:T(8,128)(2,1)}, bf16[2,128,2048]{1,2,0:T(8,128)(2,1)}, u32[]{:S(2)}, u32[]{:S(2)}) collective-permute-start(bf16[2,128,2048]{1,2,0:T(8,128)(2,1)} %collective-permute-done), channel_id=1, source_target_pairs={{0,1},{1,2},{2,3},{3,4},{4,5},{5,6},{6,7},{7,8},{8,9},{9,10},{10,1... | collective-permute-start | bytes 3145736 | tf_op jit(solution)/shard_map/ppermute | solution.py:17
  81.4 5.5 %copy-start.3 = (bf16[128,16,128]{0,2,1:T(8,128)(2,1)S(1)}, bf16[128,16,128]{0,2,1:T(8,128)(2,1)}, u32[]{:S(2)}) copy-start(bf16[128,16,128]{0,2,1:T(8,128)(2,1)} %get-tuple-element.51) | copy-start | bytes 1572868
  89.5 1.2 copy-start.2
  90.8 1.7 copy-start.7
  90.8 1.8 copy-start.10
  90.8 2.0 copy-start.8
  90.8 2.1 copy-start.9
  93.0 1.2 copy-start.5
  93.0 1.4 copy-start.14
  96.9 1.7 copy-start
  96.9 1.7 copy-start.4
  101.8 26.9 %collective-permute-start.5 = (bf16[2,128,16,128]{1,3,2,0:T(8,128)(2,1)}, bf16[2,128,16,128]{1,3,2,0:T(8,128)(2,1)}, u32[]{:S(2)}, u32[]{:S(2)}) collective-permute-start(bf16[2,128,16,128]{1,3,2,0:T(8,128)(2,1)} %pad_maximum_fusion.2), channel_id=1, source_target_pairs={{2,0},{3,1},{4,2},{5,3},{6,4},{7,5},{8,6},{9,7},{10,8},{11,9},{12,... | collective-permute-start | bytes 3145736 | tf_op jit(solution)/shard_map/ppermute | solution.py:17
  104.7 24.1 %collective-permute-start.6 = (bf16[2,128,16,128]{1,3,2,0:T(8,128)(2,1)}, bf16[2,128,16,128]{1,3,2,0:T(8,128)(2,1)}, u32[]{:S(2)}, u32[]{:S(2)}) collective-permute-start(bf16[2,128,16,128]{1,3,2,0:T(8,128)(2,1)} %pad_maximum_fusion.3), channel_id=1, source_target_pairs={{4,0},{5,1},{6,2},{7,3},{8,4},{9,5},{10,6},{11,7},{12,8},{13,9},{1... | collective-permute-start | bytes 3145736 | tf_op jit(solution)/shard_map/ppermute | solution.py:17
  107.9 44.5 %collective-permute-start.7 = (bf16[2,128,16,128]{1,3,2,0:T(8,128)(2,1)}, bf16[2,128,16,128]{1,3,2,0:T(8,128)(2,1)}, u32[]{:S(2)}, u32[]{:S(2)}) collective-permute-start(bf16[2,128,16,128]{1,3,2,0:T(8,128)(2,1)} %pad_maximum_fusion.4), channel_id=1, source_target_pairs={{8,0},{9,1},{10,2},{11,3},{12,4},{13,5},{14,6},{15,7},{24,16},{25,... | collective-permute-start | bytes 3145736 | tf_op jit(solution)/shard_map/ppermute | solution.py:17
  110.5 97.9 %collective-permute-start.4 = (bf16[2,128,16,128]{1,3,2,0:T(8,128)(2,1)}, bf16[2,128,16,128]{1,3,2,0:T(8,128)(2,1)}, u32[]{:S(2)}, u32[]{:S(2)}) collective-permute-start(bf16[2,128,16,128]{1,3,2,0:T(8,128)(2,1)} %pad_maximum_fusion.1), channel_id=1, source_target_pairs={{1,0},{2,1},{3,2},{4,3},{5,4},{6,5},{7,6},{8,7},{9,8},{10,9},{11,1... | collective-permute-start | bytes 3145736 | tf_op jit(solution)/shard_map/ppermute | solution.py:17
  116.0 92.4 %copy-start.11 = (bf16[128,16,128]{0,2,1:T(8,128)(2,1)S(1)}, bf16[128,16,128]{0,2,1:T(8,128)(2,1)}, u32[]{:S(2)}) copy-start(bf16[128,16,128]{0,2,1:T(8,128)(2,1)} %get-tuple-element.18) | copy-start | bytes 1572868
  116.0 92.4 %copy-start.12 = (bf16[128,16,128]{0,2,1:T(8,128)(2,1)S(1)}, bf16[128,16,128]{0,2,1:T(8,128)(2,1)}, u32[]{:S(2)}) copy-start(bf16[128,16,128]{0,2,1:T(8,128)(2,1)} %get-tuple-element.27) | copy-start | bytes 1572868
  119.8 92.6 %copy-start.6 = (f32[128,16,128]{0,2,1:T(8,128)S(1)}, f32[128,16,128]{0,2,1:T(8,128)}, u32[]{:S(2)}) copy-start(f32[128,16,128]{0,2,1:T(8,128)} %convolution_bitcast_fusion) | copy-start | bytes 3145732

commit v5 on v4

--- a/solution.py
+++ b/solution.py
@@ -8,7 +8,7 @@
 HEADS = 16
 HEAD_DIM = 128
 BLOCK = 128
-CHUNKS = 1
+CHUNKS = 2
 
 
 def from_behind(value, axis, steps):
@@ -154,15 +154,11 @@
     columns = [slice(chunk * chunk_width, (chunk + 1) * chunk_width) for chunk in range(CHUNKS)]
     pieces = []
     pending = []
-    previous = None
     for chunk, cols in enumerate(columns):
         key_c, value_c = key_rot[:, cols], values[:, cols]
-        if previous is not None:
-            key_c, value_c, _ = lax.optimization_barrier((key_c, value_c, previous))
-        if len(pending) >= 2:
-            key_c, value_c, _ = lax.optimization_barrier((key_c, value_c, pending[-2]))
+        if pending:
+            key_c, value_c, _ = lax.optimization_barrier((key_c, value_c, pending[-1]))
         received = send_chunk(key_c, value_c, offsets)
-        previous = received[1:]
         output, query_grad, own, outgoing = attend_chunk(
             query_rot[:, cols], received, grad_out[:, cols], allowed, offsets, chunk_heads
         )

time: 216 us -> 190 us (0.88)
  waiting for transfers between devices: 126 us -> 43.1 us
  starting transfers between devices: 25.8 us -> 59.4 us
  local copies, waits for them, and re-layouts: 36.4 us -> 51 us
  other arithmetic: 14.5 us -> 21.8 us
    ppermute x8 -> x16, waiting for transfers between devices: 126 us -> 43.1 us  [from_behind(): lax.ppermute(value, axis, [(source, source + steps) for source in range(l...]
    ppermute x8 -> x16, starting transfers between devices: 25.8 us -> 59.4 us  [from_behind(): lax.ppermute(value, axis, [(source, source + steps) for source in range(l...]
    slice x0 -> x7, local copies, waits for them, and re-layouts: none -> 10 us  [the longest x4 7.15 us: attend_chunk(): moved[1].reshape(head_shape)]
    reshape x0 -> x4, local copies, waits for them, and re-layouts: none -> 4.61 us  [the longest x2 2.65 us: on_device(): output.reshape(rows, chunk_width)]
    another operation x4 -> x6, other arithmetic: 0.79 us -> 5.35 us
    another operation x6 -> x12, local copies, waits for them, and re-layouts: 7.65 us -> 11.1 us  [attend_chunk(): jnp.stack([moved[0].reshape(head_shape) for moved in received])[None]]
    convert_element_type x1 -> x0, other arithmetic: 2.99 us -> none  [on_device(): grad_values = value_accum.astype(jnp.bfloat16)]
    concatenate x0 -> x2, other arithmetic: none -> 2.69 us  [on_device(): jnp.concatenate(parts, axis=1)]
  transfers between devices with their start and end apart: 8 -> 16, of which waited for: 8 -> 6; matrix products, arithmetic and copies ran while one was open for 12% -> 29% of each run, Pallas kernels for 0% -> 0%
where the time goes in v5:
time: 190 us; the launch traced here: 188 us
  starting transfers between devices  59.4 us (31%)
  local copies, waits for them, and re-layouts  51 us (27%)
  waiting for transfers between devices  43.1 us (23%)
  other arithmetic  21.8 us (11%)
  matrix products  10.9 us (6%)
  between operations  2.02 us (1%)
    ppermute x16, starting transfers between devices, from_behind(): lax.ppermute(value, axis, [(source, source + steps) for source in range(l...  59.4 us
    ppermute x16, waiting for transfers between devices, from_behind(): lax.ppermute(value, axis, [(source, source + steps) for source in range(l...  43.1 us
    unnamed x67, local copies, waits for them, and re-layouts  11.9 us
    another operation x12, local copies, waits for them, and re-layouts, attend_chunk(): jnp.stack([moved[0].reshape(head_shape) for moved in received])[None]  11.1 us
    slice x4, local copies, waits for them, and re-layouts, attend_chunk(): moved[0].reshape(head_shape)  7.41 us
    slice x4, local copies, waits for them, and re-layouts, attend_chunk(): moved[1].reshape(head_shape)  7.15 us
    another operation x8, other arithmetic, attend_chunk(): jnp.stack([key_terms[0, slot_index], value_terms[0, slot_index]])  6.77 us
    another operation x6, other arithmetic  5.35 us
  transfers between devices with their start and end apart: 16, of which 6 were waited for; matrix products, arithmetic and copies ran while one was open for 29% of the time, Pallas kernels for 0%

profile of v5, /device:TPU:15, one launch (start us, length us, event | category | flops | bytes accessed | tf_op | source)
XLA Modules:
  0.0 188.3 jit_solution(12400298303557747190)
XLA Ops:
  7.5 3.2 %collective-permute-start.2 = (bf16[2,128,1024]{1,2,0:T(8,128)(2,1)}, bf16[2,128,1024]{1,2,0:T(8,128)(2,1)}, u32[]{:S(2)}, u32[]{:S(2)}) collective-permute-start(bf16[2,128,1024]{1,2,0:T(8,128)(2,1)} %pad_maximum_fusion.3), channel_id=1, source_target_pairs={{0,4},{1,5},{2,6},{3,7},{4,8},{5,9},{6,10},{7,11},{8,12},{9,13},{1... | collective-permute-start | bytes 1572872 | tf_op jit(solution)/shard_map/ppermute | solution.py:17
  10.7 4.0 %collective-permute-start = (bf16[2,128,1024]{1,2,0:T(8,128)(2,1)}, bf16[2,128,1024]{1,2,0:T(8,128)(2,1)}, u32[]{:S(2)}, u32[]{:S(2)}) collective-permute-start(bf16[2,128,1024]{1,2,0:T(8,128)(2,1)} %pad_maximum_fusion.3), channel_id=1, source_target_pairs={{0,1},{1,2},{2,3},{3,4},{4,5},{5,6},{6,7},{7,8},{8,9},{9,10},{10,1... | collective-permute-start | bytes 1572872 | tf_op jit(solution)/shard_map/ppermute | solution.py:17
  18.7 3.8 %collective-permute-done.2 = bf16[2,128,1024]{1,2,0:T(8,128)(2,1)} collective-permute-done((bf16[2,128,1024]{1,2,0:T(8,128)(2,1)}, bf16[2,128,1024]{1,2,0:T(8,128)(2,1)}, u32[]{:S(2)}, u32[]{:S(2)}) %collective-permute-start.2) | collective-permute-done | bytes 524320 | tf_op jit(solution)/shard_map/ppermute | solution.py:17
  22.5 3.2 %collective-permute-start.3 = (bf16[2,128,1024]{1,2,0:T(8,128)(2,1)}, bf16[2,128,1024]{1,2,0:T(8,128)(2,1)}, u32[]{:S(2)}, u32[]{:S(2)}) collective-permute-start(bf16[2,128,1024]{1,2,0:T(8,128)(2,1)} %collective-permute-done.2), channel_id=1, source_target_pairs={{0,4},{1,5},{2,6},{3,7},{4,8},{5,9},{6,10},{7,11},{8,12},{9,13},{1... | collective-permute-start | bytes 1572872 | tf_op jit(solution)/shard_map/ppermute | solution.py:17
  28.4 5.3 %collective-permute-start.1 = (bf16[2,128,1024]{1,2,0:T(8,128)(2,1)}, bf16[2,128,1024]{1,2,0:T(8,128)(2,1)}, u32[]{:S(2)}, u32[]{:S(2)}) collective-permute-start(bf16[2,128,1024]{1,2,0:T(8,128)(2,1)} %collective-permute-done), channel_id=1, source_target_pairs={{0,1},{1,2},{2,3},{3,4},{4,5},{5,6},{6,7},{7,8},{8,9},{9,10},{10,1... | collective-permute-start | bytes 1572872 | tf_op jit(solution)/shard_map/ppermute | solution.py:17
  41.1 4.1 %collective-permute-done.1 = bf16[2,128,1024]{1,2,0:T(8,128)(2,1)} collective-permute-done((bf16[2,128,1024]{1,2,0:T(8,128)(2,1)}, bf16[2,128,1024]{1,2,0:T(8,128)(2,1)}, u32[]{:S(2)}, u32[]{:S(2)}) %collective-permute-start.1) | collective-permute-done | bytes 524320 | tf_op jit(solution)/shard_map/ppermute | solution.py:17
  45.2 1.9 fusion.46
  60.7 3.2 %collective-permute-start.6 = (bf16[2,128,1024]{1,2,0:T(8,128)(2,1)}, bf16[2,128,1024]{1,2,0:T(8,128)(2,1)}, u32[]{:S(2)}, u32[]{:S(2)}) collective-permute-start(bf16[2,128,1024]{1,2,0:T(8,128)(2,1)} %pad_maximum_fusion.9), channel_id=1, source_target_pairs={{0,4},{1,5},{2,6},{3,7},{4,8},{5,9},{6,10},{7,11},{8,12},{9,13},{1... | collective-permute-start | bytes 1572872 | tf_op jit(solution)/shard_map/ppermute | solution.py:17
  64.1 5.6 %collective-permute-start.4 = (bf16[2,128,1024]{1,2,0:T(8,128)(2,1)}, bf16[2,128,1024]{1,2,0:T(8,128)(2,1)}, u32[]{:S(2)}, u32[]{:S(2)}) collective-permute-start(bf16[2,128,1024]{1,2,0:T(8,128)(2,1)} %pad_maximum_fusion.9), channel_id=1, source_target_pairs={{0,1},{1,2},{2,3},{3,4},{4,5},{5,6},{6,7},{7,8},{8,9},{9,10},{10,1... | collective-permute-start | bytes 1572872 | tf_op jit(solution)/shard_map/ppermute | solution.py:17
  71.0 1.9 %collective-permute-start.8 = (bf16[2,128,8,128]{1,3,2,0:T(8,128)(2,1)}, bf16[2,128,8,128]{1,3,2,0:T(8,128)(2,1)}, u32[]{:S(2)}, u32[]{:S(2)}) collective-permute-start(bf16[2,128,8,128]{1,3,2,0:T(8,128)(2,1)} %pad_maximum_fusion.5), channel_id=1, source_target_pairs={{1,0},{2,1},{3,2},{4,3},{5,4},{6,5},{7,6},{8,7},{9,8},{10,9},{11,1... | collective-permute-start | bytes 1572872 | tf_op jit(solution)/shard_map/ppermute | solution.py:17
  72.9 1.9 %collective-permute-start.9 = (bf16[2,128,8,128]{1,3,2,0:T(8,128)(2,1)}, bf16[2,128,8,128]{1,3,2,0:T(8,128)(2,1)}, u32[]{:S(2)}, u32[]{:S(2)}) collective-permute-start(bf16[2,128,8,128]{1,3,2,0:T(8,128)(2,1)} %pad_maximum_fusion.6), channel_id=1, source_target_pairs={{2,0},{3,1},{4,2},{5,3},{6,4},{7,5},{8,6},{9,7},{10,8},{11,9},{12,... | collective-permute-start | bytes 1572872 | tf_op jit(solution)/shard_map/ppermute | solution.py:17
  77.4 1.8 copy.128
  79.2 2.7 %fusion.22 = f32[128,8,128]{0,2,1:T(8,128)} fusion(bf16[5,128,8,128]{3,1,0,2:T(8,128)(2,1)S(1)} %constant_dynamic-update-slice_fusion.5, bf16[1,8,128,5,128]{2,4,3,1,0:T(8,128)(2,1)} %copy-done), kind=kOutput, calls=%fused_computation.34 | convolution fusion | flops 167772160 | bytes 3145728 | tf_op jit(solution)/shard_map/bhtnu,bnuhd->bthd/dot_general | solution.py:111
  81.9 4.9 %collective-permute-start.7 = (bf16[2,128,1024]{1,2,0:T(8,128)(2,1)}, bf16[2,128,1024]{1,2,0:T(8,128)(2,1)}, u32[]{:S(2)}, u32[]{:S(2)}) collective-permute-start(bf16[2,128,1024]{1,2,0:T(8,128)(2,1)} %collective-permute-done.6), channel_id=1, source_target_pairs={{0,4},{1,5},{2,6},{3,7},{4,8},{5,9},{6,10},{7,11},{8,12},{9,13},{1... | collective-permute-start | bytes 1572872 | tf_op jit(solution)/shard_map/ppermute | solution.py:17
  86.9 1.8 fusion.41
  88.7 4.6 %collective-permute-start.5 = (bf16[2,128,1024]{1,2,0:T(8,128)(2,1)}, bf16[2,128,1024]{1,2,0:T(8,128)(2,1)}, u32[]{:S(2)}, u32[]{:S(2)}) collective-permute-start(bf16[2,128,1024]{1,2,0:T(8,128)(2,1)} %collective-permute-done.4), channel_id=1, source_target_pairs={{0,1},{1,2},{2,3},{3,4},{4,5},{5,6},{6,7},{7,8},{8,9},{9,10},{10,1... | collective-permute-start | bytes 1572872 | tf_op jit(solution)/shard_map/ppermute | solution.py:17
  93.4 1.9 fusion.43
  96.4 1.8 copy.122
  100.2 2.1 %collective-permute-start.10 = (bf16[2,128,8,128]{1,3,2,0:T(8,128)(2,1)}, bf16[2,128,8,128]{1,3,2,0:T(8,128)(2,1)}, u32[]{:S(2)}, u32[]{:S(2)}) collective-permute-start(bf16[2,128,8,128]{1,3,2,0:T(8,128)(2,1)} %pad_maximum_fusion.7), channel_id=1, source_target_pairs={{4,0},{5,1},{6,2},{7,3},{8,4},{9,5},{10,6},{11,7},{12,8},{13,9},{1... | collective-permute-start | bytes 1572872 | tf_op jit(solution)/shard_map/ppermute | solution.py:17
  102.3 1.9 fusion.40
  104.1 1.8 copy.125
  105.9 1.9 fusion.42
  107.8 1.8 copy.123
  120.9 11.9 %collective-permute-start.13 = (bf16[2,128,8,128]{1,3,2,0:T(8,128)(2,1)}, bf16[2,128,8,128]{1,3,2,0:T(8,128)(2,1)}, u32[]{:S(2)}, u32[]{:S(2)}) collective-permute-start(bf16[2,128,8,128]{1,3,2,0:T(8,128)(2,1)} %pad_maximum_fusion.13), channel_id=1, source_target_pairs={{2,0},{3,1},{4,2},{5,3},{6,4},{7,5},{8,6},{9,7},{10,8},{11,9},{12,... | collective-permute-start | bytes 1572872 | tf_op jit(solution)/shard_map/ppermute | solution.py:17
  135.4 1.9 %collective-permute-start.14 = (bf16[2,128,8,128]{1,3,2,0:T(8,128)(2,1)}, bf16[2,128,8,128]{1,3,2,0:T(8,128)(2,1)}, u32[]{:S(2)}, u32[]{:S(2)}) collective-permute-start(bf16[2,128,8,128]{1,3,2,0:T(8,128)(2,1)} %pad_maximum_fusion.14), channel_id=1, source_target_pairs={{4,0},{5,1},{6,2},{7,3},{8,4},{9,5},{10,6},{11,7},{12,8},{13,9},{1... | collective-permute-start | bytes 1572872 | tf_op jit(solution)/shard_map/ppermute | solution.py:17
  138.6 3.0 %collective-permute-start.12 = (bf16[2,128,8,128]{1,3,2,0:T(8,128)(2,1)}, bf16[2,128,8,128]{1,3,2,0:T(8,128)(2,1)}, u32[]{:S(2)}, u32[]{:S(2)}) collective-permute-start(bf16[2,128,8,128]{1,3,2,0:T(8,128)(2,1)} %pad_maximum_fusion.12), channel_id=1, source_target_pairs={{1,0},{2,1},{3,2},{4,3},{5,4},{6,5},{7,6},{8,7},{9,8},{10,9},{11,1... | collective-permute-start | bytes 1572872 | tf_op jit(solution)/shard_map/ppermute | solution.py:17
  141.6 2.6 %fusion.32 = (bf16[128,8,128]{0,2,1:T(8,128)(2,1)}, f32[128,8,128]{0,2,1:T(8,128)S(1)}) fusion(bf16[128,8,128]{0,2,1:T(8,128)(2,1)S(1)} %copy-done.16, bf16[2,128,8,128]{1,3,2,0:T(8,128)(2,1)} %collective-permute-done.11, bf16[2,128,8,128]{1,3,2,0:T(8,128)(2,1)} %collective-permute-done.10, bf16[2,128,8,128]{1,3,2,0:T(8,128)(2,1)} %collective-permute-done.9, ...), kind=kLoop, calls=%fused_computation.72 | loop fusion | flops 2490368 | bytes 3407872 | tf_op jit(solution)/shard_map/convert.23
  144.3 1.8 copy.141
  146.9 1.9 pad_maximum_fusion.10
  150.2 10.9 %collective-permute-done.14 = bf16[2,128,8,128]{1,3,2,0:T(8,128)(2,1)} collective-permute-done((bf16[2,128,8,128]{1,3,2,0:T(8,128)(2,1)}, bf16[2,128,8,128]{1,3,2,0:T(8,128)(2,1)}, u32[]{:S(2)}, u32[]{:S(2)}) %collective-permute-start.14) | collective-permute-done | bytes 524320 | tf_op jit(solution)/shard_map/ppermute | solution.py:17
  161.1 21.8 %collective-permute-done.12 = bf16[2,128,8,128]{1,3,2,0:T(8,128)(2,1)} collective-permute-done((bf16[2,128,8,128]{1,3,2,0:T(8,128)(2,1)}, bf16[2,128,8,128]{1,3,2,0:T(8,128)(2,1)}, u32[]{:S(2)}, u32[]{:S(2)}) %collective-permute-start.12) | collective-permute-done | bytes 524320 | tf_op jit(solution)/shard_map/ppermute | solution.py:17
  182.9 1.9 %fusion.31 = (bf16[128,8,128]{0,2,1:T(8,128)(2,1)S(1)}, f32[128,8,128]{0,2,1:T(8,128)S(1)}) fusion(bf16[128,8,128]{0,2,1:T(8,128)(2,1)S(1)} %copy-done.19, bf16[2,128,8,128]{1,3,2,0:T(8,128)(2,1)} %collective-permute-done.15, bf16[2,128,8,128]{1,3,2,0:T(8,128)(2,1)} %collective-permute-done.14, bf16[2,128,8,128]{1,3,2,0:T(8,128)(2,1)} %collective-permute-done.13, ...), kind=kLoop, calls=%fused_computation.67 | loop fusion | flops 2490368 | bytes 3407872 | tf_op jit(solution)/shard_map/convert.22
  (159 shorter events, 61.5 us)
Async XLA Ops:
  0.6 3.1 %copy-start.20 = (bf16[128,2048]{1,0:T(8,128)(2,1)S(1)}, bf16[128,2048]{1,0:T(8,128)(2,1)}, u32[]{:S(2)}) copy-start(bf16[128,2048]{1,0:T(8,128)(2,1)} %param.7) | copy-start | bytes 1572868
  6.6 8.8 %copy-start.21 = (bf16[128,2048]{1,0:T(8,128)(2,1)S(1)}, bf16[128,2048]{1,0:T(8,128)(2,1)}, u32[]{:S(2)}) copy-start(bf16[128,2048]{1,0:T(8,128)(2,1)} %param.10) | copy-start | bytes 1572868
  6.6 9.5 %copy-start.22 = (s32[4]{0:T(128)S(1)}, s32[4]{0:T(128)}, u32[]{:S(2)}) copy-start(s32[4]{0:T(128)} %constant.35) | copy-start | bytes 52
  7.5 15.0 %collective-permute-start.2 = (bf16[2,128,1024]{1,2,0:T(8,128)(2,1)}, bf16[2,128,1024]{1,2,0:T(8,128)(2,1)}, u32[]{:S(2)}, u32[]{:S(2)}) collective-permute-start(bf16[2,128,1024]{1,2,0:T(8,128)(2,1)} %pad_maximum_fusion.3), channel_id=1, source_target_pairs={{0,4},{1,5},{2,6},{3,7},{4,8},{5,9},{6,10},{7,11},{8,12},{9,13},{1... | collective-permute-start | bytes 1572872 | tf_op jit(solution)/shard_map/ppermute | solution.py:17
  10.7 17.7 %collective-permute-start = (bf16[2,128,1024]{1,2,0:T(8,128)(2,1)}, bf16[2,128,1024]{1,2,0:T(8,128)(2,1)}, u32[]{:S(2)}, u32[]{:S(2)}) collective-permute-start(bf16[2,128,1024]{1,2,0:T(8,128)(2,1)} %pad_maximum_fusion.3), channel_id=1, source_target_pairs={{0,1},{1,2},{2,3},{3,4},{4,5},{5,6},{6,7},{7,8},{8,9},{9,10},{10,1... | collective-permute-start | bytes 1572872 | tf_op jit(solution)/shard_map/ppermute | solution.py:17
  22.5 16.6 %collective-permute-start.3 = (bf16[2,128,1024]{1,2,0:T(8,128)(2,1)}, bf16[2,128,1024]{1,2,0:T(8,128)(2,1)}, u32[]{:S(2)}, u32[]{:S(2)}) collective-permute-start(bf16[2,128,1024]{1,2,0:T(8,128)(2,1)} %collective-permute-done.2), channel_id=1, source_target_pairs={{0,4},{1,5},{2,6},{3,7},{4,8},{5,9},{6,10},{7,11},{8,12},{9,13},{1... | collective-permute-start | bytes 1572872 | tf_op jit(solution)/shard_map/ppermute | solution.py:17
  28.4 16.9 %collective-permute-start.1 = (bf16[2,128,1024]{1,2,0:T(8,128)(2,1)}, bf16[2,128,1024]{1,2,0:T(8,128)(2,1)}, u32[]{:S(2)}, u32[]{:S(2)}) collective-permute-start(bf16[2,128,1024]{1,2,0:T(8,128)(2,1)} %collective-permute-done), channel_id=1, source_target_pairs={{0,1},{1,2},{2,3},{3,4},{4,5},{5,6},{6,7},{7,8},{8,9},{9,10},{10,1... | collective-permute-start | bytes 1572872 | tf_op jit(solution)/shard_map/ppermute | solution.py:17
  49.7 1.3 copy-start.4
  49.7 1.3 copy-start.15
  49.7 1.4 copy-start.10
  49.8 1.5 copy-start.13
  51.8 1.5 copy-start.1
  59.0 4.9 %copy-start.8 = (bf16[128,1024]{1,0:T(8,128)(2,1)S(1)}, bf16[128,1024]{1,0:T(8,128)(2,1)}, u32[]{:S(2)}) copy-start(bf16[128,1024]{1,0:T(8,128)(2,1)} %get-tuple-element.52) | copy-start | bytes 786436
  60.7 21.2 %collective-permute-start.6 = (bf16[2,128,1024]{1,2,0:T(8,128)(2,1)}, bf16[2,128,1024]{1,2,0:T(8,128)(2,1)}, u32[]{:S(2)}, u32[]{:S(2)}) collective-permute-start(bf16[2,128,1024]{1,2,0:T(8,128)(2,1)} %pad_maximum_fusion.9), channel_id=1, source_target_pairs={{0,4},{1,5},{2,6},{3,7},{4,8},{5,9},{6,10},{7,11},{8,12},{9,13},{1... | collective-permute-start | bytes 1572872 | tf_op jit(solution)/shard_map/ppermute | solution.py:17
  64.1 24.7 %collective-permute-start.4 = (bf16[2,128,1024]{1,2,0:T(8,128)(2,1)}, bf16[2,128,1024]{1,2,0:T(8,128)(2,1)}, u32[]{:S(2)}, u32[]{:S(2)}) collective-permute-start(bf16[2,128,1024]{1,2,0:T(8,128)(2,1)} %pad_maximum_fusion.9), channel_id=1, source_target_pairs={{0,1},{1,2},{2,3},{3,4},{4,5},{5,6},{6,7},{7,8},{8,9},{9,10},{10,1... | collective-permute-start | bytes 1572872 | tf_op jit(solution)/shard_map/ppermute | solution.py:17
  69.7 65.7 %collective-permute-start.11 = (bf16[2,128,8,128]{1,3,2,0:T(8,128)(2,1)}, bf16[2,128,8,128]{1,3,2,0:T(8,128)(2,1)}, u32[]{:S(2)}, u32[]{:S(2)}) collective-permute-start(bf16[2,128,8,128]{1,3,2,0:T(8,128)(2,1)} %pad_maximum_fusion.8), channel_id=1, source_target_pairs={{8,0},{9,1},{10,2},{11,3},{12,4},{13,5},{14,6},{15,7},{24,16},{25,... | collective-permute-start | bytes 1572872 | tf_op jit(solution)/shard_map/ppermute | solution.py:17
  71.0 66.3 %collective-permute-start.8 = (bf16[2,128,8,128]{1,3,2,0:T(8,128)(2,1)}, bf16[2,128,8,128]{1,3,2,0:T(8,128)(2,1)}, u32[]{:S(2)}, u32[]{:S(2)}) collective-permute-start(bf16[2,128,8,128]{1,3,2,0:T(8,128)(2,1)} %pad_maximum_fusion.5), channel_id=1, source_target_pairs={{1,0},{2,1},{3,2},{4,3},{5,4},{6,5},{7,6},{8,7},{9,8},{10,9},{11,1... | collective-permute-start | bytes 1572872 | tf_op jit(solution)/shard_map/ppermute | solution.py:17
  72.9 65.7 %collective-permute-start.9 = (bf16[2,128,8,128]{1,3,2,0:T(8,128)(2,1)}, bf16[2,128,8,128]{1,3,2,0:T(8,128)(2,1)}, u32[]{:S(2)}, u32[]{:S(2)}) collective-permute-start(bf16[2,128,8,128]{1,3,2,0:T(8,128)(2,1)} %pad_maximum_fusion.6), channel_id=1, source_target_pairs={{2,0},{3,1},{4,2},{5,3},{6,4},{7,5},{8,6},{9,7},{10,8},{11,9},{12,... | collective-permute-start | bytes 1572872 | tf_op jit(solution)/shard_map/ppermute | solution.py:17
  81.9 18.2 %collective-permute-start.7 = (bf16[2,128,1024]{1,2,0:T(8,128)(2,1)}, bf16[2,128,1024]{1,2,0:T(8,128)(2,1)}, u32[]{:S(2)}, u32[]{:S(2)}) collective-permute-start(bf16[2,128,1024]{1,2,0:T(8,128)(2,1)} %collective-permute-done.6), channel_id=1, source_target_pairs={{0,4},{1,5},{2,6},{3,7},{4,8},{5,9},{6,10},{7,11},{8,12},{9,13},{1... | collective-permute-start | bytes 1572872 | tf_op jit(solution)/shard_map/ppermute | solution.py:17
  88.7 10.4 %copy-start.5 = (bf16[5,128,8,128]{1,3,0,2:T(8,128)(2,1)S(1)}, bf16[5,128,8,128]{1,3,0,2:T(8,128)(2,1)}, u32[]{:S(2)}) copy-start(bf16[5,128,8,128]{1,3,0,2:T(8,128)(2,1)} %constant_dynamic-update-slice_fusion.14) | copy-start | bytes 3932164
  88.7 17.2 %collective-permute-start.5 = (bf16[2,128,1024]{1,2,0:T(8,128)(2,1)}, bf16[2,128,1024]{1,2,0:T(8,128)(2,1)}, u32[]{:S(2)}, u32[]{:S(2)}) collective-permute-start(bf16[2,128,1024]{1,2,0:T(8,128)(2,1)} %collective-permute-done.4), channel_id=1, source_target_pairs={{0,1},{1,2},{2,3},{3,4},{4,5},{5,6},{6,7},{7,8},{8,9},{9,10},{10,1... | collective-permute-start | bytes 1572872 | tf_op jit(solution)/shard_map/ppermute | solution.py:17
  100.2 41.5 %collective-permute-start.10 = (bf16[2,128,8,128]{1,3,2,0:T(8,128)(2,1)}, bf16[2,128,8,128]{1,3,2,0:T(8,128)(2,1)}, u32[]{:S(2)}, u32[]{:S(2)}) collective-permute-start(bf16[2,128,8,128]{1,3,2,0:T(8,128)(2,1)} %pad_maximum_fusion.7), channel_id=1, source_target_pairs={{4,0},{5,1},{6,2},{7,3},{8,4},{9,5},{10,6},{11,7},{12,8},{13,9},{1... | collective-permute-start | bytes 1572872 | tf_op jit(solution)/shard_map/ppermute | solution.py:17
  120.9 29.3 %collective-permute-start.13 = (bf16[2,128,8,128]{1,3,2,0:T(8,128)(2,1)}, bf16[2,128,8,128]{1,3,2,0:T(8,128)(2,1)}, u32[]{:S(2)}, u32[]{:S(2)}) collective-permute-start(bf16[2,128,8,128]{1,3,2,0:T(8,128)(2,1)} %pad_maximum_fusion.13), channel_id=1, source_target_pairs={{2,0},{3,1},{4,2},{5,3},{6,4},{7,5},{8,6},{9,7},{10,8},{11,9},{12,... | collective-permute-start | bytes 1572872 | tf_op jit(solution)/shard_map/ppermute | solution.py:17
  133.7 8.0 %copy-start.16 = (bf16[128,8,128]{0,2,1:T(8,128)(2,1)S(1)}, bf16[128,8,128]{0,2,1:T(8,128)(2,1)}, u32[]{:S(2)}) copy-start(bf16[128,8,128]{0,2,1:T(8,128)(2,1)} %get-tuple-element.24) | copy-start | bytes 786436
  133.7 8.0 %copy-start.17 = (bf16[128,8,128]{0,2,1:T(8,128)(2,1)S(1)}, bf16[128,8,128]{0,2,1:T(8,128)(2,1)}, u32[]{:S(2)}) copy-start(bf16[128,8,128]{0,2,1:T(8,128)(2,1)} %get-tuple-element.34) | copy-start | bytes 786436
  135.4 25.7 %collective-permute-start.14 = (bf16[2,128,8,128]{1,3,2,0:T(8,128)(2,1)}, bf16[2,128,8,128]{1,3,2,0:T(8,128)(2,1)}, u32[]{:S(2)}, u32[]{:S(2)}) collective-permute-start(bf16[2,128,8,128]{1,3,2,0:T(8,128)(2,1)} %pad_maximum_fusion.14), channel_id=1, source_target_pairs={{4,0},{5,1},{6,2},{7,3},{8,4},{9,5},{10,6},{11,7},{12,8},{13,9},{1... | collective-permute-start | bytes 1572872 | tf_op jit(solution)/shard_map/ppermute | solution.py:17
  137.3 23.8 %collective-permute-start.15 = (bf16[2,128,8,128]{1,3,2,0:T(8,128)(2,1)}, bf16[2,128,8,128]{1,3,2,0:T(8,128)(2,1)}, u32[]{:S(2)}, u32[]{:S(2)}) collective-permute-start(bf16[2,128,8,128]{1,3,2,0:T(8,128)(2,1)} %pad_maximum_fusion.15), channel_id=1, source_target_pairs={{8,0},{9,1},{10,2},{11,3},{12,4},{13,5},{14,6},{15,7},{24,16},{25,... | collective-permute-start | bytes 1572872 | tf_op jit(solution)/shard_map/ppermute | solution.py:17
  138.6 44.3 %collective-permute-start.12 = (bf16[2,128,8,128]{1,3,2,0:T(8,128)(2,1)}, bf16[2,128,8,128]{1,3,2,0:T(8,128)(2,1)}, u32[]{:S(2)}, u32[]{:S(2)}) collective-permute-start(bf16[2,128,8,128]{1,3,2,0:T(8,128)(2,1)} %pad_maximum_fusion.12), channel_id=1, source_target_pairs={{1,0},{2,1},{3,2},{4,3},{5,4},{6,5},{7,6},{8,7},{9,8},{10,9},{11,1... | collective-permute-start | bytes 1572872 | tf_op jit(solution)/shard_map/ppermute | solution.py:17
  148.8 34.1 %copy-start.18 = (bf16[128,8,128]{0,2,1:T(8,128)(2,1)S(1)}, bf16[128,8,128]{0,2,1:T(8,128)(2,1)}, u32[]{:S(2)}) copy-start(bf16[128,8,128]{0,2,1:T(8,128)(2,1)} %get-tuple-element.43) | copy-start | bytes 786436
  148.8 34.1 %copy-start.19 = (bf16[128,8,128]{0,2,1:T(8,128)(2,1)S(1)}, bf16[128,8,128]{0,2,1:T(8,128)(2,1)}, u32[]{:S(2)}) copy-start(bf16[128,8,128]{0,2,1:T(8,128)(2,1)} %get-tuple-element.29) | copy-start | bytes 786436
  150.2 34.8 %copy-start.2 = (f32[128,8,128]{0,2,1:T(8,128)S(1)}, f32[128,8,128]{0,2,1:T(8,128)}, u32[]{:S(2)}) copy-start(f32[128,8,128]{0,2,1:T(8,128)} %fusion.22) | copy-start | bytes 1572868
  150.2 34.8 %copy-start.3 = (f32[128,8,128]{0,2,1:T(8,128)S(1)}, f32[128,8,128]{0,2,1:T(8,128)}, u32[]{:S(2)}) copy-start(f32[128,8,128]{0,2,1:T(8,128)} %convolution_bitcast_fusion) | copy-start | bytes 1572868
  (7 other events, 7.6 us)

commit v6 on v5

--- a/solution.py
+++ b/solution.py
@@ -157,7 +157,7 @@
     for chunk, cols in enumerate(columns):
         key_c, value_c = key_rot[:, cols], values[:, cols]
         if pending:
-            key_c, value_c, _ = lax.optimization_barrier((key_c, value_c, pending[-1]))
+            key_c, value_c, _ = lax.optimization_barrier((key_c, value_c, pieces[-1][0]))
         received = send_chunk(key_c, value_c, offsets)
         output, query_grad, own, outgoing = attend_chunk(
             query_rot[:, cols], received, grad_out[:, cols], allowed, offsets, chunk_heads

time: 190 us -> 186 us (0.979)
  starting transfers between devices: 59.4 us -> 48.2 us
  waiting for transfers between devices: 43.1 us -> 46.5 us
  local copies, waits for them, and re-layouts: 51 us -> 53.2 us
  other arithmetic: 21.8 us -> 23.8 us
    ppermute x16, starting transfers between devices: 59.4 us -> 48.2 us  [from_behind(): lax.ppermute(value, axis, [(source, source + steps) for source in range(l...]
    slice x4 -> x8, local copies, waits for them, and re-layouts: 7.41 us -> 14.7 us  [attend_chunk(): moved[0].reshape(head_shape)]
    slice x4 -> x0, local copies, waits for them, and re-layouts: 7.15 us -> none  [attend_chunk(): moved[1].reshape(head_shape)]
    ppermute x16, waiting for transfers between devices: 43.1 us -> 46.5 us  [from_behind(): lax.ppermute(value, axis, [(source, source + steps) for source in range(l...]
    another operation x8, other arithmetic: 6.77 us -> 8.69 us  [attend_chunk(): jnp.stack([key_terms[0, slot_index], value_terms[0, slot_index]])]
    unnamed x67 -> x73, local copies, waits for them, and re-layouts: 11.9 us -> 12.9 us
  transfers between devices with their start and end apart: 16 -> 16, of which waited for: 6 -> 7; matrix products, arithmetic and copies ran while one was open for 29% -> 35% of each run, Pallas kernels for 0% -> 0%
where the time goes in v6:
time: 186 us; the launch traced here: 185 us
  local copies, waits for them, and re-layouts  53.2 us (29%)
  starting transfers between devices  48.2 us (26%)
  waiting for transfers between devices  46.5 us (25%)
  other arithmetic  23.8 us (13%)
  matrix products  11 us (6%)
  between operations  2.06 us (1%)
    ppermute x16, starting transfers between devices, from_behind(): lax.ppermute(value, axis, [(source, source + steps) for source in range(l...  48.2 us
    ppermute x16, waiting for transfers between devices, from_behind(): lax.ppermute(value, axis, [(source, source + steps) for source in range(l...  46.5 us
    slice x8, local copies, waits for them, and re-layouts, attend_chunk(): moved[0].reshape(head_shape)  14.7 us
    unnamed x73, local copies, waits for them, and re-layouts  12.9 us
    another operation x12, local copies, waits for them, and re-layouts, attend_chunk(): jnp.stack([moved[0].reshape(head_shape) for moved in received])[None]  12.7 us
    another operation x8, other arithmetic, attend_chunk(): jnp.stack([key_terms[0, slot_index], value_terms[0, slot_index]])  8.69 us
    another operation x6, other arithmetic  5.35 us
    dot_general x2, matrix products, attend_chunk(): jnp.einsum('bhtnu,bnuhd->bthd', grad_scores, key_stack, preferred_element...  4.08 us
  transfers between devices with their start and end apart: 16, of which 7 were waited for; matrix products, arithmetic and copies ran while one was open for 35% of the time, Pallas kernels for 0%

profile of v6, /device:TPU:15, one launch (start us, length us, event | category | flops | bytes accessed | tf_op | source)
XLA Modules:
  0.0 184.7 jit_solution(18317317486872107987)
XLA Ops:
  7.5 3.2 %collective-permute-start.2 = (bf16[2,128,1024]{1,2,0:T(8,128)(2,1)}, bf16[2,128,1024]{1,2,0:T(8,128)(2,1)}, u32[]{:S(2)}, u32[]{:S(2)}) collective-permute-start(bf16[2,128,1024]{1,2,0:T(8,128)(2,1)} %pad_maximum_fusion.3), channel_id=1, source_target_pairs={{0,4},{1,5},{2,6},{3,7},{4,8},{5,9},{6,10},{7,11},{8,12},{9,13},{1... | collective-permute-start | bytes 1572872 | tf_op jit(solution)/shard_map/ppermute | solution.py:17
  10.7 4.0 %collective-permute-start = (bf16[2,128,1024]{1,2,0:T(8,128)(2,1)}, bf16[2,128,1024]{1,2,0:T(8,128)(2,1)}, u32[]{:S(2)}, u32[]{:S(2)}) collective-permute-start(bf16[2,128,1024]{1,2,0:T(8,128)(2,1)} %pad_maximum_fusion.3), channel_id=1, source_target_pairs={{0,1},{1,2},{2,3},{3,4},{4,5},{5,6},{6,7},{7,8},{8,9},{9,10},{10,1... | collective-permute-start | bytes 1572872 | tf_op jit(solution)/shard_map/ppermute | solution.py:17
  18.2 4.2 %collective-permute-done.2 = bf16[2,128,1024]{1,2,0:T(8,128)(2,1)} collective-permute-done((bf16[2,128,1024]{1,2,0:T(8,128)(2,1)}, bf16[2,128,1024]{1,2,0:T(8,128)(2,1)}, u32[]{:S(2)}, u32[]{:S(2)}) %collective-permute-start.2) | collective-permute-done | bytes 524320 | tf_op jit(solution)/shard_map/ppermute | solution.py:17
  22.5 3.2 %collective-permute-start.3 = (bf16[2,128,1024]{1,2,0:T(8,128)(2,1)}, bf16[2,128,1024]{1,2,0:T(8,128)(2,1)}, u32[]{:S(2)}, u32[]{:S(2)}) collective-permute-start(bf16[2,128,1024]{1,2,0:T(8,128)(2,1)} %collective-permute-done.2), channel_id=1, source_target_pairs={{0,4},{1,5},{2,6},{3,7},{4,8},{5,9},{6,10},{7,11},{8,12},{9,13},{1... | collective-permute-start | bytes 1572872 | tf_op jit(solution)/shard_map/ppermute | solution.py:17
  28.4 5.3 %collective-permute-start.1 = (bf16[2,128,1024]{1,2,0:T(8,128)(2,1)}, bf16[2,128,1024]{1,2,0:T(8,128)(2,1)}, u32[]{:S(2)}, u32[]{:S(2)}) collective-permute-start(bf16[2,128,1024]{1,2,0:T(8,128)(2,1)} %collective-permute-done), channel_id=1, source_target_pairs={{0,1},{1,2},{2,3},{3,4},{4,5},{5,6},{6,7},{7,8},{8,9},{9,10},{10,1... | collective-permute-start | bytes 1572872 | tf_op jit(solution)/shard_map/ppermute | solution.py:17
  33.6 1.9 %fusion.43 = (bf16[1,128,1024]{1,2,0:T(8,128)(2,1)}, bf16[1,128,1024]{1,2,0:T(8,128)(2,1)}) fusion(bf16[2,128,1024]{1,2,0:T(8,128)(2,1)} %collective-permute-done), kind=kLoop, calls=%fused_computation.177 | loop fusion | bytes 1048576 | tf_op jit(solution)/shard_map/slice | solution.py:88
  39.1 1.9 %fusion.40 = (bf16[1,128,1024]{1,2,0:T(8,128)(2,1)}, bf16[1,128,1024]{1,2,0:T(8,128)(2,1)}) fusion(bf16[2,128,1024]{1,2,0:T(8,128)(2,1)} %collective-permute-done.3), kind=kLoop, calls=%fused_computation.174 | loop fusion | bytes 1048576 | tf_op jit(solution)/shard_map/slice | solution.py:88
  42.1 3.1 %collective-permute-done.1 = bf16[2,128,1024]{1,2,0:T(8,128)(2,1)} collective-permute-done((bf16[2,128,1024]{1,2,0:T(8,128)(2,1)}, bf16[2,128,1024]{1,2,0:T(8,128)(2,1)}, u32[]{:S(2)}, u32[]{:S(2)}) %collective-permute-start.1) | collective-permute-done | bytes 524320 | tf_op jit(solution)/shard_map/ppermute | solution.py:17
  45.2 1.9 %fusion.42 = (bf16[1,128,1024]{1,2,0:T(8,128)(2,1)}, bf16[1,128,1024]{1,2,0:T(8,128)(2,1)}) fusion(bf16[2,128,1024]{1,2,0:T(8,128)(2,1)} %collective-permute-done.1), kind=kLoop, calls=%fused_computation.176 | loop fusion | bytes 1048576 | tf_op jit(solution)/shard_map/slice | solution.py:88
  54.2 3.2 %collective-permute-start.6 = (bf16[2,128,1024]{1,2,0:T(8,128)(2,1)}, bf16[2,128,1024]{1,2,0:T(8,128)(2,1)}, u32[]{:S(2)}, u32[]{:S(2)}) collective-permute-start(bf16[2,128,1024]{1,2,0:T(8,128)(2,1)} %pad_maximum_fusion.5), channel_id=1, source_target_pairs={{0,4},{1,5},{2,6},{3,7},{4,8},{5,9},{6,10},{7,11},{8,12},{9,13},{1... | collective-permute-start | bytes 1572872 | tf_op jit(solution)/shard_map/ppermute | solution.py:17
  57.4 5.6 %collective-permute-start.4 = (bf16[2,128,1024]{1,2,0:T(8,128)(2,1)}, bf16[2,128,1024]{1,2,0:T(8,128)(2,1)}, u32[]{:S(2)}, u32[]{:S(2)}) collective-permute-start(bf16[2,128,1024]{1,2,0:T(8,128)(2,1)} %pad_maximum_fusion.5), channel_id=1, source_target_pairs={{0,1},{1,2},{2,3},{3,4},{4,5},{5,6},{6,7},{7,8},{8,9},{9,10},{10,1... | collective-permute-start | bytes 1572872 | tf_op jit(solution)/shard_map/ppermute | solution.py:17
  70.7 2.0 %collective-permute-start.9 = (bf16[2,128,8,128]{1,3,2,0:T(8,128)(2,1)}, bf16[2,128,8,128]{1,3,2,0:T(8,128)(2,1)}, u32[]{:S(2)}, u32[]{:S(2)}) collective-permute-start(bf16[2,128,8,128]{1,3,2,0:T(8,128)(2,1)} %pad_maximum_fusion.9), channel_id=1, source_target_pairs={{2,0},{3,1},{4,2},{5,3},{6,4},{7,5},{8,6},{9,7},{10,8},{11,9},{12,... | collective-permute-start | bytes 1572872 | tf_op jit(solution)/shard_map/ppermute | solution.py:17
  72.7 1.8 pad_maximum_fusion.10
  74.6 2.1 %collective-permute-start.10 = (bf16[2,128,8,128]{1,3,2,0:T(8,128)(2,1)}, bf16[2,128,8,128]{1,3,2,0:T(8,128)(2,1)}, u32[]{:S(2)}, u32[]{:S(2)}) collective-permute-start(bf16[2,128,8,128]{1,3,2,0:T(8,128)(2,1)} %pad_maximum_fusion.10), channel_id=1, source_target_pairs={{4,0},{5,1},{6,2},{7,3},{8,4},{9,5},{10,6},{11,7},{12,8},{13,9},{1... | collective-permute-start | bytes 1572872 | tf_op jit(solution)/shard_map/ppermute | solution.py:17
  80.4 1.8 copy.112
  82.3 2.7 %convolution_bitcast_fusion.1 = f32[128,8,128]{0,2,1:T(8,128)} fusion(bf16[5,128,8,128]{3,1,0,2:T(8,128)(2,1)S(1)} %constant_dynamic-update-slice_fusion.5, bf16[1,8,128,5,128]{2,4,3,1,0:T(8,128)(2,1)} %copy-done), kind=kOutput, calls=%fused_computation.33 | convolution fusion | flops 167772160 | bytes 3145728 | tf_op jit(solution)/shard_map/bhtnu,bnuhd->bthd/dot_general | solution.py:111
  85.0 4.0 %collective-permute-start.7 = (bf16[2,128,1024]{1,2,0:T(8,128)(2,1)}, bf16[2,128,1024]{1,2,0:T(8,128)(2,1)}, u32[]{:S(2)}, u32[]{:S(2)}) collective-permute-start(bf16[2,128,1024]{1,2,0:T(8,128)(2,1)} %collective-permute-done.6), channel_id=1, source_target_pairs={{0,4},{1,5},{2,6},{3,7},{4,8},{5,9},{6,10},{7,11},{8,12},{9,13},{1... | collective-permute-start | bytes 1572872 | tf_op jit(solution)/shard_map/ppermute | solution.py:17
  89.0 1.8 %fusion.37 = (bf16[1,128,1024]{1,2,0:T(8,128)(2,1)}, bf16[1,128,1024]{1,2,0:T(8,128)(2,1)}) fusion(bf16[2,128,1024]{1,2,0:T(8,128)(2,1)} %collective-permute-done.6), kind=kLoop, calls=%fused_computation.171 | loop fusion | bytes 1048576 | tf_op jit(solution)/shard_map/slice | solution.py:88
  90.8 3.8 %collective-permute-start.5 = (bf16[2,128,1024]{1,2,0:T(8,128)(2,1)}, bf16[2,128,1024]{1,2,0:T(8,128)(2,1)}, u32[]{:S(2)}, u32[]{:S(2)}) collective-permute-start(bf16[2,128,1024]{1,2,0:T(8,128)(2,1)} %collective-permute-done.4), channel_id=1, source_target_pairs={{0,1},{1,2},{2,3},{3,4},{4,5},{5,6},{6,7},{7,8},{8,9},{9,10},{10,1... | collective-permute-start | bytes 1572872 | tf_op jit(solution)/shard_map/ppermute | solution.py:17
  94.7 1.9 %fusion.39 = (bf16[1,128,1024]{1,2,0:T(8,128)(2,1)}, bf16[1,128,1024]{1,2,0:T(8,128)(2,1)}) fusion(bf16[2,128,1024]{1,2,0:T(8,128)(2,1)} %collective-permute-done.4), kind=kLoop, calls=%fused_computation.173 | loop fusion | bytes 1048576 | tf_op jit(solution)/shard_map/slice | solution.py:88
  101.4 3.2 %collective-permute-start.8 = (bf16[2,128,8,128]{1,3,2,0:T(8,128)(2,1)}, bf16[2,128,8,128]{1,3,2,0:T(8,128)(2,1)}, u32[]{:S(2)}, u32[]{:S(2)}) collective-permute-start(bf16[2,128,8,128]{1,3,2,0:T(8,128)(2,1)} %pad_maximum_fusion.8), channel_id=1, source_target_pairs={{1,0},{2,1},{3,2},{4,3},{5,4},{6,5},{7,6},{8,7},{9,8},{10,9},{11,1... | collective-permute-start | bytes 1572872 | tf_op jit(solution)/shard_map/ppermute | solution.py:17
  104.6 1.9 %fusion.36 = (bf16[1,128,1024]{1,2,0:T(8,128)(2,1)}, bf16[1,128,1024]{1,2,0:T(8,128)(2,1)}) fusion(bf16[2,128,1024]{1,2,0:T(8,128)(2,1)} %collective-permute-done.7), kind=kLoop, calls=%fused_computation.170 | loop fusion | bytes 1048576 | tf_op jit(solution)/shard_map/slice | solution.py:88
  108.3 1.9 %fusion.38 = (bf16[1,128,1024]{1,2,0:T(8,128)(2,1)}, bf16[1,128,1024]{1,2,0:T(8,128)(2,1)}) fusion(bf16[2,128,1024]{1,2,0:T(8,128)(2,1)} %collective-permute-done.5), kind=kLoop, calls=%fused_computation.172 | loop fusion | bytes 1048576 | tf_op jit(solution)/shard_map/slice | solution.py:88
  123.2 1.9 %collective-permute-start.13 = (bf16[2,128,8,128]{1,3,2,0:T(8,128)(2,1)}, bf16[2,128,8,128]{1,3,2,0:T(8,128)(2,1)}, u32[]{:S(2)}, u32[]{:S(2)}) collective-permute-start(bf16[2,128,8,128]{1,3,2,0:T(8,128)(2,1)} %pad_maximum_fusion.13), channel_id=1, source_target_pairs={{2,0},{3,1},{4,2},{5,3},{6,4},{7,5},{8,6},{9,7},{10,8},{11,9},{12,... | collective-permute-start | bytes 1572872 | tf_op jit(solution)/shard_map/ppermute | solution.py:17
  127.7 1.9 %collective-permute-start.14 = (bf16[2,128,8,128]{1,3,2,0:T(8,128)(2,1)}, bf16[2,128,8,128]{1,3,2,0:T(8,128)(2,1)}, u32[]{:S(2)}, u32[]{:S(2)}) collective-permute-start(bf16[2,128,8,128]{1,3,2,0:T(8,128)(2,1)} %pad_maximum_fusion.14), channel_id=1, source_target_pairs={{4,0},{5,1},{6,2},{7,3},{8,4},{9,5},{10,6},{11,7},{12,8},{13,9},{1... | collective-permute-start | bytes 1572872 | tf_op jit(solution)/shard_map/ppermute | solution.py:17
  130.9 2.2 %collective-permute-start.12 = (bf16[2,128,8,128]{1,3,2,0:T(8,128)(2,1)}, bf16[2,128,8,128]{1,3,2,0:T(8,128)(2,1)}, u32[]{:S(2)}, u32[]{:S(2)}) collective-permute-start(bf16[2,128,8,128]{1,3,2,0:T(8,128)(2,1)} %pad_maximum_fusion.12), channel_id=1, source_target_pairs={{1,0},{2,1},{3,2},{4,3},{5,4},{6,5},{7,6},{8,7},{9,8},{10,9},{11,1... | collective-permute-start | bytes 1572872 | tf_op jit(solution)/shard_map/ppermute | solution.py:17
  133.2 2.6 %fusion.27 = (bf16[128,8,128]{0,2,1:T(8,128)(2,1)}, f32[128,8,128]{0,2,1:T(8,128)S(1)}) fusion(bf16[128,8,128]{0,2,1:T(8,128)(2,1)S(1)} %copy-done.19, bf16[2,128,8,128]{1,3,2,0:T(8,128)(2,1)} %collective-permute-done.11, bf16[2,128,8,128]{1,3,2,0:T(8,128)(2,1)} %collective-permute-done.10, bf16[2,128,8,128]{1,3,2,0:T(8,128)(2,1)} %collective-permute-done.9, ...), kind=kLoop, calls=%fused_computation.70 | loop fusion | flops 2490368 | bytes 3407872 | tf_op jit(solution)/shard_map/convert.23
  138.4 1.9 %pad_maximum_fusion.6 = bf16[128,2048]{1,0:T(8,128)(2,1)} fusion(bf16[128,1024]{1,0:T(8,128)(2,1)} %copy.113, bf16[128,1024]{1,0:T(8,128)(2,1)} %copy.112), kind=kLoop, calls=%fused_computation.52 | loop fusion | flops 1048576 | bytes 1048576 | tf_op jit(solution)/shard_map/concatenate | solution.py:177
  141.7 2.5 %collective-permute-done.14 = bf16[2,128,8,128]{1,3,2,0:T(8,128)(2,1)} collective-permute-done((bf16[2,128,8,128]{1,3,2,0:T(8,128)(2,1)}, bf16[2,128,8,128]{1,3,2,0:T(8,128)(2,1)}, u32[]{:S(2)}, u32[]{:S(2)}) %collective-permute-start.14) | collective-permute-done | bytes 524320 | tf_op jit(solution)/shard_map/ppermute | solution.py:17
  144.2 13.6 %collective-permute-done.15 = bf16[2,128,8,128]{1,3,2,0:T(8,128)(2,1)} collective-permute-done((bf16[2,128,8,128]{1,3,2,0:T(8,128)(2,1)}, bf16[2,128,8,128]{1,3,2,0:T(8,128)(2,1)}, u32[]{:S(2)}, u32[]{:S(2)}) %collective-permute-start.15) | collective-permute-done | bytes 524320 | tf_op jit(solution)/shard_map/ppermute | solution.py:17
  157.8 21.6 %collective-permute-done.12 = bf16[2,128,8,128]{1,3,2,0:T(8,128)(2,1)} collective-permute-done((bf16[2,128,8,128]{1,3,2,0:T(8,128)(2,1)}, bf16[2,128,8,128]{1,3,2,0:T(8,128)(2,1)}, u32[]{:S(2)}, u32[]{:S(2)}) %collective-permute-start.12) | collective-permute-done | bytes 524320 | tf_op jit(solution)/shard_map/ppermute | solution.py:17
  179.3 1.9 %fusion.26 = (bf16[128,8,128]{0,2,1:T(8,128)(2,1)S(1)}, f32[128,8,128]{0,2,1:T(8,128)S(1)}) fusion(bf16[128,8,128]{0,2,1:T(8,128)(2,1)S(1)} %copy-done.22, bf16[2,128,8,128]{1,3,2,0:T(8,128)(2,1)} %collective-permute-done.15, bf16[2,128,8,128]{1,3,2,0:T(8,128)(2,1)} %collective-permute-done.14, bf16[2,128,8,128]{1,3,2,0:T(8,128)(2,1)} %collective-permute-done.13, ...), kind=kLoop, calls=%fused_computation.65 | loop fusion | flops 2490368 | bytes 3407872 | tf_op jit(solution)/shard_map/convert.22
  (165 shorter events, 66.3 us)
Async XLA Ops:
  0.6 3.1 %copy-start.23 = (bf16[128,2048]{1,0:T(8,128)(2,1)S(1)}, bf16[128,2048]{1,0:T(8,128)(2,1)}, u32[]{:S(2)}) copy-start(bf16[128,2048]{1,0:T(8,128)(2,1)} %param.7) | copy-start | bytes 1572868
  6.6 8.8 %copy-start.24 = (bf16[128,2048]{1,0:T(8,128)(2,1)S(1)}, bf16[128,2048]{1,0:T(8,128)(2,1)}, u32[]{:S(2)}) copy-start(bf16[128,2048]{1,0:T(8,128)(2,1)} %param.10) | copy-start | bytes 1572868
  6.6 8.8 %copy-start.25 = (s32[4]{0:T(128)S(1)}, s32[4]{0:T(128)}, u32[]{:S(2)}) copy-start(s32[4]{0:T(128)} %constant.35) | copy-start | bytes 52
  7.5 15.0 %collective-permute-start.2 = (bf16[2,128,1024]{1,2,0:T(8,128)(2,1)}, bf16[2,128,1024]{1,2,0:T(8,128)(2,1)}, u32[]{:S(2)}, u32[]{:S(2)}) collective-permute-start(bf16[2,128,1024]{1,2,0:T(8,128)(2,1)} %pad_maximum_fusion.3), channel_id=1, source_target_pairs={{0,4},{1,5},{2,6},{3,7},{4,8},{5,9},{6,10},{7,11},{8,12},{9,13},{1... | collective-permute-start | bytes 1572872 | tf_op jit(solution)/shard_map/ppermute | solution.py:17
  10.7 17.7 %collective-permute-start = (bf16[2,128,1024]{1,2,0:T(8,128)(2,1)}, bf16[2,128,1024]{1,2,0:T(8,128)(2,1)}, u32[]{:S(2)}, u32[]{:S(2)}) collective-permute-start(bf16[2,128,1024]{1,2,0:T(8,128)(2,1)} %pad_maximum_fusion.3), channel_id=1, source_target_pairs={{0,1},{1,2},{2,3},{3,4},{4,5},{5,6},{6,7},{7,8},{8,9},{9,10},{10,1... | collective-permute-start | bytes 1572872 | tf_op jit(solution)/shard_map/ppermute | solution.py:17
  22.5 16.6 %collective-permute-start.3 = (bf16[2,128,1024]{1,2,0:T(8,128)(2,1)}, bf16[2,128,1024]{1,2,0:T(8,128)(2,1)}, u32[]{:S(2)}, u32[]{:S(2)}) collective-permute-start(bf16[2,128,1024]{1,2,0:T(8,128)(2,1)} %collective-permute-done.2), channel_id=1, source_target_pairs={{0,4},{1,5},{2,6},{3,7},{4,8},{5,9},{6,10},{7,11},{8,12},{9,13},{1... | collective-permute-start | bytes 1572872 | tf_op jit(solution)/shard_map/ppermute | solution.py:17
  28.4 16.9 %collective-permute-start.1 = (bf16[2,128,1024]{1,2,0:T(8,128)(2,1)}, bf16[2,128,1024]{1,2,0:T(8,128)(2,1)}, u32[]{:S(2)}, u32[]{:S(2)}) collective-permute-start(bf16[2,128,1024]{1,2,0:T(8,128)(2,1)} %collective-permute-done), channel_id=1, source_target_pairs={{0,1},{1,2},{2,3},{3,4},{4,5},{5,6},{6,7},{7,8},{8,9},{9,10},{10,1... | collective-permute-start | bytes 1572872 | tf_op jit(solution)/shard_map/ppermute | solution.py:17
  51.4 1.5 copy-start.16
  53.4 11.3 %copy-start.1 = (bf16[1,128,8,128]{1,3,2,0:T(8,128)(2,1)}, bf16[1,128,8,128]{1,3,2,0:T(8,128)(2,1)S(1)}, u32[]{:S(2)}) copy-start(bf16[1,128,8,128]{1,3,2,0:T(8,128)(2,1)S(1)} %fusion.23) | copy-start | bytes 786436
  54.2 30.7 %collective-permute-start.6 = (bf16[2,128,1024]{1,2,0:T(8,128)(2,1)}, bf16[2,128,1024]{1,2,0:T(8,128)(2,1)}, u32[]{:S(2)}, u32[]{:S(2)}) collective-permute-start(bf16[2,128,1024]{1,2,0:T(8,128)(2,1)} %pad_maximum_fusion.5), channel_id=1, source_target_pairs={{0,4},{1,5},{2,6},{3,7},{4,8},{5,9},{6,10},{7,11},{8,12},{9,13},{1... | collective-permute-start | bytes 1572872 | tf_op jit(solution)/shard_map/ppermute | solution.py:17
  57.4 33.4 %collective-permute-start.4 = (bf16[2,128,1024]{1,2,0:T(8,128)(2,1)}, bf16[2,128,1024]{1,2,0:T(8,128)(2,1)}, u32[]{:S(2)}, u32[]{:S(2)}) collective-permute-start(bf16[2,128,1024]{1,2,0:T(8,128)(2,1)} %pad_maximum_fusion.5), channel_id=1, source_target_pairs={{0,1},{1,2},{2,3},{3,4},{4,5},{5,6},{6,7},{7,8},{8,9},{9,10},{10,1... | collective-permute-start | bytes 1572872 | tf_op jit(solution)/shard_map/ppermute | solution.py:17
  67.0 1.9 %copy-start.10 = (bf16[1,128,8,128]{1,3,2,0:T(8,128)(2,1)S(1)}, bf16[1,128,8,128]{1,3,2,0:T(8,128)(2,1)}, u32[]{:S(2)}) copy-start(bf16[1,128,8,128]{1,3,2,0:T(8,128)(2,1)} %get-tuple-element.27) | copy-start | bytes 786436
  70.7 8.1 %copy-start.11 = (bf16[1,128,8,128]{3,1,0,2:T(8,128)(2,1)S(1)}, bf16[1,128,8,128]{3,1,0,2:T(8,128)(2,1)}, u32[]{:S(2)}) copy-start(bf16[1,128,8,128]{3,1,0,2:T(8,128)(2,1)} %copy.105) | copy-start | bytes 786436
  70.7 57.0 %collective-permute-start.9 = (bf16[2,128,8,128]{1,3,2,0:T(8,128)(2,1)}, bf16[2,128,8,128]{1,3,2,0:T(8,128)(2,1)}, u32[]{:S(2)}, u32[]{:S(2)}) collective-permute-start(bf16[2,128,8,128]{1,3,2,0:T(8,128)(2,1)} %pad_maximum_fusion.9), channel_id=1, source_target_pairs={{2,0},{3,1},{4,2},{5,3},{6,4},{7,5},{8,6},{9,7},{10,8},{11,9},{12,... | collective-permute-start | bytes 1572872 | tf_op jit(solution)/shard_map/ppermute | solution.py:17
  72.7 6.1 %copy-start.8 = (bf16[1,128,8,128]{1,3,2,0:T(8,128)(2,1)S(1)}, bf16[1,128,8,128]{1,3,2,0:T(8,128)(2,1)}, u32[]{:S(2)}) copy-start(bf16[1,128,8,128]{1,3,2,0:T(8,128)(2,1)} %get-tuple-element.28) | copy-start | bytes 786436
  72.7 6.1 %copy-start.9 = (bf16[1,128,8,128]{1,3,2,0:T(8,128)(2,1)S(1)}, bf16[1,128,8,128]{1,3,2,0:T(8,128)(2,1)}, u32[]{:S(2)}) copy-start(bf16[1,128,8,128]{1,3,2,0:T(8,128)(2,1)} %get-tuple-element.34) | copy-start | bytes 786436
  74.6 55.0 %collective-permute-start.10 = (bf16[2,128,8,128]{1,3,2,0:T(8,128)(2,1)}, bf16[2,128,8,128]{1,3,2,0:T(8,128)(2,1)}, u32[]{:S(2)}, u32[]{:S(2)}) collective-permute-start(bf16[2,128,8,128]{1,3,2,0:T(8,128)(2,1)} %pad_maximum_fusion.10), channel_id=1, source_target_pairs={{4,0},{5,1},{6,2},{7,3},{8,4},{9,5},{10,6},{11,7},{12,8},{13,9},{1... | collective-permute-start | bytes 1572872 | tf_op jit(solution)/shard_map/ppermute | solution.py:17
  77.5 53.4 %collective-permute-start.11 = (bf16[2,128,8,128]{1,3,2,0:T(8,128)(2,1)}, bf16[2,128,8,128]{1,3,2,0:T(8,128)(2,1)}, u32[]{:S(2)}, u32[]{:S(2)}) collective-permute-start(bf16[2,128,8,128]{1,3,2,0:T(8,128)(2,1)} %pad_maximum_fusion.11), channel_id=1, source_target_pairs={{8,0},{9,1},{10,2},{11,3},{12,4},{13,5},{14,6},{15,7},{24,16},{25,... | collective-permute-start | bytes 1572872 | tf_op jit(solution)/shard_map/ppermute | solution.py:17
  85.0 16.5 %collective-permute-start.7 = (bf16[2,128,1024]{1,2,0:T(8,128)(2,1)}, bf16[2,128,1024]{1,2,0:T(8,128)(2,1)}, u32[]{:S(2)}, u32[]{:S(2)}) collective-permute-start(bf16[2,128,1024]{1,2,0:T(8,128)(2,1)} %collective-permute-done.6), channel_id=1, source_target_pairs={{0,4},{1,5},{2,6},{3,7},{4,8},{5,9},{6,10},{7,11},{8,12},{9,13},{1... | collective-permute-start | bytes 1572872 | tf_op jit(solution)/shard_map/ppermute | solution.py:17
  90.8 9.6 %copy-start.5 = (bf16[5,128,8,128]{1,3,0,2:T(8,128)(2,1)S(1)}, bf16[5,128,8,128]{1,3,0,2:T(8,128)(2,1)}, u32[]{:S(2)}) copy-start(bf16[5,128,8,128]{1,3,0,2:T(8,128)(2,1)} %constant_dynamic-update-slice_fusion.14) | copy-start | bytes 3932164
  90.8 17.5 %collective-permute-start.5 = (bf16[2,128,1024]{1,2,0:T(8,128)(2,1)}, bf16[2,128,1024]{1,2,0:T(8,128)(2,1)}, u32[]{:S(2)}, u32[]{:S(2)}) collective-permute-start(bf16[2,128,1024]{1,2,0:T(8,128)(2,1)} %collective-permute-done.4), channel_id=1, source_target_pairs={{0,1},{1,2},{2,3},{3,4},{4,5},{5,6},{6,7},{7,8},{8,9},{9,10},{10,1... | collective-permute-start | bytes 1572872 | tf_op jit(solution)/shard_map/ppermute | solution.py:17
  101.4 31.7 %collective-permute-start.8 = (bf16[2,128,8,128]{1,3,2,0:T(8,128)(2,1)}, bf16[2,128,8,128]{1,3,2,0:T(8,128)(2,1)}, u32[]{:S(2)}, u32[]{:S(2)}) collective-permute-start(bf16[2,128,8,128]{1,3,2,0:T(8,128)(2,1)} %pad_maximum_fusion.8), channel_id=1, source_target_pairs={{1,0},{2,1},{3,2},{4,3},{5,4},{6,5},{7,6},{8,7},{9,8},{10,9},{11,1... | collective-permute-start | bytes 1572872 | tf_op jit(solution)/shard_map/ppermute | solution.py:17
  123.2 18.5 %collective-permute-start.13 = (bf16[2,128,8,128]{1,3,2,0:T(8,128)(2,1)}, bf16[2,128,8,128]{1,3,2,0:T(8,128)(2,1)}, u32[]{:S(2)}, u32[]{:S(2)}) collective-permute-start(bf16[2,128,8,128]{1,3,2,0:T(8,128)(2,1)} %pad_maximum_fusion.13), channel_id=1, source_target_pairs={{2,0},{3,1},{4,2},{5,3},{6,4},{7,5},{8,6},{9,7},{10,8},{11,9},{12,... | collective-permute-start | bytes 1572872 | tf_op jit(solution)/shard_map/ppermute | solution.py:17
  126.0 7.2 %copy-start.19 = (bf16[128,8,128]{0,2,1:T(8,128)(2,1)S(1)}, bf16[128,8,128]{0,2,1:T(8,128)(2,1)}, u32[]{:S(2)}) copy-start(bf16[128,8,128]{0,2,1:T(8,128)(2,1)} %get-tuple-element.24) | copy-start | bytes 786436
  126.0 7.2 %copy-start.20 = (bf16[128,8,128]{0,2,1:T(8,128)(2,1)S(1)}, bf16[128,8,128]{0,2,1:T(8,128)(2,1)}, u32[]{:S(2)}) copy-start(bf16[128,8,128]{0,2,1:T(8,128)(2,1)} %get-tuple-element.38) | copy-start | bytes 786436
  127.7 16.5 %collective-permute-start.14 = (bf16[2,128,8,128]{1,3,2,0:T(8,128)(2,1)}, bf16[2,128,8,128]{1,3,2,0:T(8,128)(2,1)}, u32[]{:S(2)}, u32[]{:S(2)}) collective-permute-start(bf16[2,128,8,128]{1,3,2,0:T(8,128)(2,1)} %pad_maximum_fusion.14), channel_id=1, source_target_pairs={{4,0},{5,1},{6,2},{7,3},{8,4},{9,5},{10,6},{11,7},{12,8},{13,9},{1... | collective-permute-start | bytes 1572872 | tf_op jit(solution)/shard_map/ppermute | solution.py:17
  129.6 28.2 %collective-permute-start.15 = (bf16[2,128,8,128]{1,3,2,0:T(8,128)(2,1)}, bf16[2,128,8,128]{1,3,2,0:T(8,128)(2,1)}, u32[]{:S(2)}, u32[]{:S(2)}) collective-permute-start(bf16[2,128,8,128]{1,3,2,0:T(8,128)(2,1)} %pad_maximum_fusion.15), channel_id=1, source_target_pairs={{8,0},{9,1},{10,2},{11,3},{12,4},{13,5},{14,6},{15,7},{24,16},{25,... | collective-permute-start | bytes 1572872 | tf_op jit(solution)/shard_map/ppermute | solution.py:17
  130.9 48.4 %collective-permute-start.12 = (bf16[2,128,8,128]{1,3,2,0:T(8,128)(2,1)}, bf16[2,128,8,128]{1,3,2,0:T(8,128)(2,1)}, u32[]{:S(2)}, u32[]{:S(2)}) collective-permute-start(bf16[2,128,8,128]{1,3,2,0:T(8,128)(2,1)} %pad_maximum_fusion.12), channel_id=1, source_target_pairs={{1,0},{2,1},{3,2},{4,3},{5,4},{6,5},{7,6},{8,7},{9,8},{10,9},{11,1... | collective-permute-start | bytes 1572872 | tf_op jit(solution)/shard_map/ppermute | solution.py:17
  140.3 39.1 %copy-start.21 = (bf16[128,8,128]{0,2,1:T(8,128)(2,1)S(1)}, bf16[128,8,128]{0,2,1:T(8,128)(2,1)}, u32[]{:S(2)}) copy-start(bf16[128,8,128]{0,2,1:T(8,128)(2,1)} %get-tuple-element.43) | copy-start | bytes 786436
  140.3 39.1 %copy-start.22 = (bf16[128,8,128]{0,2,1:T(8,128)(2,1)S(1)}, bf16[128,8,128]{0,2,1:T(8,128)(2,1)}, u32[]{:S(2)}) copy-start(bf16[128,8,128]{0,2,1:T(8,128)(2,1)} %get-tuple-element.29) | copy-start | bytes 786436
  141.7 39.7 %copy-start.2 = (f32[128,8,128]{0,2,1:T(8,128)S(1)}, f32[128,8,128]{0,2,1:T(8,128)}, u32[]{:S(2)}) copy-start(f32[128,8,128]{0,2,1:T(8,128)} %convolution_bitcast_fusion.1) | copy-start | bytes 1572868
  141.7 39.8 %copy-start.3 = (f32[128,8,128]{0,2,1:T(8,128)S(1)}, f32[128,8,128]{0,2,1:T(8,128)}, u32[]{:S(2)}) copy-start(f32[128,8,128]{0,2,1:T(8,128)} %convolution_bitcast_fusion) | copy-start | bytes 1572868
  (10 other events, 11.6 us)

commit v7 on v6

--- a/solution.py
+++ b/solution.py
@@ -8,7 +8,7 @@
 HEADS = 16
 HEAD_DIM = 128
 BLOCK = 128
-CHUNKS = 2
+CHUNKS = 4
 
 
 def from_behind(value, axis, steps):

time: 186 us -> 228 us (1.23)
  starting transfers between devices: 48.2 us -> 92.5 us
  other arithmetic: 23.8 us -> 33.6 us
  local copies, waits for them, and re-layouts: 53.2 us -> 43.6 us
  waiting for transfers between devices: 46.5 us -> 40.3 us
    ppermute x16 -> x32, starting transfers between devices: 48.2 us -> 92.5 us  [from_behind(): lax.ppermute(value, axis, [(source, source + steps) for source in range(l...]
    another operation x8 -> x16, other arithmetic: 8.69 us -> 17.5 us  [attend_chunk(): jnp.stack([key_terms[0, slot_index], value_terms[0, slot_index]])]
    unnamed x73 -> x131, local copies, waits for them, and re-layouts: 12.9 us -> 5.42 us
    another operation x12 -> x24, local copies, waits for them, and re-layouts: 12.7 us -> 6.36 us  [attend_chunk(): jnp.stack([moved[0].reshape(head_shape) for moved in received])[None]]
    ppermute x16 -> x32, waiting for transfers between devices: 46.5 us -> 40.3 us  [from_behind(): lax.ppermute(value, axis, [(source, source + steps) for source in range(l...]
    slice x8 -> x16, local copies, waits for them, and re-layouts: 14.7 us -> 16.2 us  [attend_chunk(): moved[0].reshape(head_shape)]
    another operation x6 -> x8, other arithmetic: 5.35 us -> 6.58 us
  transfers between devices with their start and end apart: 16 -> 32, of which waited for: 7 -> 7; matrix products, arithmetic and copies ran while one was open for 35% -> 26% of each run, Pallas kernels for 0% -> 0%
where the time goes in v7:
time: 228 us; the launch traced here: 225 us
  starting transfers between devices  92.5 us (41%)
  local copies, waits for them, and re-layouts  43.6 us (19%)
  waiting for transfers between devices  40.3 us (18%)
  other arithmetic  33.6 us (15%)
  matrix products  12.3 us (5%)
  between operations  2.94 us (1%)
    ppermute x32, starting transfers between devices, from_behind(): lax.ppermute(value, axis, [(source, source + steps) for source in range(l...  92.5 us
    ppermute x32, waiting for transfers between devices, from_behind(): lax.ppermute(value, axis, [(source, source + steps) for source in range(l...  40.3 us
    another operation x16, other arithmetic, attend_chunk(): jnp.stack([key_terms[0, slot_index], value_terms[0, slot_index]])  17.5 us
    slice x16, local copies, waits for them, and re-layouts, attend_chunk(): moved[0].reshape(head_shape)  16.2 us
    another operation x8, other arithmetic  6.58 us
    another operation x24, local copies, waits for them, and re-layouts, attend_chunk(): jnp.stack([moved[0].reshape(head_shape) for moved in received])[None]  6.36 us
    unnamed x131, local copies, waits for them, and re-layouts  5.42 us
  transfers between devices with their start and end apart: 32, of which 7 were waited for; matrix products, arithmetic and copies ran while one was open for 26% of the time, Pallas kernels for 0%

profile of v7, /device:TPU:15, one launch (start us, length us, event | category | flops | bytes accessed | tf_op | source)
XLA Modules:
  0.0 225.2 jit_solution(6721767341322733474)
XLA Ops:
  5.6 3.2 %collective-permute-start.2 = (bf16[2,128,512]{1,2,0:T(8,128)(2,1)}, bf16[2,128,512]{1,2,0:T(8,128)(2,1)}, u32[]{:S(2)}, u32[]{:S(2)}) collective-permute-start(bf16[2,128,512]{1,2,0:T(8,128)(2,1)} %pad_maximum_fusion.8), channel_id=1, source_target_pairs={{0,4},{1,5},{2,6},{3,7},{4,8},{5,9},{6,10},{7,11},{8,12},{9,13},{1... | collective-permute-start | bytes 786440 | tf_op jit(solution)/shard_map/ppermute | solution.py:17
  8.8 4.0 %collective-permute-start = (bf16[2,128,512]{1,2,0:T(8,128)(2,1)}, bf16[2,128,512]{1,2,0:T(8,128)(2,1)}, u32[]{:S(2)}, u32[]{:S(2)}) collective-permute-start(bf16[2,128,512]{1,2,0:T(8,128)(2,1)} %pad_maximum_fusion.8), channel_id=1, source_target_pairs={{0,1},{1,2},{2,3},{3,4},{4,5},{5,6},{6,7},{7,8},{8,9},{9,10},{10,1... | collective-permute-start | bytes 786440 | tf_op jit(solution)/shard_map/ppermute | solution.py:17
  16.4 1.9 collective-permute-start.3
  20.4 4.8 %collective-permute-start.1 = (bf16[2,128,512]{1,2,0:T(8,128)(2,1)}, bf16[2,128,512]{1,2,0:T(8,128)(2,1)}, u32[]{:S(2)}, u32[]{:S(2)}) collective-permute-start(bf16[2,128,512]{1,2,0:T(8,128)(2,1)} %collective-permute-done), channel_id=1, source_target_pairs={{0,1},{1,2},{2,3},{3,4},{4,5},{5,6},{6,7},{7,8},{8,9},{9,10},{10,1... | collective-permute-start | bytes 786440 | tf_op jit(solution)/shard_map/ppermute | solution.py:17
  26.5 2.3 %collective-permute-done.1 = bf16[2,128,512]{1,2,0:T(8,128)(2,1)} collective-permute-done((bf16[2,128,512]{1,2,0:T(8,128)(2,1)}, bf16[2,128,512]{1,2,0:T(8,128)(2,1)}, u32[]{:S(2)}, u32[]{:S(2)}) %collective-permute-start.1) | collective-permute-done | bytes 262176 | tf_op jit(solution)/shard_map/ppermute | solution.py:17
  34.5 2.5 %collective-permute-start.6 = (bf16[2,128,512]{1,2,0:T(8,128)(2,1)}, bf16[2,128,512]{1,2,0:T(8,128)(2,1)}, u32[]{:S(2)}, u32[]{:S(2)}) collective-permute-start(bf16[2,128,512]{1,2,0:T(8,128)(2,1)} %pad_maximum_fusion.9), channel_id=1, source_target_pairs={{0,4},{1,5},{2,6},{3,7},{4,8},{5,9},{6,10},{7,11},{8,12},{9,13},{1... | collective-permute-start | bytes 786440 | tf_op jit(solution)/shard_map/ppermute | solution.py:17
  37.0 5.6 %collective-permute-start.4 = (bf16[2,128,512]{1,2,0:T(8,128)(2,1)}, bf16[2,128,512]{1,2,0:T(8,128)(2,1)}, u32[]{:S(2)}, u32[]{:S(2)}) collective-permute-start(bf16[2,128,512]{1,2,0:T(8,128)(2,1)} %pad_maximum_fusion.9), channel_id=1, source_target_pairs={{0,1},{1,2},{2,3},{3,4},{4,5},{5,6},{6,7},{7,8},{8,9},{9,10},{10,1... | collective-permute-start | bytes 786440 | tf_op jit(solution)/shard_map/ppermute | solution.py:17
  49.4 3.1 %collective-permute-start.17 = (bf16[2,128,4,128]{1,3,2,0:T(8,128)(2,1)}, bf16[2,128,4,128]{1,3,2,0:T(8,128)(2,1)}, u32[]{:S(2)}, u32[]{:S(2)}) collective-permute-start(bf16[2,128,4,128]{1,3,2,0:T(8,128)(2,1)} %pad_maximum_fusion.13), channel_id=1, source_target_pairs={{2,0},{3,1},{4,2},{5,3},{6,4},{7,5},{8,6},{9,7},{10,8},{11,9},{12,... | collective-permute-start | bytes 786440 | tf_op jit(solution)/shard_map/ppermute | solution.py:17
  54.1 2.7 %collective-permute-start.18 = (bf16[2,128,4,128]{1,3,2,0:T(8,128)(2,1)}, bf16[2,128,4,128]{1,3,2,0:T(8,128)(2,1)}, u32[]{:S(2)}, u32[]{:S(2)}) collective-permute-start(bf16[2,128,4,128]{1,3,2,0:T(8,128)(2,1)} %pad_maximum_fusion.14), channel_id=1, source_target_pairs={{4,0},{5,1},{6,2},{7,3},{8,4},{9,5},{10,6},{11,7},{12,8},{13,9},{1... | collective-permute-start | bytes 786440 | tf_op jit(solution)/shard_map/ppermute | solution.py:17
  64.5 3.8 %collective-permute-start.7 = (bf16[2,128,512]{1,2,0:T(8,128)(2,1)}, bf16[2,128,512]{1,2,0:T(8,128)(2,1)}, u32[]{:S(2)}, u32[]{:S(2)}) collective-permute-start(bf16[2,128,512]{1,2,0:T(8,128)(2,1)} %collective-permute-done.6), channel_id=1, source_target_pairs={{0,4},{1,5},{2,6},{3,7},{4,8},{5,9},{6,10},{7,11},{8,12},{9,13},{1... | collective-permute-start | bytes 786440 | tf_op jit(solution)/shard_map/ppermute | solution.py:17
  68.3 4.8 %collective-permute-start.5 = (bf16[2,128,512]{1,2,0:T(8,128)(2,1)}, bf16[2,128,512]{1,2,0:T(8,128)(2,1)}, u32[]{:S(2)}, u32[]{:S(2)}) collective-permute-start(bf16[2,128,512]{1,2,0:T(8,128)(2,1)} %collective-permute-done.4), channel_id=1, source_target_pairs={{0,1},{1,2},{2,3},{3,4},{4,5},{5,6},{6,7},{7,8},{8,9},{9,10},{10,1... | collective-permute-start | bytes 786440 | tf_op jit(solution)/shard_map/ppermute | solution.py:17
  73.2 6.9 %collective-permute-done.16 = bf16[2,128,4,128]{1,3,2,0:T(8,128)(2,1)S(1)} collective-permute-done((bf16[2,128,4,128]{1,3,2,0:T(8,128)(2,1)}, bf16[2,128,4,128]{1,3,2,0:T(8,128)(2,1)S(1)}, u32[]{:S(2)}, u32[]{:S(2)}) %collective-permute-start.16) | collective-permute-done | bytes 262176 | tf_op jit(solution)/shard_map/ppermute | solution.py:17
  89.7 1.9 collective-permute-start.10
  91.6 1.9 collective-permute-start.8
  99.2 1.9 collective-permute-start.21
  102.8 4.0 %collective-permute-start.22 = (bf16[2,128,4,128]{1,3,2,0:T(8,128)(2,1)}, bf16[2,128,4,128]{1,3,2,0:T(8,128)(2,1)}, u32[]{:S(2)}, u32[]{:S(2)}) collective-permute-start(bf16[2,128,4,128]{1,3,2,0:T(8,128)(2,1)} %pad_maximum_fusion.18), channel_id=1, source_target_pairs={{4,0},{5,1},{6,2},{7,3},{8,4},{9,5},{10,6},{11,7},{12,8},{13,9},{1... | collective-permute-start | bytes 786440 | tf_op jit(solution)/shard_map/ppermute | solution.py:17
  111.0 2.7 %collective-permute-start.20 = (bf16[2,128,4,128]{1,3,2,0:T(8,128)(2,1)}, bf16[2,128,4,128]{1,3,2,0:T(8,128)(2,1)}, u32[]{:S(2)}, u32[]{:S(2)}) collective-permute-start(bf16[2,128,4,128]{1,3,2,0:T(8,128)(2,1)} %pad_maximum_fusion.16), channel_id=1, source_target_pairs={{1,0},{2,1},{3,2},{4,3},{5,4},{6,5},{7,6},{8,7},{9,8},{10,9},{11,1... | collective-permute-start | bytes 786440 | tf_op jit(solution)/shard_map/ppermute | solution.py:17
  115.5 3.6 %collective-permute-start.11 = (bf16[2,128,512]{1,2,0:T(8,128)(2,1)}, bf16[2,128,512]{1,2,0:T(8,128)(2,1)S(1)}, u32[]{:S(2)}, u32[]{:S(2)}) collective-permute-start(bf16[2,128,512]{1,2,0:T(8,128)(2,1)} %collective-permute-done.10), channel_id=1, source_target_pairs={{0,4},{1,5},{2,6},{3,7},{4,8},{5,9},{6,10},{7,11},{8,12},{9,13},{1... | collective-permute-start | bytes 786440 | tf_op jit(solution)/shard_map/ppermute | solution.py:17
  119.1 5.3 %collective-permute-start.9 = (bf16[2,128,512]{1,2,0:T(8,128)(2,1)}, bf16[2,128,512]{1,2,0:T(8,128)(2,1)}, u32[]{:S(2)}, u32[]{:S(2)}) collective-permute-start(bf16[2,128,512]{1,2,0:T(8,128)(2,1)} %collective-permute-done.8), channel_id=1, source_target_pairs={{0,1},{1,2},{2,3},{3,4},{4,5},{5,6},{6,7},{7,8},{8,9},{9,10},{10,1... | collective-permute-start | bytes 786440 | tf_op jit(solution)/shard_map/ppermute | solution.py:17
  124.5 5.8 %collective-permute-done.20 = bf16[2,128,4,128]{1,3,2,0:T(8,128)(2,1)} collective-permute-done((bf16[2,128,4,128]{1,3,2,0:T(8,128)(2,1)}, bf16[2,128,4,128]{1,3,2,0:T(8,128)(2,1)}, u32[]{:S(2)}, u32[]{:S(2)}) %collective-permute-start.20) | collective-permute-done | bytes 262176 | tf_op jit(solution)/shard_map/ppermute | solution.py:17
  137.4 1.9 collective-permute-start.14
  139.4 3.0 %collective-permute-start.12 = (bf16[2,128,512]{1,2,0:T(8,128)(2,1)}, bf16[2,128,512]{1,2,0:T(8,128)(2,1)}, u32[]{:S(2)}, u32[]{:S(2)}) collective-permute-start(bf16[2,128,512]{1,2,0:T(8,128)(2,1)} %pad_maximum_fusion.11), channel_id=1, source_target_pairs={{0,1},{1,2},{2,3},{3,4},{4,5},{5,6},{6,7},{7,8},{8,9},{9,10},{10,1... | collective-permute-start | bytes 786440 | tf_op jit(solution)/shard_map/ppermute | solution.py:17
  148.0 1.9 collective-permute-start.25
  151.6 3.0 %collective-permute-start.26 = (bf16[2,128,4,128]{1,3,2,0:T(8,128)(2,1)}, bf16[2,128,4,128]{1,3,2,0:T(8,128)(2,1)}, u32[]{:S(2)}, u32[]{:S(2)}) collective-permute-start(bf16[2,128,4,128]{1,3,2,0:T(8,128)(2,1)} %pad_maximum_fusion.22), channel_id=1, source_target_pairs={{4,0},{5,1},{6,2},{7,3},{8,4},{9,5},{10,6},{11,7},{12,8},{13,9},{1... | collective-permute-start | bytes 786440 | tf_op jit(solution)/shard_map/ppermute | solution.py:17
  157.8 2.7 %collective-permute-start.24 = (bf16[2,128,4,128]{1,3,2,0:T(8,128)(2,1)}, bf16[2,128,4,128]{1,3,2,0:T(8,128)(2,1)}, u32[]{:S(2)}, u32[]{:S(2)}) collective-permute-start(bf16[2,128,4,128]{1,3,2,0:T(8,128)(2,1)} %pad_maximum_fusion.20), channel_id=1, source_target_pairs={{1,0},{2,1},{3,2},{4,3},{5,4},{6,5},{7,6},{8,7},{9,8},{10,9},{11,1... | collective-permute-start | bytes 786440 | tf_op jit(solution)/shard_map/ppermute | solution.py:17
  162.3 3.8 %collective-permute-start.15 = (bf16[2,128,512]{1,2,0:T(8,128)(2,1)}, bf16[2,128,512]{1,2,0:T(8,128)(2,1)}, u32[]{:S(2)}, u32[]{:S(2)}) collective-permute-start(bf16[2,128,512]{1,2,0:T(8,128)(2,1)} %collective-permute-done.14), channel_id=1, source_target_pairs={{0,4},{1,5},{2,6},{3,7},{4,8},{5,9},{6,10},{7,11},{8,12},{9,13},{1... | collective-permute-start | bytes 786440 | tf_op jit(solution)/shard_map/ppermute | solution.py:17
  166.1 5.3 %collective-permute-start.13 = (bf16[2,128,512]{1,2,0:T(8,128)(2,1)}, bf16[2,128,512]{1,2,0:T(8,128)(2,1)}, u32[]{:S(2)}, u32[]{:S(2)}) collective-permute-start(bf16[2,128,512]{1,2,0:T(8,128)(2,1)} %collective-permute-done.12), channel_id=1, source_target_pairs={{0,1},{1,2},{2,3},{3,4},{4,5},{5,6},{6,7},{7,8},{8,9},{9,10},{10,1... | collective-permute-start | bytes 786440 | tf_op jit(solution)/shard_map/ppermute | solution.py:17
  171.5 7.2 %collective-permute-done.24 = bf16[2,128,4,128]{1,3,2,0:T(8,128)(2,1)} collective-permute-done((bf16[2,128,4,128]{1,3,2,0:T(8,128)(2,1)}, bf16[2,128,4,128]{1,3,2,0:T(8,128)(2,1)}, u32[]{:S(2)}, u32[]{:S(2)}) %collective-permute-start.24) | collective-permute-done | bytes 262176 | tf_op jit(solution)/shard_map/ppermute | solution.py:17
  191.7 1.9 collective-permute-start.29
  199.1 2.1 collective-permute-start.28
  203.4 6.8 %collective-permute-done.30 = bf16[2,128,4,128]{1,3,2,0:T(8,128)(2,1)} collective-permute-done((bf16[2,128,4,128]{1,3,2,0:T(8,128)(2,1)}, bf16[2,128,4,128]{1,3,2,0:T(8,128)(2,1)}, u32[]{:S(2)}, u32[]{:S(2)}) %collective-permute-start.30) | collective-permute-done | bytes 262176 | tf_op jit(solution)/shard_map/ppermute | solution.py:17
  210.2 10.1 %collective-permute-done.28 = bf16[2,128,4,128]{1,3,2,0:T(8,128)(2,1)} collective-permute-done((bf16[2,128,4,128]{1,3,2,0:T(8,128)(2,1)}, bf16[2,128,4,128]{1,3,2,0:T(8,128)(2,1)}, u32[]{:S(2)}, u32[]{:S(2)}) %collective-permute-start.28) | collective-permute-done | bytes 262176 | tf_op jit(solution)/shard_map/ppermute | solution.py:17
  (323 shorter events, 99.8 us)
Async XLA Ops:
  5.6 10.7 %collective-permute-start.2 = (bf16[2,128,512]{1,2,0:T(8,128)(2,1)}, bf16[2,128,512]{1,2,0:T(8,128)(2,1)}, u32[]{:S(2)}, u32[]{:S(2)}) collective-permute-start(bf16[2,128,512]{1,2,0:T(8,128)(2,1)} %pad_maximum_fusion.8), channel_id=1, source_target_pairs={{0,4},{1,5},{2,6},{3,7},{4,8},{5,9},{6,10},{7,11},{8,12},{9,13},{1... | collective-permute-start | bytes 786440 | tf_op jit(solution)/shard_map/ppermute | solution.py:17
  8.8 10.4 %collective-permute-start = (bf16[2,128,512]{1,2,0:T(8,128)(2,1)}, bf16[2,128,512]{1,2,0:T(8,128)(2,1)}, u32[]{:S(2)}, u32[]{:S(2)}) collective-permute-start(bf16[2,128,512]{1,2,0:T(8,128)(2,1)} %pad_maximum_fusion.8), channel_id=1, source_target_pairs={{0,1},{1,2},{2,3},{3,4},{4,5},{5,6},{6,7},{7,8},{8,9},{9,10},{10,1... | collective-permute-start | bytes 786440 | tf_op jit(solution)/shard_map/ppermute | solution.py:17
  16.4 9.0 %collective-permute-start.3 = (bf16[2,128,512]{1,2,0:T(8,128)(2,1)}, bf16[2,128,512]{1,2,0:T(8,128)(2,1)}, u32[]{:S(2)}, u32[]{:S(2)}) collective-permute-start(bf16[2,128,512]{1,2,0:T(8,128)(2,1)} %collective-permute-done.2), channel_id=1, source_target_pairs={{0,4},{1,5},{2,6},{3,7},{4,8},{5,9},{6,10},{7,11},{8,12},{9,13},{1... | collective-permute-start | bytes 786440 | tf_op jit(solution)/shard_map/ppermute | solution.py:17
  20.4 8.4 %collective-permute-start.1 = (bf16[2,128,512]{1,2,0:T(8,128)(2,1)}, bf16[2,128,512]{1,2,0:T(8,128)(2,1)}, u32[]{:S(2)}, u32[]{:S(2)}) collective-permute-start(bf16[2,128,512]{1,2,0:T(8,128)(2,1)} %collective-permute-done), channel_id=1, source_target_pairs={{0,1},{1,2},{2,3},{3,4},{4,5},{5,6},{6,7},{7,8},{8,9},{9,10},{10,1... | collective-permute-start | bytes 786440 | tf_op jit(solution)/shard_map/ppermute | solution.py:17
  34.5 26.4 %collective-permute-start.6 = (bf16[2,128,512]{1,2,0:T(8,128)(2,1)}, bf16[2,128,512]{1,2,0:T(8,128)(2,1)}, u32[]{:S(2)}, u32[]{:S(2)}) collective-permute-start(bf16[2,128,512]{1,2,0:T(8,128)(2,1)} %pad_maximum_fusion.9), channel_id=1, source_target_pairs={{0,4},{1,5},{2,6},{3,7},{4,8},{5,9},{6,10},{7,11},{8,12},{9,13},{1... | collective-permute-start | bytes 786440 | tf_op jit(solution)/shard_map/ppermute | solution.py:17
  37.0 27.6 %collective-permute-start.4 = (bf16[2,128,512]{1,2,0:T(8,128)(2,1)}, bf16[2,128,512]{1,2,0:T(8,128)(2,1)}, u32[]{:S(2)}, u32[]{:S(2)}) collective-permute-start(bf16[2,128,512]{1,2,0:T(8,128)(2,1)} %pad_maximum_fusion.9), channel_id=1, source_target_pairs={{0,1},{1,2},{2,3},{3,4},{4,5},{5,6},{6,7},{7,8},{8,9},{9,10},{10,1... | collective-permute-start | bytes 786440 | tf_op jit(solution)/shard_map/ppermute | solution.py:17
  49.4 18.9 %collective-permute-start.17 = (bf16[2,128,4,128]{1,3,2,0:T(8,128)(2,1)}, bf16[2,128,4,128]{1,3,2,0:T(8,128)(2,1)}, u32[]{:S(2)}, u32[]{:S(2)}) collective-permute-start(bf16[2,128,4,128]{1,3,2,0:T(8,128)(2,1)} %pad_maximum_fusion.13), channel_id=1, source_target_pairs={{2,0},{3,1},{4,2},{5,3},{6,4},{7,5},{8,6},{9,7},{10,8},{11,9},{12,... | collective-permute-start | bytes 786440 | tf_op jit(solution)/shard_map/ppermute | solution.py:17
  54.1 19.0 %collective-permute-start.18 = (bf16[2,128,4,128]{1,3,2,0:T(8,128)(2,1)}, bf16[2,128,4,128]{1,3,2,0:T(8,128)(2,1)}, u32[]{:S(2)}, u32[]{:S(2)}) collective-permute-start(bf16[2,128,4,128]{1,3,2,0:T(8,128)(2,1)} %pad_maximum_fusion.14), channel_id=1, source_target_pairs={{4,0},{5,1},{6,2},{7,3},{8,4},{9,5},{10,6},{11,7},{12,8},{13,9},{1... | collective-permute-start | bytes 786440 | tf_op jit(solution)/shard_map/ppermute | solution.py:17
  57.7 15.5 %collective-permute-start.19 = (bf16[2,128,4,128]{1,3,2,0:T(8,128)(2,1)}, bf16[2,128,4,128]{1,3,2,0:T(8,128)(2,1)}, u32[]{:S(2)}, u32[]{:S(2)}) collective-permute-start(bf16[2,128,4,128]{1,3,2,0:T(8,128)(2,1)} %pad_maximum_fusion.15), channel_id=1, source_target_pairs={{8,0},{9,1},{10,2},{11,3},{12,4},{13,5},{14,6},{15,7},{24,16},{25,... | collective-permute-start | bytes 786440 | tf_op jit(solution)/shard_map/ppermute | solution.py:17
  60.8 19.2 %collective-permute-start.16 = (bf16[2,128,4,128]{1,3,2,0:T(8,128)(2,1)}, bf16[2,128,4,128]{1,3,2,0:T(8,128)(2,1)S(1)}, u32[]{:S(2)}, u32[]{:S(2)}) collective-permute-start(bf16[2,128,4,128]{1,3,2,0:T(8,128)(2,1)} %pad_maximum_fusion.12), channel_id=1, source_target_pairs={{1,0},{2,1},{3,2},{4,3},{5,4},{6,5},{7,6},{8,7},{9,8},{10,9},{11,1... | collective-permute-start | bytes 786440 | tf_op jit(solution)/shard_map/ppermute | solution.py:17
  64.5 19.0 %collective-permute-start.7 = (bf16[2,128,512]{1,2,0:T(8,128)(2,1)}, bf16[2,128,512]{1,2,0:T(8,128)(2,1)}, u32[]{:S(2)}, u32[]{:S(2)}) collective-permute-start(bf16[2,128,512]{1,2,0:T(8,128)(2,1)} %collective-permute-done.6), channel_id=1, source_target_pairs={{0,4},{1,5},{2,6},{3,7},{4,8},{5,9},{6,10},{7,11},{8,12},{9,13},{1... | collective-permute-start | bytes 786440 | tf_op jit(solution)/shard_map/ppermute | solution.py:17
  68.3 16.4 %collective-permute-start.5 = (bf16[2,128,512]{1,2,0:T(8,128)(2,1)}, bf16[2,128,512]{1,2,0:T(8,128)(2,1)}, u32[]{:S(2)}, u32[]{:S(2)}) collective-permute-start(bf16[2,128,512]{1,2,0:T(8,128)(2,1)} %collective-permute-done.4), channel_id=1, source_target_pairs={{0,1},{1,2},{2,3},{3,4},{4,5},{5,6},{6,7},{7,8},{8,9},{9,10},{10,1... | collective-permute-start | bytes 786440 | tf_op jit(solution)/shard_map/ppermute | solution.py:17
  89.7 21.3 %collective-permute-start.10 = (bf16[2,128,512]{1,2,0:T(8,128)(2,1)}, bf16[2,128,512]{1,2,0:T(8,128)(2,1)}, u32[]{:S(2)}, u32[]{:S(2)}) collective-permute-start(bf16[2,128,512]{1,2,0:T(8,128)(2,1)} %pad_maximum_fusion.10), channel_id=1, source_target_pairs={{0,4},{1,5},{2,6},{3,7},{4,8},{5,9},{6,10},{7,11},{8,12},{9,13},{1... | collective-permute-start | bytes 786440 | tf_op jit(solution)/shard_map/ppermute | solution.py:17
  91.6 23.9 %collective-permute-start.8 = (bf16[2,128,512]{1,2,0:T(8,128)(2,1)}, bf16[2,128,512]{1,2,0:T(8,128)(2,1)}, u32[]{:S(2)}, u32[]{:S(2)}) collective-permute-start(bf16[2,128,512]{1,2,0:T(8,128)(2,1)} %pad_maximum_fusion.10), channel_id=1, source_target_pairs={{0,1},{1,2},{2,3},{3,4},{4,5},{5,6},{6,7},{7,8},{8,9},{9,10},{10,1... | collective-permute-start | bytes 786440 | tf_op jit(solution)/shard_map/ppermute | solution.py:17
  99.2 19.9 %collective-permute-start.21 = (bf16[2,128,4,128]{1,3,2,0:T(8,128)(2,1)}, bf16[2,128,4,128]{1,3,2,0:T(8,128)(2,1)}, u32[]{:S(2)}, u32[]{:S(2)}) collective-permute-start(bf16[2,128,4,128]{1,3,2,0:T(8,128)(2,1)} %pad_maximum_fusion.17), channel_id=1, source_target_pairs={{2,0},{3,1},{4,2},{5,3},{6,4},{7,5},{8,6},{9,7},{10,8},{11,9},{12,... | collective-permute-start | bytes 786440 | tf_op jit(solution)/shard_map/ppermute | solution.py:17
  102.8 21.6 %collective-permute-start.22 = (bf16[2,128,4,128]{1,3,2,0:T(8,128)(2,1)}, bf16[2,128,4,128]{1,3,2,0:T(8,128)(2,1)}, u32[]{:S(2)}, u32[]{:S(2)}) collective-permute-start(bf16[2,128,4,128]{1,3,2,0:T(8,128)(2,1)} %pad_maximum_fusion.18), channel_id=1, source_target_pairs={{4,0},{5,1},{6,2},{7,3},{8,4},{9,5},{10,6},{11,7},{12,8},{13,9},{1... | collective-permute-start | bytes 786440 | tf_op jit(solution)/shard_map/ppermute | solution.py:17
  107.6 16.8 %collective-permute-start.23 = (bf16[2,128,4,128]{1,3,2,0:T(8,128)(2,1)}, bf16[2,128,4,128]{1,3,2,0:T(8,128)(2,1)}, u32[]{:S(2)}, u32[]{:S(2)}) collective-permute-start(bf16[2,128,4,128]{1,3,2,0:T(8,128)(2,1)} %pad_maximum_fusion.19), channel_id=1, source_target_pairs={{8,0},{9,1},{10,2},{11,3},{12,4},{13,5},{14,6},{15,7},{24,16},{25,... | collective-permute-start | bytes 786440 | tf_op jit(solution)/shard_map/ppermute | solution.py:17
  111.0 19.2 %collective-permute-start.20 = (bf16[2,128,4,128]{1,3,2,0:T(8,128)(2,1)}, bf16[2,128,4,128]{1,3,2,0:T(8,128)(2,1)}, u32[]{:S(2)}, u32[]{:S(2)}) collective-permute-start(bf16[2,128,4,128]{1,3,2,0:T(8,128)(2,1)} %pad_maximum_fusion.16), channel_id=1, source_target_pairs={{1,0},{2,1},{3,2},{4,3},{5,4},{6,5},{7,6},{8,7},{9,8},{10,9},{11,1... | collective-permute-start | bytes 786440 | tf_op jit(solution)/shard_map/ppermute | solution.py:17
  115.5 18.3 %collective-permute-start.11 = (bf16[2,128,512]{1,2,0:T(8,128)(2,1)}, bf16[2,128,512]{1,2,0:T(8,128)(2,1)S(1)}, u32[]{:S(2)}, u32[]{:S(2)}) collective-permute-start(bf16[2,128,512]{1,2,0:T(8,128)(2,1)} %collective-permute-done.10), channel_id=1, source_target_pairs={{0,4},{1,5},{2,6},{3,7},{4,8},{5,9},{6,10},{7,11},{8,12},{9,13},{1... | collective-permute-start | bytes 786440 | tf_op jit(solution)/shard_map/ppermute | solution.py:17
  119.1 14.9 %collective-permute-start.9 = (bf16[2,128,512]{1,2,0:T(8,128)(2,1)}, bf16[2,128,512]{1,2,0:T(8,128)(2,1)}, u32[]{:S(2)}, u32[]{:S(2)}) collective-permute-start(bf16[2,128,512]{1,2,0:T(8,128)(2,1)} %collective-permute-done.8), channel_id=1, source_target_pairs={{0,1},{1,2},{2,3},{3,4},{4,5},{5,6},{6,7},{7,8},{8,9},{9,10},{10,1... | collective-permute-start | bytes 786440 | tf_op jit(solution)/shard_map/ppermute | solution.py:17
  137.4 20.4 %collective-permute-start.14 = (bf16[2,128,512]{1,2,0:T(8,128)(2,1)}, bf16[2,128,512]{1,2,0:T(8,128)(2,1)}, u32[]{:S(2)}, u32[]{:S(2)}) collective-permute-start(bf16[2,128,512]{1,2,0:T(8,128)(2,1)} %pad_maximum_fusion.11), channel_id=1, source_target_pairs={{0,4},{1,5},{2,6},{3,7},{4,8},{5,9},{6,10},{7,11},{8,12},{9,13},{1... | collective-permute-start | bytes 786440 | tf_op jit(solution)/shard_map/ppermute | solution.py:17
  139.4 22.9 %collective-permute-start.12 = (bf16[2,128,512]{1,2,0:T(8,128)(2,1)}, bf16[2,128,512]{1,2,0:T(8,128)(2,1)}, u32[]{:S(2)}, u32[]{:S(2)}) collective-permute-start(bf16[2,128,512]{1,2,0:T(8,128)(2,1)} %pad_maximum_fusion.11), channel_id=1, source_target_pairs={{0,1},{1,2},{2,3},{3,4},{4,5},{5,6},{6,7},{7,8},{8,9},{9,10},{10,1... | collective-permute-start | bytes 786440 | tf_op jit(solution)/shard_map/ppermute | solution.py:17
  148.0 18.1 %collective-permute-start.25 = (bf16[2,128,4,128]{1,3,2,0:T(8,128)(2,1)}, bf16[2,128,4,128]{1,3,2,0:T(8,128)(2,1)}, u32[]{:S(2)}, u32[]{:S(2)}) collective-permute-start(bf16[2,128,4,128]{1,3,2,0:T(8,128)(2,1)} %pad_maximum_fusion.21), channel_id=1, source_target_pairs={{2,0},{3,1},{4,2},{5,3},{6,4},{7,5},{8,6},{9,7},{10,8},{11,9},{12,... | collective-permute-start | bytes 786440 | tf_op jit(solution)/shard_map/ppermute | solution.py:17
  151.6 19.9 %collective-permute-start.26 = (bf16[2,128,4,128]{1,3,2,0:T(8,128)(2,1)}, bf16[2,128,4,128]{1,3,2,0:T(8,128)(2,1)}, u32[]{:S(2)}, u32[]{:S(2)}) collective-permute-start(bf16[2,128,4,128]{1,3,2,0:T(8,128)(2,1)} %pad_maximum_fusion.22), channel_id=1, source_target_pairs={{4,0},{5,1},{6,2},{7,3},{8,4},{9,5},{10,6},{11,7},{12,8},{13,9},{1... | collective-permute-start | bytes 786440 | tf_op jit(solution)/shard_map/ppermute | solution.py:17
  155.3 16.1 %collective-permute-start.27 = (bf16[2,128,4,128]{1,3,2,0:T(8,128)(2,1)}, bf16[2,128,4,128]{1,3,2,0:T(8,128)(2,1)}, u32[]{:S(2)}, u32[]{:S(2)}) collective-permute-start(bf16[2,128,4,128]{1,3,2,0:T(8,128)(2,1)} %pad_maximum_fusion.23), channel_id=1, source_target_pairs={{8,0},{9,1},{10,2},{11,3},{12,4},{13,5},{14,6},{15,7},{24,16},{25,... | collective-permute-start | bytes 786440 | tf_op jit(solution)/shard_map/ppermute | solution.py:17
  157.8 20.9 %collective-permute-start.24 = (bf16[2,128,4,128]{1,3,2,0:T(8,128)(2,1)}, bf16[2,128,4,128]{1,3,2,0:T(8,128)(2,1)}, u32[]{:S(2)}, u32[]{:S(2)}) collective-permute-start(bf16[2,128,4,128]{1,3,2,0:T(8,128)(2,1)} %pad_maximum_fusion.20), channel_id=1, source_target_pairs={{1,0},{2,1},{3,2},{4,3},{5,4},{6,5},{7,6},{8,7},{9,8},{10,9},{11,1... | collective-permute-start | bytes 786440 | tf_op jit(solution)/shard_map/ppermute | solution.py:17
  162.3 20.8 %collective-permute-start.15 = (bf16[2,128,512]{1,2,0:T(8,128)(2,1)}, bf16[2,128,512]{1,2,0:T(8,128)(2,1)}, u32[]{:S(2)}, u32[]{:S(2)}) collective-permute-start(bf16[2,128,512]{1,2,0:T(8,128)(2,1)} %collective-permute-done.14), channel_id=1, source_target_pairs={{0,4},{1,5},{2,6},{3,7},{4,8},{5,9},{6,10},{7,11},{8,12},{9,13},{1... | collective-permute-start | bytes 786440 | tf_op jit(solution)/shard_map/ppermute | solution.py:17
  166.1 18.1 %collective-permute-start.13 = (bf16[2,128,512]{1,2,0:T(8,128)(2,1)}, bf16[2,128,512]{1,2,0:T(8,128)(2,1)}, u32[]{:S(2)}, u32[]{:S(2)}) collective-permute-start(bf16[2,128,512]{1,2,0:T(8,128)(2,1)} %collective-permute-done.12), channel_id=1, source_target_pairs={{0,1},{1,2},{2,3},{3,4},{4,5},{5,6},{6,7},{7,8},{8,9},{9,10},{10,1... | collective-permute-start | bytes 786440 | tf_op jit(solution)/shard_map/ppermute | solution.py:17
  191.7 11.7 %collective-permute-start.29 = (bf16[2,128,4,128]{1,3,2,0:T(8,128)(2,1)}, bf16[2,128,4,128]{1,3,2,0:T(8,128)(2,1)}, u32[]{:S(2)}, u32[]{:S(2)}) collective-permute-start(bf16[2,128,4,128]{1,3,2,0:T(8,128)(2,1)} %pad_maximum_fusion.25), channel_id=1, source_target_pairs={{2,0},{3,1},{4,2},{5,3},{6,4},{7,5},{8,6},{9,7},{10,8},{11,9},{12,... | collective-permute-start | bytes 786440 | tf_op jit(solution)/shard_map/ppermute | solution.py:17
  194.4 15.8 %collective-permute-start.30 = (bf16[2,128,4,128]{1,3,2,0:T(8,128)(2,1)}, bf16[2,128,4,128]{1,3,2,0:T(8,128)(2,1)}, u32[]{:S(2)}, u32[]{:S(2)}) collective-permute-start(bf16[2,128,4,128]{1,3,2,0:T(8,128)(2,1)} %pad_maximum_fusion.26), channel_id=1, source_target_pairs={{4,0},{5,1},{6,2},{7,3},{8,4},{9,5},{10,6},{11,7},{12,8},{13,9},{1... | collective-permute-start | bytes 786440 | tf_op jit(solution)/shard_map/ppermute | solution.py:17
  197.0 13.2 %collective-permute-start.31 = (bf16[2,128,4,128]{1,3,2,0:T(8,128)(2,1)}, bf16[2,128,4,128]{1,3,2,0:T(8,128)(2,1)}, u32[]{:S(2)}, u32[]{:S(2)}) collective-permute-start(bf16[2,128,4,128]{1,3,2,0:T(8,128)(2,1)} %pad_maximum_fusion.27), channel_id=1, source_target_pairs={{8,0},{9,1},{10,2},{11,3},{12,4},{13,5},{14,6},{15,7},{24,16},{25,... | collective-permute-start | bytes 786440 | tf_op jit(solution)/shard_map/ppermute | solution.py:17
  199.1 21.2 %collective-permute-start.28 = (bf16[2,128,4,128]{1,3,2,0:T(8,128)(2,1)}, bf16[2,128,4,128]{1,3,2,0:T(8,128)(2,1)}, u32[]{:S(2)}, u32[]{:S(2)}) collective-permute-start(bf16[2,128,4,128]{1,3,2,0:T(8,128)(2,1)} %pad_maximum_fusion.24), channel_id=1, source_target_pairs={{1,0},{2,1},{3,2},{4,3},{5,4},{6,5},{7,6},{8,7},{9,8},{10,9},{11,1... | collective-permute-start | bytes 786440 | tf_op jit(solution)/shard_map/ppermute | solution.py:17
  (46 other events, 393.4 us)

commit v8 on v6

--- a/solution.py
+++ b/solution.py
@@ -3,6 +3,7 @@
 import jax
 import jax.numpy as jnp
 from jax import lax
+from jax.experimental import pallas as pl
 from jax.sharding import PartitionSpec as P
 
 HEADS = 16
@@ -81,47 +82,62 @@
     return [received[0]] + [received[offset] for offset in offsets]
 
 
-def attend_chunk(query_c, received, grad_c, allowed, offsets, heads):
+def attention_kernel(*refs):
+    slots = (len(refs) - 5) // 2
+    query_ref, grad_ref, mask_ref = refs[0], refs[1], refs[2]
+    pair_refs = refs[3 : 3 + slots]
+    out_ref, qgrad_ref = refs[3 + slots], refs[4 + slots]
+    part_refs = refs[5 + slots :]
     scale_factor = 1.0 / math.sqrt(HEAD_DIM)
-    rows = query_c.shape[0]
-    head_shape = (rows, heads, HEAD_DIM)
-    key_stack = jnp.stack([moved[0].reshape(head_shape) for moved in received])[None]
-    value_stack = jnp.stack([moved[1].reshape(head_shape) for moved in received])[None]
-    query_stack = query_c.reshape((1,) + head_shape)
-    grad_stack = grad_c.reshape((1,) + head_shape)
-    raw_scores = (
-        jnp.einsum("bthd,bnuhd->bhtnu", query_stack, key_stack, preferred_element_type=jnp.float32)
-        * scale_factor
-    )
-    scores = jnp.where(allowed, raw_scores, -1e30)
-    row_peak = jnp.max(scores, axis=(3, 4), keepdims=True)
-    summed = jnp.sum(jnp.exp(scores - row_peak), axis=(3, 4), keepdims=True)
+    query = query_ref[...]
+    grad = grad_ref[...]
+    keys = jnp.concatenate([ref[0] for ref in pair_refs], axis=0)
+    vals = jnp.concatenate([ref[1] for ref in pair_refs], axis=0)
+    last = (((1,), (1,)), ((), ()))
+    first = (((0,), (0,)), ((), ()))
+    raw = lax.dot_general(query, keys, last, preferred_element_type=jnp.float32)
+    scores = jnp.where(mask_ref[...] > 0, raw * scale_factor, -1e30)
+    row_peak = jnp.max(scores, axis=1, keepdims=True)
+    summed = jnp.sum(jnp.exp(scores - row_peak), axis=1, keepdims=True)
     log_total = row_peak + jnp.log(summed)
     weights32 = jnp.exp(scores - log_total)
-    weights = rounded(weights32)
-    output = rounded(
-        jnp.einsum("bhtnu,bnuhd->bthd", weights, value_stack, preferred_element_type=jnp.float32)
-    )
-    grad_probs = jnp.einsum(
-        "bthd,bnuhd->bhtnu", grad_stack, value_stack, preferred_element_type=jnp.float32
-    )
-    delta_rows = jnp.sum(grad_stack.astype(jnp.float32) * output.astype(jnp.float32), axis=-1)
-    delta_rows = jnp.transpose(delta_rows, (0, 2, 1))[:, :, :, None, None]
-    grad_scores = rounded(weights32 * (grad_probs - delta_rows) * scale_factor)
-    query_grad = jnp.einsum(
-        "bhtnu,bnuhd->bthd", grad_scores, key_stack, preferred_element_type=jnp.float32
-    )
-    key_terms = jnp.einsum(
-        "bhtnu,bthd->bnuhd", grad_scores, query_stack, preferred_element_type=jnp.float32
-    )
-    value_terms = jnp.einsum(
-        "bhtnu,bthd->bnuhd", weights, grad_stack, preferred_element_type=jnp.float32
-    )
-    own = (rounded(key_terms[0, 0]), rounded(value_terms[0, 0]))
-    outgoing = [
-        jnp.stack([key_terms[0, slot_index], value_terms[0, slot_index]]).astype(jnp.bfloat16)
-        for slot_index in range(1, len(offsets) + 1)
-    ]
+    weights = weights32.astype(jnp.bfloat16)
+    output = jnp.dot(weights, vals, preferred_element_type=jnp.float32).astype(jnp.bfloat16)
+    out_ref[...] = output
+    grad_probs = lax.dot_general(grad, vals, last, preferred_element_type=jnp.float32)
+    delta = jnp.sum(grad.astype(jnp.float32) * output.astype(jnp.float32), axis=1, keepdims=True)
+    grad_scores = (weights32 * (grad_probs - delta) * scale_factor).astype(jnp.bfloat16)
+    qgrad_ref[...] = jnp.dot(grad_scores, keys, preferred_element_type=jnp.float32)
+    key_terms = lax.dot_general(grad_scores, query, first, preferred_element_type=jnp.float32)
+    value_terms = lax.dot_general(weights, grad, first, preferred_element_type=jnp.float32)
+    rows = query.shape[0]
+    for slot, ref in enumerate(part_refs):
+        ref[0] = key_terms[slot * rows : (slot + 1) * rows].astype(jnp.bfloat16)
+        ref[1] = value_terms[slot * rows : (slot + 1) * rows].astype(jnp.bfloat16)
+
+
+def attend_chunk(query_c, received, grad_c, allowed, offsets, heads):
+    rows, width = query_c.shape
+    slots = len(received)
+    mask = jnp.where(allowed, 1.0, 0.0).astype(jnp.float32).reshape(rows, slots * rows)
+    flat_spec = pl.BlockSpec((rows, HEAD_DIM), lambda h: (0, h))
+    pair_spec = pl.BlockSpec((2, rows, HEAD_DIM), lambda h: (0, 0, h))
+    mask_spec = pl.BlockSpec((rows, slots * rows), lambda h: (0, 0))
+    pair_shape = jax.ShapeDtypeStruct((2, rows, width), jnp.bfloat16)
+    results = pl.pallas_call(
+        attention_kernel,
+        grid=(heads,),
+        in_specs=[flat_spec, flat_spec, mask_spec] + [pair_spec] * slots,
+        out_specs=[flat_spec, flat_spec] + [pair_spec] * slots,
+        out_shape=[
+            jax.ShapeDtypeStruct((rows, width), jnp.bfloat16),
+            jax.ShapeDtypeStruct((rows, width), jnp.float32),
+        ]
+        + [pair_shape] * slots,
+    )(query_c, grad_c, mask, *received)
+    output, query_grad = results[0], results[1]
+    own = (results[2][0], results[2][1])
+    outgoing = list(results[3:])
     return output, query_grad, own, outgoing
 
 

time: 186 us -> 196 us (1.054)
  the two profiles are of different devices: /device:TPU:15 before, /device:TPU:0 now
where the time goes in v8:
time: 196 us; the launch traced here: 194 us
  waiting for transfers between devices  107 us (55%)
  starting transfers between devices  44.3 us (23%)
  Pallas kernels  20.3 us (10%)
  local copies, waits for them, and re-layouts  12.7 us (6%)
  other arithmetic  7.58 us (4%)
    ppermute x16, waiting for transfers between devices, from_behind(): lax.ppermute(value, axis, [(source, source + steps) for source in range(l...  107 us
    ppermute x16, starting transfers between devices, from_behind(): lax.ppermute(value, axis, [(source, source + steps) for source in range(l...  44.3 us
    pallas_call x2, Pallas kernels, attend_chunk(): pl.pallas_call(attention_kernel, grid=(heads,), in_specs=[flat_spec, flat...  20.3 us
    unnamed x48, local copies, waits for them, and re-layouts  8.77 us
  transfers between devices with their start and end apart: 16, of which 9 were waited for; matrix products, arithmetic and copies ran while one was open for 3% of the time, Pallas kernels for 5%

profile of v8, /device:TPU:0, one launch (start us, length us, event | category | flops | bytes accessed | tf_op | source)
XLA Modules:
  0.0 194.0 jit_solution(2708359602811895337)
XLA Ops:
  1.8 1.1 slice_bitcast_fusion.1
  6.4 5.0 %collective-permute-start.2 = (bf16[2,128,1024]{2,1,0:T(8,128)(2,1)S(1)}, bf16[2,128,1024]{2,1,0:T(8,128)(2,1)S(1)}, u32[]{:S(2)}, u32[]{:S(2)}) collective-permute-start(bf16[2,128,1024]{2,1,0:T(8,128)(2,1)S(1)} %pad_maximum_fusion.2.refs_3_), channel_id=1, source_target_pairs={{0,4},{1,5},{2,6},{3,7},{4,8},{5,9},{6,10},{7,11},{8,12},{9,13},{1... | collective-permute-start | bytes 1572872 | tf_op jit(solution)/shard_map/ppermute | solution.py:18
  11.3 1.5 collective-permute-start
  14.3 8.2 %collective-permute-done.2.refs_6_ = bf16[2,128,1024]{2,1,0:T(8,128)(2,1)S(1)} collective-permute-done((bf16[2,128,1024]{2,1,0:T(8,128)(2,1)S(1)}, bf16[2,128,1024]{2,1,0:T(8,128)(2,1)S(1)}, u32[]{:S(2)}, u32[]{:S(2)}) %collective-permute-start.2) | collective-permute-done | bytes 524320 | tf_op jit(solution)/shard_map/ppermute | solution.py:18
  22.5 5.2 %collective-permute-start.3 = (bf16[2,128,1024]{2,1,0:T(8,128)(2,1)S(1)}, bf16[2,128,1024]{2,1,0:T(8,128)(2,1)}, u32[]{:S(2)}, u32[]{:S(2)}) collective-permute-start(bf16[2,128,1024]{2,1,0:T(8,128)(2,1)S(1)} %collective-permute-done.2.refs_6_), channel_id=1, source_target_pairs={{0,4},{1,5},{2,6},{3,7},{4,8},{5,9},{6,10},{7,11},{8,12},{9,13},{1... | collective-permute-start | bytes 1572872 | tf_op jit(solution)/shard_map/ppermute | solution.py:18
  27.7 2.1 %collective-permute-start.1 = (bf16[2,128,1024]{2,1,0:T(8,128)(2,1)S(1)}, bf16[2,128,1024]{2,1,0:T(8,128)(2,1)}, u32[]{:S(2)}, u32[]{:S(2)}) collective-permute-start(bf16[2,128,1024]{2,1,0:T(8,128)(2,1)S(1)} %collective-permute-done.refs_4_), channel_id=1, source_target_pairs={{0,1},{1,2},{2,3},{3,4},{4,5},{5,6},{6,7},{7,8},{8,9},{9,10},{10,1... | collective-permute-start | bytes 1572872 | tf_op jit(solution)/shard_map/ppermute | solution.py:18
  33.6 3.6 %collective-permute-done.3.refs_7_ = bf16[2,128,1024]{2,1,0:T(8,128)(2,1)} collective-permute-done((bf16[2,128,1024]{2,1,0:T(8,128)(2,1)S(1)}, bf16[2,128,1024]{2,1,0:T(8,128)(2,1)}, u32[]{:S(2)}, u32[]{:S(2)}) %collective-permute-start.3) | collective-permute-done | bytes 524320 | tf_op jit(solution)/shard_map/ppermute | solution.py:18
  37.2 10.1 %shard_map.102 = (bf16[128,1024]{1,0:T(8,128)(2,1)}, f32[128,1024]{1,0:T(8,128)}, bf16[2,128,1024]{2,1,0:T(8,128)(2,1)}, bf16[2,128,1024]{2,1,0:T(8,128)(2,1)}, ...) custom-call(bf16[128,1024]{1,0:T(8,128)(2,1)} %get-tuple-element.54.refs_0_, ...), custom_call_target="tpu_custom_call" | custom-call | tf_op jit(solution)/shard_map/pallas_call | solution.py:127
  47.4 13.3 %collective-permute-start.6 = (bf16[2,128,1024]{2,1,0:T(8,128)(2,1)S(1)}, bf16[2,128,1024]{2,1,0:T(8,128)(2,1)S(1)}, u32[]{:S(2)}, u32[]{:S(2)}) collective-permute-start(bf16[2,128,1024]{2,1,0:T(8,128)(2,1)S(1)} %pad_maximum_fusion.3.refs_3_), channel_id=1, source_target_pairs={{0,4},{1,5},{2,6},{3,7},{4,8},{5,9},{6,10},{7,11},{8,12},{9,13},{1... | collective-permute-start | bytes 1572872 | tf_op jit(solution)/shard_map/ppermute | solution.py:18
  60.6 1.3 collective-permute-start.4
  62.0 10.4 %collective-permute-done.6.refs_6_ = bf16[2,128,1024]{2,1,0:T(8,128)(2,1)S(1)} collective-permute-done((bf16[2,128,1024]{2,1,0:T(8,128)(2,1)S(1)}, bf16[2,128,1024]{2,1,0:T(8,128)(2,1)S(1)}, u32[]{:S(2)}, u32[]{:S(2)}) %collective-permute-start.6) | collective-permute-done | bytes 524320 | tf_op jit(solution)/shard_map/ppermute | solution.py:18
  72.4 4.4 %collective-permute-start.7 = (bf16[2,128,1024]{2,1,0:T(8,128)(2,1)S(1)}, bf16[2,128,1024]{2,1,0:T(8,128)(2,1)S(1)}, u32[]{:S(2)}, u32[]{:S(2)}) collective-permute-start(bf16[2,128,1024]{2,1,0:T(8,128)(2,1)S(1)} %collective-permute-done.6.refs_6_), channel_id=1, source_target_pairs={{0,4},{1,5},{2,6},{3,7},{4,8},{5,9},{6,10},{7,11},{8,12},{9,13},{1... | collective-permute-start | bytes 1572872 | tf_op jit(solution)/shard_map/ppermute | solution.py:18
  76.8 1.3 collective-permute-start.5
  78.2 1.3 collective-permute-start.8
  79.5 1.3 collective-permute-start.9
  80.8 1.3 collective-permute-start.10
  82.1 1.4 collective-permute-done.7.refs_7_
  83.5 1.3 collective-permute-start.11
  85.6 10.2 %shard_map.103 = (bf16[128,1024]{1,0:T(8,128)(2,1)}, f32[128,1024]{1,0:T(8,128)}, bf16[2,128,1024]{2,1,0:T(8,128)(2,1)}, bf16[2,128,1024]{2,1,0:T(8,128)(2,1)}, ...) custom-call(bf16[128,1024]{1,0:T(8,128)(2,1)} %get-tuple-element.55.refs_0_, ...), custom_call_target="tpu_custom_call" | custom-call | tf_op jit(solution)/shard_map/pallas_call | solution.py:127
  95.8 1.3 collective-permute-start.12
  97.1 1.3 collective-permute-start.13
  98.4 1.5 collective-permute-done.9
  99.9 1.3 collective-permute-start.14
  101.2 20.8 %collective-permute-done.10 = bf16[2,128,1024]{2,1,0:T(8,128)(2,1)S(1)} collective-permute-done((bf16[2,128,1024]{2,1,0:T(8,128)(2,1)}, bf16[2,128,1024]{2,1,0:T(8,128)(2,1)S(1)}, u32[]{:S(2)}, u32[]{:S(2)}) %collective-permute-start.10) | collective-permute-done | bytes 524320 | tf_op jit(solution)/shard_map/ppermute | solution.py:18
  122.0 1.3 collective-permute-start.15
  123.3 19.7 %collective-permute-done.11 = bf16[2,128,1024]{2,1,0:T(8,128)(2,1)} collective-permute-done((bf16[2,128,1024]{2,1,0:T(8,128)(2,1)}, bf16[2,128,1024]{2,1,0:T(8,128)(2,1)}, u32[]{:S(2)}, u32[]{:S(2)}) %collective-permute-start.11) | collective-permute-done | bytes 524320 | tf_op jit(solution)/shard_map/ppermute | solution.py:18
  143.0 1.5 fusion
  144.7 1.0 copy-done.5
  147.8 7.1 %collective-permute-done.14 = bf16[2,128,1024]{2,1,0:T(8,128)(2,1)S(1)} collective-permute-done((bf16[2,128,1024]{2,1,0:T(8,128)(2,1)}, bf16[2,128,1024]{2,1,0:T(8,128)(2,1)S(1)}, u32[]{:S(2)}, u32[]{:S(2)}) %collective-permute-start.14) | collective-permute-done | bytes 524320 | tf_op jit(solution)/shard_map/ppermute | solution.py:18
  154.9 34.4 %collective-permute-done.15 = bf16[2,128,1024]{2,1,0:T(8,128)(2,1)S(1)} collective-permute-done((bf16[2,128,1024]{2,1,0:T(8,128)(2,1)}, bf16[2,128,1024]{2,1,0:T(8,128)(2,1)S(1)}, u32[]{:S(2)}, u32[]{:S(2)}) %collective-permute-start.15) | collective-permute-done | bytes 524320 | tf_op jit(solution)/shard_map/ppermute | solution.py:18
  191.0 0.9 copy.31
  192.2 0.9 copy.32
  (84 shorter events, 14.9 us)
Async XLA Ops:
  1.7 1.2 copy-start.2
  3.0 1.0 copy-start.3
  6.4 24.6 %copy-start = (bf16[2,128,1024]{2,1,0:T(8,128)(2,1)}, bf16[2,128,1024]{2,1,0:T(8,128)(2,1)S(1)}, u32[]{:S(2)}) copy-start(bf16[2,128,1024]{2,1,0:T(8,128)(2,1)S(1)} %pad_maximum_fusion.2.refs_3_) | copy-start | bytes 1572868
  6.4 16.1 %collective-permute-start.2 = (bf16[2,128,1024]{2,1,0:T(8,128)(2,1)S(1)}, bf16[2,128,1024]{2,1,0:T(8,128)(2,1)S(1)}, u32[]{:S(2)}, u32[]{:S(2)}) collective-permute-start(bf16[2,128,1024]{2,1,0:T(8,128)(2,1)S(1)} %pad_maximum_fusion.2.refs_3_), channel_id=1, source_target_pairs={{0,4},{1,5},{2,6},{3,7},{4,8},{5,9},{6,10},{7,11},{8,12},{9,13},{1... | collective-permute-start | bytes 1572872 | tf_op jit(solution)/shard_map/ppermute | solution.py:18
  11.3 16.3 %collective-permute-start = (bf16[2,128,1024]{2,1,0:T(8,128)(2,1)S(1)}, bf16[2,128,1024]{2,1,0:T(8,128)(2,1)S(1)}, u32[]{:S(2)}, u32[]{:S(2)}) collective-permute-start(bf16[2,128,1024]{2,1,0:T(8,128)(2,1)S(1)} %pad_maximum_fusion.2.refs_3_), channel_id=1, source_target_pairs={{0,1},{1,2},{2,3},{3,4},{4,5},{5,6},{6,7},{7,8},{8,9},{9,10},{10,1... | collective-permute-start | bytes 1572872 | tf_op jit(solution)/shard_map/ppermute | solution.py:18
  22.5 8.5 %copy-start.9 = (bf16[2,128,1024]{2,1,0:T(8,128)(2,1)}, bf16[2,128,1024]{2,1,0:T(8,128)(2,1)S(1)}, u32[]{:S(2)}) copy-start(bf16[2,128,1024]{2,1,0:T(8,128)(2,1)S(1)} %collective-permute-done.2.refs_6_) | copy-start | bytes 1572868
  22.5 14.7 %collective-permute-start.3 = (bf16[2,128,1024]{2,1,0:T(8,128)(2,1)S(1)}, bf16[2,128,1024]{2,1,0:T(8,128)(2,1)}, u32[]{:S(2)}, u32[]{:S(2)}) collective-permute-start(bf16[2,128,1024]{2,1,0:T(8,128)(2,1)S(1)} %collective-permute-done.2.refs_6_), channel_id=1, source_target_pairs={{0,4},{1,5},{2,6},{3,7},{4,8},{5,9},{6,10},{7,11},{8,12},{9,13},{1... | collective-permute-start | bytes 1572872 | tf_op jit(solution)/shard_map/ppermute | solution.py:18
  27.7 3.3 %copy-start.10 = (bf16[2,128,1024]{2,1,0:T(8,128)(2,1)}, bf16[2,128,1024]{2,1,0:T(8,128)(2,1)S(1)}, u32[]{:S(2)}) copy-start(bf16[2,128,1024]{2,1,0:T(8,128)(2,1)S(1)} %collective-permute-done.refs_4_) | copy-start | bytes 1572868
  27.7 9.5 %collective-permute-start.1 = (bf16[2,128,1024]{2,1,0:T(8,128)(2,1)S(1)}, bf16[2,128,1024]{2,1,0:T(8,128)(2,1)}, u32[]{:S(2)}, u32[]{:S(2)}) collective-permute-start(bf16[2,128,1024]{2,1,0:T(8,128)(2,1)S(1)} %collective-permute-done.refs_4_), channel_id=1, source_target_pairs={{0,1},{1,2},{2,3},{3,4},{4,5},{5,6},{6,7},{7,8},{8,9},{9,10},{10,1... | collective-permute-start | bytes 1572872 | tf_op jit(solution)/shard_map/ppermute | solution.py:18
  30.8 1.0 copy-start.4
  47.3 38.2 %copy-start.1 = (bf16[2,128,1024]{2,1,0:T(8,128)(2,1)}, bf16[2,128,1024]{2,1,0:T(8,128)(2,1)S(1)}, u32[]{:S(2)}) copy-start(bf16[2,128,1024]{2,1,0:T(8,128)(2,1)S(1)} %pad_maximum_fusion.3.refs_3_) | copy-start | bytes 1572868
  47.4 25.0 %collective-permute-start.6 = (bf16[2,128,1024]{2,1,0:T(8,128)(2,1)S(1)}, bf16[2,128,1024]{2,1,0:T(8,128)(2,1)S(1)}, u32[]{:S(2)}, u32[]{:S(2)}) collective-permute-start(bf16[2,128,1024]{2,1,0:T(8,128)(2,1)S(1)} %pad_maximum_fusion.3.refs_3_), channel_id=1, source_target_pairs={{0,4},{1,5},{2,6},{3,7},{4,8},{5,9},{6,10},{7,11},{8,12},{9,13},{1... | collective-permute-start | bytes 1572872 | tf_op jit(solution)/shard_map/ppermute | solution.py:18
  60.6 16.2 %collective-permute-start.4 = (bf16[2,128,1024]{2,1,0:T(8,128)(2,1)S(1)}, bf16[2,128,1024]{2,1,0:T(8,128)(2,1)S(1)}, u32[]{:S(2)}, u32[]{:S(2)}) collective-permute-start(bf16[2,128,1024]{2,1,0:T(8,128)(2,1)S(1)} %pad_maximum_fusion.3.refs_3_), channel_id=1, source_target_pairs={{0,1},{1,2},{2,3},{3,4},{4,5},{5,6},{6,7},{7,8},{8,9},{9,10},{10,1... | collective-permute-start | bytes 1572872 | tf_op jit(solution)/shard_map/ppermute | solution.py:18
  72.4 12.4 %copy-start.11 = (bf16[2,128,1024]{2,1,0:T(8,128)(2,1)}, bf16[2,128,1024]{2,1,0:T(8,128)(2,1)S(1)}, u32[]{:S(2)}) copy-start(bf16[2,128,1024]{2,1,0:T(8,128)(2,1)S(1)} %collective-permute-done.6.refs_6_) | copy-start | bytes 1572868
  72.4 11.1 %collective-permute-start.7 = (bf16[2,128,1024]{2,1,0:T(8,128)(2,1)S(1)}, bf16[2,128,1024]{2,1,0:T(8,128)(2,1)S(1)}, u32[]{:S(2)}, u32[]{:S(2)}) collective-permute-start(bf16[2,128,1024]{2,1,0:T(8,128)(2,1)S(1)} %collective-permute-done.6.refs_6_), channel_id=1, source_target_pairs={{0,4},{1,5},{2,6},{3,7},{4,8},{5,9},{6,10},{7,11},{8,12},{9,13},{1... | collective-permute-start | bytes 1572872 | tf_op jit(solution)/shard_map/ppermute | solution.py:18
  76.8 8.0 %copy-start.12 = (bf16[2,128,1024]{2,1,0:T(8,128)(2,1)}, bf16[2,128,1024]{2,1,0:T(8,128)(2,1)S(1)}, u32[]{:S(2)}) copy-start(bf16[2,128,1024]{2,1,0:T(8,128)(2,1)S(1)} %collective-permute-done.4.refs_4_) | copy-start | bytes 1572868
  76.8 7.9 %collective-permute-start.5 = (bf16[2,128,1024]{2,1,0:T(8,128)(2,1)S(1)}, bf16[2,128,1024]{2,1,0:T(8,128)(2,1)S(1)}, u32[]{:S(2)}, u32[]{:S(2)}) collective-permute-start(bf16[2,128,1024]{2,1,0:T(8,128)(2,1)S(1)} %collective-permute-done.4.refs_4_), channel_id=1, source_target_pairs={{0,1},{1,2},{2,3},{3,4},{4,5},{5,6},{6,7},{7,8},{8,9},{9,10},{10,1... | collective-permute-start | bytes 1572872 | tf_op jit(solution)/shard_map/ppermute | solution.py:18
  78.2 18.9 %collective-permute-start.8 = (bf16[2,128,1024]{2,1,0:T(8,128)(2,1)}, bf16[2,128,1024]{2,1,0:T(8,128)(2,1)S(1)}, u32[]{:S(2)}, u32[]{:S(2)}) collective-permute-start(bf16[2,128,1024]{2,1,0:T(8,128)(2,1)} %get-tuple-element.27), channel_id=1, source_target_pairs={{1,0},{2,1},{3,2},{4,3},{5,4},{6,5},{7,6},{8,7},{9,8},{10,9},{11,1... | collective-permute-start | bytes 1572872 | tf_op jit(solution)/shard_map/ppermute | solution.py:18
  79.5 20.4 %collective-permute-start.9 = (bf16[2,128,1024]{2,1,0:T(8,128)(2,1)}, bf16[2,128,1024]{2,1,0:T(8,128)(2,1)S(1)}, u32[]{:S(2)}, u32[]{:S(2)}) collective-permute-start(bf16[2,128,1024]{2,1,0:T(8,128)(2,1)} %get-tuple-element.28), channel_id=1, source_target_pairs={{2,0},{3,1},{4,2},{5,3},{6,4},{7,5},{8,6},{9,7},{10,8},{11,9},{12,... | collective-permute-start | bytes 1572872 | tf_op jit(solution)/shard_map/ppermute | solution.py:18
  80.8 41.2 %collective-permute-start.10 = (bf16[2,128,1024]{2,1,0:T(8,128)(2,1)}, bf16[2,128,1024]{2,1,0:T(8,128)(2,1)S(1)}, u32[]{:S(2)}, u32[]{:S(2)}) collective-permute-start(bf16[2,128,1024]{2,1,0:T(8,128)(2,1)} %get-tuple-element.29), channel_id=1, source_target_pairs={{4,0},{5,1},{6,2},{7,3},{8,4},{9,5},{10,6},{11,7},{12,8},{13,9},{1... | collective-permute-start | bytes 1572872 | tf_op jit(solution)/shard_map/ppermute | solution.py:18
  83.5 1.3 copy-start.13
  83.5 59.6 %collective-permute-start.11 = (bf16[2,128,1024]{2,1,0:T(8,128)(2,1)}, bf16[2,128,1024]{2,1,0:T(8,128)(2,1)}, u32[]{:S(2)}, u32[]{:S(2)}) collective-permute-start(bf16[2,128,1024]{2,1,0:T(8,128)(2,1)} %get-tuple-element.30), channel_id=1, source_target_pairs={{8,0},{9,1},{10,2},{11,3},{12,4},{13,5},{14,6},{15,7},{24,16},{25,... | collective-permute-start | bytes 1572872 | tf_op jit(solution)/shard_map/ppermute | solution.py:18
  85.6 57.5 %copy-start.6 = (bf16[2,128,1024]{2,1,0:T(8,128)(2,1)S(1)}, bf16[2,128,1024]{2,1,0:T(8,128)(2,1)}, u32[]{:S(2)}) copy-start(bf16[2,128,1024]{2,1,0:T(8,128)(2,1)} %get-tuple-element.26) | copy-start | bytes 1572868
  95.8 52.0 %collective-permute-start.12 = (bf16[2,128,1024]{2,1,0:T(8,128)(2,1)}, bf16[2,128,1024]{2,1,0:T(8,128)(2,1)S(1)}, u32[]{:S(2)}, u32[]{:S(2)}) collective-permute-start(bf16[2,128,1024]{2,1,0:T(8,128)(2,1)} %get-tuple-element.32), channel_id=1, source_target_pairs={{1,0},{2,1},{3,2},{4,3},{5,4},{6,5},{7,6},{8,7},{9,8},{10,9},{11,1... | collective-permute-start | bytes 1572872 | tf_op jit(solution)/shard_map/ppermute | solution.py:18
  97.1 50.7 %collective-permute-start.13 = (bf16[2,128,1024]{2,1,0:T(8,128)(2,1)}, bf16[2,128,1024]{2,1,0:T(8,128)(2,1)S(1)}, u32[]{:S(2)}, u32[]{:S(2)}) collective-permute-start(bf16[2,128,1024]{2,1,0:T(8,128)(2,1)} %get-tuple-element.33), channel_id=1, source_target_pairs={{2,0},{3,1},{4,2},{5,3},{6,4},{7,5},{8,6},{9,7},{10,8},{11,9},{12,... | collective-permute-start | bytes 1572872 | tf_op jit(solution)/shard_map/ppermute | solution.py:18
  99.9 55.0 %collective-permute-start.14 = (bf16[2,128,1024]{2,1,0:T(8,128)(2,1)}, bf16[2,128,1024]{2,1,0:T(8,128)(2,1)S(1)}, u32[]{:S(2)}, u32[]{:S(2)}) collective-permute-start(bf16[2,128,1024]{2,1,0:T(8,128)(2,1)} %get-tuple-element.34), channel_id=1, source_target_pairs={{4,0},{5,1},{6,2},{7,3},{8,4},{9,5},{10,6},{11,7},{12,8},{13,9},{1... | collective-permute-start | bytes 1572872 | tf_op jit(solution)/shard_map/ppermute | solution.py:18
  122.0 67.3 %collective-permute-start.15 = (bf16[2,128,1024]{2,1,0:T(8,128)(2,1)}, bf16[2,128,1024]{2,1,0:T(8,128)(2,1)S(1)}, u32[]{:S(2)}, u32[]{:S(2)}) collective-permute-start(bf16[2,128,1024]{2,1,0:T(8,128)(2,1)} %get-tuple-element.35), channel_id=1, source_target_pairs={{8,0},{9,1},{10,2},{11,3},{12,4},{13,5},{14,6},{15,7},{24,16},{25,... | collective-permute-start | bytes 1572872 | tf_op jit(solution)/shard_map/ppermute | solution.py:18
  144.6 1.0 copy-start.5
  144.6 1.2 copy-start.8
  145.9 1.0 copy-start.15
  145.9 1.0 copy-start.16
  146.9 42.4 %copy-start.7 = (bf16[2,128,1024]{2,1,0:T(8,128)(2,1)S(1)}, bf16[2,128,1024]{2,1,0:T(8,128)(2,1)}, u32[]{:S(2)}) copy-start(bf16[2,128,1024]{2,1,0:T(8,128)(2,1)} %get-tuple-element.31) | copy-start | bytes 1572868
  (3 other events, 2.1 us)

commit v9 on v8

--- a/solution.py
+++ b/solution.py
@@ -9,7 +9,7 @@
 HEADS = 16
 HEAD_DIM = 128
 BLOCK = 128
-CHUNKS = 2
+CHUNK_HEADS = (4, 6, 6)
 
 
 def from_behind(value, axis, steps):
@@ -165,12 +165,12 @@
     key_rot = rounded(rotary(key_vectors, positions, HEADS, HEAD_DIM, False))
     valid_slots = reach_mask(reach_table, shard_index * per_shard, per_shard, levels)
     allowed = score_mask(valid_slots, BLOCK)
-    chunk_heads = HEADS // CHUNKS
-    chunk_width = chunk_heads * HEAD_DIM
-    columns = [slice(chunk * chunk_width, (chunk + 1) * chunk_width) for chunk in range(CHUNKS)]
+    bounds = [sum(CHUNK_HEADS[:chunk]) * HEAD_DIM for chunk in range(len(CHUNK_HEADS) + 1)]
     pieces = []
     pending = []
-    for chunk, cols in enumerate(columns):
+    for chunk, chunk_heads in enumerate(CHUNK_HEADS):
+        chunk_width = chunk_heads * HEAD_DIM
+        cols = slice(bounds[chunk], bounds[chunk + 1])
         key_c, value_c = key_rot[:, cols], values[:, cols]
         if pending:
             key_c, value_c, _ = lax.optimization_barrier((key_c, value_c, pieces[-1][0]))

time: 196 us -> 204 us (1.041)
  starting transfers between devices: 44.3 us -> 59.9 us
  waiting for transfers between devices: 107 us -> 97 us
  Pallas kernels: 20.3 us -> 22.4 us
    ppermute x16 -> x24, starting transfers between devices: 44.3 us -> 59.9 us  [from_behind(): lax.ppermute(value, axis, [(source, source + steps) for source in range(l...]
    ppermute x16 -> x24, waiting for transfers between devices: 107 us -> 97 us  [from_behind(): lax.ppermute(value, axis, [(source, source + steps) for source in range(l...]
    pallas_call x2 -> x3, Pallas kernels: 20.3 us -> 22.4 us  [attend_chunk(): pl.pallas_call(attention_kernel, grid=(heads,), in_specs=[flat_spec, flat...]
    unnamed x48 -> x70, local copies, waits for them, and re-layouts: 8.77 us -> 9.29 us
  transfers between devices with their start and end apart: 16 -> 24, of which waited for: 9 -> 10; matrix products, arithmetic and copies ran while one was open for 3% -> 3% of each run, Pallas kernels for 5% -> 4%
where the time goes in v9:
time: 204 us; the launch traced here: 202 us
  waiting for transfers between devices  97 us (48%)
  starting transfers between devices  59.9 us (29%)
  Pallas kernels  22.4 us (11%)
  local copies, waits for them, and re-layouts  13.3 us (7%)
  other arithmetic  7.52 us (4%)
  between operations  2.06 us (1%)
    ppermute x24, waiting for transfers between devices, from_behind(): lax.ppermute(value, axis, [(source, source + steps) for source in range(l...  97 us
    ppermute x24, starting transfers between devices, from_behind(): lax.ppermute(value, axis, [(source, source + steps) for source in range(l...  59.9 us
    pallas_call x3, Pallas kernels, attend_chunk(): pl.pallas_call(attention_kernel, grid=(heads,), in_specs=[flat_spec, flat...  22.4 us
    unnamed x70, local copies, waits for them, and re-layouts  9.29 us
  transfers between devices with their start and end apart: 24, of which 10 were waited for; matrix products, arithmetic and copies ran while one was open for 3% of the time, Pallas kernels for 4%

profile of v9, /device:TPU:0, one launch (start us, length us, event | category | flops | bytes accessed | tf_op | source)
XLA Modules:
  0.0 202.1 jit_solution(10015815984836821096)
XLA Ops:
  7.1 2.4 %collective-permute-start = (bf16[2,128,512]{2,1,0:T(8,128)(2,1)S(1)}, bf16[2,128,512]{2,1,0:T(8,128)(2,1)S(1)}, u32[]{:S(2)}, u32[]{:S(2)}) collective-permute-start(bf16[2,128,512]{2,1,0:T(8,128)(2,1)S(1)} %pad_maximum_fusion.8.refs_3_), channel_id=1, source_target_pairs={{0,1},{1,2},{2,3},{3,4},{4,5},{5,6},{6,7},{7,8},{8,9},{9,10},{10,1... | collective-permute-start | bytes 786440 | tf_op jit(solution)/shard_map/ppermute | solution.py:18
  9.4 4.5 %collective-permute-start.2 = (bf16[2,128,512]{2,1,0:T(8,128)(2,1)S(1)}, bf16[2,128,512]{2,1,0:T(8,128)(2,1)S(1)}, u32[]{:S(2)}, u32[]{:S(2)}) collective-permute-start(bf16[2,128,512]{2,1,0:T(8,128)(2,1)S(1)} %pad_maximum_fusion.8.refs_3_), channel_id=1, source_target_pairs={{0,4},{1,5},{2,6},{3,7},{4,8},{5,9},{6,10},{7,11},{8,12},{9,13},{1... | collective-permute-start | bytes 786440 | tf_op jit(solution)/shard_map/ppermute | solution.py:18
  15.4 4.0 %collective-permute-start.1 = (bf16[2,128,512]{2,1,0:T(8,128)(2,1)S(1)}, bf16[2,128,512]{2,1,0:T(8,128)(2,1)}, u32[]{:S(2)}, u32[]{:S(2)}) collective-permute-start(bf16[2,128,512]{2,1,0:T(8,128)(2,1)S(1)} %collective-permute-done.refs_4_), channel_id=1, source_target_pairs={{0,1},{1,2},{2,3},{3,4},{4,5},{5,6},{6,7},{7,8},{8,9},{9,10},{10,1... | collective-permute-start | bytes 786440 | tf_op jit(solution)/shard_map/ppermute | solution.py:18
  20.0 5.1 %collective-permute-start.3 = (bf16[2,128,512]{2,1,0:T(8,128)(2,1)S(1)}, bf16[2,128,512]{2,1,0:T(8,128)(2,1)}, u32[]{:S(2)}, u32[]{:S(2)}) collective-permute-start(bf16[2,128,512]{2,1,0:T(8,128)(2,1)S(1)} %collective-permute-done.2.refs_6_), channel_id=1, source_target_pairs={{0,4},{1,5},{2,6},{3,7},{4,8},{5,9},{6,10},{7,11},{8,12},{9,13},{1... | collective-permute-start | bytes 786440 | tf_op jit(solution)/shard_map/ppermute | solution.py:18
  27.6 2.9 %collective-permute-done.3.refs_7_ = bf16[2,128,512]{2,1,0:T(8,128)(2,1)} collective-permute-done((bf16[2,128,512]{2,1,0:T(8,128)(2,1)S(1)}, bf16[2,128,512]{2,1,0:T(8,128)(2,1)}, u32[]{:S(2)}, u32[]{:S(2)}) %collective-permute-start.3) | collective-permute-done | bytes 262176 | tf_op jit(solution)/shard_map/ppermute | solution.py:18
  30.5 6.1 %shard_map.102 = (bf16[128,512]{1,0:T(8,128)(2,1)}, f32[128,512]{1,0:T(8,128)}, bf16[2,128,512]{2,1,0:T(8,128)(2,1)}, bf16[2,128,512]{2,1,0:T(8,128)(2,1)}, bf16...) custom-call(bf16[128,512]{1,0:T(8,128)(2,1)} %slice.202.refs_0_, ...), custom_call_target="tpu_custom_call" | custom-call | tf_op jit(solution)/shard_map/pallas_call | solution.py:127
  36.7 1.6 collective-permute-start.4
  38.3 4.9 %collective-permute-start.6 = (bf16[2,128,768]{2,1,0:T(8,128)(2,1)S(1)}, bf16[2,128,768]{2,1,0:T(8,128)(2,1)S(1)}, u32[]{:S(2)}, u32[]{:S(2)}) collective-permute-start(bf16[2,128,768]{2,1,0:T(8,128)(2,1)S(1)} %pad_maximum_fusion.6.refs_3_), channel_id=1, source_target_pairs={{0,4},{1,5},{2,6},{3,7},{4,8},{5,9},{6,10},{7,11},{8,12},{9,13},{1... | collective-permute-start | bytes 1179656 | tf_op jit(solution)/shard_map/ppermute | solution.py:18
  43.1 4.3 %collective-permute-start.5 = (bf16[2,128,768]{2,1,0:T(8,128)(2,1)S(1)}, bf16[2,128,768]{2,1,0:T(8,128)(2,1)S(1)}, u32[]{:S(2)}, u32[]{:S(2)}) collective-permute-start(bf16[2,128,768]{2,1,0:T(8,128)(2,1)S(1)} %collective-permute-done.4.refs_4_), channel_id=1, source_target_pairs={{0,1},{1,2},{2,3},{3,4},{4,5},{5,6},{6,7},{7,8},{8,9},{9,10},{10,1... | collective-permute-start | bytes 1179656 | tf_op jit(solution)/shard_map/ppermute | solution.py:18
  47.5 3.8 %collective-permute-done.6.refs_6_ = bf16[2,128,768]{2,1,0:T(8,128)(2,1)S(1)} collective-permute-done((bf16[2,128,768]{2,1,0:T(8,128)(2,1)S(1)}, bf16[2,128,768]{2,1,0:T(8,128)(2,1)S(1)}, u32[]{:S(2)}, u32[]{:S(2)}) %collective-permute-start.6) | collective-permute-done | bytes 393248 | tf_op jit(solution)/shard_map/ppermute | solution.py:18
  51.3 4.4 %collective-permute-start.7 = (bf16[2,128,768]{2,1,0:T(8,128)(2,1)S(1)}, bf16[2,128,768]{2,1,0:T(8,128)(2,1)S(1)}, u32[]{:S(2)}, u32[]{:S(2)}) collective-permute-start(bf16[2,128,768]{2,1,0:T(8,128)(2,1)S(1)} %collective-permute-done.6.refs_6_), channel_id=1, source_target_pairs={{0,4},{1,5},{2,6},{3,7},{4,8},{5,9},{6,10},{7,11},{8,12},{9,13},{1... | collective-permute-start | bytes 1179656 | tf_op jit(solution)/shard_map/ppermute | solution.py:18
  57.3 7.6 %collective-permute-done.7.refs_7_ = bf16[2,128,768]{2,1,0:T(8,128)(2,1)S(1)} collective-permute-done((bf16[2,128,768]{2,1,0:T(8,128)(2,1)S(1)}, bf16[2,128,768]{2,1,0:T(8,128)(2,1)S(1)}, u32[]{:S(2)}, u32[]{:S(2)}) %collective-permute-start.7) | collective-permute-done | bytes 393248 | tf_op jit(solution)/shard_map/ppermute | solution.py:18
  65.7 8.2 %shard_map.103 = (bf16[128,768]{1,0:T(8,128)(2,1)}, f32[128,768]{1,0:T(8,128)}, bf16[2,128,768]{2,1,0:T(8,128)(2,1)}, bf16[2,128,768]{2,1,0:T(8,128)(2,1)}, bf16...) custom-call(bf16[128,768]{1,0:T(8,128)(2,1)} %get-tuple-element.74.refs_0_, ...), custom_call_target="tpu_custom_call" | custom-call | tf_op jit(solution)/shard_map/pallas_call | solution.py:127
  74.0 4.5 %collective-permute-start.10 = (bf16[2,128,768]{2,1,0:T(8,128)(2,1)S(1)}, bf16[2,128,768]{2,1,0:T(8,128)(2,1)S(1)}, u32[]{:S(2)}, u32[]{:S(2)}) collective-permute-start(bf16[2,128,768]{2,1,0:T(8,128)(2,1)S(1)} %pad_maximum_fusion.7.refs_3_), channel_id=1, source_target_pairs={{0,4},{1,5},{2,6},{3,7},{4,8},{5,9},{6,10},{7,11},{8,12},{9,13},{1... | collective-permute-start | bytes 1179656 | tf_op jit(solution)/shard_map/ppermute | solution.py:18
  78.5 1.3 collective-permute-start.12
  79.8 3.1 %collective-permute-start.8 = (bf16[2,128,768]{2,1,0:T(8,128)(2,1)S(1)}, bf16[2,128,768]{2,1,0:T(8,128)(2,1)S(1)}, u32[]{:S(2)}, u32[]{:S(2)}) collective-permute-start(bf16[2,128,768]{2,1,0:T(8,128)(2,1)S(1)} %pad_maximum_fusion.7.refs_3_), channel_id=1, source_target_pairs={{0,1},{1,2},{2,3},{3,4},{4,5},{5,6},{6,7},{7,8},{8,9},{9,10},{10,1... | collective-permute-start | bytes 1179656 | tf_op jit(solution)/shard_map/ppermute | solution.py:18
  82.9 4.3 %collective-permute-done.10.refs_6_ = bf16[2,128,768]{2,1,0:T(8,128)(2,1)S(1)} collective-permute-done((bf16[2,128,768]{2,1,0:T(8,128)(2,1)S(1)}, bf16[2,128,768]{2,1,0:T(8,128)(2,1)S(1)}, u32[]{:S(2)}, u32[]{:S(2)}) %collective-permute-start.10) | collective-permute-done | bytes 393248 | tf_op jit(solution)/shard_map/ppermute | solution.py:18
  87.2 4.4 %collective-permute-start.11 = (bf16[2,128,768]{2,1,0:T(8,128)(2,1)S(1)}, bf16[2,128,768]{2,1,0:T(8,128)(2,1)S(1)}, u32[]{:S(2)}, u32[]{:S(2)}) collective-permute-start(bf16[2,128,768]{2,1,0:T(8,128)(2,1)S(1)} %collective-permute-done.10.refs_6_), channel_id=1, source_target_pairs={{0,4},{1,5},{2,6},{3,7},{4,8},{5,9},{6,10},{7,11},{8,12},{9,13},{1... | collective-permute-start | bytes 1179656 | tf_op jit(solution)/shard_map/ppermute | solution.py:18
  91.6 1.3 collective-permute-start.13
  92.9 1.3 collective-permute-start.14
  94.2 1.3 collective-permute-start.15
  95.5 1.3 collective-permute-start.9
  96.9 5.7 %collective-permute-done.13 = bf16[2,128,512]{2,1,0:T(8,128)(2,1)S(1)} collective-permute-done((bf16[2,128,512]{2,1,0:T(8,128)(2,1)S(1)}, bf16[2,128,512]{2,1,0:T(8,128)(2,1)S(1)}, u32[]{:S(2)}, u32[]{:S(2)}) %collective-permute-start.13) | collective-permute-done | bytes 262176 | tf_op jit(solution)/shard_map/ppermute | solution.py:18
  103.9 6.5 %collective-permute-done.14 = bf16[2,128,512]{2,1,0:T(8,128)(2,1)S(1)} collective-permute-done((bf16[2,128,512]{2,1,0:T(8,128)(2,1)S(1)}, bf16[2,128,512]{2,1,0:T(8,128)(2,1)S(1)}, u32[]{:S(2)}, u32[]{:S(2)}) %collective-permute-start.14) | collective-permute-done | bytes 262176 | tf_op jit(solution)/shard_map/ppermute | solution.py:18
  111.6 12.8 %collective-permute-done.15 = bf16[2,128,512]{2,1,0:T(8,128)(2,1)S(1)} collective-permute-done((bf16[2,128,512]{2,1,0:T(8,128)(2,1)S(1)}, bf16[2,128,512]{2,1,0:T(8,128)(2,1)S(1)}, u32[]{:S(2)}, u32[]{:S(2)}) %collective-permute-start.15) | collective-permute-done | bytes 262176 | tf_op jit(solution)/shard_map/ppermute | solution.py:18
  125.8 1.3 collective-permute-start.19
  128.1 8.1 %shard_map.104 = (bf16[128,768]{1,0:T(8,128)(2,1)}, f32[128,768]{1,0:T(8,128)}, bf16[2,128,768]{2,1,0:T(8,128)(2,1)}, bf16[2,128,768]{2,1,0:T(8,128)(2,1)}, bf16...) custom-call(bf16[128,768]{1,0:T(8,128)(2,1)} %get-tuple-element.75.refs_0_, ...), custom_call_target="tpu_custom_call" | custom-call | tf_op jit(solution)/shard_map/pallas_call | solution.py:127
  136.2 1.3 collective-permute-start.20
  137.5 1.3 collective-permute-start.21
  138.8 1.3 collective-permute-start.22
  141.4 27.6 %collective-permute-done.19 = bf16[2,128,768]{2,1,0:T(8,128)(2,1)S(1)} collective-permute-done((bf16[2,128,768]{2,1,0:T(8,128)(2,1)}, bf16[2,128,768]{2,1,0:T(8,128)(2,1)S(1)}, u32[]{:S(2)}, u32[]{:S(2)}) %collective-permute-start.19) | collective-permute-done | bytes 393248 | tf_op jit(solution)/shard_map/ppermute | solution.py:18
  172.3 25.1 %collective-permute-done.23 = bf16[2,128,768]{2,1,0:T(8,128)(2,1)S(1)} collective-permute-done((bf16[2,128,768]{2,1,0:T(8,128)(2,1)}, bf16[2,128,768]{2,1,0:T(8,128)(2,1)S(1)}, u32[]{:S(2)}, u32[]{:S(2)}) %collective-permute-start.23) | collective-permute-done | bytes 393248 | tf_op jit(solution)/shard_map/ppermute | solution.py:18
  (129 shorter events, 26.6 us)
Async XLA Ops:
  7.1 8.4 %collective-permute-start = (bf16[2,128,512]{2,1,0:T(8,128)(2,1)S(1)}, bf16[2,128,512]{2,1,0:T(8,128)(2,1)S(1)}, u32[]{:S(2)}, u32[]{:S(2)}) collective-permute-start(bf16[2,128,512]{2,1,0:T(8,128)(2,1)S(1)} %pad_maximum_fusion.8.refs_3_), channel_id=1, source_target_pairs={{0,1},{1,2},{2,3},{3,4},{4,5},{5,6},{6,7},{7,8},{8,9},{9,10},{10,1... | collective-permute-start | bytes 786440 | tf_op jit(solution)/shard_map/ppermute | solution.py:18
  9.4 10.6 %collective-permute-start.2 = (bf16[2,128,512]{2,1,0:T(8,128)(2,1)S(1)}, bf16[2,128,512]{2,1,0:T(8,128)(2,1)S(1)}, u32[]{:S(2)}, u32[]{:S(2)}) collective-permute-start(bf16[2,128,512]{2,1,0:T(8,128)(2,1)S(1)} %pad_maximum_fusion.8.refs_3_), channel_id=1, source_target_pairs={{0,4},{1,5},{2,6},{3,7},{4,8},{5,9},{6,10},{7,11},{8,12},{9,13},{1... | collective-permute-start | bytes 786440 | tf_op jit(solution)/shard_map/ppermute | solution.py:18
  15.4 12.2 %collective-permute-start.1 = (bf16[2,128,512]{2,1,0:T(8,128)(2,1)S(1)}, bf16[2,128,512]{2,1,0:T(8,128)(2,1)}, u32[]{:S(2)}, u32[]{:S(2)}) collective-permute-start(bf16[2,128,512]{2,1,0:T(8,128)(2,1)S(1)} %collective-permute-done.refs_4_), channel_id=1, source_target_pairs={{0,1},{1,2},{2,3},{3,4},{4,5},{5,6},{6,7},{7,8},{8,9},{9,10},{10,1... | collective-permute-start | bytes 786440 | tf_op jit(solution)/shard_map/ppermute | solution.py:18
  20.0 10.5 %collective-permute-start.3 = (bf16[2,128,512]{2,1,0:T(8,128)(2,1)S(1)}, bf16[2,128,512]{2,1,0:T(8,128)(2,1)}, u32[]{:S(2)}, u32[]{:S(2)}) collective-permute-start(bf16[2,128,512]{2,1,0:T(8,128)(2,1)S(1)} %collective-permute-done.2.refs_6_), channel_id=1, source_target_pairs={{0,4},{1,5},{2,6},{3,7},{4,8},{5,9},{6,10},{7,11},{8,12},{9,13},{1... | collective-permute-start | bytes 786440 | tf_op jit(solution)/shard_map/ppermute | solution.py:18
  36.7 6.4 %collective-permute-start.4 = (bf16[2,128,768]{2,1,0:T(8,128)(2,1)S(1)}, bf16[2,128,768]{2,1,0:T(8,128)(2,1)S(1)}, u32[]{:S(2)}, u32[]{:S(2)}) collective-permute-start(bf16[2,128,768]{2,1,0:T(8,128)(2,1)S(1)} %pad_maximum_fusion.6.refs_3_), channel_id=1, source_target_pairs={{0,1},{1,2},{2,3},{3,4},{4,5},{5,6},{6,7},{7,8},{8,9},{9,10},{10,1... | collective-permute-start | bytes 1179656 | tf_op jit(solution)/shard_map/ppermute | solution.py:18
  38.3 13.0 %collective-permute-start.6 = (bf16[2,128,768]{2,1,0:T(8,128)(2,1)S(1)}, bf16[2,128,768]{2,1,0:T(8,128)(2,1)S(1)}, u32[]{:S(2)}, u32[]{:S(2)}) collective-permute-start(bf16[2,128,768]{2,1,0:T(8,128)(2,1)S(1)} %pad_maximum_fusion.6.refs_3_), channel_id=1, source_target_pairs={{0,4},{1,5},{2,6},{3,7},{4,8},{5,9},{6,10},{7,11},{8,12},{9,13},{1... | collective-permute-start | bytes 1179656 | tf_op jit(solution)/shard_map/ppermute | solution.py:18
  43.1 14.2 %collective-permute-start.5 = (bf16[2,128,768]{2,1,0:T(8,128)(2,1)S(1)}, bf16[2,128,768]{2,1,0:T(8,128)(2,1)S(1)}, u32[]{:S(2)}, u32[]{:S(2)}) collective-permute-start(bf16[2,128,768]{2,1,0:T(8,128)(2,1)S(1)} %collective-permute-done.4.refs_4_), channel_id=1, source_target_pairs={{0,1},{1,2},{2,3},{3,4},{4,5},{5,6},{6,7},{7,8},{8,9},{9,10},{10,1... | collective-permute-start | bytes 1179656 | tf_op jit(solution)/shard_map/ppermute | solution.py:18
  51.3 13.7 %collective-permute-start.7 = (bf16[2,128,768]{2,1,0:T(8,128)(2,1)S(1)}, bf16[2,128,768]{2,1,0:T(8,128)(2,1)S(1)}, u32[]{:S(2)}, u32[]{:S(2)}) collective-permute-start(bf16[2,128,768]{2,1,0:T(8,128)(2,1)S(1)} %collective-permute-done.6.refs_6_), channel_id=1, source_target_pairs={{0,4},{1,5},{2,6},{3,7},{4,8},{5,9},{6,10},{7,11},{8,12},{9,13},{1... | collective-permute-start | bytes 1179656 | tf_op jit(solution)/shard_map/ppermute | solution.py:18
  65.7 25.9 %copy-start.29 = (bf16[2,128,512]{2,1,0:T(8,128)(2,1)S(1)}, bf16[2,128,512]{2,1,0:T(8,128)(2,1)}, u32[]{:S(2)}) copy-start(bf16[2,128,512]{2,1,0:T(8,128)(2,1)} %get-tuple-element.41) | copy-start | bytes 786436
  73.9 20.3 %copy-start.27 = (bf16[2,128,512]{2,1,0:T(8,128)(2,1)S(1)}, bf16[2,128,512]{2,1,0:T(8,128)(2,1)}, u32[]{:S(2)}) copy-start(bf16[2,128,512]{2,1,0:T(8,128)(2,1)} %get-tuple-element.43) | copy-start | bytes 786436
  73.9 53.2 %copy-start.18 = (bf16[2,128,512]{2,1,0:T(8,128)(2,1)S(1)}, bf16[2,128,512]{2,1,0:T(8,128)(2,1)}, u32[]{:S(2)}) copy-start(bf16[2,128,512]{2,1,0:T(8,128)(2,1)} %get-tuple-element.39) | copy-start | bytes 786436
  74.0 53.3 %copy-start = (bf16[2,128,768]{2,1,0:T(8,128)(2,1)}, bf16[2,128,768]{2,1,0:T(8,128)(2,1)S(1)}, u32[]{:S(2)}) copy-start(bf16[2,128,768]{2,1,0:T(8,128)(2,1)S(1)} %pad_maximum_fusion.7.refs_3_) | copy-start | bytes 1179652
  74.0 13.2 %collective-permute-start.10 = (bf16[2,128,768]{2,1,0:T(8,128)(2,1)S(1)}, bf16[2,128,768]{2,1,0:T(8,128)(2,1)S(1)}, u32[]{:S(2)}, u32[]{:S(2)}) collective-permute-start(bf16[2,128,768]{2,1,0:T(8,128)(2,1)S(1)} %pad_maximum_fusion.7.refs_3_), channel_id=1, source_target_pairs={{0,4},{1,5},{2,6},{3,7},{4,8},{5,9},{6,10},{7,11},{8,12},{9,13},{1... | collective-permute-start | bytes 1179656 | tf_op jit(solution)/shard_map/ppermute | solution.py:18
  78.5 15.7 %collective-permute-start.12 = (bf16[2,128,512]{2,1,0:T(8,128)(2,1)S(1)}, bf16[2,128,512]{2,1,0:T(8,128)(2,1)S(1)}, u32[]{:S(2)}, u32[]{:S(2)}) collective-permute-start(bf16[2,128,512]{2,1,0:T(8,128)(2,1)S(1)} %copy-done.30), channel_id=1, source_target_pairs={{1,0},{2,1},{3,2},{4,3},{5,4},{6,5},{7,6},{8,7},{9,8},{10,9},{11,1... | collective-permute-start | bytes 786440 | tf_op jit(solution)/shard_map/ppermute | solution.py:18
  79.8 15.7 %collective-permute-start.8 = (bf16[2,128,768]{2,1,0:T(8,128)(2,1)S(1)}, bf16[2,128,768]{2,1,0:T(8,128)(2,1)S(1)}, u32[]{:S(2)}, u32[]{:S(2)}) collective-permute-start(bf16[2,128,768]{2,1,0:T(8,128)(2,1)S(1)} %pad_maximum_fusion.7.refs_3_), channel_id=1, source_target_pairs={{0,1},{1,2},{2,3},{3,4},{4,5},{5,6},{6,7},{7,8},{8,9},{9,10},{10,1... | collective-permute-start | bytes 1179656 | tf_op jit(solution)/shard_map/ppermute | solution.py:18
  87.2 40.1 %copy-start.10 = (bf16[2,128,768]{2,1,0:T(8,128)(2,1)}, bf16[2,128,768]{2,1,0:T(8,128)(2,1)S(1)}, u32[]{:S(2)}) copy-start(bf16[2,128,768]{2,1,0:T(8,128)(2,1)S(1)} %collective-permute-done.10.refs_6_) | copy-start | bytes 1179652
  87.2 38.6 %collective-permute-start.11 = (bf16[2,128,768]{2,1,0:T(8,128)(2,1)S(1)}, bf16[2,128,768]{2,1,0:T(8,128)(2,1)S(1)}, u32[]{:S(2)}, u32[]{:S(2)}) collective-permute-start(bf16[2,128,768]{2,1,0:T(8,128)(2,1)S(1)} %collective-permute-done.10.refs_6_), channel_id=1, source_target_pairs={{0,4},{1,5},{2,6},{3,7},{4,8},{5,9},{6,10},{7,11},{8,12},{9,13},{1... | collective-permute-start | bytes 1179656 | tf_op jit(solution)/shard_map/ppermute | solution.py:18
  91.6 11.0 %collective-permute-start.13 = (bf16[2,128,512]{2,1,0:T(8,128)(2,1)S(1)}, bf16[2,128,512]{2,1,0:T(8,128)(2,1)S(1)}, u32[]{:S(2)}, u32[]{:S(2)}) collective-permute-start(bf16[2,128,512]{2,1,0:T(8,128)(2,1)S(1)} %copy-done.29), channel_id=1, source_target_pairs={{2,0},{3,1},{4,2},{5,3},{6,4},{7,5},{8,6},{9,7},{10,8},{11,9},{12,... | collective-permute-start | bytes 786440 | tf_op jit(solution)/shard_map/ppermute | solution.py:18
  92.9 17.4 %collective-permute-start.14 = (bf16[2,128,512]{2,1,0:T(8,128)(2,1)S(1)}, bf16[2,128,512]{2,1,0:T(8,128)(2,1)S(1)}, u32[]{:S(2)}, u32[]{:S(2)}) collective-permute-start(bf16[2,128,512]{2,1,0:T(8,128)(2,1)S(1)} %copy-done.28), channel_id=1, source_target_pairs={{4,0},{5,1},{6,2},{7,3},{8,4},{9,5},{10,6},{11,7},{12,8},{13,9},{1... | collective-permute-start | bytes 786440 | tf_op jit(solution)/shard_map/ppermute | solution.py:18
  94.2 30.2 %collective-permute-start.15 = (bf16[2,128,512]{2,1,0:T(8,128)(2,1)S(1)}, bf16[2,128,512]{2,1,0:T(8,128)(2,1)S(1)}, u32[]{:S(2)}, u32[]{:S(2)}) collective-permute-start(bf16[2,128,512]{2,1,0:T(8,128)(2,1)S(1)} %copy-done.27), channel_id=1, source_target_pairs={{8,0},{9,1},{10,2},{11,3},{12,4},{13,5},{14,6},{15,7},{24,16},{25,... | collective-permute-start | bytes 786440 | tf_op jit(solution)/shard_map/ppermute | solution.py:18
  95.5 31.8 %copy-start.11 = (bf16[2,128,768]{2,1,0:T(8,128)(2,1)}, bf16[2,128,768]{2,1,0:T(8,128)(2,1)S(1)}, u32[]{:S(2)}) copy-start(bf16[2,128,768]{2,1,0:T(8,128)(2,1)S(1)} %collective-permute-done.8.refs_4_) | copy-start | bytes 1179652
  95.5 31.8 %collective-permute-start.9 = (bf16[2,128,768]{2,1,0:T(8,128)(2,1)S(1)}, bf16[2,128,768]{2,1,0:T(8,128)(2,1)S(1)}, u32[]{:S(2)}, u32[]{:S(2)}) collective-permute-start(bf16[2,128,768]{2,1,0:T(8,128)(2,1)S(1)} %collective-permute-done.8.refs_4_), channel_id=1, source_target_pairs={{0,1},{1,2},{2,3},{3,4},{4,5},{5,6},{6,7},{7,8},{8,9},{9,10},{10,1... | collective-permute-start | bytes 1179656 | tf_op jit(solution)/shard_map/ppermute | solution.py:18
  102.6 34.9 %collective-permute-start.16 = (bf16[2,128,768]{2,1,0:T(8,128)(2,1)}, bf16[2,128,768]{2,1,0:T(8,128)(2,1)S(1)}, u32[]{:S(2)}, u32[]{:S(2)}) collective-permute-start(bf16[2,128,768]{2,1,0:T(8,128)(2,1)} %get-tuple-element.45), channel_id=1, source_target_pairs={{1,0},{2,1},{3,2},{4,3},{5,4},{6,5},{7,6},{8,7},{9,8},{10,9},{11,1... | collective-permute-start | bytes 1179656 | tf_op jit(solution)/shard_map/ppermute | solution.py:18
  110.3 28.5 %collective-permute-start.17 = (bf16[2,128,768]{2,1,0:T(8,128)(2,1)}, bf16[2,128,768]{2,1,0:T(8,128)(2,1)S(1)}, u32[]{:S(2)}, u32[]{:S(2)}) collective-permute-start(bf16[2,128,768]{2,1,0:T(8,128)(2,1)} %get-tuple-element.46), channel_id=1, source_target_pairs={{2,0},{3,1},{4,2},{5,3},{6,4},{7,5},{8,6},{9,7},{10,8},{11,9},{12,... | collective-permute-start | bytes 1179656 | tf_op jit(solution)/shard_map/ppermute | solution.py:18
  124.5 15.6 %collective-permute-start.18 = (bf16[2,128,768]{2,1,0:T(8,128)(2,1)}, bf16[2,128,768]{2,1,0:T(8,128)(2,1)S(1)}, u32[]{:S(2)}, u32[]{:S(2)}) collective-permute-start(bf16[2,128,768]{2,1,0:T(8,128)(2,1)} %get-tuple-element.47), channel_id=1, source_target_pairs={{4,0},{5,1},{6,2},{7,3},{8,4},{9,5},{10,6},{11,7},{12,8},{13,9},{1... | collective-permute-start | bytes 1179656 | tf_op jit(solution)/shard_map/ppermute | solution.py:18
  125.8 43.3 %collective-permute-start.19 = (bf16[2,128,768]{2,1,0:T(8,128)(2,1)}, bf16[2,128,768]{2,1,0:T(8,128)(2,1)S(1)}, u32[]{:S(2)}, u32[]{:S(2)}) collective-permute-start(bf16[2,128,768]{2,1,0:T(8,128)(2,1)} %get-tuple-element.48), channel_id=1, source_target_pairs={{8,0},{9,1},{10,2},{11,3},{12,4},{13,5},{14,6},{15,7},{24,16},{25,... | collective-permute-start | bytes 1179656 | tf_op jit(solution)/shard_map/ppermute | solution.py:18
  128.1 41.0 %copy-start.7 = (bf16[2,128,768]{2,1,0:T(8,128)(2,1)S(1)}, bf16[2,128,768]{2,1,0:T(8,128)(2,1)}, u32[]{:S(2)}) copy-start(bf16[2,128,768]{2,1,0:T(8,128)(2,1)} %get-tuple-element.44) | copy-start | bytes 1179652
  136.2 36.1 %collective-permute-start.20 = (bf16[2,128,768]{2,1,0:T(8,128)(2,1)}, bf16[2,128,768]{2,1,0:T(8,128)(2,1)S(1)}, u32[]{:S(2)}, u32[]{:S(2)}) collective-permute-start(bf16[2,128,768]{2,1,0:T(8,128)(2,1)} %get-tuple-element.50), channel_id=1, source_target_pairs={{1,0},{2,1},{3,2},{4,3},{5,4},{6,5},{7,6},{8,7},{9,8},{10,9},{11,1... | collective-permute-start | bytes 1179656 | tf_op jit(solution)/shard_map/ppermute | solution.py:18
  137.5 34.8 %collective-permute-start.21 = (bf16[2,128,768]{2,1,0:T(8,128)(2,1)}, bf16[2,128,768]{2,1,0:T(8,128)(2,1)S(1)}, u32[]{:S(2)}, u32[]{:S(2)}) collective-permute-start(bf16[2,128,768]{2,1,0:T(8,128)(2,1)} %get-tuple-element.51), channel_id=1, source_target_pairs={{2,0},{3,1},{4,2},{5,3},{6,4},{7,5},{8,6},{9,7},{10,8},{11,9},{12,... | collective-permute-start | bytes 1179656 | tf_op jit(solution)/shard_map/ppermute | solution.py:18
  138.8 33.5 %collective-permute-start.22 = (bf16[2,128,768]{2,1,0:T(8,128)(2,1)}, bf16[2,128,768]{2,1,0:T(8,128)(2,1)S(1)}, u32[]{:S(2)}, u32[]{:S(2)}) collective-permute-start(bf16[2,128,768]{2,1,0:T(8,128)(2,1)} %get-tuple-element.52), channel_id=1, source_target_pairs={{4,0},{5,1},{6,2},{7,3},{8,4},{9,5},{10,6},{11,7},{12,8},{13,9},{1... | collective-permute-start | bytes 1179656 | tf_op jit(solution)/shard_map/ppermute | solution.py:18
  140.1 57.3 %collective-permute-start.23 = (bf16[2,128,768]{2,1,0:T(8,128)(2,1)}, bf16[2,128,768]{2,1,0:T(8,128)(2,1)S(1)}, u32[]{:S(2)}, u32[]{:S(2)}) collective-permute-start(bf16[2,128,768]{2,1,0:T(8,128)(2,1)} %get-tuple-element.53), channel_id=1, source_target_pairs={{8,0},{9,1},{10,2},{11,3},{12,4},{13,5},{14,6},{15,7},{24,16},{25,... | collective-permute-start | bytes 1179656 | tf_op jit(solution)/shard_map/ppermute | solution.py:18
  171.4 26.0 %copy-start.8 = (bf16[2,128,768]{2,1,0:T(8,128)(2,1)S(1)}, bf16[2,128,768]{2,1,0:T(8,128)(2,1)}, u32[]{:S(2)}) copy-start(bf16[2,128,768]{2,1,0:T(8,128)(2,1)} %get-tuple-element.49) | copy-start | bytes 1179652
  (23 other events, 125.6 us)

commit v10 on v8

--- a/solution.py
+++ b/solution.py
@@ -173,8 +173,9 @@
     for chunk, cols in enumerate(columns):
         key_c, value_c = key_rot[:, cols], values[:, cols]
         if pending:
-            key_c, value_c, _ = lax.optimization_barrier((key_c, value_c, pieces[-1][0]))
+            key_c, value_c, _ = lax.optimization_barrier((key_c, value_c, arrived))
         received = send_chunk(key_c, value_c, offsets)
+        arrived = received[1:]
         output, query_grad, own, outgoing = attend_chunk(
             query_rot[:, cols], received, grad_out[:, cols], allowed, offsets, chunk_heads
         )

time: 196 us -> 190 us (0.969)
  waiting for transfers between devices: 107 us -> 101 us
    ppermute x16, waiting for transfers between devices: 107 us -> 101 us  [from_behind(): lax.ppermute(value, axis, [(source, source + steps) for source in range(l...]
    unnamed x48 -> x50, local copies, waits for them, and re-layouts: 8.77 us -> 10 us
  transfers between devices with their start and end apart: 16 -> 16, of which waited for: 9 -> 7; matrix products, arithmetic and copies ran while one was open for 3% -> 2% of each run, Pallas kernels for 5% -> 11%
where the time goes in v10:
time: 190 us; the launch traced here: 189 us
  waiting for transfers between devices  101 us (53%)
  starting transfers between devices  45.2 us (24%)
  Pallas kernels  20.3 us (11%)
  local copies, waits for them, and re-layouts  12.8 us (7%)
  other arithmetic  7.6 us (4%)
    ppermute x16, waiting for transfers between devices, from_behind(): lax.ppermute(value, axis, [(source, source + steps) for source in range(l...  101 us
    ppermute x16, starting transfers between devices, from_behind(): lax.ppermute(value, axis, [(source, source + steps) for source in range(l...  45.2 us
    pallas_call x2, Pallas kernels, attend_chunk(): pl.pallas_call(attention_kernel, grid=(heads,), in_specs=[flat_spec, flat...  20.3 us
    unnamed x50, local copies, waits for them, and re-layouts  10 us
  transfers between devices with their start and end apart: 16, of which 7 were waited for; matrix products, arithmetic and copies ran while one was open for 2% of the time, Pallas kernels for 11%

profile of v10, /device:TPU:0, one launch (start us, length us, event | category | flops | bytes accessed | tf_op | source)
XLA Modules:
  0.0 188.8 jit_solution(795028976685730455)
XLA Ops:
  1.7 1.1 convert_bitcast_fusion.1
  6.2 1.0 copy-done.3
  7.3 2.4 %collective-permute-start = (bf16[2,128,1024]{2,1,0:T(8,128)(2,1)S(1)}, bf16[2,128,1024]{2,1,0:T(8,128)(2,1)S(1)}, u32[]{:S(2)}, u32[]{:S(2)}) collective-permute-start(bf16[2,128,1024]{2,1,0:T(8,128)(2,1)S(1)} %pad_maximum_fusion.2.refs_3_), channel_id=1, source_target_pairs={{0,1},{1,2},{2,3},{3,4},{4,5},{5,6},{6,7},{7,8},{8,9},{9,10},{10,1... | collective-permute-start | bytes 1572872 | tf_op jit(solution)/shard_map/ppermute | solution.py:18
  9.7 4.5 %collective-permute-start.2 = (bf16[2,128,1024]{2,1,0:T(8,128)(2,1)S(1)}, bf16[2,128,1024]{2,1,0:T(8,128)(2,1)S(1)}, u32[]{:S(2)}, u32[]{:S(2)}) collective-permute-start(bf16[2,128,1024]{2,1,0:T(8,128)(2,1)S(1)} %pad_maximum_fusion.2.refs_3_), channel_id=1, source_target_pairs={{0,4},{1,5},{2,6},{3,7},{4,8},{5,9},{6,10},{7,11},{8,12},{9,13},{1... | collective-permute-start | bytes 1572872 | tf_op jit(solution)/shard_map/ppermute | solution.py:18
  14.2 6.1 %collective-permute-start.1 = (bf16[2,128,1024]{2,1,0:T(8,128)(2,1)S(1)}, bf16[2,128,1024]{2,1,0:T(8,128)(2,1)S(1)}, u32[]{:S(2)}, u32[]{:S(2)}) collective-permute-start(bf16[2,128,1024]{2,1,0:T(8,128)(2,1)S(1)} %collective-permute-done.refs_4_), channel_id=1, source_target_pairs={{0,1},{1,2},{2,3},{3,4},{4,5},{5,6},{6,7},{7,8},{8,9},{9,10},{10,1... | collective-permute-start | bytes 1572872 | tf_op jit(solution)/shard_map/ppermute | solution.py:18
  20.3 5.5 %collective-permute-done.2.refs_6_ = bf16[2,128,1024]{2,1,0:T(8,128)(2,1)S(1)} collective-permute-done((bf16[2,128,1024]{2,1,0:T(8,128)(2,1)S(1)}, bf16[2,128,1024]{2,1,0:T(8,128)(2,1)S(1)}, u32[]{:S(2)}, u32[]{:S(2)}) %collective-permute-start.2) | collective-permute-done | bytes 524320 | tf_op jit(solution)/shard_map/ppermute | solution.py:18
  25.8 4.4 %collective-permute-start.3 = (bf16[2,128,1024]{2,1,0:T(8,128)(2,1)S(1)}, bf16[2,128,1024]{2,1,0:T(8,128)(2,1)S(1)}, u32[]{:S(2)}, u32[]{:S(2)}) collective-permute-start(bf16[2,128,1024]{2,1,0:T(8,128)(2,1)S(1)} %collective-permute-done.2.refs_6_), channel_id=1, source_target_pairs={{0,4},{1,5},{2,6},{3,7},{4,8},{5,9},{6,10},{7,11},{8,12},{9,13},{1... | collective-permute-start | bytes 1572872 | tf_op jit(solution)/shard_map/ppermute | solution.py:18
  30.9 11.1 %collective-permute-done.3.refs_7_ = bf16[2,128,1024]{2,1,0:T(8,128)(2,1)S(1)} collective-permute-done((bf16[2,128,1024]{2,1,0:T(8,128)(2,1)S(1)}, bf16[2,128,1024]{2,1,0:T(8,128)(2,1)S(1)}, u32[]{:S(2)}, u32[]{:S(2)}) %collective-permute-start.3) | collective-permute-done | bytes 524320 | tf_op jit(solution)/shard_map/ppermute | solution.py:18
  42.8 1.6 collective-permute-start.4
  45.2 4.8 %collective-permute-start.6 = (bf16[2,128,1024]{2,1,0:T(8,128)(2,1)S(1)}, bf16[2,128,1024]{2,1,0:T(8,128)(2,1)S(1)}, u32[]{:S(2)}, u32[]{:S(2)}) collective-permute-start(bf16[2,128,1024]{2,1,0:T(8,128)(2,1)S(1)} %pad_maximum_fusion.3.refs_3_), channel_id=1, source_target_pairs={{0,4},{1,5},{2,6},{3,7},{4,8},{5,9},{6,10},{7,11},{8,12},{9,13},{1... | collective-permute-start | bytes 1572872 | tf_op jit(solution)/shard_map/ppermute | solution.py:18
  50.0 6.5 %collective-permute-start.5 = (bf16[2,128,1024]{2,1,0:T(8,128)(2,1)S(1)}, bf16[2,128,1024]{2,1,0:T(8,128)(2,1)}, u32[]{:S(2)}, u32[]{:S(2)}) collective-permute-start(bf16[2,128,1024]{2,1,0:T(8,128)(2,1)S(1)} %collective-permute-done.4.refs_4_), channel_id=1, source_target_pairs={{0,1},{1,2},{2,3},{3,4},{4,5},{5,6},{6,7},{7,8},{8,9},{9,10},{10,1... | collective-permute-start | bytes 1572872 | tf_op jit(solution)/shard_map/ppermute | solution.py:18
  56.8 0.8 fusion.3
  58.0 0.9 fusion.2
  58.9 1.4 collective-permute-done.6.refs_6_
  60.3 4.7 %collective-permute-start.7 = (bf16[2,128,1024]{2,1,0:T(8,128)(2,1)S(1)}, bf16[2,128,1024]{2,1,0:T(8,128)(2,1)S(1)}, u32[]{:S(2)}, u32[]{:S(2)}) collective-permute-start(bf16[2,128,1024]{2,1,0:T(8,128)(2,1)S(1)} %collective-permute-done.6.refs_6_), channel_id=1, source_target_pairs={{0,4},{1,5},{2,6},{3,7},{4,8},{5,9},{6,10},{7,11},{8,12},{9,13},{1... | collective-permute-start | bytes 1572872 | tf_op jit(solution)/shard_map/ppermute | solution.py:18
  64.9 0.9 copy.16.refs_2_
  65.8 10.1 %shard_map.102 = (bf16[128,1024]{1,0:T(8,128)(2,1)}, f32[128,1024]{1,0:T(8,128)}, bf16[2,128,1024]{2,1,0:T(8,128)(2,1)}, bf16[2,128,1024]{2,1,0:T(8,128)(2,1)}, ...) custom-call(bf16[128,1024]{1,0:T(8,128)(2,1)} %get-tuple-element.50.refs_0_, ...), custom_call_target="tpu_custom_call" | custom-call | tf_op jit(solution)/shard_map/pallas_call | solution.py:127
  76.0 1.3 collective-permute-start.10
  77.3 1.3 collective-permute-start.11
  78.6 1.3 collective-permute-start.8
  79.9 1.3 collective-permute-start.9
  82.0 10.2 %shard_map.103 = (bf16[128,1024]{1,0:T(8,128)(2,1)}, f32[128,1024]{1,0:T(8,128)}, bf16[2,128,1024]{2,1,0:T(8,128)(2,1)}, bf16[2,128,1024]{2,1,0:T(8,128)(2,1)}, ...) custom-call(bf16[128,1024]{1,0:T(8,128)(2,1)} %get-tuple-element.51.refs_0_, ...), custom_call_target="tpu_custom_call" | custom-call | tf_op jit(solution)/shard_map/pallas_call | solution.py:127
  92.1 1.3 collective-permute-start.12
  93.8 1.3 collective-permute-start.13
  95.1 22.5 %collective-permute-done.11 = bf16[2,128,1024]{2,1,0:T(8,128)(2,1)S(1)} collective-permute-done((bf16[2,128,1024]{2,1,0:T(8,128)(2,1)}, bf16[2,128,1024]{2,1,0:T(8,128)(2,1)S(1)}, u32[]{:S(2)}, u32[]{:S(2)}) %collective-permute-start.11) | collective-permute-done | bytes 524320 | tf_op jit(solution)/shard_map/ppermute | solution.py:18
  117.5 1.3 collective-permute-start.14
  118.8 1.3 collective-permute-start.15
  120.8 1.0 copy-done.5
  123.9 25.5 %collective-permute-done.14 = bf16[2,128,1024]{2,1,0:T(8,128)(2,1)S(1)} collective-permute-done((bf16[2,128,1024]{2,1,0:T(8,128)(2,1)}, bf16[2,128,1024]{2,1,0:T(8,128)(2,1)S(1)}, u32[]{:S(2)}, u32[]{:S(2)}) %collective-permute-start.14) | collective-permute-done | bytes 524320 | tf_op jit(solution)/shard_map/ppermute | solution.py:18
  149.3 34.7 %collective-permute-done.15 = bf16[2,128,1024]{2,1,0:T(8,128)(2,1)S(1)} collective-permute-done((bf16[2,128,1024]{2,1,0:T(8,128)(2,1)}, bf16[2,128,1024]{2,1,0:T(8,128)(2,1)S(1)}, u32[]{:S(2)}, u32[]{:S(2)}) %collective-permute-start.15) | collective-permute-done | bytes 524320 | tf_op jit(solution)/shard_map/ppermute | solution.py:18
  185.8 0.9 copy.31
  187.0 0.9 copy.32
  (86 shorter events, 13.2 us)
Async XLA Ops:
  2.9 1.0 copy-start.2
  6.1 1.0 copy-start.3
  7.2 35.6 %copy-start.1 = (bf16[2,128,1024]{2,1,0:T(8,128)(2,1)}, bf16[2,128,1024]{2,1,0:T(8,128)(2,1)S(1)}, u32[]{:S(2)}) copy-start(bf16[2,128,1024]{2,1,0:T(8,128)(2,1)S(1)} %pad_maximum_fusion.2.refs_3_) | copy-start | bytes 1572868
  7.3 6.9 %collective-permute-start = (bf16[2,128,1024]{2,1,0:T(8,128)(2,1)S(1)}, bf16[2,128,1024]{2,1,0:T(8,128)(2,1)S(1)}, u32[]{:S(2)}, u32[]{:S(2)}) collective-permute-start(bf16[2,128,1024]{2,1,0:T(8,128)(2,1)S(1)} %pad_maximum_fusion.2.refs_3_), channel_id=1, source_target_pairs={{0,1},{1,2},{2,3},{3,4},{4,5},{5,6},{6,7},{7,8},{8,9},{9,10},{10,1... | collective-permute-start | bytes 1572872 | tf_op jit(solution)/shard_map/ppermute | solution.py:18
  9.7 16.2 %collective-permute-start.2 = (bf16[2,128,1024]{2,1,0:T(8,128)(2,1)S(1)}, bf16[2,128,1024]{2,1,0:T(8,128)(2,1)S(1)}, u32[]{:S(2)}, u32[]{:S(2)}) collective-permute-start(bf16[2,128,1024]{2,1,0:T(8,128)(2,1)S(1)} %pad_maximum_fusion.2.refs_3_), channel_id=1, source_target_pairs={{0,4},{1,5},{2,6},{3,7},{4,8},{5,9},{6,10},{7,11},{8,12},{9,13},{1... | collective-permute-start | bytes 1572872 | tf_op jit(solution)/shard_map/ppermute | solution.py:18
  14.2 28.7 %copy-start.7 = (bf16[2,128,1024]{2,1,0:T(8,128)(2,1)}, bf16[2,128,1024]{2,1,0:T(8,128)(2,1)S(1)}, u32[]{:S(2)}) copy-start(bf16[2,128,1024]{2,1,0:T(8,128)(2,1)S(1)} %collective-permute-done.refs_4_) | copy-start | bytes 1572868
  14.2 16.7 %collective-permute-start.1 = (bf16[2,128,1024]{2,1,0:T(8,128)(2,1)S(1)}, bf16[2,128,1024]{2,1,0:T(8,128)(2,1)S(1)}, u32[]{:S(2)}, u32[]{:S(2)}) collective-permute-start(bf16[2,128,1024]{2,1,0:T(8,128)(2,1)S(1)} %collective-permute-done.refs_4_), channel_id=1, source_target_pairs={{0,1},{1,2},{2,3},{3,4},{4,5},{5,6},{6,7},{7,8},{8,9},{9,10},{10,1... | collective-permute-start | bytes 1572872 | tf_op jit(solution)/shard_map/ppermute | solution.py:18
  25.8 31.8 %copy-start.9 = (bf16[2,128,1024]{2,1,0:T(8,128)(2,1)}, bf16[2,128,1024]{2,1,0:T(8,128)(2,1)S(1)}, u32[]{:S(2)}) copy-start(bf16[2,128,1024]{2,1,0:T(8,128)(2,1)S(1)} %collective-permute-done.2.refs_6_) | copy-start | bytes 1572868
  25.8 16.1 %collective-permute-start.3 = (bf16[2,128,1024]{2,1,0:T(8,128)(2,1)S(1)}, bf16[2,128,1024]{2,1,0:T(8,128)(2,1)S(1)}, u32[]{:S(2)}, u32[]{:S(2)}) collective-permute-start(bf16[2,128,1024]{2,1,0:T(8,128)(2,1)S(1)} %collective-permute-done.2.refs_6_), channel_id=1, source_target_pairs={{0,4},{1,5},{2,6},{3,7},{4,8},{5,9},{6,10},{7,11},{8,12},{9,13},{1... | collective-permute-start | bytes 1572872 | tf_op jit(solution)/shard_map/ppermute | solution.py:18
  30.9 26.7 %copy-start.12 = (bf16[2,128,1024]{2,1,0:T(8,128)(2,1)}, bf16[2,128,1024]{2,1,0:T(8,128)(2,1)S(1)}, u32[]{:S(2)}) copy-start(bf16[2,128,1024]{2,1,0:T(8,128)(2,1)S(1)} %collective-permute-done.1.refs_5_) | copy-start | bytes 1572868
  42.8 13.9 %copy-start = (bf16[2,128,1024]{2,1,0:T(8,128)(2,1)}, bf16[2,128,1024]{2,1,0:T(8,128)(2,1)S(1)}, u32[]{:S(2)}) copy-start(bf16[2,128,1024]{2,1,0:T(8,128)(2,1)S(1)} %pad_maximum_fusion.3.refs_3_) | copy-start | bytes 1572868
  42.8 7.1 %collective-permute-start.4 = (bf16[2,128,1024]{2,1,0:T(8,128)(2,1)S(1)}, bf16[2,128,1024]{2,1,0:T(8,128)(2,1)S(1)}, u32[]{:S(2)}, u32[]{:S(2)}) collective-permute-start(bf16[2,128,1024]{2,1,0:T(8,128)(2,1)S(1)} %pad_maximum_fusion.3.refs_3_), channel_id=1, source_target_pairs={{0,1},{1,2},{2,3},{3,4},{4,5},{5,6},{6,7},{7,8},{8,9},{9,10},{10,1... | collective-permute-start | bytes 1572872 | tf_op jit(solution)/shard_map/ppermute | solution.py:18
  45.2 15.0 %collective-permute-start.6 = (bf16[2,128,1024]{2,1,0:T(8,128)(2,1)S(1)}, bf16[2,128,1024]{2,1,0:T(8,128)(2,1)S(1)}, u32[]{:S(2)}, u32[]{:S(2)}) collective-permute-start(bf16[2,128,1024]{2,1,0:T(8,128)(2,1)S(1)} %pad_maximum_fusion.3.refs_3_), channel_id=1, source_target_pairs={{0,4},{1,5},{2,6},{3,7},{4,8},{5,9},{6,10},{7,11},{8,12},{9,13},{1... | collective-permute-start | bytes 1572872 | tf_op jit(solution)/shard_map/ppermute | solution.py:18
  50.0 6.8 %copy-start.6 = (bf16[2,128,1024]{2,1,0:T(8,128)(2,1)}, bf16[2,128,1024]{2,1,0:T(8,128)(2,1)S(1)}, u32[]{:S(2)}) copy-start(bf16[2,128,1024]{2,1,0:T(8,128)(2,1)S(1)} %collective-permute-done.4.refs_4_) | copy-start | bytes 1572868
  50.0 29.9 %collective-permute-start.5 = (bf16[2,128,1024]{2,1,0:T(8,128)(2,1)S(1)}, bf16[2,128,1024]{2,1,0:T(8,128)(2,1)}, u32[]{:S(2)}, u32[]{:S(2)}) collective-permute-start(bf16[2,128,1024]{2,1,0:T(8,128)(2,1)S(1)} %collective-permute-done.4.refs_4_), channel_id=1, source_target_pairs={{0,1},{1,2},{2,3},{3,4},{4,5},{5,6},{6,7},{7,8},{8,9},{9,10},{10,1... | collective-permute-start | bytes 1572872 | tf_op jit(solution)/shard_map/ppermute | solution.py:18
  56.8 1.2 copy-start.4
  60.3 15.7 %copy-start.11 = (bf16[2,128,1024]{2,1,0:T(8,128)(2,1)}, bf16[2,128,1024]{2,1,0:T(8,128)(2,1)S(1)}, u32[]{:S(2)}) copy-start(bf16[2,128,1024]{2,1,0:T(8,128)(2,1)S(1)} %collective-permute-done.6.refs_6_) | copy-start | bytes 1572868
  60.3 20.9 %collective-permute-start.7 = (bf16[2,128,1024]{2,1,0:T(8,128)(2,1)S(1)}, bf16[2,128,1024]{2,1,0:T(8,128)(2,1)S(1)}, u32[]{:S(2)}, u32[]{:S(2)}) collective-permute-start(bf16[2,128,1024]{2,1,0:T(8,128)(2,1)S(1)} %collective-permute-done.6.refs_6_), channel_id=1, source_target_pairs={{0,4},{1,5},{2,6},{3,7},{4,8},{5,9},{6,10},{7,11},{8,12},{9,13},{1... | collective-permute-start | bytes 1572872 | tf_op jit(solution)/shard_map/ppermute | solution.py:18
  76.0 17.8 %collective-permute-start.10 = (bf16[2,128,1024]{2,1,0:T(8,128)(2,1)}, bf16[2,128,1024]{2,1,0:T(8,128)(2,1)S(1)}, u32[]{:S(2)}, u32[]{:S(2)}) collective-permute-start(bf16[2,128,1024]{2,1,0:T(8,128)(2,1)} %get-tuple-element.29), channel_id=1, source_target_pairs={{4,0},{5,1},{6,2},{7,3},{8,4},{9,5},{10,6},{11,7},{12,8},{13,9},{1... | collective-permute-start | bytes 1572872 | tf_op jit(solution)/shard_map/ppermute | solution.py:18
  77.3 40.3 %collective-permute-start.11 = (bf16[2,128,1024]{2,1,0:T(8,128)(2,1)}, bf16[2,128,1024]{2,1,0:T(8,128)(2,1)S(1)}, u32[]{:S(2)}, u32[]{:S(2)}) collective-permute-start(bf16[2,128,1024]{2,1,0:T(8,128)(2,1)} %get-tuple-element.30), channel_id=1, source_target_pairs={{8,0},{9,1},{10,2},{11,3},{12,4},{13,5},{14,6},{15,7},{24,16},{25,... | collective-permute-start | bytes 1572872 | tf_op jit(solution)/shard_map/ppermute | solution.py:18
  78.6 40.3 %collective-permute-start.8 = (bf16[2,128,1024]{2,1,0:T(8,128)(2,1)}, bf16[2,128,1024]{2,1,0:T(8,128)(2,1)S(1)}, u32[]{:S(2)}, u32[]{:S(2)}) collective-permute-start(bf16[2,128,1024]{2,1,0:T(8,128)(2,1)} %get-tuple-element.27), channel_id=1, source_target_pairs={{1,0},{2,1},{3,2},{4,3},{5,4},{6,5},{7,6},{8,7},{9,8},{10,9},{11,1... | collective-permute-start | bytes 1572872 | tf_op jit(solution)/shard_map/ppermute | solution.py:18
  79.9 40.3 %collective-permute-start.9 = (bf16[2,128,1024]{2,1,0:T(8,128)(2,1)}, bf16[2,128,1024]{2,1,0:T(8,128)(2,1)S(1)}, u32[]{:S(2)}, u32[]{:S(2)}) collective-permute-start(bf16[2,128,1024]{2,1,0:T(8,128)(2,1)} %get-tuple-element.28), channel_id=1, source_target_pairs={{2,0},{3,1},{4,2},{5,3},{6,4},{7,5},{8,6},{9,7},{10,8},{11,9},{12,... | collective-permute-start | bytes 1572872 | tf_op jit(solution)/shard_map/ppermute | solution.py:18
  82.0 38.2 %copy-start.8 = (bf16[2,128,1024]{2,1,0:T(8,128)(2,1)S(1)}, bf16[2,128,1024]{2,1,0:T(8,128)(2,1)}, u32[]{:S(2)}) copy-start(bf16[2,128,1024]{2,1,0:T(8,128)(2,1)} %get-tuple-element.26) | copy-start | bytes 1572868
  92.1 31.7 %collective-permute-start.12 = (bf16[2,128,1024]{2,1,0:T(8,128)(2,1)}, bf16[2,128,1024]{2,1,0:T(8,128)(2,1)S(1)}, u32[]{:S(2)}, u32[]{:S(2)}) collective-permute-start(bf16[2,128,1024]{2,1,0:T(8,128)(2,1)} %get-tuple-element.32), channel_id=1, source_target_pairs={{1,0},{2,1},{3,2},{4,3},{5,4},{6,5},{7,6},{8,7},{9,8},{10,9},{11,1... | collective-permute-start | bytes 1572872 | tf_op jit(solution)/shard_map/ppermute | solution.py:18
  93.8 30.1 %collective-permute-start.13 = (bf16[2,128,1024]{2,1,0:T(8,128)(2,1)}, bf16[2,128,1024]{2,1,0:T(8,128)(2,1)S(1)}, u32[]{:S(2)}, u32[]{:S(2)}) collective-permute-start(bf16[2,128,1024]{2,1,0:T(8,128)(2,1)} %get-tuple-element.33), channel_id=1, source_target_pairs={{2,0},{3,1},{4,2},{5,3},{6,4},{7,5},{8,6},{9,7},{10,8},{11,9},{12,... | collective-permute-start | bytes 1572872 | tf_op jit(solution)/shard_map/ppermute | solution.py:18
  117.5 31.8 %collective-permute-start.14 = (bf16[2,128,1024]{2,1,0:T(8,128)(2,1)}, bf16[2,128,1024]{2,1,0:T(8,128)(2,1)S(1)}, u32[]{:S(2)}, u32[]{:S(2)}) collective-permute-start(bf16[2,128,1024]{2,1,0:T(8,128)(2,1)} %get-tuple-element.34), channel_id=1, source_target_pairs={{4,0},{5,1},{6,2},{7,3},{8,4},{9,5},{10,6},{11,7},{12,8},{13,9},{1... | collective-permute-start | bytes 1572872 | tf_op jit(solution)/shard_map/ppermute | solution.py:18
  118.8 65.2 %collective-permute-start.15 = (bf16[2,128,1024]{2,1,0:T(8,128)(2,1)}, bf16[2,128,1024]{2,1,0:T(8,128)(2,1)S(1)}, u32[]{:S(2)}, u32[]{:S(2)}) collective-permute-start(bf16[2,128,1024]{2,1,0:T(8,128)(2,1)} %get-tuple-element.35), channel_id=1, source_target_pairs={{8,0},{9,1},{10,2},{11,3},{12,4},{13,5},{14,6},{15,7},{24,16},{25,... | collective-permute-start | bytes 1572872 | tf_op jit(solution)/shard_map/ppermute | solution.py:18
  120.7 1.0 copy-start.5
  120.7 1.2 copy-start.14
  122.0 1.0 copy-start.16
  122.0 1.0 copy-start.17
  123.0 61.0 %copy-start.10 = (bf16[2,128,1024]{2,1,0:T(8,128)(2,1)S(1)}, bf16[2,128,1024]{2,1,0:T(8,128)(2,1)}, u32[]{:S(2)}) copy-start(bf16[2,128,1024]{2,1,0:T(8,128)(2,1)} %get-tuple-element.31) | copy-start | bytes 1572868
  (4 other events, 2.9 us)

commit v11 on v7

--- a/solution.py
+++ b/solution.py
@@ -8,7 +8,7 @@
 HEADS = 16
 HEAD_DIM = 128
 BLOCK = 128
-CHUNKS = 4
+CHUNK_HEADS = (6, 10)
 
 
 def from_behind(value, axis, steps):
@@ -149,12 +149,12 @@
     key_rot = rounded(rotary(key_vectors, positions, HEADS, HEAD_DIM, False))
     valid_slots = reach_mask(reach_table, shard_index * per_shard, per_shard, levels)
     allowed = score_mask(valid_slots, BLOCK)
-    chunk_heads = HEADS // CHUNKS
-    chunk_width = chunk_heads * HEAD_DIM
-    columns = [slice(chunk * chunk_width, (chunk + 1) * chunk_width) for chunk in range(CHUNKS)]
+    bounds = [sum(CHUNK_HEADS[:chunk]) * HEAD_DIM for chunk in range(len(CHUNK_HEADS) + 1)]
     pieces = []
     pending = []
-    for chunk, cols in enumerate(columns):
+    for chunk, chunk_heads in enumerate(CHUNK_HEADS):
+        chunk_width = chunk_heads * HEAD_DIM
+        cols = slice(bounds[chunk], bounds[chunk + 1])
         key_c, value_c = key_rot[:, cols], values[:, cols]
         if pending:
             key_c, value_c, _ = lax.optimization_barrier((key_c, value_c, pieces[-1][0]))

time: 228 us -> 202 us (0.89)
  starting transfers between devices: 92.5 us -> 43.5 us
  waiting for transfers between devices: 40.3 us -> 89.3 us
  other arithmetic: 33.6 us -> 16 us
  local copies, waits for them, and re-layouts: 43.6 us -> 39.3 us
    ppermute x32 -> x16, starting transfers between devices: 92.5 us -> 43.5 us  [from_behind(): lax.ppermute(value, axis, [(source, source + steps) for source in range(l...]
    ppermute x32 -> x16, waiting for transfers between devices: 40.3 us -> 89.3 us  [from_behind(): lax.ppermute(value, axis, [(source, source + steps) for source in range(l...]
    another operation x16 -> x8, other arithmetic: 17.5 us -> 4.56 us  [attend_chunk(): jnp.stack([key_terms[0, slot_index], value_terms[0, slot_index]])]
    slice x16 -> x8, local copies, waits for them, and re-layouts: 16.2 us -> 9.67 us  [attend_chunk(): moved[0].reshape(head_shape)]
    another operation x8 -> x6, other arithmetic: 6.58 us -> 2.37 us
    unnamed x131 -> x97, local copies, waits for them, and re-layouts: 5.42 us -> 8.74 us
    another operation x24 -> x12, local copies, waits for them, and re-layouts: 6.36 us -> 5.76 us  [attend_chunk(): jnp.stack([moved[0].reshape(head_shape) for moved in received])[None]]
  transfers between devices with their start and end apart: 32 -> 16, of which waited for: 7 -> 9; matrix products, arithmetic and copies ran while one was open for 26% -> 11% of each run, Pallas kernels for 0% -> 0%
where the time goes in v11:
time: 202 us; the launch traced here: 201 us
  waiting for transfers between devices  89.3 us (44%)
  starting transfers between devices  43.5 us (22%)
  local copies, waits for them, and re-layouts  39.3 us (19%)
  other arithmetic  16 us (8%)
  matrix products  10.7 us (5%)
  between operations  2.36 us (1%)
    ppermute x16, waiting for transfers between devices, from_behind(): lax.ppermute(value, axis, [(source, source + steps) for source in range(l...  89.3 us
    ppermute x16, starting transfers between devices, from_behind(): lax.ppermute(value, axis, [(source, source + steps) for source in range(l...  43.5 us
    slice x8, local copies, waits for them, and re-layouts, attend_chunk(): moved[0].reshape(head_shape)  9.67 us
    unnamed x97, local copies, waits for them, and re-layouts  8.74 us
    another operation x12, local copies, waits for them, and re-layouts, attend_chunk(): jnp.stack([moved[0].reshape(head_shape) for moved in received])[None]  5.76 us
    another operation x8, other arithmetic, attend_chunk(): jnp.stack([key_terms[0, slot_index], value_terms[0, slot_index]])  4.56 us
  transfers between devices with their start and end apart: 16, of which 9 were waited for; matrix products, arithmetic and copies ran while one was open for 11% of the time, Pallas kernels for 0%

profile of v11, /device:TPU:15, one launch (start us, length us, event | category | flops | bytes accessed | tf_op | source)
XLA Modules:
  0.0 201.1 jit_solution(1823739657482505886)
XLA Ops:
  3.6 1.2 copy.191
  6.7 3.3 %collective-permute-start.2 = (bf16[2,128,768]{1,2,0:T(8,128)(2,1)}, bf16[2,128,768]{1,2,0:T(8,128)(2,1)}, u32[]{:S(2)}, u32[]{:S(2)}) collective-permute-start(bf16[2,128,768]{1,2,0:T(8,128)(2,1)} %pad_maximum_fusion.13), channel_id=1, source_target_pairs={{0,4},{1,5},{2,6},{3,7},{4,8},{5,9},{6,10},{7,11},{8,12},{9,13},{1... | collective-permute-start | bytes 1179656 | tf_op jit(solution)/shard_map/ppermute | solution.py:17
  10.0 4.0 %collective-permute-start = (bf16[2,128,768]{1,2,0:T(8,128)(2,1)}, bf16[2,128,768]{1,2,0:T(8,128)(2,1)S(1)}, u32[]{:S(2)}, u32[]{:S(2)}) collective-permute-start(bf16[2,128,768]{1,2,0:T(8,128)(2,1)} %pad_maximum_fusion.13), channel_id=1, source_target_pairs={{0,1},{1,2},{2,3},{3,4},{4,5},{5,6},{6,7},{7,8},{8,9},{9,10},{10,1... | collective-permute-start | bytes 1179656 | tf_op jit(solution)/shard_map/ppermute | solution.py:17
  19.0 3.2 %collective-permute-start.3 = (bf16[2,128,768]{1,2,0:T(8,128)(2,1)}, bf16[2,128,768]{1,2,0:T(8,128)(2,1)}, u32[]{:S(2)}, u32[]{:S(2)}) collective-permute-start(bf16[2,128,768]{1,2,0:T(8,128)(2,1)} %collective-permute-done.2), channel_id=1, source_target_pairs={{0,4},{1,5},{2,6},{3,7},{4,8},{5,9},{6,10},{7,11},{8,12},{9,13},{1... | collective-permute-start | bytes 1179656 | tf_op jit(solution)/shard_map/ppermute | solution.py:17
  22.2 1.7 fusion.44
  23.9 4.8 %collective-permute-start.1 = (bf16[2,128,768]{1,2,0:T(8,128)(2,1)S(1)}, bf16[2,128,768]{1,2,0:T(8,128)(2,1)}, u32[]{:S(2)}, u32[]{:S(2)}) collective-permute-start(bf16[2,128,768]{1,2,0:T(8,128)(2,1)S(1)} %collective-permute-done), channel_id=1, source_target_pairs={{0,1},{1,2},{2,3},{3,4},{4,5},{5,6},{6,7},{7,8},{8,9},{9,10},{10,1... | collective-permute-start | bytes 1179656 | tf_op jit(solution)/shard_map/ppermute | solution.py:17
  30.0 1.7 fusion.43
  31.9 4.1 %collective-permute-done.1 = bf16[2,128,768]{1,2,0:T(8,128)(2,1)} collective-permute-done((bf16[2,128,768]{1,2,0:T(8,128)(2,1)S(1)}, bf16[2,128,768]{1,2,0:T(8,128)(2,1)}, u32[]{:S(2)}, u32[]{:S(2)}) %collective-permute-start.1) | collective-permute-done | bytes 393248 | tf_op jit(solution)/shard_map/ppermute | solution.py:17
  36.0 1.7 fusion.45
  43.0 1.7 copy.126
  45.8 2.2 %fusion.21 = bf16[1,6,128,5,128]{2,4,3,1,0:T(8,128)(2,1)S(1)} fusion(bf16[5,128,6,128]{1,3,0,2:T(8,128)(2,1)} %copy-done.14, bf16[128,6,128,1]{0,2,3,1:T(8,128)(2,1)} %bitcast.385, f32[6,128,5,128]{1,3,2,0:T(8,128)S(1)} %bitcast.357, f32[6,128]{1,0:T(8,128)S(1)} %bitcast.412, f32[6,128]{1,0:T(8,128)} %copy-done.37, pred[128,5,128]{0,2,1:T(8,128)(4,1)S(1)} %and_bitcast_fusion), kind=kOutput, calls=%fused_computation.29 | convolution fusion | flops 129269760 | bytes 4216832 | tf_op jit(solution)/shard_map/bthd,bnuhd->bhtnu/dot_general | solution.py:105
  51.3 2.2 %collective-permute-start.10 = (bf16[2,128,6,128]{1,3,2,0:T(8,128)(2,1)S(1)}, bf16[2,128,6,128]{1,3,2,0:T(8,128)(2,1)S(1)}, u32[]{:S(2)}, u32[]{:S(2)}) collective-permute-start(bf16[2,128,6,128]{1,3,2,0:T(8,128)(2,1)S(1)} %pad_maximum_fusion.16), channel_id=1, source_target_pairs={{4,0},{5,1},{6,2},{7,3},{8,4},{9,5},{10,6},{11,7},{12,8},{13,9},{1... | collective-permute-start | bytes 1179656 | tf_op jit(solution)/shard_map/ppermute | solution.py:17
  54.6 1.3 collective-permute-start.11
  55.9 2.1 %collective-permute-start.9 = (bf16[2,128,6,128]{1,3,2,0:T(8,128)(2,1)S(1)}, bf16[2,128,6,128]{1,3,2,0:T(8,128)(2,1)S(1)}, u32[]{:S(2)}, u32[]{:S(2)}) collective-permute-start(bf16[2,128,6,128]{1,3,2,0:T(8,128)(2,1)S(1)} %pad_maximum_fusion.15), channel_id=1, source_target_pairs={{2,0},{3,1},{4,2},{5,3},{6,4},{7,5},{8,6},{9,7},{10,8},{11,9},{12,... | collective-permute-start | bytes 1179656 | tf_op jit(solution)/shard_map/ppermute | solution.py:17
  58.0 4.6 %collective-permute-start.8 = (bf16[2,128,6,128]{1,3,2,0:T(8,128)(2,1)S(1)}, bf16[2,128,6,128]{1,3,2,0:T(8,128)(2,1)S(1)}, u32[]{:S(2)}, u32[]{:S(2)}) collective-permute-start(bf16[2,128,6,128]{1,3,2,0:T(8,128)(2,1)S(1)} %pad_maximum_fusion.14), channel_id=1, source_target_pairs={{1,0},{2,1},{3,2},{4,3},{5,4},{6,5},{7,6},{8,7},{9,8},{10,9},{11,1... | collective-permute-start | bytes 1179656 | tf_op jit(solution)/shard_map/ppermute | solution.py:17
  63.6 3.3 %collective-permute-start.4 = (bf16[2,128,1280]{1,2,0:T(8,128)(2,1)}, bf16[2,128,1280]{1,2,0:T(8,128)(2,1)}, u32[]{:S(2)}, u32[]{:S(2)}) collective-permute-start(bf16[2,128,1280]{1,2,0:T(8,128)(2,1)} %pad_maximum_fusion.2), channel_id=1, source_target_pairs={{0,1},{1,2},{2,3},{3,4},{4,5},{5,6},{6,7},{7,8},{8,9},{9,10},{10,1... | collective-permute-start | bytes 1966088 | tf_op jit(solution)/shard_map/ppermute | solution.py:17
  68.9 3.7 %collective-permute-start.6 = (bf16[2,128,1280]{1,2,0:T(8,128)(2,1)}, bf16[2,128,1280]{1,2,0:T(8,128)(2,1)}, u32[]{:S(2)}, u32[]{:S(2)}) collective-permute-start(bf16[2,128,1280]{1,2,0:T(8,128)(2,1)} %pad_maximum_fusion.2), channel_id=1, source_target_pairs={{0,4},{1,5},{2,6},{3,7},{4,8},{5,9},{6,10},{7,11},{8,12},{9,13},{1... | collective-permute-start | bytes 1966088 | tf_op jit(solution)/shard_map/ppermute | solution.py:17
  72.6 11.3 %collective-permute-done.9 = bf16[2,128,6,128]{1,3,2,0:T(8,128)(2,1)S(1)} collective-permute-done((bf16[2,128,6,128]{1,3,2,0:T(8,128)(2,1)S(1)}, bf16[2,128,6,128]{1,3,2,0:T(8,128)(2,1)S(1)}, u32[]{:S(2)}, u32[]{:S(2)}) %collective-permute-start.9) | collective-permute-done | bytes 393248 | tf_op jit(solution)/shard_map/ppermute | solution.py:17
  83.8 8.5 %collective-permute-done.8 = bf16[2,128,6,128]{1,3,2,0:T(8,128)(2,1)S(1)} collective-permute-done((bf16[2,128,6,128]{1,3,2,0:T(8,128)(2,1)S(1)}, bf16[2,128,6,128]{1,3,2,0:T(8,128)(2,1)S(1)}, u32[]{:S(2)}, u32[]{:S(2)}) %collective-permute-start.8) | collective-permute-done | bytes 393248 | tf_op jit(solution)/shard_map/ppermute | solution.py:17
  94.9 1.9 collective-permute-start.5
  96.8 2.1 %collective-permute-start.7 = (bf16[2,128,1280]{1,2,0:T(8,128)(2,1)}, bf16[2,128,1280]{1,2,0:T(8,128)(2,1)}, u32[]{:S(2)}, u32[]{:S(2)}) collective-permute-start(bf16[2,128,1280]{1,2,0:T(8,128)(2,1)} %collective-permute-done.6), channel_id=1, source_target_pairs={{0,4},{1,5},{2,6},{3,7},{4,8},{5,9},{6,10},{7,11},{8,12},{9,13},{1... | collective-permute-start | bytes 1966088 | tf_op jit(solution)/shard_map/ppermute | solution.py:17
  101.8 16.9 %collective-permute-done.7 = bf16[2,128,1280]{1,2,0:T(8,128)(2,1)} collective-permute-done((bf16[2,128,1280]{1,2,0:T(8,128)(2,1)}, bf16[2,128,1280]{1,2,0:T(8,128)(2,1)}, u32[]{:S(2)}, u32[]{:S(2)}) %collective-permute-start.7) | collective-permute-done | bytes 655392 | tf_op jit(solution)/shard_map/ppermute | solution.py:17
  132.1 1.5 fusion.12
  135.6 1.9 copy.127
  137.4 1.2 pad_maximum_fusion.5
  138.7 1.9 collective-permute-start.14
  141.8 1.3 collective-permute-start.15
  143.2 1.9 collective-permute-start.13
  145.2 1.9 collective-permute-start.12
  149.1 22.5 %collective-permute-done.14 = bf16[2,128,10,128]{1,3,2,0:T(8,128)(2,1)S(1)} collective-permute-done((bf16[2,128,10,128]{1,3,2,0:T(8,128)(2,1)S(1)}, bf16[2,128,10,128]{1,3,2,0:T(8,128)(2,1)S(1)}, u32[]{:S(2)}, u32[]{:S(2)}) %collective-permute-start.14) | collective-permute-done | bytes 655392 | tf_op jit(solution)/shard_map/ppermute | solution.py:17
  171.6 14.6 %collective-permute-done.13 = bf16[2,128,10,128]{1,3,2,0:T(8,128)(2,1)S(1)} collective-permute-done((bf16[2,128,10,128]{1,3,2,0:T(8,128)(2,1)S(1)}, bf16[2,128,10,128]{1,3,2,0:T(8,128)(2,1)S(1)}, u32[]{:S(2)}, u32[]{:S(2)}) %collective-permute-start.13) | collective-permute-done | bytes 655392 | tf_op jit(solution)/shard_map/ppermute | solution.py:17
  186.2 10.3 %collective-permute-done.12 = bf16[2,128,10,128]{1,3,2,0:T(8,128)(2,1)S(1)} collective-permute-done((bf16[2,128,10,128]{1,3,2,0:T(8,128)(2,1)S(1)}, bf16[2,128,10,128]{1,3,2,0:T(8,128)(2,1)S(1)}, u32[]{:S(2)}, u32[]{:S(2)}) %collective-permute-start.12) | collective-permute-done | bytes 655392 | tf_op jit(solution)/shard_map/ppermute | solution.py:17
  (200 shorter events, 52.1 us)
Async XLA Ops:
  5.6 9.1 %copy-start.38 = (s32[4]{0:T(128)S(1)}, s32[4]{0:T(128)}, u32[]{:S(2)}) copy-start(s32[4]{0:T(128)} %constant.36) | copy-start | bytes 52
  6.7 9.1 %slice-start.1 = ((bf16[128,2048]{1,0:T(8,128)(2,1)}), bf16[128,768]{1,0:T(8,128)(2,1)S(1)}, s32[]{:S(2)}) async-start(bf16[128,2048]{1,0:T(8,128)(2,1)} %param.10), calls=%async_computation.1 | async-start | bytes 393216 | tf_op jit(solution)/shard_map/slice | solution.py:163
  6.7 12.3 %collective-permute-start.2 = (bf16[2,128,768]{1,2,0:T(8,128)(2,1)}, bf16[2,128,768]{1,2,0:T(8,128)(2,1)}, u32[]{:S(2)}, u32[]{:S(2)}) collective-permute-start(bf16[2,128,768]{1,2,0:T(8,128)(2,1)} %pad_maximum_fusion.13), channel_id=1, source_target_pairs={{0,4},{1,5},{2,6},{3,7},{4,8},{5,9},{6,10},{7,11},{8,12},{9,13},{1... | collective-permute-start | bytes 1179656 | tf_op jit(solution)/shard_map/ppermute | solution.py:17
  10.0 13.9 %collective-permute-start = (bf16[2,128,768]{1,2,0:T(8,128)(2,1)}, bf16[2,128,768]{1,2,0:T(8,128)(2,1)S(1)}, u32[]{:S(2)}, u32[]{:S(2)}) collective-permute-start(bf16[2,128,768]{1,2,0:T(8,128)(2,1)} %pad_maximum_fusion.13), channel_id=1, source_target_pairs={{0,1},{1,2},{2,3},{3,4},{4,5},{5,6},{6,7},{7,8},{8,9},{9,10},{10,1... | collective-permute-start | bytes 1179656 | tf_op jit(solution)/shard_map/ppermute | solution.py:17
  15.0 110.8 %copy-start.2 = (bf16[128,1280]{0,1:T(8,128)(2,1)}, bf16[128,1280]{0,1:T(8,128)(2,1)S(1)}, u32[]{:S(2)}) copy-start(bf16[128,1280]{0,1:T(8,128)(2,1)S(1)} %slice.315) | copy-start | bytes 983044
  19.0 11.0 %collective-permute-start.3 = (bf16[2,128,768]{1,2,0:T(8,128)(2,1)}, bf16[2,128,768]{1,2,0:T(8,128)(2,1)}, u32[]{:S(2)}, u32[]{:S(2)}) collective-permute-start(bf16[2,128,768]{1,2,0:T(8,128)(2,1)} %collective-permute-done.2), channel_id=1, source_target_pairs={{0,4},{1,5},{2,6},{3,7},{4,8},{5,9},{6,10},{7,11},{8,12},{9,13},{1... | collective-permute-start | bytes 1179656 | tf_op jit(solution)/shard_map/ppermute | solution.py:17
  23.9 12.1 %collective-permute-start.1 = (bf16[2,128,768]{1,2,0:T(8,128)(2,1)S(1)}, bf16[2,128,768]{1,2,0:T(8,128)(2,1)}, u32[]{:S(2)}, u32[]{:S(2)}) collective-permute-start(bf16[2,128,768]{1,2,0:T(8,128)(2,1)S(1)} %collective-permute-done), channel_id=1, source_target_pairs={{0,1},{1,2},{2,3},{3,4},{4,5},{5,6},{6,7},{7,8},{8,9},{9,10},{10,1... | collective-permute-start | bytes 1179656 | tf_op jit(solution)/shard_map/ppermute | solution.py:17
  28.8 9.1 %copy-start.12 = (bf16[5,128,6,128]{1,3,0,2:T(8,128)(2,1)}, bf16[5,128,6,128]{1,3,0,2:T(8,128)(2,1)S(1)}, u32[]{:S(2)}) copy-start(bf16[5,128,6,128]{1,3,0,2:T(8,128)(2,1)S(1)} %constant_dynamic-update-slice_fusion.3) | copy-start | bytes 2949124
  48.6 7.2 %copy-start.29 = (bf16[1,128,6,128]{1,3,2,0:T(8,128)(2,1)S(1)}, bf16[1,128,6,128]{1,3,2,0:T(8,128)(2,1)}, u32[]{:S(2)}) copy-start(bf16[1,128,6,128]{1,3,2,0:T(8,128)(2,1)} %get-tuple-element.33) | copy-start | bytes 589828
  49.4 8.5 %copy-start.28 = (bf16[1,128,6,128]{1,3,2,0:T(8,128)(2,1)S(1)}, bf16[1,128,6,128]{1,3,2,0:T(8,128)(2,1)}, u32[]{:S(2)}) copy-start(bf16[1,128,6,128]{1,3,2,0:T(8,128)(2,1)} %get-tuple-element.34) | copy-start | bytes 589828
  49.5 13.2 %copy-start.5 = (bf16[128,1280]{0,1:T(8,128)(2,1)S(1)}, bf16[128,1280]{0,1:T(8,128)(2,1)}, u32[]{:S(2)}) copy-start(bf16[128,1280]{0,1:T(8,128)(2,1)} %copy.193) | copy-start | bytes 983044
  51.3 15.5 %copy-start.21 = (bf16[1,128,10,128]{3,1,0,2:T(8,128)(2,1)S(1)}, bf16[1,128,10,128]{3,1,0,2:T(8,128)(2,1)}, u32[]{:S(2)}) copy-start(bf16[1,128,10,128]{3,1,0,2:T(8,128)(2,1)} %copy.119) | copy-start | bytes 983044
  51.3 17.5 %collective-permute-start.10 = (bf16[2,128,6,128]{1,3,2,0:T(8,128)(2,1)S(1)}, bf16[2,128,6,128]{1,3,2,0:T(8,128)(2,1)S(1)}, u32[]{:S(2)}, u32[]{:S(2)}) collective-permute-start(bf16[2,128,6,128]{1,3,2,0:T(8,128)(2,1)S(1)} %pad_maximum_fusion.16), channel_id=1, source_target_pairs={{4,0},{5,1},{6,2},{7,3},{8,4},{9,5},{10,6},{11,7},{12,8},{13,9},{1... | collective-permute-start | bytes 1179656 | tf_op jit(solution)/shard_map/ppermute | solution.py:17
  54.6 18.0 %collective-permute-start.11 = (bf16[2,128,6,128]{1,3,2,0:T(8,128)(2,1)S(1)}, bf16[2,128,6,128]{1,3,2,0:T(8,128)(2,1)S(1)}, u32[]{:S(2)}, u32[]{:S(2)}) collective-permute-start(bf16[2,128,6,128]{1,3,2,0:T(8,128)(2,1)S(1)} %pad_maximum_fusion.17), channel_id=1, source_target_pairs={{8,0},{9,1},{10,2},{11,3},{12,4},{13,5},{14,6},{15,7},{24,16},{25,... | collective-permute-start | bytes 1179656 | tf_op jit(solution)/shard_map/ppermute | solution.py:17
  55.9 11.8 %copy-start.1 = (bf16[1,6,128,5,128]{2,4,3,1,0:T(8,128)(2,1)S(1)}, bf16[1,6,128,5,128]{2,4,3,1,0:T(8,128)(2,1)}, u32[]{:S(2)}) copy-start(bf16[1,6,128,5,128]{2,4,3,1,0:T(8,128)(2,1)} %copy-done) | copy-start | bytes 2949124
  55.9 27.9 %collective-permute-start.9 = (bf16[2,128,6,128]{1,3,2,0:T(8,128)(2,1)S(1)}, bf16[2,128,6,128]{1,3,2,0:T(8,128)(2,1)S(1)}, u32[]{:S(2)}, u32[]{:S(2)}) collective-permute-start(bf16[2,128,6,128]{1,3,2,0:T(8,128)(2,1)S(1)} %pad_maximum_fusion.15), channel_id=1, source_target_pairs={{2,0},{3,1},{4,2},{5,3},{6,4},{7,5},{8,6},{9,7},{10,8},{11,9},{12,... | collective-permute-start | bytes 1179656 | tf_op jit(solution)/shard_map/ppermute | solution.py:17
  58.0 34.3 %collective-permute-start.8 = (bf16[2,128,6,128]{1,3,2,0:T(8,128)(2,1)S(1)}, bf16[2,128,6,128]{1,3,2,0:T(8,128)(2,1)S(1)}, u32[]{:S(2)}, u32[]{:S(2)}) collective-permute-start(bf16[2,128,6,128]{1,3,2,0:T(8,128)(2,1)S(1)} %pad_maximum_fusion.14), channel_id=1, source_target_pairs={{1,0},{2,1},{3,2},{4,3},{5,4},{6,5},{7,6},{8,7},{9,8},{10,9},{11,1... | collective-permute-start | bytes 1179656 | tf_op jit(solution)/shard_map/ppermute | solution.py:17
  63.6 28.7 %copy-start.27 = (bf16[128,6,128]{0,2,1:T(8,128)(2,1)S(1)}, bf16[128,6,128]{0,2,1:T(8,128)(2,1)}, u32[]{:S(2)}) copy-start(bf16[128,6,128]{0,2,1:T(8,128)(2,1)} %get-tuple-element.30) | copy-start | bytes 589828
  63.6 29.9 %collective-permute-start.4 = (bf16[2,128,1280]{1,2,0:T(8,128)(2,1)}, bf16[2,128,1280]{1,2,0:T(8,128)(2,1)}, u32[]{:S(2)}, u32[]{:S(2)}) collective-permute-start(bf16[2,128,1280]{1,2,0:T(8,128)(2,1)} %pad_maximum_fusion.2), channel_id=1, source_target_pairs={{0,1},{1,2},{2,3},{3,4},{4,5},{5,6},{6,7},{7,8},{8,9},{9,10},{10,1... | collective-permute-start | bytes 1966088 | tf_op jit(solution)/shard_map/ppermute | solution.py:17
  68.9 27.9 %collective-permute-start.6 = (bf16[2,128,1280]{1,2,0:T(8,128)(2,1)}, bf16[2,128,1280]{1,2,0:T(8,128)(2,1)}, u32[]{:S(2)}, u32[]{:S(2)}) collective-permute-start(bf16[2,128,1280]{1,2,0:T(8,128)(2,1)} %pad_maximum_fusion.2), channel_id=1, source_target_pairs={{0,4},{1,5},{2,6},{3,7},{4,8},{5,9},{6,10},{7,11},{8,12},{9,13},{1... | collective-permute-start | bytes 1966088 | tf_op jit(solution)/shard_map/ppermute | solution.py:17
  94.9 25.8 %collective-permute-start.5 = (bf16[2,128,1280]{1,2,0:T(8,128)(2,1)}, bf16[2,128,1280]{1,2,0:T(8,128)(2,1)}, u32[]{:S(2)}, u32[]{:S(2)}) collective-permute-start(bf16[2,128,1280]{1,2,0:T(8,128)(2,1)} %collective-permute-done.4), channel_id=1, source_target_pairs={{0,1},{1,2},{2,3},{3,4},{4,5},{5,6},{6,7},{7,8},{8,9},{9,10},{10,1... | collective-permute-start | bytes 1966088 | tf_op jit(solution)/shard_map/ppermute | solution.py:17
  96.8 21.9 %collective-permute-start.7 = (bf16[2,128,1280]{1,2,0:T(8,128)(2,1)}, bf16[2,128,1280]{1,2,0:T(8,128)(2,1)}, u32[]{:S(2)}, u32[]{:S(2)}) collective-permute-start(bf16[2,128,1280]{1,2,0:T(8,128)(2,1)} %collective-permute-done.6), channel_id=1, source_target_pairs={{0,4},{1,5},{2,6},{3,7},{4,8},{5,9},{6,10},{7,11},{8,12},{9,13},{1... | collective-permute-start | bytes 1966088 | tf_op jit(solution)/shard_map/ppermute | solution.py:17
  137.4 7.7 %copy-start.17 = (bf16[1,128,10,128]{1,3,2,0:T(8,128)(2,1)S(1)}, bf16[1,128,10,128]{1,3,2,0:T(8,128)(2,1)}, u32[]{:S(2)}) copy-start(bf16[1,128,10,128]{1,3,2,0:T(8,128)(2,1)} %get-tuple-element.14) | copy-start | bytes 983044
  137.4 7.7 %copy-start.19 = (bf16[1,128,10,128]{1,3,2,0:T(8,128)(2,1)S(1)}, bf16[1,128,10,128]{1,3,2,0:T(8,128)(2,1)}, u32[]{:S(2)}) copy-start(bf16[1,128,10,128]{1,3,2,0:T(8,128)(2,1)} %get-tuple-element.15) | copy-start | bytes 983044
  138.7 32.9 %collective-permute-start.14 = (bf16[2,128,10,128]{1,3,2,0:T(8,128)(2,1)S(1)}, bf16[2,128,10,128]{1,3,2,0:T(8,128)(2,1)S(1)}, u32[]{:S(2)}, u32[]{:S(2)}) collective-permute-start(bf16[2,128,10,128]{1,3,2,0:T(8,128)(2,1)S(1)} %pad_maximum_fusion.5), channel_id=1, source_target_pairs={{4,0},{5,1},{6,2},{7,3},{8,4},{9,5},{10,6},{11,7},{12,8},{13,9},{1... | collective-permute-start | bytes 1966088 | tf_op jit(solution)/shard_map/ppermute | solution.py:17
  140.6 6.6 %copy-start.22 = (bf16[128,1280]{1,0:T(8,128)(2,1)S(1)}, bf16[128,1280]{1,0:T(8,128)(2,1)}, u32[]{:S(2)}) copy-start(bf16[128,1280]{1,0:T(8,128)(2,1)} %copy.127) | copy-start | bytes 983044
  141.8 29.8 %collective-permute-start.15 = (bf16[2,128,10,128]{1,3,2,0:T(8,128)(2,1)S(1)}, bf16[2,128,10,128]{1,3,2,0:T(8,128)(2,1)S(1)}, u32[]{:S(2)}, u32[]{:S(2)}) collective-permute-start(bf16[2,128,10,128]{1,3,2,0:T(8,128)(2,1)S(1)} %pad_maximum_fusion.6), channel_id=1, source_target_pairs={{8,0},{9,1},{10,2},{11,3},{12,4},{13,5},{14,6},{15,7},{24,16},{25,... | collective-permute-start | bytes 1966088 | tf_op jit(solution)/shard_map/ppermute | solution.py:17
  143.2 43.0 %collective-permute-start.13 = (bf16[2,128,10,128]{1,3,2,0:T(8,128)(2,1)S(1)}, bf16[2,128,10,128]{1,3,2,0:T(8,128)(2,1)S(1)}, u32[]{:S(2)}, u32[]{:S(2)}) collective-permute-start(bf16[2,128,10,128]{1,3,2,0:T(8,128)(2,1)S(1)} %pad_maximum_fusion.4), channel_id=1, source_target_pairs={{2,0},{3,1},{4,2},{5,3},{6,4},{7,5},{8,6},{9,7},{10,8},{11,9},{12,... | collective-permute-start | bytes 1966088 | tf_op jit(solution)/shard_map/ppermute | solution.py:17
  145.2 51.3 %collective-permute-start.12 = (bf16[2,128,10,128]{1,3,2,0:T(8,128)(2,1)S(1)}, bf16[2,128,10,128]{1,3,2,0:T(8,128)(2,1)S(1)}, u32[]{:S(2)}, u32[]{:S(2)}) collective-permute-start(bf16[2,128,10,128]{1,3,2,0:T(8,128)(2,1)S(1)} %pad_maximum_fusion.3), channel_id=1, source_target_pairs={{1,0},{2,1},{3,2},{4,3},{5,4},{6,5},{7,6},{8,7},{9,8},{10,9},{11,1... | collective-permute-start | bytes 1966088 | tf_op jit(solution)/shard_map/ppermute | solution.py:17
  148.7 47.8 %copy-start.15 = (bf16[128,10,128]{0,2,1:T(8,128)(2,1)S(1)}, bf16[128,10,128]{0,2,1:T(8,128)(2,1)}, u32[]{:S(2)}) copy-start(bf16[128,10,128]{0,2,1:T(8,128)(2,1)} %get-tuple-element.10) | copy-start | bytes 983044
  148.7 47.8 %copy-start.16 = (bf16[128,10,128]{0,2,1:T(8,128)(2,1)S(1)}, bf16[128,10,128]{0,2,1:T(8,128)(2,1)}, u32[]{:S(2)}) copy-start(bf16[128,10,128]{0,2,1:T(8,128)(2,1)} %get-tuple-element.17) | copy-start | bytes 983044
  149.1 48.1 %copy-start.10 = (f32[128,6,128]{0,2,1:T(8,128)S(1)}, f32[128,6,128]{0,2,1:T(8,128)}, u32[]{:S(2)}) copy-start(f32[128,6,128]{0,2,1:T(8,128)} %get-tuple-element.21) | copy-start | bytes 1179652
  (26 other events, 57.9 us)

commit v12 on v6

--- a/solution.py
+++ b/solution.py
@@ -67,6 +67,17 @@
     inside = jnp.where(first_slot[:, None, None], causal[None], True)
     allowed = inside[None] & valid_slots[:, :, None, None]
     return jnp.transpose(allowed, (0, 2, 1, 3))[:, None]
+
+
+def gather_chunk(key_c, value_c, offsets):
+    pair = jnp.stack([key_c, value_c])
+    gathered = lax.all_gather(pair, "ctx")
+    shard_index = lax.axis_index("ctx")
+    picked = [
+        lax.dynamic_index_in_dim(gathered, jnp.maximum(shard_index - offset, 0), 0, keepdims=False)
+        for offset in offsets
+    ]
+    return [pair] + picked
 
 
 def send_chunk(key_c, value_c, offsets):
@@ -158,7 +169,8 @@
         key_c, value_c = key_rot[:, cols], values[:, cols]
         if pending:
             key_c, value_c, _ = lax.optimization_barrier((key_c, value_c, pieces[-1][0]))
-        received = send_chunk(key_c, value_c, offsets)
+        fetch = gather_chunk if chunk == 0 else send_chunk
+        received = fetch(key_c, value_c, offsets)
         output, query_grad, own, outgoing = attend_chunk(
             query_rot[:, cols], received, grad_out[:, cols], allowed, offsets, chunk_heads
         )

time: 186 us -> 256 us (1.38)
  the two profiles are of different devices: /device:TPU:15 before, /device:TPU:0 now
where the time goes in v12:
time: 256 us; the launch traced here: 254 us
  waiting for transfers between devices  122 us (48%)
  local copies, waits for them, and re-layouts  54.5 us (21%)
  starting transfers between devices  26.1 us (10%)
  other arithmetic  22.3 us (9%)
  between operations  15.5 us (6%)
  matrix products  13.5 us (5%)
    all_gather x1, waiting for transfers between devices, gather_chunk(): gathered = lax.all_gather(pair, 'ctx')  73.8 us
    ppermute x12, waiting for transfers between devices, from_behind(): lax.ppermute(value, axis, [(source, source + steps) for source in range(l...  48.5 us
    ppermute x12, starting transfers between devices, from_behind(): lax.ppermute(value, axis, [(source, source + steps) for source in range(l...  26.1 us
    unnamed x89, local copies, waits for them, and re-layouts  13.3 us
    all_gather x1, local copies, waits for them, and re-layouts, gather_chunk(): gathered = lax.all_gather(pair, 'ctx')  11.9 us
    slice x5, local copies, waits for them, and re-layouts, attend_chunk(): moved[0].reshape(head_shape)  10.1 us
    another operation x8, other arithmetic, attend_chunk(): jnp.stack([key_terms[0, slot_index], value_terms[0, slot_index]])  7.78 us
    another operation x12, local copies, waits for them, and re-layouts, attend_chunk(): jnp.stack([moved[0].reshape(head_shape) for moved in received])[None]  6.73 us
  transfers between devices with their start and end apart: 13, of which 5 were waited for; matrix products, arithmetic and copies ran while one was open for 21% of the time, Pallas kernels for 0%

profile of v12, /device:TPU:0, one launch (start us, length us, event | category | flops | bytes accessed | tf_op | source)
XLA Modules:
  0.0 254.3 jit_solution(5686344570067566514)
XLA Ops:
  17.3 73.8 %all-gather.3.cloned.1.call-done = bf16[32,128,1024]{2,1,0:T(8,128)(2,1)} async-done(((bf16[2,128,1024]{2,1,0:T(8,128)(2,1)}), bf16[32,128,1024]{2,1,0:T(8,128)(2,1)}) %all-gather.3.cloned.1.call-update) | async-done | bytes 8388624 | tf_op jit(solution)/shard_map/all_gather | solution.py:74
  91.1 11.9 %copy.142 = bf16[32,128,1024]{1,2,0:T(8,128)(2,1)} copy(bf16[32,128,1024]{2,1,0:T(8,128)(2,1)} %all-gather.3.cloned.1.call-done) | data formatting | bytes 16777216 | tf_op jit(solution)/shard_map/all_gather | solution.py:74
  103.0 2.9 %constant_dynamic-slice_fusion.4 = (bf16[1,1,128,1024]{2,3,1,0:T(8,128)(2,1)S(1)}, bf16[1,1,128,1024]{2,3,1,0:T(8,128)(2,1)}, bf16[1,1,128,1024]{2,3,1,0:T(8,128...) fusion(bf16[16,2,128,1024]{2,3,1,0:T(8,128)(2,1)} %bitcast.337,, ...), kind=kLoop, calls=%fused_computation.161 | loop fusion | bytes 4194324 | tf_op jit(solution)/shard_map/slice | solution.py:99
  107.9 1.8 fusion.42
  114.7 3.0 %collective-permute-start = (bf16[2,128,1024]{1,2,0:T(8,128)(2,1)}, bf16[2,128,1024]{1,2,0:T(8,128)(2,1)}, u32[]{:S(2)}, u32[]{:S(2)}) collective-permute-start(bf16[2,128,1024]{1,2,0:T(8,128)(2,1)} %pad_maximum_fusion.5), channel_id=1, source_target_pairs={{0,1},{1,2},{2,3},{3,4},{4,5},{5,6},{6,7},{7,8},{8,9},{9,10},{10,1... | collective-permute-start | bytes 1572872 | tf_op jit(solution)/shard_map/ppermute | solution.py:17
  117.7 2.4 collective-permute-start.2
  120.1 1.8 copy.159
  123.0 2.6 %fusion.12 = bf16[1,8,128,5,128]{2,4,3,1,0:T(8,128)(2,1)S(1)} fusion(bf16[5,128,8,128]{1,3,0,2:T(8,128)(2,1)} %copy-done.13, bf16[128,8,128,1]{0,2,3,1:T(8,128)(2,1)} %bitcast.354, f32[8,128,5,128]{1,3,2,0:T(8,128)S(1)} %bitcast.332, f32[8,128]{1,0:T(8,128)S(1)} %bitcast.383, f32[8,128]{1,0:T(8,128)} %copy-done.32, pred[128,5,128]{0,2,1:T(8,128)(4,1)S(1)} %and_bitcast_fusion), kind=kOutput, calls=%fused_computation.24 | convolution fusion | flops 172359680 | bytes 5595136 | tf_op jit(solution)/shard_map/bthd,bnuhd->bhtnu/dot_general | solution.py:116
  130.6 1.3 collective-permute-start.4
  132.7 1.3 collective-permute-start.5
  134.9 1.3 collective-permute-start.6
  138.1 1.9 pad_maximum_fusion.11
  140.7 1.4 convolution_bitcast_fusion.1
  142.1 3.9 %collective-permute-start.1 = (bf16[2,128,1024]{1,2,0:T(8,128)(2,1)}, bf16[2,128,1024]{1,2,0:T(8,128)(2,1)}, u32[]{:S(2)}, u32[]{:S(2)}) collective-permute-start(bf16[2,128,1024]{1,2,0:T(8,128)(2,1)} %collective-permute-done), channel_id=1, source_target_pairs={{0,1},{1,2},{2,3},{3,4},{4,5},{5,6},{6,7},{7,8},{8,9},{9,10},{10,1... | collective-permute-start | bytes 1572872 | tf_op jit(solution)/shard_map/ppermute | solution.py:17
  146.0 1.8 fusion.39
  147.7 6.2 %collective-permute-start.3 = (bf16[2,128,1024]{1,2,0:T(8,128)(2,1)}, bf16[2,128,1024]{1,2,0:T(8,128)(2,1)}, u32[]{:S(2)}, u32[]{:S(2)}) collective-permute-start(bf16[2,128,1024]{1,2,0:T(8,128)(2,1)} %collective-permute-done.2), channel_id=1, source_target_pairs={{0,4},{1,5},{2,6},{3,7},{4,8},{5,9},{6,10},{7,11},{8,12},{9,13},{1... | collective-permute-start | bytes 1572872 | tf_op jit(solution)/shard_map/ppermute | solution.py:17
  154.0 1.9 fusion.37
  158.2 1.5 collective-permute-start.7
  159.7 1.8 fusion.38
  162.3 2.5 collective-permute-done.3
  164.8 1.9 fusion.36
  166.6 1.8 copy.156
  174.2 2.5 fusion.13
  184.2 1.4 collective-permute-start.9
  185.6 1.3 collective-permute-start.10
  186.9 1.3 collective-permute-start.11
  188.3 2.8 %fusion.27 = (bf16[128,8,128]{0,2,1:T(8,128)(2,1)}, f32[128,8,128]{0,2,1:T(8,128)}) fusion(bf16[128,8,128]{0,2,1:T(8,128)(2,1)S(1)} %copy-done.26, bf16[2,128,8,128]{1,3,2,0:T(8,128)(2,1)} %collective-permute-done.7, bf16[2,128,8,128]{1,3,2,0:T(8,128)(2,1)} %collective-permute-done.6, bf16[2,128,8,128]{1,3,2,0:T(8,128)(2,1)} %collective-permute-done.5, ...), kind=kLoop, calls=%fused_computation.70 | loop fusion | flops 2490368 | bytes 3407872 | tf_op jit(solution)/shard_map/convert.23
  193.0 1.8 pad_maximum_fusion.6
  195.4 8.6 %collective-permute-done.9 = bf16[2,128,8,128]{1,3,2,0:T(8,128)(2,1)} collective-permute-done((bf16[2,128,8,128]{1,3,2,0:T(8,128)(2,1)}, bf16[2,128,8,128]{1,3,2,0:T(8,128)(2,1)}, u32[]{:S(2)}, u32[]{:S(2)}) %collective-permute-start.9) | collective-permute-done | bytes 524320 | tf_op jit(solution)/shard_map/ppermute | solution.py:17
  204.0 13.0 %collective-permute-done.10 = bf16[2,128,8,128]{1,3,2,0:T(8,128)(2,1)} collective-permute-done((bf16[2,128,8,128]{1,3,2,0:T(8,128)(2,1)}, bf16[2,128,8,128]{1,3,2,0:T(8,128)(2,1)}, u32[]{:S(2)}, u32[]{:S(2)}) %collective-permute-start.10) | collective-permute-done | bytes 524320 | tf_op jit(solution)/shard_map/ppermute | solution.py:17
  217.0 24.4 %collective-permute-done.11 = bf16[2,128,8,128]{1,3,2,0:T(8,128)(2,1)} collective-permute-done((bf16[2,128,8,128]{1,3,2,0:T(8,128)(2,1)}, bf16[2,128,8,128]{1,3,2,0:T(8,128)(2,1)}, u32[]{:S(2)}, u32[]{:S(2)}) %collective-permute-start.11) | collective-permute-done | bytes 524320 | tf_op jit(solution)/shard_map/ppermute | solution.py:17
  241.4 1.9 fusion.26
  (175 shorter events, 49.4 us)
Async XLA Ops:
  7.2 3.1 %copy-start.29 = (bf16[128,2048]{1,0:T(8,128)(2,1)S(1)}, bf16[128,2048]{1,0:T(8,128)(2,1)}, u32[]{:S(2)}) copy-start(bf16[128,2048]{1,0:T(8,128)(2,1)} %param.7) | copy-start | bytes 1572868
  7.2 84.0 %all-gather.3.cloned.1.call-start = ((), (), s32[]{:S(2)}) async-start(), calls=%async_computation | async-start | bytes 8912896 | tf_op jit(solution)/shard_map/all_gather | solution.py:74
  12.3 1.9 copy-start.31
  110.6 1.4 copy-start.18
  110.7 1.5 copy-start.17
  111.3 2.6 %copy-start = (bf16[1,8,128,5,128]{2,4,3,1,0:T(8,128)(2,1)}, bf16[1,8,128,5,128]{2,4,3,1,0:T(8,128)(2,1)S(1)}, u32[]{:S(2)}) copy-start(bf16[1,8,128,5,128]{2,4,3,1,0:T(8,128)(2,1)S(1)} %fusion.15) | copy-start | bytes 3932164
  114.7 27.4 %collective-permute-start = (bf16[2,128,1024]{1,2,0:T(8,128)(2,1)}, bf16[2,128,1024]{1,2,0:T(8,128)(2,1)}, u32[]{:S(2)}, u32[]{:S(2)}) collective-permute-start(bf16[2,128,1024]{1,2,0:T(8,128)(2,1)} %pad_maximum_fusion.5), channel_id=1, source_target_pairs={{0,1},{1,2},{2,3},{3,4},{4,5},{5,6},{6,7},{7,8},{8,9},{9,10},{10,1... | collective-permute-start | bytes 1572872 | tf_op jit(solution)/shard_map/ppermute | solution.py:17
  117.7 30.0 %collective-permute-start.2 = (bf16[2,128,1024]{1,2,0:T(8,128)(2,1)}, bf16[2,128,1024]{1,2,0:T(8,128)(2,1)}, u32[]{:S(2)}, u32[]{:S(2)}) collective-permute-start(bf16[2,128,1024]{1,2,0:T(8,128)(2,1)} %pad_maximum_fusion.5), channel_id=1, source_target_pairs={{0,4},{1,5},{2,6},{3,7},{4,8},{5,9},{6,10},{7,11},{8,12},{9,13},{1... | collective-permute-start | bytes 1572872 | tf_op jit(solution)/shard_map/ppermute | solution.py:17
  123.0 2.6 %copy-start.9 = (bf16[128,1024]{0,1:T(8,128)(2,1)S(1)}, bf16[128,1024]{0,1:T(8,128)(2,1)}, u32[]{:S(2)}) copy-start(bf16[128,1024]{0,1:T(8,128)(2,1)} %get-tuple-element.67) | copy-start | bytes 786436
  126.7 1.5 copy-start.1
  126.7 1.5 copy-start.7
  130.6 53.6 %collective-permute-start.4 = (bf16[2,128,8,128]{1,3,2,0:T(8,128)(2,1)}, bf16[2,128,8,128]{1,3,2,0:T(8,128)(2,1)}, u32[]{:S(2)}, u32[]{:S(2)}) collective-permute-start(bf16[2,128,8,128]{1,3,2,0:T(8,128)(2,1)} %pad_maximum_fusion.8), channel_id=1, source_target_pairs={{1,0},{2,1},{3,2},{4,3},{5,4},{6,5},{7,6},{8,7},{9,8},{10,9},{11,1... | collective-permute-start | bytes 1572872 | tf_op jit(solution)/shard_map/ppermute | solution.py:17
  132.7 52.9 %collective-permute-start.5 = (bf16[2,128,8,128]{1,3,2,0:T(8,128)(2,1)}, bf16[2,128,8,128]{1,3,2,0:T(8,128)(2,1)}, u32[]{:S(2)}, u32[]{:S(2)}) collective-permute-start(bf16[2,128,8,128]{1,3,2,0:T(8,128)(2,1)} %pad_maximum_fusion.9), channel_id=1, source_target_pairs={{2,0},{3,1},{4,2},{5,3},{6,4},{7,5},{8,6},{9,7},{10,8},{11,9},{12,... | collective-permute-start | bytes 1572872 | tf_op jit(solution)/shard_map/ppermute | solution.py:17
  134.9 52.1 %collective-permute-start.6 = (bf16[2,128,8,128]{1,3,2,0:T(8,128)(2,1)}, bf16[2,128,8,128]{1,3,2,0:T(8,128)(2,1)}, u32[]{:S(2)}, u32[]{:S(2)}) collective-permute-start(bf16[2,128,8,128]{1,3,2,0:T(8,128)(2,1)} %pad_maximum_fusion.10), channel_id=1, source_target_pairs={{4,0},{5,1},{6,2},{7,3},{8,4},{9,5},{10,6},{11,7},{12,8},{13,9},{1... | collective-permute-start | bytes 1572872 | tf_op jit(solution)/shard_map/ppermute | solution.py:17
  136.2 4.6 %copy-start.3 = (bf16[5,128,8,128]{3,1,0,2:T(8,128)(2,1)S(1)}, bf16[5,128,8,128]{3,1,0,2:T(8,128)(2,1)}, u32[]{:S(2)}) copy-start(bf16[5,128,8,128]{3,1,0,2:T(8,128)(2,1)} %copy-done.2) | copy-start | bytes 3932164
  137.0 3.7 %copy-start.5 = (bf16[1,8,128,5,128]{2,4,3,1,0:T(8,128)(2,1)S(1)}, bf16[1,8,128,5,128]{2,4,3,1,0:T(8,128)(2,1)}, u32[]{:S(2)}) copy-start(bf16[1,8,128,5,128]{2,4,3,1,0:T(8,128)(2,1)} %copy-done.4) | copy-start | bytes 3932164
  142.1 16.1 %collective-permute-start.1 = (bf16[2,128,1024]{1,2,0:T(8,128)(2,1)}, bf16[2,128,1024]{1,2,0:T(8,128)(2,1)}, u32[]{:S(2)}, u32[]{:S(2)}) collective-permute-start(bf16[2,128,1024]{1,2,0:T(8,128)(2,1)} %collective-permute-done), channel_id=1, source_target_pairs={{0,1},{1,2},{2,3},{3,4},{4,5},{5,6},{6,7},{7,8},{8,9},{9,10},{10,1... | collective-permute-start | bytes 1572872 | tf_op jit(solution)/shard_map/ppermute | solution.py:17
  147.7 9.4 %copy-start.14 = (bf16[5,128,8,128]{1,3,0,2:T(8,128)(2,1)S(1)}, bf16[5,128,8,128]{1,3,0,2:T(8,128)(2,1)}, u32[]{:S(2)}) copy-start(bf16[5,128,8,128]{1,3,0,2:T(8,128)(2,1)} %constant_dynamic-update-slice_fusion.14) | copy-start | bytes 3932164
  147.7 17.0 %collective-permute-start.3 = (bf16[2,128,1024]{1,2,0:T(8,128)(2,1)}, bf16[2,128,1024]{1,2,0:T(8,128)(2,1)}, u32[]{:S(2)}, u32[]{:S(2)}) collective-permute-start(bf16[2,128,1024]{1,2,0:T(8,128)(2,1)} %collective-permute-done.2), channel_id=1, source_target_pairs={{0,4},{1,5},{2,6},{3,7},{4,8},{5,9},{6,10},{7,11},{8,12},{9,13},{1... | collective-permute-start | bytes 1572872 | tf_op jit(solution)/shard_map/ppermute | solution.py:17
  158.2 30.1 %collective-permute-start.7 = (bf16[2,128,8,128]{1,3,2,0:T(8,128)(2,1)}, bf16[2,128,8,128]{1,3,2,0:T(8,128)(2,1)}, u32[]{:S(2)}, u32[]{:S(2)}) collective-permute-start(bf16[2,128,8,128]{1,3,2,0:T(8,128)(2,1)} %pad_maximum_fusion.11), channel_id=1, source_target_pairs={{8,0},{9,1},{10,2},{11,3},{12,4},{13,5},{14,6},{15,7},{24,16},{25,... | collective-permute-start | bytes 1572872 | tf_op jit(solution)/shard_map/ppermute | solution.py:17
  166.6 3.9 %copy-start.6 = (bf16[128,1024]{0,1:T(8,128)(2,1)S(1)}, bf16[128,1024]{0,1:T(8,128)(2,1)}, u32[]{:S(2)}) copy-start(bf16[128,1024]{0,1:T(8,128)(2,1)} %get-tuple-element.66) | copy-start | bytes 786436
  180.4 15.0 %collective-permute-start.8 = (bf16[2,128,8,128]{1,3,2,0:T(8,128)(2,1)}, bf16[2,128,8,128]{1,3,2,0:T(8,128)(2,1)}, u32[]{:S(2)}, u32[]{:S(2)}) collective-permute-start(bf16[2,128,8,128]{1,3,2,0:T(8,128)(2,1)} %pad_maximum_fusion.12), channel_id=1, source_target_pairs={{1,0},{2,1},{3,2},{4,3},{5,4},{6,5},{7,6},{8,7},{9,8},{10,9},{11,1... | collective-permute-start | bytes 1572872 | tf_op jit(solution)/shard_map/ppermute | solution.py:17
  182.5 5.7 %copy-start.25 = (bf16[128,8,128]{0,2,1:T(8,128)(2,1)S(1)}, bf16[128,8,128]{0,2,1:T(8,128)(2,1)}, u32[]{:S(2)}) copy-start(bf16[128,8,128]{0,2,1:T(8,128)(2,1)} %get-tuple-element.50) | copy-start | bytes 786436
  182.5 5.8 %copy-start.26 = (bf16[128,8,128]{0,2,1:T(8,128)(2,1)S(1)}, bf16[128,8,128]{0,2,1:T(8,128)(2,1)}, u32[]{:S(2)}) copy-start(bf16[128,8,128]{0,2,1:T(8,128)(2,1)} %get-tuple-element.36) | copy-start | bytes 786436
  184.2 8.8 %copy-start.20 = (bf16[128,1024]{1,0:T(8,128)(2,1)S(1)}, bf16[128,1024]{1,0:T(8,128)(2,1)}, u32[]{:S(2)}) copy-start(bf16[128,1024]{1,0:T(8,128)(2,1)} %copy.159) | copy-start | bytes 786436
  184.2 19.8 %collective-permute-start.9 = (bf16[2,128,8,128]{1,3,2,0:T(8,128)(2,1)}, bf16[2,128,8,128]{1,3,2,0:T(8,128)(2,1)}, u32[]{:S(2)}, u32[]{:S(2)}) collective-permute-start(bf16[2,128,8,128]{1,3,2,0:T(8,128)(2,1)} %pad_maximum_fusion.13), channel_id=1, source_target_pairs={{2,0},{3,1},{4,2},{5,3},{6,4},{7,5},{8,6},{9,7},{10,8},{11,9},{12,... | collective-permute-start | bytes 1572872 | tf_op jit(solution)/shard_map/ppermute | solution.py:17
  185.6 31.4 %collective-permute-start.10 = (bf16[2,128,8,128]{1,3,2,0:T(8,128)(2,1)}, bf16[2,128,8,128]{1,3,2,0:T(8,128)(2,1)}, u32[]{:S(2)}, u32[]{:S(2)}) collective-permute-start(bf16[2,128,8,128]{1,3,2,0:T(8,128)(2,1)} %pad_maximum_fusion.14), channel_id=1, source_target_pairs={{4,0},{5,1},{6,2},{7,3},{8,4},{9,5},{10,6},{11,7},{12,8},{13,9},{1... | collective-permute-start | bytes 1572872 | tf_op jit(solution)/shard_map/ppermute | solution.py:17
  186.9 54.5 %collective-permute-start.11 = (bf16[2,128,8,128]{1,3,2,0:T(8,128)(2,1)}, bf16[2,128,8,128]{1,3,2,0:T(8,128)(2,1)}, u32[]{:S(2)}, u32[]{:S(2)}) collective-permute-start(bf16[2,128,8,128]{1,3,2,0:T(8,128)(2,1)} %pad_maximum_fusion.15), channel_id=1, source_target_pairs={{8,0},{9,1},{10,2},{11,3},{12,4},{13,5},{14,6},{15,7},{24,16},{25,... | collective-permute-start | bytes 1572872 | tf_op jit(solution)/shard_map/ppermute | solution.py:17
  194.8 46.6 %copy-start.27 = (bf16[128,8,128]{0,2,1:T(8,128)(2,1)S(1)}, bf16[128,8,128]{0,2,1:T(8,128)(2,1)}, u32[]{:S(2)}) copy-start(bf16[128,8,128]{0,2,1:T(8,128)(2,1)} %get-tuple-element.55) | copy-start | bytes 786436
  194.8 46.6 %copy-start.28 = (bf16[128,8,128]{0,2,1:T(8,128)(2,1)S(1)}, bf16[128,8,128]{0,2,1:T(8,128)(2,1)}, u32[]{:S(2)}) copy-start(bf16[128,8,128]{0,2,1:T(8,128)(2,1)} %get-tuple-element.41) | copy-start | bytes 786436
  195.4 48.8 %copy-start.10 = (f32[128,8,128]{0,2,1:T(8,128)S(1)}, f32[128,8,128]{0,2,1:T(8,128)}, u32[]{:S(2)}) copy-start(f32[128,8,128]{0,2,1:T(8,128)} %convolution_bitcast_fusion.1) | copy-start | bytes 1572868
  195.4 48.8 %copy-start.11 = (f32[128,8,128]{0,2,1:T(8,128)S(1)}, f32[128,8,128]{0,2,1:T(8,128)}, u32[]{:S(2)}) copy-start(f32[128,8,128]{0,2,1:T(8,128)} %get-tuple-element.33) | copy-start | bytes 1572868
  (15 other events, 16.8 us)
Sparse Core Ops, SparseCore 0:
  13.5 77.5 all-gather.2

commit v13 on v11

--- a/solution.py
+++ b/solution.py
@@ -8,7 +8,7 @@
 HEADS = 16
 HEAD_DIM = 128
 BLOCK = 128
-CHUNK_HEADS = (6, 10)
+CHUNK_HEADS = (10, 6)
 
 
 def from_behind(value, axis, steps):

time: 202 us -> 213 us (1.054)
  local copies, waits for them, and re-layouts: 39.3 us -> 49.8 us
  waiting for transfers between devices: 89.3 us -> 83.4 us
  other arithmetic: 16 us -> 19.1 us
    ppermute x16, waiting for transfers between devices: 89.3 us -> 83.4 us  [from_behind(): lax.ppermute(value, axis, [(source, source + steps) for source in range(l...]
    slice x8, local copies, waits for them, and re-layouts: 9.67 us -> 12.6 us  [attend_chunk(): moved[0].reshape(head_shape)]
    unnamed x97 -> x101, local copies, waits for them, and re-layouts: 8.74 us -> 11.4 us
    slice x4 -> x2, local copies, waits for them, and re-layouts: 0.01 us -> 2.61 us  [on_device(): grad_out[:, cols]]
  transfers between devices with their start and end apart: 16 -> 16, of which waited for: 9 -> 8; matrix products, arithmetic and copies ran while one was open for 11% -> 21% of each run, Pallas kernels for 0% -> 0%
where the time goes in v13:
time: 213 us; the launch traced here: 211 us
  waiting for transfers between devices  83.4 us (39%)
  local copies, waits for them, and re-layouts  49.8 us (23%)
  starting transfers between devices  45.3 us (21%)
  other arithmetic  19.1 us (9%)
  matrix products  11.6 us (5%)
  between operations  2.29 us (1%)
    ppermute x16, waiting for transfers between devices, from_behind(): lax.ppermute(value, axis, [(source, source + steps) for source in range(l...  83.4 us
    ppermute x16, starting transfers between devices, from_behind(): lax.ppermute(value, axis, [(source, source + steps) for source in range(l...  45.3 us
    slice x8, local copies, waits for them, and re-layouts, attend_chunk(): moved[0].reshape(head_shape)  12.6 us
    unnamed x101, local copies, waits for them, and re-layouts  11.4 us
    another operation x8, other arithmetic, attend_chunk(): jnp.stack([key_terms[0, slot_index], value_terms[0, slot_index]])  6.66 us
    another operation x12, local copies, waits for them, and re-layouts, attend_chunk(): jnp.stack([moved[0].reshape(head_shape) for moved in received])[None]  5.16 us
  transfers between devices with their start and end apart: 16, of which 8 were waited for; matrix products, arithmetic and copies ran while one was open for 21% of the time, Pallas kernels for 0%

profile of v13, /device:TPU:15, one launch (start us, length us, event | category | flops | bytes accessed | tf_op | source)
XLA Modules:
  0.0 211.5 jit_solution(11758391367286885609)
XLA Ops:
  6.9 3.2 %collective-permute-start.2 = (bf16[2,128,1280]{1,2,0:T(8,128)(2,1)}, bf16[2,128,1280]{1,2,0:T(8,128)(2,1)}, u32[]{:S(2)}, u32[]{:S(2)}) collective-permute-start(bf16[2,128,1280]{1,2,0:T(8,128)(2,1)} %pad_maximum_fusion.2), channel_id=1, source_target_pairs={{0,4},{1,5},{2,6},{3,7},{4,8},{5,9},{6,10},{7,11},{8,12},{9,13},{1... | collective-permute-start | bytes 1966088 | tf_op jit(solution)/shard_map/ppermute | solution.py:17
  10.1 4.0 %collective-permute-start = (bf16[2,128,1280]{1,2,0:T(8,128)(2,1)}, bf16[2,128,1280]{1,2,0:T(8,128)(2,1)}, u32[]{:S(2)}, u32[]{:S(2)}) collective-permute-start(bf16[2,128,1280]{1,2,0:T(8,128)(2,1)} %pad_maximum_fusion.2), channel_id=1, source_target_pairs={{0,1},{1,2},{2,3},{3,4},{4,5},{5,6},{6,7},{7,8},{8,9},{9,10},{10,1... | collective-permute-start | bytes 1966088 | tf_op jit(solution)/shard_map/ppermute | solution.py:17
  21.6 1.7 copy.193
  26.2 5.8 %collective-permute-done = bf16[2,128,1280]{1,2,0:T(8,128)(2,1)} collective-permute-done((bf16[2,128,1280]{1,2,0:T(8,128)(2,1)}, bf16[2,128,1280]{1,2,0:T(8,128)(2,1)}, u32[]{:S(2)}, u32[]{:S(2)}) %collective-permute-start) | collective-permute-done | bytes 655392 | tf_op jit(solution)/shard_map/ppermute | solution.py:17
  33.3 5.3 %collective-permute-start.1 = (bf16[2,128,1280]{1,2,0:T(8,128)(2,1)}, bf16[2,128,1280]{1,2,0:T(8,128)(2,1)S(1)}, u32[]{:S(2)}, u32[]{:S(2)}) collective-permute-start(bf16[2,128,1280]{1,2,0:T(8,128)(2,1)} %collective-permute-done), channel_id=1, source_target_pairs={{0,1},{1,2},{2,3},{3,4},{4,5},{5,6},{6,7},{7,8},{8,9},{9,10},{10,1... | collective-permute-start | bytes 1966088 | tf_op jit(solution)/shard_map/ppermute | solution.py:17
  38.6 3.2 %collective-permute-start.3 = (bf16[2,128,1280]{1,2,0:T(8,128)(2,1)}, bf16[2,128,1280]{1,2,0:T(8,128)(2,1)}, u32[]{:S(2)}, u32[]{:S(2)}) collective-permute-start(bf16[2,128,1280]{1,2,0:T(8,128)(2,1)} %collective-permute-done.2), channel_id=1, source_target_pairs={{0,4},{1,5},{2,6},{3,7},{4,8},{5,9},{6,10},{7,11},{8,12},{9,13},{1... | collective-permute-start | bytes 1966088 | tf_op jit(solution)/shard_map/ppermute | solution.py:17
  41.8 1.8 fusion.39
  44.7 16.3 %collective-permute-done.3 = bf16[2,128,1280]{1,2,0:T(8,128)(2,1)} collective-permute-done((bf16[2,128,1280]{1,2,0:T(8,128)(2,1)}, bf16[2,128,1280]{1,2,0:T(8,128)(2,1)}, u32[]{:S(2)}, u32[]{:S(2)}) %collective-permute-start.3) | collective-permute-done | bytes 655392 | tf_op jit(solution)/shard_map/ppermute | solution.py:17
  61.1 1.8 fusion.38
  65.5 2.0 fusion.47
  72.8 1.9 copy.126
  74.7 1.8 pad_maximum_fusion.13
  76.5 3.2 %collective-permute-start.6 = (bf16[2,128,768]{1,2,0:T(8,128)(2,1)}, bf16[2,128,768]{1,2,0:T(8,128)(2,1)}, u32[]{:S(2)}, u32[]{:S(2)}) collective-permute-start(bf16[2,128,768]{1,2,0:T(8,128)(2,1)} %pad_maximum_fusion.13), channel_id=1, source_target_pairs={{0,4},{1,5},{2,6},{3,7},{4,8},{5,9},{6,10},{7,11},{8,12},{9,13},{1... | collective-permute-start | bytes 1179656 | tf_op jit(solution)/shard_map/ppermute | solution.py:17
  79.7 1.9 collective-permute-start.4
  81.6 2.2 %fusion.16 = bf16[1,5,128,10,128]{2,4,3,1,0:T(8,128)(2,1)S(1)} fusion(bf16[128,10,128,1]{0,2,1,3:T(8,128)(2,1)} %bitcast.366, bf16[1,10,128,5,128]{2,4,3,1,0:T(8,128)(2,1)} %copy-done), kind=kOutput, calls=%fused_computation.24 | convolution fusion | flops 210534400 | bytes 3604480 | tf_op jit(solution)/shard_map/bhtnu,bthd->bnuhd/dot_general | solution.py:117
  92.0 2.9 %collective-permute-start.10 = (bf16[2,128,10,128]{1,3,2,0:T(8,128)(2,1)}, bf16[2,128,10,128]{1,3,2,0:T(8,128)(2,1)}, u32[]{:S(2)}, u32[]{:S(2)}) collective-permute-start(bf16[2,128,10,128]{1,3,2,0:T(8,128)(2,1)} %pad_maximum_fusion.5), channel_id=1, source_target_pairs={{4,0},{5,1},{6,2},{7,3},{8,4},{9,5},{10,6},{11,7},{12,8},{13,9},{1... | collective-permute-start | bytes 1966088 | tf_op jit(solution)/shard_map/ppermute | solution.py:17
  99.2 1.9 collective-permute-start.9
  102.0 2.7 %collective-permute-start.8 = (bf16[2,128,10,128]{1,3,2,0:T(8,128)(2,1)}, bf16[2,128,10,128]{1,3,2,0:T(8,128)(2,1)}, u32[]{:S(2)}, u32[]{:S(2)}) collective-permute-start(bf16[2,128,10,128]{1,3,2,0:T(8,128)(2,1)} %pad_maximum_fusion.3), channel_id=1, source_target_pairs={{1,0},{2,1},{3,2},{4,3},{5,4},{6,5},{7,6},{8,7},{9,8},{10,9},{11,1... | collective-permute-start | bytes 1966088 | tf_op jit(solution)/shard_map/ppermute | solution.py:17
  107.3 1.8 fusion.46
  110.1 3.7 %collective-permute-start.7 = (bf16[2,128,768]{1,2,0:T(8,128)(2,1)}, bf16[2,128,768]{1,2,0:T(8,128)(2,1)}, u32[]{:S(2)}, u32[]{:S(2)}) collective-permute-start(bf16[2,128,768]{1,2,0:T(8,128)(2,1)} %collective-permute-done.6), channel_id=1, source_target_pairs={{0,4},{1,5},{2,6},{3,7},{4,8},{5,9},{6,10},{7,11},{8,12},{9,13},{1... | collective-permute-start | bytes 1179656 | tf_op jit(solution)/shard_map/ppermute | solution.py:17
  114.9 4.7 %collective-permute-start.5 = (bf16[2,128,768]{1,2,0:T(8,128)(2,1)}, bf16[2,128,768]{1,2,0:T(8,128)(2,1)}, u32[]{:S(2)}, u32[]{:S(2)}) collective-permute-start(bf16[2,128,768]{1,2,0:T(8,128)(2,1)} %collective-permute-done.4), channel_id=1, source_target_pairs={{0,1},{1,2},{2,3},{3,4},{4,5},{5,6},{6,7},{7,8},{8,9},{9,10},{10,1... | collective-permute-start | bytes 1179656 | tf_op jit(solution)/shard_map/ppermute | solution.py:17
  119.6 4.8 %collective-permute-done.11 = bf16[2,128,10,128]{1,3,2,0:T(8,128)(2,1)} collective-permute-done((bf16[2,128,10,128]{1,3,2,0:T(8,128)(2,1)}, bf16[2,128,10,128]{1,3,2,0:T(8,128)(2,1)}, u32[]{:S(2)}, u32[]{:S(2)}) %collective-permute-start.11) | collective-permute-done | bytes 655392 | tf_op jit(solution)/shard_map/ppermute | solution.py:17
  124.5 24.4 %collective-permute-done.9 = bf16[2,128,10,128]{1,3,2,0:T(8,128)(2,1)} collective-permute-done((bf16[2,128,10,128]{1,3,2,0:T(8,128)(2,1)}, bf16[2,128,10,128]{1,3,2,0:T(8,128)(2,1)}, u32[]{:S(2)}, u32[]{:S(2)}) %collective-permute-start.9) | collective-permute-done | bytes 655392 | tf_op jit(solution)/shard_map/ppermute | solution.py:17
  148.9 3.5 %collective-permute-done.8 = bf16[2,128,10,128]{1,3,2,0:T(8,128)(2,1)} collective-permute-done((bf16[2,128,10,128]{1,3,2,0:T(8,128)(2,1)}, bf16[2,128,10,128]{1,3,2,0:T(8,128)(2,1)}, u32[]{:S(2)}, u32[]{:S(2)}) %collective-permute-start.8) | collective-permute-done | bytes 655392 | tf_op jit(solution)/shard_map/ppermute | solution.py:17
  152.4 2.3 %fusion.32 = (bf16[128,10,128]{0,2,1:T(8,128)(2,1)S(1)}, f32[128,10,128]{0,2,1:T(8,128)S(1)}) fusion(bf16[128,10,128]{0,2,1:T(8,128)(2,1)S(1)} %copy-done.14, bf16[2,128,10,128]{1,3,2,0:T(8,128)(2,1)} %collective-permute-done.11, bf16[2,128,10,128]{1,3,2,0:T(8,128)(2,1)} %collective-permute-done.10, bf16[2,128,10,128]{1,3,2,0:T(8,128)(2,1)} %collective-permute-done.9, ...), kind=kLoop, calls=%fused_computation.50 | loop fusion | flops 3112960 | bytes 4259840 | tf_op jit(solution)/shard_map/convert.23
  157.6 1.8 fusion.45
  169.1 1.9 collective-permute-start.14
  174.3 1.9 collective-permute-start.13
  176.3 1.9 collective-permute-start.12
  179.2 11.2 %collective-permute-done.14 = bf16[2,128,6,128]{1,3,2,0:T(8,128)(2,1)S(1)} collective-permute-done((bf16[2,128,6,128]{1,3,2,0:T(8,128)(2,1)S(1)}, bf16[2,128,6,128]{1,3,2,0:T(8,128)(2,1)S(1)}, u32[]{:S(2)}, u32[]{:S(2)}) %collective-permute-start.14) | collective-permute-done | bytes 393248 | tf_op jit(solution)/shard_map/ppermute | solution.py:17
  190.4 11.0 %collective-permute-done.13 = bf16[2,128,6,128]{1,3,2,0:T(8,128)(2,1)S(1)} collective-permute-done((bf16[2,128,6,128]{1,3,2,0:T(8,128)(2,1)S(1)}, bf16[2,128,6,128]{1,3,2,0:T(8,128)(2,1)S(1)}, u32[]{:S(2)}, u32[]{:S(2)}) %collective-permute-start.13) | collective-permute-done | bytes 393248 | tf_op jit(solution)/shard_map/ppermute | solution.py:17
  201.3 6.3 %collective-permute-done.12 = bf16[2,128,6,128]{1,3,2,0:T(8,128)(2,1)S(1)} collective-permute-done((bf16[2,128,6,128]{1,3,2,0:T(8,128)(2,1)S(1)}, bf16[2,128,6,128]{1,3,2,0:T(8,128)(2,1)S(1)}, u32[]{:S(2)}, u32[]{:S(2)}) %collective-permute-start.12) | collective-permute-done | bytes 393248 | tf_op jit(solution)/shard_map/ppermute | solution.py:17
  (201 shorter events, 64.0 us)
Async XLA Ops:
  5.9 9.0 %copy-start.40 = (s32[4]{0:T(128)S(1)}, s32[4]{0:T(128)}, u32[]{:S(2)}) copy-start(s32[4]{0:T(128)} %constant.36) | copy-start | bytes 52
  6.9 31.7 %collective-permute-start.2 = (bf16[2,128,1280]{1,2,0:T(8,128)(2,1)}, bf16[2,128,1280]{1,2,0:T(8,128)(2,1)}, u32[]{:S(2)}, u32[]{:S(2)}) collective-permute-start(bf16[2,128,1280]{1,2,0:T(8,128)(2,1)} %pad_maximum_fusion.2), channel_id=1, source_target_pairs={{0,4},{1,5},{2,6},{3,7},{4,8},{5,9},{6,10},{7,11},{8,12},{9,13},{1... | collective-permute-start | bytes 1966088 | tf_op jit(solution)/shard_map/ppermute | solution.py:17
  10.1 21.9 %collective-permute-start = (bf16[2,128,1280]{1,2,0:T(8,128)(2,1)}, bf16[2,128,1280]{1,2,0:T(8,128)(2,1)}, u32[]{:S(2)}, u32[]{:S(2)}) collective-permute-start(bf16[2,128,1280]{1,2,0:T(8,128)(2,1)} %pad_maximum_fusion.2), channel_id=1, source_target_pairs={{0,1},{1,2},{2,3},{3,4},{4,5},{5,6},{6,7},{7,8},{8,9},{9,10},{10,1... | collective-permute-start | bytes 1966088 | tf_op jit(solution)/shard_map/ppermute | solution.py:17
  33.3 29.8 %collective-permute-start.1 = (bf16[2,128,1280]{1,2,0:T(8,128)(2,1)}, bf16[2,128,1280]{1,2,0:T(8,128)(2,1)S(1)}, u32[]{:S(2)}, u32[]{:S(2)}) collective-permute-start(bf16[2,128,1280]{1,2,0:T(8,128)(2,1)} %collective-permute-done), channel_id=1, source_target_pairs={{0,1},{1,2},{2,3},{3,4},{4,5},{5,6},{6,7},{7,8},{8,9},{9,10},{10,1... | collective-permute-start | bytes 1966088 | tf_op jit(solution)/shard_map/ppermute | solution.py:17
  38.6 22.5 %collective-permute-start.3 = (bf16[2,128,1280]{1,2,0:T(8,128)(2,1)}, bf16[2,128,1280]{1,2,0:T(8,128)(2,1)}, u32[]{:S(2)}, u32[]{:S(2)}) collective-permute-start(bf16[2,128,1280]{1,2,0:T(8,128)(2,1)} %collective-permute-done.2), channel_id=1, source_target_pairs={{0,4},{1,5},{2,6},{3,7},{4,8},{5,9},{6,10},{7,11},{8,12},{9,13},{1... | collective-permute-start | bytes 1966088 | tf_op jit(solution)/shard_map/ppermute | solution.py:17
  76.5 25.5 %collective-permute-start.6 = (bf16[2,128,768]{1,2,0:T(8,128)(2,1)}, bf16[2,128,768]{1,2,0:T(8,128)(2,1)}, u32[]{:S(2)}, u32[]{:S(2)}) collective-permute-start(bf16[2,128,768]{1,2,0:T(8,128)(2,1)} %pad_maximum_fusion.13), channel_id=1, source_target_pairs={{0,4},{1,5},{2,6},{3,7},{4,8},{5,9},{6,10},{7,11},{8,12},{9,13},{1... | collective-permute-start | bytes 1179656 | tf_op jit(solution)/shard_map/ppermute | solution.py:17
  79.7 27.5 %collective-permute-start.4 = (bf16[2,128,768]{1,2,0:T(8,128)(2,1)}, bf16[2,128,768]{1,2,0:T(8,128)(2,1)}, u32[]{:S(2)}, u32[]{:S(2)}) collective-permute-start(bf16[2,128,768]{1,2,0:T(8,128)(2,1)} %pad_maximum_fusion.13), channel_id=1, source_target_pairs={{0,1},{1,2},{2,3},{3,4},{4,5},{5,6},{6,7},{7,8},{8,9},{9,10},{10,1... | collective-permute-start | bytes 1179656 | tf_op jit(solution)/shard_map/ppermute | solution.py:17
  89.3 6.6 %copy-start.17 = (bf16[1,128,10,128]{1,3,2,0:T(8,128)(2,1)S(1)}, bf16[1,128,10,128]{1,3,2,0:T(8,128)(2,1)}, u32[]{:S(2)}) copy-start(bf16[1,128,10,128]{1,3,2,0:T(8,128)(2,1)} %get-tuple-element.11) | copy-start | bytes 983044
  90.2 8.0 %copy-start.16 = (bf16[1,128,10,128]{1,3,2,0:T(8,128)(2,1)S(1)}, bf16[1,128,10,128]{1,3,2,0:T(8,128)(2,1)}, u32[]{:S(2)}) copy-start(bf16[1,128,10,128]{1,3,2,0:T(8,128)(2,1)} %get-tuple-element.13) | copy-start | bytes 983044
  91.1 8.1 %copy-start.10 = (bf16[128,768]{0,1:T(8,128)(2,1)S(1)}, bf16[128,768]{0,1:T(8,128)(2,1)}, u32[]{:S(2)}) copy-start(bf16[128,768]{0,1:T(8,128)(2,1)} %copy.193) | copy-start | bytes 589828
  92.0 9.1 %copy-start.15 = (bf16[1,128,10,128]{1,3,2,0:T(8,128)(2,1)S(1)}, bf16[1,128,10,128]{1,3,2,0:T(8,128)(2,1)}, u32[]{:S(2)}) copy-start(bf16[1,128,10,128]{1,3,2,0:T(8,128)(2,1)} %get-tuple-element.14) | copy-start | bytes 983044
  92.0 9.1 %copy-start.18 = (bf16[1,128,10,128]{1,3,2,0:T(8,128)(2,1)S(1)}, bf16[1,128,10,128]{1,3,2,0:T(8,128)(2,1)}, u32[]{:S(2)}) copy-start(bf16[1,128,10,128]{1,3,2,0:T(8,128)(2,1)} %get-tuple-element.15) | copy-start | bytes 983044
  92.0 22.9 %collective-permute-start.10 = (bf16[2,128,10,128]{1,3,2,0:T(8,128)(2,1)}, bf16[2,128,10,128]{1,3,2,0:T(8,128)(2,1)}, u32[]{:S(2)}, u32[]{:S(2)}) collective-permute-start(bf16[2,128,10,128]{1,3,2,0:T(8,128)(2,1)} %pad_maximum_fusion.5), channel_id=1, source_target_pairs={{4,0},{5,1},{6,2},{7,3},{8,4},{9,5},{10,6},{11,7},{12,8},{13,9},{1... | collective-permute-start | bytes 1966088 | tf_op jit(solution)/shard_map/ppermute | solution.py:17
  96.8 27.7 %collective-permute-start.11 = (bf16[2,128,10,128]{1,3,2,0:T(8,128)(2,1)}, bf16[2,128,10,128]{1,3,2,0:T(8,128)(2,1)}, u32[]{:S(2)}, u32[]{:S(2)}) collective-permute-start(bf16[2,128,10,128]{1,3,2,0:T(8,128)(2,1)} %pad_maximum_fusion.6), channel_id=1, source_target_pairs={{8,0},{9,1},{10,2},{11,3},{12,4},{13,5},{14,6},{15,7},{24,16},{25,... | collective-permute-start | bytes 1966088 | tf_op jit(solution)/shard_map/ppermute | solution.py:17
  99.2 49.7 %collective-permute-start.9 = (bf16[2,128,10,128]{1,3,2,0:T(8,128)(2,1)}, bf16[2,128,10,128]{1,3,2,0:T(8,128)(2,1)}, u32[]{:S(2)}, u32[]{:S(2)}) collective-permute-start(bf16[2,128,10,128]{1,3,2,0:T(8,128)(2,1)} %pad_maximum_fusion.4), channel_id=1, source_target_pairs={{2,0},{3,1},{4,2},{5,3},{6,4},{7,5},{8,6},{9,7},{10,8},{11,9},{12,... | collective-permute-start | bytes 1966088 | tf_op jit(solution)/shard_map/ppermute | solution.py:17
  101.1 51.3 %copy-start.14 = (bf16[128,10,128]{0,2,1:T(8,128)(2,1)S(1)}, bf16[128,10,128]{0,2,1:T(8,128)(2,1)}, u32[]{:S(2)}) copy-start(bf16[128,10,128]{0,2,1:T(8,128)(2,1)} %get-tuple-element.10) | copy-start | bytes 983044
  102.0 50.4 %collective-permute-start.8 = (bf16[2,128,10,128]{1,3,2,0:T(8,128)(2,1)}, bf16[2,128,10,128]{1,3,2,0:T(8,128)(2,1)}, u32[]{:S(2)}, u32[]{:S(2)}) collective-permute-start(bf16[2,128,10,128]{1,3,2,0:T(8,128)(2,1)} %pad_maximum_fusion.3), channel_id=1, source_target_pairs={{1,0},{2,1},{3,2},{4,3},{5,4},{6,5},{7,6},{8,7},{9,8},{10,9},{11,1... | collective-permute-start | bytes 1966088 | tf_op jit(solution)/shard_map/ppermute | solution.py:17
  110.1 45.5 %collective-permute-start.7 = (bf16[2,128,768]{1,2,0:T(8,128)(2,1)}, bf16[2,128,768]{1,2,0:T(8,128)(2,1)}, u32[]{:S(2)}, u32[]{:S(2)}) collective-permute-start(bf16[2,128,768]{1,2,0:T(8,128)(2,1)} %collective-permute-done.6), channel_id=1, source_target_pairs={{0,4},{1,5},{2,6},{3,7},{4,8},{5,9},{6,10},{7,11},{8,12},{9,13},{1... | collective-permute-start | bytes 1179656 | tf_op jit(solution)/shard_map/ppermute | solution.py:17
  114.9 34.0 %copy-start.12 = (bf16[5,128,6,128]{1,3,0,2:T(8,128)(2,1)}, bf16[5,128,6,128]{1,3,0,2:T(8,128)(2,1)S(1)}, u32[]{:S(2)}) copy-start(bf16[5,128,6,128]{1,3,0,2:T(8,128)(2,1)S(1)} %constant_dynamic-update-slice_fusion.13) | copy-start | bytes 2949124
  114.9 42.7 %collective-permute-start.5 = (bf16[2,128,768]{1,2,0:T(8,128)(2,1)}, bf16[2,128,768]{1,2,0:T(8,128)(2,1)}, u32[]{:S(2)}, u32[]{:S(2)}) collective-permute-start(bf16[2,128,768]{1,2,0:T(8,128)(2,1)} %collective-permute-done.4), channel_id=1, source_target_pairs={{0,1},{1,2},{2,3},{3,4},{4,5},{5,6},{6,7},{7,8},{8,9},{9,10},{10,1... | collective-permute-start | bytes 1179656 | tf_op jit(solution)/shard_map/ppermute | solution.py:17
  154.7 5.8 %copy-start.25 = (bf16[1,128,6,128]{3,1,0,2:T(8,128)(2,1)S(1)}, bf16[1,128,6,128]{3,1,0,2:T(8,128)(2,1)}, u32[]{:S(2)}) copy-start(bf16[1,128,6,128]{3,1,0,2:T(8,128)(2,1)} %copy.122) | copy-start | bytes 589828
  154.7 5.9 %copy-start.9 = (bf16[128,768]{0,1:T(8,128)(2,1)S(1)}, bf16[128,768]{0,1:T(8,128)(2,1)}, u32[]{:S(2)}) copy-start(bf16[128,768]{0,1:T(8,128)(2,1)} %slice.315) | copy-start | bytes 589828
  166.9 6.4 %copy-start.30 = (bf16[1,128,6,128]{1,3,2,0:T(8,128)(2,1)S(1)}, bf16[1,128,6,128]{1,3,2,0:T(8,128)(2,1)}, u32[]{:S(2)}) copy-start(bf16[1,128,6,128]{1,3,2,0:T(8,128)(2,1)} %get-tuple-element.33) | copy-start | bytes 589828
  166.9 9.3 %copy-start.29 = (bf16[1,128,6,128]{1,3,2,0:T(8,128)(2,1)S(1)}, bf16[1,128,6,128]{1,3,2,0:T(8,128)(2,1)}, u32[]{:S(2)}) copy-start(bf16[1,128,6,128]{1,3,2,0:T(8,128)(2,1)} %get-tuple-element.34) | copy-start | bytes 589828
  167.9 10.4 %copy-start.23 = (bf16[128,1280]{1,0:T(8,128)(2,1)S(1)}, bf16[128,1280]{1,0:T(8,128)(2,1)}, u32[]{:S(2)}) copy-start(bf16[128,1280]{1,0:T(8,128)(2,1)} %copy.126) | copy-start | bytes 983044
  168.0 8.2 %copy-start.32 = (bf16[1,128,6,128]{1,3,2,0:T(8,128)(2,1)S(1)}, bf16[1,128,6,128]{1,3,2,0:T(8,128)(2,1)}, u32[]{:S(2)}) copy-start(bf16[1,128,6,128]{1,3,2,0:T(8,128)(2,1)} %get-tuple-element.35) | copy-start | bytes 589828
  169.1 21.2 %collective-permute-start.14 = (bf16[2,128,6,128]{1,3,2,0:T(8,128)(2,1)S(1)}, bf16[2,128,6,128]{1,3,2,0:T(8,128)(2,1)S(1)}, u32[]{:S(2)}, u32[]{:S(2)}) collective-permute-start(bf16[2,128,6,128]{1,3,2,0:T(8,128)(2,1)S(1)} %pad_maximum_fusion.16), channel_id=1, source_target_pairs={{4,0},{5,1},{6,2},{7,3},{8,4},{9,5},{10,6},{11,7},{12,8},{13,9},{1... | collective-permute-start | bytes 1179656 | tf_op jit(solution)/shard_map/ppermute | solution.py:17
  172.0 18.3 %collective-permute-start.15 = (bf16[2,128,6,128]{1,3,2,0:T(8,128)(2,1)S(1)}, bf16[2,128,6,128]{1,3,2,0:T(8,128)(2,1)S(1)}, u32[]{:S(2)}, u32[]{:S(2)}) collective-permute-start(bf16[2,128,6,128]{1,3,2,0:T(8,128)(2,1)S(1)} %pad_maximum_fusion.17), channel_id=1, source_target_pairs={{8,0},{9,1},{10,2},{11,3},{12,4},{13,5},{14,6},{15,7},{24,16},{25,... | collective-permute-start | bytes 1179656 | tf_op jit(solution)/shard_map/ppermute | solution.py:17
  174.3 27.0 %collective-permute-start.13 = (bf16[2,128,6,128]{1,3,2,0:T(8,128)(2,1)S(1)}, bf16[2,128,6,128]{1,3,2,0:T(8,128)(2,1)S(1)}, u32[]{:S(2)}, u32[]{:S(2)}) collective-permute-start(bf16[2,128,6,128]{1,3,2,0:T(8,128)(2,1)S(1)} %pad_maximum_fusion.15), channel_id=1, source_target_pairs={{2,0},{3,1},{4,2},{5,3},{6,4},{7,5},{8,6},{9,7},{10,8},{11,9},{12,... | collective-permute-start | bytes 1179656 | tf_op jit(solution)/shard_map/ppermute | solution.py:17
  176.3 31.3 %collective-permute-start.12 = (bf16[2,128,6,128]{1,3,2,0:T(8,128)(2,1)S(1)}, bf16[2,128,6,128]{1,3,2,0:T(8,128)(2,1)S(1)}, u32[]{:S(2)}, u32[]{:S(2)}) collective-permute-start(bf16[2,128,6,128]{1,3,2,0:T(8,128)(2,1)S(1)} %pad_maximum_fusion.14), channel_id=1, source_target_pairs={{1,0},{2,1},{3,2},{4,3},{5,4},{6,5},{7,6},{8,7},{9,8},{10,9},{11,1... | collective-permute-start | bytes 1179656 | tf_op jit(solution)/shard_map/ppermute | solution.py:17
  179.2 29.0 %copy-start.35 = (f32[128,64]{0,1:T(8,128)S(1)}, f32[128,64]{0,1:T(8,128)}, u32[]{:S(2)}) copy-start(f32[128,64]{0,1:T(8,128)} %copy-done.34) | copy-start | bytes 98308
  179.2 29.0 %copy-start.37 = (f32[128,64]{0,1:T(8,128)S(1)}, f32[128,64]{0,1:T(8,128)}, u32[]{:S(2)}) copy-start(f32[128,64]{0,1:T(8,128)} %copy-done.36) | copy-start | bytes 98308
  (25 other events, 41.7 us)

commit v14 on v8

--- a/solution.py
+++ b/solution.py
@@ -82,28 +82,42 @@
     return [received[0]] + [received[offset] for offset in offsets]
 
 
-def attention_kernel(*refs):
-    slots = (len(refs) - 5) // 2
-    query_ref, grad_ref, mask_ref = refs[0], refs[1], refs[2]
-    pair_refs = refs[3 : 3 + slots]
-    out_ref, qgrad_ref = refs[3 + slots], refs[4 + slots]
-    part_refs = refs[5 + slots :]
+def forward_kernel(*refs):
+    query_ref, mask_ref = refs[0], refs[1]
+    pair_refs = refs[2:-2]
+    out_ref, weights_ref = refs[-2], refs[-1]
     scale_factor = 1.0 / math.sqrt(HEAD_DIM)
     query = query_ref[...]
-    grad = grad_ref[...]
     keys = jnp.concatenate([ref[0] for ref in pair_refs], axis=0)
     vals = jnp.concatenate([ref[1] for ref in pair_refs], axis=0)
     last = (((1,), (1,)), ((), ()))
-    first = (((0,), (0,)), ((), ()))
     raw = lax.dot_general(query, keys, last, preferred_element_type=jnp.float32)
     scores = jnp.where(mask_ref[...] > 0, raw * scale_factor, -1e30)
     row_peak = jnp.max(scores, axis=1, keepdims=True)
     summed = jnp.sum(jnp.exp(scores - row_peak), axis=1, keepdims=True)
     log_total = row_peak + jnp.log(summed)
     weights32 = jnp.exp(scores - log_total)
+    weights_ref[0] = weights32
     weights = weights32.astype(jnp.bfloat16)
-    output = jnp.dot(weights, vals, preferred_element_type=jnp.float32).astype(jnp.bfloat16)
-    out_ref[...] = output
+    out_ref[...] = jnp.dot(weights, vals, preferred_element_type=jnp.float32).astype(jnp.bfloat16)
+
+
+def backward_kernel(*refs):
+    slots = (len(refs) - 5) // 2
+    query_ref, grad_ref, out_ref, weights_ref = refs[0], refs[1], refs[2], refs[3]
+    pair_refs = refs[4 : 4 + slots]
+    qgrad_ref = refs[4 + slots]
+    part_refs = refs[5 + slots :]
+    scale_factor = 1.0 / math.sqrt(HEAD_DIM)
+    query = query_ref[...]
+    grad = grad_ref[...]
+    output = out_ref[...]
+    weights32 = weights_ref[0]
+    weights = weights32.astype(jnp.bfloat16)
+    keys = jnp.concatenate([ref[0] for ref in pair_refs], axis=0)
+    vals = jnp.concatenate([ref[1] for ref in pair_refs], axis=0)
+    last = (((1,), (1,)), ((), ()))
+    first = (((0,), (0,)), ((), ()))
     grad_probs = lax.dot_general(grad, vals, last, preferred_element_type=jnp.float32)
     delta = jnp.sum(grad.astype(jnp.float32) * output.astype(jnp.float32), axis=1, keepdims=True)
     grad_scores = (weights32 * (grad_probs - delta) * scale_factor).astype(jnp.bfloat16)
@@ -116,29 +130,44 @@
         ref[1] = value_terms[slot * rows : (slot + 1) * rows].astype(jnp.bfloat16)
 
 
-def attend_chunk(query_c, received, grad_c, allowed, offsets, heads):
+def attend_forward(query_c, received, allowed, heads):
     rows, width = query_c.shape
     slots = len(received)
     mask = jnp.where(allowed, 1.0, 0.0).astype(jnp.float32).reshape(rows, slots * rows)
     flat_spec = pl.BlockSpec((rows, HEAD_DIM), lambda h: (0, h))
     pair_spec = pl.BlockSpec((2, rows, HEAD_DIM), lambda h: (0, 0, h))
     mask_spec = pl.BlockSpec((rows, slots * rows), lambda h: (0, 0))
+    weights_spec = pl.BlockSpec((1, rows, slots * rows), lambda h: (h, 0, 0))
+    return pl.pallas_call(
+        forward_kernel,
+        grid=(heads,),
+        in_specs=[flat_spec, mask_spec] + [pair_spec] * slots,
+        out_specs=[flat_spec, weights_spec],
+        out_shape=[
+            jax.ShapeDtypeStruct((rows, width), jnp.bfloat16),
+            jax.ShapeDtypeStruct((heads, rows, slots * rows), jnp.float32),
+        ],
+    )(query_c, mask, *received)
+
+
+def attend_backward(query_c, grad_c, output, weights32, received, heads):
+    rows, width = query_c.shape
+    slots = len(received)
+    flat_spec = pl.BlockSpec((rows, HEAD_DIM), lambda h: (0, h))
+    pair_spec = pl.BlockSpec((2, rows, HEAD_DIM), lambda h: (0, 0, h))
+    weights_spec = pl.BlockSpec((1, rows, slots * rows), lambda h: (h, 0, 0))
     pair_shape = jax.ShapeDtypeStruct((2, rows, width), jnp.bfloat16)
     results = pl.pallas_call(
-        attention_kernel,
+        backward_kernel,
         grid=(heads,),
-        in_specs=[flat_spec, flat_spec, mask_spec] + [pair_spec] * slots,
-        out_specs=[flat_spec, flat_spec] + [pair_spec] * slots,
-        out_shape=[
-            jax.ShapeDtypeStruct((rows, width), jnp.bfloat16),
-            jax.ShapeDtypeStruct((rows, width), jnp.float32),
-        ]
-        + [pair_shape] * slots,
-    )(query_c, grad_c, mask, *received)
-    output, query_grad = results[0], results[1]
-    own = (results[2][0], results[2][1])
-    outgoing = list(results[3:])
-    return output, query_grad, own, outgoing
+        in_specs=[flat_spec, flat_spec, flat_spec, weights_spec] + [pair_spec] * slots,
+        out_specs=[flat_spec] + [pair_spec] * slots,
+        out_shape=[jax.ShapeDtypeStruct((rows, width), jnp.float32)] + [pair_shape] * slots,
+    )(query_c, grad_c, output, weights32, *received)
+    query_grad = results[0]
+    own = (results[1][0], results[1][1])
+    outgoing = list(results[2:])
+    return query_grad, own, outgoing
 
 
 def gather_back(own, outgoing, offsets):
@@ -175,8 +204,9 @@
         if pending:
             key_c, value_c, _ = lax.optimization_barrier((key_c, value_c, pieces[-1][0]))
         received = send_chunk(key_c, value_c, offsets)
-        output, query_grad, own, outgoing = attend_chunk(
-            query_rot[:, cols], received, grad_out[:, cols], allowed, offsets, chunk_heads
+        output, weights32 = attend_forward(query_rot[:, cols], received, allowed, chunk_heads)
+        query_grad, own, outgoing = attend_backward(
+            query_rot[:, cols], grad_out[:, cols], output, weights32, received, chunk_heads
         )
         pending.append(outgoing)
         key_accum_c, value_accum_c = gather_back(own, outgoing, offsets)

time: 196 us -> 207 us (1.056)
  Pallas kernels: 20.3 us -> 31.9 us
    pallas_call x2 -> x4, Pallas kernels: 20.3 us -> 31.9 us  [the longest x2 16 us: attend_backward(): pl.pallas_call(backward_kernel, grid=(heads,), in_specs=[flat_spec, flat_...]
    unnamed x48 -> x54, local copies, waits for them, and re-layouts: 8.77 us -> 5.65 us
  transfers between devices with their start and end apart: 16 -> 16, of which waited for: 9 -> 7; matrix products, arithmetic and copies ran while one was open for 3% -> 3% of each run, Pallas kernels for 5% -> 12%
where the time goes in v14:
time: 207 us; the launch traced here: 205 us
  waiting for transfers between devices  107 us (52%)
  starting transfers between devices  42.5 us (21%)
  Pallas kernels  31.9 us (15%)
  local copies, waits for them, and re-layouts  12.6 us (6%)
  other arithmetic  9.34 us (5%)
    ppermute x16, waiting for transfers between devices, from_behind(): lax.ppermute(value, axis, [(source, source + steps) for source in range(l...  107 us
    ppermute x16, starting transfers between devices, from_behind(): lax.ppermute(value, axis, [(source, source + steps) for source in range(l...  42.5 us
    pallas_call x2, Pallas kernels, attend_backward(): pl.pallas_call(backward_kernel, grid=(heads,), in_specs=[flat_spec, flat_...  16 us
    pallas_call x2, Pallas kernels, attend_forward(): pl.pallas_call(forward_kernel, grid=(heads,), in_specs=[flat_spec, mask_s...  15.9 us
    unnamed x54, local copies, waits for them, and re-layouts  5.65 us
  transfers between devices with their start and end apart: 16, of which 7 were waited for; matrix products, arithmetic and copies ran while one was open for 3% of the time, Pallas kernels for 12%

profile of v14, /device:TPU:0, one launch (start us, length us, event | category | flops | bytes accessed | tf_op | source)
XLA Modules:
  0.0 204.9 jit_solution(14127759858472690178)
XLA Ops:
  2.5 1.8 slice_bitcast_fusion.1
  4.2 1.1 convert_bitcast_fusion.1
  8.5 5.0 %collective-permute-start.2 = (bf16[2,128,1024]{2,1,0:T(8,128)(2,1)S(1)}, bf16[2,128,1024]{2,1,0:T(8,128)(2,1)S(1)}, u32[]{:S(2)}, u32[]{:S(2)}) collective-permute-start(bf16[2,128,1024]{2,1,0:T(8,128)(2,1)S(1)} %pad_maximum_fusion.2.refs_2_.refs_4_), channel_id=1, source_target_pairs={{0,4},{1,5},{2,6},{3,7},{4,8},{5,9},{6,10},{7,11},{8,12},{9,13},{1... | collective-permute-start | bytes 1572872 | tf_op jit(solution)/shard_map/ppermute | solution.py:18
  13.5 1.5 collective-permute-start
  15.7 8.9 %collective-permute-done.2.refs_5_.refs_7_ = bf16[2,128,1024]{2,1,0:T(8,128)(2,1)S(1)} collective-permute-done((bf16[2,128,1024]{2,1,0:T(8,128)(2,1)S(1)}, bf16[2,128,1024]{2,1,0:T(8,128)(2,1)S(1)}, u32[]{:S(2)}, u32[]{:S(2)}) %collective-permute-start.2) | collective-permute-done | bytes 524320 | tf_op jit(solution)/shard_map/ppermute | solution.py:18
  24.7 4.4 %collective-permute-start.3 = (bf16[2,128,1024]{2,1,0:T(8,128)(2,1)S(1)}, bf16[2,128,1024]{2,1,0:T(8,128)(2,1)S(1)}, u32[]{:S(2)}, u32[]{:S(2)}) collective-permute-start(bf16[2,128,1024]{2,1,0:T(8,128)(2,1)S(1)} %collective-permute-done.2.refs_5_.refs_7_), channel_id=1, source_target_pairs={{0,4},{1,5},{2,6},{3,7},{4,8},{5,9},{6,10},{7,11},{8,12},{9,13},{1... | collective-permute-start | bytes 1572872 | tf_op jit(solution)/shard_map/ppermute | solution.py:18
  29.1 1.3 collective-permute-start.1
  32.6 6.8 %collective-permute-done.3.refs_6_.refs_8_ = bf16[2,128,1024]{2,1,0:T(8,128)(2,1)S(1)} collective-permute-done((bf16[2,128,1024]{2,1,0:T(8,128)(2,1)S(1)}, bf16[2,128,1024]{2,1,0:T(8,128)(2,1)S(1)}, u32[]{:S(2)}, u32[]{:S(2)}) %collective-permute-start.3) | collective-permute-done | bytes 524320 | tf_op jit(solution)/shard_map/ppermute | solution.py:18
  40.3 8.0 %shard_map.102 = (bf16[128,1024]{1,0:T(8,128)(2,1)}, f32[8,128,640]{2,1,0:T(8,128)}) custom-call(bf16[128,1024]{1,0:T(8,128)(2,1)} %get-tuple-element.58.refs_0_, f32[128,640]{1,0:T(8,128)} %copy.16.refs_1_, bf16[2,128,1024]{2,1,0:T(8,128)(2,1)} %copy-done, bf16[2,128,1024]{2,1,0:T(8,128)(2,1)} %copy-done.3, bf16[2,128,1024]{2,1,0:T(8,128)(2,1)} %copy-done.7, ...), custom_call_target="tpu_custom_call" | custom-call | tf_op jit(solution)/shard_map/pallas_call | solution.py:141
  48.4 13.0 %collective-permute-start.6 = (bf16[2,128,1024]{2,1,0:T(8,128)(2,1)S(1)}, bf16[2,128,1024]{2,1,0:T(8,128)(2,1)S(1)}, u32[]{:S(2)}, u32[]{:S(2)}) collective-permute-start(bf16[2,128,1024]{2,1,0:T(8,128)(2,1)S(1)} %pad_maximum_fusion.3.refs_2_.refs_4_), channel_id=1, source_target_pairs={{0,4},{1,5},{2,6},{3,7},{4,8},{5,9},{6,10},{7,11},{8,12},{9,13},{1... | collective-permute-start | bytes 1572872 | tf_op jit(solution)/shard_map/ppermute | solution.py:18
  61.3 1.3 collective-permute-start.4
  62.7 10.2 %collective-permute-done.6.refs_5_.refs_7_ = bf16[2,128,1024]{2,1,0:T(8,128)(2,1)S(1)} collective-permute-done((bf16[2,128,1024]{2,1,0:T(8,128)(2,1)S(1)}, bf16[2,128,1024]{2,1,0:T(8,128)(2,1)S(1)}, u32[]{:S(2)}, u32[]{:S(2)}) %collective-permute-start.6) | collective-permute-done | bytes 524320 | tf_op jit(solution)/shard_map/ppermute | solution.py:18
  72.9 4.4 %collective-permute-start.7 = (bf16[2,128,1024]{2,1,0:T(8,128)(2,1)S(1)}, bf16[2,128,1024]{2,1,0:T(8,128)(2,1)S(1)}, u32[]{:S(2)}, u32[]{:S(2)}) collective-permute-start(bf16[2,128,1024]{2,1,0:T(8,128)(2,1)S(1)} %collective-permute-done.6.refs_5_.refs_7_), channel_id=1, source_target_pairs={{0,4},{1,5},{2,6},{3,7},{4,8},{5,9},{6,10},{7,11},{8,12},{9,13},{1... | collective-permute-start | bytes 1572872 | tf_op jit(solution)/shard_map/ppermute | solution.py:18
  77.3 1.3 collective-permute-start.5
  78.6 1.9 fusion.2
  80.5 7.9 %shard_map.104 = (f32[128,1024]{1,0:T(8,128)}, bf16[2,128,1024]{2,1,0:T(8,128)(2,1)}, bf16[2,128,1024]{2,1,0:T(8,128)(2,1)}, bf16[2,128,1024]{2,1,0:T(8,128)(2,1...) custom-call(bf16[128,1024]{1,0:T(8,128)(2,1)} %get-tuple-element.58.refs_0_, ...), custom_call_target="tpu_custom_call" | custom-call | tf_op jit(solution)/shard_map/pallas_call | solution.py:160
  88.5 1.3 collective-permute-start.8
  89.8 1.3 collective-permute-start.9
  91.1 1.3 collective-permute-start.10
  92.4 1.3 collective-permute-start.11
  94.5 8.0 %shard_map.103 = (bf16[128,1024]{1,0:T(8,128)(2,1)}, f32[8,128,640]{2,1,0:T(8,128)}) custom-call(bf16[128,1024]{1,0:T(8,128)(2,1)} %get-tuple-element.59.refs_0_, f32[128,640]{1,0:T(8,128)} %copy.16.refs_1_, bf16[2,128,1024]{2,1,0:T(8,128)(2,1)} %copy-done.1, bf16[2,128,1024]{2,1,0:T(8,128)(2,1)} %copy-done.6, bf16[2,128,1024]{2,1,0:T(8,128)(2,1)} %copy-done.9, ...), custom_call_target="tpu_custom_call" | custom-call | tf_op jit(solution)/shard_map/pallas_call | solution.py:141
  102.5 8.1 %shard_map.105 = (f32[128,1024]{1,0:T(8,128)}, bf16[2,128,1024]{2,1,0:T(8,128)(2,1)}, bf16[2,128,1024]{2,1,0:T(8,128)(2,1)}, bf16[2,128,1024]{2,1,0:T(8,128)(2,1...) custom-call(bf16[128,1024]{1,0:T(8,128)(2,1)} %get-tuple-element.59.refs_0_, ...), custom_call_target="tpu_custom_call" | custom-call | tf_op jit(solution)/shard_map/pallas_call | solution.py:160
  110.5 1.3 collective-permute-start.12
  111.8 1.3 collective-permute-start.13
  113.1 1.3 collective-permute-start.14
  114.4 16.7 %collective-permute-done.10 = bf16[2,128,1024]{2,1,0:T(8,128)(2,1)} collective-permute-done((bf16[2,128,1024]{2,1,0:T(8,128)(2,1)}, bf16[2,128,1024]{2,1,0:T(8,128)(2,1)}, u32[]{:S(2)}, u32[]{:S(2)}) %collective-permute-start.10) | collective-permute-done | bytes 524320 | tf_op jit(solution)/shard_map/ppermute | solution.py:18
  131.1 1.3 collective-permute-start.15
  132.4 21.2 %collective-permute-done.11 = bf16[2,128,1024]{2,1,0:T(8,128)(2,1)S(1)} collective-permute-done((bf16[2,128,1024]{2,1,0:T(8,128)(2,1)}, bf16[2,128,1024]{2,1,0:T(8,128)(2,1)S(1)}, u32[]{:S(2)}, u32[]{:S(2)}) %collective-permute-start.11) | collective-permute-done | bytes 524320 | tf_op jit(solution)/shard_map/ppermute | solution.py:18
  153.6 1.6 fusion
  157.1 8.4 %collective-permute-done.14 = bf16[2,128,1024]{2,1,0:T(8,128)(2,1)S(1)} collective-permute-done((bf16[2,128,1024]{2,1,0:T(8,128)(2,1)}, bf16[2,128,1024]{2,1,0:T(8,128)(2,1)S(1)}, u32[]{:S(2)}, u32[]{:S(2)}) %collective-permute-start.14) | collective-permute-done | bytes 524320 | tf_op jit(solution)/shard_map/ppermute | solution.py:18
  165.6 34.4 %collective-permute-done.15 = bf16[2,128,1024]{2,1,0:T(8,128)(2,1)S(1)} collective-permute-done((bf16[2,128,1024]{2,1,0:T(8,128)(2,1)}, bf16[2,128,1024]{2,1,0:T(8,128)(2,1)S(1)}, u32[]{:S(2)}, u32[]{:S(2)}) %collective-permute-start.15) | collective-permute-done | bytes 524320 | tf_op jit(solution)/shard_map/ppermute | solution.py:18
  201.9 0.9 copy.31
  (92 shorter events, 14.7 us)
Async XLA Ops:
  0.6 4.9 %copy-start.16 = (bf16[128,2048]{1,0:T(8,128)(2,1)S(1)}, bf16[128,2048]{1,0:T(8,128)(2,1)}, u32[]{:S(2)}) copy-start(bf16[128,2048]{1,0:T(8,128)(2,1)} %param.8) | copy-start | bytes 1572868
  7.0 8.7 %copy-start.21 = (s32[4]{0:T(128)S(1)}, s32[4]{0:T(128)}, u32[]{:S(2)}) copy-start(s32[4]{0:T(128)} %constant.31) | copy-start | bytes 52
  8.5 30.8 %copy-start = (bf16[2,128,1024]{2,1,0:T(8,128)(2,1)}, bf16[2,128,1024]{2,1,0:T(8,128)(2,1)S(1)}, u32[]{:S(2)}) copy-start(bf16[2,128,1024]{2,1,0:T(8,128)(2,1)S(1)} %pad_maximum_fusion.2.refs_2_.refs_4_) | copy-start | bytes 1572868
  8.5 16.1 %collective-permute-start.2 = (bf16[2,128,1024]{2,1,0:T(8,128)(2,1)S(1)}, bf16[2,128,1024]{2,1,0:T(8,128)(2,1)S(1)}, u32[]{:S(2)}, u32[]{:S(2)}) collective-permute-start(bf16[2,128,1024]{2,1,0:T(8,128)(2,1)S(1)} %pad_maximum_fusion.2.refs_2_.refs_4_), channel_id=1, source_target_pairs={{0,4},{1,5},{2,6},{3,7},{4,8},{5,9},{6,10},{7,11},{8,12},{9,13},{1... | collective-permute-start | bytes 1572872 | tf_op jit(solution)/shard_map/ppermute | solution.py:18
  13.5 15.6 %collective-permute-start = (bf16[2,128,1024]{2,1,0:T(8,128)(2,1)S(1)}, bf16[2,128,1024]{2,1,0:T(8,128)(2,1)S(1)}, u32[]{:S(2)}, u32[]{:S(2)}) collective-permute-start(bf16[2,128,1024]{2,1,0:T(8,128)(2,1)S(1)} %pad_maximum_fusion.2.refs_2_.refs_4_), channel_id=1, source_target_pairs={{0,1},{1,2},{2,3},{3,4},{4,5},{5,6},{6,7},{7,8},{8,9},{9,10},{10,1... | collective-permute-start | bytes 1572872 | tf_op jit(solution)/shard_map/ppermute | solution.py:18
  24.6 14.7 %copy-start.2 = (bf16[2,128,1024]{2,1,0:T(8,128)(2,1)}, bf16[2,128,1024]{2,1,0:T(8,128)(2,1)S(1)}, u32[]{:S(2)}) copy-start(bf16[2,128,1024]{2,1,0:T(8,128)(2,1)S(1)} %collective-permute-done.2.refs_5_.refs_7_) | copy-start | bytes 1572868
  24.7 14.7 %collective-permute-start.3 = (bf16[2,128,1024]{2,1,0:T(8,128)(2,1)S(1)}, bf16[2,128,1024]{2,1,0:T(8,128)(2,1)S(1)}, u32[]{:S(2)}, u32[]{:S(2)}) collective-permute-start(bf16[2,128,1024]{2,1,0:T(8,128)(2,1)S(1)} %collective-permute-done.2.refs_5_.refs_7_), channel_id=1, source_target_pairs={{0,4},{1,5},{2,6},{3,7},{4,8},{5,9},{6,10},{7,11},{8,12},{9,13},{1... | collective-permute-start | bytes 1572872 | tf_op jit(solution)/shard_map/ppermute | solution.py:18
  29.1 10.3 %copy-start.3 = (bf16[2,128,1024]{2,1,0:T(8,128)(2,1)}, bf16[2,128,1024]{2,1,0:T(8,128)(2,1)S(1)}, u32[]{:S(2)}) copy-start(bf16[2,128,1024]{2,1,0:T(8,128)(2,1)S(1)} %collective-permute-done.refs_3_.refs_5_) | copy-start | bytes 1572868
  29.1 10.2 %collective-permute-start.1 = (bf16[2,128,1024]{2,1,0:T(8,128)(2,1)S(1)}, bf16[2,128,1024]{2,1,0:T(8,128)(2,1)S(1)}, u32[]{:S(2)}, u32[]{:S(2)}) collective-permute-start(bf16[2,128,1024]{2,1,0:T(8,128)(2,1)S(1)} %collective-permute-done.refs_3_.refs_5_), channel_id=1, source_target_pairs={{0,1},{1,2},{2,3},{3,4},{4,5},{5,6},{6,7},{7,8},{8,9},{9,10},{10,1... | collective-permute-start | bytes 1572872 | tf_op jit(solution)/shard_map/ppermute | solution.py:18
  31.5 16.7 %copy-start.12 = (bf16[128,1024]{1,0:T(8,128)(2,1)S(1)}, bf16[128,1024]{1,0:T(8,128)(2,1)}, u32[]{:S(2)}) copy-start(bf16[128,1024]{1,0:T(8,128)(2,1)} %get-tuple-element.24) | copy-start | bytes 786436
  31.7 16.6 %copy-start.13 = (bf16[128,1024]{1,0:T(8,128)(2,1)S(1)}, bf16[128,1024]{1,0:T(8,128)(2,1)}, u32[]{:S(2)}) copy-start(bf16[128,1024]{1,0:T(8,128)(2,1)} %get-tuple-element.23) | copy-start | bytes 786436
  48.4 40.1 %copy-start.1 = (bf16[2,128,1024]{2,1,0:T(8,128)(2,1)}, bf16[2,128,1024]{2,1,0:T(8,128)(2,1)S(1)}, u32[]{:S(2)}) copy-start(bf16[2,128,1024]{2,1,0:T(8,128)(2,1)S(1)} %pad_maximum_fusion.3.refs_2_.refs_4_) | copy-start | bytes 1572868
  48.4 24.5 %collective-permute-start.6 = (bf16[2,128,1024]{2,1,0:T(8,128)(2,1)S(1)}, bf16[2,128,1024]{2,1,0:T(8,128)(2,1)S(1)}, u32[]{:S(2)}, u32[]{:S(2)}) collective-permute-start(bf16[2,128,1024]{2,1,0:T(8,128)(2,1)S(1)} %pad_maximum_fusion.3.refs_2_.refs_4_), channel_id=1, source_target_pairs={{0,4},{1,5},{2,6},{3,7},{4,8},{5,9},{6,10},{7,11},{8,12},{9,13},{1... | collective-permute-start | bytes 1572872 | tf_op jit(solution)/shard_map/ppermute | solution.py:18
  61.3 15.9 %collective-permute-start.4 = (bf16[2,128,1024]{2,1,0:T(8,128)(2,1)S(1)}, bf16[2,128,1024]{2,1,0:T(8,128)(2,1)S(1)}, u32[]{:S(2)}, u32[]{:S(2)}) collective-permute-start(bf16[2,128,1024]{2,1,0:T(8,128)(2,1)S(1)} %pad_maximum_fusion.3.refs_2_.refs_4_), channel_id=1, source_target_pairs={{0,1},{1,2},{2,3},{3,4},{4,5},{5,6},{6,7},{7,8},{8,9},{9,10},{10,1... | collective-permute-start | bytes 1572872 | tf_op jit(solution)/shard_map/ppermute | solution.py:18
  72.9 15.6 %copy-start.4 = (bf16[2,128,1024]{2,1,0:T(8,128)(2,1)}, bf16[2,128,1024]{2,1,0:T(8,128)(2,1)S(1)}, u32[]{:S(2)}) copy-start(bf16[2,128,1024]{2,1,0:T(8,128)(2,1)S(1)} %collective-permute-done.6.refs_5_.refs_7_) | copy-start | bytes 1572868
  72.9 19.5 %collective-permute-start.7 = (bf16[2,128,1024]{2,1,0:T(8,128)(2,1)S(1)}, bf16[2,128,1024]{2,1,0:T(8,128)(2,1)S(1)}, u32[]{:S(2)}, u32[]{:S(2)}) collective-permute-start(bf16[2,128,1024]{2,1,0:T(8,128)(2,1)S(1)} %collective-permute-done.6.refs_5_.refs_7_), channel_id=1, source_target_pairs={{0,4},{1,5},{2,6},{3,7},{4,8},{5,9},{6,10},{7,11},{8,12},{9,13},{1... | collective-permute-start | bytes 1572872 | tf_op jit(solution)/shard_map/ppermute | solution.py:18
  77.3 11.2 %copy-start.6 = (bf16[2,128,1024]{2,1,0:T(8,128)(2,1)}, bf16[2,128,1024]{2,1,0:T(8,128)(2,1)S(1)}, u32[]{:S(2)}) copy-start(bf16[2,128,1024]{2,1,0:T(8,128)(2,1)S(1)} %collective-permute-done.4.refs_3_.refs_5_) | copy-start | bytes 1572868
  77.3 16.4 %collective-permute-start.5 = (bf16[2,128,1024]{2,1,0:T(8,128)(2,1)S(1)}, bf16[2,128,1024]{2,1,0:T(8,128)(2,1)S(1)}, u32[]{:S(2)}, u32[]{:S(2)}) collective-permute-start(bf16[2,128,1024]{2,1,0:T(8,128)(2,1)S(1)} %collective-permute-done.4.refs_3_.refs_5_), channel_id=1, source_target_pairs={{0,1},{1,2},{2,3},{3,4},{4,5},{5,6},{6,7},{7,8},{8,9},{9,10},{10,1... | collective-permute-start | bytes 1572872 | tf_op jit(solution)/shard_map/ppermute | solution.py:18
  88.5 23.4 %collective-permute-start.8 = (bf16[2,128,1024]{2,1,0:T(8,128)(2,1)}, bf16[2,128,1024]{2,1,0:T(8,128)(2,1)S(1)}, u32[]{:S(2)}, u32[]{:S(2)}) collective-permute-start(bf16[2,128,1024]{2,1,0:T(8,128)(2,1)} %get-tuple-element.31), channel_id=1, source_target_pairs={{1,0},{2,1},{3,2},{4,3},{5,4},{6,5},{7,6},{8,7},{9,8},{10,9},{11,1... | collective-permute-start | bytes 1572872 | tf_op jit(solution)/shard_map/ppermute | solution.py:18
  89.8 23.4 %collective-permute-start.9 = (bf16[2,128,1024]{2,1,0:T(8,128)(2,1)}, bf16[2,128,1024]{2,1,0:T(8,128)(2,1)S(1)}, u32[]{:S(2)}, u32[]{:S(2)}) collective-permute-start(bf16[2,128,1024]{2,1,0:T(8,128)(2,1)} %get-tuple-element.32), channel_id=1, source_target_pairs={{2,0},{3,1},{4,2},{5,3},{6,4},{7,5},{8,6},{9,7},{10,8},{11,9},{12,... | collective-permute-start | bytes 1572872 | tf_op jit(solution)/shard_map/ppermute | solution.py:18
  91.1 40.0 %collective-permute-start.10 = (bf16[2,128,1024]{2,1,0:T(8,128)(2,1)}, bf16[2,128,1024]{2,1,0:T(8,128)(2,1)}, u32[]{:S(2)}, u32[]{:S(2)}) collective-permute-start(bf16[2,128,1024]{2,1,0:T(8,128)(2,1)} %get-tuple-element.33), channel_id=1, source_target_pairs={{4,0},{5,1},{6,2},{7,3},{8,4},{9,5},{10,6},{11,7},{12,8},{13,9},{1... | collective-permute-start | bytes 1572872 | tf_op jit(solution)/shard_map/ppermute | solution.py:18
  92.4 1.3 copy-start.8
  92.4 61.2 %collective-permute-start.11 = (bf16[2,128,1024]{2,1,0:T(8,128)(2,1)}, bf16[2,128,1024]{2,1,0:T(8,128)(2,1)S(1)}, u32[]{:S(2)}, u32[]{:S(2)}) collective-permute-start(bf16[2,128,1024]{2,1,0:T(8,128)(2,1)} %get-tuple-element.34), channel_id=1, source_target_pairs={{8,0},{9,1},{10,2},{11,3},{12,4},{13,5},{14,6},{15,7},{24,16},{25,... | collective-permute-start | bytes 1572872 | tf_op jit(solution)/shard_map/ppermute | solution.py:18
  102.5 51.1 %copy-start.18 = (bf16[2,128,1024]{2,1,0:T(8,128)(2,1)S(1)}, bf16[2,128,1024]{2,1,0:T(8,128)(2,1)}, u32[]{:S(2)}) copy-start(bf16[2,128,1024]{2,1,0:T(8,128)(2,1)} %get-tuple-element.30) | copy-start | bytes 1572868
  110.5 46.6 %collective-permute-start.12 = (bf16[2,128,1024]{2,1,0:T(8,128)(2,1)}, bf16[2,128,1024]{2,1,0:T(8,128)(2,1)S(1)}, u32[]{:S(2)}, u32[]{:S(2)}) collective-permute-start(bf16[2,128,1024]{2,1,0:T(8,128)(2,1)} %get-tuple-element.36), channel_id=1, source_target_pairs={{1,0},{2,1},{3,2},{4,3},{5,4},{6,5},{7,6},{8,7},{9,8},{10,9},{11,1... | collective-permute-start | bytes 1572872 | tf_op jit(solution)/shard_map/ppermute | solution.py:18
  111.8 45.3 %collective-permute-start.13 = (bf16[2,128,1024]{2,1,0:T(8,128)(2,1)}, bf16[2,128,1024]{2,1,0:T(8,128)(2,1)S(1)}, u32[]{:S(2)}, u32[]{:S(2)}) collective-permute-start(bf16[2,128,1024]{2,1,0:T(8,128)(2,1)} %get-tuple-element.37), channel_id=1, source_target_pairs={{2,0},{3,1},{4,2},{5,3},{6,4},{7,5},{8,6},{9,7},{10,8},{11,9},{12,... | collective-permute-start | bytes 1572872 | tf_op jit(solution)/shard_map/ppermute | solution.py:18
  113.1 52.4 %collective-permute-start.14 = (bf16[2,128,1024]{2,1,0:T(8,128)(2,1)}, bf16[2,128,1024]{2,1,0:T(8,128)(2,1)S(1)}, u32[]{:S(2)}, u32[]{:S(2)}) collective-permute-start(bf16[2,128,1024]{2,1,0:T(8,128)(2,1)} %get-tuple-element.38), channel_id=1, source_target_pairs={{4,0},{5,1},{6,2},{7,3},{8,4},{9,5},{10,6},{11,7},{12,8},{13,9},{1... | collective-permute-start | bytes 1572872 | tf_op jit(solution)/shard_map/ppermute | solution.py:18
  131.1 68.8 %collective-permute-start.15 = (bf16[2,128,1024]{2,1,0:T(8,128)(2,1)}, bf16[2,128,1024]{2,1,0:T(8,128)(2,1)S(1)}, u32[]{:S(2)}, u32[]{:S(2)}) collective-permute-start(bf16[2,128,1024]{2,1,0:T(8,128)(2,1)} %get-tuple-element.39), channel_id=1, source_target_pairs={{8,0},{9,1},{10,2},{11,3},{12,4},{13,5},{14,6},{15,7},{24,16},{25,... | collective-permute-start | bytes 1572872 | tf_op jit(solution)/shard_map/ppermute | solution.py:18
  153.6 1.7 copy-start.17
  153.6 1.7 copy-start.20
  155.3 1.0 copy-start.11
  155.3 44.6 %copy-start.19 = (bf16[2,128,1024]{2,1,0:T(8,128)(2,1)S(1)}, bf16[2,128,1024]{2,1,0:T(8,128)(2,1)}, u32[]{:S(2)}) copy-start(bf16[2,128,1024]{2,1,0:T(8,128)(2,1)} %get-tuple-element.35) | copy-start | bytes 1572868
  (6 other events, 5.2 us)

commit v15 on v13

--- a/solution.py
+++ b/solution.py
@@ -8,7 +8,7 @@
 HEADS = 16
 HEAD_DIM = 128
 BLOCK = 128
-CHUNK_HEADS = (10, 6)
+CHUNK_HEADS = (4, 6, 6)
 
 
 def from_behind(value, axis, steps):

time: 213 us -> 218 us (1.023)
  waiting for transfers between devices: 83.4 us -> 61.1 us
  starting transfers between devices: 45.3 us -> 66.9 us
  other arithmetic: 19.1 us -> 26 us
    ppermute x16 -> x24, waiting for transfers between devices: 83.4 us -> 61.1 us  [from_behind(): lax.ppermute(value, axis, [(source, source + steps) for source in range(l...]
    ppermute x16 -> x24, starting transfers between devices: 45.3 us -> 66.9 us  [from_behind(): lax.ppermute(value, axis, [(source, source + steps) for source in range(l...]
    another operation x8 -> x12, other arithmetic: 6.66 us -> 12.1 us  [attend_chunk(): jnp.stack([key_terms[0, slot_index], value_terms[0, slot_index]])]
    another operation x12 -> x18, local copies, waits for them, and re-layouts: 5.16 us -> 9.95 us  [attend_chunk(): jnp.stack([moved[0].reshape(head_shape) for moved in received])[None]]
    slice x8 -> x12, local copies, waits for them, and re-layouts: 12.6 us -> 17.4 us  [attend_chunk(): moved[0].reshape(head_shape)]
    slice x4, local copies, waits for them, and re-layouts: 3.35 us -> 0.99 us  [on_device(): key_c, value_c = (key_rot[:, cols], values[:, cols])]
    unnamed x101 -> x88, local copies, waits for them, and re-layouts: 11.4 us -> 9.08 us
    another operation x6 -> x7, other arithmetic: 3.39 us -> 5.19 us
  transfers between devices with their start and end apart: 16 -> 24, of which waited for: 8 -> 9; matrix products, arithmetic and copies ran while one was open for 21% -> 22% of each run, Pallas kernels for 0% -> 0%
where the time goes in v15:
time: 218 us; the launch traced here: 216 us
  starting transfers between devices  66.9 us (31%)
  waiting for transfers between devices  61.1 us (28%)
  local copies, waits for them, and re-layouts  48.9 us (22%)
  other arithmetic  26 us (12%)
  matrix products  10.8 us (5%)
  between operations  2.61 us (1%)
    ppermute x24, starting transfers between devices, from_behind(): lax.ppermute(value, axis, [(source, source + steps) for source in range(l...  66.9 us
    ppermute x24, waiting for transfers between devices, from_behind(): lax.ppermute(value, axis, [(source, source + steps) for source in range(l...  61.1 us
    slice x12, local copies, waits for them, and re-layouts, attend_chunk(): moved[0].reshape(head_shape)  17.4 us
    another operation x12, other arithmetic, attend_chunk(): jnp.stack([key_terms[0, slot_index], value_terms[0, slot_index]])  12.1 us
    another operation x18, local copies, waits for them, and re-layouts, attend_chunk(): jnp.stack([moved[0].reshape(head_shape) for moved in received])[None]  9.95 us
    unnamed x88, local copies, waits for them, and re-layouts  9.08 us
    another operation x7, other arithmetic  5.19 us
  transfers between devices with their start and end apart: 24, of which 9 were waited for; matrix products, arithmetic and copies ran while one was open for 22% of the time, Pallas kernels for 0%

profile of v15, /device:TPU:15, one launch (start us, length us, event | category | flops | bytes accessed | tf_op | source)
XLA Modules:
  0.0 216.4 jit_solution(9660647569849210962)
XLA Ops:
  6.5 3.2 %collective-permute-start.2 = (bf16[2,128,512]{1,2,0:T(8,128)(2,1)}, bf16[2,128,512]{1,2,0:T(8,128)(2,1)}, u32[]{:S(2)}, u32[]{:S(2)}) collective-permute-start(bf16[2,128,512]{1,2,0:T(8,128)(2,1)} %pad_maximum_fusion.18), channel_id=1, source_target_pairs={{0,4},{1,5},{2,6},{3,7},{4,8},{5,9},{6,10},{7,11},{8,12},{9,13},{1... | collective-permute-start | bytes 786440 | tf_op jit(solution)/shard_map/ppermute | solution.py:17
  9.7 4.0 %collective-permute-start = (bf16[2,128,512]{1,2,0:T(8,128)(2,1)}, bf16[2,128,512]{1,2,0:T(8,128)(2,1)}, u32[]{:S(2)}, u32[]{:S(2)}) collective-permute-start(bf16[2,128,512]{1,2,0:T(8,128)(2,1)} %pad_maximum_fusion.18), channel_id=1, source_target_pairs={{0,1},{1,2},{2,3},{3,4},{4,5},{5,6},{6,7},{7,8},{8,9},{9,10},{10,1... | collective-permute-start | bytes 786440 | tf_op jit(solution)/shard_map/ppermute | solution.py:17
  17.6 1.9 collective-permute-start.3
  21.7 4.4 %collective-permute-start.1 = (bf16[2,128,512]{1,2,0:T(8,128)(2,1)}, bf16[2,128,512]{1,2,0:T(8,128)(2,1)}, u32[]{:S(2)}, u32[]{:S(2)}) collective-permute-start(bf16[2,128,512]{1,2,0:T(8,128)(2,1)} %collective-permute-done), channel_id=1, source_target_pairs={{0,1},{1,2},{2,3},{3,4},{4,5},{5,6},{6,7},{7,8},{8,9},{9,10},{10,1... | collective-permute-start | bytes 786440 | tf_op jit(solution)/shard_map/ppermute | solution.py:17
  37.0 2.4 %collective-permute-start.14 = (bf16[2,128,4,128]{1,3,2,0:T(8,128)(2,1)}, bf16[2,128,4,128]{1,3,2,0:T(8,128)(2,1)}, u32[]{:S(2)}, u32[]{:S(2)}) collective-permute-start(bf16[2,128,4,128]{1,3,2,0:T(8,128)(2,1)} %pad_maximum_fusion.21), channel_id=1, source_target_pairs={{4,0},{5,1},{6,2},{7,3},{8,4},{9,5},{10,6},{11,7},{12,8},{13,9},{1... | collective-permute-start | bytes 786440 | tf_op jit(solution)/shard_map/ppermute | solution.py:17
  42.2 3.6 %collective-permute-start.13 = (bf16[2,128,4,128]{1,3,2,0:T(8,128)(2,1)}, bf16[2,128,4,128]{1,3,2,0:T(8,128)(2,1)}, u32[]{:S(2)}, u32[]{:S(2)}) collective-permute-start(bf16[2,128,4,128]{1,3,2,0:T(8,128)(2,1)} %pad_maximum_fusion.20), channel_id=1, source_target_pairs={{2,0},{3,1},{4,2},{5,3},{6,4},{7,5},{8,6},{9,7},{10,8},{11,9},{12,... | collective-permute-start | bytes 786440 | tf_op jit(solution)/shard_map/ppermute | solution.py:17
  46.6 3.3 %collective-permute-start.12 = (bf16[2,128,4,128]{1,3,2,0:T(8,128)(2,1)}, bf16[2,128,4,128]{1,3,2,0:T(8,128)(2,1)}, u32[]{:S(2)}, u32[]{:S(2)}) collective-permute-start(bf16[2,128,4,128]{1,3,2,0:T(8,128)(2,1)} %pad_maximum_fusion.19), channel_id=1, source_target_pairs={{1,0},{2,1},{3,2},{4,3},{5,4},{6,5},{7,6},{8,7},{9,8},{10,9},{11,1... | collective-permute-start | bytes 786440 | tf_op jit(solution)/shard_map/ppermute | solution.py:17
  50.8 4.4 %collective-permute-start.4 = (bf16[2,128,768]{1,2,0:T(8,128)(2,1)}, bf16[2,128,768]{1,2,0:T(8,128)(2,1)}, u32[]{:S(2)}, u32[]{:S(2)}) collective-permute-start(bf16[2,128,768]{1,2,0:T(8,128)(2,1)} %pad_maximum_fusion.8), channel_id=1, source_target_pairs={{0,1},{1,2},{2,3},{3,4},{4,5},{5,6},{6,7},{7,8},{8,9},{9,10},{10,1... | collective-permute-start | bytes 1179656 | tf_op jit(solution)/shard_map/ppermute | solution.py:17
  56.1 3.8 %collective-permute-start.6 = (bf16[2,128,768]{1,2,0:T(8,128)(2,1)}, bf16[2,128,768]{1,2,0:T(8,128)(2,1)}, u32[]{:S(2)}, u32[]{:S(2)}) collective-permute-start(bf16[2,128,768]{1,2,0:T(8,128)(2,1)} %pad_maximum_fusion.8), channel_id=1, source_target_pairs={{0,4},{1,5},{2,6},{3,7},{4,8},{5,9},{6,10},{7,11},{8,12},{9,13},{1... | collective-permute-start | bytes 1179656 | tf_op jit(solution)/shard_map/ppermute | solution.py:17
  59.9 3.7 %collective-permute-done.13 = bf16[2,128,4,128]{1,3,2,0:T(8,128)(2,1)} collective-permute-done((bf16[2,128,4,128]{1,3,2,0:T(8,128)(2,1)}, bf16[2,128,4,128]{1,3,2,0:T(8,128)(2,1)}, u32[]{:S(2)}, u32[]{:S(2)}) %collective-permute-start.13) | collective-permute-done | bytes 262176 | tf_op jit(solution)/shard_map/ppermute | solution.py:17
  63.6 4.5 %collective-permute-done.12 = bf16[2,128,4,128]{1,3,2,0:T(8,128)(2,1)} collective-permute-done((bf16[2,128,4,128]{1,3,2,0:T(8,128)(2,1)}, bf16[2,128,4,128]{1,3,2,0:T(8,128)(2,1)}, u32[]{:S(2)}, u32[]{:S(2)}) %collective-permute-start.12) | collective-permute-done | bytes 262176 | tf_op jit(solution)/shard_map/ppermute | solution.py:17
  68.1 2.2 %fusion.48 = (bf16[128,4,128]{0,2,1:T(8,128)(2,1)S(1)}, f32[128,4,128]{0,2,1:T(8,128)}) fusion(bf16[128,4,128]{0,2,1:T(8,128)(2,1)S(1)} %get-tuple-element.46, bf16[2,128,4,128]{1,3,2,0:T(8,128)(2,1)} %collective-permute-done.15, bf16[2,128,4,128]{1,3,2,0:T(8,128)(2,1)} %collective-permute-done.14, bf16[2,128,4,128]{1,3,2,0:T(8,128)(2,1)} %collective-permute-done.13, ...), kind=kLoop, calls=%fused_computation.120 | loop fusion | flops 1245184 | bytes 1703936 | tf_op jit(solution)/shard_map/convert.34
  73.3 1.9 collective-permute-start.5
  75.2 1.9 collective-permute-start.7
  81.0 7.6 %collective-permute-done.7 = bf16[2,128,768]{1,2,0:T(8,128)(2,1)} collective-permute-done((bf16[2,128,768]{1,2,0:T(8,128)(2,1)}, bf16[2,128,768]{1,2,0:T(8,128)(2,1)}, u32[]{:S(2)}, u32[]{:S(2)}) %collective-permute-start.7) | collective-permute-done | bytes 393248 | tf_op jit(solution)/shard_map/ppermute | solution.py:17
  101.1 3.8 %collective-permute-start.10 = (bf16[2,128,768]{1,2,0:T(8,128)(2,1)}, bf16[2,128,768]{1,2,0:T(8,128)(2,1)}, u32[]{:S(2)}, u32[]{:S(2)}) collective-permute-start(bf16[2,128,768]{1,2,0:T(8,128)(2,1)} %pad_maximum_fusion.9), channel_id=1, source_target_pairs={{0,4},{1,5},{2,6},{3,7},{4,8},{5,9},{6,10},{7,11},{8,12},{9,13},{1... | collective-permute-start | bytes 1179656 | tf_op jit(solution)/shard_map/ppermute | solution.py:17
  105.0 2.1 collective-permute-start.8
  108.6 2.1 fusion.14
  114.9 2.2 %collective-permute-start.18 = (bf16[2,128,6,128]{1,3,2,0:T(8,128)(2,1)}, bf16[2,128,6,128]{1,3,2,0:T(8,128)(2,1)}, u32[]{:S(2)}, u32[]{:S(2)}) collective-permute-start(bf16[2,128,6,128]{1,3,2,0:T(8,128)(2,1)} %pad_maximum_fusion.12), channel_id=1, source_target_pairs={{4,0},{5,1},{6,2},{7,3},{8,4},{9,5},{10,6},{11,7},{12,8},{13,9},{1... | collective-permute-start | bytes 1179656 | tf_op jit(solution)/shard_map/ppermute | solution.py:17
  122.0 3.8 %collective-permute-start.17 = (bf16[2,128,6,128]{1,3,2,0:T(8,128)(2,1)}, bf16[2,128,6,128]{1,3,2,0:T(8,128)(2,1)}, u32[]{:S(2)}, u32[]{:S(2)}) collective-permute-start(bf16[2,128,6,128]{1,3,2,0:T(8,128)(2,1)} %pad_maximum_fusion.11), channel_id=1, source_target_pairs={{2,0},{3,1},{4,2},{5,3},{6,4},{7,5},{8,6},{9,7},{10,8},{11,9},{12,... | collective-permute-start | bytes 1179656 | tf_op jit(solution)/shard_map/ppermute | solution.py:17
  127.1 1.9 collective-permute-start.16
  131.8 4.5 %collective-permute-start.9 = (bf16[2,128,768]{1,2,0:T(8,128)(2,1)}, bf16[2,128,768]{1,2,0:T(8,128)(2,1)}, u32[]{:S(2)}, u32[]{:S(2)}) collective-permute-start(bf16[2,128,768]{1,2,0:T(8,128)(2,1)} %collective-permute-done.8), channel_id=1, source_target_pairs={{0,1},{1,2},{2,3},{3,4},{4,5},{5,6},{6,7},{7,8},{8,9},{9,10},{10,1... | collective-permute-start | bytes 1179656 | tf_op jit(solution)/shard_map/ppermute | solution.py:17
  136.4 3.8 %collective-permute-start.11 = (bf16[2,128,768]{1,2,0:T(8,128)(2,1)}, bf16[2,128,768]{1,2,0:T(8,128)(2,1)}, u32[]{:S(2)}, u32[]{:S(2)}) collective-permute-start(bf16[2,128,768]{1,2,0:T(8,128)(2,1)} %collective-permute-done.10), channel_id=1, source_target_pairs={{0,4},{1,5},{2,6},{3,7},{4,8},{5,9},{6,10},{7,11},{8,12},{9,13},{1... | collective-permute-start | bytes 1179656 | tf_op jit(solution)/shard_map/ppermute | solution.py:17
  140.3 13.6 %collective-permute-done.17 = bf16[2,128,6,128]{1,3,2,0:T(8,128)(2,1)} collective-permute-done((bf16[2,128,6,128]{1,3,2,0:T(8,128)(2,1)}, bf16[2,128,6,128]{1,3,2,0:T(8,128)(2,1)}, u32[]{:S(2)}, u32[]{:S(2)}) %collective-permute-start.17) | collective-permute-done | bytes 393248 | tf_op jit(solution)/shard_map/ppermute | solution.py:17
  153.8 2.1 collective-permute-done.16
  155.9 1.9 fusion.45
  174.3 1.9 collective-permute-start.22
  179.5 1.9 collective-permute-start.21
  181.5 2.1 collective-permute-start.20
  184.5 10.0 %collective-permute-done.22 = bf16[2,128,6,128]{1,3,2,0:T(8,128)(2,1)S(1)} collective-permute-done((bf16[2,128,6,128]{1,3,2,0:T(8,128)(2,1)S(1)}, bf16[2,128,6,128]{1,3,2,0:T(8,128)(2,1)S(1)}, u32[]{:S(2)}, u32[]{:S(2)}) %collective-permute-start.22) | collective-permute-done | bytes 393248 | tf_op jit(solution)/shard_map/ppermute | solution.py:17
  194.5 11.4 %collective-permute-done.21 = bf16[2,128,6,128]{1,3,2,0:T(8,128)(2,1)S(1)} collective-permute-done((bf16[2,128,6,128]{1,3,2,0:T(8,128)(2,1)S(1)}, bf16[2,128,6,128]{1,3,2,0:T(8,128)(2,1)S(1)}, u32[]{:S(2)}, u32[]{:S(2)}) %collective-permute-start.21) | collective-permute-done | bytes 393248 | tf_op jit(solution)/shard_map/ppermute | solution.py:17
  205.9 6.7 %collective-permute-done.20 = bf16[2,128,6,128]{1,3,2,0:T(8,128)(2,1)S(1)} collective-permute-done((bf16[2,128,6,128]{1,3,2,0:T(8,128)(2,1)S(1)}, bf16[2,128,6,128]{1,3,2,0:T(8,128)(2,1)S(1)}, u32[]{:S(2)}, u32[]{:S(2)}) %collective-permute-start.20) | collective-permute-done | bytes 393248 | tf_op jit(solution)/shard_map/ppermute | solution.py:17
  (238 shorter events, 85.0 us)
Async XLA Ops:
  6.5 11.1 %collective-permute-start.2 = (bf16[2,128,512]{1,2,0:T(8,128)(2,1)}, bf16[2,128,512]{1,2,0:T(8,128)(2,1)}, u32[]{:S(2)}, u32[]{:S(2)}) collective-permute-start(bf16[2,128,512]{1,2,0:T(8,128)(2,1)} %pad_maximum_fusion.18), channel_id=1, source_target_pairs={{0,4},{1,5},{2,6},{3,7},{4,8},{5,9},{6,10},{7,11},{8,12},{9,13},{1... | collective-permute-start | bytes 786440 | tf_op jit(solution)/shard_map/ppermute | solution.py:17
  9.7 10.8 %collective-permute-start = (bf16[2,128,512]{1,2,0:T(8,128)(2,1)}, bf16[2,128,512]{1,2,0:T(8,128)(2,1)}, u32[]{:S(2)}, u32[]{:S(2)}) collective-permute-start(bf16[2,128,512]{1,2,0:T(8,128)(2,1)} %pad_maximum_fusion.18), channel_id=1, source_target_pairs={{0,1},{1,2},{2,3},{3,4},{4,5},{5,6},{6,7},{7,8},{8,9},{9,10},{10,1... | collective-permute-start | bytes 786440 | tf_op jit(solution)/shard_map/ppermute | solution.py:17
  17.6 9.3 %collective-permute-start.3 = (bf16[2,128,512]{1,2,0:T(8,128)(2,1)}, bf16[2,128,512]{1,2,0:T(8,128)(2,1)}, u32[]{:S(2)}, u32[]{:S(2)}) collective-permute-start(bf16[2,128,512]{1,2,0:T(8,128)(2,1)} %collective-permute-done.2), channel_id=1, source_target_pairs={{0,4},{1,5},{2,6},{3,7},{4,8},{5,9},{6,10},{7,11},{8,12},{9,13},{1... | collective-permute-start | bytes 786440 | tf_op jit(solution)/shard_map/ppermute | solution.py:17
  21.7 8.0 %collective-permute-start.1 = (bf16[2,128,512]{1,2,0:T(8,128)(2,1)}, bf16[2,128,512]{1,2,0:T(8,128)(2,1)}, u32[]{:S(2)}, u32[]{:S(2)}) collective-permute-start(bf16[2,128,512]{1,2,0:T(8,128)(2,1)} %collective-permute-done), channel_id=1, source_target_pairs={{0,1},{1,2},{2,3},{3,4},{4,5},{5,6},{6,7},{7,8},{8,9},{9,10},{10,1... | collective-permute-start | bytes 786440 | tf_op jit(solution)/shard_map/ppermute | solution.py:17
  37.0 19.1 %collective-permute-start.14 = (bf16[2,128,4,128]{1,3,2,0:T(8,128)(2,1)}, bf16[2,128,4,128]{1,3,2,0:T(8,128)(2,1)}, u32[]{:S(2)}, u32[]{:S(2)}) collective-permute-start(bf16[2,128,4,128]{1,3,2,0:T(8,128)(2,1)} %pad_maximum_fusion.21), channel_id=1, source_target_pairs={{4,0},{5,1},{6,2},{7,3},{8,4},{9,5},{10,6},{11,7},{12,8},{13,9},{1... | collective-permute-start | bytes 786440 | tf_op jit(solution)/shard_map/ppermute | solution.py:17
  40.2 19.7 %collective-permute-start.15 = (bf16[2,128,4,128]{1,3,2,0:T(8,128)(2,1)}, bf16[2,128,4,128]{1,3,2,0:T(8,128)(2,1)}, u32[]{:S(2)}, u32[]{:S(2)}) collective-permute-start(bf16[2,128,4,128]{1,3,2,0:T(8,128)(2,1)} %pad_maximum_fusion.22), channel_id=1, source_target_pairs={{8,0},{9,1},{10,2},{11,3},{12,4},{13,5},{14,6},{15,7},{24,16},{25,... | collective-permute-start | bytes 786440 | tf_op jit(solution)/shard_map/ppermute | solution.py:17
  42.2 21.4 %collective-permute-start.13 = (bf16[2,128,4,128]{1,3,2,0:T(8,128)(2,1)}, bf16[2,128,4,128]{1,3,2,0:T(8,128)(2,1)}, u32[]{:S(2)}, u32[]{:S(2)}) collective-permute-start(bf16[2,128,4,128]{1,3,2,0:T(8,128)(2,1)} %pad_maximum_fusion.20), channel_id=1, source_target_pairs={{2,0},{3,1},{4,2},{5,3},{6,4},{7,5},{8,6},{9,7},{10,8},{11,9},{12,... | collective-permute-start | bytes 786440 | tf_op jit(solution)/shard_map/ppermute | solution.py:17
  46.6 21.5 %collective-permute-start.12 = (bf16[2,128,4,128]{1,3,2,0:T(8,128)(2,1)}, bf16[2,128,4,128]{1,3,2,0:T(8,128)(2,1)}, u32[]{:S(2)}, u32[]{:S(2)}) collective-permute-start(bf16[2,128,4,128]{1,3,2,0:T(8,128)(2,1)} %pad_maximum_fusion.19), channel_id=1, source_target_pairs={{1,0},{2,1},{3,2},{4,3},{5,4},{6,5},{7,6},{8,7},{9,8},{10,9},{11,1... | collective-permute-start | bytes 786440 | tf_op jit(solution)/shard_map/ppermute | solution.py:17
  50.8 19.5 %collective-permute-start.4 = (bf16[2,128,768]{1,2,0:T(8,128)(2,1)}, bf16[2,128,768]{1,2,0:T(8,128)(2,1)}, u32[]{:S(2)}, u32[]{:S(2)}) collective-permute-start(bf16[2,128,768]{1,2,0:T(8,128)(2,1)} %pad_maximum_fusion.8), channel_id=1, source_target_pairs={{0,1},{1,2},{2,3},{3,4},{4,5},{5,6},{6,7},{7,8},{8,9},{9,10},{10,1... | collective-permute-start | bytes 1179656 | tf_op jit(solution)/shard_map/ppermute | solution.py:17
  56.1 19.1 %collective-permute-start.6 = (bf16[2,128,768]{1,2,0:T(8,128)(2,1)}, bf16[2,128,768]{1,2,0:T(8,128)(2,1)}, u32[]{:S(2)}, u32[]{:S(2)}) collective-permute-start(bf16[2,128,768]{1,2,0:T(8,128)(2,1)} %pad_maximum_fusion.8), channel_id=1, source_target_pairs={{0,4},{1,5},{2,6},{3,7},{4,8},{5,9},{6,10},{7,11},{8,12},{9,13},{1... | collective-permute-start | bytes 1179656 | tf_op jit(solution)/shard_map/ppermute | solution.py:17
  73.3 18.9 %collective-permute-start.5 = (bf16[2,128,768]{1,2,0:T(8,128)(2,1)}, bf16[2,128,768]{1,2,0:T(8,128)(2,1)}, u32[]{:S(2)}, u32[]{:S(2)}) collective-permute-start(bf16[2,128,768]{1,2,0:T(8,128)(2,1)} %collective-permute-done.4), channel_id=1, source_target_pairs={{0,1},{1,2},{2,3},{3,4},{4,5},{5,6},{6,7},{7,8},{8,9},{9,10},{10,1... | collective-permute-start | bytes 1179656 | tf_op jit(solution)/shard_map/ppermute | solution.py:17
  75.2 13.4 %collective-permute-start.7 = (bf16[2,128,768]{1,2,0:T(8,128)(2,1)}, bf16[2,128,768]{1,2,0:T(8,128)(2,1)}, u32[]{:S(2)}, u32[]{:S(2)}) collective-permute-start(bf16[2,128,768]{1,2,0:T(8,128)(2,1)} %collective-permute-done.6), channel_id=1, source_target_pairs={{0,4},{1,5},{2,6},{3,7},{4,8},{5,9},{6,10},{7,11},{8,12},{9,13},{1... | collective-permute-start | bytes 1179656 | tf_op jit(solution)/shard_map/ppermute | solution.py:17
  101.1 30.7 %collective-permute-start.10 = (bf16[2,128,768]{1,2,0:T(8,128)(2,1)}, bf16[2,128,768]{1,2,0:T(8,128)(2,1)}, u32[]{:S(2)}, u32[]{:S(2)}) collective-permute-start(bf16[2,128,768]{1,2,0:T(8,128)(2,1)} %pad_maximum_fusion.9), channel_id=1, source_target_pairs={{0,4},{1,5},{2,6},{3,7},{4,8},{5,9},{6,10},{7,11},{8,12},{9,13},{1... | collective-permute-start | bytes 1179656 | tf_op jit(solution)/shard_map/ppermute | solution.py:17
  105.0 22.1 %collective-permute-start.8 = (bf16[2,128,768]{1,2,0:T(8,128)(2,1)}, bf16[2,128,768]{1,2,0:T(8,128)(2,1)}, u32[]{:S(2)}, u32[]{:S(2)}) collective-permute-start(bf16[2,128,768]{1,2,0:T(8,128)(2,1)} %pad_maximum_fusion.9), channel_id=1, source_target_pairs={{0,1},{1,2},{2,3},{3,4},{4,5},{5,6},{6,7},{7,8},{8,9},{9,10},{10,1... | collective-permute-start | bytes 1179656 | tf_op jit(solution)/shard_map/ppermute | solution.py:17
  111.2 14.6 %copy-start.15 = (bf16[1,128,6,128]{1,3,2,0:T(8,128)(2,1)S(1)}, bf16[1,128,6,128]{1,3,2,0:T(8,128)(2,1)}, u32[]{:S(2)}) copy-start(bf16[1,128,6,128]{1,3,2,0:T(8,128)(2,1)} %get-tuple-element.30) | copy-start | bytes 589828
  113.0 12.8 %copy-start.20 = (bf16[1,128,6,128]{1,3,2,0:T(8,128)(2,1)S(1)}, bf16[1,128,6,128]{1,3,2,0:T(8,128)(2,1)}, u32[]{:S(2)}) copy-start(bf16[1,128,6,128]{1,3,2,0:T(8,128)(2,1)} %get-tuple-element.36) | copy-start | bytes 589828
  114.9 21.5 %collective-permute-start.18 = (bf16[2,128,6,128]{1,3,2,0:T(8,128)(2,1)}, bf16[2,128,6,128]{1,3,2,0:T(8,128)(2,1)}, u32[]{:S(2)}, u32[]{:S(2)}) collective-permute-start(bf16[2,128,6,128]{1,3,2,0:T(8,128)(2,1)} %pad_maximum_fusion.12), channel_id=1, source_target_pairs={{4,0},{5,1},{6,2},{7,3},{8,4},{9,5},{10,6},{11,7},{12,8},{13,9},{1... | collective-permute-start | bytes 1179656 | tf_op jit(solution)/shard_map/ppermute | solution.py:17
  118.9 21.4 %collective-permute-start.19 = (bf16[2,128,6,128]{1,3,2,0:T(8,128)(2,1)}, bf16[2,128,6,128]{1,3,2,0:T(8,128)(2,1)}, u32[]{:S(2)}, u32[]{:S(2)}) collective-permute-start(bf16[2,128,6,128]{1,3,2,0:T(8,128)(2,1)} %pad_maximum_fusion.13), channel_id=1, source_target_pairs={{8,0},{9,1},{10,2},{11,3},{12,4},{13,5},{14,6},{15,7},{24,16},{25,... | collective-permute-start | bytes 1179656 | tf_op jit(solution)/shard_map/ppermute | solution.py:17
  122.0 31.9 %collective-permute-start.17 = (bf16[2,128,6,128]{1,3,2,0:T(8,128)(2,1)}, bf16[2,128,6,128]{1,3,2,0:T(8,128)(2,1)}, u32[]{:S(2)}, u32[]{:S(2)}) collective-permute-start(bf16[2,128,6,128]{1,3,2,0:T(8,128)(2,1)} %pad_maximum_fusion.11), channel_id=1, source_target_pairs={{2,0},{3,1},{4,2},{5,3},{6,4},{7,5},{8,6},{9,7},{10,8},{11,9},{12,... | collective-permute-start | bytes 1179656 | tf_op jit(solution)/shard_map/ppermute | solution.py:17
  127.1 28.8 %collective-permute-start.16 = (bf16[2,128,6,128]{1,3,2,0:T(8,128)(2,1)}, bf16[2,128,6,128]{1,3,2,0:T(8,128)(2,1)}, u32[]{:S(2)}, u32[]{:S(2)}) collective-permute-start(bf16[2,128,6,128]{1,3,2,0:T(8,128)(2,1)} %pad_maximum_fusion.10), channel_id=1, source_target_pairs={{1,0},{2,1},{3,2},{4,3},{5,4},{6,5},{7,6},{8,7},{9,8},{10,9},{11,1... | collective-permute-start | bytes 1179656 | tf_op jit(solution)/shard_map/ppermute | solution.py:17
  131.8 30.9 %collective-permute-start.9 = (bf16[2,128,768]{1,2,0:T(8,128)(2,1)}, bf16[2,128,768]{1,2,0:T(8,128)(2,1)}, u32[]{:S(2)}, u32[]{:S(2)}) collective-permute-start(bf16[2,128,768]{1,2,0:T(8,128)(2,1)} %collective-permute-done.8), channel_id=1, source_target_pairs={{0,1},{1,2},{2,3},{3,4},{4,5},{5,6},{6,7},{7,8},{8,9},{9,10},{10,1... | collective-permute-start | bytes 1179656 | tf_op jit(solution)/shard_map/ppermute | solution.py:17
  136.4 24.5 %collective-permute-start.11 = (bf16[2,128,768]{1,2,0:T(8,128)(2,1)}, bf16[2,128,768]{1,2,0:T(8,128)(2,1)}, u32[]{:S(2)}, u32[]{:S(2)}) collective-permute-start(bf16[2,128,768]{1,2,0:T(8,128)(2,1)} %collective-permute-done.10), channel_id=1, source_target_pairs={{0,4},{1,5},{2,6},{3,7},{4,8},{5,9},{6,10},{7,11},{8,12},{9,13},{1... | collective-permute-start | bytes 1179656 | tf_op jit(solution)/shard_map/ppermute | solution.py:17
  173.3 11.1 %copy-start.2 = (f32[4,128,128,1]{2,1,3,0:T(8,128)S(1)}, f32[4,128,128,1]{2,1,3,0:T(8,128)}, u32[]{:S(2)}) copy-start(f32[4,128,128,1]{2,1,3,0:T(8,128)} %fusion.41) | copy-start | bytes 786436
  174.3 20.2 %collective-permute-start.22 = (bf16[2,128,6,128]{1,3,2,0:T(8,128)(2,1)S(1)}, bf16[2,128,6,128]{1,3,2,0:T(8,128)(2,1)S(1)}, u32[]{:S(2)}, u32[]{:S(2)}) collective-permute-start(bf16[2,128,6,128]{1,3,2,0:T(8,128)(2,1)S(1)} %pad_maximum_fusion.16), channel_id=1, source_target_pairs={{4,0},{5,1},{6,2},{7,3},{8,4},{9,5},{10,6},{11,7},{12,8},{13,9},{1... | collective-permute-start | bytes 1179656 | tf_op jit(solution)/shard_map/ppermute | solution.py:17
  177.2 17.3 %collective-permute-start.23 = (bf16[2,128,6,128]{1,3,2,0:T(8,128)(2,1)S(1)}, bf16[2,128,6,128]{1,3,2,0:T(8,128)(2,1)S(1)}, u32[]{:S(2)}, u32[]{:S(2)}) collective-permute-start(bf16[2,128,6,128]{1,3,2,0:T(8,128)(2,1)S(1)} %pad_maximum_fusion.17), channel_id=1, source_target_pairs={{8,0},{9,1},{10,2},{11,3},{12,4},{13,5},{14,6},{15,7},{24,16},{25,... | collective-permute-start | bytes 1179656 | tf_op jit(solution)/shard_map/ppermute | solution.py:17
  179.5 26.4 %collective-permute-start.21 = (bf16[2,128,6,128]{1,3,2,0:T(8,128)(2,1)S(1)}, bf16[2,128,6,128]{1,3,2,0:T(8,128)(2,1)S(1)}, u32[]{:S(2)}, u32[]{:S(2)}) collective-permute-start(bf16[2,128,6,128]{1,3,2,0:T(8,128)(2,1)S(1)} %pad_maximum_fusion.15), channel_id=1, source_target_pairs={{2,0},{3,1},{4,2},{5,3},{6,4},{7,5},{8,6},{9,7},{10,8},{11,9},{12,... | collective-permute-start | bytes 1179656 | tf_op jit(solution)/shard_map/ppermute | solution.py:17
  181.5 31.1 %copy-start.12 = (bf16[128,6,128]{0,2,1:T(8,128)(2,1)S(1)}, bf16[128,6,128]{0,2,1:T(8,128)(2,1)}, u32[]{:S(2)}) copy-start(bf16[128,6,128]{0,2,1:T(8,128)(2,1)} %get-tuple-element.31) | copy-start | bytes 589828
  181.5 31.1 %copy-start.13 = (bf16[128,6,128]{0,2,1:T(8,128)(2,1)S(1)}, bf16[128,6,128]{0,2,1:T(8,128)(2,1)}, u32[]{:S(2)}) copy-start(bf16[128,6,128]{0,2,1:T(8,128)(2,1)} %get-tuple-element.43) | copy-start | bytes 589828
  181.5 31.0 %collective-permute-start.20 = (bf16[2,128,6,128]{1,3,2,0:T(8,128)(2,1)S(1)}, bf16[2,128,6,128]{1,3,2,0:T(8,128)(2,1)S(1)}, u32[]{:S(2)}, u32[]{:S(2)}) collective-permute-start(bf16[2,128,6,128]{1,3,2,0:T(8,128)(2,1)S(1)} %pad_maximum_fusion.14), channel_id=1, source_target_pairs={{1,0},{2,1},{3,2},{4,3},{5,4},{6,5},{7,6},{8,7},{9,8},{10,9},{11,1... | collective-permute-start | bytes 1179656 | tf_op jit(solution)/shard_map/ppermute | solution.py:17
  184.5 28.5 %copy-start.3 = (f32[128,4,128]{0,2,1:T(8,128)S(1)}, f32[128,4,128]{0,2,1:T(8,128)}, u32[]{:S(2)}) copy-start(f32[128,4,128]{0,2,1:T(8,128)} %get-tuple-element.25) | copy-start | bytes 786436
  184.5 28.6 %copy-start.26 = (f32[128,64]{0,1:T(8,128)S(1)}, f32[128,64]{0,1:T(8,128)}, u32[]{:S(2)}) copy-start(f32[128,64]{0,1:T(8,128)} %copy-done.25) | copy-start | bytes 98308
  184.5 28.6 %copy-start.28 = (f32[128,64]{0,1:T(8,128)S(1)}, f32[128,64]{0,1:T(8,128)}, u32[]{:S(2)}) copy-start(f32[128,64]{0,1:T(8,128)} %copy-done.27) | copy-start | bytes 98308
  (23 other events, 101.8 us)

commit v16 on v6

--- a/solution.py
+++ b/solution.py
@@ -122,7 +122,7 @@
         jnp.stack([key_terms[0, slot_index], value_terms[0, slot_index]]).astype(jnp.bfloat16)
         for slot_index in range(1, len(offsets) + 1)
     ]
-    return output, query_grad, own, outgoing
+    return output, query_grad, own, outgoing, log_total
 
 
 def gather_back(own, outgoing, offsets):
@@ -157,12 +157,13 @@
     for chunk, cols in enumerate(columns):
         key_c, value_c = key_rot[:, cols], values[:, cols]
         if pending:
-            key_c, value_c, _ = lax.optimization_barrier((key_c, value_c, pieces[-1][0]))
+            key_c, value_c, _ = lax.optimization_barrier((key_c, value_c, statistics))
         received = send_chunk(key_c, value_c, offsets)
-        output, query_grad, own, outgoing = attend_chunk(
+        output, query_grad, own, outgoing, log_total = attend_chunk(
             query_rot[:, cols], received, grad_out[:, cols], allowed, offsets, chunk_heads
         )
         pending.append(outgoing)
+        statistics = log_total
         key_accum_c, value_accum_c = gather_back(own, outgoing, offsets)
         rows = query_rot.shape[0]
         pieces.append(

time: 186 us -> 229 us (1.23)
  waiting for transfers between devices: 46.5 us -> 92.1 us
  other arithmetic: 23.8 us -> 15.7 us
  local copies, waits for them, and re-layouts: 53.2 us -> 61.3 us
  starting transfers between devices: 48.2 us -> 44.7 us
    ppermute x16, waiting for transfers between devices: 46.5 us -> 92.1 us  [from_behind(): lax.ppermute(value, axis, [(source, source + steps) for source in range(l...]
    slice x0 -> x4, local copies, waits for them, and re-layouts: none -> 7.42 us  [attend_chunk(): moved[1].reshape(head_shape)]
    slice x8 -> x4, local copies, waits for them, and re-layouts: 14.7 us -> 7.43 us  [attend_chunk(): moved[0].reshape(head_shape)]
    unnamed x73 -> x107, local copies, waits for them, and re-layouts: 12.9 us -> 20.1 us
    another operation x8, other arithmetic: 8.69 us -> 3.58 us  [attend_chunk(): jnp.stack([key_terms[0, slot_index], value_terms[0, slot_index]])]
    ppermute x16, starting transfers between devices: 48.2 us -> 44.7 us  [from_behind(): lax.ppermute(value, axis, [(source, source + steps) for source in range(l...]
    dot_general x2, matrix products: 4.08 us -> 1.17 us  [attend_chunk(): jnp.einsum('bhtnu,bnuhd->bthd', grad_scores, key_stack, preferred_element...]
    another operation x12, local copies, waits for them, and re-layouts: 12.7 us -> 15.1 us  [attend_chunk(): jnp.stack([moved[0].reshape(head_shape) for moved in received])[None]]
  transfers between devices with their start and end apart: 16 -> 16, of which waited for: 7 -> 9; matrix products, arithmetic and copies ran while one was open for 35% -> 19% of each run, Pallas kernels for 0% -> 0%
where the time goes in v16:
time: 229 us; the launch traced here: 228 us
  waiting for transfers between devices  92.1 us (40%)
  local copies, waits for them, and re-layouts  61.3 us (27%)
  starting transfers between devices  44.7 us (20%)
  other arithmetic  15.7 us (7%)
  matrix products  11.9 us (5%)
    ppermute x16, waiting for transfers between devices, from_behind(): lax.ppermute(value, axis, [(source, source + steps) for source in range(l...  92.1 us
    ppermute x16, starting transfers between devices, from_behind(): lax.ppermute(value, axis, [(source, source + steps) for source in range(l...  44.7 us
    unnamed x107, local copies, waits for them, and re-layouts  20.1 us
    another operation x12, local copies, waits for them, and re-layouts, attend_chunk(): jnp.stack([moved[0].reshape(head_shape) for moved in received])[None]  15.1 us
    slice x4, local copies, waits for them, and re-layouts, attend_chunk(): moved[0].reshape(head_shape)  7.43 us
    slice x4, local copies, waits for them, and re-layouts, attend_chunk(): moved[1].reshape(head_shape)  7.42 us
  transfers between devices with their start and end apart: 16, of which 9 were waited for; matrix products, arithmetic and copies ran while one was open for 19% of the time, Pallas kernels for 0%

profile of v16, /device:TPU:15, one launch (start us, length us, event | category | flops | bytes accessed | tf_op | source)
XLA Modules:
  0.0 227.9 jit_solution(3783518720548677844)
XLA Ops:
  6.3 3.2 %collective-permute-start.6 = (bf16[2,128,1024]{1,2,0:T(8,128)(2,1)}, bf16[2,128,1024]{1,2,0:T(8,128)(2,1)}, u32[]{:S(2)}, u32[]{:S(2)}) collective-permute-start(bf16[2,128,1024]{1,2,0:T(8,128)(2,1)} %pad_maximum_fusion.5), channel_id=1, source_target_pairs={{0,4},{1,5},{2,6},{3,7},{4,8},{5,9},{6,10},{7,11},{8,12},{9,13},{1... | collective-permute-start | bytes 1572872 | tf_op jit(solution)/shard_map/ppermute | solution.py:17
  9.5 4.0 %collective-permute-start.4 = (bf16[2,128,1024]{1,2,0:T(8,128)(2,1)}, bf16[2,128,1024]{1,2,0:T(8,128)(2,1)}, u32[]{:S(2)}, u32[]{:S(2)}) collective-permute-start(bf16[2,128,1024]{1,2,0:T(8,128)(2,1)} %pad_maximum_fusion.5), channel_id=1, source_target_pairs={{0,1},{1,2},{2,3},{3,4},{4,5},{5,6},{6,7},{7,8},{8,9},{9,10},{10,1... | collective-permute-start | bytes 1572872 | tf_op jit(solution)/shard_map/ppermute | solution.py:17
  14.5 2.0 collective-permute-start.2
  16.6 1.9 collective-permute-start
  25.7 1.9 copy.173
  27.6 1.9 fusion.42
  29.5 1.9 collective-permute-start.7
  31.6 5.3 %collective-permute-start.5 = (bf16[2,128,1024]{1,2,0:T(8,128)(2,1)}, bf16[2,128,1024]{1,2,0:T(8,128)(2,1)}, u32[]{:S(2)}, u32[]{:S(2)}) collective-permute-start(bf16[2,128,1024]{1,2,0:T(8,128)(2,1)} %collective-permute-done.4), channel_id=1, source_target_pairs={{0,1},{1,2},{2,3},{3,4},{4,5},{5,6},{6,7},{7,8},{8,9},{9,10},{10,1... | collective-permute-start | bytes 1572872 | tf_op jit(solution)/shard_map/ppermute | solution.py:17
  36.9 1.9 fusion.44
  38.8 4.5 %collective-permute-done.2 = bf16[2,128,1024]{1,2,0:T(8,128)(2,1)} collective-permute-done((bf16[2,128,1024]{1,2,0:T(8,128)(2,1)}, bf16[2,128,1024]{1,2,0:T(8,128)(2,1)}, u32[]{:S(2)}, u32[]{:S(2)}) %collective-permute-start.2) | collective-permute-done | bytes 524320 | tf_op jit(solution)/shard_map/ppermute | solution.py:17
  43.2 1.9 fusion.36
  45.1 6.0 %collective-permute-done = bf16[2,128,1024]{1,2,0:T(8,128)(2,1)} collective-permute-done((bf16[2,128,1024]{1,2,0:T(8,128)(2,1)}, bf16[2,128,1024]{1,2,0:T(8,128)(2,1)}, u32[]{:S(2)}, u32[]{:S(2)}) %collective-permute-start) | collective-permute-done | bytes 524320 | tf_op jit(solution)/shard_map/ppermute | solution.py:17
  51.1 1.8 fusion.38
  56.9 3.9 %collective-permute-start.3 = (bf16[2,128,1024]{1,2,0:T(8,128)(2,1)}, bf16[2,128,1024]{1,2,0:T(8,128)(2,1)}, u32[]{:S(2)}, u32[]{:S(2)}) collective-permute-start(bf16[2,128,1024]{1,2,0:T(8,128)(2,1)} %collective-permute-done.2), channel_id=1, source_target_pairs={{0,4},{1,5},{2,6},{3,7},{4,8},{5,9},{6,10},{7,11},{8,12},{9,13},{1... | collective-permute-start | bytes 1572872 | tf_op jit(solution)/shard_map/ppermute | solution.py:17
  66.3 5.7 %collective-permute-start.1 = (bf16[2,128,1024]{1,2,0:T(8,128)(2,1)}, bf16[2,128,1024]{1,2,0:T(8,128)(2,1)}, u32[]{:S(2)}, u32[]{:S(2)}) collective-permute-start(bf16[2,128,1024]{1,2,0:T(8,128)(2,1)} %collective-permute-done), channel_id=1, source_target_pairs={{0,1},{1,2},{2,3},{3,4},{4,5},{5,6},{6,7},{7,8},{8,9},{9,10},{10,1... | collective-permute-start | bytes 1572872 | tf_op jit(solution)/shard_map/ppermute | solution.py:17
  72.1 1.9 fusion.41
  75.7 1.9 fusion.43
  79.4 1.9 fusion.35
  83.1 1.9 fusion.37
  95.0 2.3 %fusion.15 = (bf16[1,8,128,5,128]{2,4,3,1,0:T(8,128)(2,1)}, bf16[1,8,128,5,128]{2,4,3,1,0:T(8,128)(2,1)S(1)}) fusion(f32[8,128,5,128]{1,3,2,0:T(8,128)S(1)} %bitcast.330, f32[8,128]{1,0:T(8,128)S(1)} %log_add_fusion.1, pred[128,5,128]{0,2,1:T(8,128)(4,1)S(1)} %and_bitcast_fusion, f32[8,128]{1,0:T(8,128)S(1)} %log_add_fusion, f32[8,128,5,128]{1,3,2,0:T(8,128)S(1)} %bitcast.334), kind=kLoop, calls=%fused_computation.27 | loop fusion | flops 5242880 | bytes 7954432 | tf_op jit(solution)/shard_map/convert_element_type | solution.py:21
  113.3 2.5 %fusion.12 = bf16[1,8,128,5,128]{2,4,3,1,0:T(8,128)(2,1)S(1)} fusion(bf16[5,128,8,128]{1,3,0,2:T(8,128)(2,1)} %constant_dynamic-update-slice_fusion, bf16[128,8,128,1]{0,2,3,1:T(8,128)(2,1)S(1)} %bitcast.350, f32[8,128,5,128]{1,3,2,0:T(8,128)S(1)} %bitcast.331, f32[8,128]{1,0:T(8,128)S(1)} %bitcast.381, f32[8,128]{1,0:T(8,128)S(1)} %copy-done.41, ...), kind=kOutput, calls=%fused_computation.24 | convolution fusion | flops 172359680 | bytes 5595136 | tf_op jit(solution)/shard_map/bthd,bnuhd->bhtnu/dot_general | solution.py:105
  118.0 2.3 collective-permute-start.9
  120.4 2.1 collective-permute-start.10
  124.0 2.1 collective-permute-start.8
  126.9 2.7 %collective-permute-start.13 = (bf16[2,128,8,128]{1,3,2,0:T(8,128)(2,1)}, bf16[2,128,8,128]{1,3,2,0:T(8,128)(2,1)}, u32[]{:S(2)}, u32[]{:S(2)}) collective-permute-start(bf16[2,128,8,128]{1,3,2,0:T(8,128)(2,1)} %pad_maximum_fusion.13), channel_id=1, source_target_pairs={{2,0},{3,1},{4,2},{5,3},{6,4},{7,5},{8,6},{9,7},{10,8},{11,9},{12,... | collective-permute-start | bytes 1572872 | tf_op jit(solution)/shard_map/ppermute | solution.py:17
  134.6 1.9 collective-permute-start.14
  136.5 9.9 %collective-permute-done.10 = bf16[2,128,8,128]{1,3,2,0:T(8,128)(2,1)S(1)} collective-permute-done((bf16[2,128,8,128]{1,3,2,0:T(8,128)(2,1)S(1)}, bf16[2,128,8,128]{1,3,2,0:T(8,128)(2,1)S(1)}, u32[]{:S(2)}, u32[]{:S(2)}) %collective-permute-start.10) | collective-permute-done | bytes 524320 | tf_op jit(solution)/shard_map/ppermute | solution.py:17
  147.8 3.1 %collective-permute-start.12 = (bf16[2,128,8,128]{1,3,2,0:T(8,128)(2,1)}, bf16[2,128,8,128]{1,3,2,0:T(8,128)(2,1)}, u32[]{:S(2)}, u32[]{:S(2)}) collective-permute-start(bf16[2,128,8,128]{1,3,2,0:T(8,128)(2,1)} %pad_maximum_fusion.12), channel_id=1, source_target_pairs={{1,0},{2,1},{3,2},{4,3},{5,4},{6,5},{7,6},{8,7},{9,8},{10,9},{11,1... | collective-permute-start | bytes 1572872 | tf_op jit(solution)/shard_map/ppermute | solution.py:17
  151.5 23.9 %collective-permute-done.8 = bf16[2,128,8,128]{1,3,2,0:T(8,128)(2,1)S(1)} collective-permute-done((bf16[2,128,8,128]{1,3,2,0:T(8,128)(2,1)S(1)}, bf16[2,128,8,128]{1,3,2,0:T(8,128)(2,1)S(1)}, u32[]{:S(2)}, u32[]{:S(2)}) %collective-permute-start.8) | collective-permute-done | bytes 524320 | tf_op jit(solution)/shard_map/ppermute | solution.py:17
  176.0 5.2 %collective-permute-done.13 = bf16[2,128,8,128]{1,3,2,0:T(8,128)(2,1)} collective-permute-done((bf16[2,128,8,128]{1,3,2,0:T(8,128)(2,1)}, bf16[2,128,8,128]{1,3,2,0:T(8,128)(2,1)}, u32[]{:S(2)}, u32[]{:S(2)}) %collective-permute-start.13) | collective-permute-done | bytes 524320 | tf_op jit(solution)/shard_map/ppermute | solution.py:17
  181.4 41.2 %collective-permute-done.12 = bf16[2,128,8,128]{1,3,2,0:T(8,128)(2,1)} collective-permute-done((bf16[2,128,8,128]{1,3,2,0:T(8,128)(2,1)}, bf16[2,128,8,128]{1,3,2,0:T(8,128)(2,1)}, u32[]{:S(2)}, u32[]{:S(2)}) %collective-permute-start.12) | collective-permute-done | bytes 524320 | tf_op jit(solution)/shard_map/ppermute | solution.py:17
  222.6 1.9 fusion.26
  (197 shorter events, 69.5 us)
Async XLA Ops:
  5.5 13.7 %copy-start.39 = (bf16[128,2048]{1,0:T(8,128)(2,1)S(1)}, bf16[128,2048]{1,0:T(8,128)(2,1)}, u32[]{:S(2)}) copy-start(bf16[128,2048]{1,0:T(8,128)(2,1)} %param.10) | copy-start | bytes 1572868
  6.3 21.3 %collective-permute-start.6 = (bf16[2,128,1024]{1,2,0:T(8,128)(2,1)}, bf16[2,128,1024]{1,2,0:T(8,128)(2,1)}, u32[]{:S(2)}, u32[]{:S(2)}) collective-permute-start(bf16[2,128,1024]{1,2,0:T(8,128)(2,1)} %pad_maximum_fusion.5), channel_id=1, source_target_pairs={{0,4},{1,5},{2,6},{3,7},{4,8},{5,9},{6,10},{7,11},{8,12},{9,13},{1... | collective-permute-start | bytes 1572872 | tf_op jit(solution)/shard_map/ppermute | solution.py:17
  9.5 22.1 %collective-permute-start.4 = (bf16[2,128,1024]{1,2,0:T(8,128)(2,1)}, bf16[2,128,1024]{1,2,0:T(8,128)(2,1)}, u32[]{:S(2)}, u32[]{:S(2)}) collective-permute-start(bf16[2,128,1024]{1,2,0:T(8,128)(2,1)} %pad_maximum_fusion.5), channel_id=1, source_target_pairs={{0,1},{1,2},{2,3},{3,4},{4,5},{5,6},{6,7},{7,8},{8,9},{9,10},{10,1... | collective-permute-start | bytes 1572872 | tf_op jit(solution)/shard_map/ppermute | solution.py:17
  14.5 6.2 %copy-start.42 = (s32[4]{0:T(128)S(1)}, s32[4]{0:T(128)}, u32[]{:S(2)}) copy-start(s32[4]{0:T(128)} %constant.35) | copy-start | bytes 52
  14.5 28.7 %collective-permute-start.2 = (bf16[2,128,1024]{1,2,0:T(8,128)(2,1)}, bf16[2,128,1024]{1,2,0:T(8,128)(2,1)}, u32[]{:S(2)}, u32[]{:S(2)}) collective-permute-start(bf16[2,128,1024]{1,2,0:T(8,128)(2,1)} %pad_maximum_fusion.3), channel_id=1, source_target_pairs={{0,4},{1,5},{2,6},{3,7},{4,8},{5,9},{6,10},{7,11},{8,12},{9,13},{1... | collective-permute-start | bytes 1572872 | tf_op jit(solution)/shard_map/ppermute | solution.py:17
  16.6 34.5 %collective-permute-start = (bf16[2,128,1024]{1,2,0:T(8,128)(2,1)}, bf16[2,128,1024]{1,2,0:T(8,128)(2,1)}, u32[]{:S(2)}, u32[]{:S(2)}) collective-permute-start(bf16[2,128,1024]{1,2,0:T(8,128)(2,1)} %pad_maximum_fusion.3), channel_id=1, source_target_pairs={{0,1},{1,2},{2,3},{3,4},{4,5},{5,6},{6,7},{7,8},{8,9},{9,10},{10,1... | collective-permute-start | bytes 1572872 | tf_op jit(solution)/shard_map/ppermute | solution.py:17
  29.5 42.6 %collective-permute-start.7 = (bf16[2,128,1024]{1,2,0:T(8,128)(2,1)}, bf16[2,128,1024]{1,2,0:T(8,128)(2,1)}, u32[]{:S(2)}, u32[]{:S(2)}) collective-permute-start(bf16[2,128,1024]{1,2,0:T(8,128)(2,1)} %collective-permute-done.6), channel_id=1, source_target_pairs={{0,4},{1,5},{2,6},{3,7},{4,8},{5,9},{6,10},{7,11},{8,12},{9,13},{1... | collective-permute-start | bytes 1572872 | tf_op jit(solution)/shard_map/ppermute | solution.py:17
  31.6 44.1 %collective-permute-start.5 = (bf16[2,128,1024]{1,2,0:T(8,128)(2,1)}, bf16[2,128,1024]{1,2,0:T(8,128)(2,1)}, u32[]{:S(2)}, u32[]{:S(2)}) collective-permute-start(bf16[2,128,1024]{1,2,0:T(8,128)(2,1)} %collective-permute-done.4), channel_id=1, source_target_pairs={{0,1},{1,2},{2,3},{3,4},{4,5},{5,6},{6,7},{7,8},{8,9},{9,10},{10,1... | collective-permute-start | bytes 1572872 | tf_op jit(solution)/shard_map/ppermute | solution.py:17
  55.9 6.7 %copy-start.32 = (bf16[1,128,1024]{1,2,0:T(8,128)(2,1)S(1)}, bf16[1,128,1024]{1,2,0:T(8,128)(2,1)}, u32[]{:S(2)}) copy-start(bf16[1,128,1024]{1,2,0:T(8,128)(2,1)} %get-tuple-element.62) | copy-start | bytes 786436
  56.9 22.4 %collective-permute-start.3 = (bf16[2,128,1024]{1,2,0:T(8,128)(2,1)}, bf16[2,128,1024]{1,2,0:T(8,128)(2,1)}, u32[]{:S(2)}, u32[]{:S(2)}) collective-permute-start(bf16[2,128,1024]{1,2,0:T(8,128)(2,1)} %collective-permute-done.2), channel_id=1, source_target_pairs={{0,4},{1,5},{2,6},{3,7},{4,8},{5,9},{6,10},{7,11},{8,12},{9,13},{1... | collective-permute-start | bytes 1572872 | tf_op jit(solution)/shard_map/ppermute | solution.py:17
  66.3 16.7 %collective-permute-start.1 = (bf16[2,128,1024]{1,2,0:T(8,128)(2,1)}, bf16[2,128,1024]{1,2,0:T(8,128)(2,1)}, u32[]{:S(2)}, u32[]{:S(2)}) collective-permute-start(bf16[2,128,1024]{1,2,0:T(8,128)(2,1)} %collective-permute-done), channel_id=1, source_target_pairs={{0,1},{1,2},{2,3},{3,4},{4,5},{5,6},{6,7},{7,8},{8,9},{9,10},{10,1... | collective-permute-start | bytes 1572872 | tf_op jit(solution)/shard_map/ppermute | solution.py:17
  104.4 5.3 %copy-start = (bf16[1,8,128,5,128]{2,4,3,1,0:T(8,128)(2,1)S(1)}, bf16[1,8,128,5,128]{2,4,3,1,0:T(8,128)(2,1)}, u32[]{:S(2)}) copy-start(bf16[1,8,128,5,128]{2,4,3,1,0:T(8,128)(2,1)} %get-tuple-element.79) | copy-start | bytes 3932164
  118.0 6.0 %copy-start.23 = (bf16[1,128,8,128]{1,3,2,0:T(8,128)(2,1)S(1)}, bf16[1,128,8,128]{1,3,2,0:T(8,128)(2,1)}, u32[]{:S(2)}) copy-start(bf16[1,128,8,128]{1,3,2,0:T(8,128)(2,1)} %get-tuple-element.30) | copy-start | bytes 786436
  118.0 16.6 %collective-permute-start.9 = (bf16[2,128,8,128]{1,3,2,0:T(8,128)(2,1)S(1)}, bf16[2,128,8,128]{1,3,2,0:T(8,128)(2,1)S(1)}, u32[]{:S(2)}, u32[]{:S(2)}) collective-permute-start(bf16[2,128,8,128]{1,3,2,0:T(8,128)(2,1)S(1)} %pad_maximum_fusion.9), channel_id=1, source_target_pairs={{2,0},{3,1},{4,2},{5,3},{6,4},{7,5},{8,6},{9,7},{10,8},{11,9},{12,... | collective-permute-start | bytes 1572872 | tf_op jit(solution)/shard_map/ppermute | solution.py:17
  120.3 5.7 %copy-start.17 = (bf16[1,128,8,128]{1,3,2,0:T(8,128)(2,1)S(1)}, bf16[1,128,8,128]{1,3,2,0:T(8,128)(2,1)}, u32[]{:S(2)}) copy-start(bf16[1,128,8,128]{1,3,2,0:T(8,128)(2,1)} %get-tuple-element.34) | copy-start | bytes 786436
  120.3 5.7 %copy-start.21 = (bf16[1,128,8,128]{1,3,2,0:T(8,128)(2,1)S(1)}, bf16[1,128,8,128]{1,3,2,0:T(8,128)(2,1)}, u32[]{:S(2)}) copy-start(bf16[1,128,8,128]{1,3,2,0:T(8,128)(2,1)} %get-tuple-element.44) | copy-start | bytes 786436
  120.4 26.1 %collective-permute-start.10 = (bf16[2,128,8,128]{1,3,2,0:T(8,128)(2,1)S(1)}, bf16[2,128,8,128]{1,3,2,0:T(8,128)(2,1)S(1)}, u32[]{:S(2)}, u32[]{:S(2)}) collective-permute-start(bf16[2,128,8,128]{1,3,2,0:T(8,128)(2,1)S(1)} %pad_maximum_fusion.10), channel_id=1, source_target_pairs={{4,0},{5,1},{6,2},{7,3},{8,4},{9,5},{10,6},{11,7},{12,8},{13,9},{1... | collective-permute-start | bytes 1572872 | tf_op jit(solution)/shard_map/ppermute | solution.py:17
  122.5 7.2 %copy-start.30 = (bf16[128,1024]{1,0:T(8,128)(2,1)S(1)}, bf16[128,1024]{1,0:T(8,128)(2,1)}, u32[]{:S(2)}) copy-start(bf16[128,1024]{1,0:T(8,128)(2,1)} %copy.113) | copy-start | bytes 786436
  122.5 25.3 %collective-permute-start.11 = (bf16[2,128,8,128]{1,3,2,0:T(8,128)(2,1)S(1)}, bf16[2,128,8,128]{1,3,2,0:T(8,128)(2,1)S(1)}, u32[]{:S(2)}, u32[]{:S(2)}) collective-permute-start(bf16[2,128,8,128]{1,3,2,0:T(8,128)(2,1)S(1)} %pad_maximum_fusion.11), channel_id=1, source_target_pairs={{8,0},{9,1},{10,2},{11,3},{12,4},{13,5},{14,6},{15,7},{24,16},{25,... | collective-permute-start | bytes 1572872 | tf_op jit(solution)/shard_map/ppermute | solution.py:17
  124.0 6.5 %copy-start.16 = (bf16[1,128,8,128]{1,3,2,0:T(8,128)(2,1)S(1)}, bf16[1,128,8,128]{1,3,2,0:T(8,128)(2,1)}, u32[]{:S(2)}) copy-start(bf16[1,128,8,128]{1,3,2,0:T(8,128)(2,1)} %get-tuple-element.35) | copy-start | bytes 786436
  124.0 6.5 %copy-start.20 = (bf16[1,128,8,128]{1,3,2,0:T(8,128)(2,1)S(1)}, bf16[1,128,8,128]{1,3,2,0:T(8,128)(2,1)}, u32[]{:S(2)}) copy-start(bf16[1,128,8,128]{1,3,2,0:T(8,128)(2,1)} %get-tuple-element.41) | copy-start | bytes 786436
  124.0 51.4 %collective-permute-start.8 = (bf16[2,128,8,128]{1,3,2,0:T(8,128)(2,1)S(1)}, bf16[2,128,8,128]{1,3,2,0:T(8,128)(2,1)S(1)}, u32[]{:S(2)}, u32[]{:S(2)}) collective-permute-start(bf16[2,128,8,128]{1,3,2,0:T(8,128)(2,1)S(1)} %pad_maximum_fusion.8), channel_id=1, source_target_pairs={{1,0},{2,1},{3,2},{4,3},{5,4},{6,5},{7,6},{8,7},{9,8},{10,9},{11,1... | collective-permute-start | bytes 1572872 | tf_op jit(solution)/shard_map/ppermute | solution.py:17
  126.9 54.2 %collective-permute-start.13 = (bf16[2,128,8,128]{1,3,2,0:T(8,128)(2,1)}, bf16[2,128,8,128]{1,3,2,0:T(8,128)(2,1)}, u32[]{:S(2)}, u32[]{:S(2)}) collective-permute-start(bf16[2,128,8,128]{1,3,2,0:T(8,128)(2,1)} %pad_maximum_fusion.13), channel_id=1, source_target_pairs={{2,0},{3,1},{4,2},{5,3},{6,4},{7,5},{8,6},{9,7},{10,8},{11,9},{12,... | collective-permute-start | bytes 1572872 | tf_op jit(solution)/shard_map/ppermute | solution.py:17
  133.1 17.8 %copy-start.4 = (bf16[5,128,8,128]{3,1,0,2:T(8,128)(2,1)S(1)}, bf16[5,128,8,128]{3,1,0,2:T(8,128)(2,1)}, u32[]{:S(2)}) copy-start(bf16[5,128,8,128]{3,1,0,2:T(8,128)(2,1)} %copy-done.3) | copy-start | bytes 3932164
  133.1 17.8 %copy-start.8 = (bf16[1,8,128,5,128]{2,4,3,1,0:T(8,128)(2,1)S(1)}, bf16[1,8,128,5,128]{2,4,3,1,0:T(8,128)(2,1)}, u32[]{:S(2)}) copy-start(bf16[1,8,128,5,128]{2,4,3,1,0:T(8,128)(2,1)} %copy-done.7) | copy-start | bytes 3932164
  133.7 41.7 %copy-start.35 = (bf16[128,8,128]{0,2,1:T(8,128)(2,1)S(1)}, bf16[128,8,128]{0,2,1:T(8,128)(2,1)}, u32[]{:S(2)}) copy-start(bf16[128,8,128]{0,2,1:T(8,128)(2,1)} %get-tuple-element.26) | copy-start | bytes 786436
  133.7 41.7 %copy-start.36 = (bf16[128,8,128]{0,2,1:T(8,128)(2,1)S(1)}, bf16[128,8,128]{0,2,1:T(8,128)(2,1)}, u32[]{:S(2)}) copy-start(bf16[128,8,128]{0,2,1:T(8,128)(2,1)} %get-tuple-element.40) | copy-start | bytes 786436
  134.6 46.7 %collective-permute-start.14 = (bf16[2,128,8,128]{1,3,2,0:T(8,128)(2,1)}, bf16[2,128,8,128]{1,3,2,0:T(8,128)(2,1)}, u32[]{:S(2)}, u32[]{:S(2)}) collective-permute-start(bf16[2,128,8,128]{1,3,2,0:T(8,128)(2,1)} %pad_maximum_fusion.14), channel_id=1, source_target_pairs={{4,0},{5,1},{6,2},{7,3},{8,4},{9,5},{10,6},{11,7},{12,8},{13,9},{1... | collective-permute-start | bytes 1572872 | tf_op jit(solution)/shard_map/ppermute | solution.py:17
  146.5 34.9 %collective-permute-start.15 = (bf16[2,128,8,128]{1,3,2,0:T(8,128)(2,1)}, bf16[2,128,8,128]{1,3,2,0:T(8,128)(2,1)}, u32[]{:S(2)}, u32[]{:S(2)}) collective-permute-start(bf16[2,128,8,128]{1,3,2,0:T(8,128)(2,1)} %pad_maximum_fusion.15), channel_id=1, source_target_pairs={{8,0},{9,1},{10,2},{11,3},{12,4},{13,5},{14,6},{15,7},{24,16},{25,... | collective-permute-start | bytes 1572872 | tf_op jit(solution)/shard_map/ppermute | solution.py:17
  147.8 74.8 %collective-permute-start.12 = (bf16[2,128,8,128]{1,3,2,0:T(8,128)(2,1)}, bf16[2,128,8,128]{1,3,2,0:T(8,128)(2,1)}, u32[]{:S(2)}, u32[]{:S(2)}) collective-permute-start(bf16[2,128,8,128]{1,3,2,0:T(8,128)(2,1)} %pad_maximum_fusion.12), channel_id=1, source_target_pairs={{1,0},{2,1},{3,2},{4,3},{5,4},{6,5},{7,6},{8,7},{9,8},{10,9},{11,1... | collective-permute-start | bytes 1572872 | tf_op jit(solution)/shard_map/ppermute | solution.py:17
  151.4 71.1 %copy-start.33 = (bf16[128,8,128]{0,2,1:T(8,128)(2,1)S(1)}, bf16[128,8,128]{0,2,1:T(8,128)(2,1)}, u32[]{:S(2)}) copy-start(bf16[128,8,128]{0,2,1:T(8,128)(2,1)} %get-tuple-element.31) | copy-start | bytes 786436
  151.5 71.1 %copy-start.34 = (bf16[128,8,128]{0,2,1:T(8,128)(2,1)S(1)}, bf16[128,8,128]{0,2,1:T(8,128)(2,1)}, u32[]{:S(2)}) copy-start(bf16[128,8,128]{0,2,1:T(8,128)(2,1)} %get-tuple-element.45) | copy-start | bytes 786436
  (27 other events, 57.5 us)

commit v17 on v8

--- a/solution.py
+++ b/solution.py
@@ -116,7 +116,7 @@
         ref[1] = value_terms[slot * rows : (slot + 1) * rows].astype(jnp.bfloat16)
 
 
-def attend_chunk(query_c, received, grad_c, allowed, offsets, heads):
+def attend_chunk_kernel(query_c, received, grad_c, allowed, offsets, heads):
     rows, width = query_c.shape
     slots = len(received)
     mask = jnp.where(allowed, 1.0, 0.0).astype(jnp.float32).reshape(rows, slots * rows)
@@ -138,6 +138,50 @@
     output, query_grad = results[0], results[1]
     own = (results[2][0], results[2][1])
     outgoing = list(results[3:])
+    return output, query_grad, own, outgoing
+
+
+def attend_chunk(query_c, received, grad_c, allowed, offsets, heads):
+    scale_factor = 1.0 / math.sqrt(HEAD_DIM)
+    rows = query_c.shape[0]
+    head_shape = (rows, heads, HEAD_DIM)
+    key_stack = jnp.stack([moved[0].reshape(head_shape) for moved in received])[None]
+    value_stack = jnp.stack([moved[1].reshape(head_shape) for moved in received])[None]
+    query_stack = query_c.reshape((1,) + head_shape)
+    grad_stack = grad_c.reshape((1,) + head_shape)
+    raw_scores = (
+        jnp.einsum("bthd,bnuhd->bhtnu", query_stack, key_stack, preferred_element_type=jnp.float32)
+        * scale_factor
+    )
+    scores = jnp.where(allowed, raw_scores, -1e30)
+    row_peak = jnp.max(scores, axis=(3, 4), keepdims=True)
+    summed = jnp.sum(jnp.exp(scores - row_peak), axis=(3, 4), keepdims=True)
+    log_total = row_peak + jnp.log(summed)
+    weights32 = jnp.exp(scores - log_total)
+    weights = rounded(weights32)
+    output = rounded(
+        jnp.einsum("bhtnu,bnuhd->bthd", weights, value_stack, preferred_element_type=jnp.float32)
+    )
+    grad_probs = jnp.einsum(
+        "bthd,bnuhd->bhtnu", grad_stack, value_stack, preferred_element_type=jnp.float32
+    )
+    delta_rows = jnp.sum(grad_stack.astype(jnp.float32) * output.astype(jnp.float32), axis=-1)
+    delta_rows = jnp.transpose(delta_rows, (0, 2, 1))[:, :, :, None, None]
+    grad_scores = rounded(weights32 * (grad_probs - delta_rows) * scale_factor)
+    query_grad = jnp.einsum(
+        "bhtnu,bnuhd->bthd", grad_scores, key_stack, preferred_element_type=jnp.float32
+    )
+    key_terms = jnp.einsum(
+        "bhtnu,bthd->bnuhd", grad_scores, query_stack, preferred_element_type=jnp.float32
+    )
+    value_terms = jnp.einsum(
+        "bhtnu,bthd->bnuhd", weights, grad_stack, preferred_element_type=jnp.float32
+    )
+    own = (rounded(key_terms[0, 0]), rounded(value_terms[0, 0]))
+    outgoing = [
+        jnp.stack([key_terms[0, slot_index], value_terms[0, slot_index]]).astype(jnp.bfloat16)
+        for slot_index in range(1, len(offsets) + 1)
+    ]
     return output, query_grad, own, outgoing
 
 
@@ -175,7 +219,8 @@
         if pending:
             key_c, value_c, _ = lax.optimization_barrier((key_c, value_c, pieces[-1][0]))
         received = send_chunk(key_c, value_c, offsets)
-        output, query_grad, own, outgoing = attend_chunk(
+        attend = attend_chunk_kernel if chunk == CHUNKS - 1 else attend_chunk
+        output, query_grad, own, outgoing = attend(
             query_rot[:, cols], received, grad_out[:, cols], allowed, offsets, chunk_heads
         )
         pending.append(outgoing)

time: 196 us -> 201 us (1.026)
  waiting for transfers between devices: 107 us -> 80.5 us
  local copies, waits for them, and re-layouts: 12.7 us -> 30.7 us
  Pallas kernels: 20.3 us -> 10.2 us
  starting transfers between devices: 44.3 us -> 54.1 us
  other arithmetic: 7.58 us -> 14.9 us
  matrix products: 0 us -> 6.7 us
    ppermute x16, waiting for transfers between devices: 107 us -> 80.5 us  [from_behind(): lax.ppermute(value, axis, [(source, source + steps) for source in range(l...]
    pallas_call x2 -> x1, Pallas kernels: 20.3 us -> 10.2 us  [attend_chunk_kernel(): pl.pallas_call(attention_kernel, grid=(heads,), in_specs=[flat_spec, flat...]
    ppermute x16, starting transfers between devices: 44.3 us -> 54.1 us  [from_behind(): lax.ppermute(value, axis, [(source, source + steps) for source in range(l...]
    unnamed x48 -> x83, local copies, waits for them, and re-layouts: 8.77 us -> 17 us
    another operation x1 -> x10, local copies, waits for them, and re-layouts: 0.1 us -> 7.09 us  [the longest x6 5.26 us: attend_chunk(): jnp.stack([moved[1].reshape(head_shape) for moved in received])[None]]
    dot_general x0 -> x5, matrix products: none -> 4.9 us  [the longest x1 2.02 us: attend_chunk(): jnp.einsum('bhtnu,bthd->bnuhd', weights, grad_stack, preferred_element_ty...]
    another operation x6 -> x10, other arithmetic: 3.74 us -> 8.32 us
  transfers between devices with their start and end apart: 16 -> 16, of which waited for: 9 -> 5; matrix products, arithmetic and copies ran while one was open for 3% -> 13% of each run, Pallas kernels for 5% -> 5%
where the time goes in v17:
time: 201 us; the launch traced here: 199 us
  waiting for transfers between devices  80.5 us (40%)
  starting transfers between devices  54.1 us (27%)
  local copies, waits for them, and re-layouts  30.7 us (15%)
  other arithmetic  14.9 us (7%)
  Pallas kernels  10.2 us (5%)
  matrix products  6.7 us (3%)
  between operations  2.05 us (1%)
    ppermute x16, waiting for transfers between devices, from_behind(): lax.ppermute(value, axis, [(source, source + steps) for source in range(l...  80.5 us
    ppermute x16, starting transfers between devices, from_behind(): lax.ppermute(value, axis, [(source, source + steps) for source in range(l...  54.1 us
    unnamed x83, local copies, waits for them, and re-layouts  17 us
    pallas_call x1, Pallas kernels, attend_chunk_kernel(): pl.pallas_call(attention_kernel, grid=(heads,), in_specs=[flat_spec, flat...  10.2 us
    another operation x6, local copies, waits for them, and re-layouts, attend_chunk(): jnp.stack([moved[1].reshape(head_shape) for moved in received])[None]  5.26 us
    another operation x6, other arithmetic  4.88 us
  transfers between devices with their start and end apart: 16, of which 5 were waited for; matrix products, arithmetic and copies ran while one was open for 13% of the time, Pallas kernels for 5%

profile of v17, /device:TPU:0, one launch (start us, length us, event | category | flops | bytes accessed | tf_op | source)
XLA Modules:
  0.0 199.2 jit_solution(12549982471268085604)
XLA Ops:
  2.5 1.9 slice_bitcast_fusion.24
  7.3 5.7 %collective-permute-start.2 = (bf16[2,128,1024]{2,1,0:T(8,128)(2,1)}, bf16[2,128,1024]{2,1,0:T(8,128)(2,1)}, u32[]{:S(2)}, u32[]{:S(2)}) collective-permute-start(bf16[2,128,1024]{2,1,0:T(8,128)(2,1)} %pad_maximum_fusion.3), channel_id=1, source_target_pairs={{0,4},{1,5},{2,6},{3,7},{4,8},{5,9},{6,10},{7,11},{8,12},{9,13},{1... | collective-permute-start | bytes 1572872 | tf_op jit(solution)/shard_map/ppermute | solution.py:18
  13.0 2.3 %collective-permute-start = (bf16[2,128,1024]{2,1,0:T(8,128)(2,1)}, bf16[2,128,1024]{2,1,0:T(8,128)(2,1)}, u32[]{:S(2)}, u32[]{:S(2)}) collective-permute-start(bf16[2,128,1024]{2,1,0:T(8,128)(2,1)} %pad_maximum_fusion.3), channel_id=1, source_target_pairs={{0,1},{1,2},{2,3},{3,4},{4,5},{5,6},{6,7},{7,8},{8,9},{9,10},{10,1... | collective-permute-start | bytes 1572872 | tf_op jit(solution)/shard_map/ppermute | solution.py:18
  18.9 1.8 slice_bitcast_fusion.21
  21.9 6.8 %collective-permute-start.1 = (bf16[2,128,1024]{2,1,0:T(8,128)(2,1)}, bf16[2,128,1024]{2,1,0:T(8,128)(2,1)}, u32[]{:S(2)}, u32[]{:S(2)}) collective-permute-start(bf16[2,128,1024]{2,1,0:T(8,128)(2,1)} %collective-permute-done), channel_id=1, source_target_pairs={{0,1},{1,2},{2,3},{3,4},{4,5},{5,6},{6,7},{7,8},{8,9},{9,10},{10,1... | collective-permute-start | bytes 1572872 | tf_op jit(solution)/shard_map/ppermute | solution.py:18
  28.7 11.7 %collective-permute-start.3 = (bf16[2,128,1024]{2,1,0:T(8,128)(2,1)}, bf16[2,128,1024]{2,1,0:T(8,128)(2,1)}, u32[]{:S(2)}, u32[]{:S(2)}) collective-permute-start(bf16[2,128,1024]{2,1,0:T(8,128)(2,1)} %collective-permute-done.2), channel_id=1, source_target_pairs={{0,4},{1,5},{2,6},{3,7},{4,8},{5,9},{6,10},{7,11},{8,12},{9,13},{1... | collective-permute-start | bytes 1572872 | tf_op jit(solution)/shard_map/ppermute | solution.py:18
  40.4 1.8 slice_bitcast_fusion.19
  42.3 1.3 copy.127
  44.6 2.0 collective-permute-done.3
  46.6 1.8 slice_bitcast_fusion.18
  48.4 1.8 copy.128
  53.5 1.8 fusion.22
  60.7 4.4 %collective-permute-start.6 = (bf16[2,128,1024]{2,1,0:T(8,128)(2,1)S(1)}, bf16[2,128,1024]{2,1,0:T(8,128)(2,1)S(1)}, u32[]{:S(2)}, u32[]{:S(2)}) collective-permute-start(bf16[2,128,1024]{2,1,0:T(8,128)(2,1)S(1)} %pad_maximum_fusion.5.refs_3_), channel_id=1, source_target_pairs={{0,4},{1,5},{2,6},{3,7},{4,8},{5,9},{6,10},{7,11},{8,12},{9,13},{1... | collective-permute-start | bytes 1572872 | tf_op jit(solution)/shard_map/ppermute | solution.py:18
  65.2 2.2 %collective-permute-start.4 = (bf16[2,128,1024]{2,1,0:T(8,128)(2,1)S(1)}, bf16[2,128,1024]{2,1,0:T(8,128)(2,1)}, u32[]{:S(2)}, u32[]{:S(2)}) collective-permute-start(bf16[2,128,1024]{2,1,0:T(8,128)(2,1)S(1)} %pad_maximum_fusion.5.refs_3_), channel_id=1, source_target_pairs={{0,1},{1,2},{2,3},{3,4},{4,5},{5,6},{6,7},{7,8},{8,9},{9,10},{10,1... | collective-permute-start | bytes 1572872 | tf_op jit(solution)/shard_map/ppermute | solution.py:18
  67.3 2.0 %fusion.5 = bf16[1,5,128,8,128]{2,4,3,1,0:T(8,128)(2,1)S(1)} fusion(bf16[128,8,128,1]{0,2,1,3:T(8,128)(2,1)S(1)} %bitcast.206, bf16[1,8,128,5,128]{2,4,3,1,0:T(8,128)(2,1)} %copy-done), kind=kOutput, calls=%fused_computation.11 | convolution fusion | flops 168427520 | bytes 2883584 | tf_op jit(solution)/shard_map/bhtnu,bthd->bnuhd/dot_general | solution.py:177
  73.2 3.3 %collective-permute-start.7 = (bf16[2,128,1024]{2,1,0:T(8,128)(2,1)S(1)}, bf16[2,128,1024]{2,1,0:T(8,128)(2,1)S(1)}, u32[]{:S(2)}, u32[]{:S(2)}) collective-permute-start(bf16[2,128,1024]{2,1,0:T(8,128)(2,1)S(1)} %collective-permute-done.6.refs_6_), channel_id=1, source_target_pairs={{0,4},{1,5},{2,6},{3,7},{4,8},{5,9},{6,10},{7,11},{8,12},{9,13},{1... | collective-permute-start | bytes 1572872 | tf_op jit(solution)/shard_map/ppermute | solution.py:18
  77.3 1.3 collective-permute-start.9
  79.4 1.4 collective-permute-start.10
  80.9 7.1 %collective-permute-start.5 = (bf16[2,128,1024]{2,1,0:T(8,128)(2,1)}, bf16[2,128,1024]{2,1,0:T(8,128)(2,1)S(1)}, u32[]{:S(2)}, u32[]{:S(2)}) collective-permute-start(bf16[2,128,1024]{2,1,0:T(8,128)(2,1)} %collective-permute-done.4.refs_4_), channel_id=1, source_target_pairs={{0,1},{1,2},{2,3},{3,4},{4,5},{5,6},{6,7},{7,8},{8,9},{9,10},{10,1... | collective-permute-start | bytes 1572872 | tf_op jit(solution)/shard_map/ppermute | solution.py:18
  88.8 1.3 collective-permute-start.11
  91.8 1.3 collective-permute-start.8
  94.9 10.2 %shard_map.102 = (bf16[128,1024]{1,0:T(8,128)(2,1)}, f32[128,1024]{1,0:T(8,128)}, bf16[2,128,1024]{2,1,0:T(8,128)(2,1)}, bf16[2,128,1024]{2,1,0:T(8,128)(2,1)}, ...) custom-call(bf16[128,1024]{1,0:T(8,128)(2,1)} %get-tuple-element.59.refs_0_, ...), custom_call_target="tpu_custom_call" | custom-call | tf_op jit(solution)/shard_map/pallas_call | solution.py:127
  105.2 1.3 collective-permute-start.12
  106.5 1.3 collective-permute-start.13
  107.8 6.6 %collective-permute-done.10 = bf16[2,128,8,128]{1,3,2,0:T(8,128)(2,1)} collective-permute-done((bf16[2,128,8,128]{1,3,2,0:T(8,128)(2,1)}, bf16[2,128,8,128]{1,3,2,0:T(8,128)(2,1)}, u32[]{:S(2)}, u32[]{:S(2)}) %collective-permute-start.10) | collective-permute-done | bytes 524320 | tf_op jit(solution)/shard_map/ppermute | solution.py:18
  114.3 1.3 collective-permute-start.14
  115.6 21.6 %collective-permute-done.11 = bf16[2,128,8,128]{1,3,2,0:T(8,128)(2,1)} collective-permute-done((bf16[2,128,8,128]{1,3,2,0:T(8,128)(2,1)}, bf16[2,128,8,128]{1,3,2,0:T(8,128)(2,1)}, u32[]{:S(2)}, u32[]{:S(2)}) %collective-permute-start.11) | collective-permute-done | bytes 524320 | tf_op jit(solution)/shard_map/ppermute | solution.py:18
  137.2 1.6 collective-permute-start.15
  139.4 2.0 fusion.14
  143.3 18.1 %collective-permute-done.14 = bf16[2,128,1024]{2,1,0:T(8,128)(2,1)} collective-permute-done((bf16[2,128,1024]{2,1,0:T(8,128)(2,1)}, bf16[2,128,1024]{2,1,0:T(8,128)(2,1)}, u32[]{:S(2)}, u32[]{:S(2)}) %collective-permute-start.14) | collective-permute-done | bytes 524320 | tf_op jit(solution)/shard_map/ppermute | solution.py:18
  161.4 32.2 %collective-permute-done.15 = bf16[2,128,1024]{2,1,0:T(8,128)(2,1)} collective-permute-done((bf16[2,128,1024]{2,1,0:T(8,128)(2,1)}, bf16[2,128,1024]{2,1,0:T(8,128)(2,1)}, u32[]{:S(2)}, u32[]{:S(2)}) %collective-permute-start.15) | collective-permute-done | bytes 524320 | tf_op jit(solution)/shard_map/ppermute | solution.py:18
  193.6 2.1 %fusion.17 = (bf16[128,1024]{1,0:T(8,128)(2,1)S(1)}, f32[1,128,1024]{2,1,0:T(8,128)S(1)}) fusion(bf16[2,128,1024]{2,1,0:T(8,128)(2,1)} %collective-permute-done.15, bf16[2,128,1024]{2,1,0:T(8,128)(2,1)} %collective-permute-done.14, bf16[2,128,1024]{2,1,0:T(8,128)(2,1)} %collective-permute-done.13, bf16[2,128,1024]{2,1,0:T(8,128)(2,1)} %collective-permute-done.12, ...), kind=kLoop, calls=%fused_computation.64 | loop fusion | flops 2490368 | bytes 3407872 | tf_op jit(solution)/shard_map/convert.14
  (147 shorter events, 33.9 us)
Async XLA Ops:
  0.6 3.7 %copy-start.16 = (bf16[128,2048]{1,0:T(8,128)(2,1)S(1)}, bf16[128,2048]{1,0:T(8,128)(2,1)}, u32[]{:S(2)}) copy-start(bf16[128,2048]{1,0:T(8,128)(2,1)} %param.7) | copy-start | bytes 1572868
  5.6 10.4 %copy-start.18 = (bf16[128,2048]{1,0:T(8,128)(2,1)S(1)}, bf16[128,2048]{1,0:T(8,128)(2,1)}, u32[]{:S(2)}) copy-start(bf16[128,2048]{1,0:T(8,128)(2,1)} %param.10) | copy-start | bytes 1572868
  7.3 21.4 %collective-permute-start.2 = (bf16[2,128,1024]{2,1,0:T(8,128)(2,1)}, bf16[2,128,1024]{2,1,0:T(8,128)(2,1)}, u32[]{:S(2)}, u32[]{:S(2)}) collective-permute-start(bf16[2,128,1024]{2,1,0:T(8,128)(2,1)} %pad_maximum_fusion.3), channel_id=1, source_target_pairs={{0,4},{1,5},{2,6},{3,7},{4,8},{5,9},{6,10},{7,11},{8,12},{9,13},{1... | collective-permute-start | bytes 1572872 | tf_op jit(solution)/shard_map/ppermute | solution.py:18
  13.0 5.9 %collective-permute-start = (bf16[2,128,1024]{2,1,0:T(8,128)(2,1)}, bf16[2,128,1024]{2,1,0:T(8,128)(2,1)}, u32[]{:S(2)}, u32[]{:S(2)}) collective-permute-start(bf16[2,128,1024]{2,1,0:T(8,128)(2,1)} %pad_maximum_fusion.3), channel_id=1, source_target_pairs={{0,1},{1,2},{2,3},{3,4},{4,5},{5,6},{6,7},{7,8},{8,9},{9,10},{10,1... | collective-permute-start | bytes 1572872 | tf_op jit(solution)/shard_map/ppermute | solution.py:18
  15.3 2.7 %copy-start.28 = (pred[5]{0:T(512)(128)(4,1)}, pred[5]{0:T(512)(128)(4,1)S(1)}, u32[]{:S(2)}) copy-start(pred[5]{0:T(512)(128)(4,1)S(1)} %iota_compare_fusion.1) | copy-start | bytes 19
  15.3 2.7 %copy-start.24 = (pred[128,128]{0,1:T(8,128)(4,1)}, pred[128,128]{0,1:T(8,128)(4,1)S(1)}, u32[]{:S(2)}) copy-start(pred[128,128]{0,1:T(8,128)(4,1)S(1)} %iota_compare_fusion) | copy-start | bytes 49156
  21.9 28.3 %collective-permute-start.1 = (bf16[2,128,1024]{2,1,0:T(8,128)(2,1)}, bf16[2,128,1024]{2,1,0:T(8,128)(2,1)}, u32[]{:S(2)}, u32[]{:S(2)}) collective-permute-start(bf16[2,128,1024]{2,1,0:T(8,128)(2,1)} %collective-permute-done), channel_id=1, source_target_pairs={{0,1},{1,2},{2,3},{3,4},{4,5},{5,6},{6,7},{7,8},{8,9},{9,10},{10,1... | collective-permute-start | bytes 1572872 | tf_op jit(solution)/shard_map/ppermute | solution.py:18
  28.7 17.9 %collective-permute-start.3 = (bf16[2,128,1024]{2,1,0:T(8,128)(2,1)}, bf16[2,128,1024]{2,1,0:T(8,128)(2,1)}, u32[]{:S(2)}, u32[]{:S(2)}) collective-permute-start(bf16[2,128,1024]{2,1,0:T(8,128)(2,1)} %collective-permute-done.2), channel_id=1, source_target_pairs={{0,4},{1,5},{2,6},{3,7},{4,8},{5,9},{6,10},{7,11},{8,12},{9,13},{1... | collective-permute-start | bytes 1572872 | tf_op jit(solution)/shard_map/ppermute | solution.py:18
  42.3 7.9 %copy-start.6 = (bf16[5,128,8,128]{1,3,0,2:T(8,128)(2,1)}, bf16[5,128,8,128]{1,3,0,2:T(8,128)(2,1)S(1)}, u32[]{:S(2)}) copy-start(bf16[5,128,8,128]{1,3,0,2:T(8,128)(2,1)S(1)} %constant_dynamic-update-slice_fusion.3) | copy-start | bytes 3932164
  60.7 8.6 %copy-start.5 = (bf16[2,128,1024]{2,1,0:T(8,128)(2,1)}, bf16[2,128,1024]{2,1,0:T(8,128)(2,1)S(1)}, u32[]{:S(2)}) copy-start(bf16[2,128,1024]{2,1,0:T(8,128)(2,1)S(1)} %pad_maximum_fusion.5.refs_3_) | copy-start | bytes 1572868
  60.7 12.4 %collective-permute-start.6 = (bf16[2,128,1024]{2,1,0:T(8,128)(2,1)S(1)}, bf16[2,128,1024]{2,1,0:T(8,128)(2,1)S(1)}, u32[]{:S(2)}, u32[]{:S(2)}) collective-permute-start(bf16[2,128,1024]{2,1,0:T(8,128)(2,1)S(1)} %pad_maximum_fusion.5.refs_3_), channel_id=1, source_target_pairs={{0,4},{1,5},{2,6},{3,7},{4,8},{5,9},{6,10},{7,11},{8,12},{9,13},{1... | collective-permute-start | bytes 1572872 | tf_op jit(solution)/shard_map/ppermute | solution.py:18
  65.2 15.7 %collective-permute-start.4 = (bf16[2,128,1024]{2,1,0:T(8,128)(2,1)S(1)}, bf16[2,128,1024]{2,1,0:T(8,128)(2,1)}, u32[]{:S(2)}, u32[]{:S(2)}) collective-permute-start(bf16[2,128,1024]{2,1,0:T(8,128)(2,1)S(1)} %pad_maximum_fusion.5.refs_3_), channel_id=1, source_target_pairs={{0,1},{1,2},{2,3},{3,4},{4,5},{5,6},{6,7},{7,8},{8,9},{9,10},{10,1... | collective-permute-start | bytes 1572872 | tf_op jit(solution)/shard_map/ppermute | solution.py:18
  67.3 2.1 %copy-start.9 = (bf16[5,128,8,128]{1,3,0,2:T(8,128)(2,1)S(1)}, bf16[5,128,8,128]{1,3,0,2:T(8,128)(2,1)}, u32[]{:S(2)}) copy-start(bf16[5,128,8,128]{1,3,0,2:T(8,128)(2,1)} %copy-done.8) | copy-start | bytes 3932164
  67.3 2.1 %copy-start.27 = (f32[8,128]{1,0:T(8,128)S(1)}, f32[8,128]{1,0:T(8,128)}, u32[]{:S(2)}) copy-start(f32[8,128]{1,0:T(8,128)} %copy-done.26) | copy-start | bytes 12292
  73.2 15.7 %copy-start.20 = (bf16[2,128,1024]{2,1,0:T(8,128)(2,1)}, bf16[2,128,1024]{2,1,0:T(8,128)(2,1)S(1)}, u32[]{:S(2)}) copy-start(bf16[2,128,1024]{2,1,0:T(8,128)(2,1)S(1)} %collective-permute-done.6.refs_6_) | copy-start | bytes 1572868
  73.2 17.9 %collective-permute-start.7 = (bf16[2,128,1024]{2,1,0:T(8,128)(2,1)S(1)}, bf16[2,128,1024]{2,1,0:T(8,128)(2,1)S(1)}, u32[]{:S(2)}, u32[]{:S(2)}) collective-permute-start(bf16[2,128,1024]{2,1,0:T(8,128)(2,1)S(1)} %collective-permute-done.6.refs_6_), channel_id=1, source_target_pairs={{0,4},{1,5},{2,6},{3,7},{4,8},{5,9},{6,10},{7,11},{8,12},{9,13},{1... | collective-permute-start | bytes 1572872 | tf_op jit(solution)/shard_map/ppermute | solution.py:18
  77.3 29.2 %collective-permute-start.9 = (bf16[2,128,8,128]{1,3,2,0:T(8,128)(2,1)}, bf16[2,128,8,128]{1,3,2,0:T(8,128)(2,1)}, u32[]{:S(2)}, u32[]{:S(2)}) collective-permute-start(bf16[2,128,8,128]{1,3,2,0:T(8,128)(2,1)} %pad_maximum_fusion.9), channel_id=1, source_target_pairs={{2,0},{3,1},{4,2},{5,3},{6,4},{7,5},{8,6},{9,7},{10,8},{11,9},{12,... | collective-permute-start | bytes 1572872 | tf_op jit(solution)/shard_map/ppermute | solution.py:18
  79.4 13.7 %copy-start.25 = (pred[128,128]{0,1:T(8,128)(4,1)S(1)}, pred[128,128]{0,1:T(8,128)(4,1)}, u32[]{:S(2)}) copy-start(pred[128,128]{0,1:T(8,128)(4,1)} %copy-done.24) | copy-start | bytes 49156
  79.4 13.7 %copy-start.29 = (pred[5]{0:T(512)(128)(4,1)S(1)}, pred[5]{0:T(512)(128)(4,1)}, u32[]{:S(2)}) copy-start(pred[5]{0:T(512)(128)(4,1)} %copy-done.28) | copy-start | bytes 19
  79.4 13.7 %copy-start.31 = (pred[5]{0:T(512)(128)(4,1)S(1)}, pred[5]{0:T(512)(128)(4,1)}, u32[]{:S(2)}) copy-start(pred[5]{0:T(512)(128)(4,1)} %copy-done.30) | copy-start | bytes 19
  79.4 34.9 %collective-permute-start.10 = (bf16[2,128,8,128]{1,3,2,0:T(8,128)(2,1)}, bf16[2,128,8,128]{1,3,2,0:T(8,128)(2,1)}, u32[]{:S(2)}, u32[]{:S(2)}) collective-permute-start(bf16[2,128,8,128]{1,3,2,0:T(8,128)(2,1)} %pad_maximum_fusion.10), channel_id=1, source_target_pairs={{4,0},{5,1},{6,2},{7,3},{8,4},{9,5},{10,6},{11,7},{12,8},{13,9},{1... | collective-permute-start | bytes 1572872 | tf_op jit(solution)/shard_map/ppermute | solution.py:18
  80.9 13.3 %collective-permute-start.5 = (bf16[2,128,1024]{2,1,0:T(8,128)(2,1)}, bf16[2,128,1024]{2,1,0:T(8,128)(2,1)S(1)}, u32[]{:S(2)}, u32[]{:S(2)}) collective-permute-start(bf16[2,128,1024]{2,1,0:T(8,128)(2,1)} %collective-permute-done.4.refs_4_), channel_id=1, source_target_pairs={{0,1},{1,2},{2,3},{3,4},{4,5},{5,6},{6,7},{7,8},{8,9},{9,10},{10,1... | collective-permute-start | bytes 1572872 | tf_op jit(solution)/shard_map/ppermute | solution.py:18
  88.8 48.4 %collective-permute-start.11 = (bf16[2,128,8,128]{1,3,2,0:T(8,128)(2,1)}, bf16[2,128,8,128]{1,3,2,0:T(8,128)(2,1)}, u32[]{:S(2)}, u32[]{:S(2)}) collective-permute-start(bf16[2,128,8,128]{1,3,2,0:T(8,128)(2,1)} %pad_maximum_fusion.11), channel_id=1, source_target_pairs={{8,0},{9,1},{10,2},{11,3},{12,4},{13,5},{14,6},{15,7},{24,16},{25,... | collective-permute-start | bytes 1572872 | tf_op jit(solution)/shard_map/ppermute | solution.py:18
  91.8 47.6 %collective-permute-start.8 = (bf16[2,128,8,128]{1,3,2,0:T(8,128)(2,1)}, bf16[2,128,8,128]{1,3,2,0:T(8,128)(2,1)}, u32[]{:S(2)}, u32[]{:S(2)}) collective-permute-start(bf16[2,128,8,128]{1,3,2,0:T(8,128)(2,1)} %pad_maximum_fusion.8), channel_id=1, source_target_pairs={{1,0},{2,1},{3,2},{4,3},{5,4},{6,5},{7,6},{8,7},{9,8},{10,9},{11,1... | collective-permute-start | bytes 1572872 | tf_op jit(solution)/shard_map/ppermute | solution.py:18
  94.9 43.9 %copy-start.2 = (bf16[5,128,8,128]{3,1,0,2:T(8,128)(2,1)S(1)}, bf16[5,128,8,128]{3,1,0,2:T(8,128)(2,1)}, u32[]{:S(2)}) copy-start(bf16[5,128,8,128]{3,1,0,2:T(8,128)(2,1)} %copy-done.1) | copy-start | bytes 3932164
  94.9 43.9 %copy-start.4 = (bf16[1,8,128,5,128]{2,4,3,1,0:T(8,128)(2,1)S(1)}, bf16[1,8,128,5,128]{2,4,3,1,0:T(8,128)(2,1)}, u32[]{:S(2)}) copy-start(bf16[1,8,128,5,128]{2,4,3,1,0:T(8,128)(2,1)} %copy-done.3) | copy-start | bytes 3932164
  105.2 38.1 %collective-permute-start.12 = (bf16[2,128,1024]{2,1,0:T(8,128)(2,1)}, bf16[2,128,1024]{2,1,0:T(8,128)(2,1)}, u32[]{:S(2)}, u32[]{:S(2)}) collective-permute-start(bf16[2,128,1024]{2,1,0:T(8,128)(2,1)} %get-tuple-element.18), channel_id=1, source_target_pairs={{1,0},{2,1},{3,2},{4,3},{5,4},{6,5},{7,6},{8,7},{9,8},{10,9},{11,1... | collective-permute-start | bytes 1572872 | tf_op jit(solution)/shard_map/ppermute | solution.py:18
  106.5 36.8 %collective-permute-start.13 = (bf16[2,128,1024]{2,1,0:T(8,128)(2,1)}, bf16[2,128,1024]{2,1,0:T(8,128)(2,1)}, u32[]{:S(2)}, u32[]{:S(2)}) collective-permute-start(bf16[2,128,1024]{2,1,0:T(8,128)(2,1)} %get-tuple-element.19), channel_id=1, source_target_pairs={{2,0},{3,1},{4,2},{5,3},{6,4},{7,5},{8,6},{9,7},{10,8},{11,9},{12,... | collective-permute-start | bytes 1572872 | tf_op jit(solution)/shard_map/ppermute | solution.py:18
  114.3 47.1 %collective-permute-start.14 = (bf16[2,128,1024]{2,1,0:T(8,128)(2,1)}, bf16[2,128,1024]{2,1,0:T(8,128)(2,1)}, u32[]{:S(2)}, u32[]{:S(2)}) collective-permute-start(bf16[2,128,1024]{2,1,0:T(8,128)(2,1)} %get-tuple-element.20), channel_id=1, source_target_pairs={{4,0},{5,1},{6,2},{7,3},{8,4},{9,5},{10,6},{11,7},{12,8},{13,9},{1... | collective-permute-start | bytes 1572872 | tf_op jit(solution)/shard_map/ppermute | solution.py:18
  137.2 2.2 %copy-start.15 = (bf16[128,8,128]{0,2,1:T(8,128)(2,1)S(1)}, bf16[128,8,128]{0,2,1:T(8,128)(2,1)}, u32[]{:S(2)}) copy-start(bf16[128,8,128]{0,2,1:T(8,128)(2,1)} %get-tuple-element.47) | copy-start | bytes 786436
  137.2 56.4 %collective-permute-start.15 = (bf16[2,128,1024]{2,1,0:T(8,128)(2,1)}, bf16[2,128,1024]{2,1,0:T(8,128)(2,1)}, u32[]{:S(2)}, u32[]{:S(2)}) collective-permute-start(bf16[2,128,1024]{2,1,0:T(8,128)(2,1)} %get-tuple-element.21), channel_id=1, source_target_pairs={{8,0},{9,1},{10,2},{11,3},{12,4},{13,5},{14,6},{15,7},{24,16},{25,... | collective-permute-start | bytes 1572872 | tf_op jit(solution)/shard_map/ppermute | solution.py:18
  139.4 2.2 %copy-start.19 = (f32[128,1024]{1,0:T(8,128)S(1)}, f32[128,1024]{1,0:T(8,128)}, u32[]{:S(2)}) copy-start(f32[128,1024]{1,0:T(8,128)} %get-tuple-element.16) | copy-start | bytes 1572868
  (17 other events, 20.8 us)

commit v18 on v6

--- a/solution.py
+++ b/solution.py
@@ -69,11 +69,11 @@
     return jnp.transpose(allowed, (0, 2, 1, 3))[:, None]
 
 
-def send_chunk(key_c, value_c, offsets):
+def send_chunk(key_c, value_c, offsets, relay):
     pair = jnp.stack([key_c, value_c])
     received = {0: pair}
     for offset in offsets:
-        if (offset.bit_length() - 1) % 2 == 1:
+        if relay and (offset.bit_length() - 1) % 2 == 1:
             half = offset // 2
             received[offset] = from_behind(received[half], "ctx", half)
         else:
@@ -158,7 +158,7 @@
         key_c, value_c = key_rot[:, cols], values[:, cols]
         if pending:
             key_c, value_c, _ = lax.optimization_barrier((key_c, value_c, pieces[-1][0]))
-        received = send_chunk(key_c, value_c, offsets)
+        received = send_chunk(key_c, value_c, offsets, relay=not pending)
         output, query_grad, own, outgoing = attend_chunk(
             query_rot[:, cols], received, grad_out[:, cols], allowed, offsets, chunk_heads
         )

time: 186 us -> 184 us (0.989)
  local copies, waits for them, and re-layouts: 53.2 us -> 41.2 us
  waiting for transfers between devices: 46.5 us -> 54.7 us
  starting transfers between devices: 48.2 us -> 53.7 us
  other arithmetic: 23.8 us -> 21.8 us
    ppermute x16, waiting for transfers between devices: 46.5 us -> 54.7 us  [from_behind(): lax.ppermute(value, axis, [(source, source + steps) for source in range(l...]
    another operation x12, local copies, waits for them, and re-layouts: 12.7 us -> 6.97 us  [attend_chunk(): jnp.stack([moved[0].reshape(head_shape) for moved in received])[None]]
    ppermute x16, starting transfers between devices: 48.2 us -> 53.7 us  [from_behind(): lax.ppermute(value, axis, [(source, source + steps) for source in range(l...]
    unnamed x73 -> x59, local copies, waits for them, and re-layouts: 12.9 us -> 10.4 us
    another operation x8, other arithmetic: 8.69 us -> 6.76 us  [attend_chunk(): jnp.stack([key_terms[0, slot_index], value_terms[0, slot_index]])]
  transfers between devices with their start and end apart: 16 -> 16, of which waited for: 7 -> 8; matrix products, arithmetic and copies ran while one was open for 35% -> 28% of each run, Pallas kernels for 0% -> 0%
where the time goes in v18:
time: 184 us; the launch traced here: 183 us
  waiting for transfers between devices  54.7 us (30%)
  starting transfers between devices  53.7 us (29%)
  local copies, waits for them, and re-layouts  41.2 us (22%)
  other arithmetic  21.8 us (12%)
  matrix products  9.69 us (5%)
  between operations  2.04 us (1%)
    ppermute x16, waiting for transfers between devices, from_behind(): lax.ppermute(value, axis, [(source, source + steps) for source in range(l...  54.7 us
    ppermute x16, starting transfers between devices, from_behind(): lax.ppermute(value, axis, [(source, source + steps) for source in range(l...  53.7 us
    slice x8, local copies, waits for them, and re-layouts, attend_chunk(): moved[0].reshape(head_shape)  13.1 us
    unnamed x59, local copies, waits for them, and re-layouts  10.4 us
    another operation x12, local copies, waits for them, and re-layouts, attend_chunk(): jnp.stack([moved[0].reshape(head_shape) for moved in received])[None]  6.97 us
    another operation x8, other arithmetic, attend_chunk(): jnp.stack([key_terms[0, slot_index], value_terms[0, slot_index]])  6.76 us
    another operation x6, other arithmetic  5.35 us
  transfers between devices with their start and end apart: 16, of which 8 were waited for; matrix products, arithmetic and copies ran while one was open for 28% of the time, Pallas kernels for 0%

profile of v18, /device:TPU:15, one launch (start us, length us, event | category | flops | bytes accessed | tf_op | source)
XLA Modules:
  0.0 183.1 jit_solution(3322385002323787716)
XLA Ops:
  7.1 3.2 %collective-permute-start.2 = (bf16[2,128,1024]{1,2,0:T(8,128)(2,1)}, bf16[2,128,1024]{1,2,0:T(8,128)(2,1)}, u32[]{:S(2)}, u32[]{:S(2)}) collective-permute-start(bf16[2,128,1024]{1,2,0:T(8,128)(2,1)} %pad_maximum_fusion.3), channel_id=1, source_target_pairs={{0,4},{1,5},{2,6},{3,7},{4,8},{5,9},{6,10},{7,11},{8,12},{9,13},{1... | collective-permute-start | bytes 1572872 | tf_op jit(solution)/shard_map/ppermute | solution.py:17
  10.3 4.0 %collective-permute-start = (bf16[2,128,1024]{1,2,0:T(8,128)(2,1)}, bf16[2,128,1024]{1,2,0:T(8,128)(2,1)}, u32[]{:S(2)}, u32[]{:S(2)}) collective-permute-start(bf16[2,128,1024]{1,2,0:T(8,128)(2,1)} %pad_maximum_fusion.3), channel_id=1, source_target_pairs={{0,1},{1,2},{2,3},{3,4},{4,5},{5,6},{6,7},{7,8},{8,9},{9,10},{10,1... | collective-permute-start | bytes 1572872 | tf_op jit(solution)/shard_map/ppermute | solution.py:17
  17.9 4.2 %collective-permute-done.2 = bf16[2,128,1024]{1,2,0:T(8,128)(2,1)} collective-permute-done((bf16[2,128,1024]{1,2,0:T(8,128)(2,1)}, bf16[2,128,1024]{1,2,0:T(8,128)(2,1)}, u32[]{:S(2)}, u32[]{:S(2)}) %collective-permute-start.2) | collective-permute-done | bytes 524320 | tf_op jit(solution)/shard_map/ppermute | solution.py:17
  22.1 3.2 %collective-permute-start.3 = (bf16[2,128,1024]{1,2,0:T(8,128)(2,1)}, bf16[2,128,1024]{1,2,0:T(8,128)(2,1)}, u32[]{:S(2)}, u32[]{:S(2)}) collective-permute-start(bf16[2,128,1024]{1,2,0:T(8,128)(2,1)} %collective-permute-done.2), channel_id=1, source_target_pairs={{0,4},{1,5},{2,6},{3,7},{4,8},{5,9},{6,10},{7,11},{8,12},{9,13},{1... | collective-permute-start | bytes 1572872 | tf_op jit(solution)/shard_map/ppermute | solution.py:17
  25.3 1.8 fusion.41
  28.0 5.3 %collective-permute-start.1 = (bf16[2,128,1024]{1,2,0:T(8,128)(2,1)}, bf16[2,128,1024]{1,2,0:T(8,128)(2,1)}, u32[]{:S(2)}, u32[]{:S(2)}) collective-permute-start(bf16[2,128,1024]{1,2,0:T(8,128)(2,1)} %collective-permute-done), channel_id=1, source_target_pairs={{0,1},{1,2},{2,3},{3,4},{4,5},{5,6},{6,7},{7,8},{8,9},{9,10},{10,1... | collective-permute-start | bytes 1572872 | tf_op jit(solution)/shard_map/ppermute | solution.py:17
  33.2 1.9 %fusion.43 = (bf16[1,128,1024]{1,2,0:T(8,128)(2,1)}, bf16[1,128,1024]{1,2,0:T(8,128)(2,1)}) fusion(bf16[2,128,1024]{1,2,0:T(8,128)(2,1)} %collective-permute-done), kind=kLoop, calls=%fused_computation.177 | loop fusion | bytes 1048576 | tf_op jit(solution)/shard_map/slice | solution.py:88
  36.5 1.7 constant_dynamic-update-slice_fusion.3
  38.7 1.9 %fusion.40 = (bf16[1,128,1024]{1,2,0:T(8,128)(2,1)}, bf16[1,128,1024]{1,2,0:T(8,128)(2,1)}) fusion(bf16[2,128,1024]{1,2,0:T(8,128)(2,1)} %collective-permute-done.3), kind=kLoop, calls=%fused_computation.174 | loop fusion | bytes 1048576 | tf_op jit(solution)/shard_map/slice | solution.py:88
  41.7 3.1 %collective-permute-done.1 = bf16[2,128,1024]{1,2,0:T(8,128)(2,1)} collective-permute-done((bf16[2,128,1024]{1,2,0:T(8,128)(2,1)}, bf16[2,128,1024]{1,2,0:T(8,128)(2,1)}, u32[]{:S(2)}, u32[]{:S(2)}) %collective-permute-start.1) | collective-permute-done | bytes 524320 | tf_op jit(solution)/shard_map/ppermute | solution.py:17
  44.8 1.9 %fusion.42 = (bf16[1,128,1024]{1,2,0:T(8,128)(2,1)}, bf16[1,128,1024]{1,2,0:T(8,128)(2,1)}) fusion(bf16[2,128,1024]{1,2,0:T(8,128)(2,1)} %collective-permute-done.1), kind=kLoop, calls=%fused_computation.176 | loop fusion | bytes 1048576 | tf_op jit(solution)/shard_map/slice | solution.py:88
  46.7 1.8 copy.99
  53.8 2.1 %collective-permute-start.7 = (bf16[2,128,1024]{1,2,0:T(8,128)(2,1)}, bf16[2,128,1024]{1,2,0:T(8,128)(2,1)}, u32[]{:S(2)}, u32[]{:S(2)}) collective-permute-start(bf16[2,128,1024]{1,2,0:T(8,128)(2,1)} %pad_maximum_fusion.5), channel_id=1, source_target_pairs={{0,8},{1,9},{2,10},{3,11},{4,12},{5,13},{6,14},{7,15},{16,24},{17,... | collective-permute-start | bytes 1572872 | tf_op jit(solution)/shard_map/ppermute | solution.py:17
  55.9 2.4 %collective-permute-start.6 = (bf16[2,128,1024]{1,2,0:T(8,128)(2,1)}, bf16[2,128,1024]{1,2,0:T(8,128)(2,1)}, u32[]{:S(2)}, u32[]{:S(2)}) collective-permute-start(bf16[2,128,1024]{1,2,0:T(8,128)(2,1)} %pad_maximum_fusion.5), channel_id=1, source_target_pairs={{0,4},{1,5},{2,6},{3,7},{4,8},{5,9},{6,10},{7,11},{8,12},{9,13},{1... | collective-permute-start | bytes 1572872 | tf_op jit(solution)/shard_map/ppermute | solution.py:17
  58.3 1.9 %collective-permute-start.5 = (bf16[2,128,1024]{1,2,0:T(8,128)(2,1)}, bf16[2,128,1024]{1,2,0:T(8,128)(2,1)}, u32[]{:S(2)}, u32[]{:S(2)}) collective-permute-start(bf16[2,128,1024]{1,2,0:T(8,128)(2,1)} %pad_maximum_fusion.5), channel_id=1, source_target_pairs={{0,2},{1,3},{2,4},{3,5},{4,6},{5,7},{6,8},{7,9},{8,10},{9,11},{10,... | collective-permute-start | bytes 1572872 | tf_op jit(solution)/shard_map/ppermute | solution.py:17
  66.8 3.4 %collective-permute-start.9 = (bf16[2,128,8,128]{1,3,2,0:T(8,128)(2,1)}, bf16[2,128,8,128]{1,3,2,0:T(8,128)(2,1)}, u32[]{:S(2)}, u32[]{:S(2)}) collective-permute-start(bf16[2,128,8,128]{1,3,2,0:T(8,128)(2,1)} %pad_maximum_fusion.9), channel_id=1, source_target_pairs={{2,0},{3,1},{4,2},{5,3},{6,4},{7,5},{8,6},{9,7},{10,8},{11,9},{12,... | collective-permute-start | bytes 1572872 | tf_op jit(solution)/shard_map/ppermute | solution.py:17
  76.2 7.0 %collective-permute-start.4 = (bf16[2,128,1024]{1,2,0:T(8,128)(2,1)}, bf16[2,128,1024]{1,2,0:T(8,128)(2,1)}, u32[]{:S(2)}, u32[]{:S(2)}) collective-permute-start(bf16[2,128,1024]{1,2,0:T(8,128)(2,1)} %pad_maximum_fusion.5), channel_id=1, source_target_pairs={{0,1},{1,2},{2,3},{3,4},{4,5},{5,6},{6,7},{7,8},{8,9},{9,10},{10,1... | collective-permute-start | bytes 1572872 | tf_op jit(solution)/shard_map/ppermute | solution.py:17
  83.2 4.5 %collective-permute-start.10 = (bf16[2,128,8,128]{1,3,2,0:T(8,128)(2,1)}, bf16[2,128,8,128]{1,3,2,0:T(8,128)(2,1)}, u32[]{:S(2)}, u32[]{:S(2)}) collective-permute-start(bf16[2,128,8,128]{1,3,2,0:T(8,128)(2,1)} %pad_maximum_fusion.10), channel_id=1, source_target_pairs={{4,0},{5,1},{6,2},{7,3},{8,4},{9,5},{10,6},{11,7},{12,8},{13,9},{1... | collective-permute-start | bytes 1572872 | tf_op jit(solution)/shard_map/ppermute | solution.py:17
  91.5 6.4 %collective-permute-done.5 = bf16[2,128,1024]{1,2,0:T(8,128)(2,1)} collective-permute-done((bf16[2,128,1024]{1,2,0:T(8,128)(2,1)}, bf16[2,128,1024]{1,2,0:T(8,128)(2,1)}, u32[]{:S(2)}, u32[]{:S(2)}) %collective-permute-start.5) | collective-permute-done | bytes 524320 | tf_op jit(solution)/shard_map/ppermute | solution.py:17
  97.9 8.4 %collective-permute-start.8 = (bf16[2,128,8,128]{1,3,2,0:T(8,128)(2,1)}, bf16[2,128,8,128]{1,3,2,0:T(8,128)(2,1)}, u32[]{:S(2)}, u32[]{:S(2)}) collective-permute-start(bf16[2,128,8,128]{1,3,2,0:T(8,128)(2,1)} %pad_maximum_fusion.8), channel_id=1, source_target_pairs={{1,0},{2,1},{3,2},{4,3},{5,4},{6,5},{7,6},{8,7},{9,8},{10,9},{11,1... | collective-permute-start | bytes 1572872 | tf_op jit(solution)/shard_map/ppermute | solution.py:17
  106.4 1.8 fusion.38
  108.3 1.9 %fusion.39 = (bf16[1,128,1024]{1,2,0:T(8,128)(2,1)}, bf16[1,128,1024]{1,2,0:T(8,128)(2,1)}) fusion(bf16[2,128,1024]{1,2,0:T(8,128)(2,1)} %collective-permute-done.4), kind=kLoop, calls=%fused_computation.173 | loop fusion | bytes 1048576 | tf_op jit(solution)/shard_map/slice | solution.py:88
  120.0 1.9 %collective-permute-start.13 = (bf16[2,128,8,128]{1,3,2,0:T(8,128)(2,1)}, bf16[2,128,8,128]{1,3,2,0:T(8,128)(2,1)}, u32[]{:S(2)}, u32[]{:S(2)}) collective-permute-start(bf16[2,128,8,128]{1,3,2,0:T(8,128)(2,1)} %pad_maximum_fusion.13), channel_id=1, source_target_pairs={{2,0},{3,1},{4,2},{5,3},{6,4},{7,5},{8,6},{9,7},{10,8},{11,9},{12,... | collective-permute-start | bytes 1572872 | tf_op jit(solution)/shard_map/ppermute | solution.py:17
  124.4 1.9 %collective-permute-start.14 = (bf16[2,128,8,128]{1,3,2,0:T(8,128)(2,1)}, bf16[2,128,8,128]{1,3,2,0:T(8,128)(2,1)}, u32[]{:S(2)}, u32[]{:S(2)}) collective-permute-start(bf16[2,128,8,128]{1,3,2,0:T(8,128)(2,1)} %pad_maximum_fusion.14), channel_id=1, source_target_pairs={{4,0},{5,1},{6,2},{7,3},{8,4},{9,5},{10,6},{11,7},{12,8},{13,9},{1... | collective-permute-start | bytes 1572872 | tf_op jit(solution)/shard_map/ppermute | solution.py:17
  127.7 1.9 %collective-permute-start.12 = (bf16[2,128,8,128]{1,3,2,0:T(8,128)(2,1)}, bf16[2,128,8,128]{1,3,2,0:T(8,128)(2,1)}, u32[]{:S(2)}, u32[]{:S(2)}) collective-permute-start(bf16[2,128,8,128]{1,3,2,0:T(8,128)(2,1)} %pad_maximum_fusion.12), channel_id=1, source_target_pairs={{1,0},{2,1},{3,2},{4,3},{5,4},{6,5},{7,6},{8,7},{9,8},{10,9},{11,1... | collective-permute-start | bytes 1572872 | tf_op jit(solution)/shard_map/ppermute | solution.py:17
  129.6 2.6 %fusion.27 = (bf16[128,8,128]{0,2,1:T(8,128)(2,1)}, f32[128,8,128]{0,2,1:T(8,128)S(1)}) fusion(bf16[128,8,128]{0,2,1:T(8,128)(2,1)S(1)} %copy-done.11, bf16[2,128,8,128]{1,3,2,0:T(8,128)(2,1)} %collective-permute-done.11, bf16[2,128,8,128]{1,3,2,0:T(8,128)(2,1)} %collective-permute-done.10, bf16[2,128,8,128]{1,3,2,0:T(8,128)(2,1)} %collective-permute-done.9, ...), kind=kLoop, calls=%fused_computation.70 | loop fusion | flops 2490368 | bytes 3407872 | tf_op jit(solution)/shard_map/convert.23
  132.3 1.8 copy.132
  134.9 1.9 %pad_maximum_fusion.6 = bf16[128,2048]{1,0:T(8,128)(2,1)} fusion(bf16[128,1024]{1,0:T(8,128)(2,1)} %copy.113, bf16[128,1024]{1,0:T(8,128)(2,1)} %copy.112), kind=kLoop, calls=%fused_computation.52 | loop fusion | flops 1048576 | bytes 1048576 | tf_op jit(solution)/shard_map/concatenate | solution.py:177
  138.2 3.9 %collective-permute-done.14 = bf16[2,128,8,128]{1,3,2,0:T(8,128)(2,1)} collective-permute-done((bf16[2,128,8,128]{1,3,2,0:T(8,128)(2,1)}, bf16[2,128,8,128]{1,3,2,0:T(8,128)(2,1)}, u32[]{:S(2)}, u32[]{:S(2)}) %collective-permute-start.14) | collective-permute-done | bytes 524320 | tf_op jit(solution)/shard_map/ppermute | solution.py:17
  142.2 12.1 %collective-permute-done.15 = bf16[2,128,8,128]{1,3,2,0:T(8,128)(2,1)} collective-permute-done((bf16[2,128,8,128]{1,3,2,0:T(8,128)(2,1)}, bf16[2,128,8,128]{1,3,2,0:T(8,128)(2,1)}, u32[]{:S(2)}, u32[]{:S(2)}) %collective-permute-start.15) | collective-permute-done | bytes 524320 | tf_op jit(solution)/shard_map/ppermute | solution.py:17
  154.3 23.4 %collective-permute-done.12 = bf16[2,128,8,128]{1,3,2,0:T(8,128)(2,1)} collective-permute-done((bf16[2,128,8,128]{1,3,2,0:T(8,128)(2,1)}, bf16[2,128,8,128]{1,3,2,0:T(8,128)(2,1)}, u32[]{:S(2)}, u32[]{:S(2)}) %collective-permute-start.12) | collective-permute-done | bytes 524320 | tf_op jit(solution)/shard_map/ppermute | solution.py:17
  177.7 1.9 %fusion.26 = (bf16[128,8,128]{0,2,1:T(8,128)(2,1)S(1)}, f32[128,8,128]{0,2,1:T(8,128)S(1)}) fusion(bf16[128,8,128]{0,2,1:T(8,128)(2,1)S(1)} %copy-done.14, bf16[2,128,8,128]{1,3,2,0:T(8,128)(2,1)} %collective-permute-done.15, bf16[2,128,8,128]{1,3,2,0:T(8,128)(2,1)} %collective-permute-done.14, bf16[2,128,8,128]{1,3,2,0:T(8,128)(2,1)} %collective-permute-done.13, ...), kind=kLoop, calls=%fused_computation.65 | loop fusion | flops 2490368 | bytes 3407872 | tf_op jit(solution)/shard_map/convert.22
  (151 shorter events, 54.0 us)
Async XLA Ops:
  0.6 3.1 %copy-start.15 = (bf16[128,2048]{1,0:T(8,128)(2,1)S(1)}, bf16[128,2048]{1,0:T(8,128)(2,1)}, u32[]{:S(2)}) copy-start(bf16[128,2048]{1,0:T(8,128)(2,1)} %param.7) | copy-start | bytes 1572868
  6.2 8.8 %copy-start.17 = (bf16[128,2048]{1,0:T(8,128)(2,1)S(1)}, bf16[128,2048]{1,0:T(8,128)(2,1)}, u32[]{:S(2)}) copy-start(bf16[128,2048]{1,0:T(8,128)(2,1)} %param.10) | copy-start | bytes 1572868
  6.2 8.8 %copy-start.18 = (s32[4]{0:T(128)S(1)}, s32[4]{0:T(128)}, u32[]{:S(2)}) copy-start(s32[4]{0:T(128)} %constant.35) | copy-start | bytes 52
  7.1 15.0 %collective-permute-start.2 = (bf16[2,128,1024]{1,2,0:T(8,128)(2,1)}, bf16[2,128,1024]{1,2,0:T(8,128)(2,1)}, u32[]{:S(2)}, u32[]{:S(2)}) collective-permute-start(bf16[2,128,1024]{1,2,0:T(8,128)(2,1)} %pad_maximum_fusion.3), channel_id=1, source_target_pairs={{0,4},{1,5},{2,6},{3,7},{4,8},{5,9},{6,10},{7,11},{8,12},{9,13},{1... | collective-permute-start | bytes 1572872 | tf_op jit(solution)/shard_map/ppermute | solution.py:17
  10.3 17.7 %collective-permute-start = (bf16[2,128,1024]{1,2,0:T(8,128)(2,1)}, bf16[2,128,1024]{1,2,0:T(8,128)(2,1)}, u32[]{:S(2)}, u32[]{:S(2)}) collective-permute-start(bf16[2,128,1024]{1,2,0:T(8,128)(2,1)} %pad_maximum_fusion.3), channel_id=1, source_target_pairs={{0,1},{1,2},{2,3},{3,4},{4,5},{5,6},{6,7},{7,8},{8,9},{9,10},{10,1... | collective-permute-start | bytes 1572872 | tf_op jit(solution)/shard_map/ppermute | solution.py:17
  22.1 16.6 %collective-permute-start.3 = (bf16[2,128,1024]{1,2,0:T(8,128)(2,1)}, bf16[2,128,1024]{1,2,0:T(8,128)(2,1)}, u32[]{:S(2)}, u32[]{:S(2)}) collective-permute-start(bf16[2,128,1024]{1,2,0:T(8,128)(2,1)} %collective-permute-done.2), channel_id=1, source_target_pairs={{0,4},{1,5},{2,6},{3,7},{4,8},{5,9},{6,10},{7,11},{8,12},{9,13},{1... | collective-permute-start | bytes 1572872 | tf_op jit(solution)/shard_map/ppermute | solution.py:17
  28.0 16.9 %collective-permute-start.1 = (bf16[2,128,1024]{1,2,0:T(8,128)(2,1)}, bf16[2,128,1024]{1,2,0:T(8,128)(2,1)}, u32[]{:S(2)}, u32[]{:S(2)}) collective-permute-start(bf16[2,128,1024]{1,2,0:T(8,128)(2,1)} %collective-permute-done), channel_id=1, source_target_pairs={{0,1},{1,2},{2,3},{3,4},{4,5},{5,6},{6,7},{7,8},{8,9},{9,10},{10,1... | collective-permute-start | bytes 1572872 | tf_op jit(solution)/shard_map/ppermute | solution.py:17
  51.0 1.3 copy-start.3
  51.0 1.3 copy-start.10
  51.0 1.4 copy-start.5
  51.0 1.5 copy-start.7
  53.8 29.4 %collective-permute-start.7 = (bf16[2,128,1024]{1,2,0:T(8,128)(2,1)}, bf16[2,128,1024]{1,2,0:T(8,128)(2,1)}, u32[]{:S(2)}, u32[]{:S(2)}) collective-permute-start(bf16[2,128,1024]{1,2,0:T(8,128)(2,1)} %pad_maximum_fusion.5), channel_id=1, source_target_pairs={{0,8},{1,9},{2,10},{3,11},{4,12},{5,13},{6,14},{7,15},{16,24},{17,... | collective-permute-start | bytes 1572872 | tf_op jit(solution)/shard_map/ppermute | solution.py:17
  55.9 33.1 %collective-permute-start.6 = (bf16[2,128,1024]{1,2,0:T(8,128)(2,1)}, bf16[2,128,1024]{1,2,0:T(8,128)(2,1)}, u32[]{:S(2)}, u32[]{:S(2)}) collective-permute-start(bf16[2,128,1024]{1,2,0:T(8,128)(2,1)} %pad_maximum_fusion.5), channel_id=1, source_target_pairs={{0,4},{1,5},{2,6},{3,7},{4,8},{5,9},{6,10},{7,11},{8,12},{9,13},{1... | collective-permute-start | bytes 1572872 | tf_op jit(solution)/shard_map/ppermute | solution.py:17
  58.3 39.6 %collective-permute-start.5 = (bf16[2,128,1024]{1,2,0:T(8,128)(2,1)}, bf16[2,128,1024]{1,2,0:T(8,128)(2,1)}, u32[]{:S(2)}, u32[]{:S(2)}) collective-permute-start(bf16[2,128,1024]{1,2,0:T(8,128)(2,1)} %pad_maximum_fusion.5), channel_id=1, source_target_pairs={{0,2},{1,3},{2,4},{3,5},{4,6},{5,7},{6,8},{7,9},{8,10},{9,11},{10,... | collective-permute-start | bytes 1572872 | tf_op jit(solution)/shard_map/ppermute | solution.py:17
  66.0 5.9 %copy-start.4 = (bf16[1,128,8,128]{1,3,2,0:T(8,128)(2,1)S(1)}, bf16[1,128,8,128]{1,3,2,0:T(8,128)(2,1)}, u32[]{:S(2)}) copy-start(bf16[1,128,8,128]{1,3,2,0:T(8,128)(2,1)} %get-tuple-element.25) | copy-start | bytes 786436
  66.8 57.6 %collective-permute-start.9 = (bf16[2,128,8,128]{1,3,2,0:T(8,128)(2,1)}, bf16[2,128,8,128]{1,3,2,0:T(8,128)(2,1)}, u32[]{:S(2)}, u32[]{:S(2)}) collective-permute-start(bf16[2,128,8,128]{1,3,2,0:T(8,128)(2,1)} %pad_maximum_fusion.9), channel_id=1, source_target_pairs={{2,0},{3,1},{4,2},{5,3},{6,4},{7,5},{8,6},{9,7},{10,8},{11,9},{12,... | collective-permute-start | bytes 1572872 | tf_op jit(solution)/shard_map/ppermute | solution.py:17
  76.2 32.1 %collective-permute-start.4 = (bf16[2,128,1024]{1,2,0:T(8,128)(2,1)}, bf16[2,128,1024]{1,2,0:T(8,128)(2,1)}, u32[]{:S(2)}, u32[]{:S(2)}) collective-permute-start(bf16[2,128,1024]{1,2,0:T(8,128)(2,1)} %pad_maximum_fusion.5), channel_id=1, source_target_pairs={{0,1},{1,2},{2,3},{3,4},{4,5},{5,6},{6,7},{7,8},{8,9},{9,10},{10,1... | collective-permute-start | bytes 1572872 | tf_op jit(solution)/shard_map/ppermute | solution.py:17
  83.2 43.1 %collective-permute-start.10 = (bf16[2,128,8,128]{1,3,2,0:T(8,128)(2,1)}, bf16[2,128,8,128]{1,3,2,0:T(8,128)(2,1)}, u32[]{:S(2)}, u32[]{:S(2)}) collective-permute-start(bf16[2,128,8,128]{1,3,2,0:T(8,128)(2,1)} %pad_maximum_fusion.10), channel_id=1, source_target_pairs={{4,0},{5,1},{6,2},{7,3},{8,4},{9,5},{10,6},{11,7},{12,8},{13,9},{1... | collective-permute-start | bytes 1572872 | tf_op jit(solution)/shard_map/ppermute | solution.py:17
  89.0 38.7 %collective-permute-start.11 = (bf16[2,128,8,128]{1,3,2,0:T(8,128)(2,1)}, bf16[2,128,8,128]{1,3,2,0:T(8,128)(2,1)}, u32[]{:S(2)}, u32[]{:S(2)}) collective-permute-start(bf16[2,128,8,128]{1,3,2,0:T(8,128)(2,1)} %pad_maximum_fusion.11), channel_id=1, source_target_pairs={{8,0},{9,1},{10,2},{11,3},{12,4},{13,5},{14,6},{15,7},{24,16},{25,... | collective-permute-start | bytes 1572872 | tf_op jit(solution)/shard_map/ppermute | solution.py:17
  97.9 31.7 %collective-permute-start.8 = (bf16[2,128,8,128]{1,3,2,0:T(8,128)(2,1)}, bf16[2,128,8,128]{1,3,2,0:T(8,128)(2,1)}, u32[]{:S(2)}, u32[]{:S(2)}) collective-permute-start(bf16[2,128,8,128]{1,3,2,0:T(8,128)(2,1)} %pad_maximum_fusion.8), channel_id=1, source_target_pairs={{1,0},{2,1},{3,2},{4,3},{5,4},{6,5},{7,6},{8,7},{9,8},{10,9},{11,1... | collective-permute-start | bytes 1572872 | tf_op jit(solution)/shard_map/ppermute | solution.py:17
  112.9 1.3 copy-start.9
  112.9 1.4 copy-start.8
  120.0 18.2 %collective-permute-start.13 = (bf16[2,128,8,128]{1,3,2,0:T(8,128)(2,1)}, bf16[2,128,8,128]{1,3,2,0:T(8,128)(2,1)}, u32[]{:S(2)}, u32[]{:S(2)}) collective-permute-start(bf16[2,128,8,128]{1,3,2,0:T(8,128)(2,1)} %pad_maximum_fusion.13), channel_id=1, source_target_pairs={{2,0},{3,1},{4,2},{5,3},{6,4},{7,5},{8,6},{9,7},{10,8},{11,9},{12,... | collective-permute-start | bytes 1572872 | tf_op jit(solution)/shard_map/ppermute | solution.py:17
  122.7 6.9 %copy-start.11 = (bf16[128,8,128]{0,2,1:T(8,128)(2,1)S(1)}, bf16[128,8,128]{0,2,1:T(8,128)(2,1)}, u32[]{:S(2)}) copy-start(bf16[128,8,128]{0,2,1:T(8,128)(2,1)} %get-tuple-element.24) | copy-start | bytes 786436
  122.7 6.9 %copy-start.12 = (bf16[128,8,128]{0,2,1:T(8,128)(2,1)S(1)}, bf16[128,8,128]{0,2,1:T(8,128)(2,1)}, u32[]{:S(2)}) copy-start(bf16[128,8,128]{0,2,1:T(8,128)(2,1)} %get-tuple-element.38) | copy-start | bytes 786436
  124.4 17.7 %collective-permute-start.14 = (bf16[2,128,8,128]{1,3,2,0:T(8,128)(2,1)}, bf16[2,128,8,128]{1,3,2,0:T(8,128)(2,1)}, u32[]{:S(2)}, u32[]{:S(2)}) collective-permute-start(bf16[2,128,8,128]{1,3,2,0:T(8,128)(2,1)} %pad_maximum_fusion.14), channel_id=1, source_target_pairs={{4,0},{5,1},{6,2},{7,3},{8,4},{9,5},{10,6},{11,7},{12,8},{13,9},{1... | collective-permute-start | bytes 1572872 | tf_op jit(solution)/shard_map/ppermute | solution.py:17
  126.4 27.9 %collective-permute-start.15 = (bf16[2,128,8,128]{1,3,2,0:T(8,128)(2,1)}, bf16[2,128,8,128]{1,3,2,0:T(8,128)(2,1)}, u32[]{:S(2)}, u32[]{:S(2)}) collective-permute-start(bf16[2,128,8,128]{1,3,2,0:T(8,128)(2,1)} %pad_maximum_fusion.15), channel_id=1, source_target_pairs={{8,0},{9,1},{10,2},{11,3},{12,4},{13,5},{14,6},{15,7},{24,16},{25,... | collective-permute-start | bytes 1572872 | tf_op jit(solution)/shard_map/ppermute | solution.py:17
  127.7 50.0 %collective-permute-start.12 = (bf16[2,128,8,128]{1,3,2,0:T(8,128)(2,1)}, bf16[2,128,8,128]{1,3,2,0:T(8,128)(2,1)}, u32[]{:S(2)}, u32[]{:S(2)}) collective-permute-start(bf16[2,128,8,128]{1,3,2,0:T(8,128)(2,1)} %pad_maximum_fusion.12), channel_id=1, source_target_pairs={{1,0},{2,1},{3,2},{4,3},{5,4},{6,5},{7,6},{8,7},{9,8},{10,9},{11,1... | collective-permute-start | bytes 1572872 | tf_op jit(solution)/shard_map/ppermute | solution.py:17
  136.8 40.9 %copy-start.13 = (bf16[128,8,128]{0,2,1:T(8,128)(2,1)S(1)}, bf16[128,8,128]{0,2,1:T(8,128)(2,1)}, u32[]{:S(2)}) copy-start(bf16[128,8,128]{0,2,1:T(8,128)(2,1)} %get-tuple-element.43) | copy-start | bytes 786436
  136.8 40.9 %copy-start.14 = (bf16[128,8,128]{0,2,1:T(8,128)(2,1)S(1)}, bf16[128,8,128]{0,2,1:T(8,128)(2,1)}, u32[]{:S(2)}) copy-start(bf16[128,8,128]{0,2,1:T(8,128)(2,1)} %get-tuple-element.29) | copy-start | bytes 786436
  138.2 41.6 %copy-start = (f32[128,8,128]{0,2,1:T(8,128)S(1)}, f32[128,8,128]{0,2,1:T(8,128)}, u32[]{:S(2)}) copy-start(f32[128,8,128]{0,2,1:T(8,128)} %convolution_bitcast_fusion.1) | copy-start | bytes 1572868
  138.2 41.6 %copy-start.1 = (f32[128,8,128]{0,2,1:T(8,128)S(1)}, f32[128,8,128]{0,2,1:T(8,128)}, u32[]{:S(2)}) copy-start(f32[128,8,128]{0,2,1:T(8,128)} %convolution_bitcast_fusion) | copy-start | bytes 1572868
  (3 other events, 3.4 us)

commit v19 on v18

--- a/solution.py
+++ b/solution.py
@@ -73,7 +73,7 @@
     pair = jnp.stack([key_c, value_c])
     received = {0: pair}
     for offset in offsets:
-        if relay and (offset.bit_length() - 1) % 2 == 1:
+        if relay and offset >= 8 and (offset.bit_length() - 1) % 2 == 1:
             half = offset // 2
             received[offset] = from_behind(received[half], "ctx", half)
         else:

time: 184 us -> 193 us (1.049)
  waiting for transfers between devices: 54.7 us -> 75.1 us
  starting transfers between devices: 53.7 us -> 42.8 us
    ppermute x16, waiting for transfers between devices: 54.7 us -> 75.1 us  [from_behind(): lax.ppermute(value, axis, [(source, source + steps) for source in range(l...]
    ppermute x16, starting transfers between devices: 53.7 us -> 42.8 us  [from_behind(): lax.ppermute(value, axis, [(source, source + steps) for source in range(l...]
    unnamed x59 -> x57, local copies, waits for them, and re-layouts: 10.4 us -> 10.7 us
  transfers between devices with their start and end apart: 16 -> 16, of which waited for: 8 -> 8; matrix products, arithmetic and copies ran while one was open for 28% -> 26% of each run, Pallas kernels for 0% -> 0%
where the time goes in v19:
time: 193 us; the launch traced here: 192 us
  waiting for transfers between devices  75.1 us (39%)
  starting transfers between devices  42.8 us (22%)
  local copies, waits for them, and re-layouts  40.7 us (21%)
  other arithmetic  21.8 us (11%)
  matrix products  9.69 us (5%)
  between operations  2.02 us (1%)
    ppermute x16, waiting for transfers between devices, from_behind(): lax.ppermute(value, axis, [(source, source + steps) for source in range(l...  75.1 us
    ppermute x16, starting transfers between devices, from_behind(): lax.ppermute(value, axis, [(source, source + steps) for source in range(l...  42.8 us
    slice x8, local copies, waits for them, and re-layouts, attend_chunk(): moved[0].reshape(head_shape)  13 us
    unnamed x57, local copies, waits for them, and re-layouts  10.7 us
    another operation x8, other arithmetic, attend_chunk(): jnp.stack([key_terms[0, slot_index], value_terms[0, slot_index]])  6.74 us
    another operation x12, local copies, waits for them, and re-layouts, attend_chunk(): jnp.stack([moved[0].reshape(head_shape) for moved in received])[None]  6.28 us
    another operation x6, other arithmetic  5.35 us
  transfers between devices with their start and end apart: 16, of which 8 were waited for; matrix products, arithmetic and copies ran while one was open for 26% of the time, Pallas kernels for 0%

profile of v19, /device:TPU:15, one launch (start us, length us, event | category | flops | bytes accessed | tf_op | source)
XLA Modules:
  0.0 192.1 jit_solution(3309484024655036133)
XLA Ops:
  7.1 3.2 %collective-permute-start.2 = (bf16[2,128,1024]{1,2,0:T(8,128)(2,1)}, bf16[2,128,1024]{1,2,0:T(8,128)(2,1)}, u32[]{:S(2)}, u32[]{:S(2)}) collective-permute-start(bf16[2,128,1024]{1,2,0:T(8,128)(2,1)} %pad_maximum_fusion.3), channel_id=1, source_target_pairs={{0,4},{1,5},{2,6},{3,7},{4,8},{5,9},{6,10},{7,11},{8,12},{9,13},{1... | collective-permute-start | bytes 1572872 | tf_op jit(solution)/shard_map/ppermute | solution.py:17
  10.3 3.1 %collective-permute-start.1 = (bf16[2,128,1024]{1,2,0:T(8,128)(2,1)}, bf16[2,128,1024]{1,2,0:T(8,128)(2,1)}, u32[]{:S(2)}, u32[]{:S(2)}) collective-permute-start(bf16[2,128,1024]{1,2,0:T(8,128)(2,1)} %pad_maximum_fusion.3), channel_id=1, source_target_pairs={{0,2},{1,3},{2,4},{3,5},{4,6},{5,7},{6,8},{7,9},{8,10},{9,11},{10,... | collective-permute-start | bytes 1572872 | tf_op jit(solution)/shard_map/ppermute | solution.py:17
  13.5 4.3 %collective-permute-start = (bf16[2,128,1024]{1,2,0:T(8,128)(2,1)}, bf16[2,128,1024]{1,2,0:T(8,128)(2,1)}, u32[]{:S(2)}, u32[]{:S(2)}) collective-permute-start(bf16[2,128,1024]{1,2,0:T(8,128)(2,1)} %pad_maximum_fusion.3), channel_id=1, source_target_pairs={{0,1},{1,2},{2,3},{3,4},{4,5},{5,6},{6,7},{7,8},{8,9},{9,10},{10,1... | collective-permute-start | bytes 1572872 | tf_op jit(solution)/shard_map/ppermute | solution.py:17
  21.3 11.2 %collective-permute-done.1 = bf16[2,128,1024]{1,2,0:T(8,128)(2,1)} collective-permute-done((bf16[2,128,1024]{1,2,0:T(8,128)(2,1)}, bf16[2,128,1024]{1,2,0:T(8,128)(2,1)}, u32[]{:S(2)}, u32[]{:S(2)}) %collective-permute-start.1) | collective-permute-done | bytes 524320 | tf_op jit(solution)/shard_map/ppermute | solution.py:17
  32.4 1.8 fusion.42
  34.4 4.8 %collective-permute-done = bf16[2,128,1024]{1,2,0:T(8,128)(2,1)} collective-permute-done((bf16[2,128,1024]{1,2,0:T(8,128)(2,1)}, bf16[2,128,1024]{1,2,0:T(8,128)(2,1)}, u32[]{:S(2)}, u32[]{:S(2)}) %collective-permute-start) | collective-permute-done | bytes 524320 | tf_op jit(solution)/shard_map/ppermute | solution.py:17
  39.2 1.9 fusion.43
  42.2 1.9 fusion.41
  44.1 3.3 %collective-permute-start.3 = (bf16[2,128,1024]{1,2,0:T(8,128)(2,1)}, bf16[2,128,1024]{1,2,0:T(8,128)(2,1)}, u32[]{:S(2)}, u32[]{:S(2)}) collective-permute-start(bf16[2,128,1024]{1,2,0:T(8,128)(2,1)} %collective-permute-done.2), channel_id=1, source_target_pairs={{0,4},{1,5},{2,6},{3,7},{4,8},{5,9},{6,10},{7,11},{8,12},{9,13},{1... | collective-permute-start | bytes 1572872 | tf_op jit(solution)/shard_map/ppermute | solution.py:17
  48.6 1.8 constant_dynamic-update-slice_fusion.3
  51.9 6.5 %collective-permute-done.3 = bf16[2,128,1024]{1,2,0:T(8,128)(2,1)} collective-permute-done((bf16[2,128,1024]{1,2,0:T(8,128)(2,1)}, bf16[2,128,1024]{1,2,0:T(8,128)(2,1)}, u32[]{:S(2)}, u32[]{:S(2)}) %collective-permute-start.3) | collective-permute-done | bytes 524320 | tf_op jit(solution)/shard_map/ppermute | solution.py:17
  58.4 1.8 fusion.40
  65.4 3.4 %collective-permute-start.7 = (bf16[2,128,1024]{1,2,0:T(8,128)(2,1)}, bf16[2,128,1024]{1,2,0:T(8,128)(2,1)}, u32[]{:S(2)}, u32[]{:S(2)}) collective-permute-start(bf16[2,128,1024]{1,2,0:T(8,128)(2,1)} %pad_maximum_fusion.5), channel_id=1, source_target_pairs={{0,8},{1,9},{2,10},{3,11},{4,12},{5,13},{6,14},{7,15},{16,24},{17,... | collective-permute-start | bytes 1572872 | tf_op jit(solution)/shard_map/ppermute | solution.py:17
  68.9 1.9 collective-permute-start.6
  70.8 1.9 %collective-permute-start.5 = (bf16[2,128,1024]{1,2,0:T(8,128)(2,1)}, bf16[2,128,1024]{1,2,0:T(8,128)(2,1)}, u32[]{:S(2)}, u32[]{:S(2)}) collective-permute-start(bf16[2,128,1024]{1,2,0:T(8,128)(2,1)} %pad_maximum_fusion.5), channel_id=1, source_target_pairs={{0,2},{1,3},{2,4},{3,5},{4,6},{5,7},{6,8},{7,9},{8,10},{9,11},{10,... | collective-permute-start | bytes 1572872 | tf_op jit(solution)/shard_map/ppermute | solution.py:17
  79.2 3.4 %collective-permute-start.9 = (bf16[2,128,8,128]{1,3,2,0:T(8,128)(2,1)}, bf16[2,128,8,128]{1,3,2,0:T(8,128)(2,1)}, u32[]{:S(2)}, u32[]{:S(2)}) collective-permute-start(bf16[2,128,8,128]{1,3,2,0:T(8,128)(2,1)} %pad_maximum_fusion.9), channel_id=1, source_target_pairs={{2,0},{3,1},{4,2},{5,3},{6,4},{7,5},{8,6},{9,7},{10,8},{11,9},{12,... | collective-permute-start | bytes 1572872 | tf_op jit(solution)/shard_map/ppermute | solution.py:17
  88.6 3.4 %collective-permute-start.4 = (bf16[2,128,1024]{1,2,0:T(8,128)(2,1)}, bf16[2,128,1024]{1,2,0:T(8,128)(2,1)}, u32[]{:S(2)}, u32[]{:S(2)}) collective-permute-start(bf16[2,128,1024]{1,2,0:T(8,128)(2,1)} %pad_maximum_fusion.5), channel_id=1, source_target_pairs={{0,1},{1,2},{2,3},{3,4},{4,5},{5,6},{6,7},{7,8},{8,9},{9,10},{10,1... | collective-permute-start | bytes 1572872 | tf_op jit(solution)/shard_map/ppermute | solution.py:17
  91.9 4.5 %collective-permute-start.10 = (bf16[2,128,8,128]{1,3,2,0:T(8,128)(2,1)}, bf16[2,128,8,128]{1,3,2,0:T(8,128)(2,1)}, u32[]{:S(2)}, u32[]{:S(2)}) collective-permute-start(bf16[2,128,8,128]{1,3,2,0:T(8,128)(2,1)} %pad_maximum_fusion.10), channel_id=1, source_target_pairs={{4,0},{5,1},{6,2},{7,3},{8,4},{9,5},{10,6},{11,7},{12,8},{13,9},{1... | collective-permute-start | bytes 1572872 | tf_op jit(solution)/shard_map/ppermute | solution.py:17
  97.7 4.9 %collective-permute-done.6 = bf16[2,128,1024]{1,2,0:T(8,128)(2,1)} collective-permute-done((bf16[2,128,1024]{1,2,0:T(8,128)(2,1)}, bf16[2,128,1024]{1,2,0:T(8,128)(2,1)}, u32[]{:S(2)}, u32[]{:S(2)}) %collective-permute-start.6) | collective-permute-done | bytes 524320 | tf_op jit(solution)/shard_map/ppermute | solution.py:17
  105.2 7.9 %collective-permute-done.5 = bf16[2,128,1024]{1,2,0:T(8,128)(2,1)} collective-permute-done((bf16[2,128,1024]{1,2,0:T(8,128)(2,1)}, bf16[2,128,1024]{1,2,0:T(8,128)(2,1)}, u32[]{:S(2)}, u32[]{:S(2)}) %collective-permute-start.5) | collective-permute-done | bytes 524320 | tf_op jit(solution)/shard_map/ppermute | solution.py:17
  113.0 2.1 %collective-permute-start.8 = (bf16[2,128,8,128]{1,3,2,0:T(8,128)(2,1)}, bf16[2,128,8,128]{1,3,2,0:T(8,128)(2,1)}, u32[]{:S(2)}, u32[]{:S(2)}) collective-permute-start(bf16[2,128,8,128]{1,3,2,0:T(8,128)(2,1)} %pad_maximum_fusion.8), channel_id=1, source_target_pairs={{1,0},{2,1},{3,2},{4,3},{5,4},{6,5},{7,6},{8,7},{9,8},{10,9},{11,1... | collective-permute-start | bytes 1572872 | tf_op jit(solution)/shard_map/ppermute | solution.py:17
  115.1 1.8 fusion.38
  118.6 1.9 fusion.39
  130.3 1.9 collective-permute-start.13
  134.7 1.9 collective-permute-start.14
  138.0 1.9 %collective-permute-start.12 = (bf16[2,128,8,128]{1,3,2,0:T(8,128)(2,1)}, bf16[2,128,8,128]{1,3,2,0:T(8,128)(2,1)}, u32[]{:S(2)}, u32[]{:S(2)}) collective-permute-start(bf16[2,128,8,128]{1,3,2,0:T(8,128)(2,1)} %pad_maximum_fusion.12), channel_id=1, source_target_pairs={{1,0},{2,1},{3,2},{4,3},{5,4},{6,5},{7,6},{8,7},{9,8},{10,9},{11,1... | collective-permute-start | bytes 1572872 | tf_op jit(solution)/shard_map/ppermute | solution.py:17
  139.9 2.6 %fusion.27 = (bf16[128,8,128]{0,2,1:T(8,128)(2,1)}, f32[128,8,128]{0,2,1:T(8,128)S(1)}) fusion(bf16[128,8,128]{0,2,1:T(8,128)(2,1)S(1)} %copy-done.10, bf16[2,128,8,128]{1,3,2,0:T(8,128)(2,1)} %collective-permute-done.11, bf16[2,128,8,128]{1,3,2,0:T(8,128)(2,1)} %collective-permute-done.10, bf16[2,128,8,128]{1,3,2,0:T(8,128)(2,1)} %collective-permute-done.9, ...), kind=kLoop, calls=%fused_computation.70 | loop fusion | flops 2490368 | bytes 3407872 | tf_op jit(solution)/shard_map/convert.23
  142.5 1.8 copy.132
  145.2 1.9 pad_maximum_fusion.6
  148.5 11.8 %collective-permute-done.15 = bf16[2,128,8,128]{1,3,2,0:T(8,128)(2,1)} collective-permute-done((bf16[2,128,8,128]{1,3,2,0:T(8,128)(2,1)}, bf16[2,128,8,128]{1,3,2,0:T(8,128)(2,1)}, u32[]{:S(2)}, u32[]{:S(2)}) %collective-permute-start.15) | collective-permute-done | bytes 524320 | tf_op jit(solution)/shard_map/ppermute | solution.py:17
  160.3 26.5 %collective-permute-done.12 = bf16[2,128,8,128]{1,3,2,0:T(8,128)(2,1)} collective-permute-done((bf16[2,128,8,128]{1,3,2,0:T(8,128)(2,1)}, bf16[2,128,8,128]{1,3,2,0:T(8,128)(2,1)}, u32[]{:S(2)}, u32[]{:S(2)}) %collective-permute-start.12) | collective-permute-done | bytes 524320 | tf_op jit(solution)/shard_map/ppermute | solution.py:17
  186.8 1.9 %fusion.26 = (bf16[128,8,128]{0,2,1:T(8,128)(2,1)S(1)}, f32[128,8,128]{0,2,1:T(8,128)S(1)}) fusion(bf16[128,8,128]{0,2,1:T(8,128)(2,1)S(1)} %copy-done.13, bf16[2,128,8,128]{1,3,2,0:T(8,128)(2,1)} %collective-permute-done.15, bf16[2,128,8,128]{1,3,2,0:T(8,128)(2,1)} %collective-permute-done.14, bf16[2,128,8,128]{1,3,2,0:T(8,128)(2,1)} %collective-permute-done.13, ...), kind=kLoop, calls=%fused_computation.65 | loop fusion | flops 2490368 | bytes 3407872 | tf_op jit(solution)/shard_map/convert.22
  (149 shorter events, 55.5 us)
Async XLA Ops:
  0.6 3.1 %copy-start.14 = (bf16[128,2048]{1,0:T(8,128)(2,1)S(1)}, bf16[128,2048]{1,0:T(8,128)(2,1)}, u32[]{:S(2)}) copy-start(bf16[128,2048]{1,0:T(8,128)(2,1)} %param.7) | copy-start | bytes 1572868
  6.2 12.3 %copy-start.16 = (bf16[128,2048]{1,0:T(8,128)(2,1)S(1)}, bf16[128,2048]{1,0:T(8,128)(2,1)}, u32[]{:S(2)}) copy-start(bf16[128,2048]{1,0:T(8,128)(2,1)} %param.10) | copy-start | bytes 1572868
  6.2 12.2 %copy-start.17 = (s32[4]{0:T(128)S(1)}, s32[4]{0:T(128)}, u32[]{:S(2)}) copy-start(s32[4]{0:T(128)} %constant.35) | copy-start | bytes 52
  7.1 35.1 %collective-permute-start.2 = (bf16[2,128,1024]{1,2,0:T(8,128)(2,1)}, bf16[2,128,1024]{1,2,0:T(8,128)(2,1)}, u32[]{:S(2)}, u32[]{:S(2)}) collective-permute-start(bf16[2,128,1024]{1,2,0:T(8,128)(2,1)} %pad_maximum_fusion.3), channel_id=1, source_target_pairs={{0,4},{1,5},{2,6},{3,7},{4,8},{5,9},{6,10},{7,11},{8,12},{9,13},{1... | collective-permute-start | bytes 1572872 | tf_op jit(solution)/shard_map/ppermute | solution.py:17
  10.3 22.1 %collective-permute-start.1 = (bf16[2,128,1024]{1,2,0:T(8,128)(2,1)}, bf16[2,128,1024]{1,2,0:T(8,128)(2,1)}, u32[]{:S(2)}, u32[]{:S(2)}) collective-permute-start(bf16[2,128,1024]{1,2,0:T(8,128)(2,1)} %pad_maximum_fusion.3), channel_id=1, source_target_pairs={{0,2},{1,3},{2,4},{3,5},{4,6},{5,7},{6,8},{7,9},{8,10},{9,11},{10,... | collective-permute-start | bytes 1572872 | tf_op jit(solution)/shard_map/ppermute | solution.py:17
  13.5 25.7 %collective-permute-start = (bf16[2,128,1024]{1,2,0:T(8,128)(2,1)}, bf16[2,128,1024]{1,2,0:T(8,128)(2,1)}, u32[]{:S(2)}, u32[]{:S(2)}) collective-permute-start(bf16[2,128,1024]{1,2,0:T(8,128)(2,1)} %pad_maximum_fusion.3), channel_id=1, source_target_pairs={{0,1},{1,2},{2,3},{3,4},{4,5},{5,6},{6,7},{7,8},{8,9},{9,10},{10,1... | collective-permute-start | bytes 1572872 | tf_op jit(solution)/shard_map/ppermute | solution.py:17
  44.1 6.3 %copy-start.6 = (bf16[1,128,1024]{1,2,0:T(8,128)(2,1)S(1)}, bf16[1,128,1024]{1,2,0:T(8,128)(2,1)}, u32[]{:S(2)}) copy-start(bf16[1,128,1024]{1,2,0:T(8,128)(2,1)} %get-tuple-element.69) | copy-start | bytes 786436
  44.1 14.3 %collective-permute-start.3 = (bf16[2,128,1024]{1,2,0:T(8,128)(2,1)}, bf16[2,128,1024]{1,2,0:T(8,128)(2,1)}, u32[]{:S(2)}, u32[]{:S(2)}) collective-permute-start(bf16[2,128,1024]{1,2,0:T(8,128)(2,1)} %collective-permute-done.2), channel_id=1, source_target_pairs={{0,4},{1,5},{2,6},{3,7},{4,8},{5,9},{6,10},{7,11},{8,12},{9,13},{1... | collective-permute-start | bytes 1572872 | tf_op jit(solution)/shard_map/ppermute | solution.py:17
  48.6 2.6 %copy-start.9 = (bf16[1,128,1024]{1,2,0:T(8,128)(2,1)S(1)}, bf16[1,128,1024]{1,2,0:T(8,128)(2,1)}, u32[]{:S(2)}) copy-start(bf16[1,128,1024]{1,2,0:T(8,128)(2,1)} %get-tuple-element.67) | copy-start | bytes 786436
  62.7 1.3 copy-start.3
  65.4 26.5 %collective-permute-start.7 = (bf16[2,128,1024]{1,2,0:T(8,128)(2,1)}, bf16[2,128,1024]{1,2,0:T(8,128)(2,1)}, u32[]{:S(2)}, u32[]{:S(2)}) collective-permute-start(bf16[2,128,1024]{1,2,0:T(8,128)(2,1)} %pad_maximum_fusion.5), channel_id=1, source_target_pairs={{0,8},{1,9},{2,10},{3,11},{4,12},{5,13},{6,14},{7,15},{16,24},{17,... | collective-permute-start | bytes 1572872 | tf_op jit(solution)/shard_map/ppermute | solution.py:17
  68.9 33.7 %collective-permute-start.6 = (bf16[2,128,1024]{1,2,0:T(8,128)(2,1)}, bf16[2,128,1024]{1,2,0:T(8,128)(2,1)}, u32[]{:S(2)}, u32[]{:S(2)}) collective-permute-start(bf16[2,128,1024]{1,2,0:T(8,128)(2,1)} %pad_maximum_fusion.5), channel_id=1, source_target_pairs={{0,4},{1,5},{2,6},{3,7},{4,8},{5,9},{6,10},{7,11},{8,12},{9,13},{1... | collective-permute-start | bytes 1572872 | tf_op jit(solution)/shard_map/ppermute | solution.py:17
  70.8 42.2 %collective-permute-start.5 = (bf16[2,128,1024]{1,2,0:T(8,128)(2,1)}, bf16[2,128,1024]{1,2,0:T(8,128)(2,1)}, u32[]{:S(2)}, u32[]{:S(2)}) collective-permute-start(bf16[2,128,1024]{1,2,0:T(8,128)(2,1)} %pad_maximum_fusion.5), channel_id=1, source_target_pairs={{0,2},{1,3},{2,4},{3,5},{4,6},{5,7},{6,8},{7,9},{8,10},{9,11},{10,... | collective-permute-start | bytes 1572872 | tf_op jit(solution)/shard_map/ppermute | solution.py:17
  78.4 5.9 %copy-start.4 = (bf16[1,128,8,128]{1,3,2,0:T(8,128)(2,1)S(1)}, bf16[1,128,8,128]{1,3,2,0:T(8,128)(2,1)}, u32[]{:S(2)}) copy-start(bf16[1,128,8,128]{1,3,2,0:T(8,128)(2,1)} %get-tuple-element.25) | copy-start | bytes 786436
  79.2 55.5 %collective-permute-start.9 = (bf16[2,128,8,128]{1,3,2,0:T(8,128)(2,1)}, bf16[2,128,8,128]{1,3,2,0:T(8,128)(2,1)}, u32[]{:S(2)}, u32[]{:S(2)}) collective-permute-start(bf16[2,128,8,128]{1,3,2,0:T(8,128)(2,1)} %pad_maximum_fusion.9), channel_id=1, source_target_pairs={{2,0},{3,1},{4,2},{5,3},{6,4},{7,5},{8,6},{9,7},{10,8},{11,9},{12,... | collective-permute-start | bytes 1572872 | tf_op jit(solution)/shard_map/ppermute | solution.py:17
  88.6 30.1 %collective-permute-start.4 = (bf16[2,128,1024]{1,2,0:T(8,128)(2,1)}, bf16[2,128,1024]{1,2,0:T(8,128)(2,1)}, u32[]{:S(2)}, u32[]{:S(2)}) collective-permute-start(bf16[2,128,1024]{1,2,0:T(8,128)(2,1)} %pad_maximum_fusion.5), channel_id=1, source_target_pairs={{0,1},{1,2},{2,3},{3,4},{4,5},{5,6},{6,7},{7,8},{8,9},{9,10},{10,1... | collective-permute-start | bytes 1572872 | tf_op jit(solution)/shard_map/ppermute | solution.py:17
  91.9 44.7 %collective-permute-start.10 = (bf16[2,128,8,128]{1,3,2,0:T(8,128)(2,1)}, bf16[2,128,8,128]{1,3,2,0:T(8,128)(2,1)}, u32[]{:S(2)}, u32[]{:S(2)}) collective-permute-start(bf16[2,128,8,128]{1,3,2,0:T(8,128)(2,1)} %pad_maximum_fusion.10), channel_id=1, source_target_pairs={{4,0},{5,1},{6,2},{7,3},{8,4},{9,5},{10,6},{11,7},{12,8},{13,9},{1... | collective-permute-start | bytes 1572872 | tf_op jit(solution)/shard_map/ppermute | solution.py:17
  102.6 35.3 %collective-permute-start.11 = (bf16[2,128,8,128]{1,3,2,0:T(8,128)(2,1)}, bf16[2,128,8,128]{1,3,2,0:T(8,128)(2,1)}, u32[]{:S(2)}, u32[]{:S(2)}) collective-permute-start(bf16[2,128,8,128]{1,3,2,0:T(8,128)(2,1)} %pad_maximum_fusion.11), channel_id=1, source_target_pairs={{8,0},{9,1},{10,2},{11,3},{12,4},{13,5},{14,6},{15,7},{24,16},{25,... | collective-permute-start | bytes 1572872 | tf_op jit(solution)/shard_map/ppermute | solution.py:17
  113.0 26.9 %collective-permute-start.8 = (bf16[2,128,8,128]{1,3,2,0:T(8,128)(2,1)}, bf16[2,128,8,128]{1,3,2,0:T(8,128)(2,1)}, u32[]{:S(2)}, u32[]{:S(2)}) collective-permute-start(bf16[2,128,8,128]{1,3,2,0:T(8,128)(2,1)} %pad_maximum_fusion.8), channel_id=1, source_target_pairs={{1,0},{2,1},{3,2},{4,3},{5,4},{6,5},{7,6},{8,7},{9,8},{10,9},{11,1... | collective-permute-start | bytes 1572872 | tf_op jit(solution)/shard_map/ppermute | solution.py:17
  123.2 1.3 copy-start.2
  123.2 1.3 copy-start.8
  123.2 1.4 copy-start.7
  130.3 18.2 %collective-permute-start.13 = (bf16[2,128,8,128]{1,3,2,0:T(8,128)(2,1)}, bf16[2,128,8,128]{1,3,2,0:T(8,128)(2,1)}, u32[]{:S(2)}, u32[]{:S(2)}) collective-permute-start(bf16[2,128,8,128]{1,3,2,0:T(8,128)(2,1)} %pad_maximum_fusion.13), channel_id=1, source_target_pairs={{2,0},{3,1},{4,2},{5,3},{6,4},{7,5},{8,6},{9,7},{10,8},{11,9},{12,... | collective-permute-start | bytes 1572872 | tf_op jit(solution)/shard_map/ppermute | solution.py:17
  133.0 6.9 %copy-start.10 = (bf16[128,8,128]{0,2,1:T(8,128)(2,1)S(1)}, bf16[128,8,128]{0,2,1:T(8,128)(2,1)}, u32[]{:S(2)}) copy-start(bf16[128,8,128]{0,2,1:T(8,128)(2,1)} %get-tuple-element.24) | copy-start | bytes 786436
  133.0 6.9 %copy-start.11 = (bf16[128,8,128]{0,2,1:T(8,128)(2,1)S(1)}, bf16[128,8,128]{0,2,1:T(8,128)(2,1)}, u32[]{:S(2)}) copy-start(bf16[128,8,128]{0,2,1:T(8,128)(2,1)} %get-tuple-element.38) | copy-start | bytes 786436
  134.7 13.8 %collective-permute-start.14 = (bf16[2,128,8,128]{1,3,2,0:T(8,128)(2,1)}, bf16[2,128,8,128]{1,3,2,0:T(8,128)(2,1)}, u32[]{:S(2)}, u32[]{:S(2)}) collective-permute-start(bf16[2,128,8,128]{1,3,2,0:T(8,128)(2,1)} %pad_maximum_fusion.14), channel_id=1, source_target_pairs={{4,0},{5,1},{6,2},{7,3},{8,4},{9,5},{10,6},{11,7},{12,8},{13,9},{1... | collective-permute-start | bytes 1572872 | tf_op jit(solution)/shard_map/ppermute | solution.py:17
  136.6 23.6 %collective-permute-start.15 = (bf16[2,128,8,128]{1,3,2,0:T(8,128)(2,1)}, bf16[2,128,8,128]{1,3,2,0:T(8,128)(2,1)}, u32[]{:S(2)}, u32[]{:S(2)}) collective-permute-start(bf16[2,128,8,128]{1,3,2,0:T(8,128)(2,1)} %pad_maximum_fusion.15), channel_id=1, source_target_pairs={{8,0},{9,1},{10,2},{11,3},{12,4},{13,5},{14,6},{15,7},{24,16},{25,... | collective-permute-start | bytes 1572872 | tf_op jit(solution)/shard_map/ppermute | solution.py:17
  138.0 48.8 %collective-permute-start.12 = (bf16[2,128,8,128]{1,3,2,0:T(8,128)(2,1)}, bf16[2,128,8,128]{1,3,2,0:T(8,128)(2,1)}, u32[]{:S(2)}, u32[]{:S(2)}) collective-permute-start(bf16[2,128,8,128]{1,3,2,0:T(8,128)(2,1)} %pad_maximum_fusion.12), channel_id=1, source_target_pairs={{1,0},{2,1},{3,2},{4,3},{5,4},{6,5},{7,6},{8,7},{9,8},{10,9},{11,1... | collective-permute-start | bytes 1572872 | tf_op jit(solution)/shard_map/ppermute | solution.py:17
  147.1 39.7 %copy-start.12 = (bf16[128,8,128]{0,2,1:T(8,128)(2,1)S(1)}, bf16[128,8,128]{0,2,1:T(8,128)(2,1)}, u32[]{:S(2)}) copy-start(bf16[128,8,128]{0,2,1:T(8,128)(2,1)} %get-tuple-element.43) | copy-start | bytes 786436
  147.1 39.7 %copy-start.13 = (bf16[128,8,128]{0,2,1:T(8,128)(2,1)S(1)}, bf16[128,8,128]{0,2,1:T(8,128)(2,1)}, u32[]{:S(2)}) copy-start(bf16[128,8,128]{0,2,1:T(8,128)(2,1)} %get-tuple-element.29) | copy-start | bytes 786436
  148.5 40.4 %copy-start = (f32[128,8,128]{0,2,1:T(8,128)S(1)}, f32[128,8,128]{0,2,1:T(8,128)}, u32[]{:S(2)}) copy-start(f32[128,8,128]{0,2,1:T(8,128)} %convolution_bitcast_fusion.1) | copy-start | bytes 1572868
  148.5 40.4 %copy-start.1 = (f32[128,8,128]{0,2,1:T(8,128)S(1)}, f32[128,8,128]{0,2,1:T(8,128)}, u32[]{:S(2)}) copy-start(f32[128,8,128]{0,2,1:T(8,128)} %convolution_bitcast_fusion) | copy-start | bytes 1572868
  (2 other events, 2.1 us)

commit v20 on v11

--- a/solution.py
+++ b/solution.py
@@ -69,11 +69,11 @@
     return jnp.transpose(allowed, (0, 2, 1, 3))[:, None]
 
 
-def send_chunk(key_c, value_c, offsets):
+def send_chunk(key_c, value_c, offsets, relay):
     pair = jnp.stack([key_c, value_c])
     received = {0: pair}
     for offset in offsets:
-        if (offset.bit_length() - 1) % 2 == 1:
+        if relay and (offset.bit_length() - 1) % 2 == 1:
             half = offset // 2
             received[offset] = from_behind(received[half], "ctx", half)
         else:
@@ -158,7 +158,7 @@
         key_c, value_c = key_rot[:, cols], values[:, cols]
         if pending:
             key_c, value_c, _ = lax.optimization_barrier((key_c, value_c, pieces[-1][0]))
-        received = send_chunk(key_c, value_c, offsets)
+        received = send_chunk(key_c, value_c, offsets, relay=not pending)
         output, query_grad, own, outgoing = attend_chunk(
             query_rot[:, cols], received, grad_out[:, cols], allowed, offsets, chunk_heads
         )

time: 202 us -> 222 us (1.099)
  waiting for transfers between devices: 89.3 us -> 102 us
  starting transfers between devices: 43.5 us -> 48.8 us
    ppermute x16, waiting for transfers between devices: 89.3 us -> 102 us  [from_behind(): lax.ppermute(value, axis, [(source, source + steps) for source in range(l...]
    ppermute x16, starting transfers between devices: 43.5 us -> 48.8 us  [from_behind(): lax.ppermute(value, axis, [(source, source + steps) for source in range(l...]
    unnamed x97 -> x99, local copies, waits for them, and re-layouts: 8.74 us -> 9.08 us
  transfers between devices with their start and end apart: 16 -> 16, of which waited for: 9 -> 12; matrix products, arithmetic and copies ran while one was open for 11% -> 10% of each run, Pallas kernels for 0% -> 0%
where the time goes in v20:
time: 222 us; the launch traced here: 221 us
  waiting for transfers between devices  102 us (46%)
  starting transfers between devices  48.8 us (22%)
  local copies, waits for them, and re-layouts  41 us (18%)
  other arithmetic  16 us (7%)
  matrix products  10.7 us (5%)
  between operations  2.33 us (1%)
    ppermute x16, waiting for transfers between devices, from_behind(): lax.ppermute(value, axis, [(source, source + steps) for source in range(l...  102 us
    ppermute x16, starting transfers between devices, from_behind(): lax.ppermute(value, axis, [(source, source + steps) for source in range(l...  48.8 us
    slice x8, local copies, waits for them, and re-layouts, attend_chunk(): moved[0].reshape(head_shape)  10.4 us
    unnamed x99, local copies, waits for them, and re-layouts  9.08 us
    another operation x12, local copies, waits for them, and re-layouts, attend_chunk(): jnp.stack([moved[0].reshape(head_shape) for moved in received])[None]  6.43 us
    another operation x8, other arithmetic, attend_chunk(): jnp.stack([key_terms[0, slot_index], value_terms[0, slot_index]])  4.56 us
  transfers between devices with their start and end apart: 16, of which 12 were waited for; matrix products, arithmetic and copies ran while one was open for 10% of the time, Pallas kernels for 0%

profile of v20, /device:TPU:15, one launch (start us, length us, event | category | flops | bytes accessed | tf_op | source)
XLA Modules:
  0.0 220.9 jit_solution(10873480730027335447)
XLA Ops:
  6.7 3.3 %collective-permute-start.2 = (bf16[2,128,768]{1,2,0:T(8,128)(2,1)}, bf16[2,128,768]{1,2,0:T(8,128)(2,1)}, u32[]{:S(2)}, u32[]{:S(2)}) collective-permute-start(bf16[2,128,768]{1,2,0:T(8,128)(2,1)} %pad_maximum_fusion.13), channel_id=1, source_target_pairs={{0,4},{1,5},{2,6},{3,7},{4,8},{5,9},{6,10},{7,11},{8,12},{9,13},{1... | collective-permute-start | bytes 1179656 | tf_op jit(solution)/shard_map/ppermute | solution.py:17
  10.0 4.0 %collective-permute-start = (bf16[2,128,768]{1,2,0:T(8,128)(2,1)}, bf16[2,128,768]{1,2,0:T(8,128)(2,1)S(1)}, u32[]{:S(2)}, u32[]{:S(2)}) collective-permute-start(bf16[2,128,768]{1,2,0:T(8,128)(2,1)} %pad_maximum_fusion.13), channel_id=1, source_target_pairs={{0,1},{1,2},{2,3},{3,4},{4,5},{5,6},{6,7},{7,8},{8,9},{9,10},{10,1... | collective-permute-start | bytes 1179656 | tf_op jit(solution)/shard_map/ppermute | solution.py:17
  19.0 3.2 %collective-permute-start.3 = (bf16[2,128,768]{1,2,0:T(8,128)(2,1)}, bf16[2,128,768]{1,2,0:T(8,128)(2,1)}, u32[]{:S(2)}, u32[]{:S(2)}) collective-permute-start(bf16[2,128,768]{1,2,0:T(8,128)(2,1)} %collective-permute-done.2), channel_id=1, source_target_pairs={{0,4},{1,5},{2,6},{3,7},{4,8},{5,9},{6,10},{7,11},{8,12},{9,13},{1... | collective-permute-start | bytes 1179656 | tf_op jit(solution)/shard_map/ppermute | solution.py:17
  22.2 1.7 fusion.44
  23.9 4.8 %collective-permute-start.1 = (bf16[2,128,768]{1,2,0:T(8,128)(2,1)S(1)}, bf16[2,128,768]{1,2,0:T(8,128)(2,1)}, u32[]{:S(2)}, u32[]{:S(2)}) collective-permute-start(bf16[2,128,768]{1,2,0:T(8,128)(2,1)S(1)} %collective-permute-done), channel_id=1, source_target_pairs={{0,1},{1,2},{2,3},{3,4},{4,5},{5,6},{6,7},{7,8},{8,9},{9,10},{10,1... | collective-permute-start | bytes 1179656 | tf_op jit(solution)/shard_map/ppermute | solution.py:17
  30.0 1.7 fusion.43
  31.9 4.1 %collective-permute-done.1 = bf16[2,128,768]{1,2,0:T(8,128)(2,1)} collective-permute-done((bf16[2,128,768]{1,2,0:T(8,128)(2,1)S(1)}, bf16[2,128,768]{1,2,0:T(8,128)(2,1)}, u32[]{:S(2)}, u32[]{:S(2)}) %collective-permute-start.1) | collective-permute-done | bytes 393248 | tf_op jit(solution)/shard_map/ppermute | solution.py:17
  36.0 1.7 fusion.45
  43.0 1.7 copy.126
  45.9 2.2 %fusion.21 = bf16[1,6,128,5,128]{2,4,3,1,0:T(8,128)(2,1)S(1)} fusion(bf16[5,128,6,128]{1,3,0,2:T(8,128)(2,1)} %copy-done.14, bf16[128,6,128,1]{0,2,3,1:T(8,128)(2,1)} %bitcast.385, f32[6,128,5,128]{1,3,2,0:T(8,128)S(1)} %bitcast.357, f32[6,128]{1,0:T(8,128)S(1)} %bitcast.412, f32[6,128]{1,0:T(8,128)} %copy-done.38, pred[128,5,128]{0,2,1:T(8,128)(4,1)S(1)} %and_bitcast_fusion), kind=kOutput, calls=%fused_computation.29 | convolution fusion | flops 129269760 | bytes 4216832 | tf_op jit(solution)/shard_map/bthd,bnuhd->bhtnu/dot_general | solution.py:105
  51.4 2.2 %collective-permute-start.10 = (bf16[2,128,6,128]{1,3,2,0:T(8,128)(2,1)S(1)}, bf16[2,128,6,128]{1,3,2,0:T(8,128)(2,1)S(1)}, u32[]{:S(2)}, u32[]{:S(2)}) collective-permute-start(bf16[2,128,6,128]{1,3,2,0:T(8,128)(2,1)S(1)} %pad_maximum_fusion.16), channel_id=1, source_target_pairs={{4,0},{5,1},{6,2},{7,3},{8,4},{9,5},{10,6},{11,7},{12,8},{13,9},{1... | collective-permute-start | bytes 1179656 | tf_op jit(solution)/shard_map/ppermute | solution.py:17
  56.0 2.1 collective-permute-start.9
  58.1 4.6 %collective-permute-start.8 = (bf16[2,128,6,128]{1,3,2,0:T(8,128)(2,1)S(1)}, bf16[2,128,6,128]{1,3,2,0:T(8,128)(2,1)S(1)}, u32[]{:S(2)}, u32[]{:S(2)}) collective-permute-start(bf16[2,128,6,128]{1,3,2,0:T(8,128)(2,1)S(1)} %pad_maximum_fusion.14), channel_id=1, source_target_pairs={{1,0},{2,1},{3,2},{4,3},{5,4},{6,5},{7,6},{8,7},{9,8},{10,9},{11,1... | collective-permute-start | bytes 1179656 | tf_op jit(solution)/shard_map/ppermute | solution.py:17
  63.6 6.2 %collective-permute-start.7 = (bf16[2,128,1280]{1,2,0:T(8,128)(2,1)}, bf16[2,128,1280]{1,2,0:T(8,128)(2,1)}, u32[]{:S(2)}, u32[]{:S(2)}) collective-permute-start(bf16[2,128,1280]{1,2,0:T(8,128)(2,1)} %pad_maximum_fusion.2), channel_id=1, source_target_pairs={{0,8},{1,9},{2,10},{3,11},{4,12},{5,13},{6,14},{7,15},{16,24},{17,... | collective-permute-start | bytes 1966088 | tf_op jit(solution)/shard_map/ppermute | solution.py:17
  71.9 1.9 collective-permute-start.6
  73.8 1.9 collective-permute-start.5
  75.8 8.1 %collective-permute-done.9 = bf16[2,128,6,128]{1,3,2,0:T(8,128)(2,1)S(1)} collective-permute-done((bf16[2,128,6,128]{1,3,2,0:T(8,128)(2,1)S(1)}, bf16[2,128,6,128]{1,3,2,0:T(8,128)(2,1)S(1)}, u32[]{:S(2)}, u32[]{:S(2)}) %collective-permute-start.9) | collective-permute-done | bytes 393248 | tf_op jit(solution)/shard_map/ppermute | solution.py:17
  83.9 6.2 %collective-permute-start.4 = (bf16[2,128,1280]{1,2,0:T(8,128)(2,1)}, bf16[2,128,1280]{1,2,0:T(8,128)(2,1)}, u32[]{:S(2)}, u32[]{:S(2)}) collective-permute-start(bf16[2,128,1280]{1,2,0:T(8,128)(2,1)} %pad_maximum_fusion.2), channel_id=1, source_target_pairs={{0,1},{1,2},{2,3},{3,4},{4,5},{5,6},{6,7},{7,8},{8,9},{9,10},{10,1... | collective-permute-start | bytes 1966088 | tf_op jit(solution)/shard_map/ppermute | solution.py:17
  90.1 2.3 %collective-permute-done.8 = bf16[2,128,6,128]{1,3,2,0:T(8,128)(2,1)S(1)} collective-permute-done((bf16[2,128,6,128]{1,3,2,0:T(8,128)(2,1)S(1)}, bf16[2,128,6,128]{1,3,2,0:T(8,128)(2,1)S(1)}, u32[]{:S(2)}, u32[]{:S(2)}) %collective-permute-start.8) | collective-permute-done | bytes 393248 | tf_op jit(solution)/shard_map/ppermute | solution.py:17
  93.6 3.6 %collective-permute-done.7 = bf16[2,128,1280]{1,2,0:T(8,128)(2,1)} collective-permute-done((bf16[2,128,1280]{1,2,0:T(8,128)(2,1)}, bf16[2,128,1280]{1,2,0:T(8,128)(2,1)}, u32[]{:S(2)}, u32[]{:S(2)}) %collective-permute-start.7) | collective-permute-done | bytes 655392 | tf_op jit(solution)/shard_map/ppermute | solution.py:17
  98.3 12.9 %collective-permute-done.6 = bf16[2,128,1280]{1,2,0:T(8,128)(2,1)} collective-permute-done((bf16[2,128,1280]{1,2,0:T(8,128)(2,1)}, bf16[2,128,1280]{1,2,0:T(8,128)(2,1)}, u32[]{:S(2)}, u32[]{:S(2)}) %collective-permute-start.6) | collective-permute-done | bytes 655392 | tf_op jit(solution)/shard_map/ppermute | solution.py:17
  114.2 11.1 %collective-permute-done.5 = bf16[2,128,1280]{1,2,0:T(8,128)(2,1)} collective-permute-done((bf16[2,128,1280]{1,2,0:T(8,128)(2,1)}, bf16[2,128,1280]{1,2,0:T(8,128)(2,1)}, u32[]{:S(2)}, u32[]{:S(2)}) %collective-permute-start.5) | collective-permute-done | bytes 655392 | tf_op jit(solution)/shard_map/ppermute | solution.py:17
  127.3 5.0 %collective-permute-done.4 = bf16[2,128,1280]{1,2,0:T(8,128)(2,1)} collective-permute-done((bf16[2,128,1280]{1,2,0:T(8,128)(2,1)}, bf16[2,128,1280]{1,2,0:T(8,128)(2,1)}, u32[]{:S(2)}, u32[]{:S(2)}) %collective-permute-start.4) | collective-permute-done | bytes 655392 | tf_op jit(solution)/shard_map/ppermute | solution.py:17
  132.3 1.8 fusion.41
  134.2 1.9 copy.120
  149.1 1.9 copy.127
  152.2 1.9 collective-permute-start.14
  156.7 1.9 collective-permute-start.13
  158.7 1.9 collective-permute-start.12
  162.6 22.0 %collective-permute-done.14 = bf16[2,128,10,128]{1,3,2,0:T(8,128)(2,1)S(1)} collective-permute-done((bf16[2,128,10,128]{1,3,2,0:T(8,128)(2,1)S(1)}, bf16[2,128,10,128]{1,3,2,0:T(8,128)(2,1)S(1)}, u32[]{:S(2)}, u32[]{:S(2)}) %collective-permute-start.14) | collective-permute-done | bytes 655392 | tf_op jit(solution)/shard_map/ppermute | solution.py:17
  184.7 19.2 %collective-permute-done.13 = bf16[2,128,10,128]{1,3,2,0:T(8,128)(2,1)S(1)} collective-permute-done((bf16[2,128,10,128]{1,3,2,0:T(8,128)(2,1)S(1)}, bf16[2,128,10,128]{1,3,2,0:T(8,128)(2,1)S(1)}, u32[]{:S(2)}, u32[]{:S(2)}) %collective-permute-start.13) | collective-permute-done | bytes 655392 | tf_op jit(solution)/shard_map/ppermute | solution.py:17
  203.9 12.4 %collective-permute-done.12 = bf16[2,128,10,128]{1,3,2,0:T(8,128)(2,1)S(1)} collective-permute-done((bf16[2,128,10,128]{1,3,2,0:T(8,128)(2,1)S(1)}, bf16[2,128,10,128]{1,3,2,0:T(8,128)(2,1)S(1)}, u32[]{:S(2)}, u32[]{:S(2)}) %collective-permute-start.12) | collective-permute-done | bytes 655392 | tf_op jit(solution)/shard_map/ppermute | solution.py:17
  (202 shorter events, 56.7 us)
Async XLA Ops:
  5.6 9.1 %copy-start.39 = (s32[4]{0:T(128)S(1)}, s32[4]{0:T(128)}, u32[]{:S(2)}) copy-start(s32[4]{0:T(128)} %constant.36) | copy-start | bytes 52
  6.7 9.1 %slice-start.1 = ((bf16[128,2048]{1,0:T(8,128)(2,1)}), bf16[128,768]{1,0:T(8,128)(2,1)S(1)}, s32[]{:S(2)}) async-start(bf16[128,2048]{1,0:T(8,128)(2,1)} %param.10), calls=%async_computation.1 | async-start | bytes 393216 | tf_op jit(solution)/shard_map/slice | solution.py:163
  6.7 12.3 %collective-permute-start.2 = (bf16[2,128,768]{1,2,0:T(8,128)(2,1)}, bf16[2,128,768]{1,2,0:T(8,128)(2,1)}, u32[]{:S(2)}, u32[]{:S(2)}) collective-permute-start(bf16[2,128,768]{1,2,0:T(8,128)(2,1)} %pad_maximum_fusion.13), channel_id=1, source_target_pairs={{0,4},{1,5},{2,6},{3,7},{4,8},{5,9},{6,10},{7,11},{8,12},{9,13},{1... | collective-permute-start | bytes 1179656 | tf_op jit(solution)/shard_map/ppermute | solution.py:17
  10.0 13.9 %collective-permute-start = (bf16[2,128,768]{1,2,0:T(8,128)(2,1)}, bf16[2,128,768]{1,2,0:T(8,128)(2,1)S(1)}, u32[]{:S(2)}, u32[]{:S(2)}) collective-permute-start(bf16[2,128,768]{1,2,0:T(8,128)(2,1)} %pad_maximum_fusion.13), channel_id=1, source_target_pairs={{0,1},{1,2},{2,3},{3,4},{4,5},{5,6},{6,7},{7,8},{8,9},{9,10},{10,1... | collective-permute-start | bytes 1179656 | tf_op jit(solution)/shard_map/ppermute | solution.py:17
  15.0 124.2 %copy-start.2 = (bf16[128,1280]{0,1:T(8,128)(2,1)}, bf16[128,1280]{0,1:T(8,128)(2,1)S(1)}, u32[]{:S(2)}) copy-start(bf16[128,1280]{0,1:T(8,128)(2,1)S(1)} %slice.315) | copy-start | bytes 983044
  19.0 11.0 %collective-permute-start.3 = (bf16[2,128,768]{1,2,0:T(8,128)(2,1)}, bf16[2,128,768]{1,2,0:T(8,128)(2,1)}, u32[]{:S(2)}, u32[]{:S(2)}) collective-permute-start(bf16[2,128,768]{1,2,0:T(8,128)(2,1)} %collective-permute-done.2), channel_id=1, source_target_pairs={{0,4},{1,5},{2,6},{3,7},{4,8},{5,9},{6,10},{7,11},{8,12},{9,13},{1... | collective-permute-start | bytes 1179656 | tf_op jit(solution)/shard_map/ppermute | solution.py:17
  23.9 12.1 %collective-permute-start.1 = (bf16[2,128,768]{1,2,0:T(8,128)(2,1)S(1)}, bf16[2,128,768]{1,2,0:T(8,128)(2,1)}, u32[]{:S(2)}, u32[]{:S(2)}) collective-permute-start(bf16[2,128,768]{1,2,0:T(8,128)(2,1)S(1)} %collective-permute-done), channel_id=1, source_target_pairs={{0,1},{1,2},{2,3},{3,4},{4,5},{5,6},{6,7},{7,8},{8,9},{9,10},{10,1... | collective-permute-start | bytes 1179656 | tf_op jit(solution)/shard_map/ppermute | solution.py:17
  28.8 9.1 %copy-start.12 = (bf16[5,128,6,128]{1,3,0,2:T(8,128)(2,1)}, bf16[5,128,6,128]{1,3,0,2:T(8,128)(2,1)S(1)}, u32[]{:S(2)}) copy-start(bf16[5,128,6,128]{1,3,0,2:T(8,128)(2,1)S(1)} %constant_dynamic-update-slice_fusion.3) | copy-start | bytes 2949124
  48.6 7.2 %copy-start.30 = (bf16[1,128,6,128]{1,3,2,0:T(8,128)(2,1)S(1)}, bf16[1,128,6,128]{1,3,2,0:T(8,128)(2,1)}, u32[]{:S(2)}) copy-start(bf16[1,128,6,128]{1,3,2,0:T(8,128)(2,1)} %get-tuple-element.33) | copy-start | bytes 589828
  49.5 8.5 %copy-start.29 = (bf16[1,128,6,128]{1,3,2,0:T(8,128)(2,1)S(1)}, bf16[1,128,6,128]{1,3,2,0:T(8,128)(2,1)}, u32[]{:S(2)}) copy-start(bf16[1,128,6,128]{1,3,2,0:T(8,128)(2,1)} %get-tuple-element.34) | copy-start | bytes 589828
  49.5 13.2 %copy-start.5 = (bf16[128,1280]{0,1:T(8,128)(2,1)S(1)}, bf16[128,1280]{0,1:T(8,128)(2,1)}, u32[]{:S(2)}) copy-start(bf16[128,1280]{0,1:T(8,128)(2,1)} %copy.193) | copy-start | bytes 983044
  51.4 18.5 %copy-start.21 = (bf16[1,128,10,128]{3,1,0,2:T(8,128)(2,1)S(1)}, bf16[1,128,10,128]{3,1,0,2:T(8,128)(2,1)}, u32[]{:S(2)}) copy-start(bf16[1,128,10,128]{3,1,0,2:T(8,128)(2,1)} %copy.119) | copy-start | bytes 983044
  51.4 20.5 %collective-permute-start.10 = (bf16[2,128,6,128]{1,3,2,0:T(8,128)(2,1)S(1)}, bf16[2,128,6,128]{1,3,2,0:T(8,128)(2,1)S(1)}, u32[]{:S(2)}, u32[]{:S(2)}) collective-permute-start(bf16[2,128,6,128]{1,3,2,0:T(8,128)(2,1)S(1)} %pad_maximum_fusion.16), channel_id=1, source_target_pairs={{4,0},{5,1},{6,2},{7,3},{8,4},{9,5},{10,6},{11,7},{12,8},{13,9},{1... | collective-permute-start | bytes 1179656 | tf_op jit(solution)/shard_map/ppermute | solution.py:17
  54.6 19.2 %collective-permute-start.11 = (bf16[2,128,6,128]{1,3,2,0:T(8,128)(2,1)S(1)}, bf16[2,128,6,128]{1,3,2,0:T(8,128)(2,1)S(1)}, u32[]{:S(2)}, u32[]{:S(2)}) collective-permute-start(bf16[2,128,6,128]{1,3,2,0:T(8,128)(2,1)S(1)} %pad_maximum_fusion.17), channel_id=1, source_target_pairs={{8,0},{9,1},{10,2},{11,3},{12,4},{13,5},{14,6},{15,7},{24,16},{25,... | collective-permute-start | bytes 1179656 | tf_op jit(solution)/shard_map/ppermute | solution.py:17
  55.9 14.8 %copy-start.1 = (bf16[1,6,128,5,128]{2,4,3,1,0:T(8,128)(2,1)S(1)}, bf16[1,6,128,5,128]{2,4,3,1,0:T(8,128)(2,1)}, u32[]{:S(2)}) copy-start(bf16[1,6,128,5,128]{2,4,3,1,0:T(8,128)(2,1)} %copy-done) | copy-start | bytes 2949124
  56.0 27.9 %collective-permute-start.9 = (bf16[2,128,6,128]{1,3,2,0:T(8,128)(2,1)S(1)}, bf16[2,128,6,128]{1,3,2,0:T(8,128)(2,1)S(1)}, u32[]{:S(2)}, u32[]{:S(2)}) collective-permute-start(bf16[2,128,6,128]{1,3,2,0:T(8,128)(2,1)S(1)} %pad_maximum_fusion.15), channel_id=1, source_target_pairs={{2,0},{3,1},{4,2},{5,3},{6,4},{7,5},{8,6},{9,7},{10,8},{11,9},{12,... | collective-permute-start | bytes 1179656 | tf_op jit(solution)/shard_map/ppermute | solution.py:17
  58.1 34.4 %collective-permute-start.8 = (bf16[2,128,6,128]{1,3,2,0:T(8,128)(2,1)S(1)}, bf16[2,128,6,128]{1,3,2,0:T(8,128)(2,1)S(1)}, u32[]{:S(2)}, u32[]{:S(2)}) collective-permute-start(bf16[2,128,6,128]{1,3,2,0:T(8,128)(2,1)S(1)} %pad_maximum_fusion.14), channel_id=1, source_target_pairs={{1,0},{2,1},{3,2},{4,3},{5,4},{6,5},{7,6},{8,7},{9,8},{10,9},{11,1... | collective-permute-start | bytes 1179656 | tf_op jit(solution)/shard_map/ppermute | solution.py:17
  63.6 28.8 %copy-start.28 = (bf16[128,6,128]{0,2,1:T(8,128)(2,1)S(1)}, bf16[128,6,128]{0,2,1:T(8,128)(2,1)}, u32[]{:S(2)}) copy-start(bf16[128,6,128]{0,2,1:T(8,128)(2,1)} %get-tuple-element.30) | copy-start | bytes 589828
  63.6 33.6 %collective-permute-start.7 = (bf16[2,128,1280]{1,2,0:T(8,128)(2,1)}, bf16[2,128,1280]{1,2,0:T(8,128)(2,1)}, u32[]{:S(2)}, u32[]{:S(2)}) collective-permute-start(bf16[2,128,1280]{1,2,0:T(8,128)(2,1)} %pad_maximum_fusion.2), channel_id=1, source_target_pairs={{0,8},{1,9},{2,10},{3,11},{4,12},{5,13},{6,14},{7,15},{16,24},{17,... | collective-permute-start | bytes 1966088 | tf_op jit(solution)/shard_map/ppermute | solution.py:17
  71.9 39.3 %collective-permute-start.6 = (bf16[2,128,1280]{1,2,0:T(8,128)(2,1)}, bf16[2,128,1280]{1,2,0:T(8,128)(2,1)}, u32[]{:S(2)}, u32[]{:S(2)}) collective-permute-start(bf16[2,128,1280]{1,2,0:T(8,128)(2,1)} %pad_maximum_fusion.2), channel_id=1, source_target_pairs={{0,4},{1,5},{2,6},{3,7},{4,8},{5,9},{6,10},{7,11},{8,12},{9,13},{1... | collective-permute-start | bytes 1966088 | tf_op jit(solution)/shard_map/ppermute | solution.py:17
  73.8 51.5 %collective-permute-start.5 = (bf16[2,128,1280]{1,2,0:T(8,128)(2,1)}, bf16[2,128,1280]{1,2,0:T(8,128)(2,1)}, u32[]{:S(2)}, u32[]{:S(2)}) collective-permute-start(bf16[2,128,1280]{1,2,0:T(8,128)(2,1)} %pad_maximum_fusion.2), channel_id=1, source_target_pairs={{0,2},{1,3},{2,4},{3,5},{4,6},{5,7},{6,8},{7,9},{8,10},{9,11},{10,... | collective-permute-start | bytes 1966088 | tf_op jit(solution)/shard_map/ppermute | solution.py:17
  83.9 48.5 %collective-permute-start.4 = (bf16[2,128,1280]{1,2,0:T(8,128)(2,1)}, bf16[2,128,1280]{1,2,0:T(8,128)(2,1)}, u32[]{:S(2)}, u32[]{:S(2)}) collective-permute-start(bf16[2,128,1280]{1,2,0:T(8,128)(2,1)} %pad_maximum_fusion.2), channel_id=1, source_target_pairs={{0,1},{1,2},{2,3},{3,4},{4,5},{5,6},{6,7},{7,8},{8,9},{9,10},{10,1... | collective-permute-start | bytes 1966088 | tf_op jit(solution)/shard_map/ppermute | solution.py:17
  150.9 7.7 %copy-start.17 = (bf16[1,128,10,128]{1,3,2,0:T(8,128)(2,1)S(1)}, bf16[1,128,10,128]{1,3,2,0:T(8,128)(2,1)}, u32[]{:S(2)}) copy-start(bf16[1,128,10,128]{1,3,2,0:T(8,128)(2,1)} %get-tuple-element.14) | copy-start | bytes 983044
  150.9 7.7 %copy-start.19 = (bf16[1,128,10,128]{1,3,2,0:T(8,128)(2,1)S(1)}, bf16[1,128,10,128]{1,3,2,0:T(8,128)(2,1)}, u32[]{:S(2)}) copy-start(bf16[1,128,10,128]{1,3,2,0:T(8,128)(2,1)} %get-tuple-element.15) | copy-start | bytes 983044
  152.2 32.5 %collective-permute-start.14 = (bf16[2,128,10,128]{1,3,2,0:T(8,128)(2,1)S(1)}, bf16[2,128,10,128]{1,3,2,0:T(8,128)(2,1)S(1)}, u32[]{:S(2)}, u32[]{:S(2)}) collective-permute-start(bf16[2,128,10,128]{1,3,2,0:T(8,128)(2,1)S(1)} %pad_maximum_fusion.5), channel_id=1, source_target_pairs={{4,0},{5,1},{6,2},{7,3},{8,4},{9,5},{10,6},{11,7},{12,8},{13,9},{1... | collective-permute-start | bytes 1966088 | tf_op jit(solution)/shard_map/ppermute | solution.py:17
  154.1 6.6 %copy-start.23 = (bf16[128,1280]{1,0:T(8,128)(2,1)S(1)}, bf16[128,1280]{1,0:T(8,128)(2,1)}, u32[]{:S(2)}) copy-start(bf16[128,1280]{1,0:T(8,128)(2,1)} %copy.127) | copy-start | bytes 983044
  155.3 29.3 %collective-permute-start.15 = (bf16[2,128,10,128]{1,3,2,0:T(8,128)(2,1)S(1)}, bf16[2,128,10,128]{1,3,2,0:T(8,128)(2,1)S(1)}, u32[]{:S(2)}, u32[]{:S(2)}) collective-permute-start(bf16[2,128,10,128]{1,3,2,0:T(8,128)(2,1)S(1)} %pad_maximum_fusion.6), channel_id=1, source_target_pairs={{8,0},{9,1},{10,2},{11,3},{12,4},{13,5},{14,6},{15,7},{24,16},{25,... | collective-permute-start | bytes 1966088 | tf_op jit(solution)/shard_map/ppermute | solution.py:17
  156.7 47.2 %collective-permute-start.13 = (bf16[2,128,10,128]{1,3,2,0:T(8,128)(2,1)S(1)}, bf16[2,128,10,128]{1,3,2,0:T(8,128)(2,1)S(1)}, u32[]{:S(2)}, u32[]{:S(2)}) collective-permute-start(bf16[2,128,10,128]{1,3,2,0:T(8,128)(2,1)S(1)} %pad_maximum_fusion.4), channel_id=1, source_target_pairs={{2,0},{3,1},{4,2},{5,3},{6,4},{7,5},{8,6},{9,7},{10,8},{11,9},{12,... | collective-permute-start | bytes 1966088 | tf_op jit(solution)/shard_map/ppermute | solution.py:17
  158.7 57.6 %collective-permute-start.12 = (bf16[2,128,10,128]{1,3,2,0:T(8,128)(2,1)S(1)}, bf16[2,128,10,128]{1,3,2,0:T(8,128)(2,1)S(1)}, u32[]{:S(2)}, u32[]{:S(2)}) collective-permute-start(bf16[2,128,10,128]{1,3,2,0:T(8,128)(2,1)S(1)} %pad_maximum_fusion.3), channel_id=1, source_target_pairs={{1,0},{2,1},{3,2},{4,3},{5,4},{6,5},{7,6},{8,7},{9,8},{10,9},{11,1... | collective-permute-start | bytes 1966088 | tf_op jit(solution)/shard_map/ppermute | solution.py:17
  162.2 54.1 %copy-start.15 = (bf16[128,10,128]{0,2,1:T(8,128)(2,1)S(1)}, bf16[128,10,128]{0,2,1:T(8,128)(2,1)}, u32[]{:S(2)}) copy-start(bf16[128,10,128]{0,2,1:T(8,128)(2,1)} %get-tuple-element.10) | copy-start | bytes 983044
  162.2 54.1 %copy-start.16 = (bf16[128,10,128]{0,2,1:T(8,128)(2,1)S(1)}, bf16[128,10,128]{0,2,1:T(8,128)(2,1)}, u32[]{:S(2)}) copy-start(bf16[128,10,128]{0,2,1:T(8,128)(2,1)} %get-tuple-element.17) | copy-start | bytes 983044
  162.6 54.4 %copy-start.11 = (f32[128,6,128]{0,2,1:T(8,128)S(1)}, f32[128,6,128]{0,2,1:T(8,128)}, u32[]{:S(2)}) copy-start(f32[128,6,128]{0,2,1:T(8,128)} %get-tuple-element.21) | copy-start | bytes 1179652
  (27 other events, 62.0 us)

commit v21 on v20

--- a/solution.py
+++ b/solution.py
@@ -8,7 +8,7 @@
 HEADS = 16
 HEAD_DIM = 128
 BLOCK = 128
-CHUNK_HEADS = (6, 10)
+CHUNK_HEADS = (8, 4, 4)
 
 
 def from_behind(value, axis, steps):

time: 222 us -> 187 us (0.84)
  waiting for transfers between devices: 102 us -> 22.5 us
  starting transfers between devices: 48.8 us -> 65.2 us
  other arithmetic: 16 us -> 30 us
  local copies, waits for them, and re-layouts: 41 us -> 54.3 us
    ppermute x16 -> x24, waiting for transfers between devices: 102 us -> 22.5 us  [from_behind(): lax.ppermute(value, axis, [(source, source + steps) for source in range(l...]
    ppermute x16 -> x24, starting transfers between devices: 48.8 us -> 65.2 us  [from_behind(): lax.ppermute(value, axis, [(source, source + steps) for source in range(l...]
    another operation x8 -> x12, other arithmetic: 4.56 us -> 15 us  [attend_chunk(): jnp.stack([key_terms[0, slot_index], value_terms[0, slot_index]])]
    another operation x12 -> x18, local copies, waits for them, and re-layouts: 6.43 us -> 10.6 us  [attend_chunk(): jnp.stack([moved[0].reshape(head_shape) for moved in received])[None]]
    another operation x6 -> x7, other arithmetic: 2.37 us -> 6.32 us
    unnamed x99 -> x118, local copies, waits for them, and re-layouts: 9.08 us -> 11.8 us
    slice x8 -> x12, local copies, waits for them, and re-layouts: 10.4 us -> 13.1 us  [attend_chunk(): moved[0].reshape(head_shape)]
    optimization_barrier x1 -> x2, local copies, waits for them, and re-layouts: 0.9 us -> 3.32 us  [on_device(): lax.optimization_barrier((key_c, value_c, pieces[-1][0]))]
  transfers between devices with their start and end apart: 16 -> 24, of which waited for: 12 -> 7; matrix products, arithmetic and copies ran while one was open for 10% -> 36% of each run, Pallas kernels for 0% -> 0%
where the time goes in v21:
time: 187 us; the launch traced here: 185 us
  starting transfers between devices  65.2 us (35%)
  local copies, waits for them, and re-layouts  54.3 us (29%)
  other arithmetic  30 us (16%)
  waiting for transfers between devices  22.5 us (12%)
  matrix products  10.3 us (6%)
  between operations  2.59 us (1%)
    ppermute x24, starting transfers between devices, from_behind(): lax.ppermute(value, axis, [(source, source + steps) for source in range(l...  65.2 us
    ppermute x24, waiting for transfers between devices, from_behind(): lax.ppermute(value, axis, [(source, source + steps) for source in range(l...  22.5 us
    another operation x12, other arithmetic, attend_chunk(): jnp.stack([key_terms[0, slot_index], value_terms[0, slot_index]])  15 us
    slice x12, local copies, waits for them, and re-layouts, attend_chunk(): moved[0].reshape(head_shape)  13.1 us
    unnamed x118, local copies, waits for them, and re-layouts  11.8 us
    another operation x18, local copies, waits for them, and re-layouts, attend_chunk(): jnp.stack([moved[0].reshape(head_shape) for moved in received])[None]  10.6 us
    another operation x7, other arithmetic  6.32 us
  transfers between devices with their start and end apart: 24, of which 7 were waited for; matrix products, arithmetic and copies ran while one was open for 36% of the time, Pallas kernels for 0%

profile of v21, /device:TPU:15, one launch (start us, length us, event | category | flops | bytes accessed | tf_op | source)
XLA Modules:
  0.0 184.9 jit_solution(12701696013670581650)
XLA Ops:
  5.9 3.2 %collective-permute-start.2 = (bf16[2,128,1024]{1,2,0:T(8,128)(2,1)}, bf16[2,128,1024]{1,2,0:T(8,128)(2,1)}, u32[]{:S(2)}, u32[]{:S(2)}) collective-permute-start(bf16[2,128,1024]{1,2,0:T(8,128)(2,1)} %pad_maximum_fusion.3), channel_id=1, source_target_pairs={{0,4},{1,5},{2,6},{3,7},{4,8},{5,9},{6,10},{7,11},{8,12},{9,13},{1... | collective-permute-start | bytes 1572872 | tf_op jit(solution)/shard_map/ppermute | solution.py:17
  9.1 4.0 %collective-permute-start = (bf16[2,128,1024]{1,2,0:T(8,128)(2,1)}, bf16[2,128,1024]{1,2,0:T(8,128)(2,1)}, u32[]{:S(2)}, u32[]{:S(2)}) collective-permute-start(bf16[2,128,1024]{1,2,0:T(8,128)(2,1)} %pad_maximum_fusion.3), channel_id=1, source_target_pairs={{0,1},{1,2},{2,3},{3,4},{4,5},{5,6},{6,7},{7,8},{8,9},{9,10},{10,1... | collective-permute-start | bytes 1572872 | tf_op jit(solution)/shard_map/ppermute | solution.py:17
  23.9 1.9 %collective-permute-start.3 = (bf16[2,128,1024]{1,2,0:T(8,128)(2,1)}, bf16[2,128,1024]{1,2,0:T(8,128)(2,1)}, u32[]{:S(2)}, u32[]{:S(2)}) collective-permute-start(bf16[2,128,1024]{1,2,0:T(8,128)(2,1)} %collective-permute-done.2), channel_id=1, source_target_pairs={{0,4},{1,5},{2,6},{3,7},{4,8},{5,9},{6,10},{7,11},{8,12},{9,13},{1... | collective-permute-start | bytes 1572872 | tf_op jit(solution)/shard_map/ppermute | solution.py:17
  25.8 1.9 %fusion.58 = (bf16[1,128,1024]{1,2,0:T(8,128)(2,1)}, bf16[1,128,1024]{1,2,0:T(8,128)(2,1)}) fusion(bf16[2,128,1024]{1,2,0:T(8,128)(2,1)} %collective-permute-done.2), kind=kLoop, calls=%fused_computation.236 | loop fusion | bytes 1048576 | tf_op jit(solution)/shard_map/slice | solution.py:88
  27.7 4.4 %collective-permute-start.1 = (bf16[2,128,1024]{1,2,0:T(8,128)(2,1)}, bf16[2,128,1024]{1,2,0:T(8,128)(2,1)}, u32[]{:S(2)}, u32[]{:S(2)}) collective-permute-start(bf16[2,128,1024]{1,2,0:T(8,128)(2,1)} %collective-permute-done), channel_id=1, source_target_pairs={{0,1},{1,2},{2,3},{3,4},{4,5},{5,6},{6,7},{7,8},{8,9},{9,10},{10,1... | collective-permute-start | bytes 1572872 | tf_op jit(solution)/shard_map/ppermute | solution.py:17
  32.1 1.9 %fusion.60 = (bf16[1,128,1024]{1,2,0:T(8,128)(2,1)}, bf16[1,128,1024]{1,2,0:T(8,128)(2,1)}) fusion(bf16[2,128,1024]{1,2,0:T(8,128)(2,1)} %collective-permute-done), kind=kLoop, calls=%fused_computation.238 | loop fusion | bytes 1048576 | tf_op jit(solution)/shard_map/slice | solution.py:88
  39.9 1.9 %fusion.57 = (bf16[1,128,1024]{1,2,0:T(8,128)(2,1)}, bf16[1,128,1024]{1,2,0:T(8,128)(2,1)}) fusion(bf16[2,128,1024]{1,2,0:T(8,128)(2,1)} %collective-permute-done.3), kind=kLoop, calls=%fused_computation.235 | loop fusion | bytes 1048576 | tf_op jit(solution)/shard_map/slice | solution.py:88
  43.6 1.9 %fusion.59 = (bf16[1,128,1024]{1,2,0:T(8,128)(2,1)}, bf16[1,128,1024]{1,2,0:T(8,128)(2,1)}) fusion(bf16[2,128,1024]{1,2,0:T(8,128)(2,1)} %collective-permute-done.1), kind=kLoop, calls=%fused_computation.237 | loop fusion | bytes 1048576 | tf_op jit(solution)/shard_map/slice | solution.py:88
  58.4 2.5 %collective-permute-start.7 = (bf16[2,128,512]{1,2,0:T(8,128)(2,1)}, bf16[2,128,512]{1,2,0:T(8,128)(2,1)}, u32[]{:S(2)}, u32[]{:S(2)}) collective-permute-start(bf16[2,128,512]{1,2,0:T(8,128)(2,1)} %pad_maximum_fusion.13), channel_id=1, source_target_pairs={{0,8},{1,9},{2,10},{3,11},{4,12},{5,13},{6,14},{7,15},{16,24},{17,... | collective-permute-start | bytes 786440 | tf_op jit(solution)/shard_map/ppermute | solution.py:17
  61.7 4.5 %collective-permute-start.14 = (bf16[2,128,8,128]{1,3,2,0:T(8,128)(2,1)}, bf16[2,128,8,128]{1,3,2,0:T(8,128)(2,1)}, u32[]{:S(2)}, u32[]{:S(2)}) collective-permute-start(bf16[2,128,8,128]{1,3,2,0:T(8,128)(2,1)} %pad_maximum_fusion.9), channel_id=1, source_target_pairs={{4,0},{5,1},{6,2},{7,3},{8,4},{9,5},{10,6},{11,7},{12,8},{13,9},{1... | collective-permute-start | bytes 1572872 | tf_op jit(solution)/shard_map/ppermute | solution.py:17
  68.7 1.9 %collective-permute-start.6 = (bf16[2,128,512]{1,2,0:T(8,128)(2,1)}, bf16[2,128,512]{1,2,0:T(8,128)(2,1)S(1)}, u32[]{:S(2)}, u32[]{:S(2)}) collective-permute-start(bf16[2,128,512]{1,2,0:T(8,128)(2,1)} %pad_maximum_fusion.13), channel_id=1, source_target_pairs={{0,4},{1,5},{2,6},{3,7},{4,8},{5,9},{6,10},{7,11},{8,12},{9,13},{1... | collective-permute-start | bytes 786440 | tf_op jit(solution)/shard_map/ppermute | solution.py:17
  70.7 1.9 %collective-permute-start.5 = (bf16[2,128,512]{1,2,0:T(8,128)(2,1)}, bf16[2,128,512]{1,2,0:T(8,128)(2,1)S(1)}, u32[]{:S(2)}, u32[]{:S(2)}) collective-permute-start(bf16[2,128,512]{1,2,0:T(8,128)(2,1)} %pad_maximum_fusion.13), channel_id=1, source_target_pairs={{0,2},{1,3},{2,4},{3,5},{4,6},{5,7},{6,8},{7,9},{8,10},{9,11},{10,... | collective-permute-start | bytes 786440 | tf_op jit(solution)/shard_map/ppermute | solution.py:17
  72.6 5.8 %collective-permute-start.4 = (bf16[2,128,512]{1,2,0:T(8,128)(2,1)}, bf16[2,128,512]{1,2,0:T(8,128)(2,1)S(1)}, u32[]{:S(2)}, u32[]{:S(2)}) collective-permute-start(bf16[2,128,512]{1,2,0:T(8,128)(2,1)} %pad_maximum_fusion.13), channel_id=1, source_target_pairs={{0,1},{1,2},{2,3},{3,4},{4,5},{5,6},{6,7},{7,8},{8,9},{9,10},{10,1... | collective-permute-start | bytes 786440 | tf_op jit(solution)/shard_map/ppermute | solution.py:17
  81.6 3.6 %collective-permute-start.13 = (bf16[2,128,8,128]{1,3,2,0:T(8,128)(2,1)}, bf16[2,128,8,128]{1,3,2,0:T(8,128)(2,1)}, u32[]{:S(2)}, u32[]{:S(2)}) collective-permute-start(bf16[2,128,8,128]{1,3,2,0:T(8,128)(2,1)} %pad_maximum_fusion.8), channel_id=1, source_target_pairs={{2,0},{3,1},{4,2},{5,3},{6,4},{7,5},{8,6},{9,7},{10,8},{11,9},{12,... | collective-permute-start | bytes 1572872 | tf_op jit(solution)/shard_map/ppermute | solution.py:17
  85.6 2.6 %collective-permute-start.12 = (bf16[2,128,8,128]{1,3,2,0:T(8,128)(2,1)}, bf16[2,128,8,128]{1,3,2,0:T(8,128)(2,1)}, u32[]{:S(2)}, u32[]{:S(2)}) collective-permute-start(bf16[2,128,8,128]{1,3,2,0:T(8,128)(2,1)} %pad_maximum_fusion.7), channel_id=1, source_target_pairs={{1,0},{2,1},{3,2},{4,3},{5,4},{6,5},{7,6},{8,7},{9,8},{10,9},{11,1... | collective-permute-start | bytes 1572872 | tf_op jit(solution)/shard_map/ppermute | solution.py:17
  95.7 6.8 %collective-permute-start.11 = (bf16[2,128,512]{1,2,0:T(8,128)(2,1)}, bf16[2,128,512]{1,2,0:T(8,128)(2,1)}, u32[]{:S(2)}, u32[]{:S(2)}) collective-permute-start(bf16[2,128,512]{1,2,0:T(8,128)(2,1)} %pad_maximum_fusion.14), channel_id=1, source_target_pairs={{0,8},{1,9},{2,10},{3,11},{4,12},{5,13},{6,14},{7,15},{16,24},{17,... | collective-permute-start | bytes 786440 | tf_op jit(solution)/shard_map/ppermute | solution.py:17
  111.8 1.9 %collective-permute-start.10 = (bf16[2,128,512]{1,2,0:T(8,128)(2,1)}, bf16[2,128,512]{1,2,0:T(8,128)(2,1)}, u32[]{:S(2)}, u32[]{:S(2)}) collective-permute-start(bf16[2,128,512]{1,2,0:T(8,128)(2,1)} %pad_maximum_fusion.14), channel_id=1, source_target_pairs={{0,4},{1,5},{2,6},{3,7},{4,8},{5,9},{6,10},{7,11},{8,12},{9,13},{1... | collective-permute-start | bytes 786440 | tf_op jit(solution)/shard_map/ppermute | solution.py:17
  113.8 1.9 %collective-permute-start.9 = (bf16[2,128,512]{1,2,0:T(8,128)(2,1)}, bf16[2,128,512]{1,2,0:T(8,128)(2,1)S(1)}, u32[]{:S(2)}, u32[]{:S(2)}) collective-permute-start(bf16[2,128,512]{1,2,0:T(8,128)(2,1)} %pad_maximum_fusion.14), channel_id=1, source_target_pairs={{0,2},{1,3},{2,4},{3,5},{4,6},{5,7},{6,8},{7,9},{8,10},{9,11},{10,... | collective-permute-start | bytes 786440 | tf_op jit(solution)/shard_map/ppermute | solution.py:17
  115.7 4.0 %collective-permute-done.13 = bf16[2,128,8,128]{1,3,2,0:T(8,128)(2,1)} collective-permute-done((bf16[2,128,8,128]{1,3,2,0:T(8,128)(2,1)}, bf16[2,128,8,128]{1,3,2,0:T(8,128)(2,1)}, u32[]{:S(2)}, u32[]{:S(2)}) %collective-permute-start.13) | collective-permute-done | bytes 524320 | tf_op jit(solution)/shard_map/ppermute | solution.py:17
  119.7 1.9 %collective-permute-start.8 = (bf16[2,128,512]{1,2,0:T(8,128)(2,1)}, bf16[2,128,512]{1,2,0:T(8,128)(2,1)}, u32[]{:S(2)}, u32[]{:S(2)}) collective-permute-start(bf16[2,128,512]{1,2,0:T(8,128)(2,1)} %pad_maximum_fusion.14), channel_id=1, source_target_pairs={{0,1},{1,2},{2,3},{3,4},{4,5},{5,6},{6,7},{7,8},{8,9},{9,10},{10,1... | collective-permute-start | bytes 786440 | tf_op jit(solution)/shard_map/ppermute | solution.py:17
  121.6 1.9 %collective-permute-done.12 = bf16[2,128,8,128]{1,3,2,0:T(8,128)(2,1)} collective-permute-done((bf16[2,128,8,128]{1,3,2,0:T(8,128)(2,1)}, bf16[2,128,8,128]{1,3,2,0:T(8,128)(2,1)}, u32[]{:S(2)}, u32[]{:S(2)}) %collective-permute-start.12) | collective-permute-done | bytes 524320 | tf_op jit(solution)/shard_map/ppermute | solution.py:17
  123.5 1.9 %collective-permute-start.18 = (bf16[2,128,4,128]{1,3,2,0:T(8,128)(2,1)}, bf16[2,128,4,128]{1,3,2,0:T(8,128)(2,1)}, u32[]{:S(2)}, u32[]{:S(2)}) collective-permute-start(bf16[2,128,4,128]{1,3,2,0:T(8,128)(2,1)} %pad_maximum_fusion.17), channel_id=1, source_target_pairs={{4,0},{5,1},{6,2},{7,3},{8,4},{9,5},{10,6},{11,7},{12,8},{13,9},{1... | collective-permute-start | bytes 786440 | tf_op jit(solution)/shard_map/ppermute | solution.py:17
  125.5 1.9 %fusion.46 = (bf16[128,8,128]{0,2,1:T(8,128)(2,1)S(1)}, f32[128,8,128]{0,2,1:T(8,128)S(1)}) fusion(bf16[128,8,128]{0,2,1:T(8,128)(2,1)S(1)} %copy-done.16, bf16[2,128,8,128]{1,3,2,0:T(8,128)(2,1)} %collective-permute-done.15, bf16[2,128,8,128]{1,3,2,0:T(8,128)(2,1)} %collective-permute-done.14, bf16[2,128,8,128]{1,3,2,0:T(8,128)(2,1)} %collective-permute-done.13, ...), kind=kLoop, calls=%fused_computation.81 | loop fusion | flops 2490368 | bytes 3407872 | tf_op jit(solution)/shard_map/convert.34
  129.9 1.9 %collective-permute-start.17 = (bf16[2,128,4,128]{1,3,2,0:T(8,128)(2,1)}, bf16[2,128,4,128]{1,3,2,0:T(8,128)(2,1)}, u32[]{:S(2)}, u32[]{:S(2)}) collective-permute-start(bf16[2,128,4,128]{1,3,2,0:T(8,128)(2,1)} %pad_maximum_fusion.16), channel_id=1, source_target_pairs={{2,0},{3,1},{4,2},{5,3},{6,4},{7,5},{8,6},{9,7},{10,8},{11,9},{12,... | collective-permute-start | bytes 786440 | tf_op jit(solution)/shard_map/ppermute | solution.py:17
  133.8 1.9 %collective-permute-start.16 = (bf16[2,128,4,128]{1,3,2,0:T(8,128)(2,1)}, bf16[2,128,4,128]{1,3,2,0:T(8,128)(2,1)}, u32[]{:S(2)}, u32[]{:S(2)}) collective-permute-start(bf16[2,128,4,128]{1,3,2,0:T(8,128)(2,1)} %pad_maximum_fusion.15), channel_id=1, source_target_pairs={{1,0},{2,1},{3,2},{4,3},{5,4},{6,5},{7,6},{8,7},{9,8},{10,9},{11,1... | collective-permute-start | bytes 786440 | tf_op jit(solution)/shard_map/ppermute | solution.py:17
  147.6 1.9 %collective-permute-start.22 = (bf16[2,128,4,128]{1,3,2,0:T(8,128)(2,1)}, bf16[2,128,4,128]{1,3,2,0:T(8,128)(2,1)}, u32[]{:S(2)}, u32[]{:S(2)}) collective-permute-start(bf16[2,128,4,128]{1,3,2,0:T(8,128)(2,1)} %pad_maximum_fusion.21), channel_id=1, source_target_pairs={{4,0},{5,1},{6,2},{7,3},{8,4},{9,5},{10,6},{11,7},{12,8},{13,9},{1... | collective-permute-start | bytes 786440 | tf_op jit(solution)/shard_map/ppermute | solution.py:17
  156.1 1.9 %collective-permute-start.21 = (bf16[2,128,4,128]{1,3,2,0:T(8,128)(2,1)}, bf16[2,128,4,128]{1,3,2,0:T(8,128)(2,1)}, u32[]{:S(2)}, u32[]{:S(2)}) collective-permute-start(bf16[2,128,4,128]{1,3,2,0:T(8,128)(2,1)} %pad_maximum_fusion.20), channel_id=1, source_target_pairs={{2,0},{3,1},{4,2},{5,3},{6,4},{7,5},{8,6},{9,7},{10,8},{11,9},{12,... | collective-permute-start | bytes 786440 | tf_op jit(solution)/shard_map/ppermute | solution.py:17
  158.1 2.7 %collective-permute-start.20 = (bf16[2,128,4,128]{1,3,2,0:T(8,128)(2,1)}, bf16[2,128,4,128]{1,3,2,0:T(8,128)(2,1)}, u32[]{:S(2)}, u32[]{:S(2)}) collective-permute-start(bf16[2,128,4,128]{1,3,2,0:T(8,128)(2,1)} %pad_maximum_fusion.19), channel_id=1, source_target_pairs={{1,0},{2,1},{3,2},{4,3},{5,4},{6,5},{7,6},{8,7},{9,8},{10,9},{11,1... | collective-permute-start | bytes 786440 | tf_op jit(solution)/shard_map/ppermute | solution.py:17
  160.8 2.2 %fusion.49 = (bf16[128,4,128]{0,2,1:T(8,128)(2,1)S(1)}, f32[128,4,128]{0,2,1:T(8,128)}) fusion(bf16[128,4,128]{0,2,1:T(8,128)(2,1)S(1)} %copy-done.33, bf16[2,128,4,128]{1,3,2,0:T(8,128)(2,1)} %collective-permute-done.19, bf16[2,128,4,128]{1,3,2,0:T(8,128)(2,1)} %collective-permute-done.18, bf16[2,128,4,128]{1,3,2,0:T(8,128)(2,1)} %collective-permute-done.17, ...), kind=kLoop, calls=%fused_computation.134 | loop fusion | flops 1245184 | bytes 1703936 | tf_op jit(solution)/shard_map/convert.33
  164.1 4.4 %collective-permute-done.23 = bf16[2,128,4,128]{1,3,2,0:T(8,128)(2,1)} collective-permute-done((bf16[2,128,4,128]{1,3,2,0:T(8,128)(2,1)}, bf16[2,128,4,128]{1,3,2,0:T(8,128)(2,1)}, u32[]{:S(2)}, u32[]{:S(2)}) %collective-permute-start.23) | collective-permute-done | bytes 262176 | tf_op jit(solution)/shard_map/ppermute | solution.py:17
  168.4 8.0 %collective-permute-done.21 = bf16[2,128,4,128]{1,3,2,0:T(8,128)(2,1)} collective-permute-done((bf16[2,128,4,128]{1,3,2,0:T(8,128)(2,1)}, bf16[2,128,4,128]{1,3,2,0:T(8,128)(2,1)}, u32[]{:S(2)}, u32[]{:S(2)}) %collective-permute-start.21) | collective-permute-done | bytes 262176 | tf_op jit(solution)/shard_map/ppermute | solution.py:17
  176.4 3.0 %collective-permute-done.20 = bf16[2,128,4,128]{1,3,2,0:T(8,128)(2,1)} collective-permute-done((bf16[2,128,4,128]{1,3,2,0:T(8,128)(2,1)}, bf16[2,128,4,128]{1,3,2,0:T(8,128)(2,1)}, u32[]{:S(2)}, u32[]{:S(2)}) %collective-permute-start.20) | collective-permute-done | bytes 262176 | tf_op jit(solution)/shard_map/ppermute | solution.py:17
  (267 shorter events, 88.3 us)
Async XLA Ops:
  5.1 10.9 %copy-start.44 = (s32[4]{0:T(128)S(1)}, s32[4]{0:T(128)}, u32[]{:S(2)}) copy-start(s32[4]{0:T(128)} %constant.36) | copy-start | bytes 52
  5.9 18.0 %collective-permute-start.2 = (bf16[2,128,1024]{1,2,0:T(8,128)(2,1)}, bf16[2,128,1024]{1,2,0:T(8,128)(2,1)}, u32[]{:S(2)}, u32[]{:S(2)}) collective-permute-start(bf16[2,128,1024]{1,2,0:T(8,128)(2,1)} %pad_maximum_fusion.3), channel_id=1, source_target_pairs={{0,4},{1,5},{2,6},{3,7},{4,8},{5,9},{6,10},{7,11},{8,12},{9,13},{1... | collective-permute-start | bytes 1572872 | tf_op jit(solution)/shard_map/ppermute | solution.py:17
  9.1 18.6 %collective-permute-start = (bf16[2,128,1024]{1,2,0:T(8,128)(2,1)}, bf16[2,128,1024]{1,2,0:T(8,128)(2,1)}, u32[]{:S(2)}, u32[]{:S(2)}) collective-permute-start(bf16[2,128,1024]{1,2,0:T(8,128)(2,1)} %pad_maximum_fusion.3), channel_id=1, source_target_pairs={{0,1},{1,2},{2,3},{3,4},{4,5},{5,6},{6,7},{7,8},{8,9},{9,10},{10,1... | collective-permute-start | bytes 1572872 | tf_op jit(solution)/shard_map/ppermute | solution.py:17
  23.9 16.0 %collective-permute-start.3 = (bf16[2,128,1024]{1,2,0:T(8,128)(2,1)}, bf16[2,128,1024]{1,2,0:T(8,128)(2,1)}, u32[]{:S(2)}, u32[]{:S(2)}) collective-permute-start(bf16[2,128,1024]{1,2,0:T(8,128)(2,1)} %collective-permute-done.2), channel_id=1, source_target_pairs={{0,4},{1,5},{2,6},{3,7},{4,8},{5,9},{6,10},{7,11},{8,12},{9,13},{1... | collective-permute-start | bytes 1572872 | tf_op jit(solution)/shard_map/ppermute | solution.py:17
  27.7 15.9 %collective-permute-start.1 = (bf16[2,128,1024]{1,2,0:T(8,128)(2,1)}, bf16[2,128,1024]{1,2,0:T(8,128)(2,1)}, u32[]{:S(2)}, u32[]{:S(2)}) collective-permute-start(bf16[2,128,1024]{1,2,0:T(8,128)(2,1)} %collective-permute-done), channel_id=1, source_target_pairs={{0,1},{1,2},{2,3},{3,4},{4,5},{5,6},{6,7},{7,8},{8,9},{9,10},{10,1... | collective-permute-start | bytes 1572872 | tf_op jit(solution)/shard_map/ppermute | solution.py:17
  58.4 20.9 %collective-permute-start.7 = (bf16[2,128,512]{1,2,0:T(8,128)(2,1)}, bf16[2,128,512]{1,2,0:T(8,128)(2,1)}, u32[]{:S(2)}, u32[]{:S(2)}) collective-permute-start(bf16[2,128,512]{1,2,0:T(8,128)(2,1)} %pad_maximum_fusion.13), channel_id=1, source_target_pairs={{0,8},{1,9},{2,10},{3,11},{4,12},{5,13},{6,14},{7,15},{16,24},{17,... | collective-permute-start | bytes 786440 | tf_op jit(solution)/shard_map/ppermute | solution.py:17
  61.7 50.1 %collective-permute-start.14 = (bf16[2,128,8,128]{1,3,2,0:T(8,128)(2,1)}, bf16[2,128,8,128]{1,3,2,0:T(8,128)(2,1)}, u32[]{:S(2)}, u32[]{:S(2)}) collective-permute-start(bf16[2,128,8,128]{1,3,2,0:T(8,128)(2,1)} %pad_maximum_fusion.9), channel_id=1, source_target_pairs={{4,0},{5,1},{6,2},{7,3},{8,4},{9,5},{10,6},{11,7},{12,8},{13,9},{1... | collective-permute-start | bytes 1572872 | tf_op jit(solution)/shard_map/ppermute | solution.py:17
  66.2 12.2 %copy-start.9 = (bf16[1,128,8,128]{1,3,2,0:T(8,128)(2,1)S(1)}, bf16[1,128,8,128]{1,3,2,0:T(8,128)(2,1)}, u32[]{:S(2)}) copy-start(bf16[1,128,8,128]{1,3,2,0:T(8,128)(2,1)} %get-tuple-element.15) | copy-start | bytes 786436
  68.7 12.9 %collective-permute-start.6 = (bf16[2,128,512]{1,2,0:T(8,128)(2,1)}, bf16[2,128,512]{1,2,0:T(8,128)(2,1)S(1)}, u32[]{:S(2)}, u32[]{:S(2)}) collective-permute-start(bf16[2,128,512]{1,2,0:T(8,128)(2,1)} %pad_maximum_fusion.13), channel_id=1, source_target_pairs={{0,4},{1,5},{2,6},{3,7},{4,8},{5,9},{6,10},{7,11},{8,12},{9,13},{1... | collective-permute-start | bytes 786440 | tf_op jit(solution)/shard_map/ppermute | solution.py:17
  70.7 14.9 %collective-permute-start.5 = (bf16[2,128,512]{1,2,0:T(8,128)(2,1)}, bf16[2,128,512]{1,2,0:T(8,128)(2,1)S(1)}, u32[]{:S(2)}, u32[]{:S(2)}) collective-permute-start(bf16[2,128,512]{1,2,0:T(8,128)(2,1)} %pad_maximum_fusion.13), channel_id=1, source_target_pairs={{0,2},{1,3},{2,4},{3,5},{4,6},{5,7},{6,8},{7,9},{8,10},{9,11},{10,... | collective-permute-start | bytes 786440 | tf_op jit(solution)/shard_map/ppermute | solution.py:17
  72.6 15.8 %collective-permute-start.4 = (bf16[2,128,512]{1,2,0:T(8,128)(2,1)}, bf16[2,128,512]{1,2,0:T(8,128)(2,1)S(1)}, u32[]{:S(2)}, u32[]{:S(2)}) collective-permute-start(bf16[2,128,512]{1,2,0:T(8,128)(2,1)} %pad_maximum_fusion.13), channel_id=1, source_target_pairs={{0,1},{1,2},{2,3},{3,4},{4,5},{5,6},{6,7},{7,8},{8,9},{9,10},{10,1... | collective-permute-start | bytes 786440 | tf_op jit(solution)/shard_map/ppermute | solution.py:17
  79.3 34.4 %collective-permute-start.15 = (bf16[2,128,8,128]{1,3,2,0:T(8,128)(2,1)}, bf16[2,128,8,128]{1,3,2,0:T(8,128)(2,1)}, u32[]{:S(2)}, u32[]{:S(2)}) collective-permute-start(bf16[2,128,8,128]{1,3,2,0:T(8,128)(2,1)} %pad_maximum_fusion.10), channel_id=1, source_target_pairs={{8,0},{9,1},{10,2},{11,3},{12,4},{13,5},{14,6},{15,7},{24,16},{25,... | collective-permute-start | bytes 1572872 | tf_op jit(solution)/shard_map/ppermute | solution.py:17
  81.6 38.1 %collective-permute-start.13 = (bf16[2,128,8,128]{1,3,2,0:T(8,128)(2,1)}, bf16[2,128,8,128]{1,3,2,0:T(8,128)(2,1)}, u32[]{:S(2)}, u32[]{:S(2)}) collective-permute-start(bf16[2,128,8,128]{1,3,2,0:T(8,128)(2,1)} %pad_maximum_fusion.8), channel_id=1, source_target_pairs={{2,0},{3,1},{4,2},{5,3},{6,4},{7,5},{8,6},{9,7},{10,8},{11,9},{12,... | collective-permute-start | bytes 1572872 | tf_op jit(solution)/shard_map/ppermute | solution.py:17
  85.6 37.9 %collective-permute-start.12 = (bf16[2,128,8,128]{1,3,2,0:T(8,128)(2,1)}, bf16[2,128,8,128]{1,3,2,0:T(8,128)(2,1)}, u32[]{:S(2)}, u32[]{:S(2)}) collective-permute-start(bf16[2,128,8,128]{1,3,2,0:T(8,128)(2,1)} %pad_maximum_fusion.7), channel_id=1, source_target_pairs={{1,0},{2,1},{3,2},{4,3},{5,4},{6,5},{7,6},{8,7},{9,8},{10,9},{11,1... | collective-permute-start | bytes 1572872 | tf_op jit(solution)/shard_map/ppermute | solution.py:17
  93.4 11.8 %copy-start.27 = (bf16[1,128,4,128]{1,3,2,0:T(8,128)(2,1)S(1)}, bf16[1,128,4,128]{1,3,2,0:T(8,128)(2,1)}, u32[]{:S(2)}) copy-start(bf16[1,128,4,128]{1,3,2,0:T(8,128)(2,1)} %get-tuple-element.39) | copy-start | bytes 393220
  95.7 31.8 %collective-permute-start.11 = (bf16[2,128,512]{1,2,0:T(8,128)(2,1)}, bf16[2,128,512]{1,2,0:T(8,128)(2,1)}, u32[]{:S(2)}, u32[]{:S(2)}) collective-permute-start(bf16[2,128,512]{1,2,0:T(8,128)(2,1)} %pad_maximum_fusion.14), channel_id=1, source_target_pairs={{0,8},{1,9},{2,10},{3,11},{4,12},{5,13},{6,14},{7,15},{16,24},{17,... | collective-permute-start | bytes 786440 | tf_op jit(solution)/shard_map/ppermute | solution.py:17
  107.4 18.1 %copy-start.16 = (bf16[128,8,128]{0,2,1:T(8,128)(2,1)S(1)}, bf16[128,8,128]{0,2,1:T(8,128)(2,1)}, u32[]{:S(2)}) copy-start(bf16[128,8,128]{0,2,1:T(8,128)(2,1)} %get-tuple-element.14) | copy-start | bytes 786436
  107.4 18.1 %copy-start.17 = (bf16[128,8,128]{0,2,1:T(8,128)(2,1)S(1)}, bf16[128,8,128]{0,2,1:T(8,128)(2,1)}, u32[]{:S(2)}) copy-start(bf16[128,8,128]{0,2,1:T(8,128)(2,1)} %get-tuple-element.21) | copy-start | bytes 786436
  111.8 18.0 %collective-permute-start.10 = (bf16[2,128,512]{1,2,0:T(8,128)(2,1)}, bf16[2,128,512]{1,2,0:T(8,128)(2,1)}, u32[]{:S(2)}, u32[]{:S(2)}) collective-permute-start(bf16[2,128,512]{1,2,0:T(8,128)(2,1)} %pad_maximum_fusion.14), channel_id=1, source_target_pairs={{0,4},{1,5},{2,6},{3,7},{4,8},{5,9},{6,10},{7,11},{8,12},{9,13},{1... | collective-permute-start | bytes 786440 | tf_op jit(solution)/shard_map/ppermute | solution.py:17
  113.8 19.3 %collective-permute-start.9 = (bf16[2,128,512]{1,2,0:T(8,128)(2,1)}, bf16[2,128,512]{1,2,0:T(8,128)(2,1)S(1)}, u32[]{:S(2)}, u32[]{:S(2)}) collective-permute-start(bf16[2,128,512]{1,2,0:T(8,128)(2,1)} %pad_maximum_fusion.14), channel_id=1, source_target_pairs={{0,2},{1,3},{2,4},{3,5},{4,6},{5,7},{6,8},{7,9},{8,10},{9,11},{10,... | collective-permute-start | bytes 786440 | tf_op jit(solution)/shard_map/ppermute | solution.py:17
  119.7 17.1 %collective-permute-start.8 = (bf16[2,128,512]{1,2,0:T(8,128)(2,1)}, bf16[2,128,512]{1,2,0:T(8,128)(2,1)}, u32[]{:S(2)}, u32[]{:S(2)}) collective-permute-start(bf16[2,128,512]{1,2,0:T(8,128)(2,1)} %pad_maximum_fusion.14), channel_id=1, source_target_pairs={{0,1},{1,2},{2,3},{3,4},{4,5},{5,6},{6,7},{7,8},{8,9},{9,10},{10,1... | collective-permute-start | bytes 786440 | tf_op jit(solution)/shard_map/ppermute | solution.py:17
  123.5 31.2 %collective-permute-start.18 = (bf16[2,128,4,128]{1,3,2,0:T(8,128)(2,1)}, bf16[2,128,4,128]{1,3,2,0:T(8,128)(2,1)}, u32[]{:S(2)}, u32[]{:S(2)}) collective-permute-start(bf16[2,128,4,128]{1,3,2,0:T(8,128)(2,1)} %pad_maximum_fusion.17), channel_id=1, source_target_pairs={{4,0},{5,1},{6,2},{7,3},{8,4},{9,5},{10,6},{11,7},{12,8},{13,9},{1... | collective-permute-start | bytes 786440 | tf_op jit(solution)/shard_map/ppermute | solution.py:17
  127.6 28.6 %collective-permute-start.19 = (bf16[2,128,4,128]{1,3,2,0:T(8,128)(2,1)}, bf16[2,128,4,128]{1,3,2,0:T(8,128)(2,1)}, u32[]{:S(2)}, u32[]{:S(2)}) collective-permute-start(bf16[2,128,4,128]{1,3,2,0:T(8,128)(2,1)} %pad_maximum_fusion.18), channel_id=1, source_target_pairs={{8,0},{9,1},{10,2},{11,3},{12,4},{13,5},{14,6},{15,7},{24,16},{25,... | collective-permute-start | bytes 786440 | tf_op jit(solution)/shard_map/ppermute | solution.py:17
  129.9 28.2 %collective-permute-start.17 = (bf16[2,128,4,128]{1,3,2,0:T(8,128)(2,1)}, bf16[2,128,4,128]{1,3,2,0:T(8,128)(2,1)}, u32[]{:S(2)}, u32[]{:S(2)}) collective-permute-start(bf16[2,128,4,128]{1,3,2,0:T(8,128)(2,1)} %pad_maximum_fusion.16), channel_id=1, source_target_pairs={{2,0},{3,1},{4,2},{5,3},{6,4},{7,5},{8,6},{9,7},{10,8},{11,9},{12,... | collective-permute-start | bytes 786440 | tf_op jit(solution)/shard_map/ppermute | solution.py:17
  133.8 27.0 %collective-permute-start.16 = (bf16[2,128,4,128]{1,3,2,0:T(8,128)(2,1)}, bf16[2,128,4,128]{1,3,2,0:T(8,128)(2,1)}, u32[]{:S(2)}, u32[]{:S(2)}) collective-permute-start(bf16[2,128,4,128]{1,3,2,0:T(8,128)(2,1)} %pad_maximum_fusion.15), channel_id=1, source_target_pairs={{1,0},{2,1},{3,2},{4,3},{5,4},{6,5},{7,6},{8,7},{9,8},{10,9},{11,1... | collective-permute-start | bytes 786440 | tf_op jit(solution)/shard_map/ppermute | solution.py:17
  147.6 16.5 %collective-permute-start.22 = (bf16[2,128,4,128]{1,3,2,0:T(8,128)(2,1)}, bf16[2,128,4,128]{1,3,2,0:T(8,128)(2,1)}, u32[]{:S(2)}, u32[]{:S(2)}) collective-permute-start(bf16[2,128,4,128]{1,3,2,0:T(8,128)(2,1)} %pad_maximum_fusion.21), channel_id=1, source_target_pairs={{4,0},{5,1},{6,2},{7,3},{8,4},{9,5},{10,6},{11,7},{12,8},{13,9},{1... | collective-permute-start | bytes 786440 | tf_op jit(solution)/shard_map/ppermute | solution.py:17
  154.7 13.7 %collective-permute-start.23 = (bf16[2,128,4,128]{1,3,2,0:T(8,128)(2,1)}, bf16[2,128,4,128]{1,3,2,0:T(8,128)(2,1)}, u32[]{:S(2)}, u32[]{:S(2)}) collective-permute-start(bf16[2,128,4,128]{1,3,2,0:T(8,128)(2,1)} %pad_maximum_fusion.22), channel_id=1, source_target_pairs={{8,0},{9,1},{10,2},{11,3},{12,4},{13,5},{14,6},{15,7},{24,16},{25,... | collective-permute-start | bytes 786440 | tf_op jit(solution)/shard_map/ppermute | solution.py:17
  156.1 20.3 %collective-permute-start.21 = (bf16[2,128,4,128]{1,3,2,0:T(8,128)(2,1)}, bf16[2,128,4,128]{1,3,2,0:T(8,128)(2,1)}, u32[]{:S(2)}, u32[]{:S(2)}) collective-permute-start(bf16[2,128,4,128]{1,3,2,0:T(8,128)(2,1)} %pad_maximum_fusion.20), channel_id=1, source_target_pairs={{2,0},{3,1},{4,2},{5,3},{6,4},{7,5},{8,6},{9,7},{10,8},{11,9},{12,... | collective-permute-start | bytes 786440 | tf_op jit(solution)/shard_map/ppermute | solution.py:17
  158.1 21.4 %collective-permute-start.20 = (bf16[2,128,4,128]{1,3,2,0:T(8,128)(2,1)}, bf16[2,128,4,128]{1,3,2,0:T(8,128)(2,1)}, u32[]{:S(2)}, u32[]{:S(2)}) collective-permute-start(bf16[2,128,4,128]{1,3,2,0:T(8,128)(2,1)} %pad_maximum_fusion.19), channel_id=1, source_target_pairs={{1,0},{2,1},{3,2},{4,3},{5,4},{6,5},{7,6},{8,7},{9,8},{10,9},{11,1... | collective-permute-start | bytes 786440 | tf_op jit(solution)/shard_map/ppermute | solution.py:17
  163.8 15.7 %copy-start.35 = (bf16[128,4,128]{0,2,1:T(8,128)(2,1)S(1)}, bf16[128,4,128]{0,2,1:T(8,128)(2,1)}, u32[]{:S(2)}) copy-start(bf16[128,4,128]{0,2,1:T(8,128)(2,1)} %get-tuple-element.41) | copy-start | bytes 393220
  163.8 15.7 %copy-start.36 = (bf16[128,4,128]{0,2,1:T(8,128)(2,1)S(1)}, bf16[128,4,128]{0,2,1:T(8,128)(2,1)}, u32[]{:S(2)}) copy-start(bf16[128,4,128]{0,2,1:T(8,128)(2,1)} %get-tuple-element.53) | copy-start | bytes 393220
  164.0 17.0 %copy-start.20 = (f32[128,4,128]{0,2,1:T(8,128)S(1)}, f32[128,4,128]{0,2,1:T(8,128)}, u32[]{:S(2)}) copy-start(f32[128,4,128]{0,2,1:T(8,128)} %get-tuple-element.33) | copy-start | bytes 786436
  (37 other events, 171.3 us)

commit v22 on v18

--- a/solution.py
+++ b/solution.py
@@ -76,8 +76,12 @@
         if relay and (offset.bit_length() - 1) % 2 == 1:
             half = offset // 2
             received[offset] = from_behind(received[half], "ctx", half)
+        elif relay:
+            received[offset] = from_behind(pair, "ctx", offset)
         else:
-            received[offset] = from_behind(pair, "ctx", offset)
+            moved_key = from_behind(key_c, "ctx", offset)
+            moved_value = from_behind(value_c, "ctx", offset)
+            received[offset] = jnp.stack([moved_key, moved_value])
     return [received[0]] + [received[offset] for offset in offsets]
 
 

time: 184 us -> 215 us (1.17)
  waiting for transfers between devices: 54.7 us -> 68.3 us
  starting transfers between devices: 53.7 us -> 61.4 us
  matrix products: 9.69 us -> 15.3 us
  local copies, waits for them, and re-layouts: 41.2 us -> 45.9 us
    ppermute x16 -> x20, waiting for transfers between devices: 54.7 us -> 68.3 us  [from_behind(): lax.ppermute(value, axis, [(source, source + steps) for source in range(l...]
    ppermute x16 -> x20, starting transfers between devices: 53.7 us -> 61.4 us  [from_behind(): lax.ppermute(value, axis, [(source, source + steps) for source in range(l...]
    slice x8 -> x4, local copies, waits for them, and re-layouts: 13.1 us -> 6.38 us  [attend_chunk(): moved[0].reshape(head_shape)]
    ppermute x0 -> x4, local copies, waits for them, and re-layouts: none -> 5.14 us  [from_behind(): lax.ppermute(value, axis, [(source, source + steps) for source in range(l...]
    unnamed x59 -> x101, local copies, waits for them, and re-layouts: 10.4 us -> 15.2 us
    unnamed x2, matrix products: 0.97 us -> 3.63 us
    dot_general x2, matrix products: 0.99 us -> 3.51 us  [attend_chunk(): jnp.einsum('bhtnu,bnuhd->bthd', weights, value_stack, preferred_element_t...]
  transfers between devices with their start and end apart: 16 -> 20, of which waited for: 8 -> 8; matrix products, arithmetic and copies ran while one was open for 28% -> 24% of each run, Pallas kernels for 0% -> 0%
where the time goes in v22:
time: 215 us; the launch traced here: 213 us
  waiting for transfers between devices  68.3 us (32%)
  starting transfers between devices  61.4 us (29%)
  local copies, waits for them, and re-layouts  45.9 us (21%)
  other arithmetic  20.4 us (9%)
  matrix products  15.3 us (7%)
  between operations  2.22 us (1%)
    ppermute x20, waiting for transfers between devices, from_behind(): lax.ppermute(value, axis, [(source, source + steps) for source in range(l...  68.3 us
    ppermute x20, starting transfers between devices, from_behind(): lax.ppermute(value, axis, [(source, source + steps) for source in range(l...  61.4 us
    unnamed x101, local copies, waits for them, and re-layouts  15.2 us
    another operation x8, other arithmetic, attend_chunk(): jnp.stack([key_terms[0, slot_index], value_terms[0, slot_index]])  6.73 us
    slice x4, local copies, waits for them, and re-layouts, attend_chunk(): moved[0].reshape(head_shape)  6.38 us
    another operation x12, local copies, waits for them, and re-layouts, attend_chunk(): jnp.stack([moved[0].reshape(head_shape) for moved in received])[None]  5.61 us
    ppermute x4, local copies, waits for them, and re-layouts, from_behind(): lax.ppermute(value, axis, [(source, source + steps) for source in range(l...  5.14 us
    another operation x6, other arithmetic  4.65 us
  transfers between devices with their start and end apart: 20, of which 8 were waited for; matrix products, arithmetic and copies ran while one was open for 24% of the time, Pallas kernels for 0%

profile of v22, /device:TPU:15, one launch (start us, length us, event | category | flops | bytes accessed | tf_op | source)
XLA Modules:
  0.0 213.5 jit_solution(5303516047248691682)
XLA Ops:
  7.7 3.2 %collective-permute-start.2 = (bf16[2,128,1024]{1,2,0:T(8,128)(2,1)}, bf16[2,128,1024]{1,2,0:T(8,128)(2,1)}, u32[]{:S(2)}, u32[]{:S(2)}) collective-permute-start(bf16[2,128,1024]{1,2,0:T(8,128)(2,1)} %pad_maximum_fusion.3), channel_id=1, source_target_pairs={{0,4},{1,5},{2,6},{3,7},{4,8},{5,9},{6,10},{7,11},{8,12},{9,13},{1... | collective-permute-start | bytes 1572872 | tf_op jit(solution)/shard_map/ppermute | solution.py:17
  10.9 4.0 %collective-permute-start = (bf16[2,128,1024]{1,2,0:T(8,128)(2,1)}, bf16[2,128,1024]{1,2,0:T(8,128)(2,1)}, u32[]{:S(2)}, u32[]{:S(2)}) collective-permute-start(bf16[2,128,1024]{1,2,0:T(8,128)(2,1)} %pad_maximum_fusion.3), channel_id=1, source_target_pairs={{0,1},{1,2},{2,3},{3,4},{4,5},{5,6},{6,7},{7,8},{8,9},{9,10},{10,1... | collective-permute-start | bytes 1572872 | tf_op jit(solution)/shard_map/ppermute | solution.py:17
  17.9 4.8 %collective-permute-done.2 = bf16[2,128,1024]{1,2,0:T(8,128)(2,1)} collective-permute-done((bf16[2,128,1024]{1,2,0:T(8,128)(2,1)}, bf16[2,128,1024]{1,2,0:T(8,128)(2,1)}, u32[]{:S(2)}, u32[]{:S(2)}) %collective-permute-start.2) | collective-permute-done | bytes 524320 | tf_op jit(solution)/shard_map/ppermute | solution.py:17
  22.7 3.2 %collective-permute-start.3 = (bf16[2,128,1024]{1,2,0:T(8,128)(2,1)}, bf16[2,128,1024]{1,2,0:T(8,128)(2,1)}, u32[]{:S(2)}, u32[]{:S(2)}) collective-permute-start(bf16[2,128,1024]{1,2,0:T(8,128)(2,1)} %collective-permute-done.2), channel_id=1, source_target_pairs={{0,4},{1,5},{2,6},{3,7},{4,8},{5,9},{6,10},{7,11},{8,12},{9,13},{1... | collective-permute-start | bytes 1572872 | tf_op jit(solution)/shard_map/ppermute | solution.py:17
  28.6 5.3 %collective-permute-start.1 = (bf16[2,128,1024]{1,2,0:T(8,128)(2,1)}, bf16[2,128,1024]{1,2,0:T(8,128)(2,1)}, u32[]{:S(2)}, u32[]{:S(2)}) collective-permute-start(bf16[2,128,1024]{1,2,0:T(8,128)(2,1)} %collective-permute-done), channel_id=1, source_target_pairs={{0,1},{1,2},{2,3},{3,4},{4,5},{5,6},{6,7},{7,8},{8,9},{9,10},{10,1... | collective-permute-start | bytes 1572872 | tf_op jit(solution)/shard_map/ppermute | solution.py:17
  36.1 3.3 %collective-permute-done.3 = bf16[2,128,1024]{1,2,0:T(8,128)(2,1)} collective-permute-done((bf16[2,128,1024]{1,2,0:T(8,128)(2,1)}, bf16[2,128,1024]{1,2,0:T(8,128)(2,1)}, u32[]{:S(2)}, u32[]{:S(2)}) %collective-permute-start.3) | collective-permute-done | bytes 524320 | tf_op jit(solution)/shard_map/ppermute | solution.py:17
  41.3 4.1 %collective-permute-done.1 = bf16[2,128,1024]{1,2,0:T(8,128)(2,1)} collective-permute-done((bf16[2,128,1024]{1,2,0:T(8,128)(2,1)}, bf16[2,128,1024]{1,2,0:T(8,128)(2,1)}, u32[]{:S(2)}, u32[]{:S(2)}) %collective-permute-start.1) | collective-permute-done | bytes 524320 | tf_op jit(solution)/shard_map/ppermute | solution.py:17
  48.6 1.8 fusion.42
  55.9 1.8 copy.107
  57.7 2.0 collective-permute-start.7
  59.7 2.0 collective-permute-start.11
  61.7 1.9 collective-permute-start.10
  63.6 1.9 collective-permute-start.9
  65.6 5.4 %collective-permute-start.8 = (bf16[128,1024]{0,1:T(8,128)(2,1)}, bf16[128,1024]{0,1:T(8,128)(2,1)}, u32[]{:S(2)}, u32[]{:S(2)}) collective-permute-start(bf16[128,1024]{0,1:T(8,128)(2,1)} %get-tuple-element.7), channel_id=1, source_target_pairs={{0,1},{1,2},{2,3},{3,4},{4,5},{5,6},{6,7},{7,8},{8,9},{9,10},{10,1... | collective-permute-start | bytes 786440 | tf_op jit(solution)/shard_map/ppermute | solution.py:17
  71.0 1.9 fusion.9
  84.2 1.9 collective-permute-start.6
  87.2 2.5 %collective-permute-start.5 = (bf16[128,1024]{1,0:T(8,128)(2,1)}, bf16[128,1024]{1,0:T(8,128)(2,1)}, u32[]{:S(2)}, u32[]{:S(2)}) collective-permute-start(bf16[128,1024]{1,0:T(8,128)(2,1)} %get-tuple-element.6), channel_id=1, source_target_pairs={{0,2},{1,3},{2,4},{3,5},{4,6},{5,7},{6,8},{7,9},{8,10},{9,11},{10,... | collective-permute-start | bytes 786440 | tf_op jit(solution)/shard_map/ppermute | solution.py:17
  91.1 10.2 %collective-permute-start.4 = (bf16[128,1024]{1,0:T(8,128)(2,1)}, bf16[128,1024]{1,0:T(8,128)(2,1)S(1)}, u32[]{:S(2)}, u32[]{:S(2)}) collective-permute-start(bf16[128,1024]{1,0:T(8,128)(2,1)} %get-tuple-element.6), channel_id=1, source_target_pairs={{0,1},{1,2},{2,3},{3,4},{4,5},{5,6},{6,7},{7,8},{8,9},{9,10},{10,1... | collective-permute-start | bytes 786440 | tf_op jit(solution)/shard_map/ppermute | solution.py:17
  102.4 2.1 collective-permute-start.13
  106.9 1.8 fusion.43
  112.0 1.9 collective-permute-start.14
  118.2 5.4 %collective-permute-start.12 = (bf16[2,128,8,128]{1,3,2,0:T(8,128)(2,1)}, bf16[2,128,8,128]{1,3,2,0:T(8,128)(2,1)}, u32[]{:S(2)}, u32[]{:S(2)}) collective-permute-start(bf16[2,128,8,128]{1,3,2,0:T(8,128)(2,1)} %pad_maximum_fusion.7), channel_id=1, source_target_pairs={{1,0},{2,1},{3,2},{4,3},{5,4},{6,5},{7,6},{8,7},{9,8},{10,9},{11,1... | collective-permute-start | bytes 1572872 | tf_op jit(solution)/shard_map/ppermute | solution.py:17
  123.6 1.8 copy.109
  129.8 2.3 %fusion.22 = bf16[1,128,8,128]{1,3,2,0:T(8,128)(2,1)S(1)} fusion(bf16[5,128,8,128]{1,3,0,2:T(8,128)(2,1)} %constant_dynamic-update-slice_fusion.10, bf16[1,8,128,5,128]{2,4,3,1,0:T(8,128)(2,1)} %fusion.14), kind=kOutput, calls=%fused_computation.38 | convolution fusion | flops 167903232 | bytes 2883584 | tf_op jit(solution)/shard_map/bhtnu,bnuhd->bthd/dot_general | solution.py:107
  138.0 1.9 collective-permute-start.17
  144.4 2.0 collective-permute-start.18
  147.8 1.9 collective-permute-start.16
  150.3 12.8 %collective-permute-done.12 = bf16[2,128,8,128]{1,3,2,0:T(8,128)(2,1)} collective-permute-done((bf16[2,128,8,128]{1,3,2,0:T(8,128)(2,1)}, bf16[2,128,8,128]{1,3,2,0:T(8,128)(2,1)}, u32[]{:S(2)}, u32[]{:S(2)}) %collective-permute-start.12) | collective-permute-done | bytes 524320 | tf_op jit(solution)/shard_map/ppermute | solution.py:17
  163.1 1.9 fusion.27
  165.2 9.1 %collective-permute-done.19 = bf16[2,128,8,128]{1,3,2,0:T(8,128)(2,1)} collective-permute-done((bf16[2,128,8,128]{1,3,2,0:T(8,128)(2,1)}, bf16[2,128,8,128]{1,3,2,0:T(8,128)(2,1)}, u32[]{:S(2)}, u32[]{:S(2)}) %collective-permute-start.19) | collective-permute-done | bytes 524320 | tf_op jit(solution)/shard_map/ppermute | solution.py:17
  174.3 33.1 %collective-permute-done.16 = bf16[2,128,8,128]{1,3,2,0:T(8,128)(2,1)} collective-permute-done((bf16[2,128,8,128]{1,3,2,0:T(8,128)(2,1)}, bf16[2,128,8,128]{1,3,2,0:T(8,128)(2,1)}, u32[]{:S(2)}, u32[]{:S(2)}) %collective-permute-start.16) | collective-permute-done | bytes 524320 | tf_op jit(solution)/shard_map/ppermute | solution.py:17
  207.4 1.9 fusion.26
  (200 shorter events, 70.1 us)
Async XLA Ops:
  0.6 3.8 %copy-start.31 = (bf16[128,2048]{1,0:T(8,128)(2,1)S(1)}, bf16[128,2048]{1,0:T(8,128)(2,1)}, u32[]{:S(2)}) copy-start(bf16[128,2048]{1,0:T(8,128)(2,1)} %param.7) | copy-start | bytes 1572868
  6.1 9.5 %copy-start.33 = (bf16[128,2048]{1,0:T(8,128)(2,1)S(1)}, bf16[128,2048]{1,0:T(8,128)(2,1)}, u32[]{:S(2)}) copy-start(bf16[128,2048]{1,0:T(8,128)(2,1)} %param.10) | copy-start | bytes 1572868
  6.9 8.8 %copy-start.39 = (s32[4]{0:T(128)S(1)}, s32[4]{0:T(128)}, u32[]{:S(2)}) copy-start(s32[4]{0:T(128)} %constant.35) | copy-start | bytes 52
  7.7 15.0 %collective-permute-start.2 = (bf16[2,128,1024]{1,2,0:T(8,128)(2,1)}, bf16[2,128,1024]{1,2,0:T(8,128)(2,1)}, u32[]{:S(2)}, u32[]{:S(2)}) collective-permute-start(bf16[2,128,1024]{1,2,0:T(8,128)(2,1)} %pad_maximum_fusion.3), channel_id=1, source_target_pairs={{0,4},{1,5},{2,6},{3,7},{4,8},{5,9},{6,10},{7,11},{8,12},{9,13},{1... | collective-permute-start | bytes 1572872 | tf_op jit(solution)/shard_map/ppermute | solution.py:17
  10.9 17.7 %collective-permute-start = (bf16[2,128,1024]{1,2,0:T(8,128)(2,1)}, bf16[2,128,1024]{1,2,0:T(8,128)(2,1)}, u32[]{:S(2)}, u32[]{:S(2)}) collective-permute-start(bf16[2,128,1024]{1,2,0:T(8,128)(2,1)} %pad_maximum_fusion.3), channel_id=1, source_target_pairs={{0,1},{1,2},{2,3},{3,4},{4,5},{5,6},{6,7},{7,8},{8,9},{9,10},{10,1... | collective-permute-start | bytes 1572872 | tf_op jit(solution)/shard_map/ppermute | solution.py:17
  22.7 16.6 %collective-permute-start.3 = (bf16[2,128,1024]{1,2,0:T(8,128)(2,1)}, bf16[2,128,1024]{1,2,0:T(8,128)(2,1)}, u32[]{:S(2)}, u32[]{:S(2)}) collective-permute-start(bf16[2,128,1024]{1,2,0:T(8,128)(2,1)} %collective-permute-done.2), channel_id=1, source_target_pairs={{0,4},{1,5},{2,6},{3,7},{4,8},{5,9},{6,10},{7,11},{8,12},{9,13},{1... | collective-permute-start | bytes 1572872 | tf_op jit(solution)/shard_map/ppermute | solution.py:17
  28.6 16.9 %collective-permute-start.1 = (bf16[2,128,1024]{1,2,0:T(8,128)(2,1)}, bf16[2,128,1024]{1,2,0:T(8,128)(2,1)}, u32[]{:S(2)}, u32[]{:S(2)}) collective-permute-start(bf16[2,128,1024]{1,2,0:T(8,128)(2,1)} %collective-permute-done), channel_id=1, source_target_pairs={{0,1},{1,2},{2,3},{3,4},{4,5},{5,6},{6,7},{7,8},{8,9},{9,10},{10,1... | collective-permute-start | bytes 1572872 | tf_op jit(solution)/shard_map/ppermute | solution.py:17
  57.7 70.2 %collective-permute-start.7 = (bf16[128,1024]{1,0:T(8,128)(2,1)}, bf16[128,1024]{1,0:T(8,128)(2,1)}, u32[]{:S(2)}, u32[]{:S(2)}) collective-permute-start(bf16[128,1024]{1,0:T(8,128)(2,1)} %get-tuple-element.6), channel_id=1, source_target_pairs={{0,8},{1,9},{2,10},{3,11},{4,12},{5,13},{6,14},{7,15},{16,24},{17,... | collective-permute-start | bytes 786440 | tf_op jit(solution)/shard_map/ppermute | solution.py:17
  59.7 24.5 %collective-permute-start.11 = (bf16[128,1024]{0,1:T(8,128)(2,1)}, bf16[128,1024]{0,1:T(8,128)(2,1)}, u32[]{:S(2)}, u32[]{:S(2)}) collective-permute-start(bf16[128,1024]{0,1:T(8,128)(2,1)} %get-tuple-element.7), channel_id=1, source_target_pairs={{0,8},{1,9},{2,10},{3,11},{4,12},{5,13},{6,14},{7,15},{16,24},{17,... | collective-permute-start | bytes 786440 | tf_op jit(solution)/shard_map/ppermute | solution.py:17
  61.7 25.5 %collective-permute-start.10 = (bf16[128,1024]{0,1:T(8,128)(2,1)}, bf16[128,1024]{0,1:T(8,128)(2,1)}, u32[]{:S(2)}, u32[]{:S(2)}) collective-permute-start(bf16[128,1024]{0,1:T(8,128)(2,1)} %get-tuple-element.7), channel_id=1, source_target_pairs={{0,4},{1,5},{2,6},{3,7},{4,8},{5,9},{6,10},{7,11},{8,12},{9,13},{1... | collective-permute-start | bytes 786440 | tf_op jit(solution)/shard_map/ppermute | solution.py:17
  63.6 27.5 %collective-permute-start.9 = (bf16[128,1024]{0,1:T(8,128)(2,1)}, bf16[128,1024]{0,1:T(8,128)(2,1)}, u32[]{:S(2)}, u32[]{:S(2)}) collective-permute-start(bf16[128,1024]{0,1:T(8,128)(2,1)} %get-tuple-element.7), channel_id=1, source_target_pairs={{0,2},{1,3},{2,4},{3,5},{4,6},{5,7},{6,8},{7,9},{8,10},{9,11},{10,... | collective-permute-start | bytes 786440 | tf_op jit(solution)/shard_map/ppermute | solution.py:17
  65.6 36.8 %collective-permute-start.8 = (bf16[128,1024]{0,1:T(8,128)(2,1)}, bf16[128,1024]{0,1:T(8,128)(2,1)}, u32[]{:S(2)}, u32[]{:S(2)}) collective-permute-start(bf16[128,1024]{0,1:T(8,128)(2,1)} %get-tuple-element.7), channel_id=1, source_target_pairs={{0,1},{1,2},{2,3},{3,4},{4,5},{5,6},{6,7},{7,8},{8,9},{9,10},{10,1... | collective-permute-start | bytes 786440 | tf_op jit(solution)/shard_map/ppermute | solution.py:17
  78.2 2.5 %copy-start.20 = (bf16[1,128,8,128]{1,3,2,0:T(8,128)(2,1)S(1)}, bf16[1,128,8,128]{1,3,2,0:T(8,128)(2,1)}, u32[]{:S(2)}) copy-start(bf16[1,128,8,128]{1,3,2,0:T(8,128)(2,1)} %get-tuple-element.26) | copy-start | bytes 786436
  84.2 31.6 %collective-permute-start.6 = (bf16[128,1024]{1,0:T(8,128)(2,1)}, bf16[128,1024]{1,0:T(8,128)(2,1)}, u32[]{:S(2)}, u32[]{:S(2)}) collective-permute-start(bf16[128,1024]{1,0:T(8,128)(2,1)} %get-tuple-element.6), channel_id=1, source_target_pairs={{0,4},{1,5},{2,6},{3,7},{4,8},{5,9},{6,10},{7,11},{8,12},{9,13},{1... | collective-permute-start | bytes 786440 | tf_op jit(solution)/shard_map/ppermute | solution.py:17
  87.2 31.0 %collective-permute-start.5 = (bf16[128,1024]{1,0:T(8,128)(2,1)}, bf16[128,1024]{1,0:T(8,128)(2,1)}, u32[]{:S(2)}, u32[]{:S(2)}) collective-permute-start(bf16[128,1024]{1,0:T(8,128)(2,1)} %get-tuple-element.6), channel_id=1, source_target_pairs={{0,2},{1,3},{2,4},{3,5},{4,6},{5,7},{6,8},{7,9},{8,10},{9,11},{10,... | collective-permute-start | bytes 786440 | tf_op jit(solution)/shard_map/ppermute | solution.py:17
  91.1 20.2 %collective-permute-start.4 = (bf16[128,1024]{1,0:T(8,128)(2,1)}, bf16[128,1024]{1,0:T(8,128)(2,1)S(1)}, u32[]{:S(2)}, u32[]{:S(2)}) collective-permute-start(bf16[128,1024]{1,0:T(8,128)(2,1)} %get-tuple-element.6), channel_id=1, source_target_pairs={{0,1},{1,2},{2,3},{3,4},{4,5},{5,6},{6,7},{7,8},{8,9},{9,10},{10,1... | collective-permute-start | bytes 786440 | tf_op jit(solution)/shard_map/ppermute | solution.py:17
  102.4 42.0 %collective-permute-start.13 = (bf16[2,128,8,128]{1,3,2,0:T(8,128)(2,1)}, bf16[2,128,8,128]{1,3,2,0:T(8,128)(2,1)}, u32[]{:S(2)}, u32[]{:S(2)}) collective-permute-start(bf16[2,128,8,128]{1,3,2,0:T(8,128)(2,1)} %pad_maximum_fusion.8), channel_id=1, source_target_pairs={{2,0},{3,1},{4,2},{5,3},{6,4},{7,5},{8,6},{9,7},{10,8},{11,9},{12,... | collective-permute-start | bytes 1572872 | tf_op jit(solution)/shard_map/ppermute | solution.py:17
  112.0 34.5 %collective-permute-start.14 = (bf16[2,128,8,128]{1,3,2,0:T(8,128)(2,1)}, bf16[2,128,8,128]{1,3,2,0:T(8,128)(2,1)}, u32[]{:S(2)}, u32[]{:S(2)}) collective-permute-start(bf16[2,128,8,128]{1,3,2,0:T(8,128)(2,1)} %pad_maximum_fusion.9), channel_id=1, source_target_pairs={{4,0},{5,1},{6,2},{7,3},{8,4},{9,5},{10,6},{11,7},{12,8},{13,9},{1... | collective-permute-start | bytes 1572872 | tf_op jit(solution)/shard_map/ppermute | solution.py:17
  115.8 32.0 %collective-permute-start.15 = (bf16[2,128,8,128]{1,3,2,0:T(8,128)(2,1)}, bf16[2,128,8,128]{1,3,2,0:T(8,128)(2,1)}, u32[]{:S(2)}, u32[]{:S(2)}) collective-permute-start(bf16[2,128,8,128]{1,3,2,0:T(8,128)(2,1)} %pad_maximum_fusion.10), channel_id=1, source_target_pairs={{8,0},{9,1},{10,2},{11,3},{12,4},{13,5},{14,6},{15,7},{24,16},{25,... | collective-permute-start | bytes 1572872 | tf_op jit(solution)/shard_map/ppermute | solution.py:17
  118.2 44.9 %collective-permute-start.12 = (bf16[2,128,8,128]{1,3,2,0:T(8,128)(2,1)}, bf16[2,128,8,128]{1,3,2,0:T(8,128)(2,1)}, u32[]{:S(2)}, u32[]{:S(2)}) collective-permute-start(bf16[2,128,8,128]{1,3,2,0:T(8,128)(2,1)} %pad_maximum_fusion.7), channel_id=1, source_target_pairs={{1,0},{2,1},{3,2},{4,3},{5,4},{6,5},{7,6},{8,7},{9,8},{10,9},{11,1... | collective-permute-start | bytes 1572872 | tf_op jit(solution)/shard_map/ppermute | solution.py:17
  129.8 2.3 %copy-start = (bf16[1,8,128,5,128]{2,4,3,1,0:T(8,128)(2,1)S(1)}, bf16[1,8,128,5,128]{2,4,3,1,0:T(8,128)(2,1)}, u32[]{:S(2)}) copy-start(bf16[1,8,128,5,128]{2,4,3,1,0:T(8,128)(2,1)} %fusion.14) | copy-start | bytes 3932164
  138.0 27.2 %collective-permute-start.17 = (bf16[2,128,8,128]{1,3,2,0:T(8,128)(2,1)}, bf16[2,128,8,128]{1,3,2,0:T(8,128)(2,1)}, u32[]{:S(2)}, u32[]{:S(2)}) collective-permute-start(bf16[2,128,8,128]{1,3,2,0:T(8,128)(2,1)} %pad_maximum_fusion.12), channel_id=1, source_target_pairs={{2,0},{3,1},{4,2},{5,3},{6,4},{7,5},{8,6},{9,7},{10,8},{11,9},{12,... | collective-permute-start | bytes 1572872 | tf_op jit(solution)/shard_map/ppermute | solution.py:17
  141.6 8.1 %copy-start.3 = (bf16[5,128,8,128]{3,1,0,2:T(8,128)(2,1)S(1)}, bf16[5,128,8,128]{3,1,0,2:T(8,128)(2,1)}, u32[]{:S(2)}) copy-start(bf16[5,128,8,128]{3,1,0,2:T(8,128)(2,1)} %copy-done.2) | copy-start | bytes 3932164
  141.6 8.1 %copy-start.7 = (bf16[1,8,128,5,128]{2,4,3,1,0:T(8,128)(2,1)S(1)}, bf16[1,8,128,5,128]{2,4,3,1,0:T(8,128)(2,1)}, u32[]{:S(2)}) copy-start(bf16[1,8,128,5,128]{2,4,3,1,0:T(8,128)(2,1)} %copy-done.6) | copy-start | bytes 3932164
  144.4 18.7 %copy-start.27 = (bf16[128,8,128]{0,2,1:T(8,128)(2,1)S(1)}, bf16[128,8,128]{0,2,1:T(8,128)(2,1)}, u32[]{:S(2)}) copy-start(bf16[128,8,128]{0,2,1:T(8,128)(2,1)} %get-tuple-element.24) | copy-start | bytes 786436
  144.4 18.7 %copy-start.28 = (bf16[128,8,128]{0,2,1:T(8,128)(2,1)S(1)}, bf16[128,8,128]{0,2,1:T(8,128)(2,1)}, u32[]{:S(2)}) copy-start(bf16[128,8,128]{0,2,1:T(8,128)(2,1)} %get-tuple-element.38) | copy-start | bytes 786436
  144.4 20.8 %collective-permute-start.18 = (bf16[2,128,8,128]{1,3,2,0:T(8,128)(2,1)}, bf16[2,128,8,128]{1,3,2,0:T(8,128)(2,1)}, u32[]{:S(2)}, u32[]{:S(2)}) collective-permute-start(bf16[2,128,8,128]{1,3,2,0:T(8,128)(2,1)} %pad_maximum_fusion.13), channel_id=1, source_target_pairs={{4,0},{5,1},{6,2},{7,3},{8,4},{9,5},{10,6},{11,7},{12,8},{13,9},{1... | collective-permute-start | bytes 1572872 | tf_op jit(solution)/shard_map/ppermute | solution.py:17
  146.5 27.9 %collective-permute-start.19 = (bf16[2,128,8,128]{1,3,2,0:T(8,128)(2,1)}, bf16[2,128,8,128]{1,3,2,0:T(8,128)(2,1)}, u32[]{:S(2)}, u32[]{:S(2)}) collective-permute-start(bf16[2,128,8,128]{1,3,2,0:T(8,128)(2,1)} %pad_maximum_fusion.14), channel_id=1, source_target_pairs={{8,0},{9,1},{10,2},{11,3},{12,4},{13,5},{14,6},{15,7},{24,16},{25,... | collective-permute-start | bytes 1572872 | tf_op jit(solution)/shard_map/ppermute | solution.py:17
  147.8 59.6 %collective-permute-start.16 = (bf16[2,128,8,128]{1,3,2,0:T(8,128)(2,1)}, bf16[2,128,8,128]{1,3,2,0:T(8,128)(2,1)}, u32[]{:S(2)}, u32[]{:S(2)}) collective-permute-start(bf16[2,128,8,128]{1,3,2,0:T(8,128)(2,1)} %pad_maximum_fusion.11), channel_id=1, source_target_pairs={{1,0},{2,1},{3,2},{4,3},{5,4},{6,5},{7,6},{8,7},{9,8},{10,9},{11,1... | collective-permute-start | bytes 1572872 | tf_op jit(solution)/shard_map/ppermute | solution.py:17
  150.3 57.1 %copy-start.29 = (bf16[128,8,128]{0,2,1:T(8,128)(2,1)S(1)}, bf16[128,8,128]{0,2,1:T(8,128)(2,1)}, u32[]{:S(2)}) copy-start(bf16[128,8,128]{0,2,1:T(8,128)(2,1)} %get-tuple-element.29) | copy-start | bytes 786436
  150.3 57.1 %copy-start.30 = (bf16[128,8,128]{0,2,1:T(8,128)(2,1)S(1)}, bf16[128,8,128]{0,2,1:T(8,128)(2,1)}, u32[]{:S(2)}) copy-start(bf16[128,8,128]{0,2,1:T(8,128)(2,1)} %get-tuple-element.43) | copy-start | bytes 786436
  165.2 45.0 %copy-start.12 = (f32[128,8,128]{0,2,1:T(8,128)S(1)}, f32[128,8,128]{0,2,1:T(8,128)}, u32[]{:S(2)}) copy-start(f32[128,8,128]{0,2,1:T(8,128)} %convolution_bitcast_fusion.1) | copy-start | bytes 1572868
  (28 other events, 38.6 us)

commit v23 on v18

--- a/solution.py
+++ b/solution.py
@@ -158,7 +158,7 @@
         key_c, value_c = key_rot[:, cols], values[:, cols]
         if pending:
             key_c, value_c, _ = lax.optimization_barrier((key_c, value_c, pieces[-1][0]))
-        received = send_chunk(key_c, value_c, offsets, relay=not pending)
+        received = send_chunk(key_c, value_c, offsets, relay=False)
         output, query_grad, own, outgoing = attend_chunk(
             query_rot[:, cols], received, grad_out[:, cols], allowed, offsets, chunk_heads
         )

time: 184 us -> 201 us (1.092)
  waiting for transfers between devices: 54.7 us -> 82.8 us
  starting transfers between devices: 53.7 us -> 41.6 us
    ppermute x16, waiting for transfers between devices: 54.7 us -> 82.8 us  [from_behind(): lax.ppermute(value, axis, [(source, source + steps) for source in range(l...]
    ppermute x16, starting transfers between devices: 53.7 us -> 41.6 us  [from_behind(): lax.ppermute(value, axis, [(source, source + steps) for source in range(l...]
  transfers between devices with their start and end apart: 16 -> 16, of which waited for: 8 -> 9; matrix products, arithmetic and copies ran while one was open for 28% -> 25% of each run, Pallas kernels for 0% -> 0%
where the time goes in v23:
time: 201 us; the launch traced here: 199 us
  waiting for transfers between devices  82.8 us (41%)
  local copies, waits for them, and re-layouts  42.4 us (21%)
  starting transfers between devices  41.6 us (21%)
  other arithmetic  21 us (10%)
  matrix products  9.68 us (5%)
    ppermute x16, waiting for transfers between devices, from_behind(): lax.ppermute(value, axis, [(source, source + steps) for source in range(l...  82.8 us
    ppermute x16, starting transfers between devices, from_behind(): lax.ppermute(value, axis, [(source, source + steps) for source in range(l...  41.6 us
    slice x8, local copies, waits for them, and re-layouts, attend_chunk(): moved[0].reshape(head_shape)  13.1 us
    unnamed x59, local copies, waits for them, and re-layouts  10.2 us
    another operation x12, local copies, waits for them, and re-layouts, attend_chunk(): jnp.stack([moved[0].reshape(head_shape) for moved in received])[None]  7.64 us
    another operation x8, other arithmetic, attend_chunk(): jnp.stack([key_terms[0, slot_index], value_terms[0, slot_index]])  6.76 us
    another operation x6, other arithmetic  5.35 us
  transfers between devices with their start and end apart: 16, of which 9 were waited for; matrix products, arithmetic and copies ran while one was open for 25% of the time, Pallas kernels for 0%

profile of v23, /device:TPU:15, one launch (start us, length us, event | category | flops | bytes accessed | tf_op | source)
XLA Modules:
  0.0 199.4 jit_solution(17130679568923165110)
XLA Ops:
  6.7 5.1 %collective-permute-start.3 = (bf16[2,128,1024]{1,2,0:T(8,128)(2,1)}, bf16[2,128,1024]{1,2,0:T(8,128)(2,1)}, u32[]{:S(2)}, u32[]{:S(2)}) collective-permute-start(bf16[2,128,1024]{1,2,0:T(8,128)(2,1)} %pad_maximum_fusion.3), channel_id=1, source_target_pairs={{0,8},{1,9},{2,10},{3,11},{4,12},{5,13},{6,14},{7,15},{16,24},{17,... | collective-permute-start | bytes 1572872 | tf_op jit(solution)/shard_map/ppermute | solution.py:17
  11.9 1.9 collective-permute-start.2
  13.8 1.9 collective-permute-start.1
  15.7 3.1 %collective-permute-start = (bf16[2,128,1024]{1,2,0:T(8,128)(2,1)}, bf16[2,128,1024]{1,2,0:T(8,128)(2,1)}, u32[]{:S(2)}, u32[]{:S(2)}) collective-permute-start(bf16[2,128,1024]{1,2,0:T(8,128)(2,1)} %pad_maximum_fusion.3), channel_id=1, source_target_pairs={{0,1},{1,2},{2,3},{3,4},{4,5},{5,6},{6,7},{7,8},{8,9},{9,10},{10,1... | collective-permute-start | bytes 1572872 | tf_op jit(solution)/shard_map/ppermute | solution.py:17
  23.0 11.2 %collective-permute-done.3 = bf16[2,128,1024]{1,2,0:T(8,128)(2,1)} collective-permute-done((bf16[2,128,1024]{1,2,0:T(8,128)(2,1)}, bf16[2,128,1024]{1,2,0:T(8,128)(2,1)}, u32[]{:S(2)}, u32[]{:S(2)}) %collective-permute-start.3) | collective-permute-done | bytes 524320 | tf_op jit(solution)/shard_map/ppermute | solution.py:17
  34.2 1.8 fusion.40
  36.1 9.3 %collective-permute-done.2 = bf16[2,128,1024]{1,2,0:T(8,128)(2,1)} collective-permute-done((bf16[2,128,1024]{1,2,0:T(8,128)(2,1)}, bf16[2,128,1024]{1,2,0:T(8,128)(2,1)}, u32[]{:S(2)}, u32[]{:S(2)}) %collective-permute-start.2) | collective-permute-done | bytes 524320 | tf_op jit(solution)/shard_map/ppermute | solution.py:17
  45.4 1.9 fusion.41
  48.4 8.3 %collective-permute-done.1 = bf16[2,128,1024]{1,2,0:T(8,128)(2,1)} collective-permute-done((bf16[2,128,1024]{1,2,0:T(8,128)(2,1)}, bf16[2,128,1024]{1,2,0:T(8,128)(2,1)}, u32[]{:S(2)}, u32[]{:S(2)}) %collective-permute-start.1) | collective-permute-done | bytes 524320 | tf_op jit(solution)/shard_map/ppermute | solution.py:17
  56.6 1.9 fusion.42
  58.5 1.8 copy.99
  60.3 2.1 %collective-permute-done = bf16[2,128,1024]{1,2,0:T(8,128)(2,1)} collective-permute-done((bf16[2,128,1024]{1,2,0:T(8,128)(2,1)}, bf16[2,128,1024]{1,2,0:T(8,128)(2,1)}, u32[]{:S(2)}, u32[]{:S(2)}) %collective-permute-start) | collective-permute-done | bytes 524320 | tf_op jit(solution)/shard_map/ppermute | solution.py:17
  62.4 1.9 fusion.43
  64.2 1.8 copy.98
  72.6 2.1 %collective-permute-start.7 = (bf16[2,128,1024]{1,2,0:T(8,128)(2,1)}, bf16[2,128,1024]{1,2,0:T(8,128)(2,1)}, u32[]{:S(2)}, u32[]{:S(2)}) collective-permute-start(bf16[2,128,1024]{1,2,0:T(8,128)(2,1)} %pad_maximum_fusion.5), channel_id=1, source_target_pairs={{0,8},{1,9},{2,10},{3,11},{4,12},{5,13},{6,14},{7,15},{16,24},{17,... | collective-permute-start | bytes 1572872 | tf_op jit(solution)/shard_map/ppermute | solution.py:17
  74.7 1.9 collective-permute-start.6
  76.6 2.2 %collective-permute-start.5 = (bf16[2,128,1024]{1,2,0:T(8,128)(2,1)}, bf16[2,128,1024]{1,2,0:T(8,128)(2,1)}, u32[]{:S(2)}, u32[]{:S(2)}) collective-permute-start(bf16[2,128,1024]{1,2,0:T(8,128)(2,1)} %pad_maximum_fusion.5), channel_id=1, source_target_pairs={{0,2},{1,3},{2,4},{3,5},{4,6},{5,7},{6,8},{7,9},{8,10},{9,11},{10,... | collective-permute-start | bytes 1572872 | tf_op jit(solution)/shard_map/ppermute | solution.py:17
  85.3 3.1 %collective-permute-start.9 = (bf16[2,128,8,128]{1,3,2,0:T(8,128)(2,1)}, bf16[2,128,8,128]{1,3,2,0:T(8,128)(2,1)}, u32[]{:S(2)}, u32[]{:S(2)}) collective-permute-start(bf16[2,128,8,128]{1,3,2,0:T(8,128)(2,1)} %pad_maximum_fusion.9), channel_id=1, source_target_pairs={{2,0},{3,1},{4,2},{5,3},{6,4},{7,5},{8,6},{9,7},{10,8},{11,9},{12,... | collective-permute-start | bytes 1572872 | tf_op jit(solution)/shard_map/ppermute | solution.py:17
  94.5 6.0 %collective-permute-start.4 = (bf16[2,128,1024]{1,2,0:T(8,128)(2,1)}, bf16[2,128,1024]{1,2,0:T(8,128)(2,1)}, u32[]{:S(2)}, u32[]{:S(2)}) collective-permute-start(bf16[2,128,1024]{1,2,0:T(8,128)(2,1)} %pad_maximum_fusion.5), channel_id=1, source_target_pairs={{0,1},{1,2},{2,3},{3,4},{4,5},{5,6},{6,7},{7,8},{8,9},{9,10},{10,1... | collective-permute-start | bytes 1572872 | tf_op jit(solution)/shard_map/ppermute | solution.py:17
  100.4 3.6 %collective-permute-start.10 = (bf16[2,128,8,128]{1,3,2,0:T(8,128)(2,1)}, bf16[2,128,8,128]{1,3,2,0:T(8,128)(2,1)}, u32[]{:S(2)}, u32[]{:S(2)}) collective-permute-start(bf16[2,128,8,128]{1,3,2,0:T(8,128)(2,1)} %pad_maximum_fusion.10), channel_id=1, source_target_pairs={{4,0},{5,1},{6,2},{7,3},{8,4},{9,5},{10,6},{11,7},{12,8},{13,9},{1... | collective-permute-start | bytes 1572872 | tf_op jit(solution)/shard_map/ppermute | solution.py:17
  107.9 5.2 %collective-permute-done.5 = bf16[2,128,1024]{1,2,0:T(8,128)(2,1)} collective-permute-done((bf16[2,128,1024]{1,2,0:T(8,128)(2,1)}, bf16[2,128,1024]{1,2,0:T(8,128)(2,1)}, u32[]{:S(2)}, u32[]{:S(2)}) %collective-permute-start.5) | collective-permute-done | bytes 524320 | tf_op jit(solution)/shard_map/ppermute | solution.py:17
  113.1 2.4 %collective-permute-start.8 = (bf16[2,128,8,128]{1,3,2,0:T(8,128)(2,1)}, bf16[2,128,8,128]{1,3,2,0:T(8,128)(2,1)}, u32[]{:S(2)}, u32[]{:S(2)}) collective-permute-start(bf16[2,128,8,128]{1,3,2,0:T(8,128)(2,1)} %pad_maximum_fusion.8), channel_id=1, source_target_pairs={{1,0},{2,1},{3,2},{4,3},{5,4},{6,5},{7,6},{8,7},{9,8},{10,9},{11,1... | collective-permute-start | bytes 1572872 | tf_op jit(solution)/shard_map/ppermute | solution.py:17
  118.7 1.9 fusion.39
  130.4 1.9 collective-permute-start.13
  134.8 1.9 collective-permute-start.14
  138.1 1.9 collective-permute-start.12
  140.0 11.0 %collective-permute-done.8 = bf16[2,128,8,128]{1,3,2,0:T(8,128)(2,1)} collective-permute-done((bf16[2,128,8,128]{1,3,2,0:T(8,128)(2,1)}, bf16[2,128,8,128]{1,3,2,0:T(8,128)(2,1)}, u32[]{:S(2)}, u32[]{:S(2)}) %collective-permute-start.8) | collective-permute-done | bytes 524320 | tf_op jit(solution)/shard_map/ppermute | solution.py:17
  151.0 2.6 %fusion.27 = (bf16[128,8,128]{0,2,1:T(8,128)(2,1)}, f32[128,8,128]{0,2,1:T(8,128)S(1)}) fusion(bf16[128,8,128]{0,2,1:T(8,128)(2,1)S(1)} %copy-done.12, bf16[2,128,8,128]{1,3,2,0:T(8,128)(2,1)} %collective-permute-done.11, bf16[2,128,8,128]{1,3,2,0:T(8,128)(2,1)} %collective-permute-done.10, bf16[2,128,8,128]{1,3,2,0:T(8,128)(2,1)} %collective-permute-done.9, ...), kind=kLoop, calls=%fused_computation.70 | loop fusion | flops 2490368 | bytes 3407872 | tf_op jit(solution)/shard_map/convert.23
  156.3 1.9 pad_maximum_fusion.6
  159.5 2.0 %collective-permute-done.15 = bf16[2,128,8,128]{1,3,2,0:T(8,128)(2,1)} collective-permute-done((bf16[2,128,8,128]{1,3,2,0:T(8,128)(2,1)}, bf16[2,128,8,128]{1,3,2,0:T(8,128)(2,1)}, u32[]{:S(2)}, u32[]{:S(2)}) %collective-permute-start.15) | collective-permute-done | bytes 524320 | tf_op jit(solution)/shard_map/ppermute | solution.py:17
  161.6 32.5 %collective-permute-done.12 = bf16[2,128,8,128]{1,3,2,0:T(8,128)(2,1)} collective-permute-done((bf16[2,128,8,128]{1,3,2,0:T(8,128)(2,1)}, bf16[2,128,8,128]{1,3,2,0:T(8,128)(2,1)}, u32[]{:S(2)}, u32[]{:S(2)}) %collective-permute-start.12) | collective-permute-done | bytes 524320 | tf_op jit(solution)/shard_map/ppermute | solution.py:17
  194.1 1.9 fusion.26
  (151 shorter events, 57.7 us)
Async XLA Ops:
  0.6 3.1 %copy-start.16 = (bf16[128,2048]{1,0:T(8,128)(2,1)S(1)}, bf16[128,2048]{1,0:T(8,128)(2,1)}, u32[]{:S(2)}) copy-start(bf16[128,2048]{1,0:T(8,128)(2,1)} %param.7) | copy-start | bytes 1572868
  5.8 13.7 %copy-start.17 = (bf16[128,2048]{1,0:T(8,128)(2,1)S(1)}, bf16[128,2048]{1,0:T(8,128)(2,1)}, u32[]{:S(2)}) copy-start(bf16[128,2048]{1,0:T(8,128)(2,1)} %param.10) | copy-start | bytes 1572868
  6.7 13.5 %copy-start.18 = (s32[4]{0:T(128)S(1)}, s32[4]{0:T(128)}, u32[]{:S(2)}) copy-start(s32[4]{0:T(128)} %constant.35) | copy-start | bytes 52
  6.7 27.5 %collective-permute-start.3 = (bf16[2,128,1024]{1,2,0:T(8,128)(2,1)}, bf16[2,128,1024]{1,2,0:T(8,128)(2,1)}, u32[]{:S(2)}, u32[]{:S(2)}) collective-permute-start(bf16[2,128,1024]{1,2,0:T(8,128)(2,1)} %pad_maximum_fusion.3), channel_id=1, source_target_pairs={{0,8},{1,9},{2,10},{3,11},{4,12},{5,13},{6,14},{7,15},{16,24},{17,... | collective-permute-start | bytes 1572872 | tf_op jit(solution)/shard_map/ppermute | solution.py:17
  11.9 33.5 %collective-permute-start.2 = (bf16[2,128,1024]{1,2,0:T(8,128)(2,1)}, bf16[2,128,1024]{1,2,0:T(8,128)(2,1)}, u32[]{:S(2)}, u32[]{:S(2)}) collective-permute-start(bf16[2,128,1024]{1,2,0:T(8,128)(2,1)} %pad_maximum_fusion.3), channel_id=1, source_target_pairs={{0,4},{1,5},{2,6},{3,7},{4,8},{5,9},{6,10},{7,11},{8,12},{9,13},{1... | collective-permute-start | bytes 1572872 | tf_op jit(solution)/shard_map/ppermute | solution.py:17
  13.8 42.9 %collective-permute-start.1 = (bf16[2,128,1024]{1,2,0:T(8,128)(2,1)}, bf16[2,128,1024]{1,2,0:T(8,128)(2,1)}, u32[]{:S(2)}, u32[]{:S(2)}) collective-permute-start(bf16[2,128,1024]{1,2,0:T(8,128)(2,1)} %pad_maximum_fusion.3), channel_id=1, source_target_pairs={{0,2},{1,3},{2,4},{3,5},{4,6},{5,7},{6,8},{7,9},{8,10},{9,11},{10,... | collective-permute-start | bytes 1572872 | tf_op jit(solution)/shard_map/ppermute | solution.py:17
  15.7 46.6 %collective-permute-start = (bf16[2,128,1024]{1,2,0:T(8,128)(2,1)}, bf16[2,128,1024]{1,2,0:T(8,128)(2,1)}, u32[]{:S(2)}, u32[]{:S(2)}) collective-permute-start(bf16[2,128,1024]{1,2,0:T(8,128)(2,1)} %pad_maximum_fusion.3), channel_id=1, source_target_pairs={{0,1},{1,2},{2,3},{3,4},{4,5},{5,6},{6,7},{7,8},{8,9},{9,10},{10,1... | collective-permute-start | bytes 1572872 | tf_op jit(solution)/shard_map/ppermute | solution.py:17
  69.5 1.3 copy-start.11
  69.5 1.4 copy-start.9
  69.5 1.5 copy-start.7
  72.6 27.8 %collective-permute-start.7 = (bf16[2,128,1024]{1,2,0:T(8,128)(2,1)}, bf16[2,128,1024]{1,2,0:T(8,128)(2,1)}, u32[]{:S(2)}, u32[]{:S(2)}) collective-permute-start(bf16[2,128,1024]{1,2,0:T(8,128)(2,1)} %pad_maximum_fusion.5), channel_id=1, source_target_pairs={{0,8},{1,9},{2,10},{3,11},{4,12},{5,13},{6,14},{7,15},{16,24},{17,... | collective-permute-start | bytes 1572872 | tf_op jit(solution)/shard_map/ppermute | solution.py:17
  74.7 30.6 %collective-permute-start.6 = (bf16[2,128,1024]{1,2,0:T(8,128)(2,1)}, bf16[2,128,1024]{1,2,0:T(8,128)(2,1)}, u32[]{:S(2)}, u32[]{:S(2)}) collective-permute-start(bf16[2,128,1024]{1,2,0:T(8,128)(2,1)} %pad_maximum_fusion.5), channel_id=1, source_target_pairs={{0,4},{1,5},{2,6},{3,7},{4,8},{5,9},{6,10},{7,11},{8,12},{9,13},{1... | collective-permute-start | bytes 1572872 | tf_op jit(solution)/shard_map/ppermute | solution.py:17
  76.6 36.5 %collective-permute-start.5 = (bf16[2,128,1024]{1,2,0:T(8,128)(2,1)}, bf16[2,128,1024]{1,2,0:T(8,128)(2,1)}, u32[]{:S(2)}, u32[]{:S(2)}) collective-permute-start(bf16[2,128,1024]{1,2,0:T(8,128)(2,1)} %pad_maximum_fusion.5), channel_id=1, source_target_pairs={{0,2},{1,3},{2,4},{3,5},{4,6},{5,7},{6,8},{7,9},{8,10},{9,11},{10,... | collective-permute-start | bytes 1572872 | tf_op jit(solution)/shard_map/ppermute | solution.py:17
  84.5 5.7 %copy-start.4 = (bf16[1,128,8,128]{1,3,2,0:T(8,128)(2,1)S(1)}, bf16[1,128,8,128]{1,3,2,0:T(8,128)(2,1)}, u32[]{:S(2)}) copy-start(bf16[1,128,8,128]{1,3,2,0:T(8,128)(2,1)} %get-tuple-element.25) | copy-start | bytes 786436
  85.3 49.5 %collective-permute-start.9 = (bf16[2,128,8,128]{1,3,2,0:T(8,128)(2,1)}, bf16[2,128,8,128]{1,3,2,0:T(8,128)(2,1)}, u32[]{:S(2)}, u32[]{:S(2)}) collective-permute-start(bf16[2,128,8,128]{1,3,2,0:T(8,128)(2,1)} %pad_maximum_fusion.9), channel_id=1, source_target_pairs={{2,0},{3,1},{4,2},{5,3},{6,4},{7,5},{8,6},{9,7},{10,8},{11,9},{12,... | collective-permute-start | bytes 1572872 | tf_op jit(solution)/shard_map/ppermute | solution.py:17
  94.5 24.3 %collective-permute-start.4 = (bf16[2,128,1024]{1,2,0:T(8,128)(2,1)}, bf16[2,128,1024]{1,2,0:T(8,128)(2,1)}, u32[]{:S(2)}, u32[]{:S(2)}) collective-permute-start(bf16[2,128,1024]{1,2,0:T(8,128)(2,1)} %pad_maximum_fusion.5), channel_id=1, source_target_pairs={{0,1},{1,2},{2,3},{3,4},{4,5},{5,6},{6,7},{7,8},{8,9},{9,10},{10,1... | collective-permute-start | bytes 1572872 | tf_op jit(solution)/shard_map/ppermute | solution.py:17
  100.4 36.3 %collective-permute-start.10 = (bf16[2,128,8,128]{1,3,2,0:T(8,128)(2,1)}, bf16[2,128,8,128]{1,3,2,0:T(8,128)(2,1)}, u32[]{:S(2)}, u32[]{:S(2)}) collective-permute-start(bf16[2,128,8,128]{1,3,2,0:T(8,128)(2,1)} %pad_maximum_fusion.10), channel_id=1, source_target_pairs={{4,0},{5,1},{6,2},{7,3},{8,4},{9,5},{10,6},{11,7},{12,8},{13,9},{1... | collective-permute-start | bytes 1572872 | tf_op jit(solution)/shard_map/ppermute | solution.py:17
  105.3 32.7 %collective-permute-start.11 = (bf16[2,128,8,128]{1,3,2,0:T(8,128)(2,1)}, bf16[2,128,8,128]{1,3,2,0:T(8,128)(2,1)}, u32[]{:S(2)}, u32[]{:S(2)}) collective-permute-start(bf16[2,128,8,128]{1,3,2,0:T(8,128)(2,1)} %pad_maximum_fusion.11), channel_id=1, source_target_pairs={{8,0},{9,1},{10,2},{11,3},{12,4},{13,5},{14,6},{15,7},{24,16},{25,... | collective-permute-start | bytes 1572872 | tf_op jit(solution)/shard_map/ppermute | solution.py:17
  113.1 37.8 %collective-permute-start.8 = (bf16[2,128,8,128]{1,3,2,0:T(8,128)(2,1)}, bf16[2,128,8,128]{1,3,2,0:T(8,128)(2,1)}, u32[]{:S(2)}, u32[]{:S(2)}) collective-permute-start(bf16[2,128,8,128]{1,3,2,0:T(8,128)(2,1)} %pad_maximum_fusion.8), channel_id=1, source_target_pairs={{1,0},{2,1},{3,2},{4,3},{5,4},{6,5},{7,6},{8,7},{9,8},{10,9},{11,1... | collective-permute-start | bytes 1572872 | tf_op jit(solution)/shard_map/ppermute | solution.py:17
  123.3 1.3 copy-start.2
  123.3 1.3 copy-start.10
  123.3 1.4 copy-start.8
  130.4 29.2 %collective-permute-start.13 = (bf16[2,128,8,128]{1,3,2,0:T(8,128)(2,1)}, bf16[2,128,8,128]{1,3,2,0:T(8,128)(2,1)}, u32[]{:S(2)}, u32[]{:S(2)}) collective-permute-start(bf16[2,128,8,128]{1,3,2,0:T(8,128)(2,1)} %pad_maximum_fusion.13), channel_id=1, source_target_pairs={{2,0},{3,1},{4,2},{5,3},{6,4},{7,5},{8,6},{9,7},{10,8},{11,9},{12,... | collective-permute-start | bytes 1572872 | tf_op jit(solution)/shard_map/ppermute | solution.py:17
  133.1 17.8 %copy-start.12 = (bf16[128,8,128]{0,2,1:T(8,128)(2,1)S(1)}, bf16[128,8,128]{0,2,1:T(8,128)(2,1)}, u32[]{:S(2)}) copy-start(bf16[128,8,128]{0,2,1:T(8,128)(2,1)} %get-tuple-element.24) | copy-start | bytes 786436
  133.2 17.8 %copy-start.13 = (bf16[128,8,128]{0,2,1:T(8,128)(2,1)S(1)}, bf16[128,8,128]{0,2,1:T(8,128)(2,1)}, u32[]{:S(2)}) copy-start(bf16[128,8,128]{0,2,1:T(8,128)(2,1)} %get-tuple-element.38) | copy-start | bytes 786436
  134.8 24.7 %collective-permute-start.14 = (bf16[2,128,8,128]{1,3,2,0:T(8,128)(2,1)}, bf16[2,128,8,128]{1,3,2,0:T(8,128)(2,1)}, u32[]{:S(2)}, u32[]{:S(2)}) collective-permute-start(bf16[2,128,8,128]{1,3,2,0:T(8,128)(2,1)} %pad_maximum_fusion.14), channel_id=1, source_target_pairs={{4,0},{5,1},{6,2},{7,3},{8,4},{9,5},{10,6},{11,7},{12,8},{13,9},{1... | collective-permute-start | bytes 1572872 | tf_op jit(solution)/shard_map/ppermute | solution.py:17
  136.8 24.8 %collective-permute-start.15 = (bf16[2,128,8,128]{1,3,2,0:T(8,128)(2,1)}, bf16[2,128,8,128]{1,3,2,0:T(8,128)(2,1)}, u32[]{:S(2)}, u32[]{:S(2)}) collective-permute-start(bf16[2,128,8,128]{1,3,2,0:T(8,128)(2,1)} %pad_maximum_fusion.15), channel_id=1, source_target_pairs={{8,0},{9,1},{10,2},{11,3},{12,4},{13,5},{14,6},{15,7},{24,16},{25,... | collective-permute-start | bytes 1572872 | tf_op jit(solution)/shard_map/ppermute | solution.py:17
  138.1 56.0 %collective-permute-start.12 = (bf16[2,128,8,128]{1,3,2,0:T(8,128)(2,1)}, bf16[2,128,8,128]{1,3,2,0:T(8,128)(2,1)}, u32[]{:S(2)}, u32[]{:S(2)}) collective-permute-start(bf16[2,128,8,128]{1,3,2,0:T(8,128)(2,1)} %pad_maximum_fusion.12), channel_id=1, source_target_pairs={{1,0},{2,1},{3,2},{4,3},{5,4},{6,5},{7,6},{8,7},{9,8},{10,9},{11,1... | collective-permute-start | bytes 1572872 | tf_op jit(solution)/shard_map/ppermute | solution.py:17
  158.1 36.0 %copy-start.14 = (bf16[128,8,128]{0,2,1:T(8,128)(2,1)S(1)}, bf16[128,8,128]{0,2,1:T(8,128)(2,1)}, u32[]{:S(2)}) copy-start(bf16[128,8,128]{0,2,1:T(8,128)(2,1)} %get-tuple-element.43) | copy-start | bytes 786436
  158.1 36.0 %copy-start.15 = (bf16[128,8,128]{0,2,1:T(8,128)(2,1)S(1)}, bf16[128,8,128]{0,2,1:T(8,128)(2,1)}, u32[]{:S(2)}) copy-start(bf16[128,8,128]{0,2,1:T(8,128)(2,1)} %get-tuple-element.29) | copy-start | bytes 786436
  159.5 36.6 %copy-start = (f32[128,8,128]{0,2,1:T(8,128)S(1)}, f32[128,8,128]{0,2,1:T(8,128)}, u32[]{:S(2)}) copy-start(f32[128,8,128]{0,2,1:T(8,128)} %convolution_bitcast_fusion.1) | copy-start | bytes 1572868
  159.5 36.6 %copy-start.1 = (f32[128,8,128]{0,2,1:T(8,128)S(1)}, f32[128,8,128]{0,2,1:T(8,128)}, u32[]{:S(2)}) copy-start(f32[128,8,128]{0,2,1:T(8,128)} %convolution_bitcast_fusion) | copy-start | bytes 1572868
  (3 other events, 3.5 us)

commit v24 on v18

--- a/solution.py
+++ b/solution.py
@@ -168,17 +168,18 @@
         pieces.append(
             (
                 output.reshape(rows, chunk_width),
-                query_grad.reshape(rows, chunk_width),
-                key_accum_c.reshape(rows, chunk_width),
-                value_accum_c.reshape(rows, chunk_width),
+                rotary(
+                    query_grad.reshape(rows, chunk_width), positions, chunk_heads, HEAD_DIM, True
+                ).astype(jnp.bfloat16),
+                rotary(
+                    key_accum_c.reshape(rows, chunk_width), positions, chunk_heads, HEAD_DIM, True
+                ).astype(jnp.bfloat16),
+                value_accum_c.reshape(rows, chunk_width).astype(jnp.bfloat16),
             )
         )
-    attended, query_grad, key_accum, value_accum = [
+    attended, grad_queries, grad_keys, grad_values = [
         jnp.concatenate(parts, axis=1) for parts in zip(*pieces)
     ]
-    grad_queries = rotary(query_grad, positions, HEADS, HEAD_DIM, True).astype(jnp.bfloat16)
-    grad_keys = rotary(key_accum, positions, HEADS, HEAD_DIM, True).astype(jnp.bfloat16)
-    grad_values = value_accum.astype(jnp.bfloat16)
     return (attended, grad_queries, grad_keys, grad_values)
 
 

time: 184 us -> 185 us (level)
    convert_element_type x0 -> x2, other arithmetic: none -> 4.55 us  [on_device(): value_accum_c.reshape(rows, chunk_width).astype(jnp.bfloat16)]
    another operation x6 -> x4, other arithmetic: 5.35 us -> 0.83 us
    convert_element_type x0 -> x6, local copies, waits for them, and re-layouts: none -> 2.51 us  [the longest x2 1.94 us: on_device(): value_accum_c.reshape(rows, chunk_width).astype(jnp.bfloat16)]
    reshape x2 -> x0, local copies, waits for them, and re-layouts: 1.94 us -> none  [on_device(): value_accum_c.reshape(rows, chunk_width)]
    concatenate x2 -> x4, other arithmetic: 2.69 us -> 4.35 us  [on_device(): jnp.concatenate(parts, axis=1)]
    unnamed x59 -> x57, local copies, waits for them, and re-layouts: 10.4 us -> 8.8 us
where the time goes in v24:
time: 185 us; the launch traced here: 184 us
  waiting for transfers between devices  54.7 us (30%)
  starting transfers between devices  53.7 us (29%)
  local copies, waits for them, and re-layouts  40.2 us (22%)
  other arithmetic  23.5 us (13%)
  matrix products  9.64 us (5%)
  between operations  2.09 us (1%)
    ppermute x16, waiting for transfers between devices, from_behind(): lax.ppermute(value, axis, [(source, source + steps) for source in range(l...  54.7 us
    ppermute x16, starting transfers between devices, from_behind(): lax.ppermute(value, axis, [(source, source + steps) for source in range(l...  53.7 us
    slice x8, local copies, waits for them, and re-layouts, attend_chunk(): moved[0].reshape(head_shape)  13.1 us
    unnamed x57, local copies, waits for them, and re-layouts  8.8 us
    another operation x12, local copies, waits for them, and re-layouts, attend_chunk(): jnp.stack([moved[0].reshape(head_shape) for moved in received])[None]  6.97 us
    another operation x8, other arithmetic, attend_chunk(): jnp.stack([key_terms[0, slot_index], value_terms[0, slot_index]])  6.77 us
    convert_element_type x2, other arithmetic, on_device(): value_accum_c.reshape(rows, chunk_width).astype(jnp.bfloat16)  4.55 us
    concatenate x4, other arithmetic, on_device(): jnp.concatenate(parts, axis=1)  4.35 us
  transfers between devices with their start and end apart: 16, of which 8 were waited for; matrix products, arithmetic and copies ran while one was open for 28% of the time, Pallas kernels for 0%

profile of v24, /device:TPU:15, one launch (start us, length us, event | category | flops | bytes accessed | tf_op | source)
XLA Modules:
  0.0 183.8 jit_solution(17380919840393428268)
XLA Ops:
  7.1 3.2 %collective-permute-start.2 = (bf16[2,128,1024]{1,2,0:T(8,128)(2,1)}, bf16[2,128,1024]{1,2,0:T(8,128)(2,1)}, u32[]{:S(2)}, u32[]{:S(2)}) collective-permute-start(bf16[2,128,1024]{1,2,0:T(8,128)(2,1)} %pad_maximum_fusion.1), channel_id=1, source_target_pairs={{0,4},{1,5},{2,6},{3,7},{4,8},{5,9},{6,10},{7,11},{8,12},{9,13},{1... | collective-permute-start | bytes 1572872 | tf_op jit(solution)/shard_map/ppermute | solution.py:17
  10.3 4.0 %collective-permute-start = (bf16[2,128,1024]{1,2,0:T(8,128)(2,1)}, bf16[2,128,1024]{1,2,0:T(8,128)(2,1)}, u32[]{:S(2)}, u32[]{:S(2)}) collective-permute-start(bf16[2,128,1024]{1,2,0:T(8,128)(2,1)} %pad_maximum_fusion.1), channel_id=1, source_target_pairs={{0,1},{1,2},{2,3},{3,4},{4,5},{5,6},{6,7},{7,8},{8,9},{9,10},{10,1... | collective-permute-start | bytes 1572872 | tf_op jit(solution)/shard_map/ppermute | solution.py:17
  17.9 4.2 %collective-permute-done.2 = bf16[2,128,1024]{1,2,0:T(8,128)(2,1)} collective-permute-done((bf16[2,128,1024]{1,2,0:T(8,128)(2,1)}, bf16[2,128,1024]{1,2,0:T(8,128)(2,1)}, u32[]{:S(2)}, u32[]{:S(2)}) %collective-permute-start.2) | collective-permute-done | bytes 524320 | tf_op jit(solution)/shard_map/ppermute | solution.py:17
  22.1 3.2 %collective-permute-start.3 = (bf16[2,128,1024]{1,2,0:T(8,128)(2,1)}, bf16[2,128,1024]{1,2,0:T(8,128)(2,1)}, u32[]{:S(2)}, u32[]{:S(2)}) collective-permute-start(bf16[2,128,1024]{1,2,0:T(8,128)(2,1)} %collective-permute-done.2), channel_id=1, source_target_pairs={{0,4},{1,5},{2,6},{3,7},{4,8},{5,9},{6,10},{7,11},{8,12},{9,13},{1... | collective-permute-start | bytes 1572872 | tf_op jit(solution)/shard_map/ppermute | solution.py:17
  25.3 1.8 fusion.39
  28.0 5.3 %collective-permute-start.1 = (bf16[2,128,1024]{1,2,0:T(8,128)(2,1)}, bf16[2,128,1024]{1,2,0:T(8,128)(2,1)}, u32[]{:S(2)}, u32[]{:S(2)}) collective-permute-start(bf16[2,128,1024]{1,2,0:T(8,128)(2,1)} %collective-permute-done), channel_id=1, source_target_pairs={{0,1},{1,2},{2,3},{3,4},{4,5},{5,6},{6,7},{7,8},{8,9},{9,10},{10,1... | collective-permute-start | bytes 1572872 | tf_op jit(solution)/shard_map/ppermute | solution.py:17
  33.2 1.9 %fusion.41 = (bf16[1,128,1024]{1,2,0:T(8,128)(2,1)}, bf16[1,128,1024]{1,2,0:T(8,128)(2,1)}) fusion(bf16[2,128,1024]{1,2,0:T(8,128)(2,1)} %collective-permute-done), kind=kLoop, calls=%fused_computation.177 | loop fusion | bytes 1048576 | tf_op jit(solution)/shard_map/slice | solution.py:88
  36.5 1.7 constant_dynamic-update-slice_fusion.3
  38.7 1.9 %fusion.38 = (bf16[1,128,1024]{1,2,0:T(8,128)(2,1)}, bf16[1,128,1024]{1,2,0:T(8,128)(2,1)}) fusion(bf16[2,128,1024]{1,2,0:T(8,128)(2,1)} %collective-permute-done.3), kind=kLoop, calls=%fused_computation.174 | loop fusion | bytes 1048576 | tf_op jit(solution)/shard_map/slice | solution.py:88
  41.7 3.1 %collective-permute-done.1 = bf16[2,128,1024]{1,2,0:T(8,128)(2,1)} collective-permute-done((bf16[2,128,1024]{1,2,0:T(8,128)(2,1)}, bf16[2,128,1024]{1,2,0:T(8,128)(2,1)}, u32[]{:S(2)}, u32[]{:S(2)}) %collective-permute-start.1) | collective-permute-done | bytes 524320 | tf_op jit(solution)/shard_map/ppermute | solution.py:17
  44.8 1.9 %fusion.40 = (bf16[1,128,1024]{1,2,0:T(8,128)(2,1)}, bf16[1,128,1024]{1,2,0:T(8,128)(2,1)}) fusion(bf16[2,128,1024]{1,2,0:T(8,128)(2,1)} %collective-permute-done.1), kind=kLoop, calls=%fused_computation.176 | loop fusion | bytes 1048576 | tf_op jit(solution)/shard_map/slice | solution.py:88
  46.7 1.8 copy.105
  53.8 2.1 %collective-permute-start.7 = (bf16[2,128,1024]{1,2,0:T(8,128)(2,1)}, bf16[2,128,1024]{1,2,0:T(8,128)(2,1)}, u32[]{:S(2)}, u32[]{:S(2)}) collective-permute-start(bf16[2,128,1024]{1,2,0:T(8,128)(2,1)} %pad_maximum_fusion.3), channel_id=1, source_target_pairs={{0,8},{1,9},{2,10},{3,11},{4,12},{5,13},{6,14},{7,15},{16,24},{17,... | collective-permute-start | bytes 1572872 | tf_op jit(solution)/shard_map/ppermute | solution.py:17
  55.9 2.4 %collective-permute-start.6 = (bf16[2,128,1024]{1,2,0:T(8,128)(2,1)}, bf16[2,128,1024]{1,2,0:T(8,128)(2,1)}, u32[]{:S(2)}, u32[]{:S(2)}) collective-permute-start(bf16[2,128,1024]{1,2,0:T(8,128)(2,1)} %pad_maximum_fusion.3), channel_id=1, source_target_pairs={{0,4},{1,5},{2,6},{3,7},{4,8},{5,9},{6,10},{7,11},{8,12},{9,13},{1... | collective-permute-start | bytes 1572872 | tf_op jit(solution)/shard_map/ppermute | solution.py:17
  58.3 1.9 %collective-permute-start.5 = (bf16[2,128,1024]{1,2,0:T(8,128)(2,1)}, bf16[2,128,1024]{1,2,0:T(8,128)(2,1)}, u32[]{:S(2)}, u32[]{:S(2)}) collective-permute-start(bf16[2,128,1024]{1,2,0:T(8,128)(2,1)} %pad_maximum_fusion.3), channel_id=1, source_target_pairs={{0,2},{1,3},{2,4},{3,5},{4,6},{5,7},{6,8},{7,9},{8,10},{9,11},{10,... | collective-permute-start | bytes 1572872 | tf_op jit(solution)/shard_map/ppermute | solution.py:17
  66.8 3.4 %collective-permute-start.9 = (bf16[2,128,8,128]{1,3,2,0:T(8,128)(2,1)}, bf16[2,128,8,128]{1,3,2,0:T(8,128)(2,1)}, u32[]{:S(2)}, u32[]{:S(2)}) collective-permute-start(bf16[2,128,8,128]{1,3,2,0:T(8,128)(2,1)} %pad_maximum_fusion.7), channel_id=1, source_target_pairs={{2,0},{3,1},{4,2},{5,3},{6,4},{7,5},{8,6},{9,7},{10,8},{11,9},{12,... | collective-permute-start | bytes 1572872 | tf_op jit(solution)/shard_map/ppermute | solution.py:17
  76.2 7.0 %collective-permute-start.4 = (bf16[2,128,1024]{1,2,0:T(8,128)(2,1)}, bf16[2,128,1024]{1,2,0:T(8,128)(2,1)}, u32[]{:S(2)}, u32[]{:S(2)}) collective-permute-start(bf16[2,128,1024]{1,2,0:T(8,128)(2,1)} %pad_maximum_fusion.3), channel_id=1, source_target_pairs={{0,1},{1,2},{2,3},{3,4},{4,5},{5,6},{6,7},{7,8},{8,9},{9,10},{10,1... | collective-permute-start | bytes 1572872 | tf_op jit(solution)/shard_map/ppermute | solution.py:17
  83.2 4.5 %collective-permute-start.10 = (bf16[2,128,8,128]{1,3,2,0:T(8,128)(2,1)}, bf16[2,128,8,128]{1,3,2,0:T(8,128)(2,1)}, u32[]{:S(2)}, u32[]{:S(2)}) collective-permute-start(bf16[2,128,8,128]{1,3,2,0:T(8,128)(2,1)} %pad_maximum_fusion.8), channel_id=1, source_target_pairs={{4,0},{5,1},{6,2},{7,3},{8,4},{9,5},{10,6},{11,7},{12,8},{13,9},{1... | collective-permute-start | bytes 1572872 | tf_op jit(solution)/shard_map/ppermute | solution.py:17
  91.5 6.4 %collective-permute-done.5 = bf16[2,128,1024]{1,2,0:T(8,128)(2,1)} collective-permute-done((bf16[2,128,1024]{1,2,0:T(8,128)(2,1)}, bf16[2,128,1024]{1,2,0:T(8,128)(2,1)}, u32[]{:S(2)}, u32[]{:S(2)}) %collective-permute-start.5) | collective-permute-done | bytes 524320 | tf_op jit(solution)/shard_map/ppermute | solution.py:17
  97.9 8.4 %collective-permute-start.8 = (bf16[2,128,8,128]{1,3,2,0:T(8,128)(2,1)}, bf16[2,128,8,128]{1,3,2,0:T(8,128)(2,1)}, u32[]{:S(2)}, u32[]{:S(2)}) collective-permute-start(bf16[2,128,8,128]{1,3,2,0:T(8,128)(2,1)} %pad_maximum_fusion.6), channel_id=1, source_target_pairs={{1,0},{2,1},{3,2},{4,3},{5,4},{6,5},{7,6},{8,7},{9,8},{10,9},{11,1... | collective-permute-start | bytes 1572872 | tf_op jit(solution)/shard_map/ppermute | solution.py:17
  106.4 1.8 fusion.36
  108.3 1.9 %fusion.37 = (bf16[1,128,1024]{1,2,0:T(8,128)(2,1)}, bf16[1,128,1024]{1,2,0:T(8,128)(2,1)}) fusion(bf16[2,128,1024]{1,2,0:T(8,128)(2,1)} %collective-permute-done.4), kind=kLoop, calls=%fused_computation.173 | loop fusion | bytes 1048576 | tf_op jit(solution)/shard_map/slice | solution.py:88
  120.0 1.9 %collective-permute-start.13 = (bf16[2,128,8,128]{1,3,2,0:T(8,128)(2,1)}, bf16[2,128,8,128]{1,3,2,0:T(8,128)(2,1)}, u32[]{:S(2)}, u32[]{:S(2)}) collective-permute-start(bf16[2,128,8,128]{1,3,2,0:T(8,128)(2,1)} %pad_maximum_fusion.11), channel_id=1, source_target_pairs={{2,0},{3,1},{4,2},{5,3},{6,4},{7,5},{8,6},{9,7},{10,8},{11,9},{12,... | collective-permute-start | bytes 1572872 | tf_op jit(solution)/shard_map/ppermute | solution.py:17
  124.5 1.9 %collective-permute-start.14 = (bf16[2,128,8,128]{1,3,2,0:T(8,128)(2,1)}, bf16[2,128,8,128]{1,3,2,0:T(8,128)(2,1)}, u32[]{:S(2)}, u32[]{:S(2)}) collective-permute-start(bf16[2,128,8,128]{1,3,2,0:T(8,128)(2,1)} %pad_maximum_fusion.12), channel_id=1, source_target_pairs={{4,0},{5,1},{6,2},{7,3},{8,4},{9,5},{10,6},{11,7},{12,8},{13,9},{1... | collective-permute-start | bytes 1572872 | tf_op jit(solution)/shard_map/ppermute | solution.py:17
  127.7 1.9 %collective-permute-start.12 = (bf16[2,128,8,128]{1,3,2,0:T(8,128)(2,1)}, bf16[2,128,8,128]{1,3,2,0:T(8,128)(2,1)}, u32[]{:S(2)}, u32[]{:S(2)}) collective-permute-start(bf16[2,128,8,128]{1,3,2,0:T(8,128)(2,1)} %pad_maximum_fusion.10), channel_id=1, source_target_pairs={{1,0},{2,1},{3,2},{4,3},{5,4},{6,5},{7,6},{8,7},{9,8},{10,9},{11,1... | collective-permute-start | bytes 1572872 | tf_op jit(solution)/shard_map/ppermute | solution.py:17
  129.7 2.6 %fusion.25 = (bf16[128,8,128]{0,2,1:T(8,128)(2,1)}, f32[128,8,128]{0,2,1:T(8,128)S(1)}) fusion(bf16[128,8,128]{0,2,1:T(8,128)(2,1)S(1)} %copy-done.11, bf16[2,128,8,128]{1,3,2,0:T(8,128)(2,1)} %collective-permute-done.11, bf16[2,128,8,128]{1,3,2,0:T(8,128)(2,1)} %collective-permute-done.10, bf16[2,128,8,128]{1,3,2,0:T(8,128)(2,1)} %collective-permute-done.9, ...), kind=kLoop, calls=%fused_computation.62 | loop fusion | flops 2490368 | bytes 3407872 | tf_op jit(solution)/shard_map/convert_element_type | solution.py:177
  132.3 1.8 copy.142
  135.0 1.9 %pad_maximum_fusion.4 = bf16[128,2048]{1,0:T(8,128)(2,1)} fusion(bf16[128,1024]{1,0:T(8,128)(2,1)} %copy.119, bf16[128,1024]{1,0:T(8,128)(2,1)} %copy.118), kind=kLoop, calls=%fused_computation.44 | loop fusion | flops 1048576 | bytes 1048576 | tf_op jit(solution)/shard_map/concatenate | solution.py:181
  138.2 4.0 %collective-permute-done.14 = bf16[2,128,8,128]{1,3,2,0:T(8,128)(2,1)} collective-permute-done((bf16[2,128,8,128]{1,3,2,0:T(8,128)(2,1)}, bf16[2,128,8,128]{1,3,2,0:T(8,128)(2,1)}, u32[]{:S(2)}, u32[]{:S(2)}) %collective-permute-start.14) | collective-permute-done | bytes 524320 | tf_op jit(solution)/shard_map/ppermute | solution.py:17
  142.2 12.1 %collective-permute-done.15 = bf16[2,128,8,128]{1,3,2,0:T(8,128)(2,1)} collective-permute-done((bf16[2,128,8,128]{1,3,2,0:T(8,128)(2,1)}, bf16[2,128,8,128]{1,3,2,0:T(8,128)(2,1)}, u32[]{:S(2)}, u32[]{:S(2)}) %collective-permute-start.15) | collective-permute-done | bytes 524320 | tf_op jit(solution)/shard_map/ppermute | solution.py:17
  154.3 23.4 %collective-permute-done.12 = bf16[2,128,8,128]{1,3,2,0:T(8,128)(2,1)} collective-permute-done((bf16[2,128,8,128]{1,3,2,0:T(8,128)(2,1)}, bf16[2,128,8,128]{1,3,2,0:T(8,128)(2,1)}, u32[]{:S(2)}, u32[]{:S(2)}) %collective-permute-start.12) | collective-permute-done | bytes 524320 | tf_op jit(solution)/shard_map/ppermute | solution.py:17
  177.7 1.9 %fusion.24 = (bf16[128,8,128]{0,2,1:T(8,128)(2,1)S(1)}, f32[128,8,128]{0,2,1:T(8,128)S(1)}) fusion(bf16[128,8,128]{0,2,1:T(8,128)(2,1)S(1)} %copy-done.14, bf16[2,128,8,128]{1,3,2,0:T(8,128)(2,1)} %collective-permute-done.15, bf16[2,128,8,128]{1,3,2,0:T(8,128)(2,1)} %collective-permute-done.14, bf16[2,128,8,128]{1,3,2,0:T(8,128)(2,1)} %collective-permute-done.13, ...), kind=kLoop, calls=%fused_computation.57 | loop fusion | flops 2490368 | bytes 3407872 | tf_op jit(solution)/shard_map/convert_element_type | solution.py:177
  (157 shorter events, 54.7 us)
Async XLA Ops:
  0.6 3.1 %copy-start.15 = (bf16[128,2048]{1,0:T(8,128)(2,1)S(1)}, bf16[128,2048]{1,0:T(8,128)(2,1)}, u32[]{:S(2)}) copy-start(bf16[128,2048]{1,0:T(8,128)(2,1)} %param.7) | copy-start | bytes 1572868
  6.2 8.8 %copy-start.17 = (bf16[128,2048]{1,0:T(8,128)(2,1)S(1)}, bf16[128,2048]{1,0:T(8,128)(2,1)}, u32[]{:S(2)}) copy-start(bf16[128,2048]{1,0:T(8,128)(2,1)} %param.10) | copy-start | bytes 1572868
  6.2 8.8 %copy-start.18 = (s32[4]{0:T(128)S(1)}, s32[4]{0:T(128)}, u32[]{:S(2)}) copy-start(s32[4]{0:T(128)} %constant.35) | copy-start | bytes 52
  7.1 15.0 %collective-permute-start.2 = (bf16[2,128,1024]{1,2,0:T(8,128)(2,1)}, bf16[2,128,1024]{1,2,0:T(8,128)(2,1)}, u32[]{:S(2)}, u32[]{:S(2)}) collective-permute-start(bf16[2,128,1024]{1,2,0:T(8,128)(2,1)} %pad_maximum_fusion.1), channel_id=1, source_target_pairs={{0,4},{1,5},{2,6},{3,7},{4,8},{5,9},{6,10},{7,11},{8,12},{9,13},{1... | collective-permute-start | bytes 1572872 | tf_op jit(solution)/shard_map/ppermute | solution.py:17
  10.3 17.7 %collective-permute-start = (bf16[2,128,1024]{1,2,0:T(8,128)(2,1)}, bf16[2,128,1024]{1,2,0:T(8,128)(2,1)}, u32[]{:S(2)}, u32[]{:S(2)}) collective-permute-start(bf16[2,128,1024]{1,2,0:T(8,128)(2,1)} %pad_maximum_fusion.1), channel_id=1, source_target_pairs={{0,1},{1,2},{2,3},{3,4},{4,5},{5,6},{6,7},{7,8},{8,9},{9,10},{10,1... | collective-permute-start | bytes 1572872 | tf_op jit(solution)/shard_map/ppermute | solution.py:17
  22.1 16.6 %collective-permute-start.3 = (bf16[2,128,1024]{1,2,0:T(8,128)(2,1)}, bf16[2,128,1024]{1,2,0:T(8,128)(2,1)}, u32[]{:S(2)}, u32[]{:S(2)}) collective-permute-start(bf16[2,128,1024]{1,2,0:T(8,128)(2,1)} %collective-permute-done.2), channel_id=1, source_target_pairs={{0,4},{1,5},{2,6},{3,7},{4,8},{5,9},{6,10},{7,11},{8,12},{9,13},{1... | collective-permute-start | bytes 1572872 | tf_op jit(solution)/shard_map/ppermute | solution.py:17
  28.0 16.9 %collective-permute-start.1 = (bf16[2,128,1024]{1,2,0:T(8,128)(2,1)}, bf16[2,128,1024]{1,2,0:T(8,128)(2,1)}, u32[]{:S(2)}, u32[]{:S(2)}) collective-permute-start(bf16[2,128,1024]{1,2,0:T(8,128)(2,1)} %collective-permute-done), channel_id=1, source_target_pairs={{0,1},{1,2},{2,3},{3,4},{4,5},{5,6},{6,7},{7,8},{8,9},{9,10},{10,1... | collective-permute-start | bytes 1572872 | tf_op jit(solution)/shard_map/ppermute | solution.py:17
  51.0 1.3 copy-start.3
  51.0 1.3 copy-start.10
  51.0 1.4 copy-start.6
  51.0 1.5 copy-start.7
  53.8 29.4 %collective-permute-start.7 = (bf16[2,128,1024]{1,2,0:T(8,128)(2,1)}, bf16[2,128,1024]{1,2,0:T(8,128)(2,1)}, u32[]{:S(2)}, u32[]{:S(2)}) collective-permute-start(bf16[2,128,1024]{1,2,0:T(8,128)(2,1)} %pad_maximum_fusion.3), channel_id=1, source_target_pairs={{0,8},{1,9},{2,10},{3,11},{4,12},{5,13},{6,14},{7,15},{16,24},{17,... | collective-permute-start | bytes 1572872 | tf_op jit(solution)/shard_map/ppermute | solution.py:17
  55.9 33.1 %collective-permute-start.6 = (bf16[2,128,1024]{1,2,0:T(8,128)(2,1)}, bf16[2,128,1024]{1,2,0:T(8,128)(2,1)}, u32[]{:S(2)}, u32[]{:S(2)}) collective-permute-start(bf16[2,128,1024]{1,2,0:T(8,128)(2,1)} %pad_maximum_fusion.3), channel_id=1, source_target_pairs={{0,4},{1,5},{2,6},{3,7},{4,8},{5,9},{6,10},{7,11},{8,12},{9,13},{1... | collective-permute-start | bytes 1572872 | tf_op jit(solution)/shard_map/ppermute | solution.py:17
  58.3 39.6 %collective-permute-start.5 = (bf16[2,128,1024]{1,2,0:T(8,128)(2,1)}, bf16[2,128,1024]{1,2,0:T(8,128)(2,1)}, u32[]{:S(2)}, u32[]{:S(2)}) collective-permute-start(bf16[2,128,1024]{1,2,0:T(8,128)(2,1)} %pad_maximum_fusion.3), channel_id=1, source_target_pairs={{0,2},{1,3},{2,4},{3,5},{4,6},{5,7},{6,8},{7,9},{8,10},{9,11},{10,... | collective-permute-start | bytes 1572872 | tf_op jit(solution)/shard_map/ppermute | solution.py:17
  66.0 5.9 %copy-start.4 = (bf16[1,128,8,128]{1,3,2,0:T(8,128)(2,1)S(1)}, bf16[1,128,8,128]{1,3,2,0:T(8,128)(2,1)}, u32[]{:S(2)}) copy-start(bf16[1,128,8,128]{1,3,2,0:T(8,128)(2,1)} %get-tuple-element.13) | copy-start | bytes 786436
  66.8 57.7 %collective-permute-start.9 = (bf16[2,128,8,128]{1,3,2,0:T(8,128)(2,1)}, bf16[2,128,8,128]{1,3,2,0:T(8,128)(2,1)}, u32[]{:S(2)}, u32[]{:S(2)}) collective-permute-start(bf16[2,128,8,128]{1,3,2,0:T(8,128)(2,1)} %pad_maximum_fusion.7), channel_id=1, source_target_pairs={{2,0},{3,1},{4,2},{5,3},{6,4},{7,5},{8,6},{9,7},{10,8},{11,9},{12,... | collective-permute-start | bytes 1572872 | tf_op jit(solution)/shard_map/ppermute | solution.py:17
  76.2 32.1 %collective-permute-start.4 = (bf16[2,128,1024]{1,2,0:T(8,128)(2,1)}, bf16[2,128,1024]{1,2,0:T(8,128)(2,1)}, u32[]{:S(2)}, u32[]{:S(2)}) collective-permute-start(bf16[2,128,1024]{1,2,0:T(8,128)(2,1)} %pad_maximum_fusion.3), channel_id=1, source_target_pairs={{0,1},{1,2},{2,3},{3,4},{4,5},{5,6},{6,7},{7,8},{8,9},{9,10},{10,1... | collective-permute-start | bytes 1572872 | tf_op jit(solution)/shard_map/ppermute | solution.py:17
  83.2 43.2 %collective-permute-start.10 = (bf16[2,128,8,128]{1,3,2,0:T(8,128)(2,1)}, bf16[2,128,8,128]{1,3,2,0:T(8,128)(2,1)}, u32[]{:S(2)}, u32[]{:S(2)}) collective-permute-start(bf16[2,128,8,128]{1,3,2,0:T(8,128)(2,1)} %pad_maximum_fusion.8), channel_id=1, source_target_pairs={{4,0},{5,1},{6,2},{7,3},{8,4},{9,5},{10,6},{11,7},{12,8},{13,9},{1... | collective-permute-start | bytes 1572872 | tf_op jit(solution)/shard_map/ppermute | solution.py:17
  89.0 38.7 %collective-permute-start.11 = (bf16[2,128,8,128]{1,3,2,0:T(8,128)(2,1)}, bf16[2,128,8,128]{1,3,2,0:T(8,128)(2,1)}, u32[]{:S(2)}, u32[]{:S(2)}) collective-permute-start(bf16[2,128,8,128]{1,3,2,0:T(8,128)(2,1)} %pad_maximum_fusion.9), channel_id=1, source_target_pairs={{8,0},{9,1},{10,2},{11,3},{12,4},{13,5},{14,6},{15,7},{24,16},{25,... | collective-permute-start | bytes 1572872 | tf_op jit(solution)/shard_map/ppermute | solution.py:17
  97.9 31.7 %collective-permute-start.8 = (bf16[2,128,8,128]{1,3,2,0:T(8,128)(2,1)}, bf16[2,128,8,128]{1,3,2,0:T(8,128)(2,1)}, u32[]{:S(2)}, u32[]{:S(2)}) collective-permute-start(bf16[2,128,8,128]{1,3,2,0:T(8,128)(2,1)} %pad_maximum_fusion.6), channel_id=1, source_target_pairs={{1,0},{2,1},{3,2},{4,3},{5,4},{6,5},{7,6},{8,7},{9,8},{10,9},{11,1... | collective-permute-start | bytes 1572872 | tf_op jit(solution)/shard_map/ppermute | solution.py:17
  112.9 1.3 copy-start.9
  112.9 1.4 copy-start.8
  120.0 18.2 %collective-permute-start.13 = (bf16[2,128,8,128]{1,3,2,0:T(8,128)(2,1)}, bf16[2,128,8,128]{1,3,2,0:T(8,128)(2,1)}, u32[]{:S(2)}, u32[]{:S(2)}) collective-permute-start(bf16[2,128,8,128]{1,3,2,0:T(8,128)(2,1)} %pad_maximum_fusion.11), channel_id=1, source_target_pairs={{2,0},{3,1},{4,2},{5,3},{6,4},{7,5},{8,6},{9,7},{10,8},{11,9},{12,... | collective-permute-start | bytes 1572872 | tf_op jit(solution)/shard_map/ppermute | solution.py:17
  122.8 6.9 %copy-start.11 = (bf16[128,8,128]{0,2,1:T(8,128)(2,1)S(1)}, bf16[128,8,128]{0,2,1:T(8,128)(2,1)}, u32[]{:S(2)}) copy-start(bf16[128,8,128]{0,2,1:T(8,128)(2,1)} %get-tuple-element.12) | copy-start | bytes 786436
  122.8 6.9 %copy-start.12 = (bf16[128,8,128]{0,2,1:T(8,128)(2,1)S(1)}, bf16[128,8,128]{0,2,1:T(8,128)(2,1)}, u32[]{:S(2)}) copy-start(bf16[128,8,128]{0,2,1:T(8,128)(2,1)} %get-tuple-element.26) | copy-start | bytes 786436
  124.5 17.7 %collective-permute-start.14 = (bf16[2,128,8,128]{1,3,2,0:T(8,128)(2,1)}, bf16[2,128,8,128]{1,3,2,0:T(8,128)(2,1)}, u32[]{:S(2)}, u32[]{:S(2)}) collective-permute-start(bf16[2,128,8,128]{1,3,2,0:T(8,128)(2,1)} %pad_maximum_fusion.12), channel_id=1, source_target_pairs={{4,0},{5,1},{6,2},{7,3},{8,4},{9,5},{10,6},{11,7},{12,8},{13,9},{1... | collective-permute-start | bytes 1572872 | tf_op jit(solution)/shard_map/ppermute | solution.py:17
  126.4 27.9 %collective-permute-start.15 = (bf16[2,128,8,128]{1,3,2,0:T(8,128)(2,1)}, bf16[2,128,8,128]{1,3,2,0:T(8,128)(2,1)}, u32[]{:S(2)}, u32[]{:S(2)}) collective-permute-start(bf16[2,128,8,128]{1,3,2,0:T(8,128)(2,1)} %pad_maximum_fusion.13), channel_id=1, source_target_pairs={{8,0},{9,1},{10,2},{11,3},{12,4},{13,5},{14,6},{15,7},{24,16},{25,... | collective-permute-start | bytes 1572872 | tf_op jit(solution)/shard_map/ppermute | solution.py:17
  127.7 50.0 %collective-permute-start.12 = (bf16[2,128,8,128]{1,3,2,0:T(8,128)(2,1)}, bf16[2,128,8,128]{1,3,2,0:T(8,128)(2,1)}, u32[]{:S(2)}, u32[]{:S(2)}) collective-permute-start(bf16[2,128,8,128]{1,3,2,0:T(8,128)(2,1)} %pad_maximum_fusion.10), channel_id=1, source_target_pairs={{1,0},{2,1},{3,2},{4,3},{5,4},{6,5},{7,6},{8,7},{9,8},{10,9},{11,1... | collective-permute-start | bytes 1572872 | tf_op jit(solution)/shard_map/ppermute | solution.py:17
  136.8 40.9 %copy-start.13 = (bf16[128,8,128]{0,2,1:T(8,128)(2,1)S(1)}, bf16[128,8,128]{0,2,1:T(8,128)(2,1)}, u32[]{:S(2)}) copy-start(bf16[128,8,128]{0,2,1:T(8,128)(2,1)} %get-tuple-element.31) | copy-start | bytes 786436
  136.8 40.9 %copy-start.14 = (bf16[128,8,128]{0,2,1:T(8,128)(2,1)S(1)}, bf16[128,8,128]{0,2,1:T(8,128)(2,1)}, u32[]{:S(2)}) copy-start(bf16[128,8,128]{0,2,1:T(8,128)(2,1)} %get-tuple-element.17) | copy-start | bytes 786436
  138.2 41.6 %copy-start = (f32[128,8,128]{0,2,1:T(8,128)S(1)}, f32[128,8,128]{0,2,1:T(8,128)}, u32[]{:S(2)}) copy-start(f32[128,8,128]{0,2,1:T(8,128)} %convolution_bitcast_fusion.1) | copy-start | bytes 1572868
  138.2 41.6 %copy-start.1 = (f32[128,8,128]{0,2,1:T(8,128)S(1)}, f32[128,8,128]{0,2,1:T(8,128)}, u32[]{:S(2)}) copy-start(f32[128,8,128]{0,2,1:T(8,128)} %convolution_bitcast_fusion) | copy-start | bytes 1572868
  (3 other events, 3.3 us)

commit v25 on v18

--- a/solution.py
+++ b/solution.py
@@ -157,7 +157,7 @@
     for chunk, cols in enumerate(columns):
         key_c, value_c = key_rot[:, cols], values[:, cols]
         if pending:
-            key_c, value_c, _ = lax.optimization_barrier((key_c, value_c, pieces[-1][0]))
+            key_c, value_c, _ = lax.optimization_barrier((key_c, value_c, pending[-1]))
         received = send_chunk(key_c, value_c, offsets, relay=not pending)
         output, query_grad, own, outgoing = attend_chunk(
             query_rot[:, cols], received, grad_out[:, cols], allowed, offsets, chunk_heads

time: 184 us -> 192 us (1.043)
  waiting for transfers between devices: 54.7 us -> 70.8 us
  starting transfers between devices: 53.7 us -> 47.9 us
  local copies, waits for them, and re-layouts: 41.2 us -> 38.3 us
    ppermute x16, waiting for transfers between devices: 54.7 us -> 70.8 us  [from_behind(): lax.ppermute(value, axis, [(source, source + steps) for source in range(l...]
    slice x8 -> x4, local copies, waits for them, and re-layouts: 13.1 us -> 5.05 us  [attend_chunk(): moved[0].reshape(head_shape)]
    slice x0 -> x4, local copies, waits for them, and re-layouts: none -> 7.15 us  [attend_chunk(): moved[1].reshape(head_shape)]
    ppermute x16, starting transfers between devices: 53.7 us -> 47.9 us  [from_behind(): lax.ppermute(value, axis, [(source, source + steps) for source in range(l...]
    another operation x12, local copies, waits for them, and re-layouts: 6.97 us -> 4.67 us  [attend_chunk(): jnp.stack([moved[0].reshape(head_shape) for moved in received])[None]]
    unnamed x59 -> x67, local copies, waits for them, and re-layouts: 10.4 us -> 8.88 us
  transfers between devices with their start and end apart: 16 -> 16, of which waited for: 8 -> 11; matrix products, arithmetic and copies ran while one was open for 28% -> 21% of each run, Pallas kernels for 0% -> 0%
where the time goes in v25:
time: 192 us; the launch traced here: 191 us
  waiting for transfers between devices  70.8 us (37%)
  starting transfers between devices  47.9 us (25%)
  local copies, waits for them, and re-layouts  38.3 us (20%)
  other arithmetic  21.9 us (11%)
  matrix products  9.84 us (5%)
  between operations  2.07 us (1%)
    ppermute x16, waiting for transfers between devices, from_behind(): lax.ppermute(value, axis, [(source, source + steps) for source in range(l...  70.8 us
    ppermute x16, starting transfers between devices, from_behind(): lax.ppermute(value, axis, [(source, source + steps) for source in range(l...  47.9 us
    unnamed x67, local copies, waits for them, and re-layouts  8.88 us
    slice x4, local copies, waits for them, and re-layouts, attend_chunk(): moved[1].reshape(head_shape)  7.15 us
    another operation x8, other arithmetic, attend_chunk(): jnp.stack([key_terms[0, slot_index], value_terms[0, slot_index]])  6.76 us
    another operation x6, other arithmetic  5.53 us
    slice x4, local copies, waits for them, and re-layouts, attend_chunk(): moved[0].reshape(head_shape)  5.05 us
    another operation x12, local copies, waits for them, and re-layouts, attend_chunk(): jnp.stack([moved[0].reshape(head_shape) for moved in received])[None]  4.67 us
  transfers between devices with their start and end apart: 16, of which 11 were waited for; matrix products, arithmetic and copies ran while one was open for 21% of the time, Pallas kernels for 0%

profile of v25, /device:TPU:15, one launch (start us, length us, event | category | flops | bytes accessed | tf_op | source)
XLA Modules:
  0.0 190.7 jit_solution(12147074621148949007)
XLA Ops:
  7.5 3.2 %collective-permute-start.2 = (bf16[2,128,1024]{1,2,0:T(8,128)(2,1)}, bf16[2,128,1024]{1,2,0:T(8,128)(2,1)}, u32[]{:S(2)}, u32[]{:S(2)}) collective-permute-start(bf16[2,128,1024]{1,2,0:T(8,128)(2,1)} %pad_maximum_fusion.3), channel_id=1, source_target_pairs={{0,4},{1,5},{2,6},{3,7},{4,8},{5,9},{6,10},{7,11},{8,12},{9,13},{1... | collective-permute-start | bytes 1572872 | tf_op jit(solution)/shard_map/ppermute | solution.py:17
  10.7 4.0 %collective-permute-start = (bf16[2,128,1024]{1,2,0:T(8,128)(2,1)}, bf16[2,128,1024]{1,2,0:T(8,128)(2,1)}, u32[]{:S(2)}, u32[]{:S(2)}) collective-permute-start(bf16[2,128,1024]{1,2,0:T(8,128)(2,1)} %pad_maximum_fusion.3), channel_id=1, source_target_pairs={{0,1},{1,2},{2,3},{3,4},{4,5},{5,6},{6,7},{7,8},{8,9},{9,10},{10,1... | collective-permute-start | bytes 1572872 | tf_op jit(solution)/shard_map/ppermute | solution.py:17
  18.9 3.6 %collective-permute-done.2 = bf16[2,128,1024]{1,2,0:T(8,128)(2,1)} collective-permute-done((bf16[2,128,1024]{1,2,0:T(8,128)(2,1)}, bf16[2,128,1024]{1,2,0:T(8,128)(2,1)}, u32[]{:S(2)}, u32[]{:S(2)}) %collective-permute-start.2) | collective-permute-done | bytes 524320 | tf_op jit(solution)/shard_map/ppermute | solution.py:17
  22.5 3.2 %collective-permute-start.3 = (bf16[2,128,1024]{1,2,0:T(8,128)(2,1)}, bf16[2,128,1024]{1,2,0:T(8,128)(2,1)}, u32[]{:S(2)}, u32[]{:S(2)}) collective-permute-start(bf16[2,128,1024]{1,2,0:T(8,128)(2,1)} %collective-permute-done.2), channel_id=1, source_target_pairs={{0,4},{1,5},{2,6},{3,7},{4,8},{5,9},{6,10},{7,11},{8,12},{9,13},{1... | collective-permute-start | bytes 1572872 | tf_op jit(solution)/shard_map/ppermute | solution.py:17
  25.7 1.8 fusion.45
  28.4 5.3 %collective-permute-start.1 = (bf16[2,128,1024]{1,2,0:T(8,128)(2,1)}, bf16[2,128,1024]{1,2,0:T(8,128)(2,1)}, u32[]{:S(2)}, u32[]{:S(2)}) collective-permute-start(bf16[2,128,1024]{1,2,0:T(8,128)(2,1)} %collective-permute-done), channel_id=1, source_target_pairs={{0,1},{1,2},{2,3},{3,4},{4,5},{5,6},{6,7},{7,8},{8,9},{9,10},{10,1... | collective-permute-start | bytes 1572872 | tf_op jit(solution)/shard_map/ppermute | solution.py:17
  33.6 1.8 fusion.47
  41.1 4.1 %collective-permute-done.1 = bf16[2,128,1024]{1,2,0:T(8,128)(2,1)} collective-permute-done((bf16[2,128,1024]{1,2,0:T(8,128)(2,1)}, bf16[2,128,1024]{1,2,0:T(8,128)(2,1)}, u32[]{:S(2)}, u32[]{:S(2)}) %collective-permute-start.1) | collective-permute-done | bytes 524320 | tf_op jit(solution)/shard_map/ppermute | solution.py:17
  45.2 1.9 fusion.46
  53.4 2.2 %fusion.12 = bf16[1,8,128,5,128]{2,4,3,1,0:T(8,128)(2,1)S(1)} fusion(bf16[5,128,8,128]{1,3,0,2:T(8,128)(2,1)S(1)} %constant_dynamic-update-slice_fusion, bf16[128,8,128,1]{0,2,3,1:T(8,128)(2,1)} %bitcast.366, f32[8,128,5,128]{1,3,2,0:T(8,128)S(1)} %bitcast.342, f32[8,128]{1,0:T(8,128)S(1)} %bitcast.393, f32[8,128]{1,0:T(8,128)S(1)} %log_add_fusion.1, ...), kind=kOutput, calls=%fused_computation.24 | convolution fusion | flops 172359680 | bytes 5595136 | tf_op jit(solution)/shard_map/bthd,bnuhd->bhtnu/dot_general | solution.py:105
  61.3 2.1 %collective-permute-start.7 = (bf16[2,128,1024]{1,2,0:T(8,128)(2,1)}, bf16[2,128,1024]{1,2,0:T(8,128)(2,1)}, u32[]{:S(2)}, u32[]{:S(2)}) collective-permute-start(bf16[2,128,1024]{1,2,0:T(8,128)(2,1)} %pad_maximum_fusion.9), channel_id=1, source_target_pairs={{0,8},{1,9},{2,10},{3,11},{4,12},{5,13},{6,14},{7,15},{16,24},{17,... | collective-permute-start | bytes 1572872 | tf_op jit(solution)/shard_map/ppermute | solution.py:17
  63.4 1.8 copy.185
  65.2 2.4 %collective-permute-start.6 = (bf16[2,128,1024]{1,2,0:T(8,128)(2,1)}, bf16[2,128,1024]{1,2,0:T(8,128)(2,1)}, u32[]{:S(2)}, u32[]{:S(2)}) collective-permute-start(bf16[2,128,1024]{1,2,0:T(8,128)(2,1)} %pad_maximum_fusion.9), channel_id=1, source_target_pairs={{0,4},{1,5},{2,6},{3,7},{4,8},{5,9},{6,10},{7,11},{8,12},{9,13},{1... | collective-permute-start | bytes 1572872 | tf_op jit(solution)/shard_map/ppermute | solution.py:17
  69.0 2.0 %collective-permute-start.5 = (bf16[2,128,1024]{1,2,0:T(8,128)(2,1)}, bf16[2,128,1024]{1,2,0:T(8,128)(2,1)}, u32[]{:S(2)}, u32[]{:S(2)}) collective-permute-start(bf16[2,128,1024]{1,2,0:T(8,128)(2,1)} %pad_maximum_fusion.9), channel_id=1, source_target_pairs={{0,2},{1,3},{2,4},{3,5},{4,6},{5,7},{6,8},{7,9},{8,10},{9,11},{10,... | collective-permute-start | bytes 1572872 | tf_op jit(solution)/shard_map/ppermute | solution.py:17
  71.0 5.6 %collective-permute-start.4 = (bf16[2,128,1024]{1,2,0:T(8,128)(2,1)}, bf16[2,128,1024]{1,2,0:T(8,128)(2,1)}, u32[]{:S(2)}, u32[]{:S(2)}) collective-permute-start(bf16[2,128,1024]{1,2,0:T(8,128)(2,1)} %pad_maximum_fusion.9), channel_id=1, source_target_pairs={{0,1},{1,2},{2,3},{3,4},{4,5},{5,6},{6,7},{7,8},{8,9},{9,10},{10,1... | collective-permute-start | bytes 1572872 | tf_op jit(solution)/shard_map/ppermute | solution.py:17
  79.7 3.8 %collective-permute-done.7 = bf16[2,128,1024]{1,2,0:T(8,128)(2,1)} collective-permute-done((bf16[2,128,1024]{1,2,0:T(8,128)(2,1)}, bf16[2,128,1024]{1,2,0:T(8,128)(2,1)}, u32[]{:S(2)}, u32[]{:S(2)}) %collective-permute-start.7) | collective-permute-done | bytes 524320 | tf_op jit(solution)/shard_map/ppermute | solution.py:17
  83.4 7.2 %collective-permute-start.8 = (bf16[2,128,8,128]{1,3,2,0:T(8,128)(2,1)}, bf16[2,128,8,128]{1,3,2,0:T(8,128)(2,1)}, u32[]{:S(2)}, u32[]{:S(2)}) collective-permute-start(bf16[2,128,8,128]{1,3,2,0:T(8,128)(2,1)} %pad_maximum_fusion.5), channel_id=1, source_target_pairs={{1,0},{2,1},{3,2},{4,3},{5,4},{6,5},{7,6},{8,7},{9,8},{10,9},{11,1... | collective-permute-start | bytes 1572872 | tf_op jit(solution)/shard_map/ppermute | solution.py:17
  91.9 2.8 %collective-permute-done.6 = bf16[2,128,1024]{1,2,0:T(8,128)(2,1)} collective-permute-done((bf16[2,128,1024]{1,2,0:T(8,128)(2,1)}, bf16[2,128,1024]{1,2,0:T(8,128)(2,1)}, u32[]{:S(2)}, u32[]{:S(2)}) %collective-permute-start.6) | collective-permute-done | bytes 524320 | tf_op jit(solution)/shard_map/ppermute | solution.py:17
  94.7 1.9 %collective-permute-start.9 = (bf16[2,128,8,128]{1,3,2,0:T(8,128)(2,1)}, bf16[2,128,8,128]{1,3,2,0:T(8,128)(2,1)}, u32[]{:S(2)}, u32[]{:S(2)}) collective-permute-start(bf16[2,128,8,128]{1,3,2,0:T(8,128)(2,1)} %pad_maximum_fusion.6), channel_id=1, source_target_pairs={{2,0},{3,1},{4,2},{5,3},{6,4},{7,5},{8,6},{9,7},{10,8},{11,9},{12,... | collective-permute-start | bytes 1572872 | tf_op jit(solution)/shard_map/ppermute | solution.py:17
  97.8 8.1 %collective-permute-done.5 = bf16[2,128,1024]{1,2,0:T(8,128)(2,1)} collective-permute-done((bf16[2,128,1024]{1,2,0:T(8,128)(2,1)}, bf16[2,128,1024]{1,2,0:T(8,128)(2,1)}, u32[]{:S(2)}, u32[]{:S(2)}) %collective-permute-start.5) | collective-permute-done | bytes 524320 | tf_op jit(solution)/shard_map/ppermute | solution.py:17
  106.0 2.1 %collective-permute-start.10 = (bf16[2,128,8,128]{1,3,2,0:T(8,128)(2,1)}, bf16[2,128,8,128]{1,3,2,0:T(8,128)(2,1)}, u32[]{:S(2)}, u32[]{:S(2)}) collective-permute-start(bf16[2,128,8,128]{1,3,2,0:T(8,128)(2,1)} %pad_maximum_fusion.7), channel_id=1, source_target_pairs={{4,0},{5,1},{6,2},{7,3},{8,4},{9,5},{10,6},{11,7},{12,8},{13,9},{1... | collective-permute-start | bytes 1572872 | tf_op jit(solution)/shard_map/ppermute | solution.py:17
  109.3 4.7 %collective-permute-done.4 = bf16[2,128,1024]{1,2,0:T(8,128)(2,1)} collective-permute-done((bf16[2,128,1024]{1,2,0:T(8,128)(2,1)}, bf16[2,128,1024]{1,2,0:T(8,128)(2,1)}, u32[]{:S(2)}, u32[]{:S(2)}) %collective-permute-start.4) | collective-permute-done | bytes 524320 | tf_op jit(solution)/shard_map/ppermute | solution.py:17
  114.0 1.9 fusion.43
  126.1 1.9 %collective-permute-start.13 = (bf16[2,128,8,128]{1,3,2,0:T(8,128)(2,1)}, bf16[2,128,8,128]{1,3,2,0:T(8,128)(2,1)}, u32[]{:S(2)}, u32[]{:S(2)}) collective-permute-start(bf16[2,128,8,128]{1,3,2,0:T(8,128)(2,1)} %pad_maximum_fusion.13), channel_id=1, source_target_pairs={{2,0},{3,1},{4,2},{5,3},{6,4},{7,5},{8,6},{9,7},{10,8},{11,9},{12,... | collective-permute-start | bytes 1572872 | tf_op jit(solution)/shard_map/ppermute | solution.py:17
  130.5 2.0 %collective-permute-start.14 = (bf16[2,128,8,128]{1,3,2,0:T(8,128)(2,1)}, bf16[2,128,8,128]{1,3,2,0:T(8,128)(2,1)}, u32[]{:S(2)}, u32[]{:S(2)}) collective-permute-start(bf16[2,128,8,128]{1,3,2,0:T(8,128)(2,1)} %pad_maximum_fusion.14), channel_id=1, source_target_pairs={{4,0},{5,1},{6,2},{7,3},{8,4},{9,5},{10,6},{11,7},{12,8},{13,9},{1... | collective-permute-start | bytes 1572872 | tf_op jit(solution)/shard_map/ppermute | solution.py:17
  133.9 2.5 %collective-permute-start.12 = (bf16[2,128,8,128]{1,3,2,0:T(8,128)(2,1)}, bf16[2,128,8,128]{1,3,2,0:T(8,128)(2,1)}, u32[]{:S(2)}, u32[]{:S(2)}) collective-permute-start(bf16[2,128,8,128]{1,3,2,0:T(8,128)(2,1)} %pad_maximum_fusion.12), channel_id=1, source_target_pairs={{1,0},{2,1},{3,2},{4,3},{5,4},{6,5},{7,6},{8,7},{9,8},{10,9},{11,1... | collective-permute-start | bytes 1572872 | tf_op jit(solution)/shard_map/ppermute | solution.py:17
  136.4 2.8 %fusion.32 = (bf16[128,8,128]{0,2,1:T(8,128)(2,1)}, f32[128,8,128]{0,2,1:T(8,128)}) fusion(bf16[128,8,128]{0,2,1:T(8,128)(2,1)S(1)} %copy-done.16, bf16[2,128,8,128]{1,3,2,0:T(8,128)(2,1)} %collective-permute-done.11, bf16[2,128,8,128]{1,3,2,0:T(8,128)(2,1)} %collective-permute-done.10, bf16[2,128,8,128]{1,3,2,0:T(8,128)(2,1)} %collective-permute-done.9, ...), kind=kLoop, calls=%fused_computation.72 | loop fusion | flops 2490368 | bytes 3407872 | tf_op jit(solution)/shard_map/convert.23
  141.2 1.8 pad_maximum_fusion.10
  143.6 4.0 %collective-permute-done.14 = bf16[2,128,8,128]{1,3,2,0:T(8,128)(2,1)} collective-permute-done((bf16[2,128,8,128]{1,3,2,0:T(8,128)(2,1)}, bf16[2,128,8,128]{1,3,2,0:T(8,128)(2,1)}, u32[]{:S(2)}, u32[]{:S(2)}) %collective-permute-start.14) | collective-permute-done | bytes 524320 | tf_op jit(solution)/shard_map/ppermute | solution.py:17
  147.6 3.2 %collective-permute-done.15 = bf16[2,128,8,128]{1,3,2,0:T(8,128)(2,1)} collective-permute-done((bf16[2,128,8,128]{1,3,2,0:T(8,128)(2,1)}, bf16[2,128,8,128]{1,3,2,0:T(8,128)(2,1)}, u32[]{:S(2)}, u32[]{:S(2)}) %collective-permute-start.15) | collective-permute-done | bytes 524320 | tf_op jit(solution)/shard_map/ppermute | solution.py:17
  150.8 33.9 %collective-permute-done.12 = bf16[2,128,8,128]{1,3,2,0:T(8,128)(2,1)} collective-permute-done((bf16[2,128,8,128]{1,3,2,0:T(8,128)(2,1)}, bf16[2,128,8,128]{1,3,2,0:T(8,128)(2,1)}, u32[]{:S(2)}, u32[]{:S(2)}) %collective-permute-start.12) | collective-permute-done | bytes 524320 | tf_op jit(solution)/shard_map/ppermute | solution.py:17
  184.7 1.9 %fusion.31 = (bf16[128,8,128]{0,2,1:T(8,128)(2,1)S(1)}, f32[128,8,128]{0,2,1:T(8,128)S(1)}) fusion(bf16[128,8,128]{0,2,1:T(8,128)(2,1)S(1)} %copy-done.19, bf16[2,128,8,128]{1,3,2,0:T(8,128)(2,1)} %collective-permute-done.15, bf16[2,128,8,128]{1,3,2,0:T(8,128)(2,1)} %collective-permute-done.14, bf16[2,128,8,128]{1,3,2,0:T(8,128)(2,1)} %collective-permute-done.13, ...), kind=kLoop, calls=%fused_computation.67 | loop fusion | flops 2490368 | bytes 3407872 | tf_op jit(solution)/shard_map/convert.22
  (159 shorter events, 57.3 us)
Async XLA Ops:
  0.6 3.1 %copy-start.20 = (bf16[128,2048]{1,0:T(8,128)(2,1)S(1)}, bf16[128,2048]{1,0:T(8,128)(2,1)}, u32[]{:S(2)}) copy-start(bf16[128,2048]{1,0:T(8,128)(2,1)} %param.7) | copy-start | bytes 1572868
  6.6 8.8 %copy-start.21 = (bf16[128,2048]{1,0:T(8,128)(2,1)S(1)}, bf16[128,2048]{1,0:T(8,128)(2,1)}, u32[]{:S(2)}) copy-start(bf16[128,2048]{1,0:T(8,128)(2,1)} %param.10) | copy-start | bytes 1572868
  6.6 9.5 %copy-start.22 = (s32[4]{0:T(128)S(1)}, s32[4]{0:T(128)}, u32[]{:S(2)}) copy-start(s32[4]{0:T(128)} %constant.35) | copy-start | bytes 52
  7.5 15.0 %collective-permute-start.2 = (bf16[2,128,1024]{1,2,0:T(8,128)(2,1)}, bf16[2,128,1024]{1,2,0:T(8,128)(2,1)}, u32[]{:S(2)}, u32[]{:S(2)}) collective-permute-start(bf16[2,128,1024]{1,2,0:T(8,128)(2,1)} %pad_maximum_fusion.3), channel_id=1, source_target_pairs={{0,4},{1,5},{2,6},{3,7},{4,8},{5,9},{6,10},{7,11},{8,12},{9,13},{1... | collective-permute-start | bytes 1572872 | tf_op jit(solution)/shard_map/ppermute | solution.py:17
  10.7 17.7 %collective-permute-start = (bf16[2,128,1024]{1,2,0:T(8,128)(2,1)}, bf16[2,128,1024]{1,2,0:T(8,128)(2,1)}, u32[]{:S(2)}, u32[]{:S(2)}) collective-permute-start(bf16[2,128,1024]{1,2,0:T(8,128)(2,1)} %pad_maximum_fusion.3), channel_id=1, source_target_pairs={{0,1},{1,2},{2,3},{3,4},{4,5},{5,6},{6,7},{7,8},{8,9},{9,10},{10,1... | collective-permute-start | bytes 1572872 | tf_op jit(solution)/shard_map/ppermute | solution.py:17
  17.7 35.6 %copy-start.3 = (bf16[128,1024]{0,1:T(8,128)(2,1)}, bf16[128,1024]{0,1:T(8,128)(2,1)S(1)}, u32[]{:S(2)}) copy-start(bf16[128,1024]{0,1:T(8,128)(2,1)S(1)} %copy.180) | copy-start | bytes 786436
  18.9 29.5 %copy-start.1 = (bf16[128,1024]{0,1:T(8,128)(2,1)}, bf16[128,1024]{0,1:T(8,128)(2,1)S(1)}, u32[]{:S(2)}) copy-start(bf16[128,1024]{0,1:T(8,128)(2,1)S(1)} %get-tuple-element.55) | copy-start | bytes 786436
  22.5 16.6 %collective-permute-start.3 = (bf16[2,128,1024]{1,2,0:T(8,128)(2,1)}, bf16[2,128,1024]{1,2,0:T(8,128)(2,1)}, u32[]{:S(2)}, u32[]{:S(2)}) collective-permute-start(bf16[2,128,1024]{1,2,0:T(8,128)(2,1)} %collective-permute-done.2), channel_id=1, source_target_pairs={{0,4},{1,5},{2,6},{3,7},{4,8},{5,9},{6,10},{7,11},{8,12},{9,13},{1... | collective-permute-start | bytes 1572872 | tf_op jit(solution)/shard_map/ppermute | solution.py:17
  28.4 16.9 %collective-permute-start.1 = (bf16[2,128,1024]{1,2,0:T(8,128)(2,1)}, bf16[2,128,1024]{1,2,0:T(8,128)(2,1)}, u32[]{:S(2)}, u32[]{:S(2)}) collective-permute-start(bf16[2,128,1024]{1,2,0:T(8,128)(2,1)} %collective-permute-done), channel_id=1, source_target_pairs={{0,1},{1,2},{2,3},{3,4},{4,5},{5,6},{6,7},{7,8},{8,9},{9,10},{10,1... | collective-permute-start | bytes 1572872 | tf_op jit(solution)/shard_map/ppermute | solution.py:17
  49.8 1.5 copy-start.12
  51.8 1.5 copy-start.4
  53.3 2.2 %copy-start.2 = (bf16[128,1024]{0,1:T(8,128)(2,1)S(1)}, bf16[128,1024]{0,1:T(8,128)(2,1)}, u32[]{:S(2)}) copy-start(bf16[128,1024]{0,1:T(8,128)(2,1)} %copy-done.1) | copy-start | bytes 786436
  61.3 22.2 %collective-permute-start.7 = (bf16[2,128,1024]{1,2,0:T(8,128)(2,1)}, bf16[2,128,1024]{1,2,0:T(8,128)(2,1)}, u32[]{:S(2)}, u32[]{:S(2)}) collective-permute-start(bf16[2,128,1024]{1,2,0:T(8,128)(2,1)} %pad_maximum_fusion.9), channel_id=1, source_target_pairs={{0,8},{1,9},{2,10},{3,11},{4,12},{5,13},{6,14},{7,15},{16,24},{17,... | collective-permute-start | bytes 1572872 | tf_op jit(solution)/shard_map/ppermute | solution.py:17
  65.2 29.5 %collective-permute-start.6 = (bf16[2,128,1024]{1,2,0:T(8,128)(2,1)}, bf16[2,128,1024]{1,2,0:T(8,128)(2,1)}, u32[]{:S(2)}, u32[]{:S(2)}) collective-permute-start(bf16[2,128,1024]{1,2,0:T(8,128)(2,1)} %pad_maximum_fusion.9), channel_id=1, source_target_pairs={{0,4},{1,5},{2,6},{3,7},{4,8},{5,9},{6,10},{7,11},{8,12},{9,13},{1... | collective-permute-start | bytes 1572872 | tf_op jit(solution)/shard_map/ppermute | solution.py:17
  69.0 9.9 %copy-start.5 = (bf16[1,128,8,128]{1,3,2,0:T(8,128)(2,1)S(1)}, bf16[1,128,8,128]{1,3,2,0:T(8,128)(2,1)}, u32[]{:S(2)}) copy-start(bf16[1,128,8,128]{1,3,2,0:T(8,128)(2,1)} %copy-done.4) | copy-start | bytes 786436
  69.0 37.0 %collective-permute-start.5 = (bf16[2,128,1024]{1,2,0:T(8,128)(2,1)}, bf16[2,128,1024]{1,2,0:T(8,128)(2,1)}, u32[]{:S(2)}, u32[]{:S(2)}) collective-permute-start(bf16[2,128,1024]{1,2,0:T(8,128)(2,1)} %pad_maximum_fusion.9), channel_id=1, source_target_pairs={{0,2},{1,3},{2,4},{3,5},{4,6},{5,7},{6,8},{7,9},{8,10},{9,11},{10,... | collective-permute-start | bytes 1572872 | tf_op jit(solution)/shard_map/ppermute | solution.py:17
  71.0 43.0 %collective-permute-start.4 = (bf16[2,128,1024]{1,2,0:T(8,128)(2,1)}, bf16[2,128,1024]{1,2,0:T(8,128)(2,1)}, u32[]{:S(2)}, u32[]{:S(2)}) collective-permute-start(bf16[2,128,1024]{1,2,0:T(8,128)(2,1)} %pad_maximum_fusion.9), channel_id=1, source_target_pairs={{0,1},{1,2},{2,3},{3,4},{4,5},{5,6},{6,7},{7,8},{8,9},{9,10},{10,1... | collective-permute-start | bytes 1572872 | tf_op jit(solution)/shard_map/ppermute | solution.py:17
  76.6 54.0 %collective-permute-start.11 = (bf16[2,128,8,128]{1,3,2,0:T(8,128)(2,1)}, bf16[2,128,8,128]{1,3,2,0:T(8,128)(2,1)}, u32[]{:S(2)}, u32[]{:S(2)}) collective-permute-start(bf16[2,128,8,128]{1,3,2,0:T(8,128)(2,1)} %pad_maximum_fusion.8), channel_id=1, source_target_pairs={{8,0},{9,1},{10,2},{11,3},{12,4},{13,5},{14,6},{15,7},{24,16},{25,... | collective-permute-start | bytes 1572872 | tf_op jit(solution)/shard_map/ppermute | solution.py:17
  83.4 49.2 %collective-permute-start.8 = (bf16[2,128,8,128]{1,3,2,0:T(8,128)(2,1)}, bf16[2,128,8,128]{1,3,2,0:T(8,128)(2,1)}, u32[]{:S(2)}, u32[]{:S(2)}) collective-permute-start(bf16[2,128,8,128]{1,3,2,0:T(8,128)(2,1)} %pad_maximum_fusion.5), channel_id=1, source_target_pairs={{1,0},{2,1},{3,2},{4,3},{5,4},{6,5},{7,6},{8,7},{9,8},{10,9},{11,1... | collective-permute-start | bytes 1572872 | tf_op jit(solution)/shard_map/ppermute | solution.py:17
  94.7 39.2 %collective-permute-start.9 = (bf16[2,128,8,128]{1,3,2,0:T(8,128)(2,1)}, bf16[2,128,8,128]{1,3,2,0:T(8,128)(2,1)}, u32[]{:S(2)}, u32[]{:S(2)}) collective-permute-start(bf16[2,128,8,128]{1,3,2,0:T(8,128)(2,1)} %pad_maximum_fusion.6), channel_id=1, source_target_pairs={{2,0},{3,1},{4,2},{5,3},{6,4},{7,5},{8,6},{9,7},{10,8},{11,9},{12,... | collective-permute-start | bytes 1572872 | tf_op jit(solution)/shard_map/ppermute | solution.py:17
  106.0 30.4 %collective-permute-start.10 = (bf16[2,128,8,128]{1,3,2,0:T(8,128)(2,1)}, bf16[2,128,8,128]{1,3,2,0:T(8,128)(2,1)}, u32[]{:S(2)}, u32[]{:S(2)}) collective-permute-start(bf16[2,128,8,128]{1,3,2,0:T(8,128)(2,1)} %pad_maximum_fusion.7), channel_id=1, source_target_pairs={{4,0},{5,1},{6,2},{7,3},{8,4},{9,5},{10,6},{11,7},{12,8},{13,9},{1... | collective-permute-start | bytes 1572872 | tf_op jit(solution)/shard_map/ppermute | solution.py:17
  126.1 17.5 %collective-permute-start.13 = (bf16[2,128,8,128]{1,3,2,0:T(8,128)(2,1)}, bf16[2,128,8,128]{1,3,2,0:T(8,128)(2,1)}, u32[]{:S(2)}, u32[]{:S(2)}) collective-permute-start(bf16[2,128,8,128]{1,3,2,0:T(8,128)(2,1)} %pad_maximum_fusion.13), channel_id=1, source_target_pairs={{2,0},{3,1},{4,2},{5,3},{6,4},{7,5},{8,6},{9,7},{10,8},{11,9},{12,... | collective-permute-start | bytes 1572872 | tf_op jit(solution)/shard_map/ppermute | solution.py:17
  128.9 7.6 %copy-start.16 = (bf16[128,8,128]{0,2,1:T(8,128)(2,1)S(1)}, bf16[128,8,128]{0,2,1:T(8,128)(2,1)}, u32[]{:S(2)}) copy-start(bf16[128,8,128]{0,2,1:T(8,128)(2,1)} %get-tuple-element.24) | copy-start | bytes 786436
  128.9 7.6 %copy-start.17 = (bf16[128,8,128]{0,2,1:T(8,128)(2,1)S(1)}, bf16[128,8,128]{0,2,1:T(8,128)(2,1)}, u32[]{:S(2)}) copy-start(bf16[128,8,128]{0,2,1:T(8,128)(2,1)} %get-tuple-element.34) | copy-start | bytes 786436
  130.5 10.7 %copy-start.10 = (bf16[128,1024]{1,0:T(8,128)(2,1)S(1)}, bf16[128,1024]{1,0:T(8,128)(2,1)}, u32[]{:S(2)}) copy-start(bf16[128,1024]{1,0:T(8,128)(2,1)} %copy.128) | copy-start | bytes 786436
  130.5 17.1 %collective-permute-start.14 = (bf16[2,128,8,128]{1,3,2,0:T(8,128)(2,1)}, bf16[2,128,8,128]{1,3,2,0:T(8,128)(2,1)}, u32[]{:S(2)}, u32[]{:S(2)}) collective-permute-start(bf16[2,128,8,128]{1,3,2,0:T(8,128)(2,1)} %pad_maximum_fusion.14), channel_id=1, source_target_pairs={{4,0},{5,1},{6,2},{7,3},{8,4},{9,5},{10,6},{11,7},{12,8},{13,9},{1... | collective-permute-start | bytes 1572872 | tf_op jit(solution)/shard_map/ppermute | solution.py:17
  132.6 18.2 %collective-permute-start.15 = (bf16[2,128,8,128]{1,3,2,0:T(8,128)(2,1)}, bf16[2,128,8,128]{1,3,2,0:T(8,128)(2,1)}, u32[]{:S(2)}, u32[]{:S(2)}) collective-permute-start(bf16[2,128,8,128]{1,3,2,0:T(8,128)(2,1)} %pad_maximum_fusion.15), channel_id=1, source_target_pairs={{8,0},{9,1},{10,2},{11,3},{12,4},{13,5},{14,6},{15,7},{24,16},{25,... | collective-permute-start | bytes 1572872 | tf_op jit(solution)/shard_map/ppermute | solution.py:17
  133.9 50.8 %collective-permute-start.12 = (bf16[2,128,8,128]{1,3,2,0:T(8,128)(2,1)}, bf16[2,128,8,128]{1,3,2,0:T(8,128)(2,1)}, u32[]{:S(2)}, u32[]{:S(2)}) collective-permute-start(bf16[2,128,8,128]{1,3,2,0:T(8,128)(2,1)} %pad_maximum_fusion.12), channel_id=1, source_target_pairs={{1,0},{2,1},{3,2},{4,3},{5,4},{6,5},{7,6},{8,7},{9,8},{10,9},{11,1... | collective-permute-start | bytes 1572872 | tf_op jit(solution)/shard_map/ppermute | solution.py:17
  143.0 41.7 %copy-start.18 = (bf16[128,8,128]{0,2,1:T(8,128)(2,1)S(1)}, bf16[128,8,128]{0,2,1:T(8,128)(2,1)}, u32[]{:S(2)}) copy-start(bf16[128,8,128]{0,2,1:T(8,128)(2,1)} %get-tuple-element.43) | copy-start | bytes 786436
  143.0 41.7 %copy-start.19 = (bf16[128,8,128]{0,2,1:T(8,128)(2,1)S(1)}, bf16[128,8,128]{0,2,1:T(8,128)(2,1)}, u32[]{:S(2)}) copy-start(bf16[128,8,128]{0,2,1:T(8,128)(2,1)} %get-tuple-element.29) | copy-start | bytes 786436
  143.6 43.9 %copy-start.6 = (f32[128,8,128]{0,2,1:T(8,128)S(1)}, f32[128,8,128]{0,2,1:T(8,128)}, u32[]{:S(2)}) copy-start(f32[128,8,128]{0,2,1:T(8,128)} %fusion.22) | copy-start | bytes 1572868
  143.6 43.9 %copy-start.7 = (f32[128,8,128]{0,2,1:T(8,128)S(1)}, f32[128,8,128]{0,2,1:T(8,128)}, u32[]{:S(2)}) copy-start(f32[128,8,128]{0,2,1:T(8,128)} %get-tuple-element.21) | copy-start | bytes 1572868
  (7 other events, 8.7 us)

commit v26 on v19

--- a/solution.py
+++ b/solution.py
@@ -73,7 +73,7 @@
     pair = jnp.stack([key_c, value_c])
     received = {0: pair}
     for offset in offsets:
-        if relay and offset >= 8 and (offset.bit_length() - 1) % 2 == 1:
+        if (relay or offset >= 8) and (offset.bit_length() - 1) % 2 == 1:
             half = offset // 2
             received[offset] = from_behind(received[half], "ctx", half)
         else:

time: 193 us -> 190 us (0.984)
  waiting for transfers between devices: 75.1 us -> 58.9 us
  starting transfers between devices: 42.8 us -> 49.5 us
  local copies, waits for them, and re-layouts: 40.7 us -> 44.6 us
  matrix products: 9.69 us -> 12.2 us
    ppermute x16, waiting for transfers between devices: 75.1 us -> 58.9 us  [from_behind(): lax.ppermute(value, axis, [(source, source + steps) for source in range(l...]
    ppermute x16, starting transfers between devices: 42.8 us -> 49.5 us  [from_behind(): lax.ppermute(value, axis, [(source, source + steps) for source in range(l...]
    unnamed x57 -> x95, local copies, waits for them, and re-layouts: 10.7 us -> 13 us
  transfers between devices with their start and end apart: 16 -> 16, of which waited for: 8 -> 8; matrix products, arithmetic and copies ran while one was open for 26% -> 27% of each run, Pallas kernels for 0% -> 0%
where the time goes in v26:
time: 190 us; the launch traced here: 188 us
  waiting for transfers between devices  58.9 us (31%)
  starting transfers between devices  49.5 us (26%)
  local copies, waits for them, and re-layouts  44.6 us (23%)
  other arithmetic  21.1 us (11%)
  matrix products  12.2 us (6%)
  between operations  2.21 us (1%)
    ppermute x16, waiting for transfers between devices, from_behind(): lax.ppermute(value, axis, [(source, source + steps) for source in range(l...  58.9 us
    ppermute x16, starting transfers between devices, from_behind(): lax.ppermute(value, axis, [(source, source + steps) for source in range(l...  49.5 us
    slice x8, local copies, waits for them, and re-layouts, attend_chunk(): moved[0].reshape(head_shape)  13.6 us
    unnamed x95, local copies, waits for them, and re-layouts  13 us
    another operation x8, other arithmetic, attend_chunk(): jnp.stack([key_terms[0, slot_index], value_terms[0, slot_index]])  6.76 us
    another operation x6, other arithmetic  5.53 us
    another operation x12, local copies, waits for them, and re-layouts, attend_chunk(): jnp.stack([moved[0].reshape(head_shape) for moved in received])[None]  4.67 us
  transfers between devices with their start and end apart: 16, of which 8 were waited for; matrix products, arithmetic and copies ran while one was open for 27% of the time, Pallas kernels for 0%

profile of v26, /device:TPU:15, one launch (start us, length us, event | category | flops | bytes accessed | tf_op | source)
XLA Modules:
  0.0 188.4 jit_solution(17043022358391873322)
XLA Ops:
  6.7 3.2 %collective-permute-start.2 = (bf16[2,128,1024]{1,2,0:T(8,128)(2,1)}, bf16[2,128,1024]{1,2,0:T(8,128)(2,1)}, u32[]{:S(2)}, u32[]{:S(2)}) collective-permute-start(bf16[2,128,1024]{1,2,0:T(8,128)(2,1)} %pad_maximum_fusion.3), channel_id=1, source_target_pairs={{0,4},{1,5},{2,6},{3,7},{4,8},{5,9},{6,10},{7,11},{8,12},{9,13},{1... | collective-permute-start | bytes 1572872 | tf_op jit(solution)/shard_map/ppermute | solution.py:17
  9.9 4.0 %collective-permute-start = (bf16[2,128,1024]{1,2,0:T(8,128)(2,1)}, bf16[2,128,1024]{1,2,0:T(8,128)(2,1)}, u32[]{:S(2)}, u32[]{:S(2)}) collective-permute-start(bf16[2,128,1024]{1,2,0:T(8,128)(2,1)} %pad_maximum_fusion.3), channel_id=1, source_target_pairs={{0,1},{1,2},{2,3},{3,4},{4,5},{5,6},{6,7},{7,8},{8,9},{9,10},{10,1... | collective-permute-start | bytes 1572872 | tf_op jit(solution)/shard_map/ppermute | solution.py:17
  16.8 1.8 copy.172
  21.7 3.2 %collective-permute-start.3 = (bf16[2,128,1024]{1,2,0:T(8,128)(2,1)}, bf16[2,128,1024]{1,2,0:T(8,128)(2,1)}, u32[]{:S(2)}, u32[]{:S(2)}) collective-permute-start(bf16[2,128,1024]{1,2,0:T(8,128)(2,1)} %collective-permute-done.2), channel_id=1, source_target_pairs={{0,4},{1,5},{2,6},{3,7},{4,8},{5,9},{6,10},{7,11},{8,12},{9,13},{1... | collective-permute-start | bytes 1572872 | tf_op jit(solution)/shard_map/ppermute | solution.py:17
  24.9 1.8 fusion.41
  27.6 5.3 %collective-permute-start.1 = (bf16[2,128,1024]{1,2,0:T(8,128)(2,1)}, bf16[2,128,1024]{1,2,0:T(8,128)(2,1)}, u32[]{:S(2)}, u32[]{:S(2)}) collective-permute-start(bf16[2,128,1024]{1,2,0:T(8,128)(2,1)} %collective-permute-done), channel_id=1, source_target_pairs={{0,1},{1,2},{2,3},{3,4},{4,5},{5,6},{6,7},{7,8},{8,9},{9,10},{10,1... | collective-permute-start | bytes 1572872 | tf_op jit(solution)/shard_map/ppermute | solution.py:17
  35.1 3.2 %collective-permute-done.3 = bf16[2,128,1024]{1,2,0:T(8,128)(2,1)} collective-permute-done((bf16[2,128,1024]{1,2,0:T(8,128)(2,1)}, bf16[2,128,1024]{1,2,0:T(8,128)(2,1)}, u32[]{:S(2)}, u32[]{:S(2)}) %collective-permute-start.3) | collective-permute-done | bytes 524320 | tf_op jit(solution)/shard_map/ppermute | solution.py:17
  38.4 1.8 fusion.40
  40.3 4.1 %collective-permute-done.1 = bf16[2,128,1024]{1,2,0:T(8,128)(2,1)} collective-permute-done((bf16[2,128,1024]{1,2,0:T(8,128)(2,1)}, bf16[2,128,1024]{1,2,0:T(8,128)(2,1)}, u32[]{:S(2)}, u32[]{:S(2)}) %collective-permute-start.1) | collective-permute-done | bytes 524320 | tf_op jit(solution)/shard_map/ppermute | solution.py:17
  47.6 1.8 fusion.46
  53.1 1.8 copy.112
  55.8 3.2 %collective-permute-start.6 = (bf16[2,128,1024]{1,2,0:T(8,128)(2,1)}, bf16[2,128,1024]{1,2,0:T(8,128)(2,1)}, u32[]{:S(2)}, u32[]{:S(2)}) collective-permute-start(bf16[2,128,1024]{1,2,0:T(8,128)(2,1)} %pad_maximum_fusion.5), channel_id=1, source_target_pairs={{0,4},{1,5},{2,6},{3,7},{4,8},{5,9},{6,10},{7,11},{8,12},{9,13},{1... | collective-permute-start | bytes 1572872 | tf_op jit(solution)/shard_map/ppermute | solution.py:17
  59.0 1.9 %collective-permute-start.5 = (bf16[2,128,1024]{1,2,0:T(8,128)(2,1)}, bf16[2,128,1024]{1,2,0:T(8,128)(2,1)}, u32[]{:S(2)}, u32[]{:S(2)}) collective-permute-start(bf16[2,128,1024]{1,2,0:T(8,128)(2,1)} %pad_maximum_fusion.5), channel_id=1, source_target_pairs={{0,2},{1,3},{2,4},{3,5},{4,6},{5,7},{6,8},{7,9},{8,10},{9,11},{10,... | collective-permute-start | bytes 1572872 | tf_op jit(solution)/shard_map/ppermute | solution.py:17
  60.9 5.6 %collective-permute-start.4 = (bf16[2,128,1024]{1,2,0:T(8,128)(2,1)}, bf16[2,128,1024]{1,2,0:T(8,128)(2,1)}, u32[]{:S(2)}, u32[]{:S(2)}) collective-permute-start(bf16[2,128,1024]{1,2,0:T(8,128)(2,1)} %pad_maximum_fusion.5), channel_id=1, source_target_pairs={{0,1},{1,2},{2,3},{3,4},{4,5},{5,6},{6,7},{7,8},{8,9},{9,10},{10,1... | collective-permute-start | bytes 1572872 | tf_op jit(solution)/shard_map/ppermute | solution.py:17
  66.5 1.9 %fusion.9 = bf16[1,5,128,8,128]{2,4,3,1,0:T(8,128)(2,1)S(1)} fusion(bf16[128,8,128,1]{0,2,1,3:T(8,128)(2,1)} %bitcast.351, bf16[1,8,128,5,128]{2,4,3,1,0:T(8,128)(2,1)} %copy-done), kind=kOutput, calls=%fused_computation.21 | convolution fusion | flops 168427520 | bytes 2883584 | tf_op jit(solution)/shard_map/bhtnu,bthd->bnuhd/dot_general | solution.py:117
  74.6 3.6 %collective-permute-start.9 = (bf16[2,128,8,128]{1,3,2,0:T(8,128)(2,1)}, bf16[2,128,8,128]{1,3,2,0:T(8,128)(2,1)}, u32[]{:S(2)}, u32[]{:S(2)}) collective-permute-start(bf16[2,128,8,128]{1,3,2,0:T(8,128)(2,1)} %pad_maximum_fusion.9), channel_id=1, source_target_pairs={{2,0},{3,1},{4,2},{5,3},{6,4},{7,5},{8,6},{9,7},{10,8},{11,9},{12,... | collective-permute-start | bytes 1572872 | tf_op jit(solution)/shard_map/ppermute | solution.py:17
  79.1 2.1 %collective-permute-start.10 = (bf16[2,128,8,128]{1,3,2,0:T(8,128)(2,1)}, bf16[2,128,8,128]{1,3,2,0:T(8,128)(2,1)}, u32[]{:S(2)}, u32[]{:S(2)}) collective-permute-start(bf16[2,128,8,128]{1,3,2,0:T(8,128)(2,1)} %pad_maximum_fusion.10), channel_id=1, source_target_pairs={{4,0},{5,1},{6,2},{7,3},{8,4},{9,5},{10,6},{11,7},{12,8},{13,9},{1... | collective-permute-start | bytes 1572872 | tf_op jit(solution)/shard_map/ppermute | solution.py:17
  86.3 1.8 fusion.38
  88.3 5.5 %collective-permute-start.8 = (bf16[2,128,8,128]{1,3,2,0:T(8,128)(2,1)}, bf16[2,128,8,128]{1,3,2,0:T(8,128)(2,1)}, u32[]{:S(2)}, u32[]{:S(2)}) collective-permute-start(bf16[2,128,8,128]{1,3,2,0:T(8,128)(2,1)} %pad_maximum_fusion.8), channel_id=1, source_target_pairs={{1,0},{2,1},{3,2},{4,3},{5,4},{6,5},{7,6},{8,7},{9,8},{10,9},{11,1... | collective-permute-start | bytes 1572872 | tf_op jit(solution)/shard_map/ppermute | solution.py:17
  93.8 1.9 fusion.39
  96.8 1.9 fusion.37
  98.7 2.7 %collective-permute-start.7 = (bf16[2,128,1024]{1,2,0:T(8,128)(2,1)}, bf16[2,128,1024]{1,2,0:T(8,128)(2,1)}, u32[]{:S(2)}, u32[]{:S(2)}) collective-permute-start(bf16[2,128,1024]{1,2,0:T(8,128)(2,1)} %collective-permute-done.6), channel_id=1, source_target_pairs={{0,4},{1,5},{2,6},{3,7},{4,8},{5,9},{6,10},{7,11},{8,12},{9,13},{1... | collective-permute-start | bytes 1572872 | tf_op jit(solution)/shard_map/ppermute | solution.py:17
  103.8 10.8 %collective-permute-done.7 = bf16[2,128,1024]{1,2,0:T(8,128)(2,1)} collective-permute-done((bf16[2,128,1024]{1,2,0:T(8,128)(2,1)}, bf16[2,128,1024]{1,2,0:T(8,128)(2,1)}, u32[]{:S(2)}, u32[]{:S(2)}) %collective-permute-start.7) | collective-permute-done | bytes 524320 | tf_op jit(solution)/shard_map/ppermute | solution.py:17
  114.5 1.8 fusion.36
  126.3 1.9 %collective-permute-start.13 = (bf16[2,128,8,128]{1,3,2,0:T(8,128)(2,1)}, bf16[2,128,8,128]{1,3,2,0:T(8,128)(2,1)}, u32[]{:S(2)}, u32[]{:S(2)}) collective-permute-start(bf16[2,128,8,128]{1,3,2,0:T(8,128)(2,1)} %pad_maximum_fusion.13), channel_id=1, source_target_pairs={{2,0},{3,1},{4,2},{5,3},{6,4},{7,5},{8,6},{9,7},{10,8},{11,9},{12,... | collective-permute-start | bytes 1572872 | tf_op jit(solution)/shard_map/ppermute | solution.py:17
  130.8 2.0 %collective-permute-start.14 = (bf16[2,128,8,128]{1,3,2,0:T(8,128)(2,1)}, bf16[2,128,8,128]{1,3,2,0:T(8,128)(2,1)}, u32[]{:S(2)}, u32[]{:S(2)}) collective-permute-start(bf16[2,128,8,128]{1,3,2,0:T(8,128)(2,1)} %pad_maximum_fusion.14), channel_id=1, source_target_pairs={{4,0},{5,1},{6,2},{7,3},{8,4},{9,5},{10,6},{11,7},{12,8},{13,9},{1... | collective-permute-start | bytes 1572872 | tf_op jit(solution)/shard_map/ppermute | solution.py:17
  134.1 2.7 %collective-permute-start.12 = (bf16[2,128,8,128]{1,3,2,0:T(8,128)(2,1)}, bf16[2,128,8,128]{1,3,2,0:T(8,128)(2,1)}, u32[]{:S(2)}, u32[]{:S(2)}) collective-permute-start(bf16[2,128,8,128]{1,3,2,0:T(8,128)(2,1)} %pad_maximum_fusion.12), channel_id=1, source_target_pairs={{1,0},{2,1},{3,2},{4,3},{5,4},{6,5},{7,6},{8,7},{9,8},{10,9},{11,1... | collective-permute-start | bytes 1572872 | tf_op jit(solution)/shard_map/ppermute | solution.py:17
  136.9 2.8 %fusion.27 = (bf16[128,8,128]{0,2,1:T(8,128)(2,1)}, f32[128,8,128]{0,2,1:T(8,128)}) fusion(bf16[128,8,128]{0,2,1:T(8,128)(2,1)S(1)} %copy-done.28, bf16[2,128,8,128]{1,3,2,0:T(8,128)(2,1)} %collective-permute-done.11, bf16[2,128,8,128]{1,3,2,0:T(8,128)(2,1)} %collective-permute-done.10, bf16[2,128,8,128]{1,3,2,0:T(8,128)(2,1)} %collective-permute-done.9, ...), kind=kLoop, calls=%fused_computation.70 | loop fusion | flops 2490368 | bytes 3407872 | tf_op jit(solution)/shard_map/convert.23
  141.7 1.8 pad_maximum_fusion.6
  145.8 11.5 %collective-permute-done.15 = bf16[2,128,8,128]{1,3,2,0:T(8,128)(2,1)} collective-permute-done((bf16[2,128,8,128]{1,3,2,0:T(8,128)(2,1)}, bf16[2,128,8,128]{1,3,2,0:T(8,128)(2,1)}, u32[]{:S(2)}, u32[]{:S(2)}) %collective-permute-start.15) | collective-permute-done | bytes 524320 | tf_op jit(solution)/shard_map/ppermute | solution.py:17
  157.3 25.1 %collective-permute-done.12 = bf16[2,128,8,128]{1,3,2,0:T(8,128)(2,1)} collective-permute-done((bf16[2,128,8,128]{1,3,2,0:T(8,128)(2,1)}, bf16[2,128,8,128]{1,3,2,0:T(8,128)(2,1)}, u32[]{:S(2)}, u32[]{:S(2)}) %collective-permute-start.12) | collective-permute-done | bytes 524320 | tf_op jit(solution)/shard_map/ppermute | solution.py:17
  182.4 1.9 %fusion.26 = (bf16[128,8,128]{0,2,1:T(8,128)(2,1)S(1)}, f32[128,8,128]{0,2,1:T(8,128)S(1)}) fusion(bf16[128,8,128]{0,2,1:T(8,128)(2,1)S(1)} %copy-done.31, bf16[2,128,8,128]{1,3,2,0:T(8,128)(2,1)} %collective-permute-done.15, bf16[2,128,8,128]{1,3,2,0:T(8,128)(2,1)} %collective-permute-done.14, bf16[2,128,8,128]{1,3,2,0:T(8,128)(2,1)} %collective-permute-done.13, ...), kind=kLoop, calls=%fused_computation.65 | loop fusion | flops 2490368 | bytes 3407872 | tf_op jit(solution)/shard_map/convert.22
  (187 shorter events, 59.9 us)
Async XLA Ops:
  0.6 3.1 %copy-start.32 = (bf16[128,2048]{1,0:T(8,128)(2,1)S(1)}, bf16[128,2048]{1,0:T(8,128)(2,1)}, u32[]{:S(2)}) copy-start(bf16[128,2048]{1,0:T(8,128)(2,1)} %param.7) | copy-start | bytes 1572868
  5.8 8.8 %copy-start.33 = (bf16[128,2048]{1,0:T(8,128)(2,1)S(1)}, bf16[128,2048]{1,0:T(8,128)(2,1)}, u32[]{:S(2)}) copy-start(bf16[128,2048]{1,0:T(8,128)(2,1)} %param.10) | copy-start | bytes 1572868
  5.9 9.6 %copy-start.36 = (s32[4]{0:T(128)S(1)}, s32[4]{0:T(128)}, u32[]{:S(2)}) copy-start(s32[4]{0:T(128)} %constant.35) | copy-start | bytes 52
  6.7 15.0 %collective-permute-start.2 = (bf16[2,128,1024]{1,2,0:T(8,128)(2,1)}, bf16[2,128,1024]{1,2,0:T(8,128)(2,1)}, u32[]{:S(2)}, u32[]{:S(2)}) collective-permute-start(bf16[2,128,1024]{1,2,0:T(8,128)(2,1)} %pad_maximum_fusion.3), channel_id=1, source_target_pairs={{0,4},{1,5},{2,6},{3,7},{4,8},{5,9},{6,10},{7,11},{8,12},{9,13},{1... | collective-permute-start | bytes 1572872 | tf_op jit(solution)/shard_map/ppermute | solution.py:17
  9.9 17.7 %collective-permute-start = (bf16[2,128,1024]{1,2,0:T(8,128)(2,1)}, bf16[2,128,1024]{1,2,0:T(8,128)(2,1)}, u32[]{:S(2)}, u32[]{:S(2)}) collective-permute-start(bf16[2,128,1024]{1,2,0:T(8,128)(2,1)} %pad_maximum_fusion.3), channel_id=1, source_target_pairs={{0,1},{1,2},{2,3},{3,4},{4,5},{5,6},{6,7},{7,8},{8,9},{9,10},{10,1... | collective-permute-start | bytes 1572872 | tf_op jit(solution)/shard_map/ppermute | solution.py:17
  15.8 2.8 %copy-start.25 = (bf16[128,1024]{1,0:T(8,128)(2,1)S(1)}, bf16[128,1024]{1,0:T(8,128)(2,1)}, u32[]{:S(2)}) copy-start(bf16[128,1024]{1,0:T(8,128)(2,1)} %get-tuple-element.53) | copy-start | bytes 786436
  21.7 16.6 %collective-permute-start.3 = (bf16[2,128,1024]{1,2,0:T(8,128)(2,1)}, bf16[2,128,1024]{1,2,0:T(8,128)(2,1)}, u32[]{:S(2)}, u32[]{:S(2)}) collective-permute-start(bf16[2,128,1024]{1,2,0:T(8,128)(2,1)} %collective-permute-done.2), channel_id=1, source_target_pairs={{0,4},{1,5},{2,6},{3,7},{4,8},{5,9},{6,10},{7,11},{8,12},{9,13},{1... | collective-permute-start | bytes 1572872 | tf_op jit(solution)/shard_map/ppermute | solution.py:17
  27.6 16.9 %collective-permute-start.1 = (bf16[2,128,1024]{1,2,0:T(8,128)(2,1)}, bf16[2,128,1024]{1,2,0:T(8,128)(2,1)}, u32[]{:S(2)}, u32[]{:S(2)}) collective-permute-start(bf16[2,128,1024]{1,2,0:T(8,128)(2,1)} %collective-permute-done), channel_id=1, source_target_pairs={{0,1},{1,2},{2,3},{3,4},{4,5},{5,6},{6,7},{7,8},{8,9},{9,10},{10,1... | collective-permute-start | bytes 1572872 | tf_op jit(solution)/shard_map/ppermute | solution.py:17
  51.0 2.1 %copy-start = (bf16[1,8,128,5,128]{2,4,3,1,0:T(8,128)(2,1)}, bf16[1,8,128,5,128]{2,4,3,1,0:T(8,128)(2,1)S(1)}, u32[]{:S(2)}) copy-start(bf16[1,8,128,5,128]{2,4,3,1,0:T(8,128)(2,1)S(1)} %fusion.15) | copy-start | bytes 3932164
  55.8 41.0 %collective-permute-start.6 = (bf16[2,128,1024]{1,2,0:T(8,128)(2,1)}, bf16[2,128,1024]{1,2,0:T(8,128)(2,1)}, u32[]{:S(2)}, u32[]{:S(2)}) collective-permute-start(bf16[2,128,1024]{1,2,0:T(8,128)(2,1)} %pad_maximum_fusion.5), channel_id=1, source_target_pairs={{0,4},{1,5},{2,6},{3,7},{4,8},{5,9},{6,10},{7,11},{8,12},{9,13},{1... | collective-permute-start | bytes 1572872 | tf_op jit(solution)/shard_map/ppermute | solution.py:17
  59.0 26.0 %collective-permute-start.5 = (bf16[2,128,1024]{1,2,0:T(8,128)(2,1)}, bf16[2,128,1024]{1,2,0:T(8,128)(2,1)}, u32[]{:S(2)}, u32[]{:S(2)}) collective-permute-start(bf16[2,128,1024]{1,2,0:T(8,128)(2,1)} %pad_maximum_fusion.5), channel_id=1, source_target_pairs={{0,2},{1,3},{2,4},{3,5},{4,6},{5,7},{6,8},{7,9},{8,10},{9,11},{10,... | collective-permute-start | bytes 1572872 | tf_op jit(solution)/shard_map/ppermute | solution.py:17
  60.9 27.4 %collective-permute-start.4 = (bf16[2,128,1024]{1,2,0:T(8,128)(2,1)}, bf16[2,128,1024]{1,2,0:T(8,128)(2,1)}, u32[]{:S(2)}, u32[]{:S(2)}) collective-permute-start(bf16[2,128,1024]{1,2,0:T(8,128)(2,1)} %pad_maximum_fusion.5), channel_id=1, source_target_pairs={{0,1},{1,2},{2,3},{3,4},{4,5},{5,6},{6,7},{7,8},{8,9},{9,10},{10,1... | collective-permute-start | bytes 1572872 | tf_op jit(solution)/shard_map/ppermute | solution.py:17
  73.5 4.7 %copy-start.18 = (bf16[1,128,8,128]{1,3,2,0:T(8,128)(2,1)S(1)}, bf16[1,128,8,128]{1,3,2,0:T(8,128)(2,1)}, u32[]{:S(2)}) copy-start(bf16[1,128,8,128]{1,3,2,0:T(8,128)(2,1)} %get-tuple-element.26) | copy-start | bytes 786436
  73.5 7.6 %copy-start.17 = (bf16[1,128,8,128]{1,3,2,0:T(8,128)(2,1)S(1)}, bf16[1,128,8,128]{1,3,2,0:T(8,128)(2,1)}, u32[]{:S(2)}) copy-start(bf16[1,128,8,128]{1,3,2,0:T(8,128)(2,1)} %get-tuple-element.28) | copy-start | bytes 786436
  74.6 56.2 %collective-permute-start.9 = (bf16[2,128,8,128]{1,3,2,0:T(8,128)(2,1)}, bf16[2,128,8,128]{1,3,2,0:T(8,128)(2,1)}, u32[]{:S(2)}, u32[]{:S(2)}) collective-permute-start(bf16[2,128,8,128]{1,3,2,0:T(8,128)(2,1)} %pad_maximum_fusion.9), channel_id=1, source_target_pairs={{2,0},{3,1},{4,2},{5,3},{6,4},{7,5},{8,6},{9,7},{10,8},{11,9},{12,... | collective-permute-start | bytes 1572872 | tf_op jit(solution)/shard_map/ppermute | solution.py:17
  78.2 3.8 %copy-start.16 = (bf16[1,128,8,128]{1,3,2,0:T(8,128)(2,1)S(1)}, bf16[1,128,8,128]{1,3,2,0:T(8,128)(2,1)}, u32[]{:S(2)}) copy-start(bf16[1,128,8,128]{1,3,2,0:T(8,128)(2,1)} %get-tuple-element.25) | copy-start | bytes 786436
  79.1 53.7 %collective-permute-start.10 = (bf16[2,128,8,128]{1,3,2,0:T(8,128)(2,1)}, bf16[2,128,8,128]{1,3,2,0:T(8,128)(2,1)}, u32[]{:S(2)}, u32[]{:S(2)}) collective-permute-start(bf16[2,128,8,128]{1,3,2,0:T(8,128)(2,1)} %pad_maximum_fusion.10), channel_id=1, source_target_pairs={{4,0},{5,1},{6,2},{7,3},{8,4},{9,5},{10,6},{11,7},{12,8},{13,9},{1... | collective-permute-start | bytes 1572872 | tf_op jit(solution)/shard_map/ppermute | solution.py:17
  85.0 49.1 %collective-permute-start.11 = (bf16[2,128,8,128]{1,3,2,0:T(8,128)(2,1)}, bf16[2,128,8,128]{1,3,2,0:T(8,128)(2,1)}, u32[]{:S(2)}, u32[]{:S(2)}) collective-permute-start(bf16[2,128,8,128]{1,3,2,0:T(8,128)(2,1)} %pad_maximum_fusion.11), channel_id=1, source_target_pairs={{8,0},{9,1},{10,2},{11,3},{12,4},{13,5},{14,6},{15,7},{24,16},{25,... | collective-permute-start | bytes 1572872 | tf_op jit(solution)/shard_map/ppermute | solution.py:17
  88.3 48.6 %collective-permute-start.8 = (bf16[2,128,8,128]{1,3,2,0:T(8,128)(2,1)}, bf16[2,128,8,128]{1,3,2,0:T(8,128)(2,1)}, u32[]{:S(2)}, u32[]{:S(2)}) collective-permute-start(bf16[2,128,8,128]{1,3,2,0:T(8,128)(2,1)} %pad_maximum_fusion.8), channel_id=1, source_target_pairs={{1,0},{2,1},{3,2},{4,3},{5,4},{6,5},{7,6},{8,7},{9,8},{10,9},{11,1... | collective-permute-start | bytes 1572872 | tf_op jit(solution)/shard_map/ppermute | solution.py:17
  98.6 5.0 %copy-start.22 = (bf16[1,128,1024]{1,2,0:T(8,128)(2,1)S(1)}, bf16[1,128,1024]{1,2,0:T(8,128)(2,1)}, u32[]{:S(2)}) copy-start(bf16[1,128,1024]{1,2,0:T(8,128)(2,1)} %get-tuple-element.61) | copy-start | bytes 786436
  98.7 15.9 %collective-permute-start.7 = (bf16[2,128,1024]{1,2,0:T(8,128)(2,1)}, bf16[2,128,1024]{1,2,0:T(8,128)(2,1)}, u32[]{:S(2)}, u32[]{:S(2)}) collective-permute-start(bf16[2,128,1024]{1,2,0:T(8,128)(2,1)} %collective-permute-done.6), channel_id=1, source_target_pairs={{0,4},{1,5},{2,6},{3,7},{4,8},{5,9},{6,10},{7,11},{8,12},{9,13},{1... | collective-permute-start | bytes 1572872 | tf_op jit(solution)/shard_map/ppermute | solution.py:17
  126.3 17.7 %collective-permute-start.13 = (bf16[2,128,8,128]{1,3,2,0:T(8,128)(2,1)}, bf16[2,128,8,128]{1,3,2,0:T(8,128)(2,1)}, u32[]{:S(2)}, u32[]{:S(2)}) collective-permute-start(bf16[2,128,8,128]{1,3,2,0:T(8,128)(2,1)} %pad_maximum_fusion.13), channel_id=1, source_target_pairs={{2,0},{3,1},{4,2},{5,3},{6,4},{7,5},{8,6},{9,7},{10,8},{11,9},{12,... | collective-permute-start | bytes 1572872 | tf_op jit(solution)/shard_map/ppermute | solution.py:17
  129.1 7.8 %copy-start.28 = (bf16[128,8,128]{0,2,1:T(8,128)(2,1)S(1)}, bf16[128,8,128]{0,2,1:T(8,128)(2,1)}, u32[]{:S(2)}) copy-start(bf16[128,8,128]{0,2,1:T(8,128)(2,1)} %get-tuple-element.24) | copy-start | bytes 786436
  129.1 7.8 %copy-start.29 = (bf16[128,8,128]{0,2,1:T(8,128)(2,1)S(1)}, bf16[128,8,128]{0,2,1:T(8,128)(2,1)}, u32[]{:S(2)}) copy-start(bf16[128,8,128]{0,2,1:T(8,128)(2,1)} %get-tuple-element.38) | copy-start | bytes 786436
  130.8 10.9 %copy-start.20 = (bf16[128,1024]{1,0:T(8,128)(2,1)S(1)}, bf16[128,1024]{1,0:T(8,128)(2,1)}, u32[]{:S(2)}) copy-start(bf16[128,1024]{1,0:T(8,128)(2,1)} %copy.112) | copy-start | bytes 786436
  130.8 15.0 %collective-permute-start.14 = (bf16[2,128,8,128]{1,3,2,0:T(8,128)(2,1)}, bf16[2,128,8,128]{1,3,2,0:T(8,128)(2,1)}, u32[]{:S(2)}, u32[]{:S(2)}) collective-permute-start(bf16[2,128,8,128]{1,3,2,0:T(8,128)(2,1)} %pad_maximum_fusion.14), channel_id=1, source_target_pairs={{4,0},{5,1},{6,2},{7,3},{8,4},{9,5},{10,6},{11,7},{12,8},{13,9},{1... | collective-permute-start | bytes 1572872 | tf_op jit(solution)/shard_map/ppermute | solution.py:17
  132.8 24.4 %collective-permute-start.15 = (bf16[2,128,8,128]{1,3,2,0:T(8,128)(2,1)}, bf16[2,128,8,128]{1,3,2,0:T(8,128)(2,1)}, u32[]{:S(2)}, u32[]{:S(2)}) collective-permute-start(bf16[2,128,8,128]{1,3,2,0:T(8,128)(2,1)} %pad_maximum_fusion.15), channel_id=1, source_target_pairs={{8,0},{9,1},{10,2},{11,3},{12,4},{13,5},{14,6},{15,7},{24,16},{25,... | collective-permute-start | bytes 1572872 | tf_op jit(solution)/shard_map/ppermute | solution.py:17
  134.1 48.2 %collective-permute-start.12 = (bf16[2,128,8,128]{1,3,2,0:T(8,128)(2,1)}, bf16[2,128,8,128]{1,3,2,0:T(8,128)(2,1)}, u32[]{:S(2)}, u32[]{:S(2)}) collective-permute-start(bf16[2,128,8,128]{1,3,2,0:T(8,128)(2,1)} %pad_maximum_fusion.12), channel_id=1, source_target_pairs={{1,0},{2,1},{3,2},{4,3},{5,4},{6,5},{7,6},{8,7},{9,8},{10,9},{11,1... | collective-permute-start | bytes 1572872 | tf_op jit(solution)/shard_map/ppermute | solution.py:17
  143.4 39.0 %copy-start.30 = (bf16[128,8,128]{0,2,1:T(8,128)(2,1)S(1)}, bf16[128,8,128]{0,2,1:T(8,128)(2,1)}, u32[]{:S(2)}) copy-start(bf16[128,8,128]{0,2,1:T(8,128)(2,1)} %get-tuple-element.43) | copy-start | bytes 786436
  143.4 39.0 %copy-start.31 = (bf16[128,8,128]{0,2,1:T(8,128)(2,1)S(1)}, bf16[128,8,128]{0,2,1:T(8,128)(2,1)}, u32[]{:S(2)}) copy-start(bf16[128,8,128]{0,2,1:T(8,128)(2,1)} %get-tuple-element.29) | copy-start | bytes 786436
  144.0 41.2 %copy-start.9 = (f32[128,8,128]{0,2,1:T(8,128)S(1)}, f32[128,8,128]{0,2,1:T(8,128)}, u32[]{:S(2)}) copy-start(f32[128,8,128]{0,2,1:T(8,128)} %convolution_bitcast_fusion.1) | copy-start | bytes 1572868
  144.0 41.1 %copy-start.10 = (f32[128,8,128]{0,2,1:T(8,128)S(1)}, f32[128,8,128]{0,2,1:T(8,128)}, u32[]{:S(2)}) copy-start(f32[128,8,128]{0,2,1:T(8,128)} %get-tuple-element.21) | copy-start | bytes 1572868
  (21 other events, 27.1 us)

commit v27 on v18

--- a/solution.py
+++ b/solution.py
@@ -128,7 +128,7 @@
 def gather_back(own, outgoing, offsets):
     key_accum = own[0].astype(jnp.float32)
     value_accum = own[1].astype(jnp.float32)
-    for parts, offset in zip(outgoing, offsets):
+    for parts, offset in list(zip(outgoing, offsets))[::-1]:
         returned = from_behind(parts, "ctx", -offset)
         key_accum = key_accum + returned[0].astype(jnp.float32)
         value_accum = value_accum + returned[1].astype(jnp.float32)

time: 184 us -> 188 us (1.022)
  the two profiles are of different devices: /device:TPU:15 before, /device:TPU:0 now
where the time goes in v27:
time: 188 us; the launch traced here: 187 us
  waiting for transfers between devices  66.1 us (35%)
  starting transfers between devices  45.9 us (24%)
  local copies, waits for them, and re-layouts  41.2 us (22%)
  other arithmetic  21.8 us (12%)
  matrix products  9.69 us (5%)
  between operations  1.97 us (1%)
    ppermute x16, waiting for transfers between devices, from_behind(): lax.ppermute(value, axis, [(source, source + steps) for source in range(l...  66.1 us
    ppermute x16, starting transfers between devices, from_behind(): lax.ppermute(value, axis, [(source, source + steps) for source in range(l...  45.9 us
    slice x8, local copies, waits for them, and re-layouts, attend_chunk(): moved[0].reshape(head_shape)  13.1 us
    unnamed x59, local copies, waits for them, and re-layouts  10.4 us
    another operation x12, local copies, waits for them, and re-layouts, attend_chunk(): jnp.stack([moved[0].reshape(head_shape) for moved in received])[None]  6.97 us
    another operation x8, other arithmetic, attend_chunk(): jnp.stack([key_terms[0, slot_index], value_terms[0, slot_index]])  6.76 us
    another operation x6, other arithmetic  5.35 us
  transfers between devices with their start and end apart: 16, of which 4 were waited for; matrix products, arithmetic and copies ran while one was open for 27% of the time, Pallas kernels for 0%

profile of v27, /device:TPU:0, one launch (start us, length us, event | category | flops | bytes accessed | tf_op | source)
XLA Modules:
  0.0 186.5 jit_solution(1656585776675254605)
XLA Ops:
  7.1 5.7 %collective-permute-start.2 = (bf16[2,128,1024]{1,2,0:T(8,128)(2,1)}, bf16[2,128,1024]{1,2,0:T(8,128)(2,1)}, u32[]{:S(2)}, u32[]{:S(2)}) collective-permute-start(bf16[2,128,1024]{1,2,0:T(8,128)(2,1)} %pad_maximum_fusion.3), channel_id=1, source_target_pairs={{0,4},{1,5},{2,6},{3,7},{4,8},{5,9},{6,10},{7,11},{8,12},{9,13},{1... | collective-permute-start | bytes 1572872 | tf_op jit(solution)/shard_map/ppermute | solution.py:17
  12.8 2.3 %collective-permute-start = (bf16[2,128,1024]{1,2,0:T(8,128)(2,1)}, bf16[2,128,1024]{1,2,0:T(8,128)(2,1)}, u32[]{:S(2)}, u32[]{:S(2)}) collective-permute-start(bf16[2,128,1024]{1,2,0:T(8,128)(2,1)} %pad_maximum_fusion.3), channel_id=1, source_target_pairs={{0,1},{1,2},{2,3},{3,4},{4,5},{5,6},{6,7},{7,8},{8,9},{9,10},{10,1... | collective-permute-start | bytes 1572872 | tf_op jit(solution)/shard_map/ppermute | solution.py:17
  18.6 4.9 %collective-permute-done.2 = bf16[2,128,1024]{1,2,0:T(8,128)(2,1)} collective-permute-done((bf16[2,128,1024]{1,2,0:T(8,128)(2,1)}, bf16[2,128,1024]{1,2,0:T(8,128)(2,1)}, u32[]{:S(2)}, u32[]{:S(2)}) %collective-permute-start.2) | collective-permute-done | bytes 524320 | tf_op jit(solution)/shard_map/ppermute | solution.py:17
  23.5 5.2 %collective-permute-start.3 = (bf16[2,128,1024]{1,2,0:T(8,128)(2,1)}, bf16[2,128,1024]{1,2,0:T(8,128)(2,1)}, u32[]{:S(2)}, u32[]{:S(2)}) collective-permute-start(bf16[2,128,1024]{1,2,0:T(8,128)(2,1)} %collective-permute-done.2), channel_id=1, source_target_pairs={{0,4},{1,5},{2,6},{3,7},{4,8},{5,9},{6,10},{7,11},{8,12},{9,13},{1... | collective-permute-start | bytes 1572872 | tf_op jit(solution)/shard_map/ppermute | solution.py:17
  28.7 1.8 fusion.41
  30.5 2.1 %collective-permute-start.1 = (bf16[2,128,1024]{1,2,0:T(8,128)(2,1)}, bf16[2,128,1024]{1,2,0:T(8,128)(2,1)}, u32[]{:S(2)}, u32[]{:S(2)}) collective-permute-start(bf16[2,128,1024]{1,2,0:T(8,128)(2,1)} %collective-permute-done), channel_id=1, source_target_pairs={{0,1},{1,2},{2,3},{3,4},{4,5},{5,6},{6,7},{7,8},{8,9},{9,10},{10,1... | collective-permute-start | bytes 1572872 | tf_op jit(solution)/shard_map/ppermute | solution.py:17
  32.6 1.9 fusion.43
  35.8 1.7 constant_dynamic-update-slice_fusion.3
  38.5 1.9 fusion.40
  41.5 1.9 fusion.42
  43.3 1.8 copy.99
  50.5 11.6 %collective-permute-start.7 = (bf16[2,128,1024]{1,2,0:T(8,128)(2,1)}, bf16[2,128,1024]{1,2,0:T(8,128)(2,1)}, u32[]{:S(2)}, u32[]{:S(2)}) collective-permute-start(bf16[2,128,1024]{1,2,0:T(8,128)(2,1)} %pad_maximum_fusion.5), channel_id=1, source_target_pairs={{0,8},{1,9},{2,10},{3,11},{4,12},{5,13},{6,14},{7,15},{16,24},{17,... | collective-permute-start | bytes 1572872 | tf_op jit(solution)/shard_map/ppermute | solution.py:17
  62.1 4.3 %collective-permute-start.6 = (bf16[2,128,1024]{1,2,0:T(8,128)(2,1)}, bf16[2,128,1024]{1,2,0:T(8,128)(2,1)}, u32[]{:S(2)}, u32[]{:S(2)}) collective-permute-start(bf16[2,128,1024]{1,2,0:T(8,128)(2,1)} %pad_maximum_fusion.5), channel_id=1, source_target_pairs={{0,4},{1,5},{2,6},{3,7},{4,8},{5,9},{6,10},{7,11},{8,12},{9,13},{1... | collective-permute-start | bytes 1572872 | tf_op jit(solution)/shard_map/ppermute | solution.py:17
  66.5 2.1 %collective-permute-start.5 = (bf16[2,128,1024]{1,2,0:T(8,128)(2,1)}, bf16[2,128,1024]{1,2,0:T(8,128)(2,1)}, u32[]{:S(2)}, u32[]{:S(2)}) collective-permute-start(bf16[2,128,1024]{1,2,0:T(8,128)(2,1)} %pad_maximum_fusion.5), channel_id=1, source_target_pairs={{0,2},{1,3},{2,4},{3,5},{4,6},{5,7},{6,8},{7,9},{8,10},{9,11},{10,... | collective-permute-start | bytes 1572872 | tf_op jit(solution)/shard_map/ppermute | solution.py:17
  71.4 1.4 convolution_bitcast_fusion.1
  75.1 1.3 collective-permute-start.9
  82.4 2.1 %collective-permute-start.4 = (bf16[2,128,1024]{1,2,0:T(8,128)(2,1)}, bf16[2,128,1024]{1,2,0:T(8,128)(2,1)}, u32[]{:S(2)}, u32[]{:S(2)}) collective-permute-start(bf16[2,128,1024]{1,2,0:T(8,128)(2,1)} %pad_maximum_fusion.5), channel_id=1, source_target_pairs={{0,1},{1,2},{2,3},{3,4},{4,5},{5,6},{6,7},{7,8},{8,9},{9,10},{10,1... | collective-permute-start | bytes 1572872 | tf_op jit(solution)/shard_map/ppermute | solution.py:17
  84.5 1.3 collective-permute-start.10
  87.0 1.3 collective-permute-start.11
  89.6 1.5 collective-permute-start.8
  91.1 1.8 fusion.38
  93.0 1.9 fusion.39
  108.5 1.3 collective-permute-start.14
  109.8 1.3 collective-permute-start.15
  111.1 1.3 collective-permute-start.12
  112.4 22.1 %collective-permute-done.8 = bf16[2,128,8,128]{1,3,2,0:T(8,128)(2,1)} collective-permute-done((bf16[2,128,8,128]{1,3,2,0:T(8,128)(2,1)}, bf16[2,128,8,128]{1,3,2,0:T(8,128)(2,1)}, u32[]{:S(2)}, u32[]{:S(2)}) %collective-permute-start.8) | collective-permute-done | bytes 524320 | tf_op jit(solution)/shard_map/ppermute | solution.py:17
  134.5 2.6 %fusion.27 = (bf16[128,8,128]{0,2,1:T(8,128)(2,1)}, f32[128,8,128]{0,2,1:T(8,128)S(1)}) fusion(bf16[128,8,128]{0,2,1:T(8,128)(2,1)S(1)} %copy-done.11, bf16[2,128,8,128]{1,3,2,0:T(8,128)(2,1)} %collective-permute-done.11, bf16[2,128,8,128]{1,3,2,0:T(8,128)(2,1)} %collective-permute-done.10, bf16[2,128,8,128]{1,3,2,0:T(8,128)(2,1)} %collective-permute-done.9, ...), kind=kLoop, calls=%fused_computation.70 | loop fusion | flops 2490368 | bytes 3407872 | tf_op jit(solution)/shard_map/convert.23
  137.2 1.8 copy.132
  139.8 1.9 pad_maximum_fusion.6
  141.7 1.4 convolution_bitcast_fusion
  143.1 38.0 %collective-permute-done.12 = bf16[2,128,8,128]{1,3,2,0:T(8,128)(2,1)} collective-permute-done((bf16[2,128,8,128]{1,3,2,0:T(8,128)(2,1)}, bf16[2,128,8,128]{1,3,2,0:T(8,128)(2,1)}, u32[]{:S(2)}, u32[]{:S(2)}) %collective-permute-start.12) | collective-permute-done | bytes 524320 | tf_op jit(solution)/shard_map/ppermute | solution.py:17
  181.2 1.9 %fusion.26 = (bf16[128,8,128]{0,2,1:T(8,128)(2,1)S(1)}, f32[128,8,128]{0,2,1:T(8,128)S(1)}) fusion(bf16[128,8,128]{0,2,1:T(8,128)(2,1)S(1)} %copy-done.14, bf16[2,128,8,128]{1,3,2,0:T(8,128)(2,1)} %collective-permute-done.15, bf16[2,128,8,128]{1,3,2,0:T(8,128)(2,1)} %collective-permute-done.14, bf16[2,128,8,128]{1,3,2,0:T(8,128)(2,1)} %collective-permute-done.13, ...), kind=kLoop, calls=%fused_computation.65 | loop fusion | flops 2490368 | bytes 3407872 | tf_op jit(solution)/shard_map/convert.22
  (151 shorter events, 49.5 us)
Async XLA Ops:
  0.6 3.1 %copy-start.15 = (bf16[128,2048]{1,0:T(8,128)(2,1)S(1)}, bf16[128,2048]{1,0:T(8,128)(2,1)}, u32[]{:S(2)}) copy-start(bf16[128,2048]{1,0:T(8,128)(2,1)} %param.7) | copy-start | bytes 1572868
  6.2 9.6 %copy-start.17 = (bf16[128,2048]{1,0:T(8,128)(2,1)S(1)}, bf16[128,2048]{1,0:T(8,128)(2,1)}, u32[]{:S(2)}) copy-start(bf16[128,2048]{1,0:T(8,128)(2,1)} %param.10) | copy-start | bytes 1572868
  6.2 9.6 %copy-start.18 = (s32[4]{0:T(128)S(1)}, s32[4]{0:T(128)}, u32[]{:S(2)}) copy-start(s32[4]{0:T(128)} %constant.35) | copy-start | bytes 52
  7.1 16.4 %collective-permute-start.2 = (bf16[2,128,1024]{1,2,0:T(8,128)(2,1)}, bf16[2,128,1024]{1,2,0:T(8,128)(2,1)}, u32[]{:S(2)}, u32[]{:S(2)}) collective-permute-start(bf16[2,128,1024]{1,2,0:T(8,128)(2,1)} %pad_maximum_fusion.3), channel_id=1, source_target_pairs={{0,4},{1,5},{2,6},{3,7},{4,8},{5,9},{6,10},{7,11},{8,12},{9,13},{1... | collective-permute-start | bytes 1572872 | tf_op jit(solution)/shard_map/ppermute | solution.py:17
  12.8 17.6 %collective-permute-start = (bf16[2,128,1024]{1,2,0:T(8,128)(2,1)}, bf16[2,128,1024]{1,2,0:T(8,128)(2,1)}, u32[]{:S(2)}, u32[]{:S(2)}) collective-permute-start(bf16[2,128,1024]{1,2,0:T(8,128)(2,1)} %pad_maximum_fusion.3), channel_id=1, source_target_pairs={{0,1},{1,2},{2,3},{3,4},{4,5},{5,6},{6,7},{7,8},{8,9},{9,10},{10,1... | collective-permute-start | bytes 1572872 | tf_op jit(solution)/shard_map/ppermute | solution.py:17
  23.5 15.0 %collective-permute-start.3 = (bf16[2,128,1024]{1,2,0:T(8,128)(2,1)}, bf16[2,128,1024]{1,2,0:T(8,128)(2,1)}, u32[]{:S(2)}, u32[]{:S(2)}) collective-permute-start(bf16[2,128,1024]{1,2,0:T(8,128)(2,1)} %collective-permute-done.2), channel_id=1, source_target_pairs={{0,4},{1,5},{2,6},{3,7},{4,8},{5,9},{6,10},{7,11},{8,12},{9,13},{1... | collective-permute-start | bytes 1572872 | tf_op jit(solution)/shard_map/ppermute | solution.py:17
  30.5 11.0 %collective-permute-start.1 = (bf16[2,128,1024]{1,2,0:T(8,128)(2,1)}, bf16[2,128,1024]{1,2,0:T(8,128)(2,1)}, u32[]{:S(2)}, u32[]{:S(2)}) collective-permute-start(bf16[2,128,1024]{1,2,0:T(8,128)(2,1)} %collective-permute-done), channel_id=1, source_target_pairs={{0,1},{1,2},{2,3},{3,4},{4,5},{5,6},{6,7},{7,8},{8,9},{9,10},{10,1... | collective-permute-start | bytes 1572872 | tf_op jit(solution)/shard_map/ppermute | solution.py:17
  47.6 1.3 copy-start.3
  47.6 1.3 copy-start.10
  47.6 1.4 copy-start.5
  47.7 1.5 copy-start.7
  50.5 34.0 %collective-permute-start.7 = (bf16[2,128,1024]{1,2,0:T(8,128)(2,1)}, bf16[2,128,1024]{1,2,0:T(8,128)(2,1)}, u32[]{:S(2)}, u32[]{:S(2)}) collective-permute-start(bf16[2,128,1024]{1,2,0:T(8,128)(2,1)} %pad_maximum_fusion.5), channel_id=1, source_target_pairs={{0,8},{1,9},{2,10},{3,11},{4,12},{5,13},{6,14},{7,15},{16,24},{17,... | collective-permute-start | bytes 1572872 | tf_op jit(solution)/shard_map/ppermute | solution.py:17
  62.1 24.9 %collective-permute-start.6 = (bf16[2,128,1024]{1,2,0:T(8,128)(2,1)}, bf16[2,128,1024]{1,2,0:T(8,128)(2,1)}, u32[]{:S(2)}, u32[]{:S(2)}) collective-permute-start(bf16[2,128,1024]{1,2,0:T(8,128)(2,1)} %pad_maximum_fusion.5), channel_id=1, source_target_pairs={{0,4},{1,5},{2,6},{3,7},{4,8},{5,9},{6,10},{7,11},{8,12},{9,13},{1... | collective-permute-start | bytes 1572872 | tf_op jit(solution)/shard_map/ppermute | solution.py:17
  66.5 23.1 %collective-permute-start.5 = (bf16[2,128,1024]{1,2,0:T(8,128)(2,1)}, bf16[2,128,1024]{1,2,0:T(8,128)(2,1)}, u32[]{:S(2)}, u32[]{:S(2)}) collective-permute-start(bf16[2,128,1024]{1,2,0:T(8,128)(2,1)} %pad_maximum_fusion.5), channel_id=1, source_target_pairs={{0,2},{1,3},{2,4},{3,5},{4,6},{5,7},{6,8},{7,9},{8,10},{9,11},{10,... | collective-permute-start | bytes 1572872 | tf_op jit(solution)/shard_map/ppermute | solution.py:17
  74.2 3.8 %copy-start.4 = (bf16[1,128,8,128]{1,3,2,0:T(8,128)(2,1)S(1)}, bf16[1,128,8,128]{1,3,2,0:T(8,128)(2,1)}, u32[]{:S(2)}) copy-start(bf16[1,128,8,128]{1,3,2,0:T(8,128)(2,1)} %get-tuple-element.25) | copy-start | bytes 786436
  75.1 33.4 %collective-permute-start.9 = (bf16[2,128,8,128]{1,3,2,0:T(8,128)(2,1)}, bf16[2,128,8,128]{1,3,2,0:T(8,128)(2,1)}, u32[]{:S(2)}, u32[]{:S(2)}) collective-permute-start(bf16[2,128,8,128]{1,3,2,0:T(8,128)(2,1)} %pad_maximum_fusion.9), channel_id=1, source_target_pairs={{4,0},{5,1},{6,2},{7,3},{8,4},{9,5},{10,6},{11,7},{12,8},{13,9},{1... | collective-permute-start | bytes 1572872 | tf_op jit(solution)/shard_map/ppermute | solution.py:17
  82.4 10.6 %collective-permute-start.4 = (bf16[2,128,1024]{1,2,0:T(8,128)(2,1)}, bf16[2,128,1024]{1,2,0:T(8,128)(2,1)}, u32[]{:S(2)}, u32[]{:S(2)}) collective-permute-start(bf16[2,128,1024]{1,2,0:T(8,128)(2,1)} %pad_maximum_fusion.5), channel_id=1, source_target_pairs={{0,1},{1,2},{2,3},{3,4},{4,5},{5,6},{6,7},{7,8},{8,9},{9,10},{10,1... | collective-permute-start | bytes 1572872 | tf_op jit(solution)/shard_map/ppermute | solution.py:17
  84.5 25.3 %collective-permute-start.10 = (bf16[2,128,8,128]{1,3,2,0:T(8,128)(2,1)}, bf16[2,128,8,128]{1,3,2,0:T(8,128)(2,1)}, u32[]{:S(2)}, u32[]{:S(2)}) collective-permute-start(bf16[2,128,8,128]{1,3,2,0:T(8,128)(2,1)} %pad_maximum_fusion.10), channel_id=1, source_target_pairs={{2,0},{3,1},{4,2},{5,3},{6,4},{7,5},{8,6},{9,7},{10,8},{11,9},{12,... | collective-permute-start | bytes 1572872 | tf_op jit(solution)/shard_map/ppermute | solution.py:17
  87.0 24.1 %collective-permute-start.11 = (bf16[2,128,8,128]{1,3,2,0:T(8,128)(2,1)}, bf16[2,128,8,128]{1,3,2,0:T(8,128)(2,1)}, u32[]{:S(2)}, u32[]{:S(2)}) collective-permute-start(bf16[2,128,8,128]{1,3,2,0:T(8,128)(2,1)} %pad_maximum_fusion.11), channel_id=1, source_target_pairs={{1,0},{2,1},{3,2},{4,3},{5,4},{6,5},{7,6},{8,7},{9,8},{10,9},{11,1... | collective-permute-start | bytes 1572872 | tf_op jit(solution)/shard_map/ppermute | solution.py:17
  89.6 44.9 %collective-permute-start.8 = (bf16[2,128,8,128]{1,3,2,0:T(8,128)(2,1)}, bf16[2,128,8,128]{1,3,2,0:T(8,128)(2,1)}, u32[]{:S(2)}, u32[]{:S(2)}) collective-permute-start(bf16[2,128,8,128]{1,3,2,0:T(8,128)(2,1)} %pad_maximum_fusion.8), channel_id=1, source_target_pairs={{8,0},{9,1},{10,2},{11,3},{12,4},{13,5},{14,6},{15,7},{24,16},{25,... | collective-permute-start | bytes 1572872 | tf_op jit(solution)/shard_map/ppermute | solution.py:17
  97.6 1.3 copy-start.9
  97.6 1.4 copy-start.8
  104.7 38.4 %collective-permute-start.13 = (bf16[2,128,8,128]{1,3,2,0:T(8,128)(2,1)}, bf16[2,128,8,128]{1,3,2,0:T(8,128)(2,1)}, u32[]{:S(2)}, u32[]{:S(2)}) collective-permute-start(bf16[2,128,8,128]{1,3,2,0:T(8,128)(2,1)} %pad_maximum_fusion.13), channel_id=1, source_target_pairs={{4,0},{5,1},{6,2},{7,3},{8,4},{9,5},{10,6},{11,7},{12,8},{13,9},{1... | collective-permute-start | bytes 1572872 | tf_op jit(solution)/shard_map/ppermute | solution.py:17
  106.8 27.7 %copy-start.11 = (bf16[128,8,128]{0,2,1:T(8,128)(2,1)S(1)}, bf16[128,8,128]{0,2,1:T(8,128)(2,1)}, u32[]{:S(2)}) copy-start(bf16[128,8,128]{0,2,1:T(8,128)(2,1)} %get-tuple-element.24) | copy-start | bytes 786436
  106.8 27.7 %copy-start.12 = (bf16[128,8,128]{0,2,1:T(8,128)(2,1)S(1)}, bf16[128,8,128]{0,2,1:T(8,128)(2,1)}, u32[]{:S(2)}) copy-start(bf16[128,8,128]{0,2,1:T(8,128)(2,1)} %get-tuple-element.38) | copy-start | bytes 786436
  108.5 34.6 %collective-permute-start.14 = (bf16[2,128,8,128]{1,3,2,0:T(8,128)(2,1)}, bf16[2,128,8,128]{1,3,2,0:T(8,128)(2,1)}, u32[]{:S(2)}, u32[]{:S(2)}) collective-permute-start(bf16[2,128,8,128]{1,3,2,0:T(8,128)(2,1)} %pad_maximum_fusion.14), channel_id=1, source_target_pairs={{2,0},{3,1},{4,2},{5,3},{6,4},{7,5},{8,6},{9,7},{10,8},{11,9},{12,... | collective-permute-start | bytes 1572872 | tf_op jit(solution)/shard_map/ppermute | solution.py:17
  109.8 33.3 %collective-permute-start.15 = (bf16[2,128,8,128]{1,3,2,0:T(8,128)(2,1)}, bf16[2,128,8,128]{1,3,2,0:T(8,128)(2,1)}, u32[]{:S(2)}, u32[]{:S(2)}) collective-permute-start(bf16[2,128,8,128]{1,3,2,0:T(8,128)(2,1)} %pad_maximum_fusion.15), channel_id=1, source_target_pairs={{1,0},{2,1},{3,2},{4,3},{5,4},{6,5},{7,6},{8,7},{9,8},{10,9},{11,1... | collective-permute-start | bytes 1572872 | tf_op jit(solution)/shard_map/ppermute | solution.py:17
  111.1 70.1 %collective-permute-start.12 = (bf16[2,128,8,128]{1,3,2,0:T(8,128)(2,1)}, bf16[2,128,8,128]{1,3,2,0:T(8,128)(2,1)}, u32[]{:S(2)}, u32[]{:S(2)}) collective-permute-start(bf16[2,128,8,128]{1,3,2,0:T(8,128)(2,1)} %pad_maximum_fusion.12), channel_id=1, source_target_pairs={{8,0},{9,1},{10,2},{11,3},{12,4},{13,5},{14,6},{15,7},{24,16},{25,... | collective-permute-start | bytes 1572872 | tf_op jit(solution)/shard_map/ppermute | solution.py:17
  141.7 39.5 %copy-start.13 = (bf16[128,8,128]{0,2,1:T(8,128)(2,1)S(1)}, bf16[128,8,128]{0,2,1:T(8,128)(2,1)}, u32[]{:S(2)}) copy-start(bf16[128,8,128]{0,2,1:T(8,128)(2,1)} %get-tuple-element.43) | copy-start | bytes 786436
  141.7 39.5 %copy-start.14 = (bf16[128,8,128]{0,2,1:T(8,128)(2,1)S(1)}, bf16[128,8,128]{0,2,1:T(8,128)(2,1)}, u32[]{:S(2)}) copy-start(bf16[128,8,128]{0,2,1:T(8,128)(2,1)} %get-tuple-element.29) | copy-start | bytes 786436
  143.1 40.2 %copy-start = (f32[128,8,128]{0,2,1:T(8,128)S(1)}, f32[128,8,128]{0,2,1:T(8,128)}, u32[]{:S(2)}) copy-start(f32[128,8,128]{0,2,1:T(8,128)} %convolution_bitcast_fusion.1) | copy-start | bytes 1572868
  143.1 40.2 %copy-start.1 = (f32[128,8,128]{0,2,1:T(8,128)S(1)}, f32[128,8,128]{0,2,1:T(8,128)}, u32[]{:S(2)}) copy-start(f32[128,8,128]{0,2,1:T(8,128)} %convolution_bitcast_fusion) | copy-start | bytes 1572868
  (3 other events, 3.4 us)

commit v28 on v26

--- a/solution.py
+++ b/solution.py
@@ -73,7 +73,7 @@
     pair = jnp.stack([key_c, value_c])
     received = {0: pair}
     for offset in offsets:
-        if (relay or offset >= 8) and (offset.bit_length() - 1) % 2 == 1:
+        if relay and offset >= 2:
             half = offset // 2
             received[offset] = from_behind(received[half], "ctx", half)
         else:

time: 190 us -> 196 us (1.032)
  waiting for transfers between devices: 58.9 us -> 72.1 us
  local copies, waits for them, and re-layouts: 44.6 us -> 40.5 us
  matrix products: 12.2 us -> 9.69 us
    ppermute x16, waiting for transfers between devices: 58.9 us -> 72.1 us  [from_behind(): lax.ppermute(value, axis, [(source, source + steps) for source in range(l...]
    unnamed x95 -> x53, local copies, waits for them, and re-layouts: 13 us -> 9.77 us
    another operation x12, local copies, waits for them, and re-layouts: 4.67 us -> 7.22 us  [attend_chunk(): jnp.stack([moved[0].reshape(head_shape) for moved in received])[None]]
  transfers between devices with their start and end apart: 16 -> 16, of which waited for: 8 -> 10; matrix products, arithmetic and copies ran while one was open for 27% -> 27% of each run, Pallas kernels for 0% -> 0%
where the time goes in v28:
time: 196 us; the launch traced here: 195 us
  waiting for transfers between devices  72.1 us (37%)
  starting transfers between devices  48.5 us (25%)
  local copies, waits for them, and re-layouts  40.5 us (21%)
  other arithmetic  21.8 us (11%)
  matrix products  9.69 us (5%)
  between operations  2.01 us (1%)
    ppermute x16, waiting for transfers between devices, from_behind(): lax.ppermute(value, axis, [(source, source + steps) for source in range(l...  72.1 us
    ppermute x16, starting transfers between devices, from_behind(): lax.ppermute(value, axis, [(source, source + steps) for source in range(l...  48.5 us
    slice x8, local copies, waits for them, and re-layouts, attend_chunk(): moved[0].reshape(head_shape)  12.8 us
    unnamed x53, local copies, waits for them, and re-layouts  9.77 us
    another operation x12, local copies, waits for them, and re-layouts, attend_chunk(): jnp.stack([moved[0].reshape(head_shape) for moved in received])[None]  7.22 us
    another operation x8, other arithmetic, attend_chunk(): jnp.stack([key_terms[0, slot_index], value_terms[0, slot_index]])  6.73 us
    another operation x6, other arithmetic  5.36 us
  transfers between devices with their start and end apart: 16, of which 10 were waited for; matrix products, arithmetic and copies ran while one was open for 27% of the time, Pallas kernels for 0%

profile of v28, /device:TPU:15, one launch (start us, length us, event | category | flops | bytes accessed | tf_op | source)
XLA Modules:
  0.0 194.6 jit_solution(16456601249292881640)
XLA Ops:
  7.1 3.7 %collective-permute-start = (bf16[2,128,1024]{1,2,0:T(8,128)(2,1)}, bf16[2,128,1024]{1,2,0:T(8,128)(2,1)}, u32[]{:S(2)}, u32[]{:S(2)}) collective-permute-start(bf16[2,128,1024]{1,2,0:T(8,128)(2,1)} %pad_maximum_fusion.3), channel_id=1, source_target_pairs={{0,1},{1,2},{2,3},{3,4},{4,5},{5,6},{6,7},{7,8},{8,9},{9,10},{10,1... | collective-permute-start | bytes 1572872 | tf_op jit(solution)/shard_map/ppermute | solution.py:17
  12.0 5.2 %collective-permute-done = bf16[2,128,1024]{1,2,0:T(8,128)(2,1)} collective-permute-done((bf16[2,128,1024]{1,2,0:T(8,128)(2,1)}, bf16[2,128,1024]{1,2,0:T(8,128)(2,1)}, u32[]{:S(2)}, u32[]{:S(2)}) %collective-permute-start) | collective-permute-done | bytes 524320 | tf_op jit(solution)/shard_map/ppermute | solution.py:17
  17.2 5.3 %collective-permute-start.1 = (bf16[2,128,1024]{1,2,0:T(8,128)(2,1)}, bf16[2,128,1024]{1,2,0:T(8,128)(2,1)}, u32[]{:S(2)}, u32[]{:S(2)}) collective-permute-start(bf16[2,128,1024]{1,2,0:T(8,128)(2,1)} %collective-permute-done), channel_id=1, source_target_pairs={{0,1},{1,2},{2,3},{3,4},{4,5},{5,6},{6,7},{7,8},{8,9},{9,10},{10,1... | collective-permute-start | bytes 1572872 | tf_op jit(solution)/shard_map/ppermute | solution.py:17
  24.9 1.8 fusion.43
  28.9 2.2 %collective-permute-start.2 = (bf16[2,128,1024]{1,2,0:T(8,128)(2,1)}, bf16[2,128,1024]{1,2,0:T(8,128)(2,1)}, u32[]{:S(2)}, u32[]{:S(2)}) collective-permute-start(bf16[2,128,1024]{1,2,0:T(8,128)(2,1)} %collective-permute-done.1), channel_id=1, source_target_pairs={{0,2},{1,3},{2,4},{3,5},{4,6},{5,7},{6,8},{7,9},{8,10},{9,11},{10,... | collective-permute-start | bytes 1572872 | tf_op jit(solution)/shard_map/ppermute | solution.py:17
  32.0 1.8 fusion.42
  34.9 8.9 %collective-permute-done.2 = bf16[2,128,1024]{1,2,0:T(8,128)(2,1)} collective-permute-done((bf16[2,128,1024]{1,2,0:T(8,128)(2,1)}, bf16[2,128,1024]{1,2,0:T(8,128)(2,1)}, u32[]{:S(2)}, u32[]{:S(2)}) %collective-permute-start.2) | collective-permute-done | bytes 524320 | tf_op jit(solution)/shard_map/ppermute | solution.py:17
  43.8 3.2 %collective-permute-start.3 = (bf16[2,128,1024]{1,2,0:T(8,128)(2,1)}, bf16[2,128,1024]{1,2,0:T(8,128)(2,1)}, u32[]{:S(2)}, u32[]{:S(2)}) collective-permute-start(bf16[2,128,1024]{1,2,0:T(8,128)(2,1)} %collective-permute-done.2), channel_id=1, source_target_pairs={{0,4},{1,5},{2,6},{3,7},{4,8},{5,9},{6,10},{7,11},{8,12},{9,13},{1... | collective-permute-start | bytes 1572872 | tf_op jit(solution)/shard_map/ppermute | solution.py:17
  47.8 1.8 fusion.41
  51.5 6.3 %collective-permute-done.3 = bf16[2,128,1024]{1,2,0:T(8,128)(2,1)} collective-permute-done((bf16[2,128,1024]{1,2,0:T(8,128)(2,1)}, bf16[2,128,1024]{1,2,0:T(8,128)(2,1)}, u32[]{:S(2)}, u32[]{:S(2)}) %collective-permute-start.3) | collective-permute-done | bytes 524320 | tf_op jit(solution)/shard_map/ppermute | solution.py:17
  57.8 1.8 fusion.40
  64.9 4.0 %collective-permute-start.7 = (bf16[2,128,1024]{1,2,0:T(8,128)(2,1)}, bf16[2,128,1024]{1,2,0:T(8,128)(2,1)}, u32[]{:S(2)}, u32[]{:S(2)}) collective-permute-start(bf16[2,128,1024]{1,2,0:T(8,128)(2,1)} %pad_maximum_fusion.5), channel_id=1, source_target_pairs={{0,8},{1,9},{2,10},{3,11},{4,12},{5,13},{6,14},{7,15},{16,24},{17,... | collective-permute-start | bytes 1572872 | tf_op jit(solution)/shard_map/ppermute | solution.py:17
  68.9 1.9 collective-permute-start.6
  70.8 1.9 collective-permute-start.5
  79.2 3.3 %collective-permute-start.9 = (bf16[2,128,8,128]{1,3,2,0:T(8,128)(2,1)}, bf16[2,128,8,128]{1,3,2,0:T(8,128)(2,1)}, u32[]{:S(2)}, u32[]{:S(2)}) collective-permute-start(bf16[2,128,8,128]{1,3,2,0:T(8,128)(2,1)} %pad_maximum_fusion.9), channel_id=1, source_target_pairs={{2,0},{3,1},{4,2},{5,3},{6,4},{7,5},{8,6},{9,7},{10,8},{11,9},{12,... | collective-permute-start | bytes 1572872 | tf_op jit(solution)/shard_map/ppermute | solution.py:17
  88.6 5.5 %collective-permute-start.4 = (bf16[2,128,1024]{1,2,0:T(8,128)(2,1)}, bf16[2,128,1024]{1,2,0:T(8,128)(2,1)}, u32[]{:S(2)}, u32[]{:S(2)}) collective-permute-start(bf16[2,128,1024]{1,2,0:T(8,128)(2,1)} %pad_maximum_fusion.5), channel_id=1, source_target_pairs={{0,1},{1,2},{2,3},{3,4},{4,5},{5,6},{6,7},{7,8},{8,9},{9,10},{10,1... | collective-permute-start | bytes 1572872 | tf_op jit(solution)/shard_map/ppermute | solution.py:17
  94.1 4.5 %collective-permute-start.10 = (bf16[2,128,8,128]{1,3,2,0:T(8,128)(2,1)}, bf16[2,128,8,128]{1,3,2,0:T(8,128)(2,1)}, u32[]{:S(2)}, u32[]{:S(2)}) collective-permute-start(bf16[2,128,8,128]{1,3,2,0:T(8,128)(2,1)} %pad_maximum_fusion.10), channel_id=1, source_target_pairs={{4,0},{5,1},{6,2},{7,3},{8,4},{9,5},{10,6},{11,7},{12,8},{13,9},{1... | collective-permute-start | bytes 1572872 | tf_op jit(solution)/shard_map/ppermute | solution.py:17
  99.8 1.7 collective-permute-done.6
  104.1 8.7 %collective-permute-done.5 = bf16[2,128,1024]{1,2,0:T(8,128)(2,1)} collective-permute-done((bf16[2,128,1024]{1,2,0:T(8,128)(2,1)}, bf16[2,128,1024]{1,2,0:T(8,128)(2,1)}, u32[]{:S(2)}, u32[]{:S(2)}) %collective-permute-start.5) | collective-permute-done | bytes 524320 | tf_op jit(solution)/shard_map/ppermute | solution.py:17
  112.8 4.6 %collective-permute-start.8 = (bf16[2,128,8,128]{1,3,2,0:T(8,128)(2,1)}, bf16[2,128,8,128]{1,3,2,0:T(8,128)(2,1)}, u32[]{:S(2)}, u32[]{:S(2)}) collective-permute-start(bf16[2,128,8,128]{1,3,2,0:T(8,128)(2,1)} %pad_maximum_fusion.8), channel_id=1, source_target_pairs={{1,0},{2,1},{3,2},{4,3},{5,4},{6,5},{7,6},{8,7},{9,8},{10,9},{11,1... | collective-permute-start | bytes 1572872 | tf_op jit(solution)/shard_map/ppermute | solution.py:17
  117.4 1.8 fusion.38
  119.5 1.9 fusion.39
  131.1 1.9 collective-permute-start.13
  135.5 1.9 collective-permute-start.14
  138.8 1.9 collective-permute-start.12
  140.7 2.6 %fusion.27 = (bf16[128,8,128]{0,2,1:T(8,128)(2,1)}, f32[128,8,128]{0,2,1:T(8,128)S(1)}) fusion(bf16[128,8,128]{0,2,1:T(8,128)(2,1)S(1)} %copy-done.8, bf16[2,128,8,128]{1,3,2,0:T(8,128)(2,1)} %collective-permute-done.11, bf16[2,128,8,128]{1,3,2,0:T(8,128)(2,1)} %collective-permute-done.10, bf16[2,128,8,128]{1,3,2,0:T(8,128)(2,1)} %collective-permute-done.9, ...), kind=kLoop, calls=%fused_computation.70 | loop fusion | flops 2490368 | bytes 3407872 | tf_op jit(solution)/shard_map/convert.23
  143.4 1.8 copy.132
  146.0 1.9 pad_maximum_fusion.6
  149.3 3.1 %collective-permute-done.14 = bf16[2,128,8,128]{1,3,2,0:T(8,128)(2,1)} collective-permute-done((bf16[2,128,8,128]{1,3,2,0:T(8,128)(2,1)}, bf16[2,128,8,128]{1,3,2,0:T(8,128)(2,1)}, u32[]{:S(2)}, u32[]{:S(2)}) %collective-permute-start.14) | collective-permute-done | bytes 524320 | tf_op jit(solution)/shard_map/ppermute | solution.py:17
  152.4 12.1 %collective-permute-done.15 = bf16[2,128,8,128]{1,3,2,0:T(8,128)(2,1)} collective-permute-done((bf16[2,128,8,128]{1,3,2,0:T(8,128)(2,1)}, bf16[2,128,8,128]{1,3,2,0:T(8,128)(2,1)}, u32[]{:S(2)}, u32[]{:S(2)}) %collective-permute-start.15) | collective-permute-done | bytes 524320 | tf_op jit(solution)/shard_map/ppermute | solution.py:17
  164.5 24.7 %collective-permute-done.12 = bf16[2,128,8,128]{1,3,2,0:T(8,128)(2,1)} collective-permute-done((bf16[2,128,8,128]{1,3,2,0:T(8,128)(2,1)}, bf16[2,128,8,128]{1,3,2,0:T(8,128)(2,1)}, u32[]{:S(2)}, u32[]{:S(2)}) %collective-permute-start.12) | collective-permute-done | bytes 524320 | tf_op jit(solution)/shard_map/ppermute | solution.py:17
  189.2 1.9 fusion.26
  (145 shorter events, 56.9 us)
Async XLA Ops:
  0.6 3.1 %copy-start.12 = (bf16[128,2048]{1,0:T(8,128)(2,1)S(1)}, bf16[128,2048]{1,0:T(8,128)(2,1)}, u32[]{:S(2)}) copy-start(bf16[128,2048]{1,0:T(8,128)(2,1)} %param.7) | copy-start | bytes 1572868
  3.5 1.0 copy-start.13
  6.2 5.5 %copy-start.15 = (s32[4]{0:T(128)S(1)}, s32[4]{0:T(128)}, u32[]{:S(2)}) copy-start(s32[4]{0:T(128)} %constant.35) | copy-start | bytes 52
  6.3 5.7 %copy-start.14 = (bf16[128,2048]{1,0:T(8,128)(2,1)S(1)}, bf16[128,2048]{1,0:T(8,128)(2,1)}, u32[]{:S(2)}) copy-start(bf16[128,2048]{1,0:T(8,128)(2,1)} %param.10) | copy-start | bytes 1572868
  7.1 10.1 %collective-permute-start = (bf16[2,128,1024]{1,2,0:T(8,128)(2,1)}, bf16[2,128,1024]{1,2,0:T(8,128)(2,1)}, u32[]{:S(2)}, u32[]{:S(2)}) collective-permute-start(bf16[2,128,1024]{1,2,0:T(8,128)(2,1)} %pad_maximum_fusion.3), channel_id=1, source_target_pairs={{0,1},{1,2},{2,3},{3,4},{4,5},{5,6},{6,7},{7,8},{8,9},{9,10},{10,1... | collective-permute-start | bytes 1572872 | tf_op jit(solution)/shard_map/ppermute | solution.py:17
  17.2 11.7 %collective-permute-start.1 = (bf16[2,128,1024]{1,2,0:T(8,128)(2,1)}, bf16[2,128,1024]{1,2,0:T(8,128)(2,1)}, u32[]{:S(2)}, u32[]{:S(2)}) collective-permute-start(bf16[2,128,1024]{1,2,0:T(8,128)(2,1)} %collective-permute-done), channel_id=1, source_target_pairs={{0,1},{1,2},{2,3},{3,4},{4,5},{5,6},{6,7},{7,8},{8,9},{9,10},{10,1... | collective-permute-start | bytes 1572872 | tf_op jit(solution)/shard_map/ppermute | solution.py:17
  28.9 14.9 %collective-permute-start.2 = (bf16[2,128,1024]{1,2,0:T(8,128)(2,1)}, bf16[2,128,1024]{1,2,0:T(8,128)(2,1)}, u32[]{:S(2)}, u32[]{:S(2)}) collective-permute-start(bf16[2,128,1024]{1,2,0:T(8,128)(2,1)} %collective-permute-done.1), channel_id=1, source_target_pairs={{0,2},{1,3},{2,4},{3,5},{4,6},{5,7},{6,8},{7,9},{8,10},{9,11},{10,... | collective-permute-start | bytes 1572872 | tf_op jit(solution)/shard_map/ppermute | solution.py:17
  43.8 14.0 %collective-permute-start.3 = (bf16[2,128,1024]{1,2,0:T(8,128)(2,1)}, bf16[2,128,1024]{1,2,0:T(8,128)(2,1)}, u32[]{:S(2)}, u32[]{:S(2)}) collective-permute-start(bf16[2,128,1024]{1,2,0:T(8,128)(2,1)} %collective-permute-done.2), channel_id=1, source_target_pairs={{0,4},{1,5},{2,6},{3,7},{4,8},{5,9},{6,10},{7,11},{8,12},{9,13},{1... | collective-permute-start | bytes 1572872 | tf_op jit(solution)/shard_map/ppermute | solution.py:17
  62.2 1.3 copy-start.3
  64.9 29.2 %collective-permute-start.7 = (bf16[2,128,1024]{1,2,0:T(8,128)(2,1)}, bf16[2,128,1024]{1,2,0:T(8,128)(2,1)}, u32[]{:S(2)}, u32[]{:S(2)}) collective-permute-start(bf16[2,128,1024]{1,2,0:T(8,128)(2,1)} %pad_maximum_fusion.5), channel_id=1, source_target_pairs={{0,8},{1,9},{2,10},{3,11},{4,12},{5,13},{6,14},{7,15},{16,24},{17,... | collective-permute-start | bytes 1572872 | tf_op jit(solution)/shard_map/ppermute | solution.py:17
  68.9 32.7 %collective-permute-start.6 = (bf16[2,128,1024]{1,2,0:T(8,128)(2,1)}, bf16[2,128,1024]{1,2,0:T(8,128)(2,1)}, u32[]{:S(2)}, u32[]{:S(2)}) collective-permute-start(bf16[2,128,1024]{1,2,0:T(8,128)(2,1)} %pad_maximum_fusion.5), channel_id=1, source_target_pairs={{0,4},{1,5},{2,6},{3,7},{4,8},{5,9},{6,10},{7,11},{8,12},{9,13},{1... | collective-permute-start | bytes 1572872 | tf_op jit(solution)/shard_map/ppermute | solution.py:17
  70.8 42.0 %collective-permute-start.5 = (bf16[2,128,1024]{1,2,0:T(8,128)(2,1)}, bf16[2,128,1024]{1,2,0:T(8,128)(2,1)}, u32[]{:S(2)}, u32[]{:S(2)}) collective-permute-start(bf16[2,128,1024]{1,2,0:T(8,128)(2,1)} %pad_maximum_fusion.5), channel_id=1, source_target_pairs={{0,2},{1,3},{2,4},{3,5},{4,6},{5,7},{6,8},{7,9},{8,10},{9,11},{10,... | collective-permute-start | bytes 1572872 | tf_op jit(solution)/shard_map/ppermute | solution.py:17
  78.4 5.9 %copy-start.4 = (bf16[1,128,8,128]{1,3,2,0:T(8,128)(2,1)S(1)}, bf16[1,128,8,128]{1,3,2,0:T(8,128)(2,1)}, u32[]{:S(2)}) copy-start(bf16[1,128,8,128]{1,3,2,0:T(8,128)(2,1)} %get-tuple-element.25) | copy-start | bytes 786436
  79.2 56.3 %collective-permute-start.9 = (bf16[2,128,8,128]{1,3,2,0:T(8,128)(2,1)}, bf16[2,128,8,128]{1,3,2,0:T(8,128)(2,1)}, u32[]{:S(2)}, u32[]{:S(2)}) collective-permute-start(bf16[2,128,8,128]{1,3,2,0:T(8,128)(2,1)} %pad_maximum_fusion.9), channel_id=1, source_target_pairs={{2,0},{3,1},{4,2},{5,3},{6,4},{7,5},{8,6},{9,7},{10,8},{11,9},{12,... | collective-permute-start | bytes 1572872 | tf_op jit(solution)/shard_map/ppermute | solution.py:17
  88.6 30.9 %collective-permute-start.4 = (bf16[2,128,1024]{1,2,0:T(8,128)(2,1)}, bf16[2,128,1024]{1,2,0:T(8,128)(2,1)}, u32[]{:S(2)}, u32[]{:S(2)}) collective-permute-start(bf16[2,128,1024]{1,2,0:T(8,128)(2,1)} %pad_maximum_fusion.5), channel_id=1, source_target_pairs={{0,1},{1,2},{2,3},{3,4},{4,5},{5,6},{6,7},{7,8},{8,9},{9,10},{10,1... | collective-permute-start | bytes 1572872 | tf_op jit(solution)/shard_map/ppermute | solution.py:17
  94.1 43.4 %collective-permute-start.10 = (bf16[2,128,8,128]{1,3,2,0:T(8,128)(2,1)}, bf16[2,128,8,128]{1,3,2,0:T(8,128)(2,1)}, u32[]{:S(2)}, u32[]{:S(2)}) collective-permute-start(bf16[2,128,8,128]{1,3,2,0:T(8,128)(2,1)} %pad_maximum_fusion.10), channel_id=1, source_target_pairs={{4,0},{5,1},{6,2},{7,3},{8,4},{9,5},{10,6},{11,7},{12,8},{13,9},{1... | collective-permute-start | bytes 1572872 | tf_op jit(solution)/shard_map/ppermute | solution.py:17
  101.6 37.2 %collective-permute-start.11 = (bf16[2,128,8,128]{1,3,2,0:T(8,128)(2,1)}, bf16[2,128,8,128]{1,3,2,0:T(8,128)(2,1)}, u32[]{:S(2)}, u32[]{:S(2)}) collective-permute-start(bf16[2,128,8,128]{1,3,2,0:T(8,128)(2,1)} %pad_maximum_fusion.11), channel_id=1, source_target_pairs={{8,0},{9,1},{10,2},{11,3},{12,4},{13,5},{14,6},{15,7},{24,16},{25,... | collective-permute-start | bytes 1572872 | tf_op jit(solution)/shard_map/ppermute | solution.py:17
  112.8 27.9 %collective-permute-start.8 = (bf16[2,128,8,128]{1,3,2,0:T(8,128)(2,1)}, bf16[2,128,8,128]{1,3,2,0:T(8,128)(2,1)}, u32[]{:S(2)}, u32[]{:S(2)}) collective-permute-start(bf16[2,128,8,128]{1,3,2,0:T(8,128)(2,1)} %pad_maximum_fusion.8), channel_id=1, source_target_pairs={{1,0},{2,1},{3,2},{4,3},{5,4},{6,5},{7,6},{8,7},{9,8},{10,9},{11,1... | collective-permute-start | bytes 1572872 | tf_op jit(solution)/shard_map/ppermute | solution.py:17
  124.0 1.3 copy-start.2
  124.0 1.3 copy-start.7
  124.1 1.4 copy-start.6
  131.1 18.2 %collective-permute-start.13 = (bf16[2,128,8,128]{1,3,2,0:T(8,128)(2,1)}, bf16[2,128,8,128]{1,3,2,0:T(8,128)(2,1)}, u32[]{:S(2)}, u32[]{:S(2)}) collective-permute-start(bf16[2,128,8,128]{1,3,2,0:T(8,128)(2,1)} %pad_maximum_fusion.13), channel_id=1, source_target_pairs={{2,0},{3,1},{4,2},{5,3},{6,4},{7,5},{8,6},{9,7},{10,8},{11,9},{12,... | collective-permute-start | bytes 1572872 | tf_op jit(solution)/shard_map/ppermute | solution.py:17
  133.9 6.9 %copy-start.8 = (bf16[128,8,128]{0,2,1:T(8,128)(2,1)S(1)}, bf16[128,8,128]{0,2,1:T(8,128)(2,1)}, u32[]{:S(2)}) copy-start(bf16[128,8,128]{0,2,1:T(8,128)(2,1)} %get-tuple-element.24) | copy-start | bytes 786436
  133.9 6.9 %copy-start.9 = (bf16[128,8,128]{0,2,1:T(8,128)(2,1)S(1)}, bf16[128,8,128]{0,2,1:T(8,128)(2,1)}, u32[]{:S(2)}) copy-start(bf16[128,8,128]{0,2,1:T(8,128)(2,1)} %get-tuple-element.38) | copy-start | bytes 786436
  135.5 16.9 %collective-permute-start.14 = (bf16[2,128,8,128]{1,3,2,0:T(8,128)(2,1)}, bf16[2,128,8,128]{1,3,2,0:T(8,128)(2,1)}, u32[]{:S(2)}, u32[]{:S(2)}) collective-permute-start(bf16[2,128,8,128]{1,3,2,0:T(8,128)(2,1)} %pad_maximum_fusion.14), channel_id=1, source_target_pairs={{4,0},{5,1},{6,2},{7,3},{8,4},{9,5},{10,6},{11,7},{12,8},{13,9},{1... | collective-permute-start | bytes 1572872 | tf_op jit(solution)/shard_map/ppermute | solution.py:17
  137.5 27.1 %collective-permute-start.15 = (bf16[2,128,8,128]{1,3,2,0:T(8,128)(2,1)}, bf16[2,128,8,128]{1,3,2,0:T(8,128)(2,1)}, u32[]{:S(2)}, u32[]{:S(2)}) collective-permute-start(bf16[2,128,8,128]{1,3,2,0:T(8,128)(2,1)} %pad_maximum_fusion.15), channel_id=1, source_target_pairs={{8,0},{9,1},{10,2},{11,3},{12,4},{13,5},{14,6},{15,7},{24,16},{25,... | collective-permute-start | bytes 1572872 | tf_op jit(solution)/shard_map/ppermute | solution.py:17
  138.8 50.4 %collective-permute-start.12 = (bf16[2,128,8,128]{1,3,2,0:T(8,128)(2,1)}, bf16[2,128,8,128]{1,3,2,0:T(8,128)(2,1)}, u32[]{:S(2)}, u32[]{:S(2)}) collective-permute-start(bf16[2,128,8,128]{1,3,2,0:T(8,128)(2,1)} %pad_maximum_fusion.12), channel_id=1, source_target_pairs={{1,0},{2,1},{3,2},{4,3},{5,4},{6,5},{7,6},{8,7},{9,8},{10,9},{11,1... | collective-permute-start | bytes 1572872 | tf_op jit(solution)/shard_map/ppermute | solution.py:17
  147.9 41.3 %copy-start.10 = (bf16[128,8,128]{0,2,1:T(8,128)(2,1)S(1)}, bf16[128,8,128]{0,2,1:T(8,128)(2,1)}, u32[]{:S(2)}) copy-start(bf16[128,8,128]{0,2,1:T(8,128)(2,1)} %get-tuple-element.43) | copy-start | bytes 786436
  147.9 41.3 %copy-start.11 = (bf16[128,8,128]{0,2,1:T(8,128)(2,1)S(1)}, bf16[128,8,128]{0,2,1:T(8,128)(2,1)}, u32[]{:S(2)}) copy-start(bf16[128,8,128]{0,2,1:T(8,128)(2,1)} %get-tuple-element.29) | copy-start | bytes 786436
  149.3 42.0 %copy-start = (f32[128,8,128]{0,2,1:T(8,128)S(1)}, f32[128,8,128]{0,2,1:T(8,128)}, u32[]{:S(2)}) copy-start(f32[128,8,128]{0,2,1:T(8,128)} %convolution_bitcast_fusion.1) | copy-start | bytes 1572868
  149.3 42.0 %copy-start.1 = (f32[128,8,128]{0,2,1:T(8,128)S(1)}, f32[128,8,128]{0,2,1:T(8,128)}, u32[]{:S(2)}) copy-start(f32[128,8,128]{0,2,1:T(8,128)} %convolution_bitcast_fusion) | copy-start | bytes 1572868
  192.7 1.1 copy-start.5

commit v29 on v25

--- a/solution.py
+++ b/solution.py
@@ -69,8 +69,7 @@
     return jnp.transpose(allowed, (0, 2, 1, 3))[:, None]
 
 
-def send_chunk(key_c, value_c, offsets, relay):
-    pair = jnp.stack([key_c, value_c])
+def send_chunk(pair, offsets, relay):
     received = {0: pair}
     for offset in offsets:
         if relay and (offset.bit_length() - 1) % 2 == 1:
@@ -155,10 +154,10 @@
     pieces = []
     pending = []
     for chunk, cols in enumerate(columns):
-        key_c, value_c = key_rot[:, cols], values[:, cols]
+        pair = jnp.stack([key_rot[:, cols], values[:, cols]])
         if pending:
-            key_c, value_c, _ = lax.optimization_barrier((key_c, value_c, pending[-1]))
-        received = send_chunk(key_c, value_c, offsets, relay=not pending)
+            pair, _ = lax.optimization_barrier((pair, pieces[-1][0]))
+        received = send_chunk(pair, offsets, relay=not pending)
         output, query_grad, own, outgoing = attend_chunk(
             query_rot[:, cols], received, grad_out[:, cols], allowed, offsets, chunk_heads
         )

time: 192 us -> 181 us (0.943)
  waiting for transfers between devices: 70.8 us -> 58.1 us
  starting transfers between devices: 47.9 us -> 52.6 us
    ppermute x16, waiting for transfers between devices: 70.8 us -> 58.1 us  [from_behind(): lax.ppermute(value, axis, [(source, source + steps) for source in range(l...]
    slice x4 -> x9, local copies, waits for them, and re-layouts: 5.05 us -> 13.6 us  [attend_chunk(): moved[0].reshape(head_shape)]
    slice x5 -> x2, local copies, waits for them, and re-layouts: 8.22 us -> 1.15 us  [on_device(): pair = jnp.stack([key_rot[:, cols], values[:, cols]])]
    ppermute x16, starting transfers between devices: 47.9 us -> 52.6 us  [from_behind(): lax.ppermute(value, axis, [(source, source + steps) for source in range(l...]
    unnamed x67 -> x60, local copies, waits for them, and re-layouts: 8.88 us -> 8.07 us
  transfers between devices with their start and end apart: 16 -> 16, of which waited for: 11 -> 8; matrix products, arithmetic and copies ran while one was open for 21% -> 27% of each run, Pallas kernels for 0% -> 0%
where the time goes in v29:
time: 181 us; the launch traced here: 180 us
  waiting for transfers between devices  58.1 us (32%)
  starting transfers between devices  52.6 us (29%)
  local copies, waits for them, and re-layouts  36.7 us (20%)
  other arithmetic  21 us (12%)
  matrix products  9.7 us (5%)
  between operations  2.11 us (1%)
    ppermute x16, waiting for transfers between devices, from_behind(): lax.ppermute(value, axis, [(source, source + steps) for source in range(l...  58.1 us
    ppermute x16, starting transfers between devices, from_behind(): lax.ppermute(value, axis, [(source, source + steps) for source in range(l...  52.6 us
    slice x9, local copies, waits for them, and re-layouts, attend_chunk(): moved[0].reshape(head_shape)  13.6 us
    unnamed x60, local copies, waits for them, and re-layouts  8.07 us
    another operation x8, other arithmetic, attend_chunk(): jnp.stack([key_terms[0, slot_index], value_terms[0, slot_index]])  6.77 us
    another operation x12, local copies, waits for them, and re-layouts, attend_chunk(): jnp.stack([moved[0].reshape(head_shape) for moved in received])[None]  5.61 us
    another operation x6, other arithmetic  5.35 us
  transfers between devices with their start and end apart: 16, of which 8 were waited for; matrix products, arithmetic and copies ran while one was open for 27% of the time, Pallas kernels for 0%

profile of v29, /device:TPU:15, one launch (start us, length us, event | category | flops | bytes accessed | tf_op | source)
XLA Modules:
  0.0 180.3 jit_solution(1823419791764501624)
XLA Ops:
  6.3 3.2 %collective-permute-start.2 = (bf16[2,128,1024]{1,2,0:T(8,128)(2,1)}, bf16[2,128,1024]{1,2,0:T(8,128)(2,1)}, u32[]{:S(2)}, u32[]{:S(2)}) collective-permute-start(bf16[2,128,1024]{1,2,0:T(8,128)(2,1)} %pad_maximum_fusion.3), channel_id=1, source_target_pairs={{0,4},{1,5},{2,6},{3,7},{4,8},{5,9},{6,10},{7,11},{8,12},{9,13},{1... | collective-permute-start | bytes 1572872 | tf_op jit(solution)/shard_map/ppermute | solution.py:17
  9.5 4.0 %collective-permute-start = (bf16[2,128,1024]{1,2,0:T(8,128)(2,1)}, bf16[2,128,1024]{1,2,0:T(8,128)(2,1)}, u32[]{:S(2)}, u32[]{:S(2)}) collective-permute-start(bf16[2,128,1024]{1,2,0:T(8,128)(2,1)} %pad_maximum_fusion.3), channel_id=1, source_target_pairs={{0,1},{1,2},{2,3},{3,4},{4,5},{5,6},{6,7},{7,8},{8,9},{9,10},{10,1... | collective-permute-start | bytes 1572872 | tf_op jit(solution)/shard_map/ppermute | solution.py:17
  16.9 4.4 %collective-permute-done.2 = bf16[2,128,1024]{1,2,0:T(8,128)(2,1)} collective-permute-done((bf16[2,128,1024]{1,2,0:T(8,128)(2,1)}, bf16[2,128,1024]{1,2,0:T(8,128)(2,1)}, u32[]{:S(2)}, u32[]{:S(2)}) %collective-permute-start.2) | collective-permute-done | bytes 524320 | tf_op jit(solution)/shard_map/ppermute | solution.py:17
  21.3 3.2 %collective-permute-start.3 = (bf16[2,128,1024]{1,2,0:T(8,128)(2,1)}, bf16[2,128,1024]{1,2,0:T(8,128)(2,1)}, u32[]{:S(2)}, u32[]{:S(2)}) collective-permute-start(bf16[2,128,1024]{1,2,0:T(8,128)(2,1)} %collective-permute-done.2), channel_id=1, source_target_pairs={{0,4},{1,5},{2,6},{3,7},{4,8},{5,9},{6,10},{7,11},{8,12},{9,13},{1... | collective-permute-start | bytes 1572872 | tf_op jit(solution)/shard_map/ppermute | solution.py:17
  25.6 1.6 collective-permute-done
  27.2 5.3 %collective-permute-start.1 = (bf16[2,128,1024]{1,2,0:T(8,128)(2,1)}, bf16[2,128,1024]{1,2,0:T(8,128)(2,1)}, u32[]{:S(2)}, u32[]{:S(2)}) collective-permute-start(bf16[2,128,1024]{1,2,0:T(8,128)(2,1)} %collective-permute-done), channel_id=1, source_target_pairs={{0,1},{1,2},{2,3},{3,4},{4,5},{5,6},{6,7},{7,8},{8,9},{9,10},{10,1... | collective-permute-start | bytes 1572872 | tf_op jit(solution)/shard_map/ppermute | solution.py:17
  32.5 1.8 fusion.44
  36.4 1.6 collective-permute-done.3
  38.0 1.8 fusion.41
  39.9 4.1 %collective-permute-done.1 = bf16[2,128,1024]{1,2,0:T(8,128)(2,1)} collective-permute-done((bf16[2,128,1024]{1,2,0:T(8,128)(2,1)}, bf16[2,128,1024]{1,2,0:T(8,128)(2,1)}, u32[]{:S(2)}, u32[]{:S(2)}) %collective-permute-start.1) | collective-permute-done | bytes 524320 | tf_op jit(solution)/shard_map/ppermute | solution.py:17
  44.0 1.9 %fusion.43 = (bf16[1,128,1024]{1,2,0:T(8,128)(2,1)}, bf16[1,128,1024]{1,2,0:T(8,128)(2,1)}) fusion(bf16[2,128,1024]{1,2,0:T(8,128)(2,1)} %collective-permute-done.1), kind=kLoop, calls=%fused_computation.178 | loop fusion | bytes 1048576 | tf_op jit(solution)/shard_map/slice | solution.py:87
  51.8 2.1 %collective-permute-start.7 = (bf16[2,128,1024]{1,2,0:T(8,128)(2,1)S(1)}, bf16[2,128,1024]{1,2,0:T(8,128)(2,1)}, u32[]{:S(2)}, u32[]{:S(2)}) collective-permute-start(bf16[2,128,1024]{1,2,0:T(8,128)(2,1)S(1)} %copy-done.1), channel_id=1, source_target_pairs={{0,8},{1,9},{2,10},{3,11},{4,12},{5,13},{6,14},{7,15},{16,24},{17,... | collective-permute-start | bytes 1572872 | tf_op jit(solution)/shard_map/ppermute | solution.py:17
  53.9 2.4 %collective-permute-start.6 = (bf16[2,128,1024]{1,2,0:T(8,128)(2,1)S(1)}, bf16[2,128,1024]{1,2,0:T(8,128)(2,1)}, u32[]{:S(2)}, u32[]{:S(2)}) collective-permute-start(bf16[2,128,1024]{1,2,0:T(8,128)(2,1)S(1)} %copy-done.1), channel_id=1, source_target_pairs={{0,4},{1,5},{2,6},{3,7},{4,8},{5,9},{6,10},{7,11},{8,12},{9,13},{1... | collective-permute-start | bytes 1572872 | tf_op jit(solution)/shard_map/ppermute | solution.py:17
  56.3 1.9 %collective-permute-start.5 = (bf16[2,128,1024]{1,2,0:T(8,128)(2,1)S(1)}, bf16[2,128,1024]{1,2,0:T(8,128)(2,1)}, u32[]{:S(2)}, u32[]{:S(2)}) collective-permute-start(bf16[2,128,1024]{1,2,0:T(8,128)(2,1)S(1)} %copy-done.1), channel_id=1, source_target_pairs={{0,2},{1,3},{2,4},{3,5},{4,6},{5,7},{6,8},{7,9},{8,10},{9,11},{10,... | collective-permute-start | bytes 1572872 | tf_op jit(solution)/shard_map/ppermute | solution.py:17
  64.7 3.4 %collective-permute-start.9 = (bf16[2,128,8,128]{1,3,2,0:T(8,128)(2,1)}, bf16[2,128,8,128]{1,3,2,0:T(8,128)(2,1)}, u32[]{:S(2)}, u32[]{:S(2)}) collective-permute-start(bf16[2,128,8,128]{1,3,2,0:T(8,128)(2,1)} %pad_maximum_fusion.9), channel_id=1, source_target_pairs={{2,0},{3,1},{4,2},{5,3},{6,4},{7,5},{8,6},{9,7},{10,8},{11,9},{12,... | collective-permute-start | bytes 1572872 | tf_op jit(solution)/shard_map/ppermute | solution.py:17
  72.4 7.0 %collective-permute-start.4 = (bf16[2,128,1024]{1,2,0:T(8,128)(2,1)S(1)}, bf16[2,128,1024]{1,2,0:T(8,128)(2,1)}, u32[]{:S(2)}, u32[]{:S(2)}) collective-permute-start(bf16[2,128,1024]{1,2,0:T(8,128)(2,1)S(1)} %copy-done.1), channel_id=1, source_target_pairs={{0,1},{1,2},{2,3},{3,4},{4,5},{5,6},{6,7},{7,8},{8,9},{9,10},{10,1... | collective-permute-start | bytes 1572872 | tf_op jit(solution)/shard_map/ppermute | solution.py:17
  79.5 4.5 %collective-permute-start.10 = (bf16[2,128,8,128]{1,3,2,0:T(8,128)(2,1)}, bf16[2,128,8,128]{1,3,2,0:T(8,128)(2,1)}, u32[]{:S(2)}, u32[]{:S(2)}) collective-permute-start(bf16[2,128,8,128]{1,3,2,0:T(8,128)(2,1)} %pad_maximum_fusion.10), channel_id=1, source_target_pairs={{4,0},{5,1},{6,2},{7,3},{8,4},{9,5},{10,6},{11,7},{12,8},{13,9},{1... | collective-permute-start | bytes 1572872 | tf_op jit(solution)/shard_map/ppermute | solution.py:17
  86.5 1.8 fusion.37
  88.5 7.7 %collective-permute-done.5 = bf16[2,128,1024]{1,2,0:T(8,128)(2,1)} collective-permute-done((bf16[2,128,1024]{1,2,0:T(8,128)(2,1)S(1)}, bf16[2,128,1024]{1,2,0:T(8,128)(2,1)}, u32[]{:S(2)}, u32[]{:S(2)}) %collective-permute-start.5) | collective-permute-done | bytes 524320 | tf_op jit(solution)/shard_map/ppermute | solution.py:17
  96.1 7.3 %collective-permute-start.8 = (bf16[2,128,8,128]{1,3,2,0:T(8,128)(2,1)}, bf16[2,128,8,128]{1,3,2,0:T(8,128)(2,1)}, u32[]{:S(2)}, u32[]{:S(2)}) collective-permute-start(bf16[2,128,8,128]{1,3,2,0:T(8,128)(2,1)} %pad_maximum_fusion.8), channel_id=1, source_target_pairs={{1,0},{2,1},{3,2},{4,3},{5,4},{6,5},{7,6},{8,7},{9,8},{10,9},{11,1... | collective-permute-start | bytes 1572872 | tf_op jit(solution)/shard_map/ppermute | solution.py:17
  103.5 1.9 %fusion.38 = (bf16[1,128,1024]{1,2,0:T(8,128)(2,1)}, bf16[1,128,1024]{1,2,0:T(8,128)(2,1)}) fusion(bf16[2,128,1024]{1,2,0:T(8,128)(2,1)} %collective-permute-done.5), kind=kLoop, calls=%fused_computation.173 | loop fusion | bytes 1048576 | tf_op jit(solution)/shard_map/slice | solution.py:87
  106.5 1.8 fusion.39
  118.0 1.9 %collective-permute-start.13 = (bf16[2,128,8,128]{1,3,2,0:T(8,128)(2,1)}, bf16[2,128,8,128]{1,3,2,0:T(8,128)(2,1)}, u32[]{:S(2)}, u32[]{:S(2)}) collective-permute-start(bf16[2,128,8,128]{1,3,2,0:T(8,128)(2,1)} %pad_maximum_fusion.13), channel_id=1, source_target_pairs={{2,0},{3,1},{4,2},{5,3},{6,4},{7,5},{8,6},{9,7},{10,8},{11,9},{12,... | collective-permute-start | bytes 1572872 | tf_op jit(solution)/shard_map/ppermute | solution.py:17
  122.5 1.9 %collective-permute-start.14 = (bf16[2,128,8,128]{1,3,2,0:T(8,128)(2,1)}, bf16[2,128,8,128]{1,3,2,0:T(8,128)(2,1)}, u32[]{:S(2)}, u32[]{:S(2)}) collective-permute-start(bf16[2,128,8,128]{1,3,2,0:T(8,128)(2,1)} %pad_maximum_fusion.14), channel_id=1, source_target_pairs={{4,0},{5,1},{6,2},{7,3},{8,4},{9,5},{10,6},{11,7},{12,8},{13,9},{1... | collective-permute-start | bytes 1572872 | tf_op jit(solution)/shard_map/ppermute | solution.py:17
  125.7 1.9 %collective-permute-start.12 = (bf16[2,128,8,128]{1,3,2,0:T(8,128)(2,1)}, bf16[2,128,8,128]{1,3,2,0:T(8,128)(2,1)}, u32[]{:S(2)}, u32[]{:S(2)}) collective-permute-start(bf16[2,128,8,128]{1,3,2,0:T(8,128)(2,1)} %pad_maximum_fusion.12), channel_id=1, source_target_pairs={{1,0},{2,1},{3,2},{4,3},{5,4},{6,5},{7,6},{8,7},{9,8},{10,9},{11,1... | collective-permute-start | bytes 1572872 | tf_op jit(solution)/shard_map/ppermute | solution.py:17
  127.7 2.6 %fusion.27 = (bf16[128,8,128]{0,2,1:T(8,128)(2,1)}, f32[128,8,128]{0,2,1:T(8,128)S(1)}) fusion(bf16[128,8,128]{0,2,1:T(8,128)(2,1)S(1)} %copy-done.11, bf16[2,128,8,128]{1,3,2,0:T(8,128)(2,1)} %collective-permute-done.11, bf16[2,128,8,128]{1,3,2,0:T(8,128)(2,1)} %collective-permute-done.10, bf16[2,128,8,128]{1,3,2,0:T(8,128)(2,1)} %collective-permute-done.9, ...), kind=kLoop, calls=%fused_computation.70 | loop fusion | flops 2490368 | bytes 3407872 | tf_op jit(solution)/shard_map/convert.23
  130.3 1.8 %copy.132 = bf16[128,1024]{1,0:T(8,128)(2,1)} copy(bf16[128,1024]{0,1:T(8,128)(2,1)} %bitcast.379) | data formatting | bytes 524288 | tf_op jit(solution)/shard_map/reshape | solution.py:172
  133.0 1.9 %pad_maximum_fusion.6 = bf16[128,2048]{1,0:T(8,128)(2,1)} fusion(bf16[128,1024]{1,0:T(8,128)(2,1)} %copy.113, bf16[128,1024]{1,0:T(8,128)(2,1)} %copy.112), kind=kLoop, calls=%fused_computation.52 | loop fusion | flops 1048576 | bytes 1048576 | tf_op jit(solution)/shard_map/concatenate | solution.py:176
  136.2 4.0 %collective-permute-done.14 = bf16[2,128,8,128]{1,3,2,0:T(8,128)(2,1)} collective-permute-done((bf16[2,128,8,128]{1,3,2,0:T(8,128)(2,1)}, bf16[2,128,8,128]{1,3,2,0:T(8,128)(2,1)}, u32[]{:S(2)}, u32[]{:S(2)}) %collective-permute-start.14) | collective-permute-done | bytes 524320 | tf_op jit(solution)/shard_map/ppermute | solution.py:17
  140.2 12.1 %collective-permute-done.15 = bf16[2,128,8,128]{1,3,2,0:T(8,128)(2,1)} collective-permute-done((bf16[2,128,8,128]{1,3,2,0:T(8,128)(2,1)}, bf16[2,128,8,128]{1,3,2,0:T(8,128)(2,1)}, u32[]{:S(2)}, u32[]{:S(2)}) %collective-permute-start.15) | collective-permute-done | bytes 524320 | tf_op jit(solution)/shard_map/ppermute | solution.py:17
  152.4 22.6 %collective-permute-done.12 = bf16[2,128,8,128]{1,3,2,0:T(8,128)(2,1)} collective-permute-done((bf16[2,128,8,128]{1,3,2,0:T(8,128)(2,1)}, bf16[2,128,8,128]{1,3,2,0:T(8,128)(2,1)}, u32[]{:S(2)}, u32[]{:S(2)}) %collective-permute-start.12) | collective-permute-done | bytes 524320 | tf_op jit(solution)/shard_map/ppermute | solution.py:17
  174.9 1.9 %fusion.26 = (bf16[128,8,128]{0,2,1:T(8,128)(2,1)S(1)}, f32[128,8,128]{0,2,1:T(8,128)S(1)}) fusion(bf16[128,8,128]{0,2,1:T(8,128)(2,1)S(1)} %copy-done.14, bf16[2,128,8,128]{1,3,2,0:T(8,128)(2,1)} %collective-permute-done.15, bf16[2,128,8,128]{1,3,2,0:T(8,128)(2,1)} %collective-permute-done.14, bf16[2,128,8,128]{1,3,2,0:T(8,128)(2,1)} %collective-permute-done.13, ...), kind=kLoop, calls=%fused_computation.65 | loop fusion | flops 2490368 | bytes 3407872 | tf_op jit(solution)/shard_map/convert.22
  (152 shorter events, 51.1 us)
Async XLA Ops:
  0.6 3.1 %copy-start.15 = (bf16[128,2048]{1,0:T(8,128)(2,1)S(1)}, bf16[128,2048]{1,0:T(8,128)(2,1)}, u32[]{:S(2)}) copy-start(bf16[128,2048]{1,0:T(8,128)(2,1)} %param.7) | copy-start | bytes 1572868
  5.4 8.8 %copy-start.17 = (bf16[128,2048]{1,0:T(8,128)(2,1)S(1)}, bf16[128,2048]{1,0:T(8,128)(2,1)}, u32[]{:S(2)}) copy-start(bf16[128,2048]{1,0:T(8,128)(2,1)} %param.10) | copy-start | bytes 1572868
  5.5 9.0 %copy-start.18 = (s32[4]{0:T(128)S(1)}, s32[4]{0:T(128)}, u32[]{:S(2)}) copy-start(s32[4]{0:T(128)} %constant.35) | copy-start | bytes 52
  6.3 15.0 %collective-permute-start.2 = (bf16[2,128,1024]{1,2,0:T(8,128)(2,1)}, bf16[2,128,1024]{1,2,0:T(8,128)(2,1)}, u32[]{:S(2)}, u32[]{:S(2)}) collective-permute-start(bf16[2,128,1024]{1,2,0:T(8,128)(2,1)} %pad_maximum_fusion.3), channel_id=1, source_target_pairs={{0,4},{1,5},{2,6},{3,7},{4,8},{5,9},{6,10},{7,11},{8,12},{9,13},{1... | collective-permute-start | bytes 1572872 | tf_op jit(solution)/shard_map/ppermute | solution.py:17
  9.5 17.7 %collective-permute-start = (bf16[2,128,1024]{1,2,0:T(8,128)(2,1)}, bf16[2,128,1024]{1,2,0:T(8,128)(2,1)}, u32[]{:S(2)}, u32[]{:S(2)}) collective-permute-start(bf16[2,128,1024]{1,2,0:T(8,128)(2,1)} %pad_maximum_fusion.3), channel_id=1, source_target_pairs={{0,1},{1,2},{2,3},{3,4},{4,5},{5,6},{6,7},{7,8},{8,9},{9,10},{10,1... | collective-permute-start | bytes 1572872 | tf_op jit(solution)/shard_map/ppermute | solution.py:17
  21.3 16.6 %collective-permute-start.3 = (bf16[2,128,1024]{1,2,0:T(8,128)(2,1)}, bf16[2,128,1024]{1,2,0:T(8,128)(2,1)}, u32[]{:S(2)}, u32[]{:S(2)}) collective-permute-start(bf16[2,128,1024]{1,2,0:T(8,128)(2,1)} %collective-permute-done.2), channel_id=1, source_target_pairs={{0,4},{1,5},{2,6},{3,7},{4,8},{5,9},{6,10},{7,11},{8,12},{9,13},{1... | collective-permute-start | bytes 1572872 | tf_op jit(solution)/shard_map/ppermute | solution.py:17
  27.2 16.9 %collective-permute-start.1 = (bf16[2,128,1024]{1,2,0:T(8,128)(2,1)}, bf16[2,128,1024]{1,2,0:T(8,128)(2,1)}, u32[]{:S(2)}, u32[]{:S(2)}) collective-permute-start(bf16[2,128,1024]{1,2,0:T(8,128)(2,1)} %collective-permute-done), channel_id=1, source_target_pairs={{0,1},{1,2},{2,3},{3,4},{4,5},{5,6},{6,7},{7,8},{8,9},{9,10},{10,1... | collective-permute-start | bytes 1572872 | tf_op jit(solution)/shard_map/ppermute | solution.py:17
  48.6 1.3 copy-start.4
  48.6 1.3 copy-start.10
  48.6 1.4 copy-start.8
  51.8 27.6 %collective-permute-start.7 = (bf16[2,128,1024]{1,2,0:T(8,128)(2,1)S(1)}, bf16[2,128,1024]{1,2,0:T(8,128)(2,1)}, u32[]{:S(2)}, u32[]{:S(2)}) collective-permute-start(bf16[2,128,1024]{1,2,0:T(8,128)(2,1)S(1)} %copy-done.1), channel_id=1, source_target_pairs={{0,8},{1,9},{2,10},{3,11},{4,12},{5,13},{6,14},{7,15},{16,24},{17,... | collective-permute-start | bytes 1572872 | tf_op jit(solution)/shard_map/ppermute | solution.py:17
  53.9 31.3 %collective-permute-start.6 = (bf16[2,128,1024]{1,2,0:T(8,128)(2,1)S(1)}, bf16[2,128,1024]{1,2,0:T(8,128)(2,1)}, u32[]{:S(2)}, u32[]{:S(2)}) collective-permute-start(bf16[2,128,1024]{1,2,0:T(8,128)(2,1)S(1)} %copy-done.1), channel_id=1, source_target_pairs={{0,4},{1,5},{2,6},{3,7},{4,8},{5,9},{6,10},{7,11},{8,12},{9,13},{1... | collective-permute-start | bytes 1572872 | tf_op jit(solution)/shard_map/ppermute | solution.py:17
  56.3 39.8 %collective-permute-start.5 = (bf16[2,128,1024]{1,2,0:T(8,128)(2,1)S(1)}, bf16[2,128,1024]{1,2,0:T(8,128)(2,1)}, u32[]{:S(2)}, u32[]{:S(2)}) collective-permute-start(bf16[2,128,1024]{1,2,0:T(8,128)(2,1)S(1)} %copy-done.1), channel_id=1, source_target_pairs={{0,2},{1,3},{2,4},{3,5},{4,6},{5,7},{6,8},{7,9},{8,10},{9,11},{10,... | collective-permute-start | bytes 1572872 | tf_op jit(solution)/shard_map/ppermute | solution.py:17
  64.7 57.8 %collective-permute-start.9 = (bf16[2,128,8,128]{1,3,2,0:T(8,128)(2,1)}, bf16[2,128,8,128]{1,3,2,0:T(8,128)(2,1)}, u32[]{:S(2)}, u32[]{:S(2)}) collective-permute-start(bf16[2,128,8,128]{1,3,2,0:T(8,128)(2,1)} %pad_maximum_fusion.9), channel_id=1, source_target_pairs={{2,0},{3,1},{4,2},{5,3},{6,4},{7,5},{8,6},{9,7},{10,8},{11,9},{12,... | collective-permute-start | bytes 1572872 | tf_op jit(solution)/shard_map/ppermute | solution.py:17
  68.0 2.5 %copy-start.6 = (bf16[1,128,1024]{1,2,0:T(8,128)(2,1)S(1)}, bf16[1,128,1024]{1,2,0:T(8,128)(2,1)}, u32[]{:S(2)}) copy-start(bf16[1,128,1024]{1,2,0:T(8,128)(2,1)} %get-tuple-element.62) | copy-start | bytes 786436
  72.4 34.0 %collective-permute-start.4 = (bf16[2,128,1024]{1,2,0:T(8,128)(2,1)S(1)}, bf16[2,128,1024]{1,2,0:T(8,128)(2,1)}, u32[]{:S(2)}, u32[]{:S(2)}) collective-permute-start(bf16[2,128,1024]{1,2,0:T(8,128)(2,1)S(1)} %copy-done.1), channel_id=1, source_target_pairs={{0,1},{1,2},{2,3},{3,4},{4,5},{5,6},{6,7},{7,8},{8,9},{9,10},{10,1... | collective-permute-start | bytes 1572872 | tf_op jit(solution)/shard_map/ppermute | solution.py:17
  79.5 44.9 %collective-permute-start.10 = (bf16[2,128,8,128]{1,3,2,0:T(8,128)(2,1)}, bf16[2,128,8,128]{1,3,2,0:T(8,128)(2,1)}, u32[]{:S(2)}, u32[]{:S(2)}) collective-permute-start(bf16[2,128,8,128]{1,3,2,0:T(8,128)(2,1)} %pad_maximum_fusion.10), channel_id=1, source_target_pairs={{4,0},{5,1},{6,2},{7,3},{8,4},{9,5},{10,6},{11,7},{12,8},{13,9},{1... | collective-permute-start | bytes 1572872 | tf_op jit(solution)/shard_map/ppermute | solution.py:17
  85.2 40.4 %collective-permute-start.11 = (bf16[2,128,8,128]{1,3,2,0:T(8,128)(2,1)}, bf16[2,128,8,128]{1,3,2,0:T(8,128)(2,1)}, u32[]{:S(2)}, u32[]{:S(2)}) collective-permute-start(bf16[2,128,8,128]{1,3,2,0:T(8,128)(2,1)} %pad_maximum_fusion.11), channel_id=1, source_target_pairs={{8,0},{9,1},{10,2},{11,3},{12,4},{13,5},{14,6},{15,7},{24,16},{25,... | collective-permute-start | bytes 1572872 | tf_op jit(solution)/shard_map/ppermute | solution.py:17
  96.1 31.5 %collective-permute-start.8 = (bf16[2,128,8,128]{1,3,2,0:T(8,128)(2,1)}, bf16[2,128,8,128]{1,3,2,0:T(8,128)(2,1)}, u32[]{:S(2)}, u32[]{:S(2)}) collective-permute-start(bf16[2,128,8,128]{1,3,2,0:T(8,128)(2,1)} %pad_maximum_fusion.8), channel_id=1, source_target_pairs={{1,0},{2,1},{3,2},{4,3},{5,4},{6,5},{7,6},{8,7},{9,8},{10,9},{11,1... | collective-permute-start | bytes 1572872 | tf_op jit(solution)/shard_map/ppermute | solution.py:17
  111.0 1.3 copy-start.3
  111.0 1.3 copy-start.9
  111.0 1.4 copy-start.7
  118.0 18.3 %collective-permute-start.13 = (bf16[2,128,8,128]{1,3,2,0:T(8,128)(2,1)}, bf16[2,128,8,128]{1,3,2,0:T(8,128)(2,1)}, u32[]{:S(2)}, u32[]{:S(2)}) collective-permute-start(bf16[2,128,8,128]{1,3,2,0:T(8,128)(2,1)} %pad_maximum_fusion.13), channel_id=1, source_target_pairs={{2,0},{3,1},{4,2},{5,3},{6,4},{7,5},{8,6},{9,7},{10,8},{11,9},{12,... | collective-permute-start | bytes 1572872 | tf_op jit(solution)/shard_map/ppermute | solution.py:17
  120.8 6.9 %copy-start.11 = (bf16[128,8,128]{0,2,1:T(8,128)(2,1)S(1)}, bf16[128,8,128]{0,2,1:T(8,128)(2,1)}, u32[]{:S(2)}) copy-start(bf16[128,8,128]{0,2,1:T(8,128)(2,1)} %get-tuple-element.22) | copy-start | bytes 786436
  120.8 6.9 %copy-start.12 = (bf16[128,8,128]{0,2,1:T(8,128)(2,1)S(1)}, bf16[128,8,128]{0,2,1:T(8,128)(2,1)}, u32[]{:S(2)}) copy-start(bf16[128,8,128]{0,2,1:T(8,128)(2,1)} %get-tuple-element.36) | copy-start | bytes 786436
  122.5 17.8 %collective-permute-start.14 = (bf16[2,128,8,128]{1,3,2,0:T(8,128)(2,1)}, bf16[2,128,8,128]{1,3,2,0:T(8,128)(2,1)}, u32[]{:S(2)}, u32[]{:S(2)}) collective-permute-start(bf16[2,128,8,128]{1,3,2,0:T(8,128)(2,1)} %pad_maximum_fusion.14), channel_id=1, source_target_pairs={{4,0},{5,1},{6,2},{7,3},{8,4},{9,5},{10,6},{11,7},{12,8},{13,9},{1... | collective-permute-start | bytes 1572872 | tf_op jit(solution)/shard_map/ppermute | solution.py:17
  124.4 28.0 %collective-permute-start.15 = (bf16[2,128,8,128]{1,3,2,0:T(8,128)(2,1)}, bf16[2,128,8,128]{1,3,2,0:T(8,128)(2,1)}, u32[]{:S(2)}, u32[]{:S(2)}) collective-permute-start(bf16[2,128,8,128]{1,3,2,0:T(8,128)(2,1)} %pad_maximum_fusion.15), channel_id=1, source_target_pairs={{8,0},{9,1},{10,2},{11,3},{12,4},{13,5},{14,6},{15,7},{24,16},{25,... | collective-permute-start | bytes 1572872 | tf_op jit(solution)/shard_map/ppermute | solution.py:17
  125.7 49.2 %collective-permute-start.12 = (bf16[2,128,8,128]{1,3,2,0:T(8,128)(2,1)}, bf16[2,128,8,128]{1,3,2,0:T(8,128)(2,1)}, u32[]{:S(2)}, u32[]{:S(2)}) collective-permute-start(bf16[2,128,8,128]{1,3,2,0:T(8,128)(2,1)} %pad_maximum_fusion.12), channel_id=1, source_target_pairs={{1,0},{2,1},{3,2},{4,3},{5,4},{6,5},{7,6},{8,7},{9,8},{10,9},{11,1... | collective-permute-start | bytes 1572872 | tf_op jit(solution)/shard_map/ppermute | solution.py:17
  134.8 40.1 %copy-start.13 = (bf16[128,8,128]{0,2,1:T(8,128)(2,1)S(1)}, bf16[128,8,128]{0,2,1:T(8,128)(2,1)}, u32[]{:S(2)}) copy-start(bf16[128,8,128]{0,2,1:T(8,128)(2,1)} %get-tuple-element.41) | copy-start | bytes 786436
  134.8 40.1 %copy-start.14 = (bf16[128,8,128]{0,2,1:T(8,128)(2,1)S(1)}, bf16[128,8,128]{0,2,1:T(8,128)(2,1)}, u32[]{:S(2)}) copy-start(bf16[128,8,128]{0,2,1:T(8,128)(2,1)} %get-tuple-element.27) | copy-start | bytes 786436
  136.2 40.8 %copy-start = (f32[128,8,128]{0,2,1:T(8,128)S(1)}, f32[128,8,128]{0,2,1:T(8,128)}, u32[]{:S(2)}) copy-start(f32[128,8,128]{0,2,1:T(8,128)} %convolution_bitcast_fusion.1) | copy-start | bytes 1572868
  136.2 40.8 %copy-start.2 = (f32[128,8,128]{0,2,1:T(8,128)S(1)}, f32[128,8,128]{0,2,1:T(8,128)}, u32[]{:S(2)}) copy-start(f32[128,8,128]{0,2,1:T(8,128)} %convolution_bitcast_fusion) | copy-start | bytes 1572868
  (3 other events, 3.1 us)
